TPU v7x, 32 devices: a whole 2x2x4 slice. The times are simulated.
32 devices in a mesh: outer: 4 (over z), dp: 2 (over y), cent: 4 (over x, core).
Axes of the slice: x: 2, y: 2, z: 4, core: 2. Of those that a mesh axis runs over, the one named last changes fastest.
Arguments:
- rows: float32 [2048, 1024], P(('outer', 'dp')), may hold values from -256 to 256
- centroids: float32 [4096, 1024], P(('dp', 'cent')), may hold values from -0.5 to 0.5
Outputs:
- centroid_shift: float32 [4096, 1024], P(('dp', 'cent'))
All inputs are finite; a program needn't handle non-finite values.
Results may differ from a plain program's by a relative error of at most 0.0081.
Values may be sent and summed in bfloat16 or wider, within the bound.
No kernel may reach another device: no remote copies, remote signals or barrier semaphores. Data moves between devices by JAX's collectives and lax.ppermute only.
A program may use at most 64 MiB of HBM per device.

v0:
```python
import jax
import jax.numpy as jnp
from jax import lax
from jax.sharding import PartitionSpec as P


def scores_for(piece, cent_bf, squares):
    product = lax.dot_general(
        piece, cent_bf, (((1,), (1,)), ((), ())), preferred_element_type=jnp.float32
    )
    return 0.5 * (2.0 * product - squares[None, :])


def row_summary(logits):
    local_max = jnp.max(logits, axis=1)
    local_sum = jnp.sum(jnp.exp(logits - local_max[:, None]), axis=1)
    return (local_max, local_sum)


def global_stats(local_max, local_sum):
    row_peak = lax.pmax(local_max, ("dp", "cent"))
    row_mass = lax.psum(local_sum * jnp.exp(local_max - row_peak), ("dp", "cent"))
    return (row_peak, row_mass)


def shards(rows, centroids):
    rows_bf = rows.astype(jnp.bfloat16)
    cent_bf = centroids.astype(jnp.bfloat16)
    squares = jnp.sum(centroids * centroids, axis=1)
    gathered = lax.all_gather(rows_bf, "dp", axis=0, tiled=True)
    logits = scores_for(gathered, cent_bf, squares)
    local_max, local_sum = row_summary(logits)
    row_peak, row_mass = global_stats(local_max, local_sum)
    weights = (jnp.exp(logits - row_peak[:, None]) / row_mass[:, None]).astype(jnp.bfloat16)
    weight_sum = jnp.sum(weights.astype(jnp.float32), axis=0)
    pull = lax.dot_general(
        weights, gathered, (((0,), (0,)), ((), ())), preferred_element_type=jnp.float32
    )
    delta = (pull - weight_sum[:, None] * centroids) / (weight_sum[:, None] + 1.0)
    return lax.psum(delta, "outer") / lax.axis_size("outer")


def solution(mesh):
    return jax.shard_map(
        shards,
        mesh=mesh,
        in_specs=(P(("outer", "dp"), None), P(("dp", "cent"), None)),
        out_specs=P(("dp", "cent"), None),
        check_vma=False,
    )
```

profile of v0, /device:TPU:0, one launch (start us, length us, event | category | flops | bytes accessed | tf_op | source)
XLA Modules:
  0.0 160.0 jit_solution(11891567191275131057)
XLA Ops:
  6.5 0.0 copy-start
  6.5 0.0 all-gather.2.cloned.1.call-start
  6.5 2.2 %convert_element_type.12 = bf16[256,1024]{1,0:T(8,128)(2,1)} convert(f32[256,1024]{1,0:T(8,128)} %param.2) | non-fusion elementwise | flops 262144 | bytes 1572864 | tf_op jit(solution)/shard_map/convert_element_type | solution.py:27
  8.8 0.0 all-gather.2.cloned.1.call-update
  8.8 0.0 all-reduce.2.cloned.1.call-start
  8.9 0.0 copy-done
  8.9 0.2 multiply_reduce_fusion
  9.1 23.9 %all-gather.2.cloned.1.call-done = bf16[512,1024]{1,0:T(8,128)(2,1)} async-done(((bf16[256,1024]{1,0:T(8,128)(2,1)}), bf16[512,1024]{1,0:T(8,128)(2,1)}) %all-gather.2.cloned.1.call-update) | async-done | bytes 1048592 | tf_op jit(solution)/shard_map/all_gather | solution.py:30
  33.0 2.0 %fusion.3 = (f32[512]{0:T(512)S(1)}, f32[512,512]{0,1:T(8,128)S(1)}) fusion(f32[512]{0:T(512)S(1)} %multiply_reduce_fusion, bf16[512,1024]{1,0:T(8,128)(2,1)} %all-gather.2.cloned.1.call-done, f32[512,1024]{1,0:T(8,128)S(1)} %copy-done), kind=kOutput, calls=%fused_computation.12 | convolution fusion | flops 538443264 | bytes 4198400 | tf_op jit(solution)/shard_map/dot_general | solution.py:8
  35.0 12.7 %pmax.7 = f32[512]{0:T(512)S(1)} all-reduce(f32[512]{0:T(512)S(1)} %get-tuple-element.7), channel_id=1, replica_groups=mesh['outer'=4,'dp'=2,'cent'=4] {'dp','cent'}, use_global_device_ids=true, to_apply=%region_2.0 | all-reduce | flops 512 | bytes 4096 | tf_op jit(solution)/shard_map/pmax | solution.py:21
  47.7 0.2 exponential_reduce_fusion
  47.9 11.8 %psum.14 = f32[512]{0:T(512)S(1)} all-reduce(f32[512]{0:T(512)S(1)} %exponential_multiply_fusion), channel_id=1, replica_groups=mesh['outer'=4,'dp'=2,'cent'=4] {'dp','cent'}, use_global_device_ids=true, to_apply=%region_4.0 | all-reduce | flops 512 | bytes 4096 | tf_op jit(solution)/shard_map/psum | solution.py:22
  59.7 0.3 convert_reduce_fusion
  60.0 3.3 %subtract_divide_fusion = f32[512,1024]{1,0:T(8,128)} fusion(f32[512,1024]{1,0:T(8,128)S(1)} %copy-done, bf16[512,512]{0,1:T(8,128)(2,1)S(1)} %get-tuple-element.6, bf16[512,1024]{1,0:T(8,128)(2,1)} %all-gather.2.cloned.1.call-done, f32[512]{0:T(512)S(1)} %broadcast_add_fusion, f32[512]{0:T(512)S(1)} %get-tuple-element.5), kind=kOutput, calls=%fused_computation | convolution fusion | flops 538443776 | bytes 5771264 | tf_op jit(solution)/shard_map/dot_general | solution.py:36
  63.3 0.0 all-reduce.2.cloned.1.call-update
  63.3 86.7 %all-reduce.2.cloned.1.call-done = f32[512,1024]{1,0:T(8,128)} async-done(((f32[512,1024]{1,0:T(8,128)}), f32[512,1024]{1,0:T(8,128)}) %all-reduce.2.cloned.1.call-update) | async-done | bytes 2097168 | tf_op jit(solution)/shard_map/psum | solution.py:40
  150.0 3.2 %broadcast_multiply_fusion = f32[512,1024]{1,0:T(8,128)} fusion(f32[512,1024]{1,0:T(8,128)} %all-reduce.2.cloned.1.call-done), kind=kLoop, calls=%fused_computation.5 | loop fusion | flops 524288 | bytes 4194304 | tf_op jit(solution)/shard_map/div | solution.py:40
  (2 shorter events, 0.0 us)
Async XLA Ops:
  6.5 2.3 %copy-start = (f32[512,1024]{1,0:T(8,128)S(1)}, f32[512,1024]{1,0:T(8,128)}, u32[]{:S(2)}) copy-start(f32[512,1024]{1,0:T(8,128)} %param.3) | copy-start | bytes 6291460
  6.5 26.4 %all-gather.2.cloned.1.call-start = ((), (), s32[]{:S(2)}) async-start(), calls=%async_computation | async-start | bytes 1572864 | tf_op jit(solution)/shard_map/all_gather | solution.py:30
  8.8 141.2 %all-reduce.2.cloned.1.call-start = ((), (), s32[]{:S(2)}) async-start(), calls=%async_computation.1 | async-start | bytes 4194304 | tf_op jit(solution)/shard_map/psum | solution.py:40
Sparse Core Ops, SparseCore 0:
  8.9 23.9 all-gather.1
  63.4 86.5 all-reduce.1
where the time goes:
time: 160 us
  waiting for transfers between devices  111 us (69%)
  blocking collectives  24.5 us (15%)
  between operations  13.4 us (8%)
  other arithmetic  6.15 us (4%)
  matrix products  5.29 us (3%)
    psum x1, waiting for transfers between devices, shards(): return lax.psum(delta, 'outer') / lax.axis_size('outer')  86.7 us
    all_gather x1, waiting for transfers between devices, shards(): gathered = lax.all_gather(rows_bf, 'dp', axis=0, tiled=True)  23.9 us
    pmax x1, blocking collectives, global_stats(): row_peak = lax.pmax(local_max, ('dp', 'cent'))  12.7 us
    psum x1, blocking collectives, global_stats(): lax.psum(local_sum * jnp.exp(local_max - row_peak), ('dp', 'cent'))  11.8 us
    dot_general x1, matrix products, shards(): lax.dot_general(weights, gathered, (((0,), (0,)), ((), ())), preferred_el...  3.3 us
    div x1, other arithmetic, shards(): return lax.psum(delta, 'outer') / lax.axis_size('outer')  3.22 us
  transfers between devices with their start and end apart: 2, of which 2 were waited for; matrix products, arithmetic and copies ran while one was open for 0% of the time, Pallas kernels for 0%

commit v1 on v0

--- a/solution.py
+++ b/solution.py
@@ -1,3 +1,5 @@
+import itertools
+
 import jax
 import jax.numpy as jnp
 from jax import lax
@@ -23,7 +25,15 @@
     return (row_peak, row_mass)
 
 
-def shards(rows, centroids):
+def gathered_stats(local_max, local_sum):
+    both = lax.all_gather(jnp.stack([local_max, local_sum]), ("dp", "cent"), axis=0)
+    maxes, sums = both[:, 0], both[:, 1]
+    row_peak = jnp.max(maxes, axis=0)
+    row_mass = jnp.sum(sums * jnp.exp(maxes - row_peak[None, :]), axis=0)
+    return (row_peak, row_mass)
+
+
+def shards_pod(rows, centroids):
     rows_bf = rows.astype(jnp.bfloat16)
     cent_bf = centroids.astype(jnp.bfloat16)
     squares = jnp.sum(centroids * centroids, axis=1)
@@ -40,7 +50,89 @@
     return lax.psum(delta, "outer") / lax.axis_size("outer")
 
 
+def gather_all_rows(rows_bf):
+    n_o = lax.axis_size("outer")
+    n_d = lax.axis_size("dp")
+    n_c = lax.axis_size("cent")
+    z = lax.axis_index("outer")
+    y = lax.axis_index("dp")
+    q = lax.axis_index("cent")
+    t, d = rows_bf.shape
+    tq = t // n_c
+    quarter = lax.dynamic_slice_in_dim(rows_bf, q * tq, tq, 0)
+
+    n_od = n_o * n_d
+    me = z * n_d + y
+    slots = [quarter]
+    shifts = [(sz, sy) for sz, sy in itertools.product(range(n_o), range(n_d)) if (sz, sy) != (0, 0)]
+    for sz, sy in shifts:
+        perm = []
+        for i, j in itertools.product(range(n_o), range(n_d)):
+            perm.append((i * n_d + j, ((i + sz) % n_o) * n_d + (j + sy) % n_d))
+        slots.append(lax.ppermute(quarter, ("outer", "dp"), perm))
+    stack_a = jnp.stack(slots)
+    src_of_slot = [(0, 0)] + shifts
+    inv = [0] * n_od
+    for k, (sz, sy) in enumerate(src_of_slot):
+        inv[sz * n_d + sy] = k
+    a = jnp.arange(n_od)
+    rel = ((z - a // n_d) % n_o) * n_d + (y - a % n_d) % n_d
+    stack_a = jnp.take(stack_a, jnp.asarray(inv, jnp.int32)[rel], axis=0)
+
+    bits = []
+    b = 1
+    while b < n_c:
+        bits.append(b)
+        b *= 2
+    cur = stack_a[None]
+    xs = [0]
+    for bit in reversed(bits):
+        other = lax.ppermute(cur, "cent", [(i, i ^ bit) for i in range(n_c)])
+        cur = jnp.concatenate([cur, other], axis=0)
+        xs = xs + [x ^ bit for x in xs]
+    inv_c = [0] * n_c
+    for k, x in enumerate(xs):
+        inv_c[x] = k
+    cidx = jnp.asarray(inv_c, jnp.int32)[q ^ jnp.arange(n_c)]
+    cur = jnp.take(cur, cidx, axis=0)
+    return cur.transpose(1, 0, 2, 3).reshape(n_od * n_c * tq, d)
+
+
+def shards_all(rows, centroids):
+    n_o = lax.axis_size("outer")
+    rows_bf = rows.astype(jnp.bfloat16)
+    cent_bf = centroids.astype(jnp.bfloat16)
+    squares = jnp.sum(centroids * centroids, axis=1)
+    everything = gather_all_rows(rows_bf)
+    logits = scores_for(everything, cent_bf, squares)
+    local_max, local_sum = row_summary(logits)
+    row_peak, row_mass = gathered_stats(local_max, local_sum)
+    weights = (jnp.exp(logits - row_peak[:, None]) / row_mass[:, None]).astype(jnp.bfloat16)
+    n_all, d = everything.shape
+    k = centroids.shape[0]
+    pod = n_all // n_o
+    w_pods = weights.reshape(n_o, pod, k)
+    r_pods = everything.reshape(n_o, pod, d)
+    weight_sum = jnp.sum(w_pods.astype(jnp.float32), axis=1)
+    pull = lax.dot_general(
+        w_pods, r_pods, (((1,), (1,)), ((0,), (0,))), preferred_element_type=jnp.float32
+    )
+    delta = (pull - weight_sum[:, :, None] * centroids[None]) / (weight_sum[:, :, None] + 1.0)
+    return jnp.sum(delta, axis=0) / n_o
+
+
 def solution(mesh):
+    n_o, n_d, n_c = mesh.shape["outer"], mesh.shape["dp"], mesh.shape["cent"]
+
+    def shards(rows, centroids):
+        t, d = rows.shape
+        k = centroids.shape[0]
+        n_all = t * n_o * n_d
+        footprint = n_all * d * 2 + n_all * k * 4 * 2
+        if footprint <= (24 << 20) and t % n_c == 0 and (n_c & (n_c - 1)) == 0:
+            return shards_all(rows, centroids)
+        return shards_pod(rows, centroids)
+
     return jax.shard_map(
         shards,
         mesh=mesh,

time: 160 us -> 99.4 us (0.62)
  waiting for transfers between devices: 111 us -> 39.7 us
  starting transfers between devices: 0.04 us -> 18.7 us
  blocking collectives: 24.5 us -> 9.23 us
  between operations: 13.4 us -> 0.19 us
  local copies, waits for them, and re-layouts: 0.01 us -> 9.49 us
  other arithmetic: 6.15 us -> 14.1 us
  matrix products: 5.29 us -> 6.93 us
    psum x1 -> x0, waiting for transfers between devices: 86.7 us -> none  [shards(): return lax.psum(delta, 'outer') / lax.axis_size('outer')]
    ppermute x0 -> x9, waiting for transfers between devices: none -> 39.7 us  [the longest x2 25.1 us: gather_all_rows(): other = lax.ppermute(cur, 'cent', [(i, i ^ bit) for i in range(n_c)])]
    all_gather x1 -> x0, waiting for transfers between devices: 23.9 us -> none  [shards(): gathered = lax.all_gather(rows_bf, 'dp', axis=0, tiled=True)]
    ppermute x0 -> x9, starting transfers between devices: none -> 18.7 us  [the longest x7 17.1 us: gather_all_rows(): slots.append(lax.ppermute(quarter, ('outer', 'dp'), perm))]
    pmax x1 -> x0, blocking collectives: 12.7 us -> none  [global_stats(): row_peak = lax.pmax(local_max, ('dp', 'cent'))]
    psum x1 -> x0, blocking collectives: 11.8 us -> none  [global_stats(): lax.psum(local_sum * jnp.exp(local_max - row_peak), ('dp', 'cent'))]
    all_gather x0 -> x1, blocking collectives: none -> 9.23 us  [gathered_stats(): lax.all_gather(jnp.stack([local_max, local_sum]), ('dp', 'cent'), axis=0)]
    gather x0 -> x4, local copies, waits for them, and re-layouts: none -> 6.87 us  [the longest x1 4.97 us: gather_all_rows(): cur = jnp.take(cur, cidx, axis=0)]
  transfers between devices with their start and end apart: 2 -> 9, of which waited for: 2 -> 6; matrix products, arithmetic and copies ran while one was open for 0% -> 3% of each run, Pallas kernels for 0% -> 0%
where the time goes in v1:
time: 99.4 us; the launch traced here: 98.4 us
  waiting for transfers between devices  39.7 us (40%)
  starting transfers between devices  18.7 us (19%)
  other arithmetic  14.1 us (14%)
  local copies, waits for them, and re-layouts  9.49 us (10%)
  blocking collectives  9.23 us (9%)
  matrix products  6.93 us (7%)
    ppermute x2, waiting for transfers between devices, gather_all_rows(): other = lax.ppermute(cur, 'cent', [(i, i ^ bit) for i in range(n_c)])  25.1 us
    ppermute x7, starting transfers between devices, gather_all_rows(): slots.append(lax.ppermute(quarter, ('outer', 'dp'), perm))  17.1 us
    ppermute x7, waiting for transfers between devices, gather_all_rows(): slots.append(lax.ppermute(quarter, ('outer', 'dp'), perm))  14.6 us
    all_gather x1, blocking collectives, gathered_stats(): lax.all_gather(jnp.stack([local_max, local_sum]), ('dp', 'cent'), axis=0)  9.23 us
    gather x1, local copies, waits for them, and re-layouts, gather_all_rows(): cur = jnp.take(cur, cidx, axis=0)  4.97 us
    concatenate x2, other arithmetic, gather_all_rows(): cur = jnp.concatenate([cur, other], axis=0)  4.89 us
    dot_general x1, matrix products, shards_all(): lax.dot_general(w_pods, r_pods, (((1,), (1,)), ((0,), (0,))), preferred_e...  4.07 us
    dot_general x1, matrix products, scores_for(): lax.dot_general(piece, cent_bf, (((1,), (1,)), ((), ())), preferred_eleme...  2.85 us
  transfers between devices with their start and end apart: 9, of which 6 were waited for; matrix products, arithmetic and copies ran while one was open for 3% of the time, Pallas kernels for 0%

profile of v1, /device:TPU:0, one launch (start us, length us, event | category | flops | bytes accessed | tf_op | source)
XLA Modules:
  0.0 98.4 jit_solution(709243374130906620)
XLA Ops:
  0.0 1.0 bitcast_dynamic-update-slice_fusion.7
  1.0 5.1 %collective-permute-start.4 = (bf16[64,1024]{1,0:T(8,128)(2,1)S(1)}, bf16[64,1024]{1,0:T(8,128)(2,1)S(1)}, u32[]{:S(2)}, u32[]{:S(2)}) collective-permute-start(bf16[64,1024]{1,0:T(8,128)(2,1)S(1)} %get-tuple-element.8), channel_id=1, source_target_pairs={{0,20},{4,16},{8,28},{12,24},{16,4},{20,0},{24,12},{28,8},{1,21},{... | collective-permute-start | bytes 393224 | tf_op jit(solution)/shard_map/ppermute | solution.py:72
  6.0 0.3 collective-permute-start.3
  6.4 1.5 %collective-permute-start.2 = (bf16[64,1024]{1,0:T(8,128)(2,1)S(1)}, bf16[64,1024]{1,0:T(8,128)(2,1)S(1)}, u32[]{:S(2)}, u32[]{:S(2)}) collective-permute-start(bf16[64,1024]{1,0:T(8,128)(2,1)S(1)} %get-tuple-element.8), channel_id=1, source_target_pairs={{0,12},{4,8},{8,20},{12,16},{16,28},{20,24},{24,4},{28,0},{1,13},{... | collective-permute-start | bytes 393224 | tf_op jit(solution)/shard_map/ppermute | solution.py:72
  7.9 1.6 %collective-permute-start.1 = (bf16[64,1024]{1,0:T(8,128)(2,1)S(1)}, bf16[64,1024]{1,0:T(8,128)(2,1)S(1)}, u32[]{:S(2)}, u32[]{:S(2)}) collective-permute-start(bf16[64,1024]{1,0:T(8,128)(2,1)S(1)} %get-tuple-element.8), channel_id=1, source_target_pairs={{0,8},{4,12},{8,16},{12,20},{16,24},{20,28},{24,0},{28,4},{1,9},{5... | collective-permute-start | bytes 393224 | tf_op jit(solution)/shard_map/ppermute | solution.py:72
  9.5 1.5 %collective-permute-start = (bf16[64,1024]{1,0:T(8,128)(2,1)S(1)}, bf16[64,1024]{1,0:T(8,128)(2,1)S(1)}, u32[]{:S(2)}, u32[]{:S(2)}) collective-permute-start(bf16[64,1024]{1,0:T(8,128)(2,1)S(1)} %get-tuple-element.8), channel_id=1, source_target_pairs={{0,4},{4,0},{8,12},{12,8},{16,20},{20,16},{24,28},{28,24},{1,5},{5... | collective-permute-start | bytes 393224 | tf_op jit(solution)/shard_map/ppermute | solution.py:72
  11.0 0.6 gather_fusion.1
  11.7 5.0 %collective-permute-done = bf16[64,1024]{1,0:T(8,128)(2,1)S(1)} collective-permute-done((bf16[64,1024]{1,0:T(8,128)(2,1)S(1)}, bf16[64,1024]{1,0:T(8,128)(2,1)S(1)}, u32[]{:S(2)}, u32[]{:S(2)}) %collective-permute-start) | collective-permute-done | bytes 131104 | tf_op jit(solution)/shard_map/ppermute | solution.py:72
  16.7 3.7 %collective-permute-start.5 = (bf16[64,1024]{1,0:T(8,128)(2,1)S(1)}, bf16[64,1024]{1,0:T(8,128)(2,1)S(1)}, u32[]{:S(2)}, u32[]{:S(2)}) collective-permute-start(bf16[64,1024]{1,0:T(8,128)(2,1)S(1)} %get-tuple-element.8), channel_id=1, source_target_pairs={{0,24},{4,28},{8,0},{12,4},{16,8},{20,12},{24,16},{28,20},{1,25},{... | collective-permute-start | bytes 393224 | tf_op jit(solution)/shard_map/ppermute | solution.py:72
  20.4 0.0 collective-permute-done.1
  20.4 3.4 %collective-permute-start.6 = (bf16[64,1024]{1,0:T(8,128)(2,1)S(1)}, bf16[64,1024]{1,0:T(8,128)(2,1)S(1)}, u32[]{:S(2)}, u32[]{:S(2)}) collective-permute-start(bf16[64,1024]{1,0:T(8,128)(2,1)S(1)} %get-tuple-element.8), channel_id=1, source_target_pairs={{0,28},{4,24},{8,4},{12,0},{16,12},{20,8},{24,20},{28,16},{1,29},{... | collective-permute-start | bytes 393224 | tf_op jit(solution)/shard_map/ppermute | solution.py:72
  23.9 0.0 collective-permute-done.2
  23.9 0.9 collective-permute-done.3
  24.8 0.0 collective-permute-done.4
  24.9 1.6 %collective-permute-done.5 = bf16[64,1024]{1,0:T(8,128)(2,1)S(1)} collective-permute-done((bf16[64,1024]{1,0:T(8,128)(2,1)S(1)}, bf16[64,1024]{1,0:T(8,128)(2,1)S(1)}, u32[]{:S(2)}, u32[]{:S(2)}) %collective-permute-start.5) | collective-permute-done | bytes 131104 | tf_op jit(solution)/shard_map/ppermute | solution.py:72
  26.5 7.1 %collective-permute-done.6 = bf16[64,1024]{1,0:T(8,128)(2,1)S(1)} collective-permute-done((bf16[64,1024]{1,0:T(8,128)(2,1)S(1)}, bf16[64,1024]{1,0:T(8,128)(2,1)S(1)}, u32[]{:S(2)}, u32[]{:S(2)}) %collective-permute-start.6) | collective-permute-done | bytes 131104 | tf_op jit(solution)/shard_map/ppermute | solution.py:72
  33.6 0.0 copy-start
  33.6 0.6 gather_fusion.2
  34.2 0.2 bitcast_select_fusion
  34.4 1.6 %collective-permute-start.7 = (bf16[1,8,64,1024]{3,2,1,0:T(8,128)(2,1)S(1)}, bf16[1,8,64,1024]{3,2,1,0:T(8,128)(2,1)S(1)}, u32[]{:S(2)}, u32[]{:S(2)}) collective-permute-start(bf16[1,8,64,1024]{3,2,1,0:T(8,128)(2,1)S(1)} %bitcast_select_fusion), channel_id=1, source_target_pairs={{0,2},{1,3},{2,0},{3,1},{4,6},{5,7},{6,4},{7,5},{8,10},{9,11},{10,... | collective-permute-start | bytes 3145736 | tf_op jit(solution)/shard_map/ppermute | solution.py:90
  36.0 23.1 %collective-permute-done.7 = bf16[1,8,64,1024]{3,2,1,0:T(8,128)(2,1)S(1)} collective-permute-done((bf16[1,8,64,1024]{3,2,1,0:T(8,128)(2,1)S(1)}, bf16[1,8,64,1024]{3,2,1,0:T(8,128)(2,1)S(1)}, u32[]{:S(2)}, u32[]{:S(2)}) %collective-permute-start.7) | collective-permute-done | bytes 1048608 | tf_op jit(solution)/shard_map/ppermute | solution.py:90
  59.0 1.5 %pad_maximum_fusion.1 = bf16[2,8,64,1024]{3,2,1,0:T(8,128)(2,1)} fusion(bf16[1,8,64,1024]{3,2,1,0:T(8,128)(2,1)S(1)} %collective-permute-done.7, bf16[1,8,64,1024]{3,2,1,0:T(8,128)(2,1)S(1)} %bitcast_select_fusion), kind=kLoop, calls=%fused_computation.11 | loop fusion | flops 1048576 | bytes 4194304 | tf_op jit(solution)/shard_map/concatenate | solution.py:91
  60.5 0.0 collective-permute-start.8
  60.5 0.0 copy-done
  60.5 0.6 gather_fusion
  61.2 1.8 %multiply_reduce_fusion = f32[512]{0:T(512)S(1)} fusion(f32[512,1024]{1,0:T(8,128)} %param.5), kind=kLoop, calls=%fused_computation.12 | loop fusion | flops 1048064 | bytes 2099200 | tf_op jit(solution)/shard_map/reduce_sum | solution.py:105
  63.0 2.0 %collective-permute-done.8 = bf16[2,8,64,1024]{3,2,1,0:T(8,128)(2,1)} collective-permute-done((bf16[2,8,64,1024]{3,2,1,0:T(8,128)(2,1)}, bf16[2,8,64,1024]{3,2,1,0:T(8,128)(2,1)}, u32[]{:S(2)}, u32[]{:S(2)}) %collective-permute-start.8) | collective-permute-done | bytes 2097184 | tf_op jit(solution)/shard_map/ppermute | solution.py:90
  65.0 3.4 %pad_maximum_fusion = bf16[4,8,64,1024]{3,2,1,0:T(8,128)(2,1)} fusion(bf16[2,8,64,1024]{3,2,1,0:T(8,128)(2,1)} %collective-permute-done.8, bf16[1,8,64,1024]{3,2,1,0:T(8,128)(2,1)S(1)} %collective-permute-done.7, bf16[1,8,64,1024]{3,2,1,0:T(8,128)(2,1)S(1)} %bitcast_select_fusion), kind=kLoop, calls=%fused_computation.5 | loop fusion | flops 4194304 | bytes 8388608 | tf_op jit(solution)/shard_map/concatenate | solution.py:91
  68.4 5.0 %gather_fusion.3 = bf16[4,8,64,1024]{3,2,1,0:T(8,128)(2,1)} fusion(bf16[4,8,64,1024]{3,2,1,0:T(8,128)(2,1)} %pad_maximum_fusion, s32[1024]{0:T(1024)S(1)} %pad_clamp_fusion), kind=kCustom, calls=%fused_computation.3 | custom fusion | bytes 8388624 | tf_op jit(solution)/shard_map/jit(_take)/gather | solution.py:97
  73.4 2.7 %select_bitcast_fusion = bf16[8,4,64,1024]{3,2,0,1:T(8,128)(2,1)S(1)} fusion(bf16[4,8,64,1024]{3,2,1,0:T(8,128)(2,1)} %gather_fusion.3, pred[4]{0:T(512)(128)(4,1)S(1)} %compare_and_fusion.1), kind=kLoop, calls=%fused_computation.10 | loop fusion | flops 2097152 | bytes 8388612 | tf_op jit(solution)/shard_map/jit(_take)/select_n | solution.py:97
  76.0 0.0 copy-start.1
  76.1 0.5 copy.13
  76.6 1.1 %copy-done.1 = f32[512,1024]{1,0:T(8,128)S(1)} copy-done((f32[512,1024]{1,0:T(8,128)S(1)}, f32[512,1024]{1,0:T(8,128)}, u32[]{:S(2)}) %copy-start.1) | copy-done | bytes 2097176
  77.6 2.9 %fusion.14 = (f32[2048]{0:T(1024)S(1)}, f32[2048,512]{1,0:T(8,128)S(1)}) fusion(f32[512]{0:T(512)S(1)} %multiply_reduce_fusion, bf16[2048,1024]{1,0:T(8,128)(2,1)S(1)} %bitcast.55, f32[512,1024]{1,0:T(8,128)S(1)} %copy-done.1), kind=kOutput, calls=%fused_computation.66 | convolution fusion | flops 2152200192 | bytes 10496000 | tf_op jit(solution)/shard_map/dot_general | solution.py:10
  80.5 1.7 %exponential_reduce_fusion = f32[2048]{0:T(1024)S(1)} fusion(f32[2048,512]{1,0:T(8,128)S(1)} %get-tuple-element.13, f32[2048]{0:T(1024)S(1)} %get-tuple-element.12), kind=kLoop, calls=%fused_computation.8 | loop fusion | flops 2095104 | bytes 4210688 | tf_op jit(solution)/shard_map/reduce_sum | solution.py:18
  82.2 9.2 %all-gather.1 = f32[8,2,2048]{2,1,0:T(2,128)S(1)} all-gather(f32[1,2,2048]{2,1,0:T(2,128)S(1)} %maximum_bitcast_fusion), channel_id=2, replica_groups=mesh['outer'=4,'dp'=2,'cent'=4] {'dp','cent'}, dimensions={0}, use_global_device_ids=true | all-gather | bytes 147456 | tf_op jit(solution)/shard_map/all_gather | solution.py:29
  91.5 0.1 slice_reduce_fusion
  91.6 0.1 fusion.2
  91.6 1.0 %convert_reduce_fusion = (f32[4,512]{1,0:T(4,128)S(1)}, bf16[2048,512]{1,0:T(8,128)(2,1)S(1)}) fusion(f32[2048]{0:T(1024)S(1)} %fusion.2, f32[2048,512]{1,0:T(8,128)S(1)} %get-tuple-element.13, f32[2048]{0:T(1024)S(1)} %get-tuple-element.9), kind=kLoop, calls=%fused_computation.6 | loop fusion | flops 5240832 | bytes 6316032 | tf_op jit(solution)/shard_map/reduce_sum | solution.py:116
  92.7 4.1 %divide_reduce_fusion = f32[512,1024]{1,0:T(8,128)S(1)} fusion(f32[4,512]{1,0:T(4,128)S(1)} %broadcast_add_fusion, f32[512,1024]{1,0:T(8,128)S(1)} %copy-done.1, f32[4,512]{1,0:T(4,128)S(1)} %get-tuple-element.5, bf16[4,512,512]{2,1,0:T(8,128)(2,1)S(1)} %bitcast.57, bf16[4,512,1024]{2,1,0:T(8,128)(2,1)S(1)} %bitcast.56), kind=kOutput, calls=%fused_computation.4 | convolution fusion | flops 2155347968 | bytes 10502144 | tf_op jit(solution)/shard_map/dot_general | solution.py:117
  96.8 1.6 %broadcast_multiply_fusion = f32[512,1024]{1,0:T(8,128)} fusion(f32[512,1024]{1,0:T(8,128)S(1)} %divide_reduce_fusion), kind=kLoop, calls=%fused_computation.14 | loop fusion | flops 524288 | bytes 4194304 | tf_op jit(solution)/shard_map/div | solution.py:121
  (19 shorter events, 0.2 us)
Async XLA Ops:
  1.0 23.9 %collective-permute-start.4 = (bf16[64,1024]{1,0:T(8,128)(2,1)S(1)}, bf16[64,1024]{1,0:T(8,128)(2,1)S(1)}, u32[]{:S(2)}, u32[]{:S(2)}) collective-permute-start(bf16[64,1024]{1,0:T(8,128)(2,1)S(1)} %get-tuple-element.8), channel_id=1, source_target_pairs={{0,20},{4,16},{8,28},{12,24},{16,4},{20,0},{24,12},{28,8},{1,21},{... | collective-permute-start | bytes 393224 | tf_op jit(solution)/shard_map/ppermute | solution.py:72
  6.0 18.8 %collective-permute-start.3 = (bf16[64,1024]{1,0:T(8,128)(2,1)S(1)}, bf16[64,1024]{1,0:T(8,128)(2,1)S(1)}, u32[]{:S(2)}, u32[]{:S(2)}) collective-permute-start(bf16[64,1024]{1,0:T(8,128)(2,1)S(1)} %get-tuple-element.8), channel_id=1, source_target_pairs={{0,16},{4,20},{8,24},{12,28},{16,0},{20,4},{24,8},{28,12},{1,17},{... | collective-permute-start | bytes 393224 | tf_op jit(solution)/shard_map/ppermute | solution.py:72
  6.4 17.5 %collective-permute-start.2 = (bf16[64,1024]{1,0:T(8,128)(2,1)S(1)}, bf16[64,1024]{1,0:T(8,128)(2,1)S(1)}, u32[]{:S(2)}, u32[]{:S(2)}) collective-permute-start(bf16[64,1024]{1,0:T(8,128)(2,1)S(1)} %get-tuple-element.8), channel_id=1, source_target_pairs={{0,12},{4,8},{8,20},{12,16},{16,28},{20,24},{24,4},{28,0},{1,13},{... | collective-permute-start | bytes 393224 | tf_op jit(solution)/shard_map/ppermute | solution.py:72
  7.9 12.5 %collective-permute-start.1 = (bf16[64,1024]{1,0:T(8,128)(2,1)S(1)}, bf16[64,1024]{1,0:T(8,128)(2,1)S(1)}, u32[]{:S(2)}, u32[]{:S(2)}) collective-permute-start(bf16[64,1024]{1,0:T(8,128)(2,1)S(1)} %get-tuple-element.8), channel_id=1, source_target_pairs={{0,8},{4,12},{8,16},{12,20},{16,24},{20,28},{24,0},{28,4},{1,9},{5... | collective-permute-start | bytes 393224 | tf_op jit(solution)/shard_map/ppermute | solution.py:72
  9.5 7.3 %collective-permute-start = (bf16[64,1024]{1,0:T(8,128)(2,1)S(1)}, bf16[64,1024]{1,0:T(8,128)(2,1)S(1)}, u32[]{:S(2)}, u32[]{:S(2)}) collective-permute-start(bf16[64,1024]{1,0:T(8,128)(2,1)S(1)} %get-tuple-element.8), channel_id=1, source_target_pairs={{0,4},{4,0},{8,12},{12,8},{16,20},{20,16},{24,28},{28,24},{1,5},{5... | collective-permute-start | bytes 393224 | tf_op jit(solution)/shard_map/ppermute | solution.py:72
  16.7 9.7 %collective-permute-start.5 = (bf16[64,1024]{1,0:T(8,128)(2,1)S(1)}, bf16[64,1024]{1,0:T(8,128)(2,1)S(1)}, u32[]{:S(2)}, u32[]{:S(2)}) collective-permute-start(bf16[64,1024]{1,0:T(8,128)(2,1)S(1)} %get-tuple-element.8), channel_id=1, source_target_pairs={{0,24},{4,28},{8,0},{12,4},{16,8},{20,12},{24,16},{28,20},{1,25},{... | collective-permute-start | bytes 393224 | tf_op jit(solution)/shard_map/ppermute | solution.py:72
  20.4 13.1 %collective-permute-start.6 = (bf16[64,1024]{1,0:T(8,128)(2,1)S(1)}, bf16[64,1024]{1,0:T(8,128)(2,1)S(1)}, u32[]{:S(2)}, u32[]{:S(2)}) collective-permute-start(bf16[64,1024]{1,0:T(8,128)(2,1)S(1)} %get-tuple-element.8), channel_id=1, source_target_pairs={{0,28},{4,24},{8,4},{12,0},{16,12},{20,8},{24,20},{28,16},{1,29},{... | collective-permute-start | bytes 393224 | tf_op jit(solution)/shard_map/ppermute | solution.py:72
  33.6 26.9 %copy-start = (s32[4]{0:T(128)S(1)}, s32[4]{0:T(128)}, u32[]{:S(2)}) copy-start(s32[4]{0:T(128)} %constant.111.clone) | copy-start | bytes 52
  34.4 24.6 %collective-permute-start.7 = (bf16[1,8,64,1024]{3,2,1,0:T(8,128)(2,1)S(1)}, bf16[1,8,64,1024]{3,2,1,0:T(8,128)(2,1)S(1)}, u32[]{:S(2)}, u32[]{:S(2)}) collective-permute-start(bf16[1,8,64,1024]{3,2,1,0:T(8,128)(2,1)S(1)} %bitcast_select_fusion), channel_id=1, source_target_pairs={{0,2},{1,3},{2,0},{3,1},{4,6},{5,7},{6,4},{7,5},{8,10},{9,11},{10,... | collective-permute-start | bytes 3145736 | tf_op jit(solution)/shard_map/ppermute | solution.py:90
  60.5 4.5 %collective-permute-start.8 = (bf16[2,8,64,1024]{3,2,1,0:T(8,128)(2,1)}, bf16[2,8,64,1024]{3,2,1,0:T(8,128)(2,1)}, u32[]{:S(2)}, u32[]{:S(2)}) collective-permute-start(bf16[2,8,64,1024]{3,2,1,0:T(8,128)(2,1)} %pad_maximum_fusion.1), channel_id=1, source_target_pairs={{0,1},{1,0},{2,3},{3,2},{4,5},{5,4},{6,7},{7,6},{8,9},{9,8},{10,11... | collective-permute-start | bytes 6291464 | tf_op jit(solution)/shard_map/ppermute | solution.py:90
  76.0 1.6 %copy-start.1 = (f32[512,1024]{1,0:T(8,128)S(1)}, f32[512,1024]{1,0:T(8,128)}, u32[]{:S(2)}) copy-start(f32[512,1024]{1,0:T(8,128)} %param.5) | copy-start | bytes 6291460

commit v2 on v0

--- a/solution.py
+++ b/solution.py
@@ -1,3 +1,5 @@
+import itertools
+
 import jax
 import jax.numpy as jnp
 from jax import lax
@@ -23,7 +25,7 @@
     return (row_peak, row_mass)
 
 
-def shards(rows, centroids):
+def shards_pod(rows, centroids):
     rows_bf = rows.astype(jnp.bfloat16)
     cent_bf = centroids.astype(jnp.bfloat16)
     squares = jnp.sum(centroids * centroids, axis=1)
@@ -40,7 +42,116 @@
     return lax.psum(delta, "outer") / lax.axis_size("outer")
 
 
+def shards_all(rows, centroids):
+    n_o = lax.axis_size("outer")
+    n_d = lax.axis_size("dp")
+    n_c = lax.axis_size("cent")
+    z = lax.axis_index("outer")
+    y = lax.axis_index("dp")
+    q = lax.axis_index("cent")
+    t, d = rows.shape
+    tq = t // n_c
+    n_od = n_o * n_d
+
+    rows_bf = rows.astype(jnp.bfloat16)
+    cent_bf = centroids.astype(jnp.bfloat16)
+    squares = jnp.sum(centroids * centroids, axis=1)
+
+    bits = []
+    b = 1
+    while b < n_c:
+        bits.append(b)
+        b *= 2
+    xs = [0]
+    for bit in reversed(bits):
+        xs = xs + [x ^ bit for x in xs]
+
+    def quarter_of(x):
+        return lax.dynamic_slice_in_dim(rows_bf, (q ^ x) * tq, tq, 0)
+
+    own = jnp.concatenate([quarter_of(x) for x in xs], axis=0)
+    mine = quarter_of(0)
+
+    def spread(piece):
+        cur = piece
+        for bit in reversed(bits):
+            other = lax.ppermute(cur, "cent", [(i, i ^ bit) for i in range(n_c)])
+            cur = jnp.concatenate([cur, other], axis=0)
+        return cur
+
+    shifts = list(itertools.product(range(n_o), range(n_d)))
+    blocks = []
+    for sz, sy in shifts:
+        if (sz, sy) == (0, 0):
+            blocks.append(own)
+            continue
+        perm = []
+        for i, j in itertools.product(range(n_o), range(n_d)):
+            perm.append((i * n_d + j, ((i + sz) % n_o) * n_d + (j + sy) % n_d))
+        blocks.append(spread(lax.ppermute(mine, ("outer", "dp"), perm)))
+
+    logits = [scores_for(blk, cent_bf, squares) for blk in blocks]
+    summaries = [row_summary(lg) for lg in logits]
+    local_max = jnp.concatenate([s[0] for s in summaries])
+    local_sum = jnp.concatenate([s[1] for s in summaries])
+
+    k_idx = jnp.arange(n_od * n_c * tq) // (n_c * tq)
+    j_idx = (jnp.arange(n_od * n_c * tq) // tq) % n_c
+    r_idx = jnp.arange(n_od * n_c * tq) % tq
+    sz_of = jnp.asarray([s[0] for s in shifts], jnp.int32)[k_idx]
+    sy_of = jnp.asarray([s[1] for s in shifts], jnp.int32)[k_idx]
+    x_of = jnp.asarray(xs, jnp.int32)[j_idx]
+    src = ((z - sz_of) % n_o) * n_d + (y - sy_of) % n_d
+    absolute = (src * n_c + (q ^ x_of)) * tq + r_idx
+    order = jnp.zeros_like(absolute).at[absolute].set(jnp.arange(absolute.shape[0]))
+
+    both = jnp.stack([local_max, local_sum])[:, order]
+    every = lax.all_gather(both, ("dp", "cent"), axis=0)
+    maxes, sums = every[:, 0], every[:, 1]
+    peak_abs = jnp.max(maxes, axis=0)
+    mass_abs = jnp.sum(sums * jnp.exp(maxes - peak_abs[None, :]), axis=0)
+    row_peak = peak_abs[absolute]
+    row_mass = mass_abs[absolute]
+
+    blk = n_c * tq
+    weight_sum = [None] * n_o
+    pull = [None] * n_o
+    for k, (sz, sy) in enumerate(shifts):
+        pk = row_peak[k * blk:(k + 1) * blk]
+        mk = row_mass[k * blk:(k + 1) * blk]
+        w = (jnp.exp(logits[k] - pk[:, None]) / mk[:, None]).astype(jnp.bfloat16)
+        ws = jnp.sum(w.astype(jnp.float32), axis=0)
+        pl = lax.dot_general(
+            w, blocks[k], (((0,), (0,)), ((), ())), preferred_element_type=jnp.float32
+        )
+        weight_sum[sz] = ws if weight_sum[sz] is None else weight_sum[sz] + ws
+        pull[sz] = pl if pull[sz] is None else pull[sz] + pl
+
+    total = None
+    for a in range(n_o):
+        rel = (z - a) % n_o
+        pick_pull = pull[0]
+        pick_ws = weight_sum[0]
+        for s in range(1, n_o):
+            pick_pull = jnp.where(rel == s, pull[s], pick_pull)
+            pick_ws = jnp.where(rel == s, weight_sum[s], pick_ws)
+        delta = (pick_pull - pick_ws[:, None] * centroids) / (pick_ws[:, None] + 1.0)
+        total = delta if total is None else total + delta
+    return total / n_o
+
+
 def solution(mesh):
+    n_o, n_d, n_c = mesh.shape["outer"], mesh.shape["dp"], mesh.shape["cent"]
+
+    def shards(rows, centroids):
+        t, d = rows.shape
+        k = centroids.shape[0]
+        n_all = t * n_o * n_d
+        footprint = n_all * d * 2 + n_all * k * 4 * 2
+        if footprint <= (24 << 20) and t % n_c == 0 and (n_c & (n_c - 1)) == 0:
+            return shards_all(rows, centroids)
+        return shards_pod(rows, centroids)
+
     return jax.shard_map(
         shards,
         mesh=mesh,

time: 160 us -> 126 us (0.79)
  waiting for transfers between devices: 111 us -> 11.3 us
  local copies, waits for them, and re-layouts: 0.01 us -> 59 us
  starting transfers between devices: 0.04 us -> 22 us
  blocking collectives: 24.5 us -> 9.39 us
  between operations: 13.4 us -> 0.69 us
  matrix products: 5.29 us -> 14.2 us
  other arithmetic: 6.15 us -> 8.98 us
    psum x1 -> x0, waiting for transfers between devices: 86.7 us -> none  [shards(): return lax.psum(delta, 'outer') / lax.axis_size('outer')]
    gather x0 -> x3, local copies, waits for them, and re-layouts: none -> 32.4 us  [the longest x1 11.8 us: shards_all(): row_mass = mass_abs[absolute]]
    all_gather x1 -> x0, waiting for transfers between devices: 23.9 us -> none  [shards(): gathered = lax.all_gather(rows_bf, 'dp', axis=0, tiled=True)]
    ppermute x0 -> x21, starting transfers between devices: none -> 22 us  [the longest x7 12.5 us: shards_all(): blocks.append(spread(lax.ppermute(mine, ('outer', 'dp'), perm)))]
    unnamed x2 -> x75, local copies, waits for them, and re-layouts: 0.01 us -> 15.1 us
    pmax x1 -> x0, blocking collectives: 12.7 us -> none  [global_stats(): row_peak = lax.pmax(local_max, ('dp', 'cent'))]
    psum x1 -> x0, blocking collectives: 11.8 us -> none  [global_stats(): lax.psum(local_sum * jnp.exp(local_max - row_peak), ('dp', 'cent'))]
    ppermute x0 -> x21, waiting for transfers between devices: none -> 11.3 us  [the longest x14 10.4 us: spread(): other = lax.ppermute(cur, 'cent', [(i, i ^ bit) for i in range(n_c)])]
  transfers between devices with their start and end apart: 2 -> 21, of which waited for: 2 -> 7; matrix products, arithmetic and copies ran while one was open for 0% -> 15% of each run, Pallas kernels for 0% -> 0%
where the time goes in v2:
time: 126 us
  local copies, waits for them, and re-layouts  59 us (47%)
  starting transfers between devices  22 us (17%)
  matrix products  14.2 us (11%)
  waiting for transfers between devices  11.3 us (9%)
  blocking collectives  9.39 us (7%)
  other arithmetic  8.98 us (7%)
    unnamed x75, local copies, waits for them, and re-layouts  15.1 us
    ppermute x7, starting transfers between devices, shards_all(): blocks.append(spread(lax.ppermute(mine, ('outer', 'dp'), perm)))  12.5 us
    gather x1, local copies, waits for them, and re-layouts, shards_all(): row_mass = mass_abs[absolute]  11.8 us
    gather x1, local copies, waits for them, and re-layouts, shards_all(): row_peak = peak_abs[absolute]  11.8 us
    ppermute x14, waiting for transfers between devices, spread(): other = lax.ppermute(cur, 'cent', [(i, i ^ bit) for i in range(n_c)])  10.4 us
    ppermute x14, starting transfers between devices, spread(): other = lax.ppermute(cur, 'cent', [(i, i ^ bit) for i in range(n_c)])  9.51 us
    all_gather x1, blocking collectives, shards_all(): every = lax.all_gather(both, ('dp', 'cent'), axis=0)  9.39 us
    gather x1, local copies, waits for them, and re-layouts, shards_all(): both = jnp.stack([local_max, local_sum])[:, order]  8.8 us
  transfers between devices with their start and end apart: 21, of which 7 were waited for; matrix products, arithmetic and copies ran while one was open for 15% of the time, Pallas kernels for 0%

profile of v2, /device:TPU:0, one launch (start us, length us, event | category | flops | bytes accessed | tf_op | source)
XLA Modules:
  0.0 125.5 jit_solution(12343985815201423937)
XLA Ops:
  0.0 1.4 %convert_element_type.54 = bf16[256,1024]{1,0:T(8,128)(2,1)S(1)} convert(f32[256,1024]{1,0:T(8,128)} %param.5) | non-fusion elementwise | flops 262144 | bytes 1572864 | tf_op jit(solution)/shard_map/convert_element_type | solution.py:56
  1.5 0.8 constant_dynamic-slice_fusion.3
  2.2 3.0 %collective-permute-start.3 = (bf16[64,1024]{1,0:T(8,128)(2,1)S(1)}, bf16[64,1024]{1,0:T(8,128)(2,1)S(1)}, u32[]{:S(2)}, u32[]{:S(2)}) collective-permute-start(bf16[64,1024]{1,0:T(8,128)(2,1)S(1)} %get-tuple-element.35), channel_id=1, source_target_pairs={{0,4},{4,0},{8,12},{12,8},{16,20},{20,16},{24,28},{28,24},{1,5},{5... | collective-permute-start | bytes 393224 | tf_op jit(solution)/shard_map/ppermute | solution.py:91
  5.2 1.6 %collective-permute-start.6 = (bf16[64,1024]{1,0:T(8,128)(2,1)S(1)}, bf16[64,1024]{1,0:T(8,128)(2,1)S(1)}, u32[]{:S(2)}, u32[]{:S(2)}) collective-permute-start(bf16[64,1024]{1,0:T(8,128)(2,1)S(1)} %get-tuple-element.35), channel_id=1, source_target_pairs={{0,8},{4,12},{8,16},{12,20},{16,24},{20,28},{24,0},{28,4},{1,9},{5... | collective-permute-start | bytes 393224 | tf_op jit(solution)/shard_map/ppermute | solution.py:91
  6.8 1.5 %collective-permute-start.9 = (bf16[64,1024]{1,0:T(8,128)(2,1)S(1)}, bf16[64,1024]{1,0:T(8,128)(2,1)S(1)}, u32[]{:S(2)}, u32[]{:S(2)}) collective-permute-start(bf16[64,1024]{1,0:T(8,128)(2,1)S(1)} %get-tuple-element.35), channel_id=1, source_target_pairs={{0,12},{4,8},{8,20},{12,16},{16,28},{20,24},{24,4},{28,0},{1,13},{... | collective-permute-start | bytes 393224 | tf_op jit(solution)/shard_map/ppermute | solution.py:91
  8.3 1.1 collective-permute-start.12
  9.4 2.8 %collective-permute-start.15 = (bf16[64,1024]{1,0:T(8,128)(2,1)S(1)}, bf16[64,1024]{1,0:T(8,128)(2,1)S(1)}, u32[]{:S(2)}, u32[]{:S(2)}) collective-permute-start(bf16[64,1024]{1,0:T(8,128)(2,1)S(1)} %get-tuple-element.35), channel_id=1, source_target_pairs={{0,20},{4,16},{8,28},{12,24},{16,4},{20,0},{24,12},{28,8},{1,21},{... | collective-permute-start | bytes 393224 | tf_op jit(solution)/shard_map/ppermute | solution.py:91
  12.3 1.8 %multiply_reduce_fusion = (f32[512]{0:T(512)}, bf16[512,1024]{1,0:T(8,128)(2,1)}) fusion(f32[512,1024]{1,0:T(8,128)S(1)} %copy-done.4), kind=kLoop, calls=%fused_computation.5 | loop fusion | flops 1572352 | bytes 3147776 | tf_op jit(solution)/shard_map/reduce_sum | solution.py:58
  14.2 8.0 %scatter_custom_fusion = s32[2048]{0:T(1024)S(1)} fusion(s32[2048]{0:T(1024)S(1)} %bitcast.56, s32[2048]{0:T(1024)S(1)} %iota.22, s32[]{:T(128)} %constant.112.clone.1), kind=kCustom, calls=%fused_computation.156 | custom fusion | bytes 8196 | tf_op jit(solution)/shard_map/scatter | solution.py:106
  22.3 1.9 %fusion.37 = (f32[256]{0:T(256)S(1)}, f32[256,512]{1,0:T(8,128)S(1)}) fusion(f32[512]{0:T(512)} %get-tuple-element.33, bf16[512,1024]{1,0:T(8,128)(2,1)} %get-tuple-element.34, bf16[64,1024]{1,0:T(8,128)(2,1)S(1)} %get-tuple-element.36, bf16[64,1024]{1,0:T(8,128)(2,1)} %get-tuple-element.37, bf16[64,1024]{1,0:T(8,128)(2,1)} %get-tuple-element.38, ...), kind=kOutput, calls=%fused_computation.175 | convolution fusion | flops 271056640 | bytes 2100224 | tf_op jit(solution)/shard_map/dot_general | solution.py:10
  24.4 1.3 %constant_dynamic-update-slice_fusion.21 = f32[2048]{0:T(1024)} fusion(f32[2048]{0:T(1024)} %custom-call.1, f32[256]{0:T(256)S(1)} %get-tuple-element.64), kind=kLoop, calls=%fused_computation.93 | loop fusion | bytes 2048
  25.7 1.3 %constant_dynamic-update-slice_fusion.22 = f32[2048]{0:T(1024)} fusion(f32[2048]{0:T(1024)} %custom-call, f32[256]{0:T(256)S(1)} %exponential_reduce_fusion.7), kind=kLoop, calls=%fused_computation.94 | loop fusion | bytes 2048
  27.0 2.2 %collective-permute-start = (bf16[64,1024]{1,0:T(8,128)(2,1)S(1)}, bf16[64,1024]{1,0:T(8,128)(2,1)S(1)}, u32[]{:S(2)}, u32[]{:S(2)}) collective-permute-start(bf16[64,1024]{1,0:T(8,128)(2,1)S(1)} %get-tuple-element.35), channel_id=1, source_target_pairs={{0,24},{4,28},{8,0},{12,4},{16,8},{20,12},{24,16},{28,20},{1,25},{... | collective-permute-start | bytes 393224 | tf_op jit(solution)/shard_map/ppermute | solution.py:91
  29.6 1.7 %collective-permute-start.4 = (bf16[64,1024]{1,0:T(8,128)(2,1)S(1)}, bf16[64,1024]{1,0:T(8,128)(2,1)S(1)}, u32[]{:S(2)}, u32[]{:S(2)}) collective-permute-start(bf16[64,1024]{1,0:T(8,128)(2,1)S(1)} %collective-permute-done.3), channel_id=1, source_target_pairs={{0,2},{1,3},{2,0},{3,1},{4,6},{5,7},{6,4},{7,5},{8,10},{9,11},{10,... | collective-permute-start | bytes 393224 | tf_op jit(solution)/shard_map/ppermute | solution.py:78
  31.3 0.4 collective-permute-start.7
  31.8 1.7 %collective-permute-start.10 = (bf16[64,1024]{1,0:T(8,128)(2,1)S(1)}, bf16[64,1024]{1,0:T(8,128)(2,1)S(1)}, u32[]{:S(2)}, u32[]{:S(2)}) collective-permute-start(bf16[64,1024]{1,0:T(8,128)(2,1)S(1)} %collective-permute-done.9), channel_id=1, source_target_pairs={{0,2},{1,3},{2,0},{3,1},{4,6},{5,7},{6,4},{7,5},{8,10},{9,11},{10,... | collective-permute-start | bytes 393224 | tf_op jit(solution)/shard_map/ppermute | solution.py:78
  33.6 0.8 collective-permute-start.13
  34.3 0.9 collective-permute-done.18
  35.2 1.5 %collective-permute-start.16 = (bf16[64,1024]{1,0:T(8,128)(2,1)S(1)}, bf16[64,1024]{1,0:T(8,128)(2,1)S(1)}, u32[]{:S(2)}, u32[]{:S(2)}) collective-permute-start(bf16[64,1024]{1,0:T(8,128)(2,1)S(1)} %collective-permute-done.15), channel_id=1, source_target_pairs={{0,2},{1,3},{2,0},{3,1},{4,6},{5,7},{6,4},{7,5},{8,10},{9,11},{10,... | collective-permute-start | bytes 393224 | tf_op jit(solution)/shard_map/ppermute | solution.py:78
  36.7 1.0 collective-permute-start.1
  37.8 1.1 collective-permute-done.7
  38.9 1.7 %collective-permute-start.19 = (bf16[64,1024]{1,0:T(8,128)(2,1)S(1)}, bf16[64,1024]{1,0:T(8,128)(2,1)S(1)}, u32[]{:S(2)}, u32[]{:S(2)}) collective-permute-start(bf16[64,1024]{1,0:T(8,128)(2,1)S(1)} %collective-permute-done.18), channel_id=1, source_target_pairs={{0,2},{1,3},{2,0},{3,1},{4,6},{5,7},{6,4},{7,5},{8,10},{9,11},{10,... | collective-permute-start | bytes 393224 | tf_op jit(solution)/shard_map/ppermute | solution.py:78
  40.6 1.1 collective-permute-done.10
  41.8 2.7 %collective-permute-done.13 = bf16[64,1024]{1,0:T(8,128)(2,1)S(1)} collective-permute-done((bf16[64,1024]{1,0:T(8,128)(2,1)S(1)}, bf16[64,1024]{1,0:T(8,128)(2,1)S(1)}, u32[]{:S(2)}, u32[]{:S(2)}) %collective-permute-start.13) | collective-permute-done | bytes 131104 | tf_op jit(solution)/shard_map/ppermute | solution.py:78
  44.6 2.7 %collective-permute-done.16 = bf16[64,1024]{1,0:T(8,128)(2,1)S(1)} collective-permute-done((bf16[64,1024]{1,0:T(8,128)(2,1)S(1)}, bf16[64,1024]{1,0:T(8,128)(2,1)S(1)}, u32[]{:S(2)}, u32[]{:S(2)}) %collective-permute-start.16) | collective-permute-done | bytes 131104 | tf_op jit(solution)/shard_map/ppermute | solution.py:78
  47.3 1.4 %collective-permute-done.1 = bf16[64,1024]{1,0:T(8,128)(2,1)S(1)} collective-permute-done((bf16[64,1024]{1,0:T(8,128)(2,1)S(1)}, bf16[64,1024]{1,0:T(8,128)(2,1)S(1)}, u32[]{:S(2)}, u32[]{:S(2)}) %collective-permute-start.1) | collective-permute-done | bytes 131104 | tf_op jit(solution)/shard_map/ppermute | solution.py:78
  48.7 1.4 %collective-permute-done.19 = bf16[64,1024]{1,0:T(8,128)(2,1)S(1)} collective-permute-done((bf16[64,1024]{1,0:T(8,128)(2,1)S(1)}, bf16[64,1024]{1,0:T(8,128)(2,1)S(1)}, u32[]{:S(2)}, u32[]{:S(2)}) %collective-permute-start.19) | collective-permute-done | bytes 131104 | tf_op jit(solution)/shard_map/ppermute | solution.py:78
  50.2 0.6 collective-permute-start.2
  50.8 0.6 fusion.38
  51.5 0.6 fusion.39
  52.1 0.6 fusion.40
  52.7 0.6 fusion.41
  53.5 0.6 fusion.42
  54.2 0.6 fusion.43
  55.1 0.6 fusion.44
  55.9 1.3 %constant_dynamic-update-slice_fusion.35 = f32[2048]{0:T(1024)} fusion(f32[2048]{0:T(1024)} %constant_dynamic-update-slice_fusion.21, f32[256]{0:T(256)S(1)} %get-tuple-element.66), kind=kLoop, calls=%fused_computation.153 | loop fusion | bytes 2048
  57.4 1.3 %constant_dynamic-update-slice_fusion.33 = f32[2048]{0:T(1024)} fusion(f32[2048]{0:T(1024)} %constant_dynamic-update-slice_fusion.35, f32[256]{0:T(256)S(1)} %get-tuple-element.68), kind=kLoop, calls=%fused_computation.151 | loop fusion | bytes 2048
  58.9 1.3 %constant_dynamic-update-slice_fusion.31 = f32[2048]{0:T(1024)} fusion(f32[2048]{0:T(1024)} %constant_dynamic-update-slice_fusion.33, f32[256]{0:T(256)S(1)} %get-tuple-element.70), kind=kLoop, calls=%fused_computation.149 | loop fusion | bytes 2048
  60.4 1.3 %constant_dynamic-update-slice_fusion.29 = f32[2048]{0:T(1024)} fusion(f32[2048]{0:T(1024)} %constant_dynamic-update-slice_fusion.31, f32[256]{0:T(256)S(1)} %get-tuple-element.72), kind=kLoop, calls=%fused_computation.147 | loop fusion | bytes 2048
  61.9 1.3 %constant_dynamic-update-slice_fusion.27 = f32[2048]{0:T(1024)} fusion(f32[2048]{0:T(1024)} %constant_dynamic-update-slice_fusion.29, f32[256]{0:T(256)S(1)} %get-tuple-element.74), kind=kLoop, calls=%fused_computation.145 | loop fusion | bytes 2048
  63.4 1.3 %constant_dynamic-update-slice_fusion.25 = f32[2048]{0:T(1024)} fusion(f32[2048]{0:T(1024)} %constant_dynamic-update-slice_fusion.27, f32[256]{0:T(256)S(1)} %get-tuple-element.76), kind=kLoop, calls=%fused_computation.143 | loop fusion | bytes 2048
  65.0 1.3 %constant_dynamic-update-slice_fusion.23 = f32[2048]{0:T(1024)} fusion(f32[2048]{0:T(1024)} %constant_dynamic-update-slice_fusion.25, f32[256]{0:T(256)S(1)} %get-tuple-element.78), kind=kLoop, calls=%fused_computation.141 | loop fusion | bytes 2048 | tf_op jit(solution)/shard_map/concatenate | solution.py:95
  66.3 0.7 pad_maximum_fusion.10
  67.1 1.3 %copy.11 = f32[2,2048]{0,1:T(8,128)} copy(f32[2,2048]{1,0:T(2,128)S(1)} %pad_maximum_fusion.10) | data formatting | bytes 32768 | tf_op jit(solution)/shard_map/stack | solution.py:108
  68.4 8.8 %gather_fusion = f32[2048,2]{1,0:T(8,128)} fusion(f32[2,2048]{0,1:T(8,128)} %copy.11, s32[2048]{0:T(1024)S(1)} %fusion.23), kind=kCustom, calls=%fused_computation | custom fusion | bytes 40960 | tf_op jit(solution)/shard_map/gather | solution.py:108
  77.2 1.6 %copy.12 = f32[1,2,2048]{2,1,0:T(2,128)S(1)} copy(f32[1,2,2048]{1,2,0:T(8,128)} %bitcast.54) | data formatting | bytes 32768
  78.7 9.4 %all-gather.1 = f32[8,2,2048]{2,1,0:T(2,128)S(1)} all-gather(f32[1,2,2048]{2,1,0:T(2,128)S(1)} %copy.12), channel_id=2, replica_groups=mesh['outer'=4,'dp'=2,'cent'=4] {'dp','cent'}, dimensions={0}, use_global_device_ids=true | all-gather | bytes 147456 | tf_op jit(solution)/shard_map/all_gather | solution.py:109
  88.1 0.7 slice_reduce_fusion
  88.9 11.8 %gather_fusion.1 = f32[2048]{0:T(1024)S(1)} fusion(f32[2048]{0:T(1024)S(1)} %get-tuple-element.39, s32[2048]{0:T(1024)S(1)} %broadcast_clamp_fusion), kind=kCustom, calls=%fused_computation.1 | custom fusion | bytes 24576 | tf_op jit(solution)/shard_map/gather | solution.py:113
  100.7 0.9 fusion.18
  101.6 11.8 %gather_fusion.2 = f32[2048]{0:T(1024)S(1)} fusion(f32[2048]{0:T(1024)S(1)} %fusion.18, s32[2048]{0:T(1024)S(1)} %broadcast_clamp_fusion), kind=kCustom, calls=%fused_computation.2 | custom fusion | bytes 24576 | tf_op jit(solution)/shard_map/gather | solution.py:114
  113.4 0.3 convert_reduce_fusion
  113.7 1.5 %fusion.16 = f32[512,1024]{1,0:T(8,128)S(1)} fusion(bf16[256,512]{1,0:T(8,128)(2,1)S(1)} %get-tuple-element.81, bf16[64,1024]{1,0:T(8,128)(2,1)S(1)} %get-tuple-element.36, bf16[64,1024]{1,0:T(8,128)(2,1)} %get-tuple-element.37, bf16[64,1024]{1,0:T(8,128)(2,1)} %get-tuple-element.38, bf16[64,1024]{1,0:T(8,128)(2,1)S(1)} %get-tuple-element.35), kind=kOutput, calls=%fused_computation.62 | convolution fusion | flops 270532608 | bytes 2883584 | tf_op jit(solution)/shard_map/dot_general | solution.py:124
  115.2 0.3 convert_reduce_fusion.2
  115.5 0.5 fusion.49
  116.2 0.5 fusion.50
  116.7 0.4 copy-done.1
  117.4 0.5 fusion.47
  118.2 0.5 fusion.48
  118.6 0.3 copy-done.3
  119.3 0.5 fusion.45
  120.0 0.5 fusion.46
  120.5 0.8 copy-done.5
  121.4 4.1 %add_multiply_fusion = f32[512,1024]{1,0:T(8,128)} fusion(f32[512,1024]{1,0:T(8,128)S(1)} %copy-done.5, f32[512,1024]{1,0:T(8,128)S(1)} %fusion.16, f32[512,1024]{1,0:T(8,128)S(1)} %fusion.49, f32[512,1024]{1,0:T(8,128)S(1)} %fusion.50, f32[512,1024]{1,0:T(8,128)S(1)} %fusion.47, f32[512,1024]{1,0:T(8,128)S(1)} %fusion.48, f32[512,1024]{1,0:T(8,128)S(1)} %fusion.45, ...), kind=kOutput, calls=%fused_computation.4 | convolution fusion | flops 285212672 | bytes 19677196 | tf_op jit(solution)/shard_map/dot_general | solution.py:124
  (123 shorter events, 5.0 us)
Async XLA Ops:
  0.0 12.2 %copy-start.4 = (f32[512,1024]{1,0:T(8,128)S(1)}, f32[512,1024]{1,0:T(8,128)}, u32[]{:S(2)}) copy-start(f32[512,1024]{1,0:T(8,128)} %param.6) | copy-start | bytes 6291460
  2.2 24.8 %collective-permute-start.3 = (bf16[64,1024]{1,0:T(8,128)(2,1)S(1)}, bf16[64,1024]{1,0:T(8,128)(2,1)S(1)}, u32[]{:S(2)}, u32[]{:S(2)}) collective-permute-start(bf16[64,1024]{1,0:T(8,128)(2,1)S(1)} %get-tuple-element.35), channel_id=1, source_target_pairs={{0,4},{4,0},{8,12},{12,8},{16,20},{20,16},{24,28},{28,24},{1,5},{5... | collective-permute-start | bytes 393224 | tf_op jit(solution)/shard_map/ppermute | solution.py:91
  5.2 24.1 %collective-permute-start.6 = (bf16[64,1024]{1,0:T(8,128)(2,1)S(1)}, bf16[64,1024]{1,0:T(8,128)(2,1)S(1)}, u32[]{:S(2)}, u32[]{:S(2)}) collective-permute-start(bf16[64,1024]{1,0:T(8,128)(2,1)S(1)} %get-tuple-element.35), channel_id=1, source_target_pairs={{0,8},{4,12},{8,16},{12,20},{16,24},{20,28},{24,0},{28,4},{1,9},{5... | collective-permute-start | bytes 393224 | tf_op jit(solution)/shard_map/ppermute | solution.py:91
  6.8 22.8 %collective-permute-start.9 = (bf16[64,1024]{1,0:T(8,128)(2,1)S(1)}, bf16[64,1024]{1,0:T(8,128)(2,1)S(1)}, u32[]{:S(2)}, u32[]{:S(2)}) collective-permute-start(bf16[64,1024]{1,0:T(8,128)(2,1)S(1)} %get-tuple-element.35), channel_id=1, source_target_pairs={{0,12},{4,8},{8,20},{12,16},{16,28},{20,24},{24,4},{28,0},{1,13},{... | collective-permute-start | bytes 393224 | tf_op jit(solution)/shard_map/ppermute | solution.py:91
  8.3 23.0 %collective-permute-start.12 = (bf16[64,1024]{1,0:T(8,128)(2,1)S(1)}, bf16[64,1024]{1,0:T(8,128)(2,1)S(1)}, u32[]{:S(2)}, u32[]{:S(2)}) collective-permute-start(bf16[64,1024]{1,0:T(8,128)(2,1)S(1)} %get-tuple-element.35), channel_id=1, source_target_pairs={{0,16},{4,20},{8,24},{12,28},{16,0},{20,4},{24,8},{28,12},{1,17},{... | collective-permute-start | bytes 393224 | tf_op jit(solution)/shard_map/ppermute | solution.py:91
  9.4 22.4 %collective-permute-start.15 = (bf16[64,1024]{1,0:T(8,128)(2,1)S(1)}, bf16[64,1024]{1,0:T(8,128)(2,1)S(1)}, u32[]{:S(2)}, u32[]{:S(2)}) collective-permute-start(bf16[64,1024]{1,0:T(8,128)(2,1)S(1)} %get-tuple-element.35), channel_id=1, source_target_pairs={{0,20},{4,16},{8,28},{12,24},{16,4},{20,0},{24,12},{28,8},{1,21},{... | collective-permute-start | bytes 393224 | tf_op jit(solution)/shard_map/ppermute | solution.py:91
  27.0 6.5 %collective-permute-start = (bf16[64,1024]{1,0:T(8,128)(2,1)S(1)}, bf16[64,1024]{1,0:T(8,128)(2,1)S(1)}, u32[]{:S(2)}, u32[]{:S(2)}) collective-permute-start(bf16[64,1024]{1,0:T(8,128)(2,1)S(1)} %get-tuple-element.35), channel_id=1, source_target_pairs={{0,24},{4,28},{8,0},{12,4},{16,8},{20,12},{24,16},{28,20},{1,25},{... | collective-permute-start | bytes 393224 | tf_op jit(solution)/shard_map/ppermute | solution.py:91
  29.3 5.9 %collective-permute-start.18 = (bf16[64,1024]{1,0:T(8,128)(2,1)S(1)}, bf16[64,1024]{1,0:T(8,128)(2,1)S(1)}, u32[]{:S(2)}, u32[]{:S(2)}) collective-permute-start(bf16[64,1024]{1,0:T(8,128)(2,1)S(1)} %get-tuple-element.35), channel_id=1, source_target_pairs={{0,28},{4,24},{8,4},{12,0},{16,12},{20,8},{24,20},{28,16},{1,29},{... | collective-permute-start | bytes 393224 | tf_op jit(solution)/shard_map/ppermute | solution.py:91
  29.6 7.1 %collective-permute-start.4 = (bf16[64,1024]{1,0:T(8,128)(2,1)S(1)}, bf16[64,1024]{1,0:T(8,128)(2,1)S(1)}, u32[]{:S(2)}, u32[]{:S(2)}) collective-permute-start(bf16[64,1024]{1,0:T(8,128)(2,1)S(1)} %collective-permute-done.3), channel_id=1, source_target_pairs={{0,2},{1,3},{2,0},{3,1},{4,6},{5,7},{6,4},{7,5},{8,10},{9,11},{10,... | collective-permute-start | bytes 393224 | tf_op jit(solution)/shard_map/ppermute | solution.py:78
  31.3 7.6 %collective-permute-start.7 = (bf16[64,1024]{1,0:T(8,128)(2,1)S(1)}, bf16[64,1024]{1,0:T(8,128)(2,1)S(1)}, u32[]{:S(2)}, u32[]{:S(2)}) collective-permute-start(bf16[64,1024]{1,0:T(8,128)(2,1)S(1)} %collective-permute-done.6), channel_id=1, source_target_pairs={{0,2},{1,3},{2,0},{3,1},{4,6},{5,7},{6,4},{7,5},{8,10},{9,11},{10,... | collective-permute-start | bytes 393224 | tf_op jit(solution)/shard_map/ppermute | solution.py:78
  31.8 9.9 %collective-permute-start.10 = (bf16[64,1024]{1,0:T(8,128)(2,1)S(1)}, bf16[64,1024]{1,0:T(8,128)(2,1)S(1)}, u32[]{:S(2)}, u32[]{:S(2)}) collective-permute-start(bf16[64,1024]{1,0:T(8,128)(2,1)S(1)} %collective-permute-done.9), channel_id=1, source_target_pairs={{0,2},{1,3},{2,0},{3,1},{4,6},{5,7},{6,4},{7,5},{8,10},{9,11},{10,... | collective-permute-start | bytes 393224 | tf_op jit(solution)/shard_map/ppermute | solution.py:78
  33.6 11.0 %collective-permute-start.13 = (bf16[64,1024]{1,0:T(8,128)(2,1)S(1)}, bf16[64,1024]{1,0:T(8,128)(2,1)S(1)}, u32[]{:S(2)}, u32[]{:S(2)}) collective-permute-start(bf16[64,1024]{1,0:T(8,128)(2,1)S(1)} %collective-permute-done.12), channel_id=1, source_target_pairs={{0,2},{1,3},{2,0},{3,1},{4,6},{5,7},{6,4},{7,5},{8,10},{9,11},{10,... | collective-permute-start | bytes 393224 | tf_op jit(solution)/shard_map/ppermute | solution.py:78
  35.2 12.0 %collective-permute-start.16 = (bf16[64,1024]{1,0:T(8,128)(2,1)S(1)}, bf16[64,1024]{1,0:T(8,128)(2,1)S(1)}, u32[]{:S(2)}, u32[]{:S(2)}) collective-permute-start(bf16[64,1024]{1,0:T(8,128)(2,1)S(1)} %collective-permute-done.15), channel_id=1, source_target_pairs={{0,2},{1,3},{2,0},{3,1},{4,6},{5,7},{6,4},{7,5},{8,10},{9,11},{10,... | collective-permute-start | bytes 393224 | tf_op jit(solution)/shard_map/ppermute | solution.py:78
  36.7 11.9 %collective-permute-start.1 = (bf16[64,1024]{1,0:T(8,128)(2,1)S(1)}, bf16[64,1024]{1,0:T(8,128)(2,1)S(1)}, u32[]{:S(2)}, u32[]{:S(2)}) collective-permute-start(bf16[64,1024]{1,0:T(8,128)(2,1)S(1)} %collective-permute-done), channel_id=1, source_target_pairs={{0,2},{1,3},{2,0},{3,1},{4,6},{5,7},{6,4},{7,5},{8,10},{9,11},{10,... | collective-permute-start | bytes 393224 | tf_op jit(solution)/shard_map/ppermute | solution.py:78
  38.9 11.2 %collective-permute-start.19 = (bf16[64,1024]{1,0:T(8,128)(2,1)S(1)}, bf16[64,1024]{1,0:T(8,128)(2,1)S(1)}, u32[]{:S(2)}, u32[]{:S(2)}) collective-permute-start(bf16[64,1024]{1,0:T(8,128)(2,1)S(1)} %collective-permute-done.18), channel_id=1, source_target_pairs={{0,2},{1,3},{2,0},{3,1},{4,6},{5,7},{6,4},{7,5},{8,10},{9,11},{10,... | collective-permute-start | bytes 393224 | tf_op jit(solution)/shard_map/ppermute | solution.py:78
  41.7 8.4 %collective-permute-start.5 = (bf16[128,1024]{1,0:T(8,128)(2,1)S(1)}, bf16[128,1024]{1,0:T(8,128)(2,1)S(1)}, u32[]{:S(2)}, u32[]{:S(2)}) collective-permute-start(bf16[128,1024]{1,0:T(8,128)(2,1)S(1)} %pad_maximum_fusion.2), channel_id=1, source_target_pairs={{0,1},{1,0},{2,3},{3,2},{4,5},{5,4},{6,7},{7,6},{8,9},{9,8},{10,11... | collective-permute-start | bytes 786440 | tf_op jit(solution)/shard_map/ppermute | solution.py:78
  41.8 9.0 %copy-start.6 = (bf16[512,1024]{1,0:T(8,128)(2,1)S(1)}, bf16[512,1024]{1,0:T(8,128)(2,1)}, u32[]{:S(2)}) copy-start(bf16[512,1024]{1,0:T(8,128)(2,1)} %get-tuple-element.34) | copy-start | bytes 3145732
  41.8 9.0 %copy-start.22 = (f32[512]{0:T(512)S(1)}, f32[512]{0:T(512)}, u32[]{:S(2)}) copy-start(f32[512]{0:T(512)} %get-tuple-element.33) | copy-start | bytes 6148
  44.5 6.8 %collective-permute-start.8 = (bf16[128,1024]{1,0:T(8,128)(2,1)S(1)}, bf16[128,1024]{1,0:T(8,128)(2,1)S(1)}, u32[]{:S(2)}, u32[]{:S(2)}) collective-permute-start(bf16[128,1024]{1,0:T(8,128)(2,1)S(1)} %pad_maximum_fusion.3), channel_id=1, source_target_pairs={{0,1},{1,0},{2,3},{3,2},{4,5},{5,4},{6,7},{7,6},{8,9},{9,8},{10,11... | collective-permute-start | bytes 786440 | tf_op jit(solution)/shard_map/ppermute | solution.py:78
  47.3 4.8 %collective-permute-start.11 = (bf16[128,1024]{1,0:T(8,128)(2,1)S(1)}, bf16[128,1024]{1,0:T(8,128)(2,1)S(1)}, u32[]{:S(2)}, u32[]{:S(2)}) collective-permute-start(bf16[128,1024]{1,0:T(8,128)(2,1)S(1)} %pad_maximum_fusion.4), channel_id=1, source_target_pairs={{0,1},{1,0},{2,3},{3,2},{4,5},{5,4},{6,7},{7,6},{8,9},{9,8},{10,11... | collective-permute-start | bytes 786440 | tf_op jit(solution)/shard_map/ppermute | solution.py:78
  48.7 4.0 %collective-permute-start.14 = (bf16[128,1024]{1,0:T(8,128)(2,1)S(1)}, bf16[128,1024]{1,0:T(8,128)(2,1)S(1)}, u32[]{:S(2)}, u32[]{:S(2)}) collective-permute-start(bf16[128,1024]{1,0:T(8,128)(2,1)S(1)} %pad_maximum_fusion.5), channel_id=1, source_target_pairs={{0,1},{1,0},{2,3},{3,2},{4,5},{5,4},{6,7},{7,6},{8,9},{9,8},{10,11... | collective-permute-start | bytes 786440 | tf_op jit(solution)/shard_map/ppermute | solution.py:78
  50.1 3.2 %collective-permute-start.17 = (bf16[128,1024]{1,0:T(8,128)(2,1)S(1)}, bf16[128,1024]{1,0:T(8,128)(2,1)S(1)}, u32[]{:S(2)}, u32[]{:S(2)}) collective-permute-start(bf16[128,1024]{1,0:T(8,128)(2,1)S(1)} %pad_maximum_fusion.6), channel_id=1, source_target_pairs={{0,1},{1,0},{2,3},{3,2},{4,5},{5,4},{6,7},{7,6},{8,9},{9,8},{10,11... | collective-permute-start | bytes 786440 | tf_op jit(solution)/shard_map/ppermute | solution.py:78
  50.2 4.0 %collective-permute-start.2 = (bf16[128,1024]{1,0:T(8,128)(2,1)S(1)}, bf16[128,1024]{1,0:T(8,128)(2,1)S(1)}, u32[]{:S(2)}, u32[]{:S(2)}) collective-permute-start(bf16[128,1024]{1,0:T(8,128)(2,1)S(1)} %pad_maximum_fusion.1), channel_id=1, source_target_pairs={{0,1},{1,0},{2,3},{3,2},{4,5},{5,4},{6,7},{7,6},{8,9},{9,8},{10,11... | collective-permute-start | bytes 786440 | tf_op jit(solution)/shard_map/ppermute | solution.py:78
  50.8 1.3 %copy-start.19 = (bf16[256,1024]{1,0:T(8,128)(2,1)}, bf16[256,1024]{1,0:T(8,128)(2,1)S(1)}, u32[]{:S(2)}) copy-start(bf16[256,1024]{1,0:T(8,128)(2,1)S(1)} %constant_dynamic-update-slice_fusion.3) | copy-start | bytes 1572868
  51.4 3.4 %collective-permute-start.20 = (bf16[128,1024]{1,0:T(8,128)(2,1)S(1)}, bf16[128,1024]{1,0:T(8,128)(2,1)S(1)}, u32[]{:S(2)}, u32[]{:S(2)}) collective-permute-start(bf16[128,1024]{1,0:T(8,128)(2,1)S(1)} %pad_maximum_fusion.7), channel_id=1, source_target_pairs={{0,1},{1,0},{2,3},{3,2},{4,5},{5,4},{6,7},{7,6},{8,9},{9,8},{10,11... | collective-permute-start | bytes 786440 | tf_op jit(solution)/shard_map/ppermute | solution.py:78
  51.5 1.2 copy-start.17
  52.1 1.2 copy-start.15
  52.7 0.8 copy-start.13
  53.5 1.2 copy-start.11
  54.1 7.6 %copy-start = (f32[256,512]{1,0:T(8,128)}, f32[256,512]{1,0:T(8,128)S(1)}, u32[]{:S(2)}) copy-start(f32[256,512]{1,0:T(8,128)S(1)} %get-tuple-element.75) | copy-start | bytes 1572868
  54.1 0.9 copy-start.9
  55.1 5.4 %copy-start.7 = (bf16[256,1024]{1,0:T(8,128)(2,1)}, bf16[256,1024]{1,0:T(8,128)(2,1)S(1)}, u32[]{:S(2)}) copy-start(bf16[256,1024]{1,0:T(8,128)(2,1)S(1)} %constant_dynamic-update-slice_fusion.18) | copy-start | bytes 1572868
  55.6 9.1 %copy-start.2 = (f32[256,512]{1,0:T(8,128)}, f32[256,512]{1,0:T(8,128)S(1)}, u32[]{:S(2)}) copy-start(f32[256,512]{1,0:T(8,128)S(1)} %get-tuple-element.79) | copy-start | bytes 1572868
  55.6 10.6 %copy-start.21 = (f32[2048]{0:T(1024)S(1)}, f32[2048]{0:T(1024)}, u32[]{:S(2)}) copy-start(f32[2048]{0:T(1024)} %constant_dynamic-update-slice_fusion.22) | copy-start | bytes 24580
  113.7 1.8 %copy-start.18 = (bf16[256,1024]{1,0:T(8,128)(2,1)S(1)}, bf16[256,1024]{1,0:T(8,128)(2,1)}, u32[]{:S(2)}) copy-start(bf16[256,1024]{1,0:T(8,128)(2,1)} %copy-done.17) | copy-start | bytes 1572868
  115.2 1.0 copy-start.16
  116.0 1.1 copy-start.1
  116.2 1.2 copy-start.14
  117.1 1.1 copy-start.12
  117.9 1.1 copy-start.3
  118.2 1.1 copy-start.10
  118.9 1.1 copy-start.8
  119.7 1.6 %copy-start.5 = (f32[512,1024]{1,0:T(8,128)S(1)}, f32[512,1024]{1,0:T(8,128)}, u32[]{:S(2)}) copy-start(f32[512,1024]{1,0:T(8,128)} %param.6) | copy-start | bytes 6291460
  119.7 1.7 %copy-start.20 = (bf16[256,1024]{1,0:T(8,128)(2,1)S(1)}, bf16[256,1024]{1,0:T(8,128)(2,1)}, u32[]{:S(2)}) copy-start(bf16[256,1024]{1,0:T(8,128)(2,1)} %copy-done.19) | copy-start | bytes 1572868

commit v3 on v2

--- a/solution.py
+++ b/solution.py
@@ -95,23 +95,28 @@
     local_max = jnp.concatenate([s[0] for s in summaries])
     local_sum = jnp.concatenate([s[1] for s in summaries])
 
-    k_idx = jnp.arange(n_od * n_c * tq) // (n_c * tq)
-    j_idx = (jnp.arange(n_od * n_c * tq) // tq) % n_c
-    r_idx = jnp.arange(n_od * n_c * tq) % tq
-    sz_of = jnp.asarray([s[0] for s in shifts], jnp.int32)[k_idx]
-    sy_of = jnp.asarray([s[1] for s in shifts], jnp.int32)[k_idx]
-    x_of = jnp.asarray(xs, jnp.int32)[j_idx]
-    src = ((z - sz_of) % n_o) * n_d + (y - sy_of) % n_d
-    absolute = (src * n_c + (q ^ x_of)) * tq + r_idx
-    order = jnp.zeros_like(absolute).at[absolute].set(jnp.arange(absolute.shape[0]))
+    src_vec = jnp.stack([((z - sz) % n_o) * n_d + (y - sy) % n_d for sz, sy in shifts])
+    hot_k = src_vec[None, :] == jnp.arange(n_od)[:, None]
+    c_vec = jnp.stack([q ^ x for x in xs])
+    hot_c = c_vec[None, :] == jnp.arange(n_c)[:, None]
 
-    both = jnp.stack([local_max, local_sum])[:, order]
+    def to_absolute(v):
+        v = v.reshape(n_od, n_c, tq)
+        v = jnp.sum(jnp.where(hot_c[None, :, :, None], v[:, None, :, :], 0.0), axis=2)
+        return jnp.sum(jnp.where(hot_k[:, :, None, None], v[None], 0.0), axis=1)
+
+    def to_local(v):
+        v = jnp.sum(jnp.where(hot_k[:, :, None, None], v[:, None], 0.0), axis=0)
+        v = jnp.sum(jnp.where(hot_c[:, :, None], v[:, :, None, :], 0.0), axis=1)
+        return v.reshape(n_od * n_c * tq)
+
+    both = jnp.stack([to_absolute(local_max), to_absolute(local_sum)])
     every = lax.all_gather(both, ("dp", "cent"), axis=0)
     maxes, sums = every[:, 0], every[:, 1]
     peak_abs = jnp.max(maxes, axis=0)
-    mass_abs = jnp.sum(sums * jnp.exp(maxes - peak_abs[None, :]), axis=0)
-    row_peak = peak_abs[absolute]
-    row_mass = mass_abs[absolute]
+    mass_abs = jnp.sum(sums * jnp.exp(maxes - peak_abs[None]), axis=0)
+    row_peak = to_local(peak_abs)
+    row_mass = to_local(mass_abs)
 
     blk = n_c * tq
     weight_sum = [None] * n_o

time: 126 us -> 140 us (1.11)
  matrix products: 14.2 us -> 26.3 us
  local copies, waits for them, and re-layouts: 59 us -> 47.1 us
  other arithmetic: 8.98 us -> 19 us
  waiting for transfers between devices: 11.3 us -> 16 us
  starting transfers between devices: 22 us -> 20.3 us
    gather x3 -> x0, local copies, waits for them, and re-layouts: 32.4 us -> none  [the longest x1 11.8 us: shards_all(): row_mass = mass_abs[absolute]]
    div x0 -> x8, local copies, waits for them, and re-layouts: none -> 10.4 us  [shards_all(): w = (jnp.exp(logits[k] - pk[:, None]) / mk[:, None]).astype(jnp.bfloat16)]
    dot_general x8, matrix products: 5.86 us -> 15.8 us  [scores_for(): lax.dot_general(piece, cent_bf, (((1,), (1,)), ((), ())), preferred_eleme...]
    concatenate x7, local copies, waits for them, and re-layouts: 0.13 us -> 9.62 us  [spread(): cur = jnp.concatenate([cur, other], axis=0)]
    unnamed x75 -> x94, local copies, waits for them, and re-layouts: 15.1 us -> 5.97 us
    ppermute x7, waiting for transfers between devices: 0.88 us -> 9.27 us  [shards_all(): blocks.append(spread(lax.ppermute(mine, ('outer', 'dp'), perm)))]
    scatter x1 -> x0, local copies, waits for them, and re-layouts: 8.05 us -> none  [shards_all(): jnp.zeros_like(absolute).at[absolute].set(jnp.arange(absolute.shape[0]))]
    concatenate x1 -> x9, local copies, waits for them, and re-layouts: 0.01 us -> 6.76 us  [shards_all(): local_sum = jnp.concatenate([s[1] for s in summaries])]
  transfers between devices with their start and end apart: 21 -> 21, of which waited for: 7 -> 8; matrix products, arithmetic and copies ran while one was open for 15% -> 31% of each run, Pallas kernels for 0% -> 0%
where the time goes in v3:
time: 140 us; the launch traced here: 139 us
  local copies, waits for them, and re-layouts  47.1 us (34%)
  matrix products  26.3 us (19%)
  starting transfers between devices  20.3 us (14%)
  other arithmetic  19 us (14%)
  waiting for transfers between devices  16 us (11%)
  blocking collectives  9.48 us (7%)
    dot_general x8, matrix products, scores_for(): lax.dot_general(piece, cent_bf, (((1,), (1,)), ((), ())), preferred_eleme...  15.8 us
    ppermute x7, starting transfers between devices, shards_all(): blocks.append(spread(lax.ppermute(mine, ('outer', 'dp'), perm)))  11 us
    dot_general x8, matrix products, shards_all(): lax.dot_general(w, blocks[k], (((0,), (0,)), ((), ())), preferred_element...  10.5 us
    div x8, local copies, waits for them, and re-layouts, shards_all(): w = (jnp.exp(logits[k] - pk[:, None]) / mk[:, None]).astype(jnp.bfloat16)  10.4 us
    concatenate x7, local copies, waits for them, and re-layouts, spread(): cur = jnp.concatenate([cur, other], axis=0)  9.62 us
    all_gather x1, blocking collectives, shards_all(): every = lax.all_gather(both, ('dp', 'cent'), axis=0)  9.48 us
    ppermute x14, starting transfers between devices, spread(): other = lax.ppermute(cur, 'cent', [(i, i ^ bit) for i in range(n_c)])  9.32 us
    ppermute x7, waiting for transfers between devices, shards_all(): blocks.append(spread(lax.ppermute(mine, ('outer', 'dp'), perm)))  9.27 us
  transfers between devices with their start and end apart: 21, of which 8 were waited for; matrix products, arithmetic and copies ran while one was open for 31% of the time, Pallas kernels for 0%

profile of v3, /device:TPU:0, one launch (start us, length us, event | category | flops | bytes accessed | tf_op | source)
XLA Modules:
  0.0 138.9 jit_solution(12536461401902188232)
XLA Ops:
  0.0 1.4 %convert_element_type.54 = bf16[256,1024]{1,0:T(8,128)(2,1)S(1)} convert(f32[256,1024]{1,0:T(8,128)} %param.2) | non-fusion elementwise | flops 262144 | bytes 1572864 | tf_op jit(solution)/shard_map/convert_element_type | solution.py:56
  1.5 0.8 constant_dynamic-slice_fusion.3
  2.2 6.0 %collective-permute-start.18 = (bf16[64,1024]{1,0:T(8,128)(2,1)S(1)}, bf16[64,1024]{1,0:T(8,128)(2,1)S(1)}, u32[]{:S(2)}, u32[]{:S(2)}) collective-permute-start(bf16[64,1024]{1,0:T(8,128)(2,1)S(1)} %get-tuple-element.59), channel_id=1, source_target_pairs={{0,28},{4,24},{8,4},{12,0},{16,12},{20,8},{24,20},{28,16},{1,29},{... | collective-permute-start | bytes 393224 | tf_op jit(solution)/shard_map/ppermute | solution.py:91
  8.3 2.9 %collective-permute-start.12 = (bf16[64,1024]{1,0:T(8,128)(2,1)S(1)}, bf16[64,1024]{1,0:T(8,128)(2,1)S(1)}, u32[]{:S(2)}, u32[]{:S(2)}) collective-permute-start(bf16[64,1024]{1,0:T(8,128)(2,1)S(1)} %get-tuple-element.59), channel_id=1, source_target_pairs={{0,16},{4,20},{8,24},{12,28},{16,0},{20,4},{24,8},{28,12},{1,17},{... | collective-permute-start | bytes 393224 | tf_op jit(solution)/shard_map/ppermute | solution.py:91
  11.1 1.5 %collective-permute-start.6 = (bf16[64,1024]{1,0:T(8,128)(2,1)S(1)}, bf16[64,1024]{1,0:T(8,128)(2,1)S(1)}, u32[]{:S(2)}, u32[]{:S(2)}) collective-permute-start(bf16[64,1024]{1,0:T(8,128)(2,1)S(1)} %get-tuple-element.59), channel_id=1, source_target_pairs={{0,8},{4,12},{8,16},{12,20},{16,24},{20,28},{24,0},{28,4},{1,9},{5... | collective-permute-start | bytes 393224 | tf_op jit(solution)/shard_map/ppermute | solution.py:91
  14.3 1.0 copy-done.9
  18.7 7.4 %collective-permute-done.15 = bf16[64,1024]{1,0:T(8,128)(2,1)S(1)} collective-permute-done((bf16[64,1024]{1,0:T(8,128)(2,1)S(1)}, bf16[64,1024]{1,0:T(8,128)(2,1)S(1)}, u32[]{:S(2)}, u32[]{:S(2)}) %collective-permute-start.15) | collective-permute-done | bytes 131104 | tf_op jit(solution)/shard_map/ppermute | solution.py:91
  26.7 1.9 %collective-permute-done.12 = bf16[64,1024]{1,0:T(8,128)(2,1)S(1)} collective-permute-done((bf16[64,1024]{1,0:T(8,128)(2,1)S(1)}, bf16[64,1024]{1,0:T(8,128)(2,1)S(1)}, u32[]{:S(2)}, u32[]{:S(2)}) %collective-permute-start.12) | collective-permute-done | bytes 131104 | tf_op jit(solution)/shard_map/ppermute | solution.py:91
  28.6 1.5 %collective-permute-start.19 = (bf16[64,1024]{1,0:T(8,128)(2,1)S(1)}, bf16[64,1024]{1,0:T(8,128)(2,1)S(1)}, u32[]{:S(2)}, u32[]{:S(2)}) collective-permute-start(bf16[64,1024]{1,0:T(8,128)(2,1)S(1)} %collective-permute-done.18), channel_id=1, source_target_pairs={{0,2},{1,3},{2,0},{3,1},{4,6},{5,7},{6,4},{7,5},{8,10},{9,11},{10,... | collective-permute-start | bytes 393224 | tf_op jit(solution)/shard_map/ppermute | solution.py:78
  30.7 1.6 %collective-permute-start.13 = (bf16[64,1024]{1,0:T(8,128)(2,1)S(1)}, bf16[64,1024]{1,0:T(8,128)(2,1)S(1)}, u32[]{:S(2)}, u32[]{:S(2)}) collective-permute-start(bf16[64,1024]{1,0:T(8,128)(2,1)S(1)} %collective-permute-done.12), channel_id=1, source_target_pairs={{0,2},{1,3},{2,0},{3,1},{4,6},{5,7},{6,4},{7,5},{8,10},{9,11},{10,... | collective-permute-start | bytes 393224 | tf_op jit(solution)/shard_map/ppermute | solution.py:78
  33.0 1.6 %collective-permute-start.7 = (bf16[64,1024]{1,0:T(8,128)(2,1)S(1)}, bf16[64,1024]{1,0:T(8,128)(2,1)S(1)}, u32[]{:S(2)}, u32[]{:S(2)}) collective-permute-start(bf16[64,1024]{1,0:T(8,128)(2,1)S(1)} %collective-permute-done.6), channel_id=1, source_target_pairs={{0,2},{1,3},{2,0},{3,1},{4,6},{5,7},{6,4},{7,5},{8,10},{9,11},{10,... | collective-permute-start | bytes 393224 | tf_op jit(solution)/shard_map/ppermute | solution.py:78
  35.0 1.5 %collective-permute-start.4 = (bf16[64,1024]{1,0:T(8,128)(2,1)S(1)}, bf16[64,1024]{1,0:T(8,128)(2,1)S(1)}, u32[]{:S(2)}, u32[]{:S(2)}) collective-permute-start(bf16[64,1024]{1,0:T(8,128)(2,1)S(1)} %collective-permute-done.3), channel_id=1, source_target_pairs={{0,2},{1,3},{2,0},{3,1},{4,6},{5,7},{6,4},{7,5},{8,10},{9,11},{10,... | collective-permute-start | bytes 393224 | tf_op jit(solution)/shard_map/ppermute | solution.py:78
  37.9 1.5 %collective-permute-start.1 = (bf16[64,1024]{1,0:T(8,128)(2,1)S(1)}, bf16[64,1024]{1,0:T(8,128)(2,1)S(1)}, u32[]{:S(2)}, u32[]{:S(2)}) collective-permute-start(bf16[64,1024]{1,0:T(8,128)(2,1)S(1)} %collective-permute-done), channel_id=1, source_target_pairs={{0,2},{1,3},{2,0},{3,1},{4,6},{5,7},{6,4},{7,5},{8,10},{9,11},{10,... | collective-permute-start | bytes 393224 | tf_op jit(solution)/shard_map/ppermute | solution.py:78
  40.0 0.7 pad_maximum_fusion.7
  40.8 0.8 copy-done.20
  41.6 0.7 pad_maximum_fusion.6
  42.3 1.2 collective-permute-done.10
  43.5 0.8 pad_maximum_fusion.5
  44.3 2.0 %collective-permute-done.7 = bf16[64,1024]{1,0:T(8,128)(2,1)S(1)} collective-permute-done((bf16[64,1024]{1,0:T(8,128)(2,1)S(1)}, bf16[64,1024]{1,0:T(8,128)(2,1)S(1)}, u32[]{:S(2)}, u32[]{:S(2)}) %collective-permute-start.7) | collective-permute-done | bytes 131104 | tf_op jit(solution)/shard_map/ppermute | solution.py:78
  46.3 0.8 pad_maximum_fusion.4
  47.1 1.0 collective-permute-done.4
  48.1 1.4 collective-permute-done.1
  49.5 0.8 pad_maximum_fusion.1
  50.3 0.7 pad_maximum_fusion.3
  53.9 1.7 %constant_dynamic-update-slice_fusion.6 = bf16[256,1024]{1,0:T(8,128)(2,1)} fusion(bf16[256,1024]{1,0:T(8,128)(2,1)} %copy-done.16, bf16[128,1024]{1,0:T(8,128)(2,1)} %collective-permute-done.8), kind=kLoop, calls=%fused_computation.79 | loop fusion | bytes 524288 | tf_op jit(solution)/shard_map/concatenate | solution.py:79
  55.6 2.7 %fusion.24 = (f32[256]{0:T(256)S(1)}, f32[256,512]{1,0:T(8,128)}) fusion(f32[512]{0:T(512)S(1)} %get-tuple-element.57, bf16[256,1024]{1,0:T(8,128)(2,1)} %constant_dynamic-update-slice_fusion.6, bf16[512,1024]{1,0:T(8,128)(2,1)} %copy-done.9), kind=kOutput, calls=%fused_computation.130 | convolution fusion | flops 268959488 | bytes 2100224 | tf_op jit(solution)/shard_map/dot_general | solution.py:10
  59.0 1.7 %constant_dynamic-update-slice_fusion.9 = bf16[256,1024]{1,0:T(8,128)(2,1)} fusion(bf16[256,1024]{1,0:T(8,128)(2,1)} %copy-done.18, bf16[128,1024]{1,0:T(8,128)(2,1)} %collective-permute-done.11), kind=kLoop, calls=%fused_computation.82 | loop fusion | bytes 524288 | tf_op jit(solution)/shard_map/concatenate | solution.py:79
  60.7 2.7 %fusion.25 = (f32[256]{0:T(256)S(1)}, f32[256,512]{1,0:T(8,128)}) fusion(f32[512]{0:T(512)S(1)} %get-tuple-element.57, bf16[256,1024]{1,0:T(8,128)(2,1)} %constant_dynamic-update-slice_fusion.9, bf16[512,1024]{1,0:T(8,128)(2,1)} %copy-done.9), kind=kOutput, calls=%fused_computation.131 | convolution fusion | flops 268959488 | bytes 2100224 | tf_op jit(solution)/shard_map/dot_general | solution.py:10
  64.9 1.3 exponential_reduce_fusion.4
  66.9 1.7 %constant_dynamic-update-slice_fusion.12 = bf16[256,1024]{1,0:T(8,128)(2,1)} fusion(bf16[256,1024]{1,0:T(8,128)(2,1)} %copy-done.20, bf16[128,1024]{1,0:T(8,128)(2,1)} %collective-permute-done.14), kind=kLoop, calls=%fused_computation.85 | loop fusion | bytes 524288 | tf_op jit(solution)/shard_map/concatenate | solution.py:79
  68.6 2.7 %fusion.26 = (f32[256]{0:T(256)S(1)}, f32[256,512]{1,0:T(8,128)}) fusion(f32[512]{0:T(512)S(1)} %get-tuple-element.57, bf16[256,1024]{1,0:T(8,128)(2,1)} %constant_dynamic-update-slice_fusion.12, bf16[512,1024]{1,0:T(8,128)(2,1)} %copy-done.9), kind=kOutput, calls=%fused_computation.132 | convolution fusion | flops 268959488 | bytes 2100224 | tf_op jit(solution)/shard_map/dot_general | solution.py:10
  71.9 1.7 %constant_dynamic-update-slice_fusion.15 = bf16[256,1024]{1,0:T(8,128)(2,1)} fusion(bf16[256,1024]{1,0:T(8,128)(2,1)} %constant_dynamic-update-slice_fusion.16, bf16[128,1024]{1,0:T(8,128)(2,1)} %collective-permute-done.17), kind=kLoop, calls=%fused_computation.88 | loop fusion | bytes 524288 | tf_op jit(solution)/shard_map/concatenate | solution.py:79
  73.7 2.7 %fusion.27 = (f32[256]{0:T(256)S(1)}, f32[256,512]{1,0:T(8,128)}) fusion(f32[512]{0:T(512)S(1)} %get-tuple-element.57, bf16[256,1024]{1,0:T(8,128)(2,1)} %constant_dynamic-update-slice_fusion.15, bf16[512,1024]{1,0:T(8,128)(2,1)} %copy-done.9), kind=kOutput, calls=%fused_computation.133 | convolution fusion | flops 268959488 | bytes 2100224 | tf_op jit(solution)/shard_map/dot_general | solution.py:10
  77.9 1.3 exponential_reduce_fusion.2
  79.9 1.8 %constant_dynamic-update-slice_fusion.18 = bf16[256,1024]{1,0:T(8,128)(2,1)} fusion(bf16[256,1024]{1,0:T(8,128)(2,1)} %constant_dynamic-update-slice_fusion.19, bf16[128,1024]{1,0:T(8,128)(2,1)} %collective-permute-done.20), kind=kLoop, calls=%fused_computation.91 | loop fusion | bytes 524288 | tf_op jit(solution)/shard_map/concatenate | solution.py:79
  81.7 2.7 %fusion.29 = (f32[256]{0:T(256)S(1)}, f32[256,512]{1,0:T(8,128)}) fusion(f32[512]{0:T(512)S(1)} %get-tuple-element.57, bf16[256,1024]{1,0:T(8,128)(2,1)} %constant_dynamic-update-slice_fusion.18, bf16[512,1024]{1,0:T(8,128)(2,1)} %copy-done.9), kind=kOutput, calls=%fused_computation.135 | convolution fusion | flops 268959488 | bytes 2100224 | tf_op jit(solution)/shard_map/dot_general | solution.py:10
  84.3 1.0 constant_dynamic-update-slice_fusion
  85.3 1.3 fusion.28
  87.3 1.3 exponential_reduce_fusion
  89.9 1.3 exponential_reduce_fusion.1
  91.8 0.7 concatenate.115
  92.5 1.4 concatenate.124
  93.9 0.8 select_reduce_fusion.7
  94.7 0.8 select_reduce_fusion.3
  95.6 9.5 %all-gather = f32[16,8,4,64]{3,1,2,0:T(8,128)S(1)} all-gather(f32[2,8,4,64]{3,1,2,0:T(8,128)S(1)} %copy.15), channel_id=2, replica_groups=mesh['outer'=4,'dp'=2,'cent'=4] {'dp','cent'}, dimensions={0}, use_global_device_ids=true | all-gather | bytes 147456 | tf_op jit(solution)/shard_map/all_gather | solution.py:114
  105.1 0.8 select_reduce_fusion.1
  105.9 0.8 select_reduce_fusion.5
  107.4 1.3 div.139
  108.7 1.3 div.136
  110.0 1.3 div.133
  111.3 1.3 div.130
  112.6 1.2 div.127
  113.9 1.3 div.124
  115.1 1.3 div.121
  116.5 1.4 div.118
  117.8 1.3 sub.264
  119.1 1.3 sub.269
  120.4 1.3 sub.272
  121.8 1.3 sub.275
  124.5 0.9 convert_reduce_fusion.1
  125.4 1.4 fusion.19
  129.2 1.6 %fusion.33 = f32[512,1024]{1,0:T(8,128)S(1)} fusion(bf16[256,512]{1,0:T(8,128)(2,1)S(1)} %get-tuple-element.50, bf16[256,1024]{1,0:T(8,128)(2,1)} %constant_dynamic-update-slice_fusion.15), kind=kOutput, calls=%fused_computation.139 | convolution fusion | flops 268435456 | bytes 2883584 | tf_op jit(solution)/shard_map/dot_general | solution.py:129
  132.1 1.6 %fusion.31 = f32[512,1024]{1,0:T(8,128)S(1)} fusion(bf16[256,512]{1,0:T(8,128)(2,1)S(1)} %get-tuple-element.54, bf16[256,1024]{1,0:T(8,128)(2,1)} %constant_dynamic-update-slice_fusion.18), kind=kOutput, calls=%fused_computation.137 | convolution fusion | flops 268435456 | bytes 2883584 | tf_op jit(solution)/shard_map/dot_general | solution.py:129
  134.8 4.1 %add_multiply_fusion = f32[512,1024]{1,0:T(8,128)} fusion(f32[512,1024]{1,0:T(8,128)S(1)} %copy-done, f32[512,1024]{1,0:T(8,128)S(1)} %fusion.19, f32[512,1024]{1,0:T(8,128)S(1)} %fusion.34, f32[512,1024]{1,0:T(8,128)S(1)} %fusion.35, f32[512,1024]{1,0:T(8,128)S(1)} %fusion.32, f32[512,1024]{1,0:T(8,128)S(1)} %fusion.33, f32[512,1024]{1,0:T(8,128)S(1)} %fusion.30, ...), kind=kOutput, calls=%fused_computation | convolution fusion | flops 285212672 | bytes 19677196 | tf_op jit(solution)/shard_map/dot_general | solution.py:129
  (173 shorter events, 27.7 us)
Async XLA Ops:
  0.0 14.0 %copy-start = (f32[512,1024]{1,0:T(8,128)S(1)}, f32[512,1024]{1,0:T(8,128)}, u32[]{:S(2)}) copy-start(f32[512,1024]{1,0:T(8,128)} %param.3) | copy-start | bytes 6291460
  2.2 15.2 %collective-permute-start.18 = (bf16[64,1024]{1,0:T(8,128)(2,1)S(1)}, bf16[64,1024]{1,0:T(8,128)(2,1)S(1)}, u32[]{:S(2)}, u32[]{:S(2)}) collective-permute-start(bf16[64,1024]{1,0:T(8,128)(2,1)S(1)} %get-tuple-element.59), channel_id=1, source_target_pairs={{0,28},{4,24},{8,4},{12,0},{16,12},{20,8},{24,20},{28,16},{1,29},{... | collective-permute-start | bytes 393224 | tf_op jit(solution)/shard_map/ppermute | solution.py:91
  8.2 17.8 %collective-permute-start.15 = (bf16[64,1024]{1,0:T(8,128)(2,1)S(1)}, bf16[64,1024]{1,0:T(8,128)(2,1)S(1)}, u32[]{:S(2)}, u32[]{:S(2)}) collective-permute-start(bf16[64,1024]{1,0:T(8,128)(2,1)S(1)} %get-tuple-element.59), channel_id=1, source_target_pairs={{0,20},{4,16},{8,28},{12,24},{16,4},{20,0},{24,12},{28,8},{1,21},{... | collective-permute-start | bytes 393224 | tf_op jit(solution)/shard_map/ppermute | solution.py:91
  8.3 20.4 %collective-permute-start.12 = (bf16[64,1024]{1,0:T(8,128)(2,1)S(1)}, bf16[64,1024]{1,0:T(8,128)(2,1)S(1)}, u32[]{:S(2)}, u32[]{:S(2)}) collective-permute-start(bf16[64,1024]{1,0:T(8,128)(2,1)S(1)} %get-tuple-element.59), channel_id=1, source_target_pairs={{0,16},{4,20},{8,24},{12,28},{16,0},{20,4},{24,8},{28,12},{1,17},{... | collective-permute-start | bytes 393224 | tf_op jit(solution)/shard_map/ppermute | solution.py:91
  11.1 19.0 %collective-permute-start.9 = (bf16[64,1024]{1,0:T(8,128)(2,1)S(1)}, bf16[64,1024]{1,0:T(8,128)(2,1)S(1)}, u32[]{:S(2)}, u32[]{:S(2)}) collective-permute-start(bf16[64,1024]{1,0:T(8,128)(2,1)S(1)} %get-tuple-element.59), channel_id=1, source_target_pairs={{0,12},{4,8},{8,20},{12,16},{16,28},{20,24},{24,4},{28,0},{1,13},{... | collective-permute-start | bytes 393224 | tf_op jit(solution)/shard_map/ppermute | solution.py:91
  11.1 19.6 %collective-permute-start.6 = (bf16[64,1024]{1,0:T(8,128)(2,1)S(1)}, bf16[64,1024]{1,0:T(8,128)(2,1)S(1)}, u32[]{:S(2)}, u32[]{:S(2)}) collective-permute-start(bf16[64,1024]{1,0:T(8,128)(2,1)S(1)} %get-tuple-element.59), channel_id=1, source_target_pairs={{0,8},{4,12},{8,16},{12,20},{16,24},{20,28},{24,0},{28,4},{1,9},{5... | collective-permute-start | bytes 393224 | tf_op jit(solution)/shard_map/ppermute | solution.py:91
  13.4 1.9 %copy-start.22 = (bf16[64,1024]{1,0:T(8,128)(2,1)S(1)}, bf16[64,1024]{1,0:T(8,128)(2,1)}, u32[]{:S(2)}) copy-start(bf16[64,1024]{1,0:T(8,128)(2,1)} %get-tuple-element.61) | copy-start | bytes 393220
  13.4 1.9 %copy-start.24 = (bf16[64,1024]{1,0:T(8,128)(2,1)S(1)}, bf16[64,1024]{1,0:T(8,128)(2,1)}, u32[]{:S(2)}) copy-start(bf16[64,1024]{1,0:T(8,128)(2,1)} %get-tuple-element.62) | copy-start | bytes 393220
  14.3 1.0 copy-start.9
  17.5 14.8 %collective-permute-start.3 = (bf16[64,1024]{1,0:T(8,128)(2,1)S(1)}, bf16[64,1024]{1,0:T(8,128)(2,1)S(1)}, u32[]{:S(2)}, u32[]{:S(2)}) collective-permute-start(bf16[64,1024]{1,0:T(8,128)(2,1)S(1)} %get-tuple-element.59), channel_id=1, source_target_pairs={{0,4},{4,0},{8,12},{12,8},{16,20},{20,16},{24,28},{28,24},{1,5},{5... | collective-permute-start | bytes 393224 | tf_op jit(solution)/shard_map/ppermute | solution.py:91
  26.0 6.9 %collective-permute-start = (bf16[64,1024]{1,0:T(8,128)(2,1)S(1)}, bf16[64,1024]{1,0:T(8,128)(2,1)S(1)}, u32[]{:S(2)}, u32[]{:S(2)}) collective-permute-start(bf16[64,1024]{1,0:T(8,128)(2,1)S(1)} %get-tuple-element.59), channel_id=1, source_target_pairs={{0,24},{4,28},{8,0},{12,4},{16,8},{20,12},{24,16},{28,20},{1,25},{... | collective-permute-start | bytes 393224 | tf_op jit(solution)/shard_map/ppermute | solution.py:91
  28.6 6.4 %collective-permute-start.19 = (bf16[64,1024]{1,0:T(8,128)(2,1)S(1)}, bf16[64,1024]{1,0:T(8,128)(2,1)S(1)}, u32[]{:S(2)}, u32[]{:S(2)}) collective-permute-start(bf16[64,1024]{1,0:T(8,128)(2,1)S(1)} %collective-permute-done.18), channel_id=1, source_target_pairs={{0,2},{1,3},{2,0},{3,1},{4,6},{5,7},{6,4},{7,5},{8,10},{9,11},{10,... | collective-permute-start | bytes 393224 | tf_op jit(solution)/shard_map/ppermute | solution.py:78
  30.1 7.7 %collective-permute-start.16 = (bf16[64,1024]{1,0:T(8,128)(2,1)S(1)}, bf16[64,1024]{1,0:T(8,128)(2,1)S(1)}, u32[]{:S(2)}, u32[]{:S(2)}) collective-permute-start(bf16[64,1024]{1,0:T(8,128)(2,1)S(1)} %collective-permute-done.15), channel_id=1, source_target_pairs={{0,2},{1,3},{2,0},{3,1},{4,6},{5,7},{6,4},{7,5},{8,10},{9,11},{10,... | collective-permute-start | bytes 393224 | tf_op jit(solution)/shard_map/ppermute | solution.py:78
  30.7 10.0 %collective-permute-start.13 = (bf16[64,1024]{1,0:T(8,128)(2,1)S(1)}, bf16[64,1024]{1,0:T(8,128)(2,1)S(1)}, u32[]{:S(2)}, u32[]{:S(2)}) collective-permute-start(bf16[64,1024]{1,0:T(8,128)(2,1)S(1)} %collective-permute-done.12), channel_id=1, source_target_pairs={{0,2},{1,3},{2,0},{3,1},{4,6},{5,7},{6,4},{7,5},{8,10},{9,11},{10,... | collective-permute-start | bytes 393224 | tf_op jit(solution)/shard_map/ppermute | solution.py:78
  32.3 11.1 %collective-permute-start.10 = (bf16[64,1024]{1,0:T(8,128)(2,1)S(1)}, bf16[64,1024]{1,0:T(8,128)(2,1)S(1)}, u32[]{:S(2)}, u32[]{:S(2)}) collective-permute-start(bf16[64,1024]{1,0:T(8,128)(2,1)S(1)} %collective-permute-done.9), channel_id=1, source_target_pairs={{0,2},{1,3},{2,0},{3,1},{4,6},{5,7},{6,4},{7,5},{8,10},{9,11},{10,... | collective-permute-start | bytes 393224 | tf_op jit(solution)/shard_map/ppermute | solution.py:78
  33.0 13.3 %collective-permute-start.7 = (bf16[64,1024]{1,0:T(8,128)(2,1)S(1)}, bf16[64,1024]{1,0:T(8,128)(2,1)S(1)}, u32[]{:S(2)}, u32[]{:S(2)}) collective-permute-start(bf16[64,1024]{1,0:T(8,128)(2,1)S(1)} %collective-permute-done.6), channel_id=1, source_target_pairs={{0,2},{1,3},{2,0},{3,1},{4,6},{5,7},{6,4},{7,5},{8,10},{9,11},{10,... | collective-permute-start | bytes 393224 | tf_op jit(solution)/shard_map/ppermute | solution.py:78
  35.0 13.0 %collective-permute-start.4 = (bf16[64,1024]{1,0:T(8,128)(2,1)S(1)}, bf16[64,1024]{1,0:T(8,128)(2,1)S(1)}, u32[]{:S(2)}, u32[]{:S(2)}) collective-permute-start(bf16[64,1024]{1,0:T(8,128)(2,1)S(1)} %collective-permute-done.3), channel_id=1, source_target_pairs={{0,2},{1,3},{2,0},{3,1},{4,6},{5,7},{6,4},{7,5},{8,10},{9,11},{10,... | collective-permute-start | bytes 393224 | tf_op jit(solution)/shard_map/ppermute | solution.py:78
  37.9 11.6 %collective-permute-start.1 = (bf16[64,1024]{1,0:T(8,128)(2,1)S(1)}, bf16[64,1024]{1,0:T(8,128)(2,1)S(1)}, u32[]{:S(2)}, u32[]{:S(2)}) collective-permute-start(bf16[64,1024]{1,0:T(8,128)(2,1)S(1)} %collective-permute-done), channel_id=1, source_target_pairs={{0,2},{1,3},{2,0},{3,1},{4,6},{5,7},{6,4},{7,5},{8,10},{9,11},{10,... | collective-permute-start | bytes 393224 | tf_op jit(solution)/shard_map/ppermute | solution.py:78
  40.7 39.1 %collective-permute-start.20 = (bf16[128,1024]{1,0:T(8,128)(2,1)}, bf16[128,1024]{1,0:T(8,128)(2,1)}, u32[]{:S(2)}, u32[]{:S(2)}) collective-permute-start(bf16[128,1024]{1,0:T(8,128)(2,1)} %pad_maximum_fusion.7), channel_id=1, source_target_pairs={{0,1},{1,0},{2,3},{3,2},{4,5},{5,4},{6,7},{7,6},{8,9},{9,8},{10,11... | collective-permute-start | bytes 786440 | tf_op jit(solution)/shard_map/ppermute | solution.py:78
  40.8 0.8 copy-start.20
  42.3 9.2 %copy-start.10 = (bf16[512,1024]{1,0:T(8,128)(2,1)S(1)}, bf16[512,1024]{1,0:T(8,128)(2,1)}, u32[]{:S(2)}) copy-start(bf16[512,1024]{1,0:T(8,128)(2,1)} %copy-done.9) | copy-start | bytes 3145732
  43.5 28.4 %collective-permute-start.17 = (bf16[128,1024]{1,0:T(8,128)(2,1)}, bf16[128,1024]{1,0:T(8,128)(2,1)}, u32[]{:S(2)}, u32[]{:S(2)}) collective-permute-start(bf16[128,1024]{1,0:T(8,128)(2,1)} %pad_maximum_fusion.6), channel_id=1, source_target_pairs={{0,1},{1,0},{2,3},{3,2},{4,5},{5,4},{6,7},{7,6},{8,9},{9,8},{10,11... | collective-permute-start | bytes 786440 | tf_op jit(solution)/shard_map/ppermute | solution.py:78
  43.5 8.0 %copy-start.18 = (bf16[256,1024]{1,0:T(8,128)(2,1)}, bf16[256,1024]{1,0:T(8,128)(2,1)S(1)}, u32[]{:S(2)}) copy-start(bf16[256,1024]{1,0:T(8,128)(2,1)S(1)} %constant_dynamic-update-slice_fusion.10) | copy-start | bytes 1572868
  46.3 20.6 %collective-permute-start.14 = (bf16[128,1024]{1,0:T(8,128)(2,1)}, bf16[128,1024]{1,0:T(8,128)(2,1)}, u32[]{:S(2)}, u32[]{:S(2)}) collective-permute-start(bf16[128,1024]{1,0:T(8,128)(2,1)} %pad_maximum_fusion.5), channel_id=1, source_target_pairs={{0,1},{1,0},{2,3},{3,2},{4,5},{5,4},{6,7},{7,6},{8,9},{9,8},{10,11... | collective-permute-start | bytes 786440 | tf_op jit(solution)/shard_map/ppermute | solution.py:78
  46.3 5.2 %copy-start.16 = (bf16[256,1024]{1,0:T(8,128)(2,1)}, bf16[256,1024]{1,0:T(8,128)(2,1)S(1)}, u32[]{:S(2)}) copy-start(bf16[256,1024]{1,0:T(8,128)(2,1)S(1)} %constant_dynamic-update-slice_fusion.7) | copy-start | bytes 1572868
  48.1 10.9 %collective-permute-start.11 = (bf16[128,1024]{1,0:T(8,128)(2,1)}, bf16[128,1024]{1,0:T(8,128)(2,1)}, u32[]{:S(2)}, u32[]{:S(2)}) collective-permute-start(bf16[128,1024]{1,0:T(8,128)(2,1)} %pad_maximum_fusion.4), channel_id=1, source_target_pairs={{0,1},{1,0},{2,3},{3,2},{4,5},{5,4},{6,7},{7,6},{8,9},{9,8},{10,11... | collective-permute-start | bytes 786440 | tf_op jit(solution)/shard_map/ppermute | solution.py:78
  49.5 1.5 %collective-permute-start.5 = (bf16[128,1024]{1,0:T(8,128)(2,1)S(1)}, bf16[128,1024]{1,0:T(8,128)(2,1)S(1)}, u32[]{:S(2)}, u32[]{:S(2)}) collective-permute-start(bf16[128,1024]{1,0:T(8,128)(2,1)S(1)} %pad_maximum_fusion.2), channel_id=1, source_target_pairs={{0,1},{1,0},{2,3},{3,2},{4,5},{5,4},{6,7},{7,6},{8,9},{9,8},{10,11... | collective-permute-start | bytes 786440 | tf_op jit(solution)/shard_map/ppermute | solution.py:78
  49.5 2.0 %copy-start.12 = (bf16[256,1024]{1,0:T(8,128)(2,1)}, bf16[256,1024]{1,0:T(8,128)(2,1)S(1)}, u32[]{:S(2)}) copy-start(bf16[256,1024]{1,0:T(8,128)(2,1)S(1)} %constant_dynamic-update-slice_fusion.1) | copy-start | bytes 1572868
  51.0 2.9 %collective-permute-start.8 = (bf16[128,1024]{1,0:T(8,128)(2,1)}, bf16[128,1024]{1,0:T(8,128)(2,1)}, u32[]{:S(2)}, u32[]{:S(2)}) collective-permute-start(bf16[128,1024]{1,0:T(8,128)(2,1)} %pad_maximum_fusion.3), channel_id=1, source_target_pairs={{0,1},{1,0},{2,3},{3,2},{4,5},{5,4},{6,7},{7,6},{8,9},{9,8},{10,11... | collective-permute-start | bytes 786440 | tf_op jit(solution)/shard_map/ppermute | solution.py:78
  51.5 0.8 copy-start.25
  53.9 30.4 %collective-permute-start.2 = (bf16[128,1024]{1,0:T(8,128)(2,1)}, bf16[128,1024]{1,0:T(8,128)(2,1)}, u32[]{:S(2)}, u32[]{:S(2)}) collective-permute-start(bf16[128,1024]{1,0:T(8,128)(2,1)} %pad_maximum_fusion.1), channel_id=1, source_target_pairs={{0,1},{1,0},{2,3},{3,2},{4,5},{5,4},{6,7},{7,6},{8,9},{9,8},{10,11... | collective-permute-start | bytes 786440 | tf_op jit(solution)/shard_map/ppermute | solution.py:78
  59.0 4.4 %copy-start.1 = (f32[256,512]{1,0:T(8,128)S(1)}, f32[256,512]{1,0:T(8,128)}, u32[]{:S(2)}) copy-start(f32[256,512]{1,0:T(8,128)} %get-tuple-element.72) | copy-start | bytes 1572868
  71.9 4.4 %copy-start.3 = (f32[256,512]{1,0:T(8,128)S(1)}, f32[256,512]{1,0:T(8,128)}, u32[]{:S(2)}) copy-start(f32[256,512]{1,0:T(8,128)} %get-tuple-element.76) | copy-start | bytes 1572868
  79.9 4.5 %copy-start.13 = (bf16[256,1024]{1,0:T(8,128)(2,1)S(1)}, bf16[256,1024]{1,0:T(8,128)(2,1)}, u32[]{:S(2)}) copy-start(bf16[256,1024]{1,0:T(8,128)(2,1)} %copy-done.12) | copy-start | bytes 1572868
  79.9 5.4 %copy-start.11 = (bf16[512,1024]{1,0:T(8,128)(2,1)S(1)}, bf16[512,1024]{1,0:T(8,128)(2,1)}, u32[]{:S(2)}) copy-start(bf16[512,1024]{1,0:T(8,128)(2,1)} %copy-done.9) | copy-start | bytes 3145732
  85.3 1.3 copy-start.14
  86.6 38.8 %copy-start.23 = (bf16[64,1024]{1,0:T(8,128)(2,1)S(1)}, bf16[64,1024]{1,0:T(8,128)(2,1)}, u32[]{:S(2)}) copy-start(bf16[64,1024]{1,0:T(8,128)(2,1)} %get-tuple-element.61) | copy-start | bytes 393220
  123.7 3.1 %copy-start.37 = (f32[256]{0:T(256)S(1)}, f32[256]{0:T(256)}, u32[]{:S(2)}) copy-start(f32[256]{0:T(256)} %div.133) | copy-start | bytes 3076
  124.5 2.3 %copy-start.5 = (f32[256,512]{1,0:T(8,128)S(1)}, f32[256,512]{1,0:T(8,128)}, u32[]{:S(2)}) copy-start(f32[256,512]{1,0:T(8,128)} %get-tuple-element.74) | copy-start | bytes 1572868
  124.5 2.3 %copy-start.39 = (f32[256]{0:T(256)S(1)}, f32[256]{0:T(256)}, u32[]{:S(2)}) copy-start(f32[256]{0:T(256)} %sub.281) | copy-start | bytes 3076
  124.5 2.6 %copy-start.19 = (bf16[256,1024]{1,0:T(8,128)(2,1)S(1)}, bf16[256,1024]{1,0:T(8,128)(2,1)}, u32[]{:S(2)}) copy-start(bf16[256,1024]{1,0:T(8,128)(2,1)} %constant_dynamic-update-slice_fusion.9) | copy-start | bytes 1572868
  126.8 1.0 copy-start.2
  126.8 1.0 copy-start.35
  126.9 1.0 copy-start.38
  126.9 1.2 copy-start.17
  127.9 1.1 copy-start.6
  127.9 1.1 copy-start.33
  127.9 1.1 copy-start.36
  129.0 1.8 %copy-start.4 = (f32[256,512]{1,0:T(8,128)S(1)}, f32[256,512]{1,0:T(8,128)}, u32[]{:S(2)}) copy-start(f32[256,512]{1,0:T(8,128)} %get-tuple-element.76) | copy-start | bytes 1572868
  129.0 1.9 %copy-start.32 = (f32[256]{0:T(256)S(1)}, f32[256]{0:T(256)}, u32[]{:S(2)}) copy-start(f32[256]{0:T(256)} %div.124) | copy-start | bytes 3076
  129.0 1.9 %copy-start.34 = (f32[256]{0:T(256)S(1)}, f32[256]{0:T(256)}, u32[]{:S(2)}) copy-start(f32[256]{0:T(256)} %sub.272) | copy-start | bytes 3076
  129.0 2.1 %copy-start.21 = (bf16[256,1024]{1,0:T(8,128)(2,1)S(1)}, bf16[256,1024]{1,0:T(8,128)(2,1)}, u32[]{:S(2)}) copy-start(bf16[256,1024]{1,0:T(8,128)(2,1)} %constant_dynamic-update-slice_fusion.12) | copy-start | bytes 1572868
  130.8 1.0 copy-start.7
  130.8 1.0 copy-start.30
  130.9 1.0 copy-start.31
  131.9 1.8 %copy-start.8 = (f32[256,512]{1,0:T(8,128)S(1)}, f32[256,512]{1,0:T(8,128)}, u32[]{:S(2)}) copy-start(f32[256,512]{1,0:T(8,128)} %get-tuple-element.80) | copy-start | bytes 1572868
  131.9 1.9 %copy-start.28 = (f32[256]{0:T(256)S(1)}, f32[256]{0:T(256)}, u32[]{:S(2)}) copy-start(f32[256]{0:T(256)} %div.118) | copy-start | bytes 3076
  131.9 1.9 %copy-start.29 = (f32[256]{0:T(256)S(1)}, f32[256]{0:T(256)}, u32[]{:S(2)}) copy-start(f32[256]{0:T(256)} %sub.264) | copy-start | bytes 3076
  131.9 2.1 %copy-start.15 = (bf16[256,1024]{1,0:T(8,128)(2,1)S(1)}, bf16[256,1024]{1,0:T(8,128)(2,1)}, u32[]{:S(2)}) copy-start(bf16[256,1024]{1,0:T(8,128)(2,1)} %copy-done.14) | copy-start | bytes 1572868
  133.8 0.7 copy-start.27
  133.8 1.0 copy-start.26

commit v4 on v3

--- a/solution.py
+++ b/solution.py
@@ -66,34 +66,22 @@
     for bit in reversed(bits):
         xs = xs + [x ^ bit for x in xs]
 
-    def quarter_of(x):
-        return lax.dynamic_slice_in_dim(rows_bf, (q ^ x) * tq, tq, 0)
-
-    own = jnp.concatenate([quarter_of(x) for x in xs], axis=0)
-    mine = quarter_of(0)
-
-    def spread(piece):
-        cur = piece
-        for bit in reversed(bits):
-            other = lax.ppermute(cur, "cent", [(i, i ^ bit) for i in range(n_c)])
-            cur = jnp.concatenate([cur, other], axis=0)
-        return cur
-
+    mine = lax.dynamic_slice_in_dim(rows_bf, q * tq, tq, 0)
     shifts = list(itertools.product(range(n_o), range(n_d)))
-    blocks = []
-    for sz, sy in shifts:
-        if (sz, sy) == (0, 0):
-            blocks.append(own)
-            continue
+    slots = [mine]
+    for sz, sy in shifts[1:]:
         perm = []
         for i, j in itertools.product(range(n_o), range(n_d)):
             perm.append((i * n_d + j, ((i + sz) % n_o) * n_d + (j + sy) % n_d))
-        blocks.append(spread(lax.ppermute(mine, ("outer", "dp"), perm)))
+        slots.append(lax.ppermute(mine, ("outer", "dp"), perm))
+    cur = jnp.stack(slots)
+    for bit in reversed(bits):
+        other = lax.ppermute(cur, "cent", [(i, i ^ bit) for i in range(n_c)])
+        cur = jnp.concatenate([cur, other], axis=1)
+    everything = cur.reshape(n_od * n_c * tq, d)
 
-    logits = [scores_for(blk, cent_bf, squares) for blk in blocks]
-    summaries = [row_summary(lg) for lg in logits]
-    local_max = jnp.concatenate([s[0] for s in summaries])
-    local_sum = jnp.concatenate([s[1] for s in summaries])
+    logits = scores_for(everything, cent_bf, squares)
+    local_max, local_sum = row_summary(logits)
 
     src_vec = jnp.stack([((z - sz) % n_o) * n_d + (y - sy) % n_d for sz, sy in shifts])
     hot_k = src_vec[None, :] == jnp.arange(n_od)[:, None]
@@ -118,19 +106,15 @@
     row_peak = to_local(peak_abs)
     row_mass = to_local(mass_abs)
 
-    blk = n_c * tq
-    weight_sum = [None] * n_o
-    pull = [None] * n_o
-    for k, (sz, sy) in enumerate(shifts):
-        pk = row_peak[k * blk:(k + 1) * blk]
-        mk = row_mass[k * blk:(k + 1) * blk]
-        w = (jnp.exp(logits[k] - pk[:, None]) / mk[:, None]).astype(jnp.bfloat16)
-        ws = jnp.sum(w.astype(jnp.float32), axis=0)
-        pl = lax.dot_general(
-            w, blocks[k], (((0,), (0,)), ((), ())), preferred_element_type=jnp.float32
-        )
-        weight_sum[sz] = ws if weight_sum[sz] is None else weight_sum[sz] + ws
-        pull[sz] = pl if pull[sz] is None else pull[sz] + pl
+    weights = (jnp.exp(logits - row_peak[:, None]) / row_mass[:, None]).astype(jnp.bfloat16)
+    k = centroids.shape[0]
+    pod = n_d * n_c * tq
+    w_pods = weights.reshape(n_o, pod, k)
+    r_pods = everything.reshape(n_o, pod, d)
+    weight_sum = jnp.sum(w_pods.astype(jnp.float32), axis=1)
+    pull = lax.dot_general(
+        w_pods, r_pods, (((1,), (1,)), ((0,), (0,))), preferred_element_type=jnp.float32
+    )
 
     total = None
     for a in range(n_o):

time: 140 us -> 90.7 us (0.65)
  the two profiles are of different devices: /device:TPU:0 before, /device:TPU:11 now
where the time goes in v4:
time: 90.7 us; the launch traced here: 90.5 us
  waiting for transfers between devices  45.5 us (50%)
  other arithmetic  14.1 us (16%)
  starting transfers between devices  11 us (12%)
  blocking collectives  9.53 us (11%)
  matrix products  7.12 us (8%)
  local copies, waits for them, and re-layouts  3.02 us (3%)
    ppermute x2, waiting for transfers between devices, shards_all(): other = lax.ppermute(cur, 'cent', [(i, i ^ bit) for i in range(n_c)])  27.7 us
    ppermute x7, waiting for transfers between devices, shards_all(): slots.append(lax.ppermute(mine, ('outer', 'dp'), perm))  17.8 us
    all_gather x1, blocking collectives, shards_all(): every = lax.all_gather(both, ('dp', 'cent'), axis=0)  9.53 us
    ppermute x7, starting transfers between devices, shards_all(): slots.append(lax.ppermute(mine, ('outer', 'dp'), perm))  9.29 us
    dot_general x1, matrix products, scores_for(): lax.dot_general(piece, cent_bf, (((1,), (1,)), ((), ())), preferred_eleme...  4.69 us
    div x1, other arithmetic, shards_all(): return total / n_o  3.73 us
    concatenate x2, other arithmetic, shards_all(): cur = jnp.concatenate([cur, other], axis=1)  3.36 us
    reduce_sum x1, other arithmetic, row_summary(): local_sum = jnp.sum(jnp.exp(logits - local_max[:, None]), axis=1)  3.31 us
  transfers between devices with their start and end apart: 9, of which 6 were waited for; matrix products, arithmetic and copies ran while one was open for 0% of the time, Pallas kernels for 0%

profile of v4, /device:TPU:11, one launch (start us, length us, event | category | flops | bytes accessed | tf_op | source)
XLA Modules:
  0.0 90.5 jit_solution(4124552051522448741)
XLA Ops:
  0.0 1.0 %bitcast_dynamic-update-slice_fusion.7 = (bf16[8,64,1024]{2,1,0:T(8,128)(2,1)S(1)}, bf16[64,1024]{1,0:T(8,128)(2,1)S(1)}) fusion(f32[256,1024]{1,0:T(8,128)} %param.2, s32[]{:T(128)S(6)} %select_n.360), kind=kLoop, calls=%fused_computation.34 | loop fusion | bytes 393220
  1.0 1.3 %collective-permute-start = (bf16[64,1024]{1,0:T(8,128)(2,1)S(1)}, bf16[64,1024]{1,0:T(8,128)(2,1)S(1)}, u32[]{:S(2)}, u32[]{:S(2)}) collective-permute-start(bf16[64,1024]{1,0:T(8,128)(2,1)S(1)} %get-tuple-element.16), channel_id=1, source_target_pairs={{0,4},{4,0},{8,12},{12,8},{16,20},{20,16},{24,28},{28,24},{1,5},{5... | collective-permute-start | bytes 393224 | tf_op jit(solution)/shard_map/ppermute | solution.py:76
  2.3 1.3 %collective-permute-start.1 = (bf16[64,1024]{1,0:T(8,128)(2,1)S(1)}, bf16[64,1024]{1,0:T(8,128)(2,1)S(1)}, u32[]{:S(2)}, u32[]{:S(2)}) collective-permute-start(bf16[64,1024]{1,0:T(8,128)(2,1)S(1)} %get-tuple-element.16), channel_id=1, source_target_pairs={{0,8},{4,12},{8,16},{12,20},{16,24},{20,28},{24,0},{28,4},{1,9},{5... | collective-permute-start | bytes 393224 | tf_op jit(solution)/shard_map/ppermute | solution.py:76
  3.6 1.2 %collective-permute-start.2 = (bf16[64,1024]{1,0:T(8,128)(2,1)S(1)}, bf16[64,1024]{1,0:T(8,128)(2,1)S(1)}, u32[]{:S(2)}, u32[]{:S(2)}) collective-permute-start(bf16[64,1024]{1,0:T(8,128)(2,1)S(1)} %get-tuple-element.16), channel_id=1, source_target_pairs={{0,12},{4,8},{8,20},{12,16},{16,28},{20,24},{24,4},{28,0},{1,13},{... | collective-permute-start | bytes 393224 | tf_op jit(solution)/shard_map/ppermute | solution.py:76
  4.8 1.0 %collective-permute-start.3 = (bf16[64,1024]{1,0:T(8,128)(2,1)S(1)}, bf16[64,1024]{1,0:T(8,128)(2,1)S(1)}, u32[]{:S(2)}, u32[]{:S(2)}) collective-permute-start(bf16[64,1024]{1,0:T(8,128)(2,1)S(1)} %get-tuple-element.16), channel_id=1, source_target_pairs={{0,16},{4,20},{8,24},{12,28},{16,0},{20,4},{24,8},{28,12},{1,17},{... | collective-permute-start | bytes 393224 | tf_op jit(solution)/shard_map/ppermute | solution.py:76
  5.8 2.4 %collective-permute-start.4 = (bf16[64,1024]{1,0:T(8,128)(2,1)S(1)}, bf16[64,1024]{1,0:T(8,128)(2,1)S(1)}, u32[]{:S(2)}, u32[]{:S(2)}) collective-permute-start(bf16[64,1024]{1,0:T(8,128)(2,1)S(1)} %get-tuple-element.16), channel_id=1, source_target_pairs={{0,20},{4,16},{8,28},{12,24},{16,4},{20,0},{24,12},{28,8},{1,21},{... | collective-permute-start | bytes 393224 | tf_op jit(solution)/shard_map/ppermute | solution.py:76
  8.1 0.0 collective-permute-done
  8.1 0.2 collective-permute-start.5
  8.3 0.0 collective-permute-done.1
  8.3 2.0 %collective-permute-start.6 = (bf16[64,1024]{1,0:T(8,128)(2,1)S(1)}, bf16[64,1024]{1,0:T(8,128)(2,1)S(1)}, u32[]{:S(2)}, u32[]{:S(2)}) collective-permute-start(bf16[64,1024]{1,0:T(8,128)(2,1)S(1)} %get-tuple-element.16), channel_id=1, source_target_pairs={{0,28},{4,24},{8,4},{12,0},{16,12},{20,8},{24,20},{28,16},{1,29},{... | collective-permute-start | bytes 393224 | tf_op jit(solution)/shard_map/ppermute | solution.py:76
  10.3 0.0 collective-permute-done.2
  10.3 11.9 %collective-permute-done.3 = bf16[64,1024]{1,0:T(8,128)(2,1)S(1)} collective-permute-done((bf16[64,1024]{1,0:T(8,128)(2,1)S(1)}, bf16[64,1024]{1,0:T(8,128)(2,1)S(1)}, u32[]{:S(2)}, u32[]{:S(2)}) %collective-permute-start.3) | collective-permute-done | bytes 131104 | tf_op jit(solution)/shard_map/ppermute | solution.py:76
  22.3 2.8 %collective-permute-done.4 = bf16[64,1024]{1,0:T(8,128)(2,1)S(1)} collective-permute-done((bf16[64,1024]{1,0:T(8,128)(2,1)S(1)}, bf16[64,1024]{1,0:T(8,128)(2,1)S(1)}, u32[]{:S(2)}, u32[]{:S(2)}) %collective-permute-start.4) | collective-permute-done | bytes 131104 | tf_op jit(solution)/shard_map/ppermute | solution.py:76
  25.1 0.3 collective-permute-done.5
  25.4 2.7 %collective-permute-done.6 = bf16[64,1024]{1,0:T(8,128)(2,1)S(1)} collective-permute-done((bf16[64,1024]{1,0:T(8,128)(2,1)S(1)}, bf16[64,1024]{1,0:T(8,128)(2,1)S(1)}, u32[]{:S(2)}, u32[]{:S(2)}) %collective-permute-start.6) | collective-permute-done | bytes 131104 | tf_op jit(solution)/shard_map/ppermute | solution.py:76
  28.2 0.0 copy-start.2
  28.2 0.3 collective-permute-start.7
  28.5 24.0 %collective-permute-done.7 = bf16[8,64,1024]{2,1,0:T(8,128)(2,1)S(1)} collective-permute-done((bf16[8,64,1024]{2,1,0:T(8,128)(2,1)S(1)}, bf16[8,64,1024]{2,1,0:T(8,128)(2,1)S(1)}, u32[]{:S(2)}, u32[]{:S(2)}) %collective-permute-start.7) | collective-permute-done | bytes 1048608 | tf_op jit(solution)/shard_map/ppermute | solution.py:79
  52.5 0.0 copy-start.3
  52.5 1.0 %copy-done.3 = bf16[8,64,1024]{2,1,0:T(8,128)(2,1)} copy-done((bf16[8,64,1024]{2,1,0:T(8,128)(2,1)}, bf16[8,64,1024]{2,1,0:T(8,128)(2,1)S(1)}, u32[]{:S(2)}) %copy-start.3) | copy-done | bytes 1048600
  53.5 1.6 %pad_maximum_fusion.1 = bf16[8,128,1024]{2,1,0:T(8,128)(2,1)} fusion(bf16[8,64,1024]{2,1,0:T(8,128)(2,1)S(1)} %collective-permute-done.7, bf16[8,64,1024]{2,1,0:T(8,128)(2,1)S(1)} %bitcast_dynamic-update-slice_fusion), kind=kLoop, calls=%fused_computation.5 | loop fusion | flops 4194304 | bytes 4194304 | tf_op jit(solution)/shard_map/concatenate | solution.py:80
  55.1 1.3 %collective-permute-start.8 = (bf16[8,128,1024]{2,1,0:T(8,128)(2,1)}, bf16[8,128,1024]{2,1,0:T(8,128)(2,1)}, u32[]{:S(2)}, u32[]{:S(2)}) collective-permute-start(bf16[8,128,1024]{2,1,0:T(8,128)(2,1)} %pad_maximum_fusion.1), channel_id=1, source_target_pairs={{0,1},{1,0},{2,3},{3,2},{4,5},{5,4},{6,7},{7,6},{8,9},{9,8},{10,11... | collective-permute-start | bytes 6291464 | tf_op jit(solution)/shard_map/ppermute | solution.py:79
  56.4 0.1 stack.100
  56.5 0.0 copy-start.4
  56.5 0.1 pad_add_fusion
  56.6 0.0 copy-done.2
  56.6 0.2 multiply_reduce_fusion
  56.8 3.7 %collective-permute-done.8 = bf16[8,128,1024]{2,1,0:T(8,128)(2,1)} collective-permute-done((bf16[8,128,1024]{2,1,0:T(8,128)(2,1)}, bf16[8,128,1024]{2,1,0:T(8,128)(2,1)}, u32[]{:S(2)}, u32[]{:S(2)}) %collective-permute-start.8) | collective-permute-done | bytes 2097184 | tf_op jit(solution)/shard_map/ppermute | solution.py:79
  60.5 0.0 copy-done.4
  60.5 1.8 %pad_maximum_fusion = bf16[8,256,1024]{2,1,0:T(8,128)(2,1)S(1)} fusion(bf16[8,128,1024]{2,1,0:T(8,128)(2,1)} %collective-permute-done.8, bf16[8,64,1024]{2,1,0:T(8,128)(2,1)S(1)} %copy-done.4, bf16[8,64,1024]{2,1,0:T(8,128)(2,1)S(1)} %bitcast_dynamic-update-slice_fusion), kind=kLoop, calls=%fused_computation | loop fusion | flops 12582912 | bytes 8388608 | tf_op jit(solution)/shard_map/concatenate | solution.py:80
  62.3 0.0 copy-start
  62.3 4.7 %fusion.12 = (f32[2048]{0:T(1024)S(1)}, f32[2048,512]{1,0:T(8,128)}) fusion(f32[512]{0:T(512)S(1)} %multiply_reduce_fusion, bf16[2048,1024]{1,0:T(8,128)(2,1)S(1)} %bitcast.89, f32[512,1024]{1,0:T(8,128)S(1)} %copy-done.2), kind=kOutput, calls=%fused_computation.63 | convolution fusion | flops 2152200192 | bytes 10496000 | tf_op jit(solution)/shard_map/dot_general | solution.py:10
  67.0 0.0 copy-done
  67.0 0.1 broadcast_in_dim.143
  67.1 3.3 %exponential_reduce_fusion = f32[2048]{0:T(1024)S(1)} fusion(f32[2048,512]{1,0:T(8,128)} %get-tuple-element.22, f32[2048]{0:T(1024)S(1)} %get-tuple-element.21), kind=kLoop, calls=%fused_computation.3 | loop fusion | flops 2095104 | bytes 4210688 | tf_op jit(solution)/shard_map/reduce_sum | solution.py:18
  70.4 0.1 broadcast_in_dim.148
  70.5 0.1 select_reduce_fusion.7
  70.6 0.2 select_reduce_fusion.3
  70.8 9.5 %all-gather = f32[16,8,4,64]{3,1,2,0:T(8,128)S(1)} all-gather(f32[2,8,4,64]{3,1,2,0:T(8,128)S(1)} %copy.31), channel_id=2, replica_groups=mesh['outer'=4,'dp'=2,'cent'=4] {'dp','cent'}, dimensions={0}, use_global_device_ids=true | all-gather | bytes 147456 | tf_op jit(solution)/shard_map/all_gather | solution.py:102
  80.4 0.1 select_reduce_fusion.1
  80.5 0.1 select_reduce_fusion.5
  80.6 0.1 div.48
  80.7 0.1 sub.75
  80.8 0.0 copy-start.1
  80.8 2.9 %convert_reduce_fusion = (f32[4,512]{1,0:T(4,128)S(1)}, bf16[2048,512]{1,0:T(8,128)(2,1)S(1)}) fusion(f32[2048]{0:T(1024)S(1)} %div.48, f32[2048,512]{1,0:T(8,128)} %get-tuple-element.22, f32[2048]{0:T(1024)S(1)} %sub.75), kind=kLoop, calls=%fused_computation.1 | loop fusion | flops 5240832 | bytes 6316032 | tf_op jit(solution)/shard_map/reduce_sum | solution.py:114
  83.7 0.5 copy-done.1
  84.2 2.4 %fusion.13 = f32[4,512,1024]{2,1,0:T(8,128)S(1)} fusion(bf16[4,512,512]{2,1,0:T(8,128)(2,1)S(1)} %bitcast.91, bf16[4,512,1024]{2,1,0:T(8,128)(2,1)S(1)} %bitcast.90), kind=kOutput, calls=%fused_computation.64 | convolution fusion | flops 2147483648 | bytes 14680064 | tf_op jit(solution)/shard_map/dot_general | solution.py:115
  86.7 3.7 %fusion.2 = f32[512,1024]{1,0:T(8,128)} fusion(f32[512,1024]{1,0:T(8,128)S(1)} %copy-done.2, f32[4,512,1024]{2,1,0:T(8,128)S(1)} %fusion.13, f32[512]{0:T(512)S(1)} %get-tuple-element.23, f32[512]{0:T(512)S(1)} %bitcast.99, f32[512]{0:T(512)S(1)} %get-tuple-element.24, f32[512]{0:T(512)S(1)} %bitcast.97, f32[512]{0:T(512)S(1)} %get-tuple-element.25, ...), kind=kLoop, calls=%fused_computation.9 | loop fusion | flops 14680064 | bytes 12599308 | tf_op jit(solution)/shard_map/div | solution.py:129
  (23 shorter events, 0.2 us)
Async XLA Ops:
  1.0 7.2 %collective-permute-start = (bf16[64,1024]{1,0:T(8,128)(2,1)S(1)}, bf16[64,1024]{1,0:T(8,128)(2,1)S(1)}, u32[]{:S(2)}, u32[]{:S(2)}) collective-permute-start(bf16[64,1024]{1,0:T(8,128)(2,1)S(1)} %get-tuple-element.16), channel_id=1, source_target_pairs={{0,4},{4,0},{8,12},{12,8},{16,20},{20,16},{24,28},{28,24},{1,5},{5... | collective-permute-start | bytes 393224 | tf_op jit(solution)/shard_map/ppermute | solution.py:76
  2.3 6.0 %collective-permute-start.1 = (bf16[64,1024]{1,0:T(8,128)(2,1)S(1)}, bf16[64,1024]{1,0:T(8,128)(2,1)S(1)}, u32[]{:S(2)}, u32[]{:S(2)}) collective-permute-start(bf16[64,1024]{1,0:T(8,128)(2,1)S(1)} %get-tuple-element.16), channel_id=1, source_target_pairs={{0,8},{4,12},{8,16},{12,20},{16,24},{20,28},{24,0},{28,4},{1,9},{5... | collective-permute-start | bytes 393224 | tf_op jit(solution)/shard_map/ppermute | solution.py:76
  3.6 6.7 %collective-permute-start.2 = (bf16[64,1024]{1,0:T(8,128)(2,1)S(1)}, bf16[64,1024]{1,0:T(8,128)(2,1)S(1)}, u32[]{:S(2)}, u32[]{:S(2)}) collective-permute-start(bf16[64,1024]{1,0:T(8,128)(2,1)S(1)} %get-tuple-element.16), channel_id=1, source_target_pairs={{0,12},{4,8},{8,20},{12,16},{16,28},{20,24},{24,4},{28,0},{1,13},{... | collective-permute-start | bytes 393224 | tf_op jit(solution)/shard_map/ppermute | solution.py:76
  4.8 17.5 %collective-permute-start.3 = (bf16[64,1024]{1,0:T(8,128)(2,1)S(1)}, bf16[64,1024]{1,0:T(8,128)(2,1)S(1)}, u32[]{:S(2)}, u32[]{:S(2)}) collective-permute-start(bf16[64,1024]{1,0:T(8,128)(2,1)S(1)} %get-tuple-element.16), channel_id=1, source_target_pairs={{0,16},{4,20},{8,24},{12,28},{16,0},{20,4},{24,8},{28,12},{1,17},{... | collective-permute-start | bytes 393224 | tf_op jit(solution)/shard_map/ppermute | solution.py:76
  5.8 19.3 %collective-permute-start.4 = (bf16[64,1024]{1,0:T(8,128)(2,1)S(1)}, bf16[64,1024]{1,0:T(8,128)(2,1)S(1)}, u32[]{:S(2)}, u32[]{:S(2)}) collective-permute-start(bf16[64,1024]{1,0:T(8,128)(2,1)S(1)} %get-tuple-element.16), channel_id=1, source_target_pairs={{0,20},{4,16},{8,28},{12,24},{16,4},{20,0},{24,12},{28,8},{1,21},{... | collective-permute-start | bytes 393224 | tf_op jit(solution)/shard_map/ppermute | solution.py:76
  8.1 17.3 %collective-permute-start.5 = (bf16[64,1024]{1,0:T(8,128)(2,1)S(1)}, bf16[64,1024]{1,0:T(8,128)(2,1)S(1)}, u32[]{:S(2)}, u32[]{:S(2)}) collective-permute-start(bf16[64,1024]{1,0:T(8,128)(2,1)S(1)} %get-tuple-element.16), channel_id=1, source_target_pairs={{0,24},{4,28},{8,0},{12,4},{16,8},{20,12},{24,16},{28,20},{1,25},{... | collective-permute-start | bytes 393224 | tf_op jit(solution)/shard_map/ppermute | solution.py:76
  8.3 19.8 %collective-permute-start.6 = (bf16[64,1024]{1,0:T(8,128)(2,1)S(1)}, bf16[64,1024]{1,0:T(8,128)(2,1)S(1)}, u32[]{:S(2)}, u32[]{:S(2)}) collective-permute-start(bf16[64,1024]{1,0:T(8,128)(2,1)S(1)} %get-tuple-element.16), channel_id=1, source_target_pairs={{0,28},{4,24},{8,4},{12,0},{16,12},{20,8},{24,20},{28,16},{1,29},{... | collective-permute-start | bytes 393224 | tf_op jit(solution)/shard_map/ppermute | solution.py:76
  28.2 28.4 %copy-start.2 = (f32[512,1024]{1,0:T(8,128)S(1)}, f32[512,1024]{1,0:T(8,128)}, u32[]{:S(2)}) copy-start(f32[512,1024]{1,0:T(8,128)} %param.3) | copy-start | bytes 6291460
  28.2 24.3 %collective-permute-start.7 = (bf16[8,64,1024]{2,1,0:T(8,128)(2,1)S(1)}, bf16[8,64,1024]{2,1,0:T(8,128)(2,1)S(1)}, u32[]{:S(2)}, u32[]{:S(2)}) collective-permute-start(bf16[8,64,1024]{2,1,0:T(8,128)(2,1)S(1)} %bitcast_dynamic-update-slice_fusion), channel_id=1, source_target_pairs={{0,2},{1,3},{2,0},{3,1},{4,6},{5,7},{6,4},{7,5},{8,10},{9,11},{10,... | collective-permute-start | bytes 3145736 | tf_op jit(solution)/shard_map/ppermute | solution.py:79
  52.5 1.0 %copy-start.3 = (bf16[8,64,1024]{2,1,0:T(8,128)(2,1)}, bf16[8,64,1024]{2,1,0:T(8,128)(2,1)S(1)}, u32[]{:S(2)}) copy-start(bf16[8,64,1024]{2,1,0:T(8,128)(2,1)S(1)} %collective-permute-done.7) | copy-start | bytes 3145732
  55.1 5.5 %collective-permute-start.8 = (bf16[8,128,1024]{2,1,0:T(8,128)(2,1)}, bf16[8,128,1024]{2,1,0:T(8,128)(2,1)}, u32[]{:S(2)}, u32[]{:S(2)}) collective-permute-start(bf16[8,128,1024]{2,1,0:T(8,128)(2,1)} %pad_maximum_fusion.1), channel_id=1, source_target_pairs={{0,1},{1,0},{2,3},{3,2},{4,5},{5,4},{6,7},{7,6},{8,9},{9,8},{10,11... | collective-permute-start | bytes 6291464 | tf_op jit(solution)/shard_map/ppermute | solution.py:79
  56.5 4.0 %copy-start.4 = (bf16[8,64,1024]{2,1,0:T(8,128)(2,1)S(1)}, bf16[8,64,1024]{2,1,0:T(8,128)(2,1)}, u32[]{:S(2)}) copy-start(bf16[8,64,1024]{2,1,0:T(8,128)(2,1)} %copy-done.3) | copy-start | bytes 3145732
  62.3 4.7 %copy-start = (bf16[8,256,1024]{2,1,0:T(8,128)(2,1)}, bf16[8,256,1024]{2,1,0:T(8,128)(2,1)S(1)}, u32[]{:S(2)}) copy-start(bf16[8,256,1024]{2,1,0:T(8,128)(2,1)S(1)} %pad_maximum_fusion) | copy-start | bytes 12582916
  80.8 3.4 %copy-start.1 = (bf16[8,256,1024]{2,1,0:T(8,128)(2,1)S(1)}, bf16[8,256,1024]{2,1,0:T(8,128)(2,1)}, u32[]{:S(2)}) copy-start(bf16[8,256,1024]{2,1,0:T(8,128)(2,1)} %copy-done) | copy-start | bytes 12582916

commit v5 on v4

--- a/solution.py
+++ b/solution.py
@@ -74,10 +74,16 @@
         for i, j in itertools.product(range(n_o), range(n_d)):
             perm.append((i * n_d + j, ((i + sz) % n_o) * n_d + (j + sy) % n_d))
         slots.append(lax.ppermute(mine, ("outer", "dp"), perm))
-    cur = jnp.stack(slots)
-    for bit in reversed(bits):
-        other = lax.ppermute(cur, "cent", [(i, i ^ bit) for i in range(n_c)])
-        cur = jnp.concatenate([cur, other], axis=1)
+    groups = 2 if n_od % 2 == 0 else 1
+    per = n_od // groups
+    parts = []
+    for g in range(groups):
+        cur = jnp.stack(slots[g * per:(g + 1) * per])
+        for bit in reversed(bits):
+            other = lax.ppermute(cur, "cent", [(i, i ^ bit) for i in range(n_c)])
+            cur = jnp.concatenate([cur, other], axis=1)
+        parts.append(cur)
+    cur = jnp.concatenate(parts, axis=0)
     everything = cur.reshape(n_od * n_c * tq, d)
 
     logits = scores_for(everything, cent_bf, squares)

time: 90.7 us -> 89.6 us (0.988)
  the two profiles are of different devices: /device:TPU:11 before, /device:TPU:0 now
where the time goes in v5:
time: 89.6 us; the launch traced here: 89.3 us
  waiting for transfers between devices  38.3 us (43%)
  other arithmetic  15.6 us (17%)
  starting transfers between devices  14.6 us (16%)
  blocking collectives  9.3 us (10%)
  matrix products  7.11 us (8%)
  local copies, waits for them, and re-layouts  3.9 us (4%)
    ppermute x4, waiting for transfers between devices, shards_all(): other = lax.ppermute(cur, 'cent', [(i, i ^ bit) for i in range(n_c)])  22.3 us
    ppermute x7, waiting for transfers between devices, shards_all(): slots.append(lax.ppermute(mine, ('outer', 'dp'), perm))  16 us
    ppermute x7, starting transfers between devices, shards_all(): slots.append(lax.ppermute(mine, ('outer', 'dp'), perm))  12.4 us
    all_gather x1, blocking collectives, shards_all(): every = lax.all_gather(both, ('dp', 'cent'), axis=0)  9.3 us
    dot_general x1, matrix products, scores_for(): lax.dot_general(piece, cent_bf, (((1,), (1,)), ((), ())), preferred_eleme...  4.68 us
    div x1, other arithmetic, shards_all(): return total / n_o  3.73 us
    unnamed x36, local copies, waits for them, and re-layouts  3.43 us
    reduce_sum x1, other arithmetic, row_summary(): local_sum = jnp.sum(jnp.exp(logits - local_max[:, None]), axis=1)  3.31 us
  transfers between devices with their start and end apart: 11, of which 6 were waited for; matrix products, arithmetic and copies ran while one was open for 3% of the time, Pallas kernels for 0%

profile of v5, /device:TPU:0, one launch (start us, length us, event | category | flops | bytes accessed | tf_op | source)
XLA Modules:
  0.0 89.3 jit_solution(11851442636320694403)
XLA Ops:
  0.0 0.0 copy-start
  0.0 1.2 %copy-done = f32[256,1024]{1,0:T(8,128)S(1)} copy-done((f32[256,1024]{1,0:T(8,128)S(1)}, f32[256,1024]{1,0:T(8,128)}, u32[]{:S(2)}) %copy-start) | copy-done | bytes 1048600
  1.2 6.1 %collective-permute-start.8 = (bf16[64,1024]{1,0:T(8,128)(2,1)S(1)}, bf16[64,1024]{1,0:T(8,128)(2,1)S(1)}, u32[]{:S(2)}, u32[]{:S(2)}) collective-permute-start(bf16[64,1024]{1,0:T(8,128)(2,1)S(1)} %dynamic-slice_convert_fusion), channel_id=1, source_target_pairs={{0,28},{4,24},{8,4},{12,0},{16,12},{20,8},{24,20},{28,16},{1,29},{... | collective-permute-start | bytes 393224 | tf_op jit(solution)/shard_map/ppermute | solution.py:76
  7.3 0.4 collective-permute-start.7
  7.8 0.0 collective-permute-start.6
  7.8 2.9 %collective-permute-start.5 = (bf16[64,1024]{1,0:T(8,128)(2,1)S(1)}, bf16[64,1024]{1,0:T(8,128)(2,1)S(1)}, u32[]{:S(2)}, u32[]{:S(2)}) collective-permute-start(bf16[64,1024]{1,0:T(8,128)(2,1)S(1)} %dynamic-slice_convert_fusion), channel_id=1, source_target_pairs={{0,16},{4,20},{8,24},{12,28},{16,0},{20,4},{24,8},{28,12},{1,17},{... | collective-permute-start | bytes 393224 | tf_op jit(solution)/shard_map/ppermute | solution.py:76
  10.6 2.5 %collective-permute-start.2 = (bf16[64,1024]{1,0:T(8,128)(2,1)S(1)}, bf16[64,1024]{1,0:T(8,128)(2,1)S(1)}, u32[]{:S(2)}, u32[]{:S(2)}) collective-permute-start(bf16[64,1024]{1,0:T(8,128)(2,1)S(1)} %dynamic-slice_convert_fusion), channel_id=1, source_target_pairs={{0,12},{4,8},{8,20},{12,16},{16,28},{20,24},{24,4},{28,0},{1,13},{... | collective-permute-start | bytes 393224 | tf_op jit(solution)/shard_map/ppermute | solution.py:76
  13.2 0.0 collective-permute-done.8
  13.2 0.0 collective-permute-start.1
  13.2 0.9 %collective-permute-done.7 = bf16[64,1024]{1,0:T(8,128)(2,1)S(1)} collective-permute-done((bf16[64,1024]{1,0:T(8,128)(2,1)S(1)}, bf16[64,1024]{1,0:T(8,128)(2,1)S(1)}, u32[]{:S(2)}, u32[]{:S(2)}) %collective-permute-start.7) | collective-permute-done | bytes 131104 | tf_op jit(solution)/shard_map/ppermute | solution.py:76
  14.1 0.5 collective-permute-start
  14.6 13.3 %collective-permute-done.6 = bf16[64,1024]{1,0:T(8,128)(2,1)S(1)} collective-permute-done((bf16[64,1024]{1,0:T(8,128)(2,1)S(1)}, bf16[64,1024]{1,0:T(8,128)(2,1)S(1)}, u32[]{:S(2)}, u32[]{:S(2)}) %collective-permute-start.6) | collective-permute-done | bytes 131104 | tf_op jit(solution)/shard_map/ppermute | solution.py:76
  27.9 1.7 %collective-permute-done.5 = bf16[64,1024]{1,0:T(8,128)(2,1)S(1)} collective-permute-done((bf16[64,1024]{1,0:T(8,128)(2,1)S(1)}, bf16[64,1024]{1,0:T(8,128)(2,1)S(1)}, u32[]{:S(2)}, u32[]{:S(2)}) %collective-permute-start.5) | collective-permute-done | bytes 131104 | tf_op jit(solution)/shard_map/ppermute | solution.py:76
  29.6 0.1 pad_maximum_fusion.3
  29.7 1.6 %collective-permute-start.9 = (bf16[4,64,1024]{2,1,0:T(8,128)(2,1)S(1)}, bf16[4,64,1024]{2,1,0:T(8,128)(2,1)S(1)}, u32[]{:S(2)}, u32[]{:S(2)}) collective-permute-start(bf16[4,64,1024]{2,1,0:T(8,128)(2,1)S(1)} %pad_maximum_fusion.3), channel_id=1, source_target_pairs={{0,2},{1,3},{2,0},{3,1},{4,6},{5,7},{6,4},{7,5},{8,10},{9,11},{10,... | collective-permute-start | bytes 1572872 | tf_op jit(solution)/shard_map/ppermute | solution.py:83
  31.3 0.0 collective-permute-done.2
  31.3 0.0 copy-start.12
  31.3 0.0 collective-permute-done.1
  31.3 0.0 copy-start.14
  31.3 0.0 collective-permute-done
  31.3 0.0 copy-start.16
  31.3 0.1 pad_maximum_fusion.2
  31.4 0.0 copy-start.3
  31.4 0.6 collective-permute-start.3
  32.0 12.6 %collective-permute-done.9 = bf16[4,64,1024]{2,1,0:T(8,128)(2,1)S(1)} collective-permute-done((bf16[4,64,1024]{2,1,0:T(8,128)(2,1)S(1)}, bf16[4,64,1024]{2,1,0:T(8,128)(2,1)S(1)}, u32[]{:S(2)}, u32[]{:S(2)}) %collective-permute-start.9) | collective-permute-done | bytes 524320 | tf_op jit(solution)/shard_map/ppermute | solution.py:83
  44.6 0.8 copy-done.4
  45.4 1.1 %pad_maximum_fusion.1 = bf16[4,128,1024]{2,1,0:T(8,128)(2,1)} fusion(bf16[4,64,1024]{2,1,0:T(8,128)(2,1)S(1)} %collective-permute-done.9, bf16[1,64,1024]{2,1,0:T(8,128)(2,1)S(1)} %bitcast.88, bf16[1,64,1024]{2,1,0:T(8,128)(2,1)S(1)} %bitcast.91, bf16[1,64,1024]{2,1,0:T(8,128)(2,1)S(1)} %bitcast.94, bf16[1,64,1024]{2,1,0:T(8,128)(2,1)S(1)} %bitcast.97), kind=kLoop, calls=%fused_computation.19 | loop fusion | flops 5242880 | bytes 2097152 | tf_op jit(solution)/shard_map/concatenate | solution.py:84
  46.5 0.0 copy-done.8
  46.5 0.0 copy-done.10
  46.5 0.0 collective-permute-start.10
  46.5 7.3 %collective-permute-done.3 = bf16[4,64,1024]{2,1,0:T(8,128)(2,1)S(1)} collective-permute-done((bf16[4,64,1024]{2,1,0:T(8,128)(2,1)S(1)}, bf16[4,64,1024]{2,1,0:T(8,128)(2,1)S(1)}, u32[]{:S(2)}, u32[]{:S(2)}) %collective-permute-start.3) | collective-permute-done | bytes 524320 | tf_op jit(solution)/shard_map/ppermute | solution.py:83
  53.8 0.8 copy-done.6
  54.6 1.1 %pad_maximum_fusion = bf16[4,128,1024]{2,1,0:T(8,128)(2,1)} fusion(bf16[4,64,1024]{2,1,0:T(8,128)(2,1)S(1)} %collective-permute-done.3, bf16[1,64,1024]{2,1,0:T(8,128)(2,1)S(1)} %bitcast.100, bf16[1,64,1024]{2,1,0:T(8,128)(2,1)S(1)} %bitcast.103, bf16[1,64,1024]{2,1,0:T(8,128)(2,1)S(1)} %bitcast.106, bf16[1,64,1024]{2,1,0:T(8,128)(2,1)S(1)} %fusion.17), kind=kLoop, calls=%fused_computation.18 | loop fusion | flops 5242880 | bytes 2097152 | tf_op jit(solution)/shard_map/concatenate | solution.py:84
  55.7 0.0 copy-done.12
  55.7 0.0 copy-done.14
  55.7 0.0 copy-done.16
  55.7 0.1 collective-permute-start.4
  55.9 0.1 stack.104
  55.9 0.0 copy-start.9
  56.0 0.0 copy-start.11
  56.0 0.0 copy-start.13
  56.0 0.0 copy-start.15
  56.0 0.1 pad_add_fusion
  56.1 0.0 copy-done.3
  56.1 0.2 multiply_reduce_fusion
  56.3 0.0 collective-permute-done.10
  56.3 2.4 %collective-permute-done.4 = bf16[4,128,1024]{2,1,0:T(8,128)(2,1)} collective-permute-done((bf16[4,128,1024]{2,1,0:T(8,128)(2,1)}, bf16[4,128,1024]{2,1,0:T(8,128)(2,1)}, u32[]{:S(2)}, u32[]{:S(2)}) %collective-permute-start.4) | collective-permute-done | bytes 1048608 | tf_op jit(solution)/shard_map/ppermute | solution.py:83
  58.7 0.0 copy-done.5
  58.8 2.6 %maximum_maximum_fusion = bf16[8,256,1024]{2,1,0:T(8,128)(2,1)S(1)} fusion(bf16[4,128,1024]{2,1,0:T(8,128)(2,1)} %collective-permute-done.10, bf16[4,64,1024]{2,1,0:T(8,128)(2,1)S(1)} %copy-done.5, bf16[1,64,1024]{2,1,0:T(8,128)(2,1)S(1)} %bitcast.89, bf16[1,64,1024]{2,1,0:T(8,128)(2,1)S(1)} %bitcast.92, bf16[1,64,1024]{2,1,0:T(8,128)(2,1)S(1)} %bitcast.95, ...), kind=kLoop, calls=%fused_computation | loop fusion | flops 50331648 | bytes 8388608 | tf_op jit(solution)/shard_map/concatenate | solution.py:86
  61.4 4.7 %fusion.12 = (f32[2048]{0:T(1024)S(1)}, f32[2048,512]{1,0:T(8,128)}) fusion(f32[512]{0:T(512)S(1)} %multiply_reduce_fusion, bf16[2048,1024]{1,0:T(8,128)(2,1)S(1)} %bitcast.82, f32[512,1024]{1,0:T(8,128)S(1)} %copy-done.3), kind=kOutput, calls=%fused_computation.58 | convolution fusion | flops 2152200192 | bytes 10496000 | tf_op jit(solution)/shard_map/dot_general | solution.py:10
  66.1 0.1 broadcast_in_dim.143
  66.2 3.3 %exponential_reduce_fusion = f32[2048]{0:T(1024)S(1)} fusion(f32[2048,512]{1,0:T(8,128)} %get-tuple-element.20, f32[2048]{0:T(1024)S(1)} %get-tuple-element.19), kind=kLoop, calls=%fused_computation.3 | loop fusion | flops 2095104 | bytes 4210688 | tf_op jit(solution)/shard_map/reduce_sum | solution.py:18
  69.5 0.1 broadcast_in_dim.148
  69.6 0.1 select_reduce_fusion.7
  69.7 0.2 select_reduce_fusion.3
  69.9 9.3 %all-gather = f32[16,8,4,64]{3,1,2,0:T(8,128)S(1)} all-gather(f32[2,8,4,64]{3,1,2,0:T(8,128)S(1)} %copy.31), channel_id=2, replica_groups=mesh['outer'=4,'dp'=2,'cent'=4] {'dp','cent'}, dimensions={0}, use_global_device_ids=true | all-gather | bytes 147456 | tf_op jit(solution)/shard_map/all_gather | solution.py:108
  79.3 0.1 select_reduce_fusion.1
  79.4 0.1 select_reduce_fusion.5
  79.5 0.1 div.48
  79.6 0.1 sub.75
  79.7 2.9 %convert_reduce_fusion = (f32[4,512]{1,0:T(4,128)S(1)}, bf16[2048,512]{1,0:T(8,128)(2,1)S(1)}) fusion(f32[2048]{0:T(1024)S(1)} %div.48, f32[2048,512]{1,0:T(8,128)} %get-tuple-element.20, f32[2048]{0:T(1024)S(1)} %sub.75), kind=kLoop, calls=%fused_computation.1 | loop fusion | flops 5240832 | bytes 6316032 | tf_op jit(solution)/shard_map/reduce_sum | solution.py:120
  82.5 0.5 copy-done.2
  83.1 2.4 %fusion.13 = f32[4,512,1024]{2,1,0:T(8,128)S(1)} fusion(bf16[4,512,512]{2,1,0:T(8,128)(2,1)S(1)} %bitcast.84, bf16[4,512,1024]{2,1,0:T(8,128)(2,1)S(1)} %bitcast.83), kind=kOutput, calls=%fused_computation.59 | convolution fusion | flops 2147483648 | bytes 14680064 | tf_op jit(solution)/shard_map/dot_general | solution.py:121
  85.6 3.7 %fusion.2 = f32[512,1024]{1,0:T(8,128)} fusion(f32[512,1024]{1,0:T(8,128)S(1)} %copy-done.3, f32[4,512,1024]{2,1,0:T(8,128)S(1)} %fusion.13, f32[512]{0:T(512)S(1)} %get-tuple-element.21, f32[512]{0:T(512)S(1)} %bitcast.113, f32[512]{0:T(512)S(1)} %get-tuple-element.22, f32[512]{0:T(512)S(1)} %bitcast.111, f32[512]{0:T(512)S(1)} %get-tuple-element.23, ...), kind=kLoop, calls=%fused_computation.8 | loop fusion | flops 14680064 | bytes 12599308 | tf_op jit(solution)/shard_map/div | solution.py:135
  (34 shorter events, 0.2 us)
Async XLA Ops:
  0.0 1.2 %copy-start = (f32[256,1024]{1,0:T(8,128)S(1)}, f32[256,1024]{1,0:T(8,128)}, u32[]{:S(2)}) copy-start(f32[256,1024]{1,0:T(8,128)} %param.2) | copy-start | bytes 3145732
  1.2 11.9 %collective-permute-start.8 = (bf16[64,1024]{1,0:T(8,128)(2,1)S(1)}, bf16[64,1024]{1,0:T(8,128)(2,1)S(1)}, u32[]{:S(2)}, u32[]{:S(2)}) collective-permute-start(bf16[64,1024]{1,0:T(8,128)(2,1)S(1)} %dynamic-slice_convert_fusion), channel_id=1, source_target_pairs={{0,28},{4,24},{8,4},{12,0},{16,12},{20,8},{24,20},{28,16},{1,29},{... | collective-permute-start | bytes 393224 | tf_op jit(solution)/shard_map/ppermute | solution.py:76
  7.3 6.8 %collective-permute-start.7 = (bf16[64,1024]{1,0:T(8,128)(2,1)S(1)}, bf16[64,1024]{1,0:T(8,128)(2,1)S(1)}, u32[]{:S(2)}, u32[]{:S(2)}) collective-permute-start(bf16[64,1024]{1,0:T(8,128)(2,1)S(1)} %dynamic-slice_convert_fusion), channel_id=1, source_target_pairs={{0,24},{4,28},{8,0},{12,4},{16,8},{20,12},{24,16},{28,20},{1,25},{... | collective-permute-start | bytes 393224 | tf_op jit(solution)/shard_map/ppermute | solution.py:76
  7.8 20.1 %collective-permute-start.6 = (bf16[64,1024]{1,0:T(8,128)(2,1)S(1)}, bf16[64,1024]{1,0:T(8,128)(2,1)S(1)}, u32[]{:S(2)}, u32[]{:S(2)}) collective-permute-start(bf16[64,1024]{1,0:T(8,128)(2,1)S(1)} %dynamic-slice_convert_fusion), channel_id=1, source_target_pairs={{0,20},{4,16},{8,28},{12,24},{16,4},{20,0},{24,12},{28,8},{1,21},{... | collective-permute-start | bytes 393224 | tf_op jit(solution)/shard_map/ppermute | solution.py:76
  7.8 21.9 %collective-permute-start.5 = (bf16[64,1024]{1,0:T(8,128)(2,1)S(1)}, bf16[64,1024]{1,0:T(8,128)(2,1)S(1)}, u32[]{:S(2)}, u32[]{:S(2)}) collective-permute-start(bf16[64,1024]{1,0:T(8,128)(2,1)S(1)} %dynamic-slice_convert_fusion), channel_id=1, source_target_pairs={{0,16},{4,20},{8,24},{12,28},{16,0},{20,4},{24,8},{28,12},{1,17},{... | collective-permute-start | bytes 393224 | tf_op jit(solution)/shard_map/ppermute | solution.py:76
  10.6 20.6 %collective-permute-start.2 = (bf16[64,1024]{1,0:T(8,128)(2,1)S(1)}, bf16[64,1024]{1,0:T(8,128)(2,1)S(1)}, u32[]{:S(2)}, u32[]{:S(2)}) collective-permute-start(bf16[64,1024]{1,0:T(8,128)(2,1)S(1)} %dynamic-slice_convert_fusion), channel_id=1, source_target_pairs={{0,12},{4,8},{8,20},{12,16},{16,28},{20,24},{24,4},{28,0},{1,13},{... | collective-permute-start | bytes 393224 | tf_op jit(solution)/shard_map/ppermute | solution.py:76
  13.2 18.1 %collective-permute-start.1 = (bf16[64,1024]{1,0:T(8,128)(2,1)S(1)}, bf16[64,1024]{1,0:T(8,128)(2,1)S(1)}, u32[]{:S(2)}, u32[]{:S(2)}) collective-permute-start(bf16[64,1024]{1,0:T(8,128)(2,1)S(1)} %dynamic-slice_convert_fusion), channel_id=1, source_target_pairs={{0,8},{4,12},{8,16},{12,20},{16,24},{20,28},{24,0},{28,4},{1,9},{5... | collective-permute-start | bytes 393224 | tf_op jit(solution)/shard_map/ppermute | solution.py:76
  14.1 17.2 %collective-permute-start = (bf16[64,1024]{1,0:T(8,128)(2,1)S(1)}, bf16[64,1024]{1,0:T(8,128)(2,1)S(1)}, u32[]{:S(2)}, u32[]{:S(2)}) collective-permute-start(bf16[64,1024]{1,0:T(8,128)(2,1)S(1)} %dynamic-slice_convert_fusion), channel_id=1, source_target_pairs={{0,4},{4,0},{8,12},{12,8},{16,20},{20,16},{24,28},{28,24},{1,5},{5... | collective-permute-start | bytes 393224 | tf_op jit(solution)/shard_map/ppermute | solution.py:76
  27.9 18.6 %copy-start.8 = (bf16[64,1024]{1,0:T(8,128)(2,1)}, bf16[64,1024]{1,0:T(8,128)(2,1)S(1)}, u32[]{:S(2)}) copy-start(bf16[64,1024]{1,0:T(8,128)(2,1)S(1)} %collective-permute-done.6) | copy-start | bytes 393220
  29.6 16.8 %copy-start.10 = (bf16[64,1024]{1,0:T(8,128)(2,1)}, bf16[64,1024]{1,0:T(8,128)(2,1)S(1)}, u32[]{:S(2)}) copy-start(bf16[64,1024]{1,0:T(8,128)(2,1)S(1)} %collective-permute-done.5) | copy-start | bytes 393220
  29.7 14.9 %collective-permute-start.9 = (bf16[4,64,1024]{2,1,0:T(8,128)(2,1)S(1)}, bf16[4,64,1024]{2,1,0:T(8,128)(2,1)S(1)}, u32[]{:S(2)}, u32[]{:S(2)}) collective-permute-start(bf16[4,64,1024]{2,1,0:T(8,128)(2,1)S(1)} %pad_maximum_fusion.3), channel_id=1, source_target_pairs={{0,2},{1,3},{2,0},{3,1},{4,6},{5,7},{6,4},{7,5},{8,10},{9,11},{10,... | collective-permute-start | bytes 1572872 | tf_op jit(solution)/shard_map/ppermute | solution.py:83
  31.3 24.4 %copy-start.12 = (bf16[64,1024]{1,0:T(8,128)(2,1)}, bf16[64,1024]{1,0:T(8,128)(2,1)S(1)}, u32[]{:S(2)}) copy-start(bf16[64,1024]{1,0:T(8,128)(2,1)S(1)} %collective-permute-done.2) | copy-start | bytes 393220
  31.3 24.4 %copy-start.14 = (bf16[64,1024]{1,0:T(8,128)(2,1)}, bf16[64,1024]{1,0:T(8,128)(2,1)S(1)}, u32[]{:S(2)}) copy-start(bf16[64,1024]{1,0:T(8,128)(2,1)S(1)} %collective-permute-done.1) | copy-start | bytes 393220
  31.3 24.4 %copy-start.16 = (bf16[64,1024]{1,0:T(8,128)(2,1)}, bf16[64,1024]{1,0:T(8,128)(2,1)S(1)}, u32[]{:S(2)}) copy-start(bf16[64,1024]{1,0:T(8,128)(2,1)S(1)} %collective-permute-done) | copy-start | bytes 393220
  31.4 24.7 %copy-start.3 = (f32[512,1024]{1,0:T(8,128)S(1)}, f32[512,1024]{1,0:T(8,128)}, u32[]{:S(2)}) copy-start(f32[512,1024]{1,0:T(8,128)} %param.3) | copy-start | bytes 6291460
  31.4 22.4 %collective-permute-start.3 = (bf16[4,64,1024]{2,1,0:T(8,128)(2,1)S(1)}, bf16[4,64,1024]{2,1,0:T(8,128)(2,1)S(1)}, u32[]{:S(2)}, u32[]{:S(2)}) collective-permute-start(bf16[4,64,1024]{2,1,0:T(8,128)(2,1)S(1)} %pad_maximum_fusion.2), channel_id=1, source_target_pairs={{0,2},{1,3},{2,0},{3,1},{4,6},{5,7},{6,4},{7,5},{8,10},{9,11},{10,... | collective-permute-start | bytes 1572872 | tf_op jit(solution)/shard_map/ppermute | solution.py:83
  44.6 0.8 copy-start.4
  46.5 9.9 %collective-permute-start.10 = (bf16[4,128,1024]{2,1,0:T(8,128)(2,1)}, bf16[4,128,1024]{2,1,0:T(8,128)(2,1)}, u32[]{:S(2)}, u32[]{:S(2)}) collective-permute-start(bf16[4,128,1024]{2,1,0:T(8,128)(2,1)} %pad_maximum_fusion.1), channel_id=1, source_target_pairs={{0,1},{1,0},{2,3},{3,2},{4,5},{5,4},{6,7},{7,6},{8,9},{9,8},{10,11... | collective-permute-start | bytes 3145736 | tf_op jit(solution)/shard_map/ppermute | solution.py:83
  53.8 0.8 copy-start.6
  55.7 3.1 %collective-permute-start.4 = (bf16[4,128,1024]{2,1,0:T(8,128)(2,1)}, bf16[4,128,1024]{2,1,0:T(8,128)(2,1)}, u32[]{:S(2)}, u32[]{:S(2)}) collective-permute-start(bf16[4,128,1024]{2,1,0:T(8,128)(2,1)} %pad_maximum_fusion), channel_id=1, source_target_pairs={{0,1},{1,0},{2,3},{3,2},{4,5},{5,4},{6,7},{7,6},{8,9},{9,8},{10,11... | collective-permute-start | bytes 3145736 | tf_op jit(solution)/shard_map/ppermute | solution.py:83
  55.9 2.8 %copy-start.5 = (bf16[4,64,1024]{2,1,0:T(8,128)(2,1)S(1)}, bf16[4,64,1024]{2,1,0:T(8,128)(2,1)}, u32[]{:S(2)}) copy-start(bf16[4,64,1024]{2,1,0:T(8,128)(2,1)} %copy-done.4) | copy-start | bytes 1572868
  55.9 2.8 %copy-start.7 = (bf16[4,64,1024]{2,1,0:T(8,128)(2,1)S(1)}, bf16[4,64,1024]{2,1,0:T(8,128)(2,1)}, u32[]{:S(2)}) copy-start(bf16[4,64,1024]{2,1,0:T(8,128)(2,1)} %copy-done.6) | copy-start | bytes 1572868
  55.9 2.8 %copy-start.9 = (bf16[64,1024]{1,0:T(8,128)(2,1)S(1)}, bf16[64,1024]{1,0:T(8,128)(2,1)}, u32[]{:S(2)}) copy-start(bf16[64,1024]{1,0:T(8,128)(2,1)} %copy-done.8) | copy-start | bytes 393220
  56.0 2.8 %copy-start.11 = (bf16[64,1024]{1,0:T(8,128)(2,1)S(1)}, bf16[64,1024]{1,0:T(8,128)(2,1)}, u32[]{:S(2)}) copy-start(bf16[64,1024]{1,0:T(8,128)(2,1)} %copy-done.10) | copy-start | bytes 393220
  56.0 2.8 %copy-start.13 = (bf16[64,1024]{1,0:T(8,128)(2,1)S(1)}, bf16[64,1024]{1,0:T(8,128)(2,1)}, u32[]{:S(2)}) copy-start(bf16[64,1024]{1,0:T(8,128)(2,1)} %copy-done.12) | copy-start | bytes 393220
  56.0 2.8 %copy-start.15 = (bf16[64,1024]{1,0:T(8,128)(2,1)S(1)}, bf16[64,1024]{1,0:T(8,128)(2,1)}, u32[]{:S(2)}) copy-start(bf16[64,1024]{1,0:T(8,128)(2,1)} %copy-done.14) | copy-start | bytes 393220
  56.0 2.8 %copy-start.17 = (bf16[64,1024]{1,0:T(8,128)(2,1)S(1)}, bf16[64,1024]{1,0:T(8,128)(2,1)}, u32[]{:S(2)}) copy-start(bf16[64,1024]{1,0:T(8,128)(2,1)} %copy-done.16) | copy-start | bytes 393220
  61.4 4.7 %copy-start.1 = (bf16[8,256,1024]{2,1,0:T(8,128)(2,1)}, bf16[8,256,1024]{2,1,0:T(8,128)(2,1)S(1)}, u32[]{:S(2)}) copy-start(bf16[8,256,1024]{2,1,0:T(8,128)(2,1)S(1)} %maximum_maximum_fusion) | copy-start | bytes 12582916
  79.6 3.4 %copy-start.2 = (bf16[8,256,1024]{2,1,0:T(8,128)(2,1)S(1)}, bf16[8,256,1024]{2,1,0:T(8,128)(2,1)}, u32[]{:S(2)}) copy-start(bf16[8,256,1024]{2,1,0:T(8,128)(2,1)} %copy-done.1) | copy-start | bytes 12582916

commit v6 on v5

--- a/solution.py
+++ b/solution.py
@@ -68,21 +68,21 @@
 
     mine = lax.dynamic_slice_in_dim(rows_bf, q * tq, tq, 0)
     shifts = list(itertools.product(range(n_o), range(n_d)))
-    slots = [mine]
-    for sz, sy in shifts[1:]:
-        perm = []
-        for i, j in itertools.product(range(n_o), range(n_d)):
-            perm.append((i * n_d + j, ((i + sz) % n_o) * n_d + (j + sy) % n_d))
-        slots.append(lax.ppermute(mine, ("outer", "dp"), perm))
-    groups = 2 if n_od % 2 == 0 else 1
-    per = n_od // groups
-    parts = []
-    for g in range(groups):
-        cur = jnp.stack(slots[g * per:(g + 1) * per])
+    across = [mine]
+    for sy in range(1, n_d):
+        across.append(lax.ppermute(mine, "dp", [(j, (j + sy) % n_d) for j in range(n_d)]))
+    pair = jnp.stack(across)
+
+    def spread(cur):
         for bit in reversed(bits):
             other = lax.ppermute(cur, "cent", [(i, i ^ bit) for i in range(n_c)])
             cur = jnp.concatenate([cur, other], axis=1)
-        parts.append(cur)
+        return cur
+
+    parts = [spread(pair)]
+    for sz in range(1, n_o):
+        moved = lax.ppermute(pair, "outer", [(i, (i + sz) % n_o) for i in range(n_o)])
+        parts.append(spread(moved))
     cur = jnp.concatenate(parts, axis=0)
     everything = cur.reshape(n_od * n_c * tq, d)
 

time: 89.6 us -> 78.1 us (0.87)
  waiting for transfers between devices: 38.3 us -> 29.7 us
  local copies, waits for them, and re-layouts: 3.9 us -> 2.28 us
  starting transfers between devices: 14.6 us -> 13.7 us
    ppermute x11 -> x12, waiting for transfers between devices: 38.3 us -> 29.7 us  [the longest x3 17.4 us: shards_all(): lax.ppermute(pair, 'outer', [(i, (i + sz) % n_o) for i in range(n_o)])]
    concatenate x2 -> x4, other arithmetic: 2.12 us -> 0.14 us  [spread(): cur = jnp.concatenate([cur, other], axis=1)]
    unnamed x36 -> x20, local copies, waits for them, and re-layouts: 3.43 us -> 1.81 us
    reduce_sum x1, other arithmetic: 0.21 us -> 1.8 us  [shards_all(): squares = jnp.sum(centroids * centroids, axis=1)]
    ppermute x11 -> x12, starting transfers between devices: 14.6 us -> 13.7 us  [the longest x8 5.83 us: spread(): other = lax.ppermute(cur, 'cent', [(i, i ^ bit) for i in range(n_c)])]
  transfers between devices with their start and end apart: 11 -> 12, of which waited for: 6 -> 6; matrix products, arithmetic and copies ran while one was open for 3% -> 3% of each run, Pallas kernels for 0% -> 0%
where the time goes in v6:
time: 78.1 us; the launch traced here: 77.7 us
  waiting for transfers between devices  29.7 us (38%)
  other arithmetic  15.2 us (19%)
  starting transfers between devices  13.7 us (18%)
  blocking collectives  9.33 us (12%)
  matrix products  7.1 us (9%)
  local copies, waits for them, and re-layouts  2.28 us (3%)
    ppermute x3, waiting for transfers between devices, shards_all(): lax.ppermute(pair, 'outer', [(i, (i + sz) % n_o) for i in range(n_o)])  17.4 us
    all_gather x1, blocking collectives, shards_all(): every = lax.all_gather(both, ('dp', 'cent'), axis=0)  9.33 us
    ppermute x8, waiting for transfers between devices, spread(): other = lax.ppermute(cur, 'cent', [(i, i ^ bit) for i in range(n_c)])  8.75 us
    ppermute x8, starting transfers between devices, spread(): other = lax.ppermute(cur, 'cent', [(i, i ^ bit) for i in range(n_c)])  5.83 us
    ppermute x3, starting transfers between devices, shards_all(): lax.ppermute(pair, 'outer', [(i, (i + sz) % n_o) for i in range(n_o)])  4.89 us
    dot_general x1, matrix products, scores_for(): lax.dot_general(piece, cent_bf, (((1,), (1,)), ((), ())), preferred_eleme...  4.68 us
    div x1, other arithmetic, shards_all(): return total / n_o  3.72 us
    ppermute x1, waiting for transfers between devices, shards_all(): lax.ppermute(mine, 'dp', [(j, (j + sy) % n_d) for j in range(n_d)])  3.48 us
  transfers between devices with their start and end apart: 12, of which 6 were waited for; matrix products, arithmetic and copies ran while one was open for 3% of the time, Pallas kernels for 0%

profile of v6, /device:TPU:0, one launch (start us, length us, event | category | flops | bytes accessed | tf_op | source)
XLA Modules:
  0.0 77.7 jit_solution(3005745409946565279)
XLA Ops:
  0.0 0.0 copy-start
  0.0 1.2 %copy-done = f32[256,1024]{1,0:T(8,128)S(1)} copy-done((f32[256,1024]{1,0:T(8,128)S(1)}, f32[256,1024]{1,0:T(8,128)}, u32[]{:S(2)}) %copy-start) | copy-done | bytes 1048600
  1.2 3.0 %collective-permute-start = (bf16[64,1024]{1,0:T(8,128)(2,1)S(1)}, bf16[64,1024]{1,0:T(8,128)(2,1)S(1)}, u32[]{:S(2)}, u32[]{:S(2)}) collective-permute-start(bf16[64,1024]{1,0:T(8,128)(2,1)S(1)} %dynamic-slice_convert_fusion), channel_id=1, source_target_pairs={{0,4},{4,0},{1,5},{5,1},{2,6},{6,2},{3,7},{7,3},{8,12},{12,8},{9,1... | collective-permute-start | bytes 393224 | tf_op jit(solution)/shard_map/ppermute | solution.py:73
  4.3 3.5 %collective-permute-done = bf16[64,1024]{1,0:T(8,128)(2,1)S(1)} collective-permute-done((bf16[64,1024]{1,0:T(8,128)(2,1)S(1)}, bf16[64,1024]{1,0:T(8,128)(2,1)S(1)}, u32[]{:S(2)}, u32[]{:S(2)}) %collective-permute-start) | collective-permute-done | bytes 131104 | tf_op jit(solution)/shard_map/ppermute | solution.py:73
  7.8 3.9 %collective-permute-start.9 = (bf16[2,64,1024]{2,1,0:T(8,128)(2,1)S(1)}, bf16[2,64,1024]{2,1,0:T(8,128)(2,1)S(1)}, u32[]{:S(2)}, u32[]{:S(2)}) collective-permute-start(bf16[2,64,1024]{2,1,0:T(8,128)(2,1)S(1)} %pad_maximum_fusion.4), channel_id=1, source_target_pairs={{0,24},{8,0},{16,8},{24,16},{1,25},{9,1},{17,9},{25,17},{2,26},{10... | collective-permute-start | bytes 786440 | tf_op jit(solution)/shard_map/ppermute | solution.py:84
  11.7 0.0 collective-permute-start.6
  11.7 1.0 %collective-permute-start.3 = (bf16[2,64,1024]{2,1,0:T(8,128)(2,1)S(1)}, bf16[2,64,1024]{2,1,0:T(8,128)(2,1)S(1)}, u32[]{:S(2)}, u32[]{:S(2)}) collective-permute-start(bf16[2,64,1024]{2,1,0:T(8,128)(2,1)S(1)} %pad_maximum_fusion.4), channel_id=1, source_target_pairs={{0,8},{8,16},{16,24},{24,0},{1,9},{9,17},{17,25},{25,1},{2,10},{10... | collective-permute-start | bytes 786440 | tf_op jit(solution)/shard_map/ppermute | solution.py:84
  12.7 1.5 %collective-permute-start.1 = (bf16[2,64,1024]{2,1,0:T(8,128)(2,1)S(1)}, bf16[2,64,1024]{2,1,0:T(8,128)(2,1)S(1)}, u32[]{:S(2)}, u32[]{:S(2)}) collective-permute-start(bf16[2,64,1024]{2,1,0:T(8,128)(2,1)S(1)} %pad_maximum_fusion.4), channel_id=1, source_target_pairs={{0,2},{1,3},{2,0},{3,1},{4,6},{5,7},{6,4},{7,5},{8,10},{9,11},{10,... | collective-permute-start | bytes 786440 | tf_op jit(solution)/shard_map/ppermute | solution.py:78
  14.2 4.3 %collective-permute-done.9 = bf16[2,64,1024]{2,1,0:T(8,128)(2,1)S(1)} collective-permute-done((bf16[2,64,1024]{2,1,0:T(8,128)(2,1)S(1)}, bf16[2,64,1024]{2,1,0:T(8,128)(2,1)S(1)}, u32[]{:S(2)}, u32[]{:S(2)}) %collective-permute-start.9) | collective-permute-done | bytes 262176 | tf_op jit(solution)/shard_map/ppermute | solution.py:84
  18.5 0.0 copy-start.4
  18.5 1.5 %collective-permute-start.10 = (bf16[2,64,1024]{2,1,0:T(8,128)(2,1)S(1)}, bf16[2,64,1024]{2,1,0:T(8,128)(2,1)S(1)}, u32[]{:S(2)}, u32[]{:S(2)}) collective-permute-start(bf16[2,64,1024]{2,1,0:T(8,128)(2,1)S(1)} %collective-permute-done.9), channel_id=1, source_target_pairs={{0,2},{1,3},{2,0},{3,1},{4,6},{5,7},{6,4},{7,5},{8,10},{9,11},{10,... | collective-permute-start | bytes 786440 | tf_op jit(solution)/shard_map/ppermute | solution.py:78
  20.0 13.1 %collective-permute-done.6 = bf16[2,64,1024]{2,1,0:T(8,128)(2,1)S(1)} collective-permute-done((bf16[2,64,1024]{2,1,0:T(8,128)(2,1)S(1)}, bf16[2,64,1024]{2,1,0:T(8,128)(2,1)S(1)}, u32[]{:S(2)}, u32[]{:S(2)}) %collective-permute-start.6) | collective-permute-done | bytes 262176 | tf_op jit(solution)/shard_map/ppermute | solution.py:84
  33.1 0.0 copy-start.5
  33.1 1.5 %collective-permute-start.7 = (bf16[2,64,1024]{2,1,0:T(8,128)(2,1)S(1)}, bf16[2,64,1024]{2,1,0:T(8,128)(2,1)S(1)}, u32[]{:S(2)}, u32[]{:S(2)}) collective-permute-start(bf16[2,64,1024]{2,1,0:T(8,128)(2,1)S(1)} %collective-permute-done.6), channel_id=1, source_target_pairs={{0,2},{1,3},{2,0},{3,1},{4,6},{5,7},{6,4},{7,5},{8,10},{9,11},{10,... | collective-permute-start | bytes 786440 | tf_op jit(solution)/shard_map/ppermute | solution.py:78
  34.6 1.8 %multiply_reduce_fusion = f32[512]{0:T(512)S(1)} fusion(f32[512,1024]{1,0:T(8,128)} %param.3), kind=kLoop, calls=%fused_computation.17 | loop fusion | flops 1048064 | bytes 2099200 | tf_op jit(solution)/shard_map/reduce_sum | solution.py:58
  36.5 0.1 stack.76
  36.6 0.0 collective-permute-done.3
  36.6 0.0 copy-start.6
  36.6 0.6 collective-permute-start.4
  37.2 0.0 collective-permute-done.1
  37.2 0.0 copy-start.7
  37.3 0.1 collective-permute-start.2
  37.3 0.0 collective-permute-done.10
  37.4 0.0 copy-start.8
  37.4 0.5 collective-permute-start.11
  37.9 4.1 %collective-permute-done.7 = bf16[2,64,1024]{2,1,0:T(8,128)(2,1)S(1)} collective-permute-done((bf16[2,64,1024]{2,1,0:T(8,128)(2,1)S(1)}, bf16[2,64,1024]{2,1,0:T(8,128)(2,1)S(1)}, u32[]{:S(2)}, u32[]{:S(2)}) %collective-permute-start.7) | collective-permute-done | bytes 262176 | tf_op jit(solution)/shard_map/ppermute | solution.py:78
  42.0 0.0 copy-start.9
  42.1 0.1 collective-permute-start.8
  42.2 3.0 %collective-permute-done.4 = bf16[2,64,1024]{2,1,0:T(8,128)(2,1)S(1)} collective-permute-done((bf16[2,64,1024]{2,1,0:T(8,128)(2,1)S(1)}, bf16[2,64,1024]{2,1,0:T(8,128)(2,1)S(1)}, u32[]{:S(2)}, u32[]{:S(2)}) %collective-permute-start.4) | collective-permute-done | bytes 262176 | tf_op jit(solution)/shard_map/ppermute | solution.py:78
  45.1 0.1 collective-permute-start.5
  45.2 0.1 pad_add_fusion
  45.3 0.0 copy-done.4
  45.3 0.0 copy-done.5
  45.3 0.0 copy-done.6
  45.3 0.0 copy-done.7
  45.3 0.0 copy-done.8
  45.4 0.0 copy-done.9
  45.4 0.0 copy-start.3
  45.4 0.0 collective-permute-done.2
  45.4 0.0 collective-permute-done.11
  45.4 0.0 collective-permute-done.8
  45.4 1.7 %collective-permute-done.5 = bf16[2,128,1024]{2,1,0:T(8,128)(2,1)S(1)} collective-permute-done((bf16[2,128,1024]{2,1,0:T(8,128)(2,1)S(1)}, bf16[2,128,1024]{2,1,0:T(8,128)(2,1)S(1)}, u32[]{:S(2)}, u32[]{:S(2)}) %collective-permute-start.5) | collective-permute-done | bytes 524320 | tf_op jit(solution)/shard_map/ppermute | solution.py:78
  47.1 2.6 %maximum_maximum_fusion = bf16[8,256,1024]{2,1,0:T(8,128)(2,1)S(1)} fusion(bf16[2,128,1024]{2,1,0:T(8,128)(2,1)S(1)} %collective-permute-done.11, bf16[2,64,1024]{2,1,0:T(8,128)(2,1)} %copy-done.8, bf16[2,64,1024]{2,1,0:T(8,128)(2,1)} %copy-done.4, bf16[2,128,1024]{2,1,0:T(8,128)(2,1)S(1)} %collective-permute-done.8, bf16[2,64,1024]{2,1,0:T(8,128)(2,1)} %copy-done.9, ...), kind=kLoop, calls=%fused_computation | loop fusion | flops 54525952 | bytes 8388608 | tf_op jit(solution)/shard_map/concatenate | solution.py:86
  49.8 0.0 copy-start.1
  49.8 0.0 copy-done.3
  49.8 4.7 %fusion.12 = (f32[2048]{0:T(1024)S(1)}, f32[2048,512]{1,0:T(8,128)}) fusion(f32[512]{0:T(512)S(1)} %multiply_reduce_fusion, bf16[2048,1024]{1,0:T(8,128)(2,1)S(1)} %bitcast.76, f32[512,1024]{1,0:T(8,128)S(1)} %copy-done.3), kind=kOutput, calls=%fused_computation.59 | convolution fusion | flops 2152200192 | bytes 10496000 | tf_op jit(solution)/shard_map/dot_general | solution.py:10
  54.5 0.0 copy-done.1
  54.5 0.1 broadcast_in_dim.143
  54.5 3.3 %exponential_reduce_fusion = f32[2048]{0:T(1024)S(1)} fusion(f32[2048,512]{1,0:T(8,128)} %get-tuple-element.20, f32[2048]{0:T(1024)S(1)} %get-tuple-element.19), kind=kLoop, calls=%fused_computation.3 | loop fusion | flops 2095104 | bytes 4210688 | tf_op jit(solution)/shard_map/reduce_sum | solution.py:18
  57.9 0.1 broadcast_in_dim.148
  58.0 0.1 select_reduce_fusion.7
  58.0 0.2 select_reduce_fusion.3
  58.3 9.3 %all-gather = f32[16,8,4,64]{3,1,2,0:T(8,128)S(1)} all-gather(f32[2,8,4,64]{3,1,2,0:T(8,128)S(1)} %copy.31), channel_id=2, replica_groups=mesh['outer'=4,'dp'=2,'cent'=4] {'dp','cent'}, dimensions={0}, use_global_device_ids=true | all-gather | bytes 147456 | tf_op jit(solution)/shard_map/all_gather | solution.py:108
  67.7 0.1 select_reduce_fusion.1
  67.8 0.1 select_reduce_fusion.5
  67.9 0.1 div.48
  68.0 0.1 sub.75
  68.0 0.0 copy-start.2
  68.0 2.9 %convert_reduce_fusion = (f32[4,512]{1,0:T(4,128)S(1)}, bf16[2048,512]{1,0:T(8,128)(2,1)S(1)}) fusion(f32[2048]{0:T(1024)S(1)} %div.48, f32[2048,512]{1,0:T(8,128)} %get-tuple-element.20, f32[2048]{0:T(1024)S(1)} %sub.75), kind=kLoop, calls=%fused_computation.1 | loop fusion | flops 5240832 | bytes 6316032 | tf_op jit(solution)/shard_map/reduce_sum | solution.py:120
  70.9 0.5 copy-done.2
  71.5 2.4 %fusion.13 = f32[4,512,1024]{2,1,0:T(8,128)S(1)} fusion(bf16[4,512,512]{2,1,0:T(8,128)(2,1)S(1)} %bitcast.78, bf16[4,512,1024]{2,1,0:T(8,128)(2,1)S(1)} %bitcast.77), kind=kOutput, calls=%fused_computation.60 | convolution fusion | flops 2147483648 | bytes 14680064 | tf_op jit(solution)/shard_map/dot_general | solution.py:121
  74.0 3.7 %fusion.2 = f32[512,1024]{1,0:T(8,128)} fusion(f32[512,1024]{1,0:T(8,128)S(1)} %copy-done.3, f32[4,512,1024]{2,1,0:T(8,128)S(1)} %fusion.13, f32[512]{0:T(512)S(1)} %get-tuple-element.21, f32[512]{0:T(512)S(1)} %bitcast.89, f32[512]{0:T(512)S(1)} %get-tuple-element.22, f32[512]{0:T(512)S(1)} %bitcast.87, f32[512]{0:T(512)S(1)} %get-tuple-element.23, ...), kind=kLoop, calls=%fused_computation.8 | loop fusion | flops 14680064 | bytes 12599308 | tf_op jit(solution)/shard_map/div | solution.py:135
  (23 shorter events, 0.4 us)
Async XLA Ops:
  0.0 1.2 %copy-start = (f32[256,1024]{1,0:T(8,128)S(1)}, f32[256,1024]{1,0:T(8,128)}, u32[]{:S(2)}) copy-start(f32[256,1024]{1,0:T(8,128)} %param.2) | copy-start | bytes 3145732
  1.2 6.5 %collective-permute-start = (bf16[64,1024]{1,0:T(8,128)(2,1)S(1)}, bf16[64,1024]{1,0:T(8,128)(2,1)S(1)}, u32[]{:S(2)}, u32[]{:S(2)}) collective-permute-start(bf16[64,1024]{1,0:T(8,128)(2,1)S(1)} %dynamic-slice_convert_fusion), channel_id=1, source_target_pairs={{0,4},{4,0},{1,5},{5,1},{2,6},{6,2},{3,7},{7,3},{8,12},{12,8},{9,1... | collective-permute-start | bytes 393224 | tf_op jit(solution)/shard_map/ppermute | solution.py:73
  7.8 10.7 %collective-permute-start.9 = (bf16[2,64,1024]{2,1,0:T(8,128)(2,1)S(1)}, bf16[2,64,1024]{2,1,0:T(8,128)(2,1)S(1)}, u32[]{:S(2)}, u32[]{:S(2)}) collective-permute-start(bf16[2,64,1024]{2,1,0:T(8,128)(2,1)S(1)} %pad_maximum_fusion.4), channel_id=1, source_target_pairs={{0,24},{8,0},{16,8},{24,16},{1,25},{9,1},{17,9},{25,17},{2,26},{10... | collective-permute-start | bytes 786440 | tf_op jit(solution)/shard_map/ppermute | solution.py:84
  11.7 21.4 %collective-permute-start.6 = (bf16[2,64,1024]{2,1,0:T(8,128)(2,1)S(1)}, bf16[2,64,1024]{2,1,0:T(8,128)(2,1)S(1)}, u32[]{:S(2)}, u32[]{:S(2)}) collective-permute-start(bf16[2,64,1024]{2,1,0:T(8,128)(2,1)S(1)} %pad_maximum_fusion.4), channel_id=1, source_target_pairs={{0,16},{8,24},{16,0},{24,8},{1,17},{9,25},{17,1},{25,9},{2,18},{10... | collective-permute-start | bytes 786440 | tf_op jit(solution)/shard_map/ppermute | solution.py:84
  11.7 24.9 %collective-permute-start.3 = (bf16[2,64,1024]{2,1,0:T(8,128)(2,1)S(1)}, bf16[2,64,1024]{2,1,0:T(8,128)(2,1)S(1)}, u32[]{:S(2)}, u32[]{:S(2)}) collective-permute-start(bf16[2,64,1024]{2,1,0:T(8,128)(2,1)S(1)} %pad_maximum_fusion.4), channel_id=1, source_target_pairs={{0,8},{8,16},{16,24},{24,0},{1,9},{9,17},{17,25},{25,1},{2,10},{10... | collective-permute-start | bytes 786440 | tf_op jit(solution)/shard_map/ppermute | solution.py:84
  12.7 24.5 %collective-permute-start.1 = (bf16[2,64,1024]{2,1,0:T(8,128)(2,1)S(1)}, bf16[2,64,1024]{2,1,0:T(8,128)(2,1)S(1)}, u32[]{:S(2)}, u32[]{:S(2)}) collective-permute-start(bf16[2,64,1024]{2,1,0:T(8,128)(2,1)S(1)} %pad_maximum_fusion.4), channel_id=1, source_target_pairs={{0,2},{1,3},{2,0},{3,1},{4,6},{5,7},{6,4},{7,5},{8,10},{9,11},{10,... | collective-permute-start | bytes 786440 | tf_op jit(solution)/shard_map/ppermute | solution.py:78
  18.5 26.8 %copy-start.4 = (bf16[2,64,1024]{2,1,0:T(8,128)(2,1)}, bf16[2,64,1024]{2,1,0:T(8,128)(2,1)S(1)}, u32[]{:S(2)}) copy-start(bf16[2,64,1024]{2,1,0:T(8,128)(2,1)S(1)} %collective-permute-done.9) | copy-start | bytes 786436
  18.5 18.9 %collective-permute-start.10 = (bf16[2,64,1024]{2,1,0:T(8,128)(2,1)S(1)}, bf16[2,64,1024]{2,1,0:T(8,128)(2,1)S(1)}, u32[]{:S(2)}, u32[]{:S(2)}) collective-permute-start(bf16[2,64,1024]{2,1,0:T(8,128)(2,1)S(1)} %collective-permute-done.9), channel_id=1, source_target_pairs={{0,2},{1,3},{2,0},{3,1},{4,6},{5,7},{6,4},{7,5},{8,10},{9,11},{10,... | collective-permute-start | bytes 786440 | tf_op jit(solution)/shard_map/ppermute | solution.py:78
  33.1 12.2 %copy-start.5 = (bf16[2,64,1024]{2,1,0:T(8,128)(2,1)}, bf16[2,64,1024]{2,1,0:T(8,128)(2,1)S(1)}, u32[]{:S(2)}) copy-start(bf16[2,64,1024]{2,1,0:T(8,128)(2,1)S(1)} %collective-permute-done.6) | copy-start | bytes 786436
  33.1 8.9 %collective-permute-start.7 = (bf16[2,64,1024]{2,1,0:T(8,128)(2,1)S(1)}, bf16[2,64,1024]{2,1,0:T(8,128)(2,1)S(1)}, u32[]{:S(2)}, u32[]{:S(2)}) collective-permute-start(bf16[2,64,1024]{2,1,0:T(8,128)(2,1)S(1)} %collective-permute-done.6), channel_id=1, source_target_pairs={{0,2},{1,3},{2,0},{3,1},{4,6},{5,7},{6,4},{7,5},{8,10},{9,11},{10,... | collective-permute-start | bytes 786440 | tf_op jit(solution)/shard_map/ppermute | solution.py:78
  36.6 8.7 %copy-start.6 = (bf16[2,64,1024]{2,1,0:T(8,128)(2,1)}, bf16[2,64,1024]{2,1,0:T(8,128)(2,1)S(1)}, u32[]{:S(2)}) copy-start(bf16[2,64,1024]{2,1,0:T(8,128)(2,1)S(1)} %collective-permute-done.3) | copy-start | bytes 786436
  36.6 8.5 %collective-permute-start.4 = (bf16[2,64,1024]{2,1,0:T(8,128)(2,1)S(1)}, bf16[2,64,1024]{2,1,0:T(8,128)(2,1)S(1)}, u32[]{:S(2)}, u32[]{:S(2)}) collective-permute-start(bf16[2,64,1024]{2,1,0:T(8,128)(2,1)S(1)} %collective-permute-done.3), channel_id=1, source_target_pairs={{0,2},{1,3},{2,0},{3,1},{4,6},{5,7},{6,4},{7,5},{8,10},{9,11},{10,... | collective-permute-start | bytes 786440 | tf_op jit(solution)/shard_map/ppermute | solution.py:78
  37.2 8.1 %copy-start.7 = (bf16[2,64,1024]{2,1,0:T(8,128)(2,1)}, bf16[2,64,1024]{2,1,0:T(8,128)(2,1)S(1)}, u32[]{:S(2)}) copy-start(bf16[2,64,1024]{2,1,0:T(8,128)(2,1)S(1)} %collective-permute-done.1) | copy-start | bytes 786436
  37.3 8.1 %collective-permute-start.2 = (bf16[2,128,1024]{2,1,0:T(8,128)(2,1)S(1)}, bf16[2,128,1024]{2,1,0:T(8,128)(2,1)S(1)}, u32[]{:S(2)}, u32[]{:S(2)}) collective-permute-start(bf16[2,128,1024]{2,1,0:T(8,128)(2,1)S(1)} %pad_maximum_fusion), channel_id=1, source_target_pairs={{0,1},{1,0},{2,3},{3,2},{4,5},{5,4},{6,7},{7,6},{8,9},{9,8},{10,11... | collective-permute-start | bytes 1572872 | tf_op jit(solution)/shard_map/ppermute | solution.py:78
  37.4 8.0 %copy-start.8 = (bf16[2,64,1024]{2,1,0:T(8,128)(2,1)}, bf16[2,64,1024]{2,1,0:T(8,128)(2,1)S(1)}, u32[]{:S(2)}) copy-start(bf16[2,64,1024]{2,1,0:T(8,128)(2,1)S(1)} %collective-permute-done.10) | copy-start | bytes 786436
  37.4 8.0 %collective-permute-start.11 = (bf16[2,128,1024]{2,1,0:T(8,128)(2,1)S(1)}, bf16[2,128,1024]{2,1,0:T(8,128)(2,1)S(1)}, u32[]{:S(2)}, u32[]{:S(2)}) collective-permute-start(bf16[2,128,1024]{2,1,0:T(8,128)(2,1)S(1)} %pad_maximum_fusion.3), channel_id=1, source_target_pairs={{0,1},{1,0},{2,3},{3,2},{4,5},{5,4},{6,7},{7,6},{8,9},{9,8},{10,11... | collective-permute-start | bytes 1572872 | tf_op jit(solution)/shard_map/ppermute | solution.py:78
  42.0 3.3 %copy-start.9 = (bf16[2,64,1024]{2,1,0:T(8,128)(2,1)}, bf16[2,64,1024]{2,1,0:T(8,128)(2,1)S(1)}, u32[]{:S(2)}) copy-start(bf16[2,64,1024]{2,1,0:T(8,128)(2,1)S(1)} %collective-permute-done.7) | copy-start | bytes 786436
  42.1 3.3 %collective-permute-start.8 = (bf16[2,128,1024]{2,1,0:T(8,128)(2,1)S(1)}, bf16[2,128,1024]{2,1,0:T(8,128)(2,1)S(1)}, u32[]{:S(2)}, u32[]{:S(2)}) collective-permute-start(bf16[2,128,1024]{2,1,0:T(8,128)(2,1)S(1)} %pad_maximum_fusion.2), channel_id=1, source_target_pairs={{0,1},{1,0},{2,3},{3,2},{4,5},{5,4},{6,7},{7,6},{8,9},{9,8},{10,11... | collective-permute-start | bytes 1572872 | tf_op jit(solution)/shard_map/ppermute | solution.py:78
  45.1 2.0 %collective-permute-start.5 = (bf16[2,128,1024]{2,1,0:T(8,128)(2,1)S(1)}, bf16[2,128,1024]{2,1,0:T(8,128)(2,1)S(1)}, u32[]{:S(2)}, u32[]{:S(2)}) collective-permute-start(bf16[2,128,1024]{2,1,0:T(8,128)(2,1)S(1)} %pad_maximum_fusion.1), channel_id=1, source_target_pairs={{0,1},{1,0},{2,3},{3,2},{4,5},{5,4},{6,7},{7,6},{8,9},{9,8},{10,11... | collective-permute-start | bytes 1572872 | tf_op jit(solution)/shard_map/ppermute | solution.py:78
  45.4 4.4 %copy-start.3 = (f32[512,1024]{1,0:T(8,128)S(1)}, f32[512,1024]{1,0:T(8,128)}, u32[]{:S(2)}) copy-start(f32[512,1024]{1,0:T(8,128)} %param.3) | copy-start | bytes 6291460
  49.8 4.7 %copy-start.1 = (bf16[8,256,1024]{2,1,0:T(8,128)(2,1)}, bf16[8,256,1024]{2,1,0:T(8,128)(2,1)S(1)}, u32[]{:S(2)}) copy-start(bf16[8,256,1024]{2,1,0:T(8,128)(2,1)S(1)} %maximum_maximum_fusion) | copy-start | bytes 12582916
  68.0 3.4 %copy-start.2 = (bf16[8,256,1024]{2,1,0:T(8,128)(2,1)S(1)}, bf16[8,256,1024]{2,1,0:T(8,128)(2,1)}, u32[]{:S(2)}) copy-start(bf16[8,256,1024]{2,1,0:T(8,128)(2,1)} %copy-done.1) | copy-start | bytes 12582916

commit v7 on v6

--- a/solution.py
+++ b/solution.py
@@ -83,11 +83,15 @@
     for sz in range(1, n_o):
         moved = lax.ppermute(pair, "outer", [(i, (i + sz) % n_o) for i in range(n_o)])
         parts.append(spread(moved))
+    part_rows = [p.reshape(n_d * n_c * tq, d) for p in parts]
+    part_logits = [scores_for(r, cent_bf, squares) for r in part_rows]
+    part_stats = [row_summary(lg) for lg in part_logits]
+    local_max = jnp.concatenate([st[0] for st in part_stats])
+    local_sum = jnp.concatenate([st[1] for st in part_stats])
     cur = jnp.concatenate(parts, axis=0)
     everything = cur.reshape(n_od * n_c * tq, d)
 
-    logits = scores_for(everything, cent_bf, squares)
-    local_max, local_sum = row_summary(logits)
+    logits = jnp.concatenate(part_logits, axis=0)
 
     src_vec = jnp.stack([((z - sz) % n_o) * n_d + (y - sy) % n_d for sz, sy in shifts])
     hot_k = src_vec[None, :] == jnp.arange(n_od)[:, None]

time: 78.1 us -> 106 us (1.36)
  local copies, waits for them, and re-layouts: 2.28 us -> 17.6 us
  other arithmetic: 15.2 us -> 29.4 us
  matrix products: 7.1 us -> 12.5 us
  waiting for transfers between devices: 29.7 us -> 24.8 us
  starting transfers between devices: 13.7 us -> 11.8 us
    concatenate x0 -> x11, local copies, waits for them, and re-layouts: none -> 11.3 us  [the longest x3 5.67 us: spread(): cur = jnp.concatenate([cur, other], axis=1)]
    dot_general x1 -> x4, matrix products: 4.68 us -> 10.2 us  [scores_for(): lax.dot_general(piece, cent_bf, (((1,), (1,)), ((), ())), preferred_eleme...]
    unnamed x20 -> x34, local copies, waits for them, and re-layouts: 1.81 us -> 5.94 us
    concatenate x0 -> x1, other arithmetic: none -> 3.87 us  [shards_all(): logits = jnp.concatenate(part_logits, axis=0)]
    ppermute x1, waiting for transfers between devices: 3.48 us -> 0.01 us  [shards_all(): lax.ppermute(mine, 'dp', [(j, (j + sy) % n_d) for j in range(n_d)])]
    concatenate x4 -> x5, other arithmetic: 0.14 us -> 3.59 us  [spread(): cur = jnp.concatenate([cur, other], axis=1)]
    reduce_sum x1 -> x4, other arithmetic: 3.31 us -> 5.6 us  [row_summary(): local_sum = jnp.sum(jnp.exp(logits - local_max[:, None]), axis=1)]
    reduce_sum x1, other arithmetic: 1.8 us -> 3.49 us  [shards_all(): squares = jnp.sum(centroids * centroids, axis=1)]
  transfers between devices with their start and end apart: 12 -> 12, of which waited for: 6 -> 5; matrix products, arithmetic and copies ran while one was open for 3% -> 22% of each run, Pallas kernels for 0% -> 0%
where the time goes in v7:
time: 106 us; the launch traced here: 105 us
  other arithmetic  29.4 us (28%)
  waiting for transfers between devices  24.8 us (23%)
  local copies, waits for them, and re-layouts  17.6 us (17%)
  matrix products  12.5 us (12%)
  starting transfers between devices  11.8 us (11%)
  blocking collectives  8.34 us (8%)
    ppermute x3, waiting for transfers between devices, shards_all(): lax.ppermute(pair, 'outer', [(i, (i + sz) % n_o) for i in range(n_o)])  16.8 us
    dot_general x4, matrix products, scores_for(): lax.dot_general(piece, cent_bf, (((1,), (1,)), ((), ())), preferred_eleme...  10.2 us
    all_gather x1, blocking collectives, shards_all(): every = lax.all_gather(both, ('dp', 'cent'), axis=0)  8.34 us
    ppermute x8, waiting for transfers between devices, spread(): other = lax.ppermute(cur, 'cent', [(i, i ^ bit) for i in range(n_c)])  7.97 us
    unnamed x34, local copies, waits for them, and re-layouts  5.94 us
    concatenate x3, local copies, waits for them, and re-layouts, spread(): cur = jnp.concatenate([cur, other], axis=1)  5.67 us
    reduce_sum x4, other arithmetic, row_summary(): local_sum = jnp.sum(jnp.exp(logits - local_max[:, None]), axis=1)  5.6 us
    concatenate x4, local copies, waits for them, and re-layouts, shards_all(): local_sum = jnp.concatenate([st[1] for st in part_stats])  4.69 us
  transfers between devices with their start and end apart: 12, of which 5 were waited for; matrix products, arithmetic and copies ran while one was open for 22% of the time, Pallas kernels for 0%

profile of v7, /device:TPU:0, one launch (start us, length us, event | category | flops | bytes accessed | tf_op | source)
XLA Modules:
  0.0 104.8 jit_solution(7437057813865397529)
XLA Ops:
  0.0 1.2 %copy-done = f32[256,1024]{1,0:T(8,128)S(1)} copy-done((f32[256,1024]{1,0:T(8,128)S(1)}, f32[256,1024]{1,0:T(8,128)}, u32[]{:S(2)}) %copy-start) | copy-done | bytes 1048600
  1.2 3.0 %collective-permute-start = (bf16[64,1024]{1,0:T(8,128)(2,1)S(1)}, bf16[64,1024]{1,0:T(8,128)(2,1)S(1)}, u32[]{:S(2)}, u32[]{:S(2)}) collective-permute-start(bf16[64,1024]{1,0:T(8,128)(2,1)S(1)} %dynamic-slice_convert_fusion), channel_id=1, source_target_pairs={{0,4},{4,0},{1,5},{5,1},{2,6},{6,2},{3,7},{7,3},{8,12},{12,8},{9,1... | collective-permute-start | bytes 393224 | tf_op jit(solution)/shard_map/ppermute | solution.py:73
  4.3 3.5 %multiply_reduce_fusion = (f32[512]{0:T(512)S(1)}, bf16[512,1024]{1,0:T(8,128)(2,1)}) fusion(f32[512,1024]{1,0:T(8,128)} %param.3), kind=kLoop, calls=%fused_computation.19 | loop fusion | flops 1572352 | bytes 3147776 | tf_op jit(solution)/shard_map/reduce_sum | solution.py:58
  7.8 0.1 stack.76
  7.9 0.5 iota_compare_fusion
  8.4 0.7 pad_maximum_fusion.7
  9.2 1.5 %collective-permute-start.1 = (bf16[2,64,1024]{2,1,0:T(8,128)(2,1)}, bf16[2,64,1024]{2,1,0:T(8,128)(2,1)S(1)}, u32[]{:S(2)}, u32[]{:S(2)}) collective-permute-start(bf16[2,64,1024]{2,1,0:T(8,128)(2,1)} %pad_maximum_fusion.7), channel_id=1, source_target_pairs={{0,2},{1,3},{2,0},{3,1},{4,6},{5,7},{6,4},{7,5},{8,10},{9,11},{10,... | collective-permute-start | bytes 786440 | tf_op jit(solution)/shard_map/ppermute | solution.py:78
  10.7 0.1 pad_add_fusion
  10.7 3.6 %collective-permute-start.9 = (bf16[2,64,1024]{2,1,0:T(8,128)(2,1)}, bf16[2,64,1024]{2,1,0:T(8,128)(2,1)}, u32[]{:S(2)}, u32[]{:S(2)}) collective-permute-start(bf16[2,64,1024]{2,1,0:T(8,128)(2,1)} %pad_maximum_fusion.7), channel_id=1, source_target_pairs={{0,24},{8,0},{16,8},{24,16},{1,25},{9,1},{17,9},{25,17},{2,26},{10... | collective-permute-start | bytes 786440 | tf_op jit(solution)/shard_map/ppermute | solution.py:84
  14.3 0.0 collective-permute-start.6
  14.3 0.5 iota_compare_fusion.1
  14.9 1.0 collective-permute-start.3
  15.9 1.3 %collective-permute-done.1 = bf16[2,64,1024]{2,1,0:T(8,128)(2,1)S(1)} collective-permute-done((bf16[2,64,1024]{2,1,0:T(8,128)(2,1)}, bf16[2,64,1024]{2,1,0:T(8,128)(2,1)S(1)}, u32[]{:S(2)}, u32[]{:S(2)}) %collective-permute-start.1) | collective-permute-done | bytes 262176 | tf_op jit(solution)/shard_map/ppermute | solution.py:78
  17.2 0.1 collective-permute-start.2
  17.3 4.2 %collective-permute-done.9 = bf16[2,64,1024]{2,1,0:T(8,128)(2,1)} collective-permute-done((bf16[2,64,1024]{2,1,0:T(8,128)(2,1)}, bf16[2,64,1024]{2,1,0:T(8,128)(2,1)}, u32[]{:S(2)}, u32[]{:S(2)}) %collective-permute-start.9) | collective-permute-done | bytes 262176 | tf_op jit(solution)/shard_map/ppermute | solution.py:84
  21.5 0.5 collective-permute-start.10
  22.0 1.7 %constant_dynamic-update-slice_fusion.8 = bf16[2,256,1024]{2,1,0:T(8,128)(2,1)} fusion(bf16[2,64,1024]{2,1,0:T(8,128)(2,1)} %collective-permute-done.9), kind=kLoop, calls=%fused_computation.66 | loop fusion | bytes 524288
  23.7 12.6 %collective-permute-done.6 = bf16[2,64,1024]{2,1,0:T(8,128)(2,1)S(1)} collective-permute-done((bf16[2,64,1024]{2,1,0:T(8,128)(2,1)}, bf16[2,64,1024]{2,1,0:T(8,128)(2,1)S(1)}, u32[]{:S(2)}, u32[]{:S(2)}) %collective-permute-start.6) | collective-permute-done | bytes 262176 | tf_op jit(solution)/shard_map/ppermute | solution.py:84
  36.3 0.5 collective-permute-start.7
  36.9 1.6 %collective-permute-start.4 = (bf16[2,64,1024]{2,1,0:T(8,128)(2,1)S(1)}, bf16[2,64,1024]{2,1,0:T(8,128)(2,1)S(1)}, u32[]{:S(2)}, u32[]{:S(2)}) collective-permute-start(bf16[2,64,1024]{2,1,0:T(8,128)(2,1)S(1)} %collective-permute-done.3), channel_id=1, source_target_pairs={{0,2},{1,3},{2,0},{3,1},{4,6},{5,7},{6,4},{7,5},{8,10},{9,11},{10,... | collective-permute-start | bytes 786440 | tf_op jit(solution)/shard_map/ppermute | solution.py:78
  38.4 0.7 constant_dynamic-update-slice_fusion.2
  39.1 1.8 %pad_maximum_fusion.6 = bf16[2,128,1024]{2,1,0:T(8,128)(2,1)} fusion(bf16[2,64,1024]{2,1,0:T(8,128)(2,1)S(1)} %collective-permute-done.10, bf16[2,64,1024]{2,1,0:T(8,128)(2,1)} %collective-permute-done.9), kind=kLoop, calls=%fused_computation.40 | loop fusion | flops 1048576 | bytes 1048576 | tf_op jit(solution)/shard_map/concatenate | solution.py:79
  40.9 4.6 %collective-permute-done.7 = bf16[2,64,1024]{2,1,0:T(8,128)(2,1)S(1)} collective-permute-done((bf16[2,64,1024]{2,1,0:T(8,128)(2,1)S(1)}, bf16[2,64,1024]{2,1,0:T(8,128)(2,1)S(1)}, u32[]{:S(2)}, u32[]{:S(2)}) %collective-permute-start.7) | collective-permute-done | bytes 262176 | tf_op jit(solution)/shard_map/ppermute | solution.py:78
  45.5 0.8 pad_maximum_fusion.5
  46.4 2.1 %collective-permute-done.4 = bf16[2,64,1024]{2,1,0:T(8,128)(2,1)S(1)} collective-permute-done((bf16[2,64,1024]{2,1,0:T(8,128)(2,1)S(1)}, bf16[2,64,1024]{2,1,0:T(8,128)(2,1)S(1)}, u32[]{:S(2)}, u32[]{:S(2)}) %collective-permute-start.4) | collective-permute-done | bytes 262176 | tf_op jit(solution)/shard_map/ppermute | solution.py:78
  48.5 0.8 pad_maximum_fusion.4
  49.3 0.7 constant_dynamic-update-slice_fusion.7
  50.1 0.8 constant_dynamic-update-slice_fusion.1
  50.8 0.1 pad_maximum_fusion.2
  50.9 0.3 copy-done.6
  51.2 0.5 copy-done.4
  51.6 0.8 fusion.26
  52.4 0.1 concatenate.70
  52.5 0.2 exponential_reduce_fusion.3
  52.7 0.7 concatenate.75
  53.4 1.9 %constant_dynamic-update-slice_fusion.6 = bf16[2,256,1024]{2,1,0:T(8,128)(2,1)} fusion(bf16[2,256,1024]{2,1,0:T(8,128)(2,1)} %constant_dynamic-update-slice_fusion.7, bf16[2,128,1024]{2,1,0:T(8,128)(2,1)} %collective-permute-done.11), kind=kLoop, calls=%fused_computation.64 | loop fusion | bytes 1048576 | tf_op jit(solution)/shard_map/concatenate | solution.py:79
  55.3 2.3 %fusion.23 = (f32[512]{0:T(512)S(1)}, f32[512,512]{0,1:T(8,128)S(1)}) fusion(f32[512]{0:T(512)S(1)} %get-tuple-element.15, bf16[512,1024]{1,0:T(8,128)(2,1)} %bitcast.5, bf16[512,1024]{1,0:T(8,128)(2,1)} %get-tuple-element.16), kind=kOutput, calls=%fused_computation.88 | convolution fusion | flops 537918976 | bytes 3149824 | tf_op jit(solution)/shard_map/dot_general | solution.py:10
  57.6 0.1 concatenate.73
  57.7 1.9 %constant_dynamic-update-slice_fusion.3 = bf16[2,256,1024]{2,1,0:T(8,128)(2,1)} fusion(bf16[2,256,1024]{2,1,0:T(8,128)(2,1)} %copy-done.6, bf16[2,128,1024]{2,1,0:T(8,128)(2,1)} %collective-permute-done.8), kind=kLoop, calls=%fused_computation.61 | loop fusion | bytes 1048576 | tf_op jit(solution)/shard_map/concatenate | solution.py:79
  59.6 3.3 %fusion.24 = (f32[512]{0:T(512)S(1)}, f32[512,512]{0,1:T(8,128)}) fusion(f32[512]{0:T(512)} %copy-done.13, bf16[512,1024]{1,0:T(8,128)(2,1)} %bitcast.106, bf16[512,1024]{1,0:T(8,128)(2,1)} %get-tuple-element.16), kind=kOutput, calls=%fused_computation.89 | convolution fusion | flops 537918976 | bytes 3149824 | tf_op jit(solution)/shard_map/dot_general | solution.py:10
  62.8 0.1 concatenate.72
  62.9 1.9 %constant_dynamic-update-slice_fusion = bf16[2,256,1024]{2,1,0:T(8,128)(2,1)} fusion(bf16[2,256,1024]{2,1,0:T(8,128)(2,1)} %constant_dynamic-update-slice_fusion.1, bf16[2,128,1024]{2,1,0:T(8,128)(2,1)} %collective-permute-done.5), kind=kLoop, calls=%fused_computation.58 | loop fusion | bytes 1048576 | tf_op jit(solution)/shard_map/concatenate | solution.py:79
  64.8 3.9 %fusion.25 = (f32[512]{0:T(512)}, f32[512,512]{0,1:T(8,128)}) fusion(f32[512]{0:T(512)} %copy-done.13, bf16[512,1024]{1,0:T(8,128)(2,1)} %bitcast.3, bf16[512,1024]{1,0:T(8,128)(2,1)} %get-tuple-element.16), kind=kOutput, calls=%fused_computation.90 | convolution fusion | flops 537918976 | bytes 3149824 | tf_op jit(solution)/shard_map/dot_general | solution.py:10
  68.7 0.7 concatenate.71
  69.4 1.4 %exponential_reduce_fusion = f32[512]{0:T(512)} fusion(f32[512,512]{0,1:T(8,128)S(1)} %get-tuple-element.22, f32[512]{0:T(512)} %copy-done.9), kind=kLoop, calls=%fused_computation.33 | loop fusion | flops 523776 | bytes 1052672 | tf_op jit(solution)/shard_map/reduce_sum | solution.py:18
  70.8 1.3 %concatenate.78 = f32[2,1,4,64]{3,2,0,1:T(4,128)} reshape(f32[512]{0:T(512)} %exponential_reduce_fusion) | data formatting | bytes 4096 | tf_op jit(solution)/shard_map/concatenate | solution.py:90
  72.2 2.0 %exponential_reduce_fusion.1 = f32[512]{0:T(512)} fusion(f32[512,512]{0,1:T(8,128)} %get-tuple-element.24, f32[512]{0:T(512)} %copy-done.10), kind=kLoop, calls=%fused_computation.34 | loop fusion | flops 523776 | bytes 1052672 | tf_op jit(solution)/shard_map/reduce_sum | solution.py:18
  74.2 1.3 %concatenate.77 = f32[2,1,4,64]{3,2,0,1:T(4,128)} reshape(f32[512]{0:T(512)} %exponential_reduce_fusion.1) | data formatting | bytes 4096 | tf_op jit(solution)/shard_map/concatenate | solution.py:90
  75.5 2.0 %exponential_reduce_fusion.2 = f32[512]{0:T(512)} fusion(f32[512,512]{0,1:T(8,128)} %get-tuple-element.26, f32[512]{0:T(512)} %get-tuple-element.25), kind=kLoop, calls=%fused_computation.35 | loop fusion | flops 523776 | bytes 1052672 | tf_op jit(solution)/shard_map/reduce_sum | solution.py:18
  77.5 1.3 %concatenate.76 = f32[2,1,4,64]{3,2,0,1:T(4,128)} reshape(f32[512]{0:T(512)} %exponential_reduce_fusion.2) | data formatting | bytes 4096 | tf_op jit(solution)/shard_map/concatenate | solution.py:90
  78.8 0.7 maximum_bitcast_fusion.1
  79.6 0.7 select_reduce_fusion.7
  80.3 0.8 select_reduce_fusion.3
  81.1 8.3 %all-gather = f32[16,8,4,64]{3,1,2,0:T(8,128)S(1)} all-gather(f32[2,8,4,64]{3,1,2,0:T(8,128)S(1)} %copy.31), channel_id=2, replica_groups=mesh['outer'=4,'dp'=2,'cent'=4] {'dp','cent'}, dimensions={0}, use_global_device_ids=true | all-gather | bytes 147456 | tf_op jit(solution)/shard_map/all_gather | solution.py:112
  89.5 3.9 %pad_maximum_fusion = f32[2048,512]{0,1:T(8,128)} fusion(f32[512,512]{0,1:T(8,128)S(1)} %get-tuple-element.22, f32[512,512]{0,1:T(8,128)} %get-tuple-element.24, f32[512,512]{0,1:T(8,128)} %get-tuple-element.26, f32[512,512]{0,1:T(8,128)S(1)} %get-tuple-element.28), kind=kLoop, calls=%fused_computation.4 | loop fusion | flops 3145728 | bytes 8388608 | tf_op jit(solution)/shard_map/concatenate | solution.py:94
  93.4 0.1 select_reduce_fusion.1
  93.5 0.1 select_reduce_fusion.5
  93.6 0.1 div.49
  93.7 0.1 sub.127
  93.8 3.1 %convert_reduce_fusion = (f32[4,512]{1,0:T(4,128)S(1)}, bf16[4,512,512]{1,2,0:T(8,128)(2,1)S(1)}) fusion(f32[4,512]{1,0:T(4,128)S(1)} %div.49, f32[4,512]{1,0:T(4,128)S(1)} %sub.127, f32[64,4,8,512]{3,2,1,0:T(8,128)} %bitcast.99), kind=kLoop, calls=%fused_computation.6 | loop fusion | flops 5240832 | bytes 6316032 | tf_op jit(solution)/shard_map/reduce_sum | solution.py:124
  97.0 1.8 %pad_maximum_fusion.1 = bf16[8,256,1024]{2,1,0:T(8,128)(2,1)S(1)} fusion(bf16[2,256,1024]{2,1,0:T(8,128)(2,1)} %constant_dynamic-update-slice_fusion.6, bf16[2,256,1024]{2,1,0:T(8,128)(2,1)S(1)} %copy-done.7, bf16[2,256,1024]{2,1,0:T(8,128)(2,1)} %constant_dynamic-update-slice_fusion, bf16[2,128,1024]{2,1,0:T(8,128)(2,1)S(1)} %copy-done.5, ...), kind=kLoop, calls=%fused_computation.5 | loop fusion | flops 29360128 | bytes 8388608 | tf_op jit(solution)/shard_map/concatenate | solution.py:91
  98.8 0.0 copy-start.1
  98.8 2.3 %fusion.27 = f32[4,512,1024]{2,1,0:T(8,128)S(1)} fusion(bf16[4,512,512]{1,2,0:T(8,128)(2,1)S(1)} %get-tuple-element.14, bf16[4,512,1024]{2,1,0:T(8,128)(2,1)S(1)} %bitcast.98), kind=kOutput, calls=%fused_computation.92 | convolution fusion | flops 2147483648 | bytes 14680064 | tf_op jit(solution)/shard_map/dot_general | solution.py:125
  101.2 3.6 %fusion.5 = f32[512,1024]{1,0:T(8,128)} fusion(f32[512,1024]{1,0:T(8,128)S(1)} %copy-done.1, f32[4,512,1024]{2,1,0:T(8,128)S(1)} %fusion.27, f32[512]{0:T(512)S(1)} %get-tuple-element.29, f32[512]{0:T(512)S(1)} %bitcast.113, f32[512]{0:T(512)S(1)} %get-tuple-element.30, f32[512]{0:T(512)S(1)} %bitcast.111, f32[512]{0:T(512)S(1)} %get-tuple-element.31, ...), kind=kLoop, calls=%fused_computation.10 | loop fusion | flops 14680064 | bytes 12599308 | tf_op jit(solution)/shard_map/div | solution.py:139
  (54 shorter events, 0.3 us)
Async XLA Ops:
  0.0 1.2 %copy-start = (f32[256,1024]{1,0:T(8,128)S(1)}, f32[256,1024]{1,0:T(8,128)}, u32[]{:S(2)}) copy-start(f32[256,1024]{1,0:T(8,128)} %param.2) | copy-start | bytes 3145732
  1.2 7.2 %collective-permute-start = (bf16[64,1024]{1,0:T(8,128)(2,1)S(1)}, bf16[64,1024]{1,0:T(8,128)(2,1)S(1)}, u32[]{:S(2)}, u32[]{:S(2)}) collective-permute-start(bf16[64,1024]{1,0:T(8,128)(2,1)S(1)} %dynamic-slice_convert_fusion), channel_id=1, source_target_pairs={{0,4},{4,0},{1,5},{5,1},{2,6},{6,2},{3,7},{7,3},{8,12},{12,8},{9,1... | collective-permute-start | bytes 393224 | tf_op jit(solution)/shard_map/ppermute | solution.py:73
  7.8 47.5 %copy-start.13 = (f32[512]{0:T(512)}, f32[512]{0:T(512)S(1)}, u32[]{:S(2)}) copy-start(f32[512]{0:T(512)S(1)} %get-tuple-element.15) | copy-start | bytes 6148
  8.4 42.4 %copy-start.2 = (bf16[64,1024]{1,0:T(8,128)(2,1)}, bf16[64,1024]{1,0:T(8,128)(2,1)S(1)}, u32[]{:S(2)}) copy-start(bf16[64,1024]{1,0:T(8,128)(2,1)S(1)} %collective-permute-done) | copy-start | bytes 393220
  9.2 8.0 %collective-permute-start.1 = (bf16[2,64,1024]{2,1,0:T(8,128)(2,1)}, bf16[2,64,1024]{2,1,0:T(8,128)(2,1)S(1)}, u32[]{:S(2)}, u32[]{:S(2)}) collective-permute-start(bf16[2,64,1024]{2,1,0:T(8,128)(2,1)} %pad_maximum_fusion.7), channel_id=1, source_target_pairs={{0,2},{1,3},{2,0},{3,1},{4,6},{5,7},{6,4},{7,5},{8,10},{9,11},{10,... | collective-permute-start | bytes 786440 | tf_op jit(solution)/shard_map/ppermute | solution.py:78
  10.7 10.7 %collective-permute-start.9 = (bf16[2,64,1024]{2,1,0:T(8,128)(2,1)}, bf16[2,64,1024]{2,1,0:T(8,128)(2,1)}, u32[]{:S(2)}, u32[]{:S(2)}) collective-permute-start(bf16[2,64,1024]{2,1,0:T(8,128)(2,1)} %pad_maximum_fusion.7), channel_id=1, source_target_pairs={{0,24},{8,0},{16,8},{24,16},{1,25},{9,1},{17,9},{25,17},{2,26},{10... | collective-permute-start | bytes 786440 | tf_op jit(solution)/shard_map/ppermute | solution.py:84
  14.3 22.0 %collective-permute-start.6 = (bf16[2,64,1024]{2,1,0:T(8,128)(2,1)}, bf16[2,64,1024]{2,1,0:T(8,128)(2,1)S(1)}, u32[]{:S(2)}, u32[]{:S(2)}) collective-permute-start(bf16[2,64,1024]{2,1,0:T(8,128)(2,1)} %pad_maximum_fusion.7), channel_id=1, source_target_pairs={{0,16},{8,24},{16,0},{24,8},{1,17},{9,25},{17,1},{25,9},{2,18},{10... | collective-permute-start | bytes 786440 | tf_op jit(solution)/shard_map/ppermute | solution.py:84
  14.9 22.0 %collective-permute-start.3 = (bf16[2,64,1024]{2,1,0:T(8,128)(2,1)}, bf16[2,64,1024]{2,1,0:T(8,128)(2,1)S(1)}, u32[]{:S(2)}, u32[]{:S(2)}) collective-permute-start(bf16[2,64,1024]{2,1,0:T(8,128)(2,1)} %pad_maximum_fusion.7), channel_id=1, source_target_pairs={{0,8},{8,16},{16,24},{24,0},{1,9},{9,17},{17,25},{25,1},{2,10},{10... | collective-permute-start | bytes 786440 | tf_op jit(solution)/shard_map/ppermute | solution.py:84
  17.2 33.7 %collective-permute-start.2 = (bf16[2,128,1024]{2,1,0:T(8,128)(2,1)S(1)}, bf16[2,128,1024]{2,1,0:T(8,128)(2,1)S(1)}, u32[]{:S(2)}, u32[]{:S(2)}) collective-permute-start(bf16[2,128,1024]{2,1,0:T(8,128)(2,1)S(1)} %pad_maximum_fusion.3), channel_id=1, source_target_pairs={{0,1},{1,0},{2,3},{3,2},{4,5},{5,4},{6,7},{7,6},{8,9},{9,8},{10,11... | collective-permute-start | bytes 1572872 | tf_op jit(solution)/shard_map/ppermute | solution.py:78
  21.5 17.7 %collective-permute-start.10 = (bf16[2,64,1024]{2,1,0:T(8,128)(2,1)}, bf16[2,64,1024]{2,1,0:T(8,128)(2,1)S(1)}, u32[]{:S(2)}, u32[]{:S(2)}) collective-permute-start(bf16[2,64,1024]{2,1,0:T(8,128)(2,1)} %collective-permute-done.9), channel_id=1, source_target_pairs={{0,2},{1,3},{2,0},{3,1},{4,6},{5,7},{6,4},{7,5},{8,10},{9,11},{10,... | collective-permute-start | bytes 786440 | tf_op jit(solution)/shard_map/ppermute | solution.py:78
  36.3 9.2 %collective-permute-start.7 = (bf16[2,64,1024]{2,1,0:T(8,128)(2,1)S(1)}, bf16[2,64,1024]{2,1,0:T(8,128)(2,1)S(1)}, u32[]{:S(2)}, u32[]{:S(2)}) collective-permute-start(bf16[2,64,1024]{2,1,0:T(8,128)(2,1)S(1)} %collective-permute-done.6), channel_id=1, source_target_pairs={{0,2},{1,3},{2,0},{3,1},{4,6},{5,7},{6,4},{7,5},{8,10},{9,11},{10,... | collective-permute-start | bytes 786440 | tf_op jit(solution)/shard_map/ppermute | solution.py:78
  36.9 11.6 %collective-permute-start.4 = (bf16[2,64,1024]{2,1,0:T(8,128)(2,1)S(1)}, bf16[2,64,1024]{2,1,0:T(8,128)(2,1)S(1)}, u32[]{:S(2)}, u32[]{:S(2)}) collective-permute-start(bf16[2,64,1024]{2,1,0:T(8,128)(2,1)S(1)} %collective-permute-done.3), channel_id=1, source_target_pairs={{0,2},{1,3},{2,0},{3,1},{4,6},{5,7},{6,4},{7,5},{8,10},{9,11},{10,... | collective-permute-start | bytes 786440 | tf_op jit(solution)/shard_map/ppermute | solution.py:78
  40.9 12.4 %collective-permute-start.11 = (bf16[2,128,1024]{2,1,0:T(8,128)(2,1)}, bf16[2,128,1024]{2,1,0:T(8,128)(2,1)}, u32[]{:S(2)}, u32[]{:S(2)}) collective-permute-start(bf16[2,128,1024]{2,1,0:T(8,128)(2,1)} %pad_maximum_fusion.6), channel_id=1, source_target_pairs={{0,1},{1,0},{2,3},{3,2},{4,5},{5,4},{6,7},{7,6},{8,9},{9,8},{10,11... | collective-permute-start | bytes 1572872 | tf_op jit(solution)/shard_map/ppermute | solution.py:78
  46.4 11.3 %collective-permute-start.8 = (bf16[2,128,1024]{2,1,0:T(8,128)(2,1)}, bf16[2,128,1024]{2,1,0:T(8,128)(2,1)}, u32[]{:S(2)}, u32[]{:S(2)}) collective-permute-start(bf16[2,128,1024]{2,1,0:T(8,128)(2,1)} %pad_maximum_fusion.5), channel_id=1, source_target_pairs={{0,1},{1,0},{2,3},{3,2},{4,5},{5,4},{6,7},{7,6},{8,9},{9,8},{10,11... | collective-permute-start | bytes 1572872 | tf_op jit(solution)/shard_map/ppermute | solution.py:78
  49.3 2.3 %copy-start.8 = (bf16[512,1024]{1,0:T(8,128)(2,1)S(1)}, bf16[512,1024]{1,0:T(8,128)(2,1)}, u32[]{:S(2)}) copy-start(bf16[512,1024]{1,0:T(8,128)(2,1)} %get-tuple-element.16) | copy-start | bytes 3145732
  49.3 13.6 %collective-permute-start.5 = (bf16[2,128,1024]{2,1,0:T(8,128)(2,1)}, bf16[2,128,1024]{2,1,0:T(8,128)(2,1)}, u32[]{:S(2)}, u32[]{:S(2)}) collective-permute-start(bf16[2,128,1024]{2,1,0:T(8,128)(2,1)} %pad_maximum_fusion.4), channel_id=1, source_target_pairs={{0,1},{1,0},{2,3},{3,2},{4,5},{5,4},{6,7},{7,6},{8,9},{9,8},{10,11... | collective-permute-start | bytes 1572872 | tf_op jit(solution)/shard_map/ppermute | solution.py:78
  50.1 1.1 %copy-start.6 = (bf16[2,256,1024]{2,1,0:T(8,128)(2,1)}, bf16[2,256,1024]{2,1,0:T(8,128)(2,1)S(1)}, u32[]{:S(2)}) copy-start(bf16[2,256,1024]{2,1,0:T(8,128)(2,1)S(1)} %constant_dynamic-update-slice_fusion.4) | copy-start | bytes 3145732
  50.8 0.8 copy-start.4
  57.6 5.3 %copy-start.9 = (f32[512]{0:T(512)}, f32[512]{0:T(512)S(1)}, u32[]{:S(2)}) copy-start(f32[512]{0:T(512)S(1)} %get-tuple-element.21) | copy-start | bytes 6148
  62.8 5.8 %copy-start.10 = (f32[512]{0:T(512)}, f32[512]{0:T(512)S(1)}, u32[]{:S(2)}) copy-start(f32[512]{0:T(512)S(1)} %get-tuple-element.23) | copy-start | bytes 6148
  89.5 3.9 %copy-start.11 = (pred[8,8]{1,0:T(8,128)(4,1)S(1)}, pred[8,8]{1,0:T(8,128)(4,1)}, u32[]{:S(2)}) copy-start(pred[8,8]{1,0:T(8,128)(4,1)} %iota_compare_fusion) | copy-start | bytes 196
  89.5 4.0 %copy-start.12 = (pred[4,4]{1,0:T(4,128)(4,1)S(1)}, pred[4,4]{1,0:T(4,128)(4,1)}, u32[]{:S(2)}) copy-start(pred[4,4]{1,0:T(4,128)(4,1)} %iota_compare_fusion.1) | copy-start | bytes 52
  93.8 3.2 %copy-start.3 = (bf16[64,1024]{1,0:T(8,128)(2,1)S(1)}, bf16[64,1024]{1,0:T(8,128)(2,1)}, u32[]{:S(2)}) copy-start(bf16[64,1024]{1,0:T(8,128)(2,1)} %copy-done.2) | copy-start | bytes 393220
  93.8 3.2 %copy-start.5 = (bf16[2,128,1024]{2,1,0:T(8,128)(2,1)S(1)}, bf16[2,128,1024]{2,1,0:T(8,128)(2,1)}, u32[]{:S(2)}) copy-start(bf16[2,128,1024]{2,1,0:T(8,128)(2,1)} %copy-done.4) | copy-start | bytes 1572868
  93.8 3.2 %copy-start.7 = (bf16[2,256,1024]{2,1,0:T(8,128)(2,1)S(1)}, bf16[2,256,1024]{2,1,0:T(8,128)(2,1)}, u32[]{:S(2)}) copy-start(bf16[2,256,1024]{2,1,0:T(8,128)(2,1)} %constant_dynamic-update-slice_fusion.3) | copy-start | bytes 3145732
  98.8 2.4 %copy-start.1 = (f32[512,1024]{1,0:T(8,128)S(1)}, f32[512,1024]{1,0:T(8,128)}, u32[]{:S(2)}) copy-start(f32[512,1024]{1,0:T(8,128)} %param.3) | copy-start | bytes 6291460

commit v8 on v6

--- a/solution.py
+++ b/solution.py
@@ -68,10 +68,11 @@
 
     mine = lax.dynamic_slice_in_dim(rows_bf, q * tq, tq, 0)
     shifts = list(itertools.product(range(n_o), range(n_d)))
-    across = [mine]
-    for sy in range(1, n_d):
-        across.append(lax.ppermute(mine, "dp", [(j, (j + sy) % n_d) for j in range(n_d)]))
-    pair = jnp.stack(across)
+    def pair_of(piece):
+        across = [piece]
+        for sy in range(1, n_d):
+            across.append(lax.ppermute(piece, "dp", [(j, (j + sy) % n_d) for j in range(n_d)]))
+        return jnp.stack(across)
 
     def spread(cur):
         for bit in reversed(bits):
@@ -79,10 +80,10 @@
             cur = jnp.concatenate([cur, other], axis=1)
         return cur
 
-    parts = [spread(pair)]
+    landed = [mine]
     for sz in range(1, n_o):
-        moved = lax.ppermute(pair, "outer", [(i, (i + sz) % n_o) for i in range(n_o)])
-        parts.append(spread(moved))
+        landed.append(lax.ppermute(mine, "outer", [(i, (i + sz) % n_o) for i in range(n_o)]))
+    parts = [spread(pair_of(piece)) for piece in landed]
     cur = jnp.concatenate(parts, axis=0)
     everything = cur.reshape(n_od * n_c * tq, d)
 

time: 78.1 us -> 77.6 us (level)
  waiting for transfers between devices: 29.7 us -> 24.7 us
  starting transfers between devices: 13.7 us -> 16.9 us
  other arithmetic: 15.2 us -> 16.5 us
    ppermute x4 -> x7, waiting for transfers between devices: 20.9 us -> 6.89 us  [the longest x3 5.57 us: shards_all(): lax.ppermute(mine, 'outer', [(i, (i + sz) % n_o) for i in range(n_o)])]
    ppermute x8, waiting for transfers between devices: 8.75 us -> 17.8 us  [spread(): other = lax.ppermute(cur, 'cent', [(i, i ^ bit) for i in range(n_c)])]
    ppermute x4 -> x7, starting transfers between devices: 7.92 us -> 10.7 us  [the longest x3 6.11 us: shards_all(): lax.ppermute(mine, 'outer', [(i, (i + sz) % n_o) for i in range(n_o)])]
    concatenate x1, other arithmetic: 2.62 us -> 3.85 us  [shards_all(): cur = jnp.concatenate(parts, axis=0)]
    unnamed x20 -> x14, local copies, waits for them, and re-layouts: 1.81 us -> 1.8 us
  transfers between devices with their start and end apart: 12 -> 15, of which waited for: 6 -> 8; matrix products, arithmetic and copies ran while one was open for 3% -> 3% of each run, Pallas kernels for 0% -> 0%
where the time goes in v8:
time: 77.6 us; the launch traced here: 77.1 us
  waiting for transfers between devices  24.7 us (32%)
  starting transfers between devices  16.9 us (22%)
  other arithmetic  16.5 us (21%)
  blocking collectives  9.3 us (12%)
  matrix products  7.11 us (9%)
  local copies, waits for them, and re-layouts  2.27 us (3%)
    ppermute x8, waiting for transfers between devices, spread(): other = lax.ppermute(cur, 'cent', [(i, i ^ bit) for i in range(n_c)])  17.8 us
    all_gather x1, blocking collectives, shards_all(): every = lax.all_gather(both, ('dp', 'cent'), axis=0)  9.3 us
    ppermute x8, starting transfers between devices, spread(): other = lax.ppermute(cur, 'cent', [(i, i ^ bit) for i in range(n_c)])  6.15 us
    ppermute x3, starting transfers between devices, shards_all(): lax.ppermute(mine, 'outer', [(i, (i + sz) % n_o) for i in range(n_o)])  6.11 us
    ppermute x3, waiting for transfers between devices, shards_all(): lax.ppermute(mine, 'outer', [(i, (i + sz) % n_o) for i in range(n_o)])  5.57 us
    dot_general x1, matrix products, scores_for(): lax.dot_general(piece, cent_bf, (((1,), (1,)), ((), ())), preferred_eleme...  4.68 us
    ppermute x4, starting transfers between devices, pair_of(): lax.ppermute(piece, 'dp', [(j, (j + sy) % n_d) for j in range(n_d)])  4.63 us
    concatenate x1, other arithmetic, shards_all(): cur = jnp.concatenate(parts, axis=0)  3.85 us
  transfers between devices with their start and end apart: 15, of which 8 were waited for; matrix products, arithmetic and copies ran while one was open for 3% of the time, Pallas kernels for 0%

profile of v8, /device:TPU:0, one launch (start us, length us, event | category | flops | bytes accessed | tf_op | source)
XLA Modules:
  0.0 77.1 jit_solution(4754412846688595003)
XLA Ops:
  0.0 0.0 copy-start
  0.0 1.2 %copy-done = f32[256,1024]{1,0:T(8,128)S(1)} copy-done((f32[256,1024]{1,0:T(8,128)S(1)}, f32[256,1024]{1,0:T(8,128)}, u32[]{:S(2)}) %copy-start) | copy-done | bytes 1048600
  1.2 5.1 %collective-permute-start.11 = (bf16[64,1024]{1,0:T(8,128)(2,1)S(1)}, bf16[64,1024]{1,0:T(8,128)(2,1)S(1)}, u32[]{:S(2)}, u32[]{:S(2)}) collective-permute-start(bf16[64,1024]{1,0:T(8,128)(2,1)S(1)} %dynamic-slice_convert_fusion), channel_id=1, source_target_pairs={{0,24},{8,0},{16,8},{24,16},{1,25},{9,1},{17,9},{25,17},{2,26},{10... | collective-permute-start | bytes 393224 | tf_op jit(solution)/shard_map/ppermute | solution.py:85
  6.3 0.0 collective-permute-start.7
  6.3 1.0 %collective-permute-start.3 = (bf16[64,1024]{1,0:T(8,128)(2,1)S(1)}, bf16[64,1024]{1,0:T(8,128)(2,1)S(1)}, u32[]{:S(2)}, u32[]{:S(2)}) collective-permute-start(bf16[64,1024]{1,0:T(8,128)(2,1)S(1)} %dynamic-slice_convert_fusion), channel_id=1, source_target_pairs={{0,8},{8,16},{16,24},{24,0},{1,9},{9,17},{17,25},{25,1},{2,10},{10... | collective-permute-start | bytes 393224 | tf_op jit(solution)/shard_map/ppermute | solution.py:85
  7.4 1.5 %collective-permute-start = (bf16[64,1024]{1,0:T(8,128)(2,1)S(1)}, bf16[64,1024]{1,0:T(8,128)(2,1)S(1)}, u32[]{:S(2)}, u32[]{:S(2)}) collective-permute-start(bf16[64,1024]{1,0:T(8,128)(2,1)S(1)} %dynamic-slice_convert_fusion), channel_id=1, source_target_pairs={{0,4},{4,0},{1,5},{5,1},{2,6},{6,2},{3,7},{7,3},{8,12},{12,8},{9,1... | collective-permute-start | bytes 393224 | tf_op jit(solution)/shard_map/ppermute | solution.py:74
  8.9 1.8 %multiply_reduce_fusion = f32[512]{0:T(512)S(1)} fusion(f32[512,1024]{1,0:T(8,128)} %param.3), kind=kLoop, calls=%fused_computation.17 | loop fusion | flops 1048064 | bytes 2099200 | tf_op jit(solution)/shard_map/reduce_sum | solution.py:58
  10.7 0.0 collective-permute-done.11
  10.7 1.1 %collective-permute-start.12 = (bf16[64,1024]{1,0:T(8,128)(2,1)S(1)}, bf16[64,1024]{1,0:T(8,128)(2,1)S(1)}, u32[]{:S(2)}, u32[]{:S(2)}) collective-permute-start(bf16[64,1024]{1,0:T(8,128)(2,1)S(1)} %collective-permute-done.11), channel_id=1, source_target_pairs={{0,4},{4,0},{1,5},{5,1},{2,6},{6,2},{3,7},{7,3},{8,12},{12,8},{9,1... | collective-permute-start | bytes 393224 | tf_op jit(solution)/shard_map/ppermute | solution.py:74
  11.9 0.1 stack.112
  12.0 5.6 %collective-permute-done.7 = bf16[64,1024]{1,0:T(8,128)(2,1)S(1)} collective-permute-done((bf16[64,1024]{1,0:T(8,128)(2,1)S(1)}, bf16[64,1024]{1,0:T(8,128)(2,1)S(1)}, u32[]{:S(2)}, u32[]{:S(2)}) %collective-permute-start.7) | collective-permute-done | bytes 131104 | tf_op jit(solution)/shard_map/ppermute | solution.py:85
  17.6 1.5 %collective-permute-start.8 = (bf16[64,1024]{1,0:T(8,128)(2,1)S(1)}, bf16[64,1024]{1,0:T(8,128)(2,1)S(1)}, u32[]{:S(2)}, u32[]{:S(2)}) collective-permute-start(bf16[64,1024]{1,0:T(8,128)(2,1)S(1)} %collective-permute-done.7), channel_id=1, source_target_pairs={{0,4},{4,0},{1,5},{5,1},{2,6},{6,2},{3,7},{7,3},{8,12},{12,8},{9,1... | collective-permute-start | bytes 393224 | tf_op jit(solution)/shard_map/ppermute | solution.py:74
  19.1 0.0 collective-permute-done
  19.1 0.0 copy-start.5
  19.1 1.6 %collective-permute-start.1 = (bf16[2,64,1024]{2,1,0:T(8,128)(2,1)S(1)}, bf16[2,64,1024]{2,1,0:T(8,128)(2,1)S(1)}, u32[]{:S(2)}, u32[]{:S(2)}) collective-permute-start(bf16[2,64,1024]{2,1,0:T(8,128)(2,1)S(1)} %pad_maximum_fusion.4), channel_id=1, source_target_pairs={{0,2},{1,3},{2,0},{3,1},{4,6},{5,7},{6,4},{7,5},{8,10},{9,11},{10,... | collective-permute-start | bytes 786440 | tf_op jit(solution)/shard_map/ppermute | solution.py:79
  20.7 0.0 collective-permute-done.3
  20.7 0.0 copy-start.4
  20.7 0.5 collective-permute-start.4
  21.2 0.0 collective-permute-done.12
  21.2 0.0 copy-start.6
  21.2 0.6 collective-permute-start.13
  21.8 1.2 %collective-permute-done.8 = bf16[64,1024]{1,0:T(8,128)(2,1)S(1)} collective-permute-done((bf16[64,1024]{1,0:T(8,128)(2,1)S(1)}, bf16[64,1024]{1,0:T(8,128)(2,1)S(1)}, u32[]{:S(2)}, u32[]{:S(2)}) %collective-permute-start.8) | collective-permute-done | bytes 131104 | tf_op jit(solution)/shard_map/ppermute | solution.py:74
  23.0 2.5 %collective-permute-start.9 = (bf16[2,64,1024]{2,1,0:T(8,128)(2,1)S(1)}, bf16[2,64,1024]{2,1,0:T(8,128)(2,1)S(1)}, u32[]{:S(2)}, u32[]{:S(2)}) collective-permute-start(bf16[2,64,1024]{2,1,0:T(8,128)(2,1)S(1)} %pad_maximum_fusion.6), channel_id=1, source_target_pairs={{0,2},{1,3},{2,0},{3,1},{4,6},{5,7},{6,4},{7,5},{8,10},{9,11},{10,... | collective-permute-start | bytes 786440 | tf_op jit(solution)/shard_map/ppermute | solution.py:79
  25.5 0.1 collective-permute-done.4
  25.7 1.2 %collective-permute-start.5 = (bf16[2,64,1024]{2,1,0:T(8,128)(2,1)S(1)}, bf16[2,64,1024]{2,1,0:T(8,128)(2,1)S(1)}, u32[]{:S(2)}, u32[]{:S(2)}) collective-permute-start(bf16[2,64,1024]{2,1,0:T(8,128)(2,1)S(1)} %pad_maximum_fusion.5), channel_id=1, source_target_pairs={{0,2},{1,3},{2,0},{3,1},{4,6},{5,7},{6,4},{7,5},{8,10},{9,11},{10,... | collective-permute-start | bytes 786440 | tf_op jit(solution)/shard_map/ppermute | solution.py:79
  26.9 1.5 %collective-permute-done.1 = bf16[2,64,1024]{2,1,0:T(8,128)(2,1)S(1)} collective-permute-done((bf16[2,64,1024]{2,1,0:T(8,128)(2,1)S(1)}, bf16[2,64,1024]{2,1,0:T(8,128)(2,1)S(1)}, u32[]{:S(2)}, u32[]{:S(2)}) %collective-permute-start.1) | collective-permute-done | bytes 262176 | tf_op jit(solution)/shard_map/ppermute | solution.py:79
  28.5 0.1 collective-permute-start.2
  28.5 5.5 %collective-permute-done.13 = bf16[2,64,1024]{2,1,0:T(8,128)(2,1)S(1)} collective-permute-done((bf16[2,64,1024]{2,1,0:T(8,128)(2,1)S(1)}, bf16[2,64,1024]{2,1,0:T(8,128)(2,1)S(1)}, u32[]{:S(2)}, u32[]{:S(2)}) %collective-permute-start.13) | collective-permute-done | bytes 262176 | tf_op jit(solution)/shard_map/ppermute | solution.py:79
  34.1 0.1 collective-permute-start.14
  34.1 5.5 %collective-permute-done.9 = bf16[2,64,1024]{2,1,0:T(8,128)(2,1)S(1)} collective-permute-done((bf16[2,64,1024]{2,1,0:T(8,128)(2,1)S(1)}, bf16[2,64,1024]{2,1,0:T(8,128)(2,1)S(1)}, u32[]{:S(2)}, u32[]{:S(2)}) %collective-permute-start.9) | collective-permute-done | bytes 262176 | tf_op jit(solution)/shard_map/ppermute | solution.py:79
  39.7 0.1 collective-permute-start.10
  39.8 3.5 %collective-permute-done.5 = bf16[2,64,1024]{2,1,0:T(8,128)(2,1)S(1)} collective-permute-done((bf16[2,64,1024]{2,1,0:T(8,128)(2,1)S(1)}, bf16[2,64,1024]{2,1,0:T(8,128)(2,1)S(1)}, u32[]{:S(2)}, u32[]{:S(2)}) %collective-permute-start.5) | collective-permute-done | bytes 262176 | tf_op jit(solution)/shard_map/ppermute | solution.py:79
  43.3 0.1 collective-permute-start.6
  43.4 0.1 pad_add_fusion
  43.5 0.0 copy-done.5
  43.5 0.0 copy-done.4
  43.5 0.0 copy-done.6
  43.6 0.0 copy-start.3
  43.6 0.0 collective-permute-done.2
  43.6 0.0 collective-permute-done.14
  43.6 0.0 collective-permute-done.10
  43.6 1.7 %collective-permute-done.6 = bf16[2,128,1024]{2,1,0:T(8,128)(2,1)S(1)} collective-permute-done((bf16[2,128,1024]{2,1,0:T(8,128)(2,1)S(1)}, bf16[2,128,1024]{2,1,0:T(8,128)(2,1)S(1)}, u32[]{:S(2)}, u32[]{:S(2)}) %collective-permute-start.6) | collective-permute-done | bytes 524320 | tf_op jit(solution)/shard_map/ppermute | solution.py:79
  45.3 3.9 %maximum_maximum_fusion = bf16[8,256,1024]{2,1,0:T(8,128)(2,1)S(1)} fusion(bf16[2,128,1024]{2,1,0:T(8,128)(2,1)S(1)} %collective-permute-done.14, bf16[2,64,1024]{2,1,0:T(8,128)(2,1)S(1)} %collective-permute-done.13, bf16[1,64,1024]{2,1,0:T(8,128)(2,1)} %bitcast.101, bf16[1,64,1024]{2,1,0:T(8,128)(2,1)S(1)} %bitcast.89, ...), kind=kLoop, calls=%fused_computation | loop fusion | flops 67108864 | bytes 8388608 | tf_op jit(solution)/shard_map/concatenate | solution.py:87
  49.2 0.0 copy-start.1
  49.2 0.0 copy-done.3
  49.2 4.7 %fusion.12 = (f32[2048]{0:T(1024)S(1)}, f32[2048,512]{1,0:T(8,128)}) fusion(f32[512]{0:T(512)S(1)} %multiply_reduce_fusion, bf16[2048,1024]{1,0:T(8,128)(2,1)S(1)} %bitcast.82, f32[512,1024]{1,0:T(8,128)S(1)} %copy-done.3), kind=kOutput, calls=%fused_computation.62 | convolution fusion | flops 2152200192 | bytes 10496000 | tf_op jit(solution)/shard_map/dot_general | solution.py:10
  53.9 0.0 copy-done.1
  53.9 0.1 broadcast_in_dim.143
  54.0 3.3 %exponential_reduce_fusion = f32[2048]{0:T(1024)S(1)} fusion(f32[2048,512]{1,0:T(8,128)} %get-tuple-element.20, f32[2048]{0:T(1024)S(1)} %get-tuple-element.19), kind=kLoop, calls=%fused_computation.3 | loop fusion | flops 2095104 | bytes 4210688 | tf_op jit(solution)/shard_map/reduce_sum | solution.py:18
  57.3 0.1 broadcast_in_dim.148
  57.4 0.1 select_reduce_fusion.7
  57.5 0.2 select_reduce_fusion.3
  57.7 9.3 %all-gather = f32[16,8,4,64]{3,1,2,0:T(8,128)S(1)} all-gather(f32[2,8,4,64]{3,1,2,0:T(8,128)S(1)} %copy.31), channel_id=2, replica_groups=mesh['outer'=4,'dp'=2,'cent'=4] {'dp','cent'}, dimensions={0}, use_global_device_ids=true | all-gather | bytes 147456 | tf_op jit(solution)/shard_map/all_gather | solution.py:109
  67.1 0.1 select_reduce_fusion.1
  67.2 0.1 select_reduce_fusion.5
  67.3 0.1 div.48
  67.4 0.1 sub.75
  67.4 0.0 copy-start.2
  67.4 2.9 %convert_reduce_fusion = (f32[4,512]{1,0:T(4,128)S(1)}, bf16[2048,512]{1,0:T(8,128)(2,1)S(1)}) fusion(f32[2048]{0:T(1024)S(1)} %div.48, f32[2048,512]{1,0:T(8,128)} %get-tuple-element.20, f32[2048]{0:T(1024)S(1)} %sub.75), kind=kLoop, calls=%fused_computation.1 | loop fusion | flops 5240832 | bytes 6316032 | tf_op jit(solution)/shard_map/reduce_sum | solution.py:121
  70.3 0.5 copy-done.2
  70.9 2.4 %fusion.13 = f32[4,512,1024]{2,1,0:T(8,128)S(1)} fusion(bf16[4,512,512]{2,1,0:T(8,128)(2,1)S(1)} %bitcast.84, bf16[4,512,1024]{2,1,0:T(8,128)(2,1)S(1)} %bitcast.83), kind=kOutput, calls=%fused_computation.63 | convolution fusion | flops 2147483648 | bytes 14680064 | tf_op jit(solution)/shard_map/dot_general | solution.py:122
  73.4 3.7 %fusion.2 = f32[512,1024]{1,0:T(8,128)} fusion(f32[512,1024]{1,0:T(8,128)S(1)} %copy-done.3, f32[4,512,1024]{2,1,0:T(8,128)S(1)} %fusion.13, f32[512]{0:T(512)S(1)} %get-tuple-element.21, f32[512]{0:T(512)S(1)} %bitcast.113, f32[512]{0:T(512)S(1)} %get-tuple-element.22, f32[512]{0:T(512)S(1)} %bitcast.111, f32[512]{0:T(512)S(1)} %get-tuple-element.23, ...), kind=kLoop, calls=%fused_computation.8 | loop fusion | flops 14680064 | bytes 12599308 | tf_op jit(solution)/shard_map/div | solution.py:136
  (26 shorter events, 0.4 us)
Async XLA Ops:
  0.0 1.2 %copy-start = (f32[256,1024]{1,0:T(8,128)S(1)}, f32[256,1024]{1,0:T(8,128)}, u32[]{:S(2)}) copy-start(f32[256,1024]{1,0:T(8,128)} %param.2) | copy-start | bytes 3145732
  1.2 9.4 %collective-permute-start.11 = (bf16[64,1024]{1,0:T(8,128)(2,1)S(1)}, bf16[64,1024]{1,0:T(8,128)(2,1)S(1)}, u32[]{:S(2)}, u32[]{:S(2)}) collective-permute-start(bf16[64,1024]{1,0:T(8,128)(2,1)S(1)} %dynamic-slice_convert_fusion), channel_id=1, source_target_pairs={{0,24},{8,0},{16,8},{24,16},{1,25},{9,1},{17,9},{25,17},{2,26},{10... | collective-permute-start | bytes 393224 | tf_op jit(solution)/shard_map/ppermute | solution.py:85
  6.3 11.2 %collective-permute-start.7 = (bf16[64,1024]{1,0:T(8,128)(2,1)S(1)}, bf16[64,1024]{1,0:T(8,128)(2,1)S(1)}, u32[]{:S(2)}, u32[]{:S(2)}) collective-permute-start(bf16[64,1024]{1,0:T(8,128)(2,1)S(1)} %dynamic-slice_convert_fusion), channel_id=1, source_target_pairs={{0,16},{8,24},{16,0},{24,8},{1,17},{9,25},{17,1},{25,9},{2,18},{10... | collective-permute-start | bytes 393224 | tf_op jit(solution)/shard_map/ppermute | solution.py:85
  6.3 14.3 %collective-permute-start.3 = (bf16[64,1024]{1,0:T(8,128)(2,1)S(1)}, bf16[64,1024]{1,0:T(8,128)(2,1)S(1)}, u32[]{:S(2)}, u32[]{:S(2)}) collective-permute-start(bf16[64,1024]{1,0:T(8,128)(2,1)S(1)} %dynamic-slice_convert_fusion), channel_id=1, source_target_pairs={{0,8},{8,16},{16,24},{24,0},{1,9},{9,17},{17,25},{25,1},{2,10},{10... | collective-permute-start | bytes 393224 | tf_op jit(solution)/shard_map/ppermute | solution.py:85
  7.4 11.7 %collective-permute-start = (bf16[64,1024]{1,0:T(8,128)(2,1)S(1)}, bf16[64,1024]{1,0:T(8,128)(2,1)S(1)}, u32[]{:S(2)}, u32[]{:S(2)}) collective-permute-start(bf16[64,1024]{1,0:T(8,128)(2,1)S(1)} %dynamic-slice_convert_fusion), channel_id=1, source_target_pairs={{0,4},{4,0},{1,5},{5,1},{2,6},{6,2},{3,7},{7,3},{8,12},{12,8},{9,1... | collective-permute-start | bytes 393224 | tf_op jit(solution)/shard_map/ppermute | solution.py:74
  10.7 10.5 %collective-permute-start.12 = (bf16[64,1024]{1,0:T(8,128)(2,1)S(1)}, bf16[64,1024]{1,0:T(8,128)(2,1)S(1)}, u32[]{:S(2)}, u32[]{:S(2)}) collective-permute-start(bf16[64,1024]{1,0:T(8,128)(2,1)S(1)} %collective-permute-done.11), channel_id=1, source_target_pairs={{0,4},{4,0},{1,5},{5,1},{2,6},{6,2},{3,7},{7,3},{8,12},{12,8},{9,1... | collective-permute-start | bytes 393224 | tf_op jit(solution)/shard_map/ppermute | solution.py:74
  17.6 5.4 %collective-permute-start.8 = (bf16[64,1024]{1,0:T(8,128)(2,1)S(1)}, bf16[64,1024]{1,0:T(8,128)(2,1)S(1)}, u32[]{:S(2)}, u32[]{:S(2)}) collective-permute-start(bf16[64,1024]{1,0:T(8,128)(2,1)S(1)} %collective-permute-done.7), channel_id=1, source_target_pairs={{0,4},{4,0},{1,5},{5,1},{2,6},{6,2},{3,7},{7,3},{8,12},{12,8},{9,1... | collective-permute-start | bytes 393224 | tf_op jit(solution)/shard_map/ppermute | solution.py:74
  19.1 24.4 %copy-start.5 = (bf16[64,1024]{1,0:T(8,128)(2,1)}, bf16[64,1024]{1,0:T(8,128)(2,1)S(1)}, u32[]{:S(2)}) copy-start(bf16[64,1024]{1,0:T(8,128)(2,1)S(1)} %collective-permute-done) | copy-start | bytes 393220
  19.1 9.3 %collective-permute-start.1 = (bf16[2,64,1024]{2,1,0:T(8,128)(2,1)S(1)}, bf16[2,64,1024]{2,1,0:T(8,128)(2,1)S(1)}, u32[]{:S(2)}, u32[]{:S(2)}) collective-permute-start(bf16[2,64,1024]{2,1,0:T(8,128)(2,1)S(1)} %pad_maximum_fusion.4), channel_id=1, source_target_pairs={{0,2},{1,3},{2,0},{3,1},{4,6},{5,7},{6,4},{7,5},{8,10},{9,11},{10,... | collective-permute-start | bytes 786440 | tf_op jit(solution)/shard_map/ppermute | solution.py:79
  20.7 22.9 %copy-start.4 = (bf16[64,1024]{1,0:T(8,128)(2,1)}, bf16[64,1024]{1,0:T(8,128)(2,1)S(1)}, u32[]{:S(2)}) copy-start(bf16[64,1024]{1,0:T(8,128)(2,1)S(1)} %collective-permute-done.3) | copy-start | bytes 393220
  20.7 5.0 %collective-permute-start.4 = (bf16[64,1024]{1,0:T(8,128)(2,1)S(1)}, bf16[64,1024]{1,0:T(8,128)(2,1)S(1)}, u32[]{:S(2)}, u32[]{:S(2)}) collective-permute-start(bf16[64,1024]{1,0:T(8,128)(2,1)S(1)} %collective-permute-done.3), channel_id=1, source_target_pairs={{0,4},{4,0},{1,5},{5,1},{2,6},{6,2},{3,7},{7,3},{8,12},{12,8},{9,1... | collective-permute-start | bytes 393224 | tf_op jit(solution)/shard_map/ppermute | solution.py:74
  21.2 22.4 %copy-start.6 = (bf16[64,1024]{1,0:T(8,128)(2,1)}, bf16[64,1024]{1,0:T(8,128)(2,1)S(1)}, u32[]{:S(2)}) copy-start(bf16[64,1024]{1,0:T(8,128)(2,1)S(1)} %collective-permute-done.12) | copy-start | bytes 393220
  21.2 12.8 %collective-permute-start.13 = (bf16[2,64,1024]{2,1,0:T(8,128)(2,1)S(1)}, bf16[2,64,1024]{2,1,0:T(8,128)(2,1)S(1)}, u32[]{:S(2)}, u32[]{:S(2)}) collective-permute-start(bf16[2,64,1024]{2,1,0:T(8,128)(2,1)S(1)} %pad_maximum_fusion.7), channel_id=1, source_target_pairs={{0,2},{1,3},{2,0},{3,1},{4,6},{5,7},{6,4},{7,5},{8,10},{9,11},{10,... | collective-permute-start | bytes 786440 | tf_op jit(solution)/shard_map/ppermute | solution.py:79
  23.0 16.6 %collective-permute-start.9 = (bf16[2,64,1024]{2,1,0:T(8,128)(2,1)S(1)}, bf16[2,64,1024]{2,1,0:T(8,128)(2,1)S(1)}, u32[]{:S(2)}, u32[]{:S(2)}) collective-permute-start(bf16[2,64,1024]{2,1,0:T(8,128)(2,1)S(1)} %pad_maximum_fusion.6), channel_id=1, source_target_pairs={{0,2},{1,3},{2,0},{3,1},{4,6},{5,7},{6,4},{7,5},{8,10},{9,11},{10,... | collective-permute-start | bytes 786440 | tf_op jit(solution)/shard_map/ppermute | solution.py:79
  25.7 17.6 %collective-permute-start.5 = (bf16[2,64,1024]{2,1,0:T(8,128)(2,1)S(1)}, bf16[2,64,1024]{2,1,0:T(8,128)(2,1)S(1)}, u32[]{:S(2)}, u32[]{:S(2)}) collective-permute-start(bf16[2,64,1024]{2,1,0:T(8,128)(2,1)S(1)} %pad_maximum_fusion.5), channel_id=1, source_target_pairs={{0,2},{1,3},{2,0},{3,1},{4,6},{5,7},{6,4},{7,5},{8,10},{9,11},{10,... | collective-permute-start | bytes 786440 | tf_op jit(solution)/shard_map/ppermute | solution.py:79
  28.5 15.1 %collective-permute-start.2 = (bf16[2,128,1024]{2,1,0:T(8,128)(2,1)S(1)}, bf16[2,128,1024]{2,1,0:T(8,128)(2,1)S(1)}, u32[]{:S(2)}, u32[]{:S(2)}) collective-permute-start(bf16[2,128,1024]{2,1,0:T(8,128)(2,1)S(1)} %pad_maximum_fusion), channel_id=1, source_target_pairs={{0,1},{1,0},{2,3},{3,2},{4,5},{5,4},{6,7},{7,6},{8,9},{9,8},{10,11... | collective-permute-start | bytes 1572872 | tf_op jit(solution)/shard_map/ppermute | solution.py:79
  34.1 9.5 %collective-permute-start.14 = (bf16[2,128,1024]{2,1,0:T(8,128)(2,1)S(1)}, bf16[2,128,1024]{2,1,0:T(8,128)(2,1)S(1)}, u32[]{:S(2)}, u32[]{:S(2)}) collective-permute-start(bf16[2,128,1024]{2,1,0:T(8,128)(2,1)S(1)} %pad_maximum_fusion.3), channel_id=1, source_target_pairs={{0,1},{1,0},{2,3},{3,2},{4,5},{5,4},{6,7},{7,6},{8,9},{9,8},{10,11... | collective-permute-start | bytes 1572872 | tf_op jit(solution)/shard_map/ppermute | solution.py:79
  39.7 3.9 %collective-permute-start.10 = (bf16[2,128,1024]{2,1,0:T(8,128)(2,1)S(1)}, bf16[2,128,1024]{2,1,0:T(8,128)(2,1)S(1)}, u32[]{:S(2)}, u32[]{:S(2)}) collective-permute-start(bf16[2,128,1024]{2,1,0:T(8,128)(2,1)S(1)} %pad_maximum_fusion.2), channel_id=1, source_target_pairs={{0,1},{1,0},{2,3},{3,2},{4,5},{5,4},{6,7},{7,6},{8,9},{9,8},{10,11... | collective-permute-start | bytes 1572872 | tf_op jit(solution)/shard_map/ppermute | solution.py:79
  43.3 2.0 %collective-permute-start.6 = (bf16[2,128,1024]{2,1,0:T(8,128)(2,1)S(1)}, bf16[2,128,1024]{2,1,0:T(8,128)(2,1)S(1)}, u32[]{:S(2)}, u32[]{:S(2)}) collective-permute-start(bf16[2,128,1024]{2,1,0:T(8,128)(2,1)S(1)} %pad_maximum_fusion.1), channel_id=1, source_target_pairs={{0,1},{1,0},{2,3},{3,2},{4,5},{5,4},{6,7},{7,6},{8,9},{9,8},{10,11... | collective-permute-start | bytes 1572872 | tf_op jit(solution)/shard_map/ppermute | solution.py:79
  43.6 5.6 %copy-start.3 = (f32[512,1024]{1,0:T(8,128)S(1)}, f32[512,1024]{1,0:T(8,128)}, u32[]{:S(2)}) copy-start(f32[512,1024]{1,0:T(8,128)} %param.3) | copy-start | bytes 6291460
  49.2 4.7 %copy-start.1 = (bf16[8,256,1024]{2,1,0:T(8,128)(2,1)}, bf16[8,256,1024]{2,1,0:T(8,128)(2,1)S(1)}, u32[]{:S(2)}) copy-start(bf16[8,256,1024]{2,1,0:T(8,128)(2,1)S(1)} %maximum_maximum_fusion) | copy-start | bytes 12582916
  67.4 3.4 %copy-start.2 = (bf16[8,256,1024]{2,1,0:T(8,128)(2,1)S(1)}, bf16[8,256,1024]{2,1,0:T(8,128)(2,1)}, u32[]{:S(2)}) copy-start(bf16[8,256,1024]{2,1,0:T(8,128)(2,1)} %copy-done.1) | copy-start | bytes 12582916

commit v9 on v6

--- a/solution.py
+++ b/solution.py
@@ -68,21 +68,24 @@
 
     mine = lax.dynamic_slice_in_dim(rows_bf, q * tq, tq, 0)
     shifts = list(itertools.product(range(n_o), range(n_d)))
-    across = [mine]
-    for sy in range(1, n_d):
-        across.append(lax.ppermute(mine, "dp", [(j, (j + sy) % n_d) for j in range(n_d)]))
-    pair = jnp.stack(across)
-
     def spread(cur):
         for bit in reversed(bits):
             other = lax.ppermute(cur, "cent", [(i, i ^ bit) for i in range(n_c)])
             cur = jnp.concatenate([cur, other], axis=1)
         return cur
 
-    parts = [spread(pair)]
-    for sz in range(1, n_o):
-        moved = lax.ppermute(pair, "outer", [(i, (i + sz) % n_o) for i in range(n_o)])
-        parts.append(spread(moved))
+    parts = []
+    for sz in range(n_o):
+        group = []
+        for sy in range(n_d):
+            if (sz, sy) == (0, 0):
+                group.append(mine)
+                continue
+            perm = []
+            for i, j in itertools.product(range(n_o), range(n_d)):
+                perm.append((i * n_d + j, ((i + sz) % n_o) * n_d + (j + sy) % n_d))
+            group.append(lax.ppermute(mine, ("outer", "dp"), perm))
+        parts.append(spread(jnp.stack(group)))
     cur = jnp.concatenate(parts, axis=0)
     everything = cur.reshape(n_od * n_c * tq, d)
 

time: 78.1 us -> 85.2 us (1.091)
  starting transfers between devices: 13.7 us -> 18 us
  waiting for transfers between devices: 29.7 us -> 31.1 us
  other arithmetic: 15.2 us -> 16.5 us
    ppermute x8, waiting for transfers between devices: 8.75 us -> 18.9 us  [spread(): other = lax.ppermute(cur, 'cent', [(i, i ^ bit) for i in range(n_c)])]
    ppermute x4 -> x7, waiting for transfers between devices: 20.9 us -> 12.3 us  [shards_all(): group.append(lax.ppermute(mine, ('outer', 'dp'), perm))]
    ppermute x4 -> x7, starting transfers between devices: 7.92 us -> 12.5 us  [shards_all(): group.append(lax.ppermute(mine, ('outer', 'dp'), perm))]
    concatenate x1, other arithmetic: 2.62 us -> 3.85 us  [shards_all(): cur = jnp.concatenate(parts, axis=0)]
    unnamed x20 -> x14, local copies, waits for them, and re-layouts: 1.81 us -> 1.8 us
  transfers between devices with their start and end apart: 12 -> 15, of which waited for: 6 -> 7; matrix products, arithmetic and copies ran while one was open for 3% -> 3% of each run, Pallas kernels for 0% -> 0%
where the time goes in v9:
time: 85.2 us; the launch traced here: 84.7 us
  waiting for transfers between devices  31.1 us (37%)
  starting transfers between devices  18 us (21%)
  other arithmetic  16.5 us (19%)
  blocking collectives  9.29 us (11%)
  matrix products  7.12 us (8%)
  local copies, waits for them, and re-layouts  2.27 us (3%)
    ppermute x8, waiting for transfers between devices, spread(): other = lax.ppermute(cur, 'cent', [(i, i ^ bit) for i in range(n_c)])  18.9 us
    ppermute x7, starting transfers between devices, shards_all(): group.append(lax.ppermute(mine, ('outer', 'dp'), perm))  12.5 us
    ppermute x7, waiting for transfers between devices, shards_all(): group.append(lax.ppermute(mine, ('outer', 'dp'), perm))  12.3 us
    all_gather x1, blocking collectives, shards_all(): every = lax.all_gather(both, ('dp', 'cent'), axis=0)  9.29 us
    ppermute x8, starting transfers between devices, spread(): other = lax.ppermute(cur, 'cent', [(i, i ^ bit) for i in range(n_c)])  5.49 us
    dot_general x1, matrix products, scores_for(): lax.dot_general(piece, cent_bf, (((1,), (1,)), ((), ())), preferred_eleme...  4.69 us
    concatenate x1, other arithmetic, shards_all(): cur = jnp.concatenate(parts, axis=0)  3.85 us
    div x1, other arithmetic, shards_all(): return total / n_o  3.72 us
  transfers between devices with their start and end apart: 15, of which 7 were waited for; matrix products, arithmetic and copies ran while one was open for 3% of the time, Pallas kernels for 0%

profile of v9, /device:TPU:0, one launch (start us, length us, event | category | flops | bytes accessed | tf_op | source)
XLA Modules:
  0.0 84.7 jit_solution(12461128676680890940)
XLA Ops:
  0.0 0.0 copy-start
  0.0 1.2 %copy-done = f32[256,1024]{1,0:T(8,128)S(1)} copy-done((f32[256,1024]{1,0:T(8,128)S(1)}, f32[256,1024]{1,0:T(8,128)}, u32[]{:S(2)}) %copy-start) | copy-done | bytes 1048600
  1.2 6.1 %collective-permute-start.12 = (bf16[64,1024]{1,0:T(8,128)(2,1)S(1)}, bf16[64,1024]{1,0:T(8,128)(2,1)S(1)}, u32[]{:S(2)}, u32[]{:S(2)}) collective-permute-start(bf16[64,1024]{1,0:T(8,128)(2,1)S(1)} %dynamic-slice_convert_fusion), channel_id=1, source_target_pairs={{0,28},{4,24},{8,4},{12,0},{16,12},{20,8},{24,20},{28,16},{1,29},{... | collective-permute-start | bytes 393224 | tf_op jit(solution)/shard_map/ppermute | solution.py:87
  7.3 0.4 collective-permute-start.11
  7.8 0.0 collective-permute-start.8
  7.8 2.9 %collective-permute-start.7 = (bf16[64,1024]{1,0:T(8,128)(2,1)S(1)}, bf16[64,1024]{1,0:T(8,128)(2,1)S(1)}, u32[]{:S(2)}, u32[]{:S(2)}) collective-permute-start(bf16[64,1024]{1,0:T(8,128)(2,1)S(1)} %dynamic-slice_convert_fusion), channel_id=1, source_target_pairs={{0,16},{4,20},{8,24},{12,28},{16,0},{20,4},{24,8},{28,12},{1,17},{... | collective-permute-start | bytes 393224 | tf_op jit(solution)/shard_map/ppermute | solution.py:87
  10.6 2.5 %collective-permute-start.4 = (bf16[64,1024]{1,0:T(8,128)(2,1)S(1)}, bf16[64,1024]{1,0:T(8,128)(2,1)S(1)}, u32[]{:S(2)}, u32[]{:S(2)}) collective-permute-start(bf16[64,1024]{1,0:T(8,128)(2,1)S(1)} %dynamic-slice_convert_fusion), channel_id=1, source_target_pairs={{0,12},{4,8},{8,20},{12,16},{16,28},{20,24},{24,4},{28,0},{1,13},{... | collective-permute-start | bytes 393224 | tf_op jit(solution)/shard_map/ppermute | solution.py:87
  13.2 1.8 %multiply_reduce_fusion = f32[512]{0:T(512)S(1)} fusion(f32[512,1024]{1,0:T(8,128)} %param.3), kind=kLoop, calls=%fused_computation.17 | loop fusion | flops 1048064 | bytes 2099200 | tf_op jit(solution)/shard_map/reduce_sum | solution.py:58
  15.1 0.1 stack.112
  15.2 0.0 collective-permute-done.12
  15.2 0.1 collective-permute-start.3
  15.2 0.0 collective-permute-done.11
  15.3 0.6 collective-permute-start
  15.9 12.0 %collective-permute-done.8 = bf16[64,1024]{1,0:T(8,128)(2,1)S(1)} collective-permute-done((bf16[64,1024]{1,0:T(8,128)(2,1)S(1)}, bf16[64,1024]{1,0:T(8,128)(2,1)S(1)}, u32[]{:S(2)}, u32[]{:S(2)}) %collective-permute-start.8) | collective-permute-done | bytes 131104 | tf_op jit(solution)/shard_map/ppermute | solution.py:87
  27.9 0.0 copy-start.4
  27.9 1.5 %collective-permute-start.13 = (bf16[2,64,1024]{2,1,0:T(8,128)(2,1)S(1)}, bf16[2,64,1024]{2,1,0:T(8,128)(2,1)S(1)}, u32[]{:S(2)}, u32[]{:S(2)}) collective-permute-start(bf16[2,64,1024]{2,1,0:T(8,128)(2,1)S(1)} %pad_maximum_fusion.7), channel_id=1, source_target_pairs={{0,2},{1,3},{2,0},{3,1},{4,6},{5,7},{6,4},{7,5},{8,10},{9,11},{10,... | collective-permute-start | bytes 786440 | tf_op jit(solution)/shard_map/ppermute | solution.py:73
  29.4 0.2 collective-permute-done.7
  29.6 0.0 copy-start.5
  29.6 1.6 %collective-permute-start.9 = (bf16[2,64,1024]{2,1,0:T(8,128)(2,1)S(1)}, bf16[2,64,1024]{2,1,0:T(8,128)(2,1)S(1)}, u32[]{:S(2)}, u32[]{:S(2)}) collective-permute-start(bf16[2,64,1024]{2,1,0:T(8,128)(2,1)S(1)} %pad_maximum_fusion.6), channel_id=1, source_target_pairs={{0,2},{1,3},{2,0},{3,1},{4,6},{5,7},{6,4},{7,5},{8,10},{9,11},{10,... | collective-permute-start | bytes 786440 | tf_op jit(solution)/shard_map/ppermute | solution.py:73
  31.2 0.0 collective-permute-done.4
  31.2 0.0 copy-start.6
  31.2 0.0 collective-permute-done.3
  31.2 0.6 collective-permute-start.5
  31.8 0.0 collective-permute-done
  31.9 1.6 %collective-permute-start.1 = (bf16[2,64,1024]{2,1,0:T(8,128)(2,1)S(1)}, bf16[2,64,1024]{2,1,0:T(8,128)(2,1)S(1)}, u32[]{:S(2)}, u32[]{:S(2)}) collective-permute-start(bf16[2,64,1024]{2,1,0:T(8,128)(2,1)S(1)} %pad_maximum_fusion.4), channel_id=1, source_target_pairs={{0,2},{1,3},{2,0},{3,1},{4,6},{5,7},{6,4},{7,5},{8,10},{9,11},{10,... | collective-permute-start | bytes 786440 | tf_op jit(solution)/shard_map/ppermute | solution.py:73
  33.4 3.6 %collective-permute-done.13 = bf16[2,64,1024]{2,1,0:T(8,128)(2,1)S(1)} collective-permute-done((bf16[2,64,1024]{2,1,0:T(8,128)(2,1)S(1)}, bf16[2,64,1024]{2,1,0:T(8,128)(2,1)S(1)}, u32[]{:S(2)}, u32[]{:S(2)}) %collective-permute-start.13) | collective-permute-done | bytes 262176 | tf_op jit(solution)/shard_map/ppermute | solution.py:73
  37.1 0.1 collective-permute-start.14
  37.2 5.5 %collective-permute-done.9 = bf16[2,64,1024]{2,1,0:T(8,128)(2,1)S(1)} collective-permute-done((bf16[2,64,1024]{2,1,0:T(8,128)(2,1)S(1)}, bf16[2,64,1024]{2,1,0:T(8,128)(2,1)S(1)}, u32[]{:S(2)}, u32[]{:S(2)}) %collective-permute-start.9) | collective-permute-done | bytes 262176 | tf_op jit(solution)/shard_map/ppermute | solution.py:73
  42.7 0.1 collective-permute-start.10
  42.8 5.3 %collective-permute-done.5 = bf16[2,64,1024]{2,1,0:T(8,128)(2,1)S(1)} collective-permute-done((bf16[2,64,1024]{2,1,0:T(8,128)(2,1)S(1)}, bf16[2,64,1024]{2,1,0:T(8,128)(2,1)S(1)}, u32[]{:S(2)}, u32[]{:S(2)}) %collective-permute-start.5) | collective-permute-done | bytes 262176 | tf_op jit(solution)/shard_map/ppermute | solution.py:73
  48.2 0.1 collective-permute-start.6
  48.2 2.7 %collective-permute-done.1 = bf16[2,64,1024]{2,1,0:T(8,128)(2,1)S(1)} collective-permute-done((bf16[2,64,1024]{2,1,0:T(8,128)(2,1)S(1)}, bf16[2,64,1024]{2,1,0:T(8,128)(2,1)S(1)}, u32[]{:S(2)}, u32[]{:S(2)}) %collective-permute-start.1) | collective-permute-done | bytes 262176 | tf_op jit(solution)/shard_map/ppermute | solution.py:73
  51.0 0.1 collective-permute-start.2
  51.0 0.1 pad_add_fusion
  51.1 0.0 copy-done.4
  51.1 0.0 copy-done.5
  51.1 0.0 copy-done.6
  51.2 0.0 copy-start.3
  51.2 0.0 collective-permute-done.14
  51.2 0.0 collective-permute-done.10
  51.2 0.0 collective-permute-done.6
  51.2 1.7 %collective-permute-done.2 = bf16[2,128,1024]{2,1,0:T(8,128)(2,1)S(1)} collective-permute-done((bf16[2,128,1024]{2,1,0:T(8,128)(2,1)S(1)}, bf16[2,128,1024]{2,1,0:T(8,128)(2,1)S(1)}, u32[]{:S(2)}, u32[]{:S(2)}) %collective-permute-start.2) | collective-permute-done | bytes 524320 | tf_op jit(solution)/shard_map/ppermute | solution.py:73
  52.9 3.9 %maximum_maximum_fusion = bf16[8,256,1024]{2,1,0:T(8,128)(2,1)S(1)} fusion(bf16[2,128,1024]{2,1,0:T(8,128)(2,1)S(1)} %collective-permute-done.14, bf16[2,64,1024]{2,1,0:T(8,128)(2,1)S(1)} %collective-permute-done.13, bf16[1,64,1024]{2,1,0:T(8,128)(2,1)S(1)} %bitcast.89, bf16[1,64,1024]{2,1,0:T(8,128)(2,1)S(1)} %bitcast.92, ...), kind=kLoop, calls=%fused_computation | loop fusion | flops 67108864 | bytes 8388608 | tf_op jit(solution)/shard_map/concatenate | solution.py:89
  56.8 0.0 copy-start.1
  56.8 0.0 copy-done.3
  56.8 4.7 %fusion.12 = (f32[2048]{0:T(1024)S(1)}, f32[2048,512]{1,0:T(8,128)}) fusion(f32[512]{0:T(512)S(1)} %multiply_reduce_fusion, bf16[2048,1024]{1,0:T(8,128)(2,1)S(1)} %bitcast.82, f32[512,1024]{1,0:T(8,128)S(1)} %copy-done.3), kind=kOutput, calls=%fused_computation.62 | convolution fusion | flops 2152200192 | bytes 10496000 | tf_op jit(solution)/shard_map/dot_general | solution.py:10
  61.5 0.0 copy-done.1
  61.5 0.1 broadcast_in_dim.143
  61.6 3.3 %exponential_reduce_fusion = f32[2048]{0:T(1024)S(1)} fusion(f32[2048,512]{1,0:T(8,128)} %get-tuple-element.20, f32[2048]{0:T(1024)S(1)} %get-tuple-element.19), kind=kLoop, calls=%fused_computation.3 | loop fusion | flops 2095104 | bytes 4210688 | tf_op jit(solution)/shard_map/reduce_sum | solution.py:18
  64.9 0.1 broadcast_in_dim.148
  65.0 0.1 select_reduce_fusion.7
  65.1 0.2 select_reduce_fusion.3
  65.3 9.3 %all-gather = f32[16,8,4,64]{3,1,2,0:T(8,128)S(1)} all-gather(f32[2,8,4,64]{3,1,2,0:T(8,128)S(1)} %copy.31), channel_id=2, replica_groups=mesh['outer'=4,'dp'=2,'cent'=4] {'dp','cent'}, dimensions={0}, use_global_device_ids=true | all-gather | bytes 147456 | tf_op jit(solution)/shard_map/all_gather | solution.py:111
  74.7 0.1 select_reduce_fusion.1
  74.8 0.1 select_reduce_fusion.5
  74.9 0.1 div.48
  75.0 0.1 sub.75
  75.1 0.0 copy-start.2
  75.1 2.9 %convert_reduce_fusion = (f32[4,512]{1,0:T(4,128)S(1)}, bf16[2048,512]{1,0:T(8,128)(2,1)S(1)}) fusion(f32[2048]{0:T(1024)S(1)} %div.48, f32[2048,512]{1,0:T(8,128)} %get-tuple-element.20, f32[2048]{0:T(1024)S(1)} %sub.75), kind=kLoop, calls=%fused_computation.1 | loop fusion | flops 5240832 | bytes 6316032 | tf_op jit(solution)/shard_map/reduce_sum | solution.py:123
  78.0 0.5 copy-done.2
  78.5 2.4 %fusion.13 = f32[4,512,1024]{2,1,0:T(8,128)S(1)} fusion(bf16[4,512,512]{2,1,0:T(8,128)(2,1)S(1)} %bitcast.84, bf16[4,512,1024]{2,1,0:T(8,128)(2,1)S(1)} %bitcast.83), kind=kOutput, calls=%fused_computation.63 | convolution fusion | flops 2147483648 | bytes 14680064 | tf_op jit(solution)/shard_map/dot_general | solution.py:124
  81.0 3.7 %fusion.2 = f32[512,1024]{1,0:T(8,128)} fusion(f32[512,1024]{1,0:T(8,128)S(1)} %copy-done.3, f32[4,512,1024]{2,1,0:T(8,128)S(1)} %fusion.13, f32[512]{0:T(512)S(1)} %get-tuple-element.21, f32[512]{0:T(512)S(1)} %bitcast.113, f32[512]{0:T(512)S(1)} %get-tuple-element.22, f32[512]{0:T(512)S(1)} %bitcast.111, f32[512]{0:T(512)S(1)} %get-tuple-element.23, ...), kind=kLoop, calls=%fused_computation.8 | loop fusion | flops 14680064 | bytes 12599308 | tf_op jit(solution)/shard_map/div | solution.py:138
  (26 shorter events, 0.4 us)
Async XLA Ops:
  0.0 1.2 %copy-start = (f32[256,1024]{1,0:T(8,128)S(1)}, f32[256,1024]{1,0:T(8,128)}, u32[]{:S(2)}) copy-start(f32[256,1024]{1,0:T(8,128)} %param.2) | copy-start | bytes 3145732
  1.2 13.9 %collective-permute-start.12 = (bf16[64,1024]{1,0:T(8,128)(2,1)S(1)}, bf16[64,1024]{1,0:T(8,128)(2,1)S(1)}, u32[]{:S(2)}, u32[]{:S(2)}) collective-permute-start(bf16[64,1024]{1,0:T(8,128)(2,1)S(1)} %dynamic-slice_convert_fusion), channel_id=1, source_target_pairs={{0,28},{4,24},{8,4},{12,0},{16,12},{20,8},{24,20},{28,16},{1,29},{... | collective-permute-start | bytes 393224 | tf_op jit(solution)/shard_map/ppermute | solution.py:87
  7.3 7.9 %collective-permute-start.11 = (bf16[64,1024]{1,0:T(8,128)(2,1)S(1)}, bf16[64,1024]{1,0:T(8,128)(2,1)S(1)}, u32[]{:S(2)}, u32[]{:S(2)}) collective-permute-start(bf16[64,1024]{1,0:T(8,128)(2,1)S(1)} %dynamic-slice_convert_fusion), channel_id=1, source_target_pairs={{0,24},{4,28},{8,0},{12,4},{16,8},{20,12},{24,16},{28,20},{1,25},{... | collective-permute-start | bytes 393224 | tf_op jit(solution)/shard_map/ppermute | solution.py:87
  7.8 20.1 %collective-permute-start.8 = (bf16[64,1024]{1,0:T(8,128)(2,1)S(1)}, bf16[64,1024]{1,0:T(8,128)(2,1)S(1)}, u32[]{:S(2)}, u32[]{:S(2)}) collective-permute-start(bf16[64,1024]{1,0:T(8,128)(2,1)S(1)} %dynamic-slice_convert_fusion), channel_id=1, source_target_pairs={{0,20},{4,16},{8,28},{12,24},{16,4},{20,0},{24,12},{28,8},{1,21},{... | collective-permute-start | bytes 393224 | tf_op jit(solution)/shard_map/ppermute | solution.py:87
  7.8 21.9 %collective-permute-start.7 = (bf16[64,1024]{1,0:T(8,128)(2,1)S(1)}, bf16[64,1024]{1,0:T(8,128)(2,1)S(1)}, u32[]{:S(2)}, u32[]{:S(2)}) collective-permute-start(bf16[64,1024]{1,0:T(8,128)(2,1)S(1)} %dynamic-slice_convert_fusion), channel_id=1, source_target_pairs={{0,16},{4,20},{8,24},{12,28},{16,0},{20,4},{24,8},{28,12},{1,17},{... | collective-permute-start | bytes 393224 | tf_op jit(solution)/shard_map/ppermute | solution.py:87
  10.6 20.6 %collective-permute-start.4 = (bf16[64,1024]{1,0:T(8,128)(2,1)S(1)}, bf16[64,1024]{1,0:T(8,128)(2,1)S(1)}, u32[]{:S(2)}, u32[]{:S(2)}) collective-permute-start(bf16[64,1024]{1,0:T(8,128)(2,1)S(1)} %dynamic-slice_convert_fusion), channel_id=1, source_target_pairs={{0,12},{4,8},{8,20},{12,16},{16,28},{20,24},{24,4},{28,0},{1,13},{... | collective-permute-start | bytes 393224 | tf_op jit(solution)/shard_map/ppermute | solution.py:87
  15.2 16.0 %collective-permute-start.3 = (bf16[64,1024]{1,0:T(8,128)(2,1)S(1)}, bf16[64,1024]{1,0:T(8,128)(2,1)S(1)}, u32[]{:S(2)}, u32[]{:S(2)}) collective-permute-start(bf16[64,1024]{1,0:T(8,128)(2,1)S(1)} %dynamic-slice_convert_fusion), channel_id=1, source_target_pairs={{0,8},{4,12},{8,16},{12,20},{16,24},{20,28},{24,0},{28,4},{1,9},{5... | collective-permute-start | bytes 393224 | tf_op jit(solution)/shard_map/ppermute | solution.py:87
  15.3 16.6 %collective-permute-start = (bf16[64,1024]{1,0:T(8,128)(2,1)S(1)}, bf16[64,1024]{1,0:T(8,128)(2,1)S(1)}, u32[]{:S(2)}, u32[]{:S(2)}) collective-permute-start(bf16[64,1024]{1,0:T(8,128)(2,1)S(1)} %dynamic-slice_convert_fusion), channel_id=1, source_target_pairs={{0,4},{4,0},{8,12},{12,8},{16,20},{20,16},{24,28},{28,24},{1,5},{5... | collective-permute-start | bytes 393224 | tf_op jit(solution)/shard_map/ppermute | solution.py:87
  27.9 23.2 %copy-start.4 = (bf16[64,1024]{1,0:T(8,128)(2,1)}, bf16[64,1024]{1,0:T(8,128)(2,1)S(1)}, u32[]{:S(2)}) copy-start(bf16[64,1024]{1,0:T(8,128)(2,1)S(1)} %collective-permute-done.8) | copy-start | bytes 393220
  27.9 9.2 %collective-permute-start.13 = (bf16[2,64,1024]{2,1,0:T(8,128)(2,1)S(1)}, bf16[2,64,1024]{2,1,0:T(8,128)(2,1)S(1)}, u32[]{:S(2)}, u32[]{:S(2)}) collective-permute-start(bf16[2,64,1024]{2,1,0:T(8,128)(2,1)S(1)} %pad_maximum_fusion.7), channel_id=1, source_target_pairs={{0,2},{1,3},{2,0},{3,1},{4,6},{5,7},{6,4},{7,5},{8,10},{9,11},{10,... | collective-permute-start | bytes 786440 | tf_op jit(solution)/shard_map/ppermute | solution.py:73
  29.6 21.5 %copy-start.5 = (bf16[64,1024]{1,0:T(8,128)(2,1)}, bf16[64,1024]{1,0:T(8,128)(2,1)S(1)}, u32[]{:S(2)}) copy-start(bf16[64,1024]{1,0:T(8,128)(2,1)S(1)} %collective-permute-done.7) | copy-start | bytes 393220
  29.6 13.0 %collective-permute-start.9 = (bf16[2,64,1024]{2,1,0:T(8,128)(2,1)S(1)}, bf16[2,64,1024]{2,1,0:T(8,128)(2,1)S(1)}, u32[]{:S(2)}, u32[]{:S(2)}) collective-permute-start(bf16[2,64,1024]{2,1,0:T(8,128)(2,1)S(1)} %pad_maximum_fusion.6), channel_id=1, source_target_pairs={{0,2},{1,3},{2,0},{3,1},{4,6},{5,7},{6,4},{7,5},{8,10},{9,11},{10,... | collective-permute-start | bytes 786440 | tf_op jit(solution)/shard_map/ppermute | solution.py:73
  31.2 19.9 %copy-start.6 = (bf16[64,1024]{1,0:T(8,128)(2,1)}, bf16[64,1024]{1,0:T(8,128)(2,1)S(1)}, u32[]{:S(2)}) copy-start(bf16[64,1024]{1,0:T(8,128)(2,1)S(1)} %collective-permute-done.4) | copy-start | bytes 393220
  31.2 16.9 %collective-permute-start.5 = (bf16[2,64,1024]{2,1,0:T(8,128)(2,1)S(1)}, bf16[2,64,1024]{2,1,0:T(8,128)(2,1)S(1)}, u32[]{:S(2)}, u32[]{:S(2)}) collective-permute-start(bf16[2,64,1024]{2,1,0:T(8,128)(2,1)S(1)} %pad_maximum_fusion.5), channel_id=1, source_target_pairs={{0,2},{1,3},{2,0},{3,1},{4,6},{5,7},{6,4},{7,5},{8,10},{9,11},{10,... | collective-permute-start | bytes 786440 | tf_op jit(solution)/shard_map/ppermute | solution.py:73
  31.9 19.0 %collective-permute-start.1 = (bf16[2,64,1024]{2,1,0:T(8,128)(2,1)S(1)}, bf16[2,64,1024]{2,1,0:T(8,128)(2,1)S(1)}, u32[]{:S(2)}, u32[]{:S(2)}) collective-permute-start(bf16[2,64,1024]{2,1,0:T(8,128)(2,1)S(1)} %pad_maximum_fusion.4), channel_id=1, source_target_pairs={{0,2},{1,3},{2,0},{3,1},{4,6},{5,7},{6,4},{7,5},{8,10},{9,11},{10,... | collective-permute-start | bytes 786440 | tf_op jit(solution)/shard_map/ppermute | solution.py:73
  37.1 14.1 %collective-permute-start.14 = (bf16[2,128,1024]{2,1,0:T(8,128)(2,1)S(1)}, bf16[2,128,1024]{2,1,0:T(8,128)(2,1)S(1)}, u32[]{:S(2)}, u32[]{:S(2)}) collective-permute-start(bf16[2,128,1024]{2,1,0:T(8,128)(2,1)S(1)} %pad_maximum_fusion.3), channel_id=1, source_target_pairs={{0,1},{1,0},{2,3},{3,2},{4,5},{5,4},{6,7},{7,6},{8,9},{9,8},{10,11... | collective-permute-start | bytes 1572872 | tf_op jit(solution)/shard_map/ppermute | solution.py:73
  42.7 8.5 %collective-permute-start.10 = (bf16[2,128,1024]{2,1,0:T(8,128)(2,1)S(1)}, bf16[2,128,1024]{2,1,0:T(8,128)(2,1)S(1)}, u32[]{:S(2)}, u32[]{:S(2)}) collective-permute-start(bf16[2,128,1024]{2,1,0:T(8,128)(2,1)S(1)} %pad_maximum_fusion.2), channel_id=1, source_target_pairs={{0,1},{1,0},{2,3},{3,2},{4,5},{5,4},{6,7},{7,6},{8,9},{9,8},{10,11... | collective-permute-start | bytes 1572872 | tf_op jit(solution)/shard_map/ppermute | solution.py:73
  48.2 3.0 %collective-permute-start.6 = (bf16[2,128,1024]{2,1,0:T(8,128)(2,1)S(1)}, bf16[2,128,1024]{2,1,0:T(8,128)(2,1)S(1)}, u32[]{:S(2)}, u32[]{:S(2)}) collective-permute-start(bf16[2,128,1024]{2,1,0:T(8,128)(2,1)S(1)} %pad_maximum_fusion.1), channel_id=1, source_target_pairs={{0,1},{1,0},{2,3},{3,2},{4,5},{5,4},{6,7},{7,6},{8,9},{9,8},{10,11... | collective-permute-start | bytes 1572872 | tf_op jit(solution)/shard_map/ppermute | solution.py:73
  51.0 2.0 %collective-permute-start.2 = (bf16[2,128,1024]{2,1,0:T(8,128)(2,1)S(1)}, bf16[2,128,1024]{2,1,0:T(8,128)(2,1)S(1)}, u32[]{:S(2)}, u32[]{:S(2)}) collective-permute-start(bf16[2,128,1024]{2,1,0:T(8,128)(2,1)S(1)} %pad_maximum_fusion), channel_id=1, source_target_pairs={{0,1},{1,0},{2,3},{3,2},{4,5},{5,4},{6,7},{7,6},{8,9},{9,8},{10,11... | collective-permute-start | bytes 1572872 | tf_op jit(solution)/shard_map/ppermute | solution.py:73
  51.2 5.6 %copy-start.3 = (f32[512,1024]{1,0:T(8,128)S(1)}, f32[512,1024]{1,0:T(8,128)}, u32[]{:S(2)}) copy-start(f32[512,1024]{1,0:T(8,128)} %param.3) | copy-start | bytes 6291460
  56.8 4.7 %copy-start.1 = (bf16[8,256,1024]{2,1,0:T(8,128)(2,1)}, bf16[8,256,1024]{2,1,0:T(8,128)(2,1)S(1)}, u32[]{:S(2)}) copy-start(bf16[8,256,1024]{2,1,0:T(8,128)(2,1)S(1)} %maximum_maximum_fusion) | copy-start | bytes 12582916
  75.1 3.4 %copy-start.2 = (bf16[8,256,1024]{2,1,0:T(8,128)(2,1)S(1)}, bf16[8,256,1024]{2,1,0:T(8,128)(2,1)}, u32[]{:S(2)}) copy-start(bf16[8,256,1024]{2,1,0:T(8,128)(2,1)} %copy-done.1) | copy-start | bytes 12582916

commit v10 on v8

--- a/solution.py
+++ b/solution.py
@@ -84,13 +84,15 @@
     for sz in range(1, n_o):
         landed.append(lax.ppermute(mine, "outer", [(i, (i + sz) % n_o) for i in range(n_o)]))
     parts = [spread(pair_of(piece)) for piece in landed]
-    cur = jnp.concatenate(parts, axis=0)
+    cur = jnp.zeros((n_o * n_d,) + parts[0].shape[1:], parts[0].dtype)
+    for sz in range(n_o):
+        cur = lax.dynamic_update_slice_in_dim(cur, parts[sz], ((z - sz) % n_o) * n_d, axis=0)
     everything = cur.reshape(n_od * n_c * tq, d)
 
     logits = scores_for(everything, cent_bf, squares)
     local_max, local_sum = row_summary(logits)
 
-    src_vec = jnp.stack([((z - sz) % n_o) * n_d + (y - sy) % n_d for sz, sy in shifts])
+    src_vec = jnp.stack([a * n_d + (y - sy) % n_d for a, sy in shifts])
     hot_k = src_vec[None, :] == jnp.arange(n_od)[:, None]
     c_vec = jnp.stack([q ^ x for x in xs])
     hot_c = c_vec[None, :] == jnp.arange(n_c)[:, None]
@@ -116,24 +118,18 @@
     weights = (jnp.exp(logits - row_peak[:, None]) / row_mass[:, None]).astype(jnp.bfloat16)
     k = centroids.shape[0]
     pod = n_d * n_c * tq
-    w_pods = weights.reshape(n_o, pod, k)
-    r_pods = everything.reshape(n_o, pod, d)
-    weight_sum = jnp.sum(w_pods.astype(jnp.float32), axis=1)
+    w_pods = weights.reshape(n_o, pod, k).astype(jnp.float32)
+    weight_sum = jnp.sum(w_pods, axis=1)
+    scaled = (w_pods / (weight_sum[:, None, :] + 1.0)).astype(jnp.bfloat16)
     pull = lax.dot_general(
-        w_pods, r_pods, (((1,), (1,)), ((0,), (0,))), preferred_element_type=jnp.float32
+        scaled.reshape(n_o * pod, k), everything, (((0,), (0,)), ((), ())),
+        preferred_element_type=jnp.float32,
     )
-
-    total = None
+    coef = None
     for a in range(n_o):
-        rel = (z - a) % n_o
-        pick_pull = pull[0]
-        pick_ws = weight_sum[0]
-        for s in range(1, n_o):
-            pick_pull = jnp.where(rel == s, pull[s], pick_pull)
-            pick_ws = jnp.where(rel == s, weight_sum[s], pick_ws)
-        delta = (pick_pull - pick_ws[:, None] * centroids) / (pick_ws[:, None] + 1.0)
-        total = delta if total is None else total + delta
-    return total / n_o
+        term = weight_sum[a] / (weight_sum[a] + 1.0)
+        coef = term if coef is None else coef + term
+    return (pull - coef[:, None] * centroids) / n_o
 
 
 def solution(mesh):

time: 77.6 us -> 72.5 us (0.934)
  other arithmetic: 16.5 us -> 10.5 us
  local copies, waits for them, and re-layouts: 2.27 us -> 5.2 us
  waiting for transfers between devices: 24.7 us -> 22.1 us
  matrix products: 7.11 us -> 8.28 us
    ppermute x8, waiting for transfers between devices: 17.8 us -> 13.3 us  [spread(): other = lax.ppermute(cur, 'cent', [(i, i ^ bit) for i in range(n_c)])]
    concatenate x1 -> x0, other arithmetic: 3.85 us -> none  [shards_all(): cur = jnp.concatenate(parts, axis=0)]
    div x1 -> x0, other arithmetic: 3.72 us -> none  [shards_all(): return total / n_o]
    unnamed x14 -> x22, local copies, waits for them, and re-layouts: 1.8 us -> 4.2 us
    concatenate x4, other arithmetic: 0.14 us -> 2.01 us  [spread(): cur = jnp.concatenate([cur, other], axis=1)]
    reduce_sum x1, other arithmetic: 1.8 us -> 0.21 us  [shards_all(): squares = jnp.sum(centroids * centroids, axis=1)]
    dot_general x1, matrix products: 2.43 us -> 3.67 us  [shards_all(): lax.dot_general(scaled.reshape(n_o * pod, k), everything, (((0,), (0,)),...]
    convert_element_type x0 -> x1, other arithmetic: none -> 0.99 us  [shards_all(): scaled = (w_pods / (weight_sum[:, None, :] + 1.0)).astype(jnp.bfloat16)]
  transfers between devices with their start and end apart: 15 -> 15, of which waited for: 8 -> 7; matrix products, arithmetic and copies ran while one was open for 3% -> 5% of each run, Pallas kernels for 0% -> 0%
where the time goes in v10:
time: 72.5 us; the launch traced here: 72.2 us
  waiting for transfers between devices  22.1 us (30%)
  starting transfers between devices  16.4 us (23%)
  other arithmetic  10.5 us (14%)
  blocking collectives  9.37 us (13%)
  matrix products  8.28 us (11%)
  local copies, waits for them, and re-layouts  5.2 us (7%)
    ppermute x8, waiting for transfers between devices, spread(): other = lax.ppermute(cur, 'cent', [(i, i ^ bit) for i in range(n_c)])  13.3 us
    all_gather x1, blocking collectives, shards_all(): every = lax.all_gather(both, ('dp', 'cent'), axis=0)  9.37 us
    ppermute x3, waiting for transfers between devices, shards_all(): lax.ppermute(mine, 'outer', [(i, (i + sz) % n_o) for i in range(n_o)])  6.52 us
    ppermute x8, starting transfers between devices, spread(): other = lax.ppermute(cur, 'cent', [(i, i ^ bit) for i in range(n_c)])  5.6 us
    ppermute x3, starting transfers between devices, shards_all(): lax.ppermute(mine, 'outer', [(i, (i + sz) % n_o) for i in range(n_o)])  5.51 us
    ppermute x4, starting transfers between devices, pair_of(): lax.ppermute(piece, 'dp', [(j, (j + sy) % n_d) for j in range(n_d)])  5.27 us
    dot_general x1, matrix products, scores_for(): lax.dot_general(piece, cent_bf, (((1,), (1,)), ((), ())), preferred_eleme...  4.61 us
    unnamed x22, local copies, waits for them, and re-layouts  4.2 us
  transfers between devices with their start and end apart: 15, of which 7 were waited for; matrix products, arithmetic and copies ran while one was open for 5% of the time, Pallas kernels for 0%

profile of v10, /device:TPU:0, one launch (start us, length us, event | category | flops | bytes accessed | tf_op | source)
XLA Modules:
  0.0 72.2 jit_solution(16152621675768859372)
XLA Ops:
  0.0 0.0 copy-start
  0.0 1.2 %copy-done = f32[256,1024]{1,0:T(8,128)S(1)} copy-done((f32[256,1024]{1,0:T(8,128)S(1)}, f32[256,1024]{1,0:T(8,128)}, u32[]{:S(2)}) %copy-start) | copy-done | bytes 1048600
  1.2 3.0 %collective-permute-start = (bf16[64,1024]{1,0:T(8,128)(2,1)S(1)}, bf16[64,1024]{1,0:T(8,128)(2,1)S(1)}, u32[]{:S(2)}, u32[]{:S(2)}) collective-permute-start(bf16[64,1024]{1,0:T(8,128)(2,1)S(1)} %dynamic-slice_convert_fusion), channel_id=1, source_target_pairs={{0,4},{4,0},{1,5},{5,1},{2,6},{6,2},{3,7},{7,3},{8,12},{12,8},{9,1... | collective-permute-start | bytes 393224 | tf_op jit(solution)/shard_map/ppermute | solution.py:74
  4.3 1.6 %collective-permute-start.3 = (bf16[64,1024]{1,0:T(8,128)(2,1)S(1)}, bf16[64,1024]{1,0:T(8,128)(2,1)S(1)}, u32[]{:S(2)}, u32[]{:S(2)}) collective-permute-start(bf16[64,1024]{1,0:T(8,128)(2,1)S(1)} %dynamic-slice_convert_fusion), channel_id=1, source_target_pairs={{0,8},{8,16},{16,24},{24,0},{1,9},{9,17},{17,25},{25,1},{2,10},{10... | collective-permute-start | bytes 393224 | tf_op jit(solution)/shard_map/ppermute | solution.py:85
  5.9 2.6 %collective-permute-start.7 = (bf16[64,1024]{1,0:T(8,128)(2,1)S(1)}, bf16[64,1024]{1,0:T(8,128)(2,1)S(1)}, u32[]{:S(2)}, u32[]{:S(2)}) collective-permute-start(bf16[64,1024]{1,0:T(8,128)(2,1)S(1)} %dynamic-slice_convert_fusion), channel_id=1, source_target_pairs={{0,16},{8,24},{16,0},{24,8},{1,17},{9,25},{17,1},{25,9},{2,18},{10... | collective-permute-start | bytes 393224 | tf_op jit(solution)/shard_map/ppermute | solution.py:85
  8.4 1.3 %collective-permute-start.11 = (bf16[64,1024]{1,0:T(8,128)(2,1)S(1)}, bf16[64,1024]{1,0:T(8,128)(2,1)S(1)}, u32[]{:S(2)}, u32[]{:S(2)}) collective-permute-start(bf16[64,1024]{1,0:T(8,128)(2,1)S(1)} %dynamic-slice_convert_fusion), channel_id=1, source_target_pairs={{0,24},{8,0},{16,8},{24,16},{1,25},{9,1},{17,9},{25,17},{2,26},{10... | collective-permute-start | bytes 393224 | tf_op jit(solution)/shard_map/ppermute | solution.py:85
  9.8 0.1 stack.112
  9.9 0.1 pad_add_fusion
  10.0 2.6 %collective-permute-done.3 = bf16[64,1024]{1,0:T(8,128)(2,1)S(1)} collective-permute-done((bf16[64,1024]{1,0:T(8,128)(2,1)S(1)}, bf16[64,1024]{1,0:T(8,128)(2,1)S(1)}, u32[]{:S(2)}, u32[]{:S(2)}) %collective-permute-start.3) | collective-permute-done | bytes 131104 | tf_op jit(solution)/shard_map/ppermute | solution.py:85
  12.6 0.3 collective-permute-start.4
  12.9 3.9 %collective-permute-done.7 = bf16[64,1024]{1,0:T(8,128)(2,1)S(1)} collective-permute-done((bf16[64,1024]{1,0:T(8,128)(2,1)S(1)}, bf16[64,1024]{1,0:T(8,128)(2,1)S(1)}, u32[]{:S(2)}, u32[]{:S(2)}) %collective-permute-start.7) | collective-permute-done | bytes 131104 | tf_op jit(solution)/shard_map/ppermute | solution.py:85
  16.8 0.5 collective-permute-start.8
  17.3 0.0 collective-permute-done
  17.3 1.6 %collective-permute-start.1 = (bf16[2,64,1024]{2,1,0:T(8,128)(2,1)S(1)}, bf16[2,64,1024]{2,1,0:T(8,128)(2,1)S(1)}, u32[]{:S(2)}, u32[]{:S(2)}) collective-permute-start(bf16[2,64,1024]{2,1,0:T(8,128)(2,1)S(1)} %pad_maximum_fusion.4), channel_id=1, source_target_pairs={{0,2},{1,3},{2,0},{3,1},{4,6},{5,7},{6,4},{7,5},{8,10},{9,11},{10,... | collective-permute-start | bytes 786440 | tf_op jit(solution)/shard_map/ppermute | solution.py:79
  18.9 0.0 collective-permute-done.11
  18.9 1.5 %collective-permute-start.12 = (bf16[64,1024]{1,0:T(8,128)(2,1)S(1)}, bf16[64,1024]{1,0:T(8,128)(2,1)S(1)}, u32[]{:S(2)}, u32[]{:S(2)}) collective-permute-start(bf16[64,1024]{1,0:T(8,128)(2,1)S(1)} %collective-permute-done.11), channel_id=1, source_target_pairs={{0,4},{4,0},{1,5},{5,1},{2,6},{6,2},{3,7},{7,3},{8,12},{12,8},{9,1... | collective-permute-start | bytes 393224 | tf_op jit(solution)/shard_map/ppermute | solution.py:74
  20.5 0.0 collective-permute-done.4
  20.5 0.6 collective-permute-start.5
  21.1 2.1 %collective-permute-done.8 = bf16[64,1024]{1,0:T(8,128)(2,1)S(1)} collective-permute-done((bf16[64,1024]{1,0:T(8,128)(2,1)S(1)}, bf16[64,1024]{1,0:T(8,128)(2,1)S(1)}, u32[]{:S(2)}, u32[]{:S(2)}) %collective-permute-start.8) | collective-permute-done | bytes 131104 | tf_op jit(solution)/shard_map/ppermute | solution.py:74
  23.2 1.6 %collective-permute-start.9 = (bf16[2,64,1024]{2,1,0:T(8,128)(2,1)S(1)}, bf16[2,64,1024]{2,1,0:T(8,128)(2,1)S(1)}, u32[]{:S(2)}, u32[]{:S(2)}) collective-permute-start(bf16[2,64,1024]{2,1,0:T(8,128)(2,1)S(1)} %pad_maximum_fusion.6), channel_id=1, source_target_pairs={{0,2},{1,3},{2,0},{3,1},{4,6},{5,7},{6,4},{7,5},{8,10},{9,11},{10,... | collective-permute-start | bytes 786440 | tf_op jit(solution)/shard_map/ppermute | solution.py:79
  24.8 0.2 collective-permute-done.12
  25.0 0.0 copy-done.5
  25.0 0.0 copy-done.7
  25.0 0.0 copy-start.4
  25.0 1.6 %collective-permute-start.13 = (bf16[2,64,1024]{2,1,0:T(8,128)(2,1)S(1)}, bf16[2,64,1024]{2,1,0:T(8,128)(2,1)S(1)}, u32[]{:S(2)}, u32[]{:S(2)}) collective-permute-start(bf16[2,64,1024]{2,1,0:T(8,128)(2,1)S(1)} %pad_maximum_fusion.7), channel_id=1, source_target_pairs={{0,2},{1,3},{2,0},{3,1},{4,6},{5,7},{6,4},{7,5},{8,10},{9,11},{10,... | collective-permute-start | bytes 786440 | tf_op jit(solution)/shard_map/ppermute | solution.py:79
  26.6 0.0 collective-permute-done.1
  26.6 0.9 %pad_maximum_fusion = bf16[2,128,1024]{2,1,0:T(8,128)(2,1)S(1)} fusion(bf16[2,64,1024]{2,1,0:T(8,128)(2,1)S(1)} %collective-permute-done.1, bf16[1,64,1024]{2,1,0:T(8,128)(2,1)} %bitcast.69, bf16[1,64,1024]{2,1,0:T(8,128)(2,1)S(1)} %fusion.14), kind=kLoop, calls=%fused_computation.14 | loop fusion | flops 1572864 | bytes 1048576 | tf_op jit(solution)/shard_map/concatenate | solution.py:80
  27.6 0.1 collective-permute-start.2
  27.7 4.6 %collective-permute-done.5 = bf16[2,64,1024]{2,1,0:T(8,128)(2,1)S(1)} collective-permute-done((bf16[2,64,1024]{2,1,0:T(8,128)(2,1)S(1)}, bf16[2,64,1024]{2,1,0:T(8,128)(2,1)S(1)}, u32[]{:S(2)}, u32[]{:S(2)}) %collective-permute-start.5) | collective-permute-done | bytes 262176 | tf_op jit(solution)/shard_map/ppermute | solution.py:79
  32.2 1.0 %pad_maximum_fusion.1 = bf16[2,128,1024]{2,1,0:T(8,128)(2,1)S(1)} fusion(bf16[2,64,1024]{2,1,0:T(8,128)(2,1)S(1)} %collective-permute-done.5, bf16[1,64,1024]{2,1,0:T(8,128)(2,1)} %bitcast.72, bf16[1,64,1024]{2,1,0:T(8,128)(2,1)} %bitcast.66), kind=kLoop, calls=%fused_computation.15 | loop fusion | flops 1572864 | bytes 1048576 | tf_op jit(solution)/shard_map/concatenate | solution.py:80
  33.3 0.1 collective-permute-start.6
  33.3 4.5 %collective-permute-done.9 = bf16[2,64,1024]{2,1,0:T(8,128)(2,1)S(1)} collective-permute-done((bf16[2,64,1024]{2,1,0:T(8,128)(2,1)S(1)}, bf16[2,64,1024]{2,1,0:T(8,128)(2,1)S(1)}, u32[]{:S(2)}, u32[]{:S(2)}) %collective-permute-start.9) | collective-permute-done | bytes 262176 | tf_op jit(solution)/shard_map/ppermute | solution.py:79
  37.9 0.1 collective-permute-start.10
  38.0 4.1 %collective-permute-done.13 = bf16[2,64,1024]{2,1,0:T(8,128)(2,1)S(1)} collective-permute-done((bf16[2,64,1024]{2,1,0:T(8,128)(2,1)S(1)}, bf16[2,64,1024]{2,1,0:T(8,128)(2,1)S(1)}, u32[]{:S(2)}, u32[]{:S(2)}) %collective-permute-start.13) | collective-permute-done | bytes 262176 | tf_op jit(solution)/shard_map/ppermute | solution.py:79
  42.2 0.1 collective-permute-start.14
  42.3 0.2 multiply_reduce_fusion
  42.5 0.0 collective-permute-done.2
  42.5 0.5 broadcast_in_dim.138
  43.0 0.4 copy-done.8
  43.4 0.1 maximum_dynamic-update-slice_fusion
  43.5 0.0 collective-permute-done.6
  43.5 0.8 %copy-done.6 = bf16[64,1024]{1,0:T(8,128)(2,1)S(1)} copy-done((bf16[64,1024]{1,0:T(8,128)(2,1)S(1)}, bf16[64,1024]{1,0:T(8,128)(2,1)}, u32[]{:S(2)}) %copy-start.6) | copy-done | bytes 131096
  44.3 0.1 copy-done.10
  44.3 0.1 maximum_dynamic-update-slice_fusion.1
  44.4 0.0 collective-permute-done.10
  44.5 0.1 maximum_dynamic-update-slice_fusion.2
  44.6 0.0 collective-permute-done.14
  44.6 0.1 maximum_dynamic-update-slice_fusion.3
  44.7 4.6 %fusion.10 = (f32[2048]{0:T(1024)S(1)}, f32[2048,512]{1,0:T(8,128)}) fusion(f32[512]{0:T(512)S(1)} %multiply_reduce_fusion, bf16[2048,1024]{1,0:T(8,128)(2,1)S(1)} %bitcast.55, f32[512,1024]{1,0:T(8,128)S(1)} %copy-done.4), kind=kOutput, calls=%fused_computation.50 | convolution fusion | flops 2152200192 | bytes 10496000 | tf_op jit(solution)/shard_map/dot_general | solution.py:10
  49.3 0.1 broadcast_in_dim.141
  49.4 3.3 %exponential_reduce_fusion = f32[2048]{0:T(1024)S(1)} fusion(f32[2048,512]{1,0:T(8,128)} %get-tuple-element.18, f32[2048]{0:T(1024)S(1)} %get-tuple-element.17), kind=kLoop, calls=%fused_computation.4 | loop fusion | flops 2095104 | bytes 4210688 | tf_op jit(solution)/shard_map/reduce_sum | solution.py:18
  52.7 0.1 broadcast_in_dim.146
  52.8 0.1 select_reduce_fusion.7
  52.9 0.2 select_reduce_fusion.3
  53.1 9.4 %all-gather = f32[16,8,4,64]{3,1,2,0:T(8,128)S(1)} all-gather(f32[2,8,4,64]{3,1,2,0:T(8,128)S(1)} %copy.26), channel_id=2, replica_groups=mesh['outer'=4,'dp'=2,'cent'=4] {'dp','cent'}, dimensions={0}, use_global_device_ids=true | all-gather | bytes 147456 | tf_op jit(solution)/shard_map/all_gather | solution.py:111
  62.6 0.1 select_reduce_fusion.1
  62.7 0.1 select_reduce_fusion.5
  62.8 0.1 div.55
  62.8 0.1 sub.60
  62.9 2.8 %bitcast_reduce_fusion = f32[4,512]{1,0:T(4,128)S(1)} fusion(f32[2048]{0:T(1024)S(1)} %div.55, f32[2048,512]{1,0:T(8,128)} %get-tuple-element.18, f32[2048]{0:T(1024)S(1)} %sub.60), kind=kLoop, calls=%fused_computation.2 | loop fusion | flops 5240832 | bytes 4218880 | tf_op jit(solution)/shard_map/reduce_sum | solution.py:122
  65.8 0.6 copy-done.1
  66.4 1.0 %fusion = bf16[2048,512]{1,0:T(8,128)(2,1)S(1)} fusion(f32[4,512]{1,0:T(4,128)S(1)} %broadcast_add_fusion, f32[2048]{0:T(1024)S(1)} %div.55, f32[2048,512]{1,0:T(8,128)S(1)} %copy-done.1, f32[2048]{0:T(1024)S(1)} %sub.60), kind=kLoop, calls=%fused_computation.1 | loop fusion | flops 6291456 | bytes 6316032 | tf_op jit(solution)/shard_map/convert_element_type | solution.py:123
  67.4 1.2 %copy-done.3 = bf16[8,256,1024]{2,1,0:T(8,128)(2,1)S(1)} copy-done((bf16[8,256,1024]{2,1,0:T(8,128)(2,1)S(1)}, bf16[8,256,1024]{2,1,0:T(8,128)(2,1)}, u32[]{:S(2)}) %copy-start.3) | copy-done | bytes 4194328
  68.6 3.7 %subtract_multiply_fusion.1 = f32[512,1024]{1,0:T(8,128)} fusion(f32[512,1024]{1,0:T(8,128)S(1)} %copy-done.4, bf16[2048,512]{1,0:T(8,128)(2,1)S(1)} %fusion, bf16[2048,1024]{1,0:T(8,128)(2,1)S(1)} %bitcast.56, f32[512]{0:T(512)S(1)} %fusion.8), kind=kOutput, calls=%fused_computation.7 | convolution fusion | flops 2149056512 | bytes 10487808 | tf_op jit(solution)/shard_map/dot_general | solution.py:124
  (35 shorter events, 0.4 us)
Async XLA Ops:
  0.0 1.2 %copy-start = (f32[256,1024]{1,0:T(8,128)S(1)}, f32[256,1024]{1,0:T(8,128)}, u32[]{:S(2)}) copy-start(f32[256,1024]{1,0:T(8,128)} %param.2) | copy-start | bytes 3145732
  1.2 16.1 %collective-permute-start = (bf16[64,1024]{1,0:T(8,128)(2,1)S(1)}, bf16[64,1024]{1,0:T(8,128)(2,1)S(1)}, u32[]{:S(2)}, u32[]{:S(2)}) collective-permute-start(bf16[64,1024]{1,0:T(8,128)(2,1)S(1)} %dynamic-slice_convert_fusion), channel_id=1, source_target_pairs={{0,4},{4,0},{1,5},{5,1},{2,6},{6,2},{3,7},{7,3},{8,12},{12,8},{9,1... | collective-permute-start | bytes 393224 | tf_op jit(solution)/shard_map/ppermute | solution.py:74
  4.3 8.3 %collective-permute-start.3 = (bf16[64,1024]{1,0:T(8,128)(2,1)S(1)}, bf16[64,1024]{1,0:T(8,128)(2,1)S(1)}, u32[]{:S(2)}, u32[]{:S(2)}) collective-permute-start(bf16[64,1024]{1,0:T(8,128)(2,1)S(1)} %dynamic-slice_convert_fusion), channel_id=1, source_target_pairs={{0,8},{8,16},{16,24},{24,0},{1,9},{9,17},{17,25},{25,1},{2,10},{10... | collective-permute-start | bytes 393224 | tf_op jit(solution)/shard_map/ppermute | solution.py:85
  5.9 11.0 %collective-permute-start.7 = (bf16[64,1024]{1,0:T(8,128)(2,1)S(1)}, bf16[64,1024]{1,0:T(8,128)(2,1)S(1)}, u32[]{:S(2)}, u32[]{:S(2)}) collective-permute-start(bf16[64,1024]{1,0:T(8,128)(2,1)S(1)} %dynamic-slice_convert_fusion), channel_id=1, source_target_pairs={{0,16},{8,24},{16,0},{24,8},{1,17},{9,25},{17,1},{25,9},{2,18},{10... | collective-permute-start | bytes 393224 | tf_op jit(solution)/shard_map/ppermute | solution.py:85
  8.4 10.5 %collective-permute-start.11 = (bf16[64,1024]{1,0:T(8,128)(2,1)S(1)}, bf16[64,1024]{1,0:T(8,128)(2,1)S(1)}, u32[]{:S(2)}, u32[]{:S(2)}) collective-permute-start(bf16[64,1024]{1,0:T(8,128)(2,1)S(1)} %dynamic-slice_convert_fusion), channel_id=1, source_target_pairs={{0,24},{8,0},{16,8},{24,16},{1,25},{9,1},{17,9},{25,17},{2,26},{10... | collective-permute-start | bytes 393224 | tf_op jit(solution)/shard_map/ppermute | solution.py:85
  12.6 12.4 %copy-start.5 = (bf16[64,1024]{1,0:T(8,128)(2,1)}, bf16[64,1024]{1,0:T(8,128)(2,1)S(1)}, u32[]{:S(2)}) copy-start(bf16[64,1024]{1,0:T(8,128)(2,1)S(1)} %collective-permute-done.3) | copy-start | bytes 393220
  12.6 7.9 %collective-permute-start.4 = (bf16[64,1024]{1,0:T(8,128)(2,1)S(1)}, bf16[64,1024]{1,0:T(8,128)(2,1)S(1)}, u32[]{:S(2)}, u32[]{:S(2)}) collective-permute-start(bf16[64,1024]{1,0:T(8,128)(2,1)S(1)} %collective-permute-done.3), channel_id=1, source_target_pairs={{0,4},{4,0},{1,5},{5,1},{2,6},{6,2},{3,7},{7,3},{8,12},{12,8},{9,1... | collective-permute-start | bytes 393224 | tf_op jit(solution)/shard_map/ppermute | solution.py:74
  16.8 6.4 %collective-permute-start.8 = (bf16[64,1024]{1,0:T(8,128)(2,1)S(1)}, bf16[64,1024]{1,0:T(8,128)(2,1)S(1)}, u32[]{:S(2)}, u32[]{:S(2)}) collective-permute-start(bf16[64,1024]{1,0:T(8,128)(2,1)S(1)} %collective-permute-done.7), channel_id=1, source_target_pairs={{0,4},{4,0},{1,5},{5,1},{2,6},{6,2},{3,7},{7,3},{8,12},{12,8},{9,1... | collective-permute-start | bytes 393224 | tf_op jit(solution)/shard_map/ppermute | solution.py:74
  17.3 7.7 %copy-start.7 = (bf16[64,1024]{1,0:T(8,128)(2,1)}, bf16[64,1024]{1,0:T(8,128)(2,1)S(1)}, u32[]{:S(2)}) copy-start(bf16[64,1024]{1,0:T(8,128)(2,1)S(1)} %collective-permute-done) | copy-start | bytes 393220
  17.3 9.3 %collective-permute-start.1 = (bf16[2,64,1024]{2,1,0:T(8,128)(2,1)S(1)}, bf16[2,64,1024]{2,1,0:T(8,128)(2,1)S(1)}, u32[]{:S(2)}, u32[]{:S(2)}) collective-permute-start(bf16[2,64,1024]{2,1,0:T(8,128)(2,1)S(1)} %pad_maximum_fusion.4), channel_id=1, source_target_pairs={{0,2},{1,3},{2,0},{3,1},{4,6},{5,7},{6,4},{7,5},{8,10},{9,11},{10,... | collective-permute-start | bytes 786440 | tf_op jit(solution)/shard_map/ppermute | solution.py:79
  18.9 6.0 %collective-permute-start.12 = (bf16[64,1024]{1,0:T(8,128)(2,1)S(1)}, bf16[64,1024]{1,0:T(8,128)(2,1)S(1)}, u32[]{:S(2)}, u32[]{:S(2)}) collective-permute-start(bf16[64,1024]{1,0:T(8,128)(2,1)S(1)} %collective-permute-done.11), channel_id=1, source_target_pairs={{0,4},{4,0},{1,5},{5,1},{2,6},{6,2},{3,7},{7,3},{8,12},{12,8},{9,1... | collective-permute-start | bytes 393224 | tf_op jit(solution)/shard_map/ppermute | solution.py:74
  20.5 4.5 %copy-start.9 = (bf16[64,1024]{1,0:T(8,128)(2,1)}, bf16[64,1024]{1,0:T(8,128)(2,1)S(1)}, u32[]{:S(2)}) copy-start(bf16[64,1024]{1,0:T(8,128)(2,1)S(1)} %collective-permute-done.4) | copy-start | bytes 393220
  20.5 11.7 %collective-permute-start.5 = (bf16[2,64,1024]{2,1,0:T(8,128)(2,1)S(1)}, bf16[2,64,1024]{2,1,0:T(8,128)(2,1)S(1)}, u32[]{:S(2)}, u32[]{:S(2)}) collective-permute-start(bf16[2,64,1024]{2,1,0:T(8,128)(2,1)S(1)} %pad_maximum_fusion.5), channel_id=1, source_target_pairs={{0,2},{1,3},{2,0},{3,1},{4,6},{5,7},{6,4},{7,5},{8,10},{9,11},{10,... | collective-permute-start | bytes 786440 | tf_op jit(solution)/shard_map/ppermute | solution.py:79
  23.2 14.6 %collective-permute-start.9 = (bf16[2,64,1024]{2,1,0:T(8,128)(2,1)S(1)}, bf16[2,64,1024]{2,1,0:T(8,128)(2,1)S(1)}, u32[]{:S(2)}, u32[]{:S(2)}) collective-permute-start(bf16[2,64,1024]{2,1,0:T(8,128)(2,1)S(1)} %pad_maximum_fusion.6), channel_id=1, source_target_pairs={{0,2},{1,3},{2,0},{3,1},{4,6},{5,7},{6,4},{7,5},{8,10},{9,11},{10,... | collective-permute-start | bytes 786440 | tf_op jit(solution)/shard_map/ppermute | solution.py:79
  25.0 17.2 %copy-start.4 = (f32[512,1024]{1,0:T(8,128)S(1)}, f32[512,1024]{1,0:T(8,128)}, u32[]{:S(2)}) copy-start(f32[512,1024]{1,0:T(8,128)} %param.3) | copy-start | bytes 6291460
  25.0 17.1 %collective-permute-start.13 = (bf16[2,64,1024]{2,1,0:T(8,128)(2,1)S(1)}, bf16[2,64,1024]{2,1,0:T(8,128)(2,1)S(1)}, u32[]{:S(2)}, u32[]{:S(2)}) collective-permute-start(bf16[2,64,1024]{2,1,0:T(8,128)(2,1)S(1)} %pad_maximum_fusion.7), channel_id=1, source_target_pairs={{0,2},{1,3},{2,0},{3,1},{4,6},{5,7},{6,4},{7,5},{8,10},{9,11},{10,... | collective-permute-start | bytes 786440 | tf_op jit(solution)/shard_map/ppermute | solution.py:79
  27.6 14.9 %collective-permute-start.2 = (bf16[2,128,1024]{2,1,0:T(8,128)(2,1)S(1)}, bf16[2,128,1024]{2,1,0:T(8,128)(2,1)S(1)}, u32[]{:S(2)}, u32[]{:S(2)}) collective-permute-start(bf16[2,128,1024]{2,1,0:T(8,128)(2,1)S(1)} %pad_maximum_fusion), channel_id=1, source_target_pairs={{0,1},{1,0},{2,3},{3,2},{4,5},{5,4},{6,7},{7,6},{8,9},{9,8},{10,11... | collective-permute-start | bytes 1572872 | tf_op jit(solution)/shard_map/ppermute | solution.py:79
  33.3 10.2 %collective-permute-start.6 = (bf16[2,128,1024]{2,1,0:T(8,128)(2,1)S(1)}, bf16[2,128,1024]{2,1,0:T(8,128)(2,1)S(1)}, u32[]{:S(2)}, u32[]{:S(2)}) collective-permute-start(bf16[2,128,1024]{2,1,0:T(8,128)(2,1)S(1)} %pad_maximum_fusion.1), channel_id=1, source_target_pairs={{0,1},{1,0},{2,3},{3,2},{4,5},{5,4},{6,7},{7,6},{8,9},{9,8},{10,11... | collective-permute-start | bytes 1572872 | tf_op jit(solution)/shard_map/ppermute | solution.py:79
  37.9 6.5 %collective-permute-start.10 = (bf16[2,128,1024]{2,1,0:T(8,128)(2,1)S(1)}, bf16[2,128,1024]{2,1,0:T(8,128)(2,1)S(1)}, u32[]{:S(2)}, u32[]{:S(2)}) collective-permute-start(bf16[2,128,1024]{2,1,0:T(8,128)(2,1)S(1)} %pad_maximum_fusion.2), channel_id=1, source_target_pairs={{0,1},{1,0},{2,3},{3,2},{4,5},{5,4},{6,7},{7,6},{8,9},{9,8},{10,11... | collective-permute-start | bytes 1572872 | tf_op jit(solution)/shard_map/ppermute | solution.py:79
  42.2 2.4 %collective-permute-start.14 = (bf16[2,128,1024]{2,1,0:T(8,128)(2,1)S(1)}, bf16[2,128,1024]{2,1,0:T(8,128)(2,1)S(1)}, u32[]{:S(2)}, u32[]{:S(2)}) collective-permute-start(bf16[2,128,1024]{2,1,0:T(8,128)(2,1)S(1)} %pad_maximum_fusion.3), channel_id=1, source_target_pairs={{0,1},{1,0},{2,3},{3,2},{4,5},{5,4},{6,7},{7,6},{8,9},{9,8},{10,11... | collective-permute-start | bytes 1572872 | tf_op jit(solution)/shard_map/ppermute | solution.py:79
  42.5 0.9 %copy-start.8 = (bf16[64,1024]{1,0:T(8,128)(2,1)S(1)}, bf16[64,1024]{1,0:T(8,128)(2,1)}, u32[]{:S(2)}) copy-start(bf16[64,1024]{1,0:T(8,128)(2,1)} %copy-done.7) | copy-start | bytes 393220
  43.4 0.9 %copy-start.6 = (bf16[64,1024]{1,0:T(8,128)(2,1)S(1)}, bf16[64,1024]{1,0:T(8,128)(2,1)}, u32[]{:S(2)}) copy-start(bf16[64,1024]{1,0:T(8,128)(2,1)} %copy-done.5) | copy-start | bytes 393220
  43.4 1.0 %copy-start.10 = (bf16[64,1024]{1,0:T(8,128)(2,1)S(1)}, bf16[64,1024]{1,0:T(8,128)(2,1)}, u32[]{:S(2)}) copy-start(bf16[64,1024]{1,0:T(8,128)(2,1)} %copy-done.9) | copy-start | bytes 393220
  44.7 4.6 %copy-start.2 = (bf16[8,256,1024]{2,1,0:T(8,128)(2,1)}, bf16[8,256,1024]{2,1,0:T(8,128)(2,1)S(1)}, u32[]{:S(2)}) copy-start(bf16[8,256,1024]{2,1,0:T(8,128)(2,1)S(1)} %maximum_dynamic-update-slice_fusion.3) | copy-start | bytes 12582916
  62.9 3.4 %copy-start.1 = (f32[2048,512]{1,0:T(8,128)S(1)}, f32[2048,512]{1,0:T(8,128)}, u32[]{:S(2)}) copy-start(f32[2048,512]{1,0:T(8,128)} %get-tuple-element.18) | copy-start | bytes 12582916
  66.4 2.2 %copy-start.3 = (bf16[8,256,1024]{2,1,0:T(8,128)(2,1)S(1)}, bf16[8,256,1024]{2,1,0:T(8,128)(2,1)}, u32[]{:S(2)}) copy-start(bf16[8,256,1024]{2,1,0:T(8,128)(2,1)} %copy-done.2) | copy-start | bytes 12582916

commit v11 on v10

--- a/solution.py
+++ b/solution.py
@@ -83,14 +83,41 @@
     landed = [mine]
     for sz in range(1, n_o):
         landed.append(lax.ppermute(mine, "outer", [(i, (i + sz) % n_o) for i in range(n_o)]))
-    parts = [spread(pair_of(piece)) for piece in landed]
-    cur = jnp.zeros((n_o * n_d,) + parts[0].shape[1:], parts[0].dtype)
+
+    k = centroids.shape[0]
+    pod = n_d * n_c * tq
+    everything = jnp.zeros((n_o * pod, d), rows_bf.dtype)
+    logits = jnp.zeros((n_o * pod, k), jnp.float32)
+    local_max = jnp.zeros((n_o * pod,), jnp.float32)
+    local_sum = jnp.zeros((n_o * pod,), jnp.float32)
+
+    def store(done, bufs):
+        part, lg, mx, sm, sz = done
+        at = ((z - sz) % n_o) * pod
+        e_b, l_b, m_b, s_b = bufs
+        e_b = lax.dynamic_update_slice_in_dim(e_b, part, at, 0)
+        l_b = lax.dynamic_update_slice_in_dim(l_b, lg, at, 0)
+        m_b = lax.dynamic_update_slice_in_dim(m_b, mx, at, 0)
+        s_b = lax.dynamic_update_slice_in_dim(s_b, sm, at, 0)
+        return (e_b, l_b, m_b, s_b)
+
+    bufs = (everything, logits, local_max, local_sum)
+    prev = None
     for sz in range(n_o):
-        cur = lax.dynamic_update_slice_in_dim(cur, parts[sz], ((z - sz) % n_o) * n_d, axis=0)
-    everything = cur.reshape(n_od * n_c * tq, d)
-
-    logits = scores_for(everything, cent_bf, squares)
-    local_max, local_sum = row_summary(logits)
+        cur = pair_of(landed[sz])
+        for bi, bit in enumerate(reversed(bits)):
+            if bi == len(bits) - 1 and prev is not None:
+                prev_arrays, cur = lax.optimization_barrier((prev[:4], cur))
+                prev = prev_arrays + (prev[4],)
+            other = lax.ppermute(cur, "cent", [(i, i ^ bit) for i in range(n_c)])
+            cur = jnp.concatenate([cur, other], axis=1)
+        if prev is not None:
+            bufs = store(prev, bufs)
+        part = cur.reshape(pod, d)
+        lg = scores_for(part, cent_bf, squares)
+        mx, sm = row_summary(lg)
+        prev = (part, lg, mx, sm, sz)
+    everything, logits, local_max, local_sum = store(prev, bufs)
 
     src_vec = jnp.stack([a * n_d + (y - sy) % n_d for a, sy in shifts])
     hot_k = src_vec[None, :] == jnp.arange(n_od)[:, None]
@@ -116,8 +143,6 @@
     row_mass = to_local(mass_abs)
 
     weights = (jnp.exp(logits - row_peak[:, None]) / row_mass[:, None]).astype(jnp.bfloat16)
-    k = centroids.shape[0]
-    pod = n_d * n_c * tq
     w_pods = weights.reshape(n_o, pod, k).astype(jnp.float32)
     weight_sum = jnp.sum(w_pods, axis=1)
     scaled = (w_pods / (weight_sum[:, None, :] + 1.0)).astype(jnp.bfloat16)

time: 72.5 us -> 101 us (1.39); the launches traced: 72.2 us -> 99.4 us
  local copies, waits for them, and re-layouts: 5.2 us -> 29.9 us
  waiting for transfers between devices: 22.1 us -> 6.6 us
  other arithmetic: 10.5 us -> 24.6 us
  matrix products: 8.28 us -> 10.4 us
  starting transfers between devices: 16.4 us -> 17.8 us
    ppermute x8, waiting for transfers between devices: 13.3 us -> 1.29 us  [shards_all(): other = lax.ppermute(cur, 'cent', [(i, i ^ bit) for i in range(n_c)])]
    dynamic_update_slice x0 -> x15, local copies, waits for them, and re-layouts: none -> 8.29 us  [the longest x4 3.32 us: store(): e_b = lax.dynamic_update_slice_in_dim(e_b, part, at, 0)]
    concatenate x4 -> x8, other arithmetic: 2.01 us -> 9.15 us  [shards_all(): cur = jnp.concatenate([cur, other], axis=1)]
    convert_element_type x0 -> x1, local copies, waits for them, and re-layouts: none -> 6 us  [shards_all(): w_pods = weights.reshape(n_o, pod, k).astype(jnp.float32)]
    unnamed x22 -> x29, local copies, waits for them, and re-layouts: 4.2 us -> 9.64 us
    convert_element_type x1, other arithmetic: 0.99 us -> 4.92 us  [shards_all(): w_pods = weights.reshape(n_o, pod, k).astype(jnp.float32)]
    reduce_sum x1, other arithmetic: 0.21 us -> 3.55 us  [shards_all(): squares = jnp.sum(centroids * centroids, axis=1)]
    ppermute x3, waiting for transfers between devices: 6.52 us -> 3.2 us  [shards_all(): lax.ppermute(mine, 'outer', [(i, (i + sz) % n_o) for i in range(n_o)])]
  transfers between devices with their start and end apart: 15 -> 15, of which waited for: 7 -> 3; matrix products, arithmetic and copies ran while one was open for 5% -> 27% of each run, Pallas kernels for 0% -> 0%
where the time goes in v11:
time: 101 us; the launch traced here: 99.4 us
  local copies, waits for them, and re-layouts  29.9 us (30%)
  other arithmetic  24.6 us (24%)
  starting transfers between devices  17.8 us (18%)
  matrix products  10.4 us (10%)
  blocking collectives  9.72 us (10%)
  waiting for transfers between devices  6.6 us (7%)
    all_gather x1, blocking collectives, shards_all(): every = lax.all_gather(both, ('dp', 'cent'), axis=0)  9.72 us
    unnamed x29, local copies, waits for them, and re-layouts  9.64 us
    concatenate x8, other arithmetic, shards_all(): cur = jnp.concatenate([cur, other], axis=1)  9.15 us
    dot_general x4, matrix products, scores_for(): lax.dot_general(piece, cent_bf, (((1,), (1,)), ((), ())), preferred_eleme...  6.73 us
    ppermute x4, starting transfers between devices, pair_of(): lax.ppermute(piece, 'dp', [(j, (j + sy) % n_d) for j in range(n_d)])  6.72 us
    convert_element_type x1, local copies, waits for them, and re-layouts, shards_all(): w_pods = weights.reshape(n_o, pod, k).astype(jnp.float32)  6 us
    ppermute x8, starting transfers between devices, shards_all(): other = lax.ppermute(cur, 'cent', [(i, i ^ bit) for i in range(n_c)])  5.53 us
    ppermute x3, starting transfers between devices, shards_all(): lax.ppermute(mine, 'outer', [(i, (i + sz) % n_o) for i in range(n_o)])  5.51 us
  transfers between devices with their start and end apart: 15, of which 3 were waited for; matrix products, arithmetic and copies ran while one was open for 27% of the time, Pallas kernels for 0%

profile of v11, /device:TPU:0, one launch (start us, length us, event | category | flops | bytes accessed | tf_op | source)
XLA Modules:
  0.0 99.4 jit_solution(14706680734851824609)
XLA Ops:
  0.0 1.2 %copy-done = f32[256,1024]{1,0:T(8,128)S(1)} copy-done((f32[256,1024]{1,0:T(8,128)S(1)}, f32[256,1024]{1,0:T(8,128)}, u32[]{:S(2)}) %copy-start) | copy-done | bytes 1048600
  1.2 0.7 dynamic-slice_convert_fusion
  1.9 3.0 %collective-permute-start = (bf16[64,1024]{1,0:T(8,128)(2,1)}, bf16[64,1024]{1,0:T(8,128)(2,1)S(1)}, u32[]{:S(2)}, u32[]{:S(2)}) collective-permute-start(bf16[64,1024]{1,0:T(8,128)(2,1)} %dynamic-slice_convert_fusion), channel_id=1, source_target_pairs={{0,4},{4,0},{1,5},{5,1},{2,6},{6,2},{3,7},{7,3},{8,12},{12,8},{9,1... | collective-permute-start | bytes 393224 | tf_op jit(solution)/shard_map/ppermute | solution.py:74
  4.9 1.6 %collective-permute-start.3 = (bf16[64,1024]{1,0:T(8,128)(2,1)}, bf16[64,1024]{1,0:T(8,128)(2,1)S(1)}, u32[]{:S(2)}, u32[]{:S(2)}) collective-permute-start(bf16[64,1024]{1,0:T(8,128)(2,1)} %dynamic-slice_convert_fusion), channel_id=1, source_target_pairs={{0,8},{8,16},{16,24},{24,0},{1,9},{9,17},{17,25},{25,1},{2,10},{10... | collective-permute-start | bytes 393224 | tf_op jit(solution)/shard_map/ppermute | solution.py:85
  6.5 2.1 %collective-permute-done = bf16[64,1024]{1,0:T(8,128)(2,1)S(1)} collective-permute-done((bf16[64,1024]{1,0:T(8,128)(2,1)}, bf16[64,1024]{1,0:T(8,128)(2,1)S(1)}, u32[]{:S(2)}, u32[]{:S(2)}) %collective-permute-start) | collective-permute-done | bytes 131104 | tf_op jit(solution)/shard_map/ppermute | solution.py:74
  8.6 1.8 %collective-permute-start.1 = (bf16[2,64,1024]{2,1,0:T(8,128)(2,1)S(1)}, bf16[2,64,1024]{2,1,0:T(8,128)(2,1)S(1)}, u32[]{:S(2)}, u32[]{:S(2)}) collective-permute-start(bf16[2,64,1024]{2,1,0:T(8,128)(2,1)S(1)} %pad_maximum_fusion.8), channel_id=1, source_target_pairs={{0,2},{1,3},{2,0},{3,1},{4,6},{5,7},{6,4},{7,5},{8,10},{9,11},{10,... | collective-permute-start | bytes 786440 | tf_op jit(solution)/shard_map/ppermute | solution.py:112
  10.4 2.6 %collective-permute-start.7 = (bf16[64,1024]{1,0:T(8,128)(2,1)}, bf16[64,1024]{1,0:T(8,128)(2,1)S(1)}, u32[]{:S(2)}, u32[]{:S(2)}) collective-permute-start(bf16[64,1024]{1,0:T(8,128)(2,1)} %dynamic-slice_convert_fusion), channel_id=1, source_target_pairs={{0,16},{8,24},{16,0},{24,8},{1,17},{9,25},{17,1},{25,9},{2,18},{10... | collective-permute-start | bytes 393224 | tf_op jit(solution)/shard_map/ppermute | solution.py:85
  13.0 1.5 %collective-permute-start.4 = (bf16[64,1024]{1,0:T(8,128)(2,1)S(1)}, bf16[64,1024]{1,0:T(8,128)(2,1)S(1)}, u32[]{:S(2)}, u32[]{:S(2)}) collective-permute-start(bf16[64,1024]{1,0:T(8,128)(2,1)S(1)} %collective-permute-done.3), channel_id=1, source_target_pairs={{0,4},{4,0},{1,5},{5,1},{2,6},{6,2},{3,7},{7,3},{8,12},{12,8},{9,1... | collective-permute-start | bytes 393224 | tf_op jit(solution)/shard_map/ppermute | solution.py:74
  14.5 1.3 %collective-permute-start.11 = (bf16[64,1024]{1,0:T(8,128)(2,1)}, bf16[64,1024]{1,0:T(8,128)(2,1)S(1)}, u32[]{:S(2)}, u32[]{:S(2)}) collective-permute-start(bf16[64,1024]{1,0:T(8,128)(2,1)} %dynamic-slice_convert_fusion), channel_id=1, source_target_pairs={{0,24},{8,0},{16,8},{24,16},{1,25},{9,1},{17,9},{25,17},{2,26},{10... | collective-permute-start | bytes 393224 | tf_op jit(solution)/shard_map/ppermute | solution.py:85
  15.8 3.2 %collective-permute-done.7 = bf16[64,1024]{1,0:T(8,128)(2,1)S(1)} collective-permute-done((bf16[64,1024]{1,0:T(8,128)(2,1)}, bf16[64,1024]{1,0:T(8,128)(2,1)S(1)}, u32[]{:S(2)}, u32[]{:S(2)}) %collective-permute-start.7) | collective-permute-done | bytes 131104 | tf_op jit(solution)/shard_map/ppermute | solution.py:85
  19.0 2.0 %collective-permute-start.8 = (bf16[64,1024]{1,0:T(8,128)(2,1)S(1)}, bf16[64,1024]{1,0:T(8,128)(2,1)S(1)}, u32[]{:S(2)}, u32[]{:S(2)}) collective-permute-start(bf16[64,1024]{1,0:T(8,128)(2,1)S(1)} %collective-permute-done.7), channel_id=1, source_target_pairs={{0,4},{4,0},{1,5},{5,1},{2,6},{6,2},{3,7},{7,3},{8,12},{12,8},{9,1... | collective-permute-start | bytes 393224 | tf_op jit(solution)/shard_map/ppermute | solution.py:74
  21.1 0.6 collective-permute-start.5
  21.8 3.6 %multiply_reduce_fusion = (f32[512]{0:T(512)S(1)}, bf16[512,1024]{1,0:T(8,128)(2,1)}) fusion(f32[512,1024]{1,0:T(8,128)} %param.3), kind=kLoop, calls=%fused_computation.4 | loop fusion | flops 1572352 | bytes 3147776 | tf_op jit(solution)/shard_map/reduce_sum | solution.py:58
  25.4 0.7 stack.112
  26.1 0.2 collective-permute-start.12
  26.3 0.7 pad_maximum_fusion.10
  27.0 1.3 %collective-permute-start.9 = (bf16[2,64,1024]{2,1,0:T(8,128)(2,1)}, bf16[2,64,1024]{2,1,0:T(8,128)(2,1)}, u32[]{:S(2)}, u32[]{:S(2)}) collective-permute-start(bf16[2,64,1024]{2,1,0:T(8,128)(2,1)} %pad_maximum_fusion.10), channel_id=1, source_target_pairs={{0,2},{1,3},{2,0},{3,1},{4,6},{5,7},{6,4},{7,5},{8,10},{9,11},{10,... | collective-permute-start | bytes 786440 | tf_op jit(solution)/shard_map/ppermute | solution.py:112
  28.3 1.8 %pad_maximum_fusion.5 = bf16[2,128,1024]{2,1,0:T(8,128)(2,1)} fusion(bf16[2,64,1024]{2,1,0:T(8,128)(2,1)} %collective-permute-done.5, bf16[1,64,1024]{2,1,0:T(8,128)(2,1)S(1)} %bitcast.84, bf16[1,64,1024]{2,1,0:T(8,128)(2,1)S(1)} %bitcast.82), kind=kLoop, calls=%fused_computation.27 | loop fusion | flops 1572864 | bytes 1048576 | tf_op jit(solution)/shard_map/concatenate | solution.py:113
  30.1 2.0 %fusion.16 = (f32[512]{0:T(512)S(1)}, f32[512,512]{0,1:T(8,128)S(1)}) fusion(f32[512]{0:T(512)S(1)} %get-tuple-element.47, bf16[512,1024]{1,0:T(8,128)(2,1)S(1)} %bitcast.61, bf16[512,1024]{1,0:T(8,128)(2,1)} %get-tuple-element.48), kind=kOutput, calls=%fused_computation.73 | convolution fusion | flops 537918976 | bytes 3149824 | tf_op jit(solution)/shard_map/dot_general | solution.py:10
  32.1 0.2 exponential_reduce_fusion.3
  32.3 0.3 collective-permute-start.6
  32.7 0.9 pad_maximum_fusion.11
  33.7 0.9 collective-permute-start.13
  34.5 1.3 %collective-permute-done.9 = bf16[2,64,1024]{2,1,0:T(8,128)(2,1)} collective-permute-done((bf16[2,64,1024]{2,1,0:T(8,128)(2,1)}, bf16[2,64,1024]{2,1,0:T(8,128)(2,1)}, u32[]{:S(2)}, u32[]{:S(2)}) %collective-permute-start.9) | collective-permute-done | bytes 262176 | tf_op jit(solution)/shard_map/ppermute | solution.py:112
  35.8 1.8 %pad_maximum_fusion.6 = bf16[2,128,1024]{2,1,0:T(8,128)(2,1)} fusion(bf16[2,64,1024]{2,1,0:T(8,128)(2,1)} %collective-permute-done.9, bf16[1,64,1024]{2,1,0:T(8,128)(2,1)S(1)} %bitcast.80, bf16[1,64,1024]{2,1,0:T(8,128)(2,1)S(1)} %bitcast.78), kind=kLoop, calls=%fused_computation.28 | loop fusion | flops 1572864 | bytes 1048576 | tf_op jit(solution)/shard_map/concatenate | solution.py:113
  37.6 1.3 %pad_maximum_fusion.1 = bf16[2,256,1024]{2,1,0:T(8,128)(2,1)S(1)} fusion(bf16[2,128,1024]{2,1,0:T(8,128)(2,1)} %collective-permute-done.6, bf16[2,128,1024]{2,1,0:T(8,128)(2,1)} %pad_maximum_fusion.5), kind=kLoop, calls=%fused_computation.19 | loop fusion | flops 2097152 | bytes 2097152 | tf_op jit(solution)/shard_map/concatenate | solution.py:113
  38.9 1.0 copy-done.2
  39.9 2.0 %fusion.17 = (f32[512]{0:T(512)S(1)}, f32[512,512]{0,1:T(8,128)S(1)}) fusion(f32[512]{0:T(512)S(1)} %get-tuple-element.47, bf16[512,1024]{1,0:T(8,128)(2,1)S(1)} %bitcast.65, bf16[512,1024]{1,0:T(8,128)(2,1)} %get-tuple-element.48), kind=kOutput, calls=%fused_computation.74 | convolution fusion | flops 537918976 | bytes 3149824 | tf_op jit(solution)/shard_map/dot_general | solution.py:10
  41.9 1.0 %copy-done.4 = f32[512,512]{0,1:T(8,128)} copy-done((f32[512,512]{0,1:T(8,128)}, f32[512,512]{0,1:T(8,128)S(1)}, u32[]{:S(2)}) %copy-start.4) | copy-done | bytes 1048600
  42.9 0.2 exponential_reduce_fusion.2
  43.2 1.7 %pad_maximum_fusion.7 = bf16[2,128,1024]{2,1,0:T(8,128)(2,1)} fusion(bf16[2,64,1024]{2,1,0:T(8,128)(2,1)S(1)} %collective-permute-done.13, bf16[1,64,1024]{2,1,0:T(8,128)(2,1)} %bitcast.10, bf16[1,64,1024]{2,1,0:T(8,128)(2,1)S(1)} %bitcast.76), kind=kLoop, calls=%fused_computation.29 | loop fusion | flops 1572864 | bytes 1048576 | tf_op jit(solution)/shard_map/concatenate | solution.py:113
  44.9 0.2 dynamic_update_slice.52
  45.1 0.3 dynamic_update_slice.56
  45.3 0.5 broadcast_in_dim.162
  46.0 1.9 %copy-done.8 = bf16[2048,1024]{1,0:T(8,128)(2,1)} copy-done((bf16[2048,1024]{1,0:T(8,128)(2,1)}, bf16[2048,1024]{1,0:T(8,128)(2,1)S(1)}, u32[]{:S(2)}) %copy-start.8) | copy-done | bytes 4194328
  47.9 2.5 %broadcast_in_dim.147 = f32[2048,512]{0,1:T(8,128)} broadcast(f32[]{:T(128)} %constant.78.clone.1), dimensions={} | broadcast | bytes 4194308 | tf_op jit(solution)/shard_map/broadcast_in_dim | solution.py:90
  50.4 1.1 %constant_dynamic-update-slice_fusion.7 = f32[2048,512]{0,1:T(8,128)} fusion(f32[2048,512]{0,1:T(8,128)} %broadcast_in_dim.147, f32[512,512]{0,1:T(8,128)S(1)} %get-tuple-element.20, s32[]{:T(128)S(6)} %select_n.96), kind=kLoop, calls=%fused_computation.67 | loop fusion | bytes 2097156 | tf_op jit(solution)/shard_map/dynamic_update_slice | solution.py:99
  51.7 0.2 dynamic_update_slice.57
  51.9 1.4 %pad_maximum_fusion.2 = bf16[2,256,1024]{2,1,0:T(8,128)(2,1)S(1)} fusion(bf16[2,128,1024]{2,1,0:T(8,128)(2,1)} %collective-permute-done.10, bf16[2,128,1024]{2,1,0:T(8,128)(2,1)} %pad_maximum_fusion.6), kind=kLoop, calls=%fused_computation.20 | loop fusion | flops 2097152 | bytes 2097152 | tf_op jit(solution)/shard_map/concatenate | solution.py:113
  53.3 2.0 %fusion.18 = (f32[512]{0:T(512)S(1)}, f32[512,512]{0,1:T(8,128)S(1)}) fusion(f32[512]{0:T(512)S(1)} %get-tuple-element.47, bf16[512,1024]{1,0:T(8,128)(2,1)S(1)} %bitcast.67, bf16[512,1024]{1,0:T(8,128)(2,1)} %get-tuple-element.48), kind=kOutput, calls=%fused_computation.75 | convolution fusion | flops 537918976 | bytes 3149824 | tf_op jit(solution)/shard_map/dot_general | solution.py:10
  55.3 1.0 %copy-done.6 = f32[512,512]{0,1:T(8,128)} copy-done((f32[512,512]{0,1:T(8,128)}, f32[512,512]{0,1:T(8,128)S(1)}, u32[]{:S(2)}) %copy-start.6) | copy-done | bytes 1048600
  56.3 0.2 exponential_reduce_fusion.1
  56.5 0.5 collective-permute-start.14
  57.0 1.0 %constant_dynamic-update-slice_fusion.2 = bf16[2048,1024]{1,0:T(8,128)(2,1)} fusion(bf16[2048,1024]{1,0:T(8,128)(2,1)} %copy-done.8, bf16[512,1024]{1,0:T(8,128)(2,1)S(1)} %bitcast.66, s32[]{:T(128)S(6)} %select_n.98), kind=kLoop, calls=%fused_computation.62 | loop fusion | bytes 2097156 | tf_op jit(solution)/shard_map/dynamic_update_slice | solution.py:98
  58.1 1.1 %constant_dynamic-update-slice_fusion.6 = f32[2048,512]{0,1:T(8,128)} fusion(f32[2048,512]{0,1:T(8,128)} %constant_dynamic-update-slice_fusion.7, f32[512,512]{0,1:T(8,128)S(1)} %copy-done.5, s32[]{:T(128)S(6)} %select_n.98), kind=kLoop, calls=%fused_computation.66 | loop fusion | bytes 2097156 | tf_op jit(solution)/shard_map/dynamic_update_slice | solution.py:99
  59.4 0.2 dynamic_update_slice.58
  59.6 1.1 %constant_dynamic-update-slice_fusion.1 = bf16[2048,1024]{1,0:T(8,128)(2,1)} fusion(bf16[2048,1024]{1,0:T(8,128)(2,1)} %constant_dynamic-update-slice_fusion.2, bf16[512,1024]{1,0:T(8,128)(2,1)S(1)} %bitcast.68, s32[]{:T(128)S(6)} %select_n.100), kind=kLoop, calls=%fused_computation.61 | loop fusion | bytes 2097156 | tf_op jit(solution)/shard_map/dynamic_update_slice | solution.py:98
  60.6 1.1 %constant_dynamic-update-slice_fusion.5 = f32[2048,512]{0,1:T(8,128)} fusion(f32[2048,512]{0,1:T(8,128)} %constant_dynamic-update-slice_fusion.6, f32[512,512]{0,1:T(8,128)S(1)} %copy-done.7, s32[]{:T(128)S(6)} %select_n.100), kind=kLoop, calls=%fused_computation.65 | loop fusion | bytes 2097156 | tf_op jit(solution)/shard_map/dynamic_update_slice | solution.py:99
  61.7 1.1 %pad_maximum_fusion.3 = bf16[2,256,1024]{2,1,0:T(8,128)(2,1)S(1)} fusion(bf16[2,128,1024]{2,1,0:T(8,128)(2,1)} %collective-permute-done.14, bf16[2,128,1024]{2,1,0:T(8,128)(2,1)S(1)} %copy-done.11), kind=kLoop, calls=%fused_computation.21 | loop fusion | flops 2097152 | bytes 2097152 | tf_op jit(solution)/shard_map/concatenate | solution.py:113
  62.8 0.8 fusion.19
  63.6 0.3 dynamic_update_slice.55
  64.0 1.2 %exponential_reduce_fusion = (f32[512]{0:T(512)S(1)}, f32[2048,512]{0,1:T(8,128)}) fusion(f32[512,512]{0,1:T(8,128)S(1)} %get-tuple-element.58, f32[512]{0:T(512)S(1)} %get-tuple-element.57, f32[2048,512]{0,1:T(8,128)} %constant_dynamic-update-slice_fusion.5, s32[]{:T(128)S(6)} %select_n.102), kind=kLoop, calls=%fused_computation.22 | loop fusion | flops 523776 | bytes 2101252 | tf_op jit(solution)/shard_map/reduce_sum | solution.py:18
  65.2 0.2 dynamic_update_slice.59
  65.8 9.7 %all-gather = f32[16,8,4,64]{3,1,2,0:T(8,128)S(1)} all-gather(f32[2,8,4,64]{3,1,2,0:T(8,128)S(1)} %copy.35), channel_id=2, replica_groups=mesh['outer'=4,'dp'=2,'cent'=4] {'dp','cent'}, dimensions={0}, use_global_device_ids=true | all-gather | bytes 147456 | tf_op jit(solution)/shard_map/all_gather | solution.py:138
  75.9 4.9 %fusion = f32[2048,512]{0,1:T(8,128)} fusion(f32[2048,512]{0,1:T(8,128)} %get-tuple-element.50, f32[2048]{0:T(1024)S(1)} %div.55, f32[2048]{0:T(1024)S(1)} %sub.111), kind=kLoop, calls=%fused_computation.2 | loop fusion | flops 4194304 | bytes 8404992 | tf_op jit(solution)/shard_map/convert_element_type | solution.py:146
  80.9 6.0 %reshape.118 = f32[4,512,512]{1,0,2:T(4,128)} reshape(f32[2048,512]{0,1:T(8,128)} %fusion) | data formatting | bytes 8388608 | tf_op jit(solution)/shard_map/convert_element_type | solution.py:146
  86.9 2.8 %reduce_sum.149 = f32[4,512]{0,1:T(8,128)S(1)} reduce(f32[4,512,512]{1,0,2:T(4,128)} %reshape.118, f32[]{:T(128)} %constant.78.clone.1), dimensions={1}, to_apply=%region_19.20 | reduce | flops 1046528 | bytes 4202500 | tf_op jit(solution)/shard_map/reduce_sum | solution.py:147
  89.7 0.6 slice_reduce_fusion.3
  90.3 1.1 %constant_dynamic-update-slice_fusion = bf16[2048,1024]{1,0:T(8,128)(2,1)} fusion(bf16[2048,1024]{1,0:T(8,128)(2,1)} %constant_dynamic-update-slice_fusion.1, bf16[512,1024]{1,0:T(8,128)(2,1)S(1)} %bitcast.64, s32[]{:T(128)S(6)} %select_n.102), kind=kLoop, calls=%fused_computation.60 | loop fusion | bytes 2097156 | tf_op jit(solution)/shard_map/dynamic_update_slice | solution.py:98
  91.4 0.7 div.58
  92.1 2.0 %copy.45 = f32[64,8,4,512]{3,1,2,0:T(8,128)S(1)} copy(f32[64,8,4,512]{3,2,1,0:T(4,128)S(1)} %bitcast.60) | data formatting | bytes 8388608
  94.2 0.2 copy-done.1
  94.5 1.2 %copy-done.9 = bf16[2048,1024]{1,0:T(8,128)(2,1)S(1)} copy-done((bf16[2048,1024]{1,0:T(8,128)(2,1)S(1)}, bf16[2048,1024]{1,0:T(8,128)(2,1)}, u32[]{:S(2)}) %copy-start.9) | copy-done | bytes 4194328
  95.7 3.7 %subtract_multiply_fusion = f32[512,1024]{1,0:T(8,128)} fusion(f32[512,1024]{1,0:T(8,128)S(1)} %copy-done.10, bf16[2048,1024]{1,0:T(8,128)(2,1)S(1)} %copy-done.9, f32[2048,512]{0,1:T(8,128)S(1)} %copy-done.1, f32[2048,512]{0,1:T(8,128)S(1)} %bitcast.69, f32[512]{0:T(512)S(1)} %fusion.15), kind=kOutput, calls=%fused_computation.3 | convolution fusion | flops 2151153664 | bytes 16779264 | tf_op jit(solution)/shard_map/dot_general | solution.py:149
  (68 shorter events, 1.8 us)
Async XLA Ops:
  0.0 1.2 %copy-start = (f32[256,1024]{1,0:T(8,128)S(1)}, f32[256,1024]{1,0:T(8,128)}, u32[]{:S(2)}) copy-start(f32[256,1024]{1,0:T(8,128)} %param.2) | copy-start | bytes 3145732
  1.9 6.7 %collective-permute-start = (bf16[64,1024]{1,0:T(8,128)(2,1)}, bf16[64,1024]{1,0:T(8,128)(2,1)S(1)}, u32[]{:S(2)}, u32[]{:S(2)}) collective-permute-start(bf16[64,1024]{1,0:T(8,128)(2,1)} %dynamic-slice_convert_fusion), channel_id=1, source_target_pairs={{0,4},{4,0},{1,5},{5,1},{2,6},{6,2},{3,7},{7,3},{8,12},{12,8},{9,1... | collective-permute-start | bytes 393224 | tf_op jit(solution)/shard_map/ppermute | solution.py:74
  4.9 8.1 %collective-permute-start.3 = (bf16[64,1024]{1,0:T(8,128)(2,1)}, bf16[64,1024]{1,0:T(8,128)(2,1)S(1)}, u32[]{:S(2)}, u32[]{:S(2)}) collective-permute-start(bf16[64,1024]{1,0:T(8,128)(2,1)} %dynamic-slice_convert_fusion), channel_id=1, source_target_pairs={{0,8},{8,16},{16,24},{24,0},{1,9},{9,17},{17,25},{25,1},{2,10},{10... | collective-permute-start | bytes 393224 | tf_op jit(solution)/shard_map/ppermute | solution.py:85
  8.6 13.1 %collective-permute-start.1 = (bf16[2,64,1024]{2,1,0:T(8,128)(2,1)S(1)}, bf16[2,64,1024]{2,1,0:T(8,128)(2,1)S(1)}, u32[]{:S(2)}, u32[]{:S(2)}) collective-permute-start(bf16[2,64,1024]{2,1,0:T(8,128)(2,1)S(1)} %pad_maximum_fusion.8), channel_id=1, source_target_pairs={{0,2},{1,3},{2,0},{3,1},{4,6},{5,7},{6,4},{7,5},{8,10},{9,11},{10,... | collective-permute-start | bytes 786440 | tf_op jit(solution)/shard_map/ppermute | solution.py:112
  10.4 8.7 %collective-permute-start.7 = (bf16[64,1024]{1,0:T(8,128)(2,1)}, bf16[64,1024]{1,0:T(8,128)(2,1)S(1)}, u32[]{:S(2)}, u32[]{:S(2)}) collective-permute-start(bf16[64,1024]{1,0:T(8,128)(2,1)} %dynamic-slice_convert_fusion), channel_id=1, source_target_pairs={{0,16},{8,24},{16,0},{24,8},{1,17},{9,25},{17,1},{25,9},{2,18},{10... | collective-permute-start | bytes 393224 | tf_op jit(solution)/shard_map/ppermute | solution.py:85
  13.0 8.1 %collective-permute-start.4 = (bf16[64,1024]{1,0:T(8,128)(2,1)S(1)}, bf16[64,1024]{1,0:T(8,128)(2,1)S(1)}, u32[]{:S(2)}, u32[]{:S(2)}) collective-permute-start(bf16[64,1024]{1,0:T(8,128)(2,1)S(1)} %collective-permute-done.3), channel_id=1, source_target_pairs={{0,4},{4,0},{1,5},{5,1},{2,6},{6,2},{3,7},{7,3},{8,12},{12,8},{9,1... | collective-permute-start | bytes 393224 | tf_op jit(solution)/shard_map/ppermute | solution.py:74
  14.5 11.6 %collective-permute-start.11 = (bf16[64,1024]{1,0:T(8,128)(2,1)}, bf16[64,1024]{1,0:T(8,128)(2,1)S(1)}, u32[]{:S(2)}, u32[]{:S(2)}) collective-permute-start(bf16[64,1024]{1,0:T(8,128)(2,1)} %dynamic-slice_convert_fusion), channel_id=1, source_target_pairs={{0,24},{8,0},{16,8},{24,16},{1,25},{9,1},{17,9},{25,17},{2,26},{10... | collective-permute-start | bytes 393224 | tf_op jit(solution)/shard_map/ppermute | solution.py:85
  19.0 7.2 %collective-permute-start.8 = (bf16[64,1024]{1,0:T(8,128)(2,1)S(1)}, bf16[64,1024]{1,0:T(8,128)(2,1)S(1)}, u32[]{:S(2)}, u32[]{:S(2)}) collective-permute-start(bf16[64,1024]{1,0:T(8,128)(2,1)S(1)} %collective-permute-done.7), channel_id=1, source_target_pairs={{0,4},{4,0},{1,5},{5,1},{2,6},{6,2},{3,7},{7,3},{8,12},{12,8},{9,1... | collective-permute-start | bytes 393224 | tf_op jit(solution)/shard_map/ppermute | solution.py:74
  21.1 7.2 %collective-permute-start.5 = (bf16[2,64,1024]{2,1,0:T(8,128)(2,1)S(1)}, bf16[2,64,1024]{2,1,0:T(8,128)(2,1)}, u32[]{:S(2)}, u32[]{:S(2)}) collective-permute-start(bf16[2,64,1024]{2,1,0:T(8,128)(2,1)S(1)} %pad_maximum_fusion.9), channel_id=1, source_target_pairs={{0,2},{1,3},{2,0},{3,1},{4,6},{5,7},{6,4},{7,5},{8,10},{9,11},{10,... | collective-permute-start | bytes 786440 | tf_op jit(solution)/shard_map/ppermute | solution.py:112
  21.8 8.3 %collective-permute-start.2 = (bf16[2,128,1024]{2,1,0:T(8,128)(2,1)S(1)}, bf16[2,128,1024]{2,1,0:T(8,128)(2,1)S(1)}, u32[]{:S(2)}, u32[]{:S(2)}) collective-permute-start(bf16[2,128,1024]{2,1,0:T(8,128)(2,1)S(1)} %pad_maximum_fusion.4), channel_id=1, source_target_pairs={{0,1},{1,0},{2,3},{3,2},{4,5},{5,4},{6,7},{7,6},{8,9},{9,8},{10,11... | collective-permute-start | bytes 1572872 | tf_op jit(solution)/shard_map/ppermute | solution.py:112
  26.1 6.7 %collective-permute-start.12 = (bf16[64,1024]{1,0:T(8,128)(2,1)S(1)}, bf16[64,1024]{1,0:T(8,128)(2,1)}, u32[]{:S(2)}, u32[]{:S(2)}) collective-permute-start(bf16[64,1024]{1,0:T(8,128)(2,1)S(1)} %collective-permute-done.11), channel_id=1, source_target_pairs={{0,4},{4,0},{1,5},{5,1},{2,6},{6,2},{3,7},{7,3},{8,12},{12,8},{9,1... | collective-permute-start | bytes 393224 | tf_op jit(solution)/shard_map/ppermute | solution.py:74
  27.0 5.6 %copy-start.13 = (s32[8]{0:T(128)S(1)}, s32[8]{0:T(128)}, u32[]{:S(2)}) copy-start(s32[8]{0:T(128)} %stack.112) | copy-start | bytes 100
  27.0 8.8 %collective-permute-start.9 = (bf16[2,64,1024]{2,1,0:T(8,128)(2,1)}, bf16[2,64,1024]{2,1,0:T(8,128)(2,1)}, u32[]{:S(2)}, u32[]{:S(2)}) collective-permute-start(bf16[2,64,1024]{2,1,0:T(8,128)(2,1)} %pad_maximum_fusion.10), channel_id=1, source_target_pairs={{0,2},{1,3},{2,0},{3,1},{4,6},{5,7},{6,4},{7,5},{8,10},{9,11},{10,... | collective-permute-start | bytes 786440 | tf_op jit(solution)/shard_map/ppermute | solution.py:112
  32.3 5.3 %collective-permute-start.6 = (bf16[2,128,1024]{2,1,0:T(8,128)(2,1)}, bf16[2,128,1024]{2,1,0:T(8,128)(2,1)}, u32[]{:S(2)}, u32[]{:S(2)}) collective-permute-start(bf16[2,128,1024]{2,1,0:T(8,128)(2,1)} %pad_maximum_fusion.5), channel_id=1, source_target_pairs={{0,1},{1,0},{2,3},{3,2},{4,5},{5,4},{6,7},{7,6},{8,9},{9,8},{10,11... | collective-permute-start | bytes 1572872 | tf_op jit(solution)/shard_map/ppermute | solution.py:112
  33.7 9.5 %collective-permute-start.13 = (bf16[2,64,1024]{2,1,0:T(8,128)(2,1)S(1)}, bf16[2,64,1024]{2,1,0:T(8,128)(2,1)S(1)}, u32[]{:S(2)}, u32[]{:S(2)}) collective-permute-start(bf16[2,64,1024]{2,1,0:T(8,128)(2,1)S(1)} %pad_maximum_fusion.11), channel_id=1, source_target_pairs={{0,2},{1,3},{2,0},{3,1},{4,6},{5,7},{6,4},{7,5},{8,10},{9,11},{10,... | collective-permute-start | bytes 786440 | tf_op jit(solution)/shard_map/ppermute | solution.py:112
  38.9 1.0 copy-start.2
  41.9 1.0 %copy-start.4 = (f32[512,512]{0,1:T(8,128)}, f32[512,512]{0,1:T(8,128)S(1)}, u32[]{:S(2)}) copy-start(f32[512,512]{0,1:T(8,128)S(1)} %get-tuple-element.22) | copy-start | bytes 3145732
  43.1 8.8 %collective-permute-start.10 = (bf16[2,128,1024]{2,1,0:T(8,128)(2,1)}, bf16[2,128,1024]{2,1,0:T(8,128)(2,1)}, u32[]{:S(2)}, u32[]{:S(2)}) collective-permute-start(bf16[2,128,1024]{2,1,0:T(8,128)(2,1)} %pad_maximum_fusion.6), channel_id=1, source_target_pairs={{0,1},{1,0},{2,3},{3,2},{4,5},{5,4},{6,7},{7,6},{8,9},{9,8},{10,11... | collective-permute-start | bytes 1572872 | tf_op jit(solution)/shard_map/ppermute | solution.py:112
  46.0 1.9 %copy-start.8 = (bf16[2048,1024]{1,0:T(8,128)(2,1)}, bf16[2048,1024]{1,0:T(8,128)(2,1)S(1)}, u32[]{:S(2)}) copy-start(bf16[2048,1024]{1,0:T(8,128)(2,1)S(1)} %constant_dynamic-update-slice_fusion.3) | copy-start | bytes 12582916
  50.4 6.6 %copy-start.3 = (bf16[2,256,1024]{2,1,0:T(8,128)(2,1)S(1)}, bf16[2,256,1024]{2,1,0:T(8,128)(2,1)}, u32[]{:S(2)}) copy-start(bf16[2,256,1024]{2,1,0:T(8,128)(2,1)} %copy-done.2) | copy-start | bytes 3145732
  51.9 6.2 %copy-start.5 = (f32[512,512]{0,1:T(8,128)S(1)}, f32[512,512]{0,1:T(8,128)}, u32[]{:S(2)}) copy-start(f32[512,512]{0,1:T(8,128)} %copy-done.4) | copy-start | bytes 3145732
  55.3 1.0 %copy-start.6 = (f32[512,512]{0,1:T(8,128)}, f32[512,512]{0,1:T(8,128)S(1)}, u32[]{:S(2)}) copy-start(f32[512,512]{0,1:T(8,128)S(1)} %get-tuple-element.24) | copy-start | bytes 3145732
  56.5 5.2 %collective-permute-start.14 = (bf16[2,128,1024]{2,1,0:T(8,128)(2,1)}, bf16[2,128,1024]{2,1,0:T(8,128)(2,1)}, u32[]{:S(2)}, u32[]{:S(2)}) collective-permute-start(bf16[2,128,1024]{2,1,0:T(8,128)(2,1)} %pad_maximum_fusion.7), channel_id=1, source_target_pairs={{0,1},{1,0},{2,3},{3,2},{4,5},{5,4},{6,7},{7,6},{8,9},{9,8},{10,11... | collective-permute-start | bytes 1572872 | tf_op jit(solution)/shard_map/ppermute | solution.py:112
  58.1 2.6 %copy-start.7 = (f32[512,512]{0,1:T(8,128)S(1)}, f32[512,512]{0,1:T(8,128)}, u32[]{:S(2)}) copy-start(f32[512,512]{0,1:T(8,128)} %copy-done.6) | copy-start | bytes 3145732
  59.6 2.1 %copy-start.11 = (bf16[2,128,1024]{2,1,0:T(8,128)(2,1)S(1)}, bf16[2,128,1024]{2,1,0:T(8,128)(2,1)}, u32[]{:S(2)}) copy-start(bf16[2,128,1024]{2,1,0:T(8,128)(2,1)} %pad_maximum_fusion.7) | copy-start | bytes 1572868
  59.6 3.3 %copy-start.12 = (bf16[512,1024]{1,0:T(8,128)(2,1)S(1)}, bf16[512,1024]{1,0:T(8,128)(2,1)}, u32[]{:S(2)}) copy-start(bf16[512,1024]{1,0:T(8,128)(2,1)} %get-tuple-element.48) | copy-start | bytes 3145732
  91.4 2.8 %copy-start.10 = (f32[512,1024]{1,0:T(8,128)S(1)}, f32[512,1024]{1,0:T(8,128)}, u32[]{:S(2)}) copy-start(f32[512,1024]{1,0:T(8,128)} %param.3) | copy-start | bytes 6291460
  92.1 2.3 %copy-start.1 = (f32[2048,512]{0,1:T(8,128)S(1)}, f32[2048,512]{0,1:T(8,128)}, u32[]{:S(2)}) copy-start(f32[2048,512]{0,1:T(8,128)} %fusion) | copy-start | bytes 12582916
  92.1 3.5 %copy-start.9 = (bf16[2048,1024]{1,0:T(8,128)(2,1)S(1)}, bf16[2048,1024]{1,0:T(8,128)(2,1)}, u32[]{:S(2)}) copy-start(bf16[2048,1024]{1,0:T(8,128)(2,1)} %constant_dynamic-update-slice_fusion) | copy-start | bytes 12582916

commit v12 on v10

--- a/solution.py
+++ b/solution.py
@@ -83,7 +83,18 @@
     landed = [mine]
     for sz in range(1, n_o):
         landed.append(lax.ppermute(mine, "outer", [(i, (i + sz) % n_o) for i in range(n_o)]))
-    parts = [spread(pair_of(piece)) for piece in landed]
+    parts = [None] + [spread(pair_of(piece)) for piece in landed[1:]]
+
+    h = q % 2
+    half = t // 2
+    my_half = lax.dynamic_slice_in_dim(rows_bf, h * half, half, 0)
+    own_blocks = [rows_bf]
+    for sy in range(1, n_d):
+        got = lax.ppermute(my_half, "dp", [(j, (j + sy) % n_d) for j in range(n_d)])
+        mate = lax.ppermute(got, "cent", [(i, i ^ 1) for i in range(n_c)])
+        own_blocks.append(jnp.concatenate([got, mate], axis=0))
+    parts[0] = jnp.stack(own_blocks)
+
     cur = jnp.zeros((n_o * n_d,) + parts[0].shape[1:], parts[0].dtype)
     for sz in range(n_o):
         cur = lax.dynamic_update_slice_in_dim(cur, parts[sz], ((z - sz) % n_o) * n_d, axis=0)
@@ -94,17 +105,25 @@
 
     src_vec = jnp.stack([a * n_d + (y - sy) % n_d for a, sy in shifts])
     hot_k = src_vec[None, :] == jnp.arange(n_od)[:, None]
-    c_vec = jnp.stack([q ^ x for x in xs])
-    hot_c = c_vec[None, :] == jnp.arange(n_c)[:, None]
+    jj = jnp.arange(n_c)
+    xor_map = q ^ jnp.asarray(xs, jnp.int32)
+    hq = n_c // 2
+    half_map = ((jj // hq) ^ h) * hq + jj % hq
+    maps = []
+    for a, sy in shifts:
+        own_map = jj if sy == 0 else half_map
+        maps.append(jnp.where(a == z, own_map, xor_map))
+    c_map = jnp.stack(maps)
+    hot_kc = c_map[:, None, :] == jj[None, :, None]
 
     def to_absolute(v):
         v = v.reshape(n_od, n_c, tq)
-        v = jnp.sum(jnp.where(hot_c[None, :, :, None], v[:, None, :, :], 0.0), axis=2)
+        v = jnp.sum(jnp.where(hot_kc[:, :, :, None], v[:, None, :, :], 0.0), axis=2)
         return jnp.sum(jnp.where(hot_k[:, :, None, None], v[None], 0.0), axis=1)
 
     def to_local(v):
         v = jnp.sum(jnp.where(hot_k[:, :, None, None], v[:, None], 0.0), axis=0)
-        v = jnp.sum(jnp.where(hot_c[:, :, None], v[:, :, None, :], 0.0), axis=1)
+        v = jnp.sum(jnp.where(hot_kc[:, :, :, None], v[:, :, None, :], 0.0), axis=1)
         return v.reshape(n_od * n_c * tq)
 
     both = jnp.stack([to_absolute(local_max), to_absolute(local_sum)])
@@ -140,7 +159,7 @@
         k = centroids.shape[0]
         n_all = t * n_o * n_d
         footprint = n_all * d * 2 + n_all * k * 4 * 2
-        if footprint <= (24 << 20) and t % n_c == 0 and (n_c & (n_c - 1)) == 0:
+        if footprint <= (24 << 20) and t % n_c == 0 and n_c >= 2 and (n_c & (n_c - 1)) == 0:
             return shards_all(rows, centroids)
         return shards_pod(rows, centroids)
 

time: 72.5 us -> 71.9 us (level)
  other arithmetic: 10.5 us -> 20 us
  waiting for transfers between devices: 22.1 us -> 14.3 us
  local copies, waits for them, and re-layouts: 5.2 us -> 3.83 us
  starting transfers between devices: 16.4 us -> 15.3 us
    ppermute x8 -> x6, waiting for transfers between devices: 13.3 us -> 8.11 us  [spread(): other = lax.ppermute(cur, 'cent', [(i, i ^ bit) for i in range(n_c)])]
    ppermute x3, waiting for transfers between devices: 6.52 us -> 2.28 us  [shards_all(): lax.ppermute(mine, 'outer', [(i, (i + sz) % n_o) for i in range(n_o)])]
    dynamic_update_slice x4, other arithmetic: 0.39 us -> 3.35 us  [shards_all(): lax.dynamic_update_slice_in_dim(cur, parts[sz], (z - sz) % n_o * n_d, axi...]
    another operation x1 -> x3, other arithmetic: 0.08 us -> 3.03 us  [the longest x2 2.36 us: shards_all(): parts[0] = jnp.stack(own_blocks)]
    ppermute x4 -> x3, starting transfers between devices: 5.27 us -> 2.6 us  [pair_of(): lax.ppermute(piece, 'dp', [(j, (j + sy) % n_d) for j in range(n_d)])]
    unnamed x22 -> x12, local copies, waits for them, and re-layouts: 4.2 us -> 2.01 us
    ppermute x4 -> x3, waiting for transfers between devices: 2.29 us -> 3.9 us  [pair_of(): lax.ppermute(piece, 'dp', [(j, (j + sy) % n_d) for j in range(n_d)])]
    ppermute x0 -> x2, starting transfers between devices: none -> 1.52 us  [the longest x1 1.52 us: shards_all(): got = lax.ppermute(my_half, 'dp', [(j, (j + sy) % n_d) for j in range(n_d)])]
  transfers between devices with their start and end apart: 15 -> 14, of which waited for: 7 -> 6; matrix products, arithmetic and copies ran while one was open for 5% -> 16% of each run, Pallas kernels for 0% -> 0%
where the time goes in v12:
time: 71.9 us; the launch traced here: 71.5 us
  other arithmetic  20 us (28%)
  starting transfers between devices  15.3 us (21%)
  waiting for transfers between devices  14.3 us (20%)
  blocking collectives  9.32 us (13%)
  matrix products  8.3 us (12%)
  local copies, waits for them, and re-layouts  3.83 us (5%)
    all_gather x1, blocking collectives, shards_all(): every = lax.all_gather(both, ('dp', 'cent'), axis=0)  9.32 us
    ppermute x6, waiting for transfers between devices, spread(): other = lax.ppermute(cur, 'cent', [(i, i ^ bit) for i in range(n_c)])  8.11 us
    ppermute x3, starting transfers between devices, shards_all(): lax.ppermute(mine, 'outer', [(i, (i + sz) % n_o) for i in range(n_o)])  7.01 us
    dot_general x1, matrix products, scores_for(): lax.dot_general(piece, cent_bf, (((1,), (1,)), ((), ())), preferred_eleme...  4.61 us
    ppermute x6, starting transfers between devices, spread(): other = lax.ppermute(cur, 'cent', [(i, i ^ bit) for i in range(n_c)])  4.19 us
    ppermute x3, waiting for transfers between devices, pair_of(): lax.ppermute(piece, 'dp', [(j, (j + sy) % n_d) for j in range(n_d)])  3.9 us
    dot_general x1, matrix products, shards_all(): lax.dot_general(scaled.reshape(n_o * pod, k), everything, (((0,), (0,)),...  3.68 us
    dynamic_update_slice x4, other arithmetic, shards_all(): lax.dynamic_update_slice_in_dim(cur, parts[sz], (z - sz) % n_o * n_d, axi...  3.35 us
  transfers between devices with their start and end apart: 14, of which 6 were waited for; matrix products, arithmetic and copies ran while one was open for 16% of the time, Pallas kernels for 0%

profile of v12, /device:TPU:0, one launch (start us, length us, event | category | flops | bytes accessed | tf_op | source)
XLA Modules:
  0.0 71.5 jit_solution(11379985991794514789)
XLA Ops:
  0.0 1.4 %convert_element_type.22 = bf16[256,1024]{1,0:T(8,128)(2,1)S(1)} convert(f32[256,1024]{1,0:T(8,128)} %param.3) | non-fusion elementwise | flops 262144 | bytes 1572864 | tf_op jit(solution)/shard_map/convert_element_type | solution.py:56
  1.5 3.1 %collective-permute-start.2 = (bf16[64,1024]{1,0:T(8,128)(2,1)S(1)}, bf16[64,1024]{1,0:T(8,128)(2,1)S(1)}, u32[]{:S(2)}, u32[]{:S(2)}) collective-permute-start(bf16[64,1024]{1,0:T(8,128)(2,1)S(1)} %constant_dynamic-slice_fusion), channel_id=1, source_target_pairs={{0,8},{8,16},{16,24},{24,0},{1,9},{9,17},{17,25},{25,1},{2,10},{10... | collective-permute-start | bytes 393224 | tf_op jit(solution)/shard_map/ppermute | solution.py:85
  4.6 2.6 %collective-permute-start.6 = (bf16[64,1024]{1,0:T(8,128)(2,1)S(1)}, bf16[64,1024]{1,0:T(8,128)(2,1)S(1)}, u32[]{:S(2)}, u32[]{:S(2)}) collective-permute-start(bf16[64,1024]{1,0:T(8,128)(2,1)S(1)} %constant_dynamic-slice_fusion), channel_id=1, source_target_pairs={{0,16},{8,24},{16,0},{24,8},{1,17},{9,25},{17,1},{25,9},{2,18},{10... | collective-permute-start | bytes 393224 | tf_op jit(solution)/shard_map/ppermute | solution.py:85
  7.1 1.3 %collective-permute-start.10 = (bf16[64,1024]{1,0:T(8,128)(2,1)S(1)}, bf16[64,1024]{1,0:T(8,128)(2,1)S(1)}, u32[]{:S(2)}, u32[]{:S(2)}) collective-permute-start(bf16[64,1024]{1,0:T(8,128)(2,1)S(1)} %constant_dynamic-slice_fusion), channel_id=1, source_target_pairs={{0,24},{8,0},{16,8},{24,16},{1,25},{9,1},{17,9},{25,17},{2,26},{10... | collective-permute-start | bytes 393224 | tf_op jit(solution)/shard_map/ppermute | solution.py:85
  8.5 0.7 %constant_dynamic-slice_fusion.1 = bf16[128,1024]{1,0:T(8,128)(2,1)} fusion(bf16[256,1024]{1,0:T(8,128)(2,1)S(1)} %convert_element_type.22, s32[]{:T(128)S(6)} %select_n.143), kind=kLoop, calls=%fused_computation.49 | loop fusion | bytes 524292 | tf_op jit(solution)/shard_map/dynamic_slice | solution.py:90
  9.2 1.5 %collective-permute-start = (bf16[128,1024]{1,0:T(8,128)(2,1)}, bf16[128,1024]{1,0:T(8,128)(2,1)}, u32[]{:S(2)}, u32[]{:S(2)}) collective-permute-start(bf16[128,1024]{1,0:T(8,128)(2,1)} %constant_dynamic-slice_fusion.1), channel_id=1, source_target_pairs={{0,4},{4,0},{1,5},{5,1},{2,6},{6,2},{3,7},{7,3},{8,12},{12,8},{9,1... | collective-permute-start | bytes 786440 | tf_op jit(solution)/shard_map/ppermute | solution.py:93
  10.7 1.3 %convert_bitcast_fusion = bf16[1,256,1024]{2,1,0:T(8,128)(2,1)S(1)} fusion(f32[256,1024]{1,0:T(8,128)} %param.3), kind=kLoop, calls=%fused_computation.74 | loop fusion | flops 262144 | bytes 1572864 | tf_op jit(solution)/shard_map/stack | solution.py:96
  12.1 0.7 fusion.17
  12.8 0.1 copy.27
  12.9 0.1 stack.128
  12.9 0.0 collective-permute-done.2
  12.9 0.6 collective-permute-start.3
  13.5 2.3 %collective-permute-done.6 = bf16[64,1024]{1,0:T(8,128)(2,1)S(1)} collective-permute-done((bf16[64,1024]{1,0:T(8,128)(2,1)S(1)}, bf16[64,1024]{1,0:T(8,128)(2,1)S(1)}, u32[]{:S(2)}, u32[]{:S(2)}) %collective-permute-start.6) | collective-permute-done | bytes 131104 | tf_op jit(solution)/shard_map/ppermute | solution.py:85
  15.8 1.5 %collective-permute-start.7 = (bf16[64,1024]{1,0:T(8,128)(2,1)S(1)}, bf16[64,1024]{1,0:T(8,128)(2,1)S(1)}, u32[]{:S(2)}, u32[]{:S(2)}) collective-permute-start(bf16[64,1024]{1,0:T(8,128)(2,1)S(1)} %collective-permute-done.6), channel_id=1, source_target_pairs={{0,4},{4,0},{1,5},{5,1},{2,6},{6,2},{3,7},{7,3},{8,12},{12,8},{9,1... | collective-permute-start | bytes 393224 | tf_op jit(solution)/shard_map/ppermute | solution.py:74
  17.3 0.0 collective-permute-done.10
  17.3 0.5 collective-permute-start.11
  17.8 2.7 %collective-permute-done.3 = bf16[64,1024]{1,0:T(8,128)(2,1)S(1)} collective-permute-done((bf16[64,1024]{1,0:T(8,128)(2,1)S(1)}, bf16[64,1024]{1,0:T(8,128)(2,1)S(1)}, u32[]{:S(2)}, u32[]{:S(2)}) %collective-permute-start.3) | collective-permute-done | bytes 131104 | tf_op jit(solution)/shard_map/ppermute | solution.py:74
  20.5 1.6 %collective-permute-start.4 = (bf16[2,64,1024]{2,1,0:T(8,128)(2,1)S(1)}, bf16[2,64,1024]{2,1,0:T(8,128)(2,1)S(1)}, u32[]{:S(2)}, u32[]{:S(2)}) collective-permute-start(bf16[2,64,1024]{2,1,0:T(8,128)(2,1)S(1)} %pad_maximum_fusion.3), channel_id=1, source_target_pairs={{0,2},{1,3},{2,0},{3,1},{4,6},{5,7},{6,4},{7,5},{8,10},{9,11},{10,... | collective-permute-start | bytes 786440 | tf_op jit(solution)/shard_map/ppermute | solution.py:79
  22.1 1.2 %collective-permute-done.7 = bf16[64,1024]{1,0:T(8,128)(2,1)S(1)} collective-permute-done((bf16[64,1024]{1,0:T(8,128)(2,1)S(1)}, bf16[64,1024]{1,0:T(8,128)(2,1)S(1)}, u32[]{:S(2)}, u32[]{:S(2)}) %collective-permute-start.7) | collective-permute-done | bytes 131104 | tf_op jit(solution)/shard_map/ppermute | solution.py:74
  23.3 0.7 %pad_maximum_fusion.4 = bf16[2,64,1024]{2,1,0:T(8,128)(2,1)} fusion(bf16[1,64,1024]{2,1,0:T(8,128)(2,1)S(1)} %bitcast.84, bf16[1,64,1024]{2,1,0:T(8,128)(2,1)S(1)} %bitcast.75), kind=kLoop, calls=%fused_computation.19 | loop fusion | flops 131072 | bytes 524288 | tf_op jit(solution)/shard_map/stack | solution.py:75
  24.1 1.5 %collective-permute-start.8 = (bf16[2,64,1024]{2,1,0:T(8,128)(2,1)}, bf16[2,64,1024]{2,1,0:T(8,128)(2,1)}, u32[]{:S(2)}, u32[]{:S(2)}) collective-permute-start(bf16[2,64,1024]{2,1,0:T(8,128)(2,1)} %pad_maximum_fusion.4), channel_id=1, source_target_pairs={{0,2},{1,3},{2,0},{3,1},{4,6},{5,7},{6,4},{7,5},{8,10},{9,11},{10,... | collective-permute-start | bytes 786440 | tf_op jit(solution)/shard_map/ppermute | solution.py:79
  25.5 0.0 collective-permute-done.11
  25.6 0.8 %pad_maximum_fusion.5 = bf16[2,64,1024]{2,1,0:T(8,128)(2,1)} fusion(bf16[1,64,1024]{2,1,0:T(8,128)(2,1)S(1)} %bitcast.81, bf16[1,64,1024]{2,1,0:T(8,128)(2,1)S(1)} %bitcast.72), kind=kLoop, calls=%fused_computation.20 | loop fusion | flops 131072 | bytes 524288 | tf_op jit(solution)/shard_map/stack | solution.py:75
  26.3 1.0 %collective-permute-start.12 = (bf16[2,64,1024]{2,1,0:T(8,128)(2,1)}, bf16[2,64,1024]{2,1,0:T(8,128)(2,1)}, u32[]{:S(2)}, u32[]{:S(2)}) collective-permute-start(bf16[2,64,1024]{2,1,0:T(8,128)(2,1)} %pad_maximum_fusion.5), channel_id=1, source_target_pairs={{0,2},{1,3},{2,0},{3,1},{4,6},{5,7},{6,4},{7,5},{8,10},{9,11},{10,... | collective-permute-start | bytes 786440 | tf_op jit(solution)/shard_map/ppermute | solution.py:79
  27.3 0.0 collective-permute-done
  27.3 0.0 collective-permute-start.1
  27.3 1.8 %collective-permute-done.4 = bf16[2,64,1024]{2,1,0:T(8,128)(2,1)S(1)} collective-permute-done((bf16[2,64,1024]{2,1,0:T(8,128)(2,1)S(1)}, bf16[2,64,1024]{2,1,0:T(8,128)(2,1)S(1)}, u32[]{:S(2)}, u32[]{:S(2)}) %collective-permute-start.4) | collective-permute-done | bytes 262176 | tf_op jit(solution)/shard_map/ppermute | solution.py:79
  29.2 0.7 copy-done.4
  29.9 0.8 %pad_maximum_fusion = bf16[2,128,1024]{2,1,0:T(8,128)(2,1)} fusion(bf16[2,64,1024]{2,1,0:T(8,128)(2,1)S(1)} %collective-permute-done.4, bf16[1,64,1024]{2,1,0:T(8,128)(2,1)S(1)} %bitcast.88, bf16[1,64,1024]{2,1,0:T(8,128)(2,1)S(1)} %bitcast.79), kind=kLoop, calls=%fused_computation.15 | loop fusion | flops 1572864 | bytes 1048576 | tf_op jit(solution)/shard_map/concatenate | solution.py:80
  30.7 0.0 collective-permute-start.5
  30.7 0.2 multiply_reduce_fusion
  31.0 3.9 %collective-permute-done.8 = bf16[2,64,1024]{2,1,0:T(8,128)(2,1)} collective-permute-done((bf16[2,64,1024]{2,1,0:T(8,128)(2,1)}, bf16[2,64,1024]{2,1,0:T(8,128)(2,1)}, u32[]{:S(2)}, u32[]{:S(2)}) %collective-permute-start.8) | collective-permute-done | bytes 262176 | tf_op jit(solution)/shard_map/ppermute | solution.py:79
  34.9 1.0 %pad_maximum_fusion.1 = bf16[2,128,1024]{2,1,0:T(8,128)(2,1)S(1)} fusion(bf16[2,64,1024]{2,1,0:T(8,128)(2,1)} %collective-permute-done.8, bf16[1,64,1024]{2,1,0:T(8,128)(2,1)S(1)} %bitcast.85, bf16[1,64,1024]{2,1,0:T(8,128)(2,1)S(1)} %bitcast.76), kind=kLoop, calls=%fused_computation.16 | loop fusion | flops 1572864 | bytes 1048576 | tf_op jit(solution)/shard_map/concatenate | solution.py:80
  35.9 0.0 copy-start.5
  35.9 0.1 collective-permute-start.9
  36.0 2.4 %collective-permute-done.12 = bf16[2,64,1024]{2,1,0:T(8,128)(2,1)} collective-permute-done((bf16[2,64,1024]{2,1,0:T(8,128)(2,1)}, bf16[2,64,1024]{2,1,0:T(8,128)(2,1)}, u32[]{:S(2)}, u32[]{:S(2)}) %collective-permute-start.12) | collective-permute-done | bytes 262176 | tf_op jit(solution)/shard_map/ppermute | solution.py:79
  38.3 1.0 %pad_maximum_fusion.2 = bf16[2,128,1024]{2,1,0:T(8,128)(2,1)S(1)} fusion(bf16[2,64,1024]{2,1,0:T(8,128)(2,1)} %collective-permute-done.12, bf16[1,64,1024]{2,1,0:T(8,128)(2,1)S(1)} %bitcast.82, bf16[1,64,1024]{2,1,0:T(8,128)(2,1)S(1)} %bitcast.73), kind=kLoop, calls=%fused_computation.17 | loop fusion | flops 1572864 | bytes 1048576 | tf_op jit(solution)/shard_map/concatenate | solution.py:80
  39.3 0.1 collective-permute-start.13
  39.4 0.0 collective-permute-done.1
  39.4 1.1 %maximum_bitcast_fusion = bf16[1,256,1024]{2,1,0:T(8,128)(2,1)S(1)} fusion(bf16[128,1024]{1,0:T(8,128)(2,1)} %collective-permute-done.1, bf16[128,1024]{1,0:T(8,128)(2,1)} %collective-permute-done), kind=kLoop, calls=%fused_computation.14 | loop fusion | flops 1048576 | bytes 1048576 | tf_op jit(solution)/shard_map/stack | solution.py:96
  40.5 0.5 broadcast_in_dim.138
  41.0 0.1 maximum_dynamic-update-slice_fusion
  41.1 0.0 collective-permute-done.5
  41.1 1.1 %maximum_dynamic-update-slice_fusion.1 = bf16[8,256,1024]{2,1,0:T(8,128)(2,1)S(1)} fusion(bf16[8,256,1024]{2,1,0:T(8,128)(2,1)S(1)} %maximum_dynamic-update-slice_fusion, s32[]{:T(128)S(6)} %select_n.148, bf16[2,128,1024]{2,1,0:T(8,128)(2,1)} %collective-permute-done.5, bf16[2,64,1024]{2,1,0:T(8,128)(2,1)S(1)} %copy-done.5, ...), kind=kLoop, calls=%fused_computation.10 | loop fusion | flops 4194304 | bytes 2097156 | tf_op jit(solution)/shard_map/dynamic_update_slice | solution.py:100
  42.3 0.0 collective-permute-done.9
  42.3 1.1 %maximum_dynamic-update-slice_fusion.2 = bf16[8,256,1024]{2,1,0:T(8,128)(2,1)S(1)} fusion(bf16[8,256,1024]{2,1,0:T(8,128)(2,1)S(1)} %maximum_dynamic-update-slice_fusion.1, s32[]{:T(128)S(6)} %select_n.150, bf16[2,128,1024]{2,1,0:T(8,128)(2,1)S(1)} %collective-permute-done.9, bf16[2,64,1024]{2,1,0:T(8,128)(2,1)} %collective-permute-done.8, ...), kind=kLoop, calls=%fused_computation.11 | loop fusion | flops 4194304 | bytes 2097156 | tf_op jit(solution)/shard_map/dynamic_update_slice | solution.py:100
  43.3 0.0 collective-permute-done.13
  43.3 1.1 %maximum_dynamic-update-slice_fusion.3 = bf16[8,256,1024]{2,1,0:T(8,128)(2,1)S(1)} fusion(bf16[8,256,1024]{2,1,0:T(8,128)(2,1)S(1)} %maximum_dynamic-update-slice_fusion.2, s32[]{:T(128)S(6)} %select_n.152, bf16[2,128,1024]{2,1,0:T(8,128)(2,1)S(1)} %collective-permute-done.13, bf16[2,64,1024]{2,1,0:T(8,128)(2,1)} %collective-permute-done.12, ...), kind=kLoop, calls=%fused_computation.12 | loop fusion | flops 4194304 | bytes 2097156 | tf_op jit(solution)/shard_map/dynamic_update_slice | solution.py:100
  44.4 4.6 %fusion.21 = (f32[2048]{0:T(1024)S(1)}, f32[2048,512]{1,0:T(8,128)}) fusion(f32[512]{0:T(512)S(1)} %multiply_reduce_fusion, bf16[2048,1024]{1,0:T(8,128)(2,1)S(1)} %bitcast.68, f32[512,1024]{1,0:T(8,128)S(1)} %copy-done.3), kind=kOutput, calls=%fused_computation.73 | convolution fusion | flops 2152200192 | bytes 10496000 | tf_op jit(solution)/shard_map/dot_general | solution.py:10
  49.0 0.1 broadcast_in_dim.141
  49.1 3.3 %exponential_reduce_fusion = f32[2048]{0:T(1024)S(1)} fusion(f32[2048,512]{1,0:T(8,128)} %get-tuple-element.26, f32[2048]{0:T(1024)S(1)} %get-tuple-element.25), kind=kLoop, calls=%fused_computation.4 | loop fusion | flops 2095104 | bytes 4210688 | tf_op jit(solution)/shard_map/reduce_sum | solution.py:18
  52.4 0.1 broadcast_in_dim.146
  52.5 0.1 select_reduce_fusion.7
  52.6 0.2 select_reduce_fusion.3
  52.8 9.3 %all-gather = f32[16,8,4,64]{3,1,2,0:T(8,128)S(1)} all-gather(f32[2,8,4,64]{3,1,2,0:T(8,128)S(1)} %copy.30), channel_id=2, replica_groups=mesh['outer'=4,'dp'=2,'cent'=4] {'dp','cent'}, dimensions={0}, use_global_device_ids=true | all-gather | bytes 147456 | tf_op jit(solution)/shard_map/all_gather | solution.py:130
  62.2 0.1 select_reduce_fusion.1
  62.3 0.1 select_reduce_fusion.5
  62.5 0.1 div.62
  62.5 0.1 sub.65
  62.6 2.8 %bitcast_reduce_fusion = f32[4,512]{1,0:T(4,128)S(1)} fusion(f32[2048]{0:T(1024)S(1)} %div.62, f32[2048,512]{1,0:T(8,128)} %get-tuple-element.26, f32[2048]{0:T(1024)S(1)} %sub.65), kind=kLoop, calls=%fused_computation.2 | loop fusion | flops 5240832 | bytes 4218880 | tf_op jit(solution)/shard_map/reduce_sum | solution.py:141
  65.5 0.6 copy-done
  66.1 1.0 %fusion = bf16[2048,512]{1,0:T(8,128)(2,1)S(1)} fusion(f32[4,512]{1,0:T(4,128)S(1)} %broadcast_add_fusion, f32[2048]{0:T(1024)S(1)} %div.62, f32[2048,512]{1,0:T(8,128)S(1)} %copy-done, f32[2048]{0:T(1024)S(1)} %sub.65), kind=kLoop, calls=%fused_computation.1 | loop fusion | flops 6291456 | bytes 6316032 | tf_op jit(solution)/shard_map/convert_element_type | solution.py:142
  67.1 0.7 %copy-done.2 = bf16[8,256,1024]{2,1,0:T(8,128)(2,1)S(1)} copy-done((bf16[8,256,1024]{2,1,0:T(8,128)(2,1)S(1)}, bf16[8,256,1024]{2,1,0:T(8,128)(2,1)}, u32[]{:S(2)}) %copy-start.2) | copy-done | bytes 4194328
  67.8 3.7 %subtract_multiply_fusion.1 = f32[512,1024]{1,0:T(8,128)} fusion(f32[512,1024]{1,0:T(8,128)S(1)} %copy-done.3, bf16[2048,512]{1,0:T(8,128)(2,1)S(1)} %fusion, bf16[2048,1024]{1,0:T(8,128)(2,1)S(1)} %bitcast.69, f32[512]{0:T(512)S(1)} %fusion.8), kind=kOutput, calls=%fused_computation.7 | convolution fusion | flops 2149056512 | bytes 10487808 | tf_op jit(solution)/shard_map/dot_general | solution.py:143
  (26 shorter events, 0.2 us)
Async XLA Ops:
  0.0 30.7 %copy-start.3 = (f32[512,1024]{1,0:T(8,128)S(1)}, f32[512,1024]{1,0:T(8,128)}, u32[]{:S(2)}) copy-start(f32[512,1024]{1,0:T(8,128)} %param.4) | copy-start | bytes 6291460
  1.5 11.5 %collective-permute-start.2 = (bf16[64,1024]{1,0:T(8,128)(2,1)S(1)}, bf16[64,1024]{1,0:T(8,128)(2,1)S(1)}, u32[]{:S(2)}, u32[]{:S(2)}) collective-permute-start(bf16[64,1024]{1,0:T(8,128)(2,1)S(1)} %constant_dynamic-slice_fusion), channel_id=1, source_target_pairs={{0,8},{8,16},{16,24},{24,0},{1,9},{9,17},{17,25},{25,1},{2,10},{10... | collective-permute-start | bytes 393224 | tf_op jit(solution)/shard_map/ppermute | solution.py:85
  4.6 11.2 %collective-permute-start.6 = (bf16[64,1024]{1,0:T(8,128)(2,1)S(1)}, bf16[64,1024]{1,0:T(8,128)(2,1)S(1)}, u32[]{:S(2)}, u32[]{:S(2)}) collective-permute-start(bf16[64,1024]{1,0:T(8,128)(2,1)S(1)} %constant_dynamic-slice_fusion), channel_id=1, source_target_pairs={{0,16},{8,24},{16,0},{24,8},{1,17},{9,25},{17,1},{25,9},{2,18},{10... | collective-permute-start | bytes 393224 | tf_op jit(solution)/shard_map/ppermute | solution.py:85
  7.1 10.2 %collective-permute-start.10 = (bf16[64,1024]{1,0:T(8,128)(2,1)S(1)}, bf16[64,1024]{1,0:T(8,128)(2,1)S(1)}, u32[]{:S(2)}, u32[]{:S(2)}) collective-permute-start(bf16[64,1024]{1,0:T(8,128)(2,1)S(1)} %constant_dynamic-slice_fusion), channel_id=1, source_target_pairs={{0,24},{8,0},{16,8},{24,16},{1,25},{9,1},{17,9},{25,17},{2,26},{10... | collective-permute-start | bytes 393224 | tf_op jit(solution)/shard_map/ppermute | solution.py:85
  9.2 18.1 %collective-permute-start = (bf16[128,1024]{1,0:T(8,128)(2,1)}, bf16[128,1024]{1,0:T(8,128)(2,1)}, u32[]{:S(2)}, u32[]{:S(2)}) collective-permute-start(bf16[128,1024]{1,0:T(8,128)(2,1)} %constant_dynamic-slice_fusion.1), channel_id=1, source_target_pairs={{0,4},{4,0},{1,5},{5,1},{2,6},{6,2},{3,7},{7,3},{8,12},{12,8},{9,1... | collective-permute-start | bytes 786440 | tf_op jit(solution)/shard_map/ppermute | solution.py:93
  12.9 7.6 %collective-permute-start.3 = (bf16[64,1024]{1,0:T(8,128)(2,1)S(1)}, bf16[64,1024]{1,0:T(8,128)(2,1)S(1)}, u32[]{:S(2)}, u32[]{:S(2)}) collective-permute-start(bf16[64,1024]{1,0:T(8,128)(2,1)S(1)} %collective-permute-done.2), channel_id=1, source_target_pairs={{0,4},{4,0},{1,5},{5,1},{2,6},{6,2},{3,7},{7,3},{8,12},{12,8},{9,1... | collective-permute-start | bytes 393224 | tf_op jit(solution)/shard_map/ppermute | solution.py:74
  15.8 7.5 %collective-permute-start.7 = (bf16[64,1024]{1,0:T(8,128)(2,1)S(1)}, bf16[64,1024]{1,0:T(8,128)(2,1)S(1)}, u32[]{:S(2)}, u32[]{:S(2)}) collective-permute-start(bf16[64,1024]{1,0:T(8,128)(2,1)S(1)} %collective-permute-done.6), channel_id=1, source_target_pairs={{0,4},{4,0},{1,5},{5,1},{2,6},{6,2},{3,7},{7,3},{8,12},{12,8},{9,1... | collective-permute-start | bytes 393224 | tf_op jit(solution)/shard_map/ppermute | solution.py:74
  17.3 8.2 %collective-permute-start.11 = (bf16[64,1024]{1,0:T(8,128)(2,1)S(1)}, bf16[64,1024]{1,0:T(8,128)(2,1)S(1)}, u32[]{:S(2)}, u32[]{:S(2)}) collective-permute-start(bf16[64,1024]{1,0:T(8,128)(2,1)S(1)} %collective-permute-done.10), channel_id=1, source_target_pairs={{0,4},{4,0},{1,5},{5,1},{2,6},{6,2},{3,7},{7,3},{8,12},{12,8},{9,1... | collective-permute-start | bytes 393224 | tf_op jit(solution)/shard_map/ppermute | solution.py:74
  20.5 8.6 %collective-permute-start.4 = (bf16[2,64,1024]{2,1,0:T(8,128)(2,1)S(1)}, bf16[2,64,1024]{2,1,0:T(8,128)(2,1)S(1)}, u32[]{:S(2)}, u32[]{:S(2)}) collective-permute-start(bf16[2,64,1024]{2,1,0:T(8,128)(2,1)S(1)} %pad_maximum_fusion.3), channel_id=1, source_target_pairs={{0,2},{1,3},{2,0},{3,1},{4,6},{5,7},{6,4},{7,5},{8,10},{9,11},{10,... | collective-permute-start | bytes 786440 | tf_op jit(solution)/shard_map/ppermute | solution.py:79
  24.1 10.8 %collective-permute-start.8 = (bf16[2,64,1024]{2,1,0:T(8,128)(2,1)}, bf16[2,64,1024]{2,1,0:T(8,128)(2,1)}, u32[]{:S(2)}, u32[]{:S(2)}) collective-permute-start(bf16[2,64,1024]{2,1,0:T(8,128)(2,1)} %pad_maximum_fusion.4), channel_id=1, source_target_pairs={{0,2},{1,3},{2,0},{3,1},{4,6},{5,7},{6,4},{7,5},{8,10},{9,11},{10,... | collective-permute-start | bytes 786440 | tf_op jit(solution)/shard_map/ppermute | solution.py:79
  26.3 12.0 %collective-permute-start.12 = (bf16[2,64,1024]{2,1,0:T(8,128)(2,1)}, bf16[2,64,1024]{2,1,0:T(8,128)(2,1)}, u32[]{:S(2)}, u32[]{:S(2)}) collective-permute-start(bf16[2,64,1024]{2,1,0:T(8,128)(2,1)} %pad_maximum_fusion.5), channel_id=1, source_target_pairs={{0,2},{1,3},{2,0},{3,1},{4,6},{5,7},{6,4},{7,5},{8,10},{9,11},{10,... | collective-permute-start | bytes 786440 | tf_op jit(solution)/shard_map/ppermute | solution.py:79
  27.3 12.1 %collective-permute-start.1 = (bf16[128,1024]{1,0:T(8,128)(2,1)}, bf16[128,1024]{1,0:T(8,128)(2,1)}, u32[]{:S(2)}, u32[]{:S(2)}) collective-permute-start(bf16[128,1024]{1,0:T(8,128)(2,1)} %collective-permute-done), channel_id=1, source_target_pairs={{0,1},{1,0},{2,3},{3,2},{4,5},{5,4},{6,7},{7,6},{8,9},{9,8},{10,11... | collective-permute-start | bytes 786440 | tf_op jit(solution)/shard_map/ppermute | solution.py:94
  29.2 0.7 copy-start.4
  30.7 10.4 %collective-permute-start.5 = (bf16[2,128,1024]{2,1,0:T(8,128)(2,1)}, bf16[2,128,1024]{2,1,0:T(8,128)(2,1)}, u32[]{:S(2)}, u32[]{:S(2)}) collective-permute-start(bf16[2,128,1024]{2,1,0:T(8,128)(2,1)} %pad_maximum_fusion), channel_id=1, source_target_pairs={{0,1},{1,0},{2,3},{3,2},{4,5},{5,4},{6,7},{7,6},{8,9},{9,8},{10,11... | collective-permute-start | bytes 1572872 | tf_op jit(solution)/shard_map/ppermute | solution.py:79
  35.9 5.2 %copy-start.5 = (bf16[2,64,1024]{2,1,0:T(8,128)(2,1)S(1)}, bf16[2,64,1024]{2,1,0:T(8,128)(2,1)}, u32[]{:S(2)}) copy-start(bf16[2,64,1024]{2,1,0:T(8,128)(2,1)} %copy-done.4) | copy-start | bytes 786436
  35.9 6.4 %collective-permute-start.9 = (bf16[2,128,1024]{2,1,0:T(8,128)(2,1)S(1)}, bf16[2,128,1024]{2,1,0:T(8,128)(2,1)S(1)}, u32[]{:S(2)}, u32[]{:S(2)}) collective-permute-start(bf16[2,128,1024]{2,1,0:T(8,128)(2,1)S(1)} %pad_maximum_fusion.1), channel_id=1, source_target_pairs={{0,1},{1,0},{2,3},{3,2},{4,5},{5,4},{6,7},{7,6},{8,9},{9,8},{10,11... | collective-permute-start | bytes 1572872 | tf_op jit(solution)/shard_map/ppermute | solution.py:79
  39.3 4.0 %collective-permute-start.13 = (bf16[2,128,1024]{2,1,0:T(8,128)(2,1)S(1)}, bf16[2,128,1024]{2,1,0:T(8,128)(2,1)S(1)}, u32[]{:S(2)}, u32[]{:S(2)}) collective-permute-start(bf16[2,128,1024]{2,1,0:T(8,128)(2,1)S(1)} %pad_maximum_fusion.2), channel_id=1, source_target_pairs={{0,1},{1,0},{2,3},{3,2},{4,5},{5,4},{6,7},{7,6},{8,9},{9,8},{10,11... | collective-permute-start | bytes 1572872 | tf_op jit(solution)/shard_map/ppermute | solution.py:79
  44.4 4.6 %copy-start.1 = (bf16[8,256,1024]{2,1,0:T(8,128)(2,1)}, bf16[8,256,1024]{2,1,0:T(8,128)(2,1)S(1)}, u32[]{:S(2)}) copy-start(bf16[8,256,1024]{2,1,0:T(8,128)(2,1)S(1)} %maximum_dynamic-update-slice_fusion.3) | copy-start | bytes 12582916
  62.6 3.4 %copy-start = (f32[2048,512]{1,0:T(8,128)S(1)}, f32[2048,512]{1,0:T(8,128)}, u32[]{:S(2)}) copy-start(f32[2048,512]{1,0:T(8,128)} %get-tuple-element.26) | copy-start | bytes 12582916
  65.5 2.3 %copy-start.2 = (bf16[8,256,1024]{2,1,0:T(8,128)(2,1)S(1)}, bf16[8,256,1024]{2,1,0:T(8,128)(2,1)}, u32[]{:S(2)}) copy-start(bf16[8,256,1024]{2,1,0:T(8,128)(2,1)} %copy-done.1) | copy-start | bytes 12582916

commit v13 on v12

--- a/solution.py
+++ b/solution.py
@@ -66,7 +66,7 @@
     for bit in reversed(bits):
         xs = xs + [x ^ bit for x in xs]
 
-    mine = lax.dynamic_slice_in_dim(rows_bf, q * tq, tq, 0)
+    mine = lax.dynamic_slice_in_dim(rows, q * tq, tq, 0).astype(jnp.bfloat16)
     shifts = list(itertools.product(range(n_o), range(n_d)))
     def pair_of(piece):
         across = [piece]
@@ -87,7 +87,7 @@
 
     h = q % 2
     half = t // 2
-    my_half = lax.dynamic_slice_in_dim(rows_bf, h * half, half, 0)
+    my_half = lax.dynamic_slice_in_dim(rows, h * half, half, 0).astype(jnp.bfloat16)
     own_blocks = [rows_bf]
     for sy in range(1, n_d):
         got = lax.ppermute(my_half, "dp", [(j, (j + sy) % n_d) for j in range(n_d)])

time: 71.9 us -> 72.4 us (level)
  local copies, waits for them, and re-layouts: 3.83 us -> 5.98 us
  other arithmetic: 20 us -> 18.6 us
    convert_element_type x0 -> x2, local copies, waits for them, and re-layouts: none -> 2.89 us  [the longest x1 1.78 us: shards_all(): lax.dynamic_slice_in_dim(rows, h * half, half, 0).astype(jnp.bfloat16)]
    convert_element_type x1 -> x0, other arithmetic: 1.44 us -> none  [shards_all(): rows_bf = rows.astype(jnp.bfloat16)]
    ppermute x3, waiting for transfers between devices: 3.9 us -> 5.3 us  [pair_of(): lax.ppermute(piece, 'dp', [(j, (j + sy) % n_d) for j in range(n_d)])]
    ppermute x3, waiting for transfers between devices: 2.28 us -> 1.22 us  [shards_all(): lax.ppermute(mine, 'outer', [(i, (i + sz) % n_o) for i in range(n_o)])]
    dynamic_slice x2 -> x0, local copies, waits for them, and re-layouts: 0.74 us -> none  [the longest x1 0.72 us: shards_all(): my_half = lax.dynamic_slice_in_dim(rows_bf, h * half, half, 0)]
  transfers between devices with their start and end apart: 14 -> 14, of which waited for: 6 -> 6; matrix products, arithmetic and copies ran while one was open for 16% -> 17% of each run, Pallas kernels for 0% -> 0%
where the time goes in v13:
time: 72.4 us; the launch traced here: 71.9 us
  other arithmetic  18.6 us (26%)
  starting transfers between devices  15 us (21%)
  waiting for transfers between devices  14.3 us (20%)
  blocking collectives  9.32 us (13%)
  matrix products  8.28 us (11%)
  local copies, waits for them, and re-layouts  5.98 us (8%)
    all_gather x1, blocking collectives, shards_all(): every = lax.all_gather(both, ('dp', 'cent'), axis=0)  9.32 us
    ppermute x6, waiting for transfers between devices, spread(): other = lax.ppermute(cur, 'cent', [(i, i ^ bit) for i in range(n_c)])  7.81 us
    ppermute x3, starting transfers between devices, shards_all(): lax.ppermute(mine, 'outer', [(i, (i + sz) % n_o) for i in range(n_o)])  7.01 us
    ppermute x3, waiting for transfers between devices, pair_of(): lax.ppermute(piece, 'dp', [(j, (j + sy) % n_d) for j in range(n_d)])  5.3 us
    dot_general x1, matrix products, scores_for(): lax.dot_general(piece, cent_bf, (((1,), (1,)), ((), ())), preferred_eleme...  4.62 us
    ppermute x6, starting transfers between devices, spread(): other = lax.ppermute(cur, 'cent', [(i, i ^ bit) for i in range(n_c)])  3.85 us
    dot_general x1, matrix products, shards_all(): lax.dot_general(scaled.reshape(n_o * pod, k), everything, (((0,), (0,)),...  3.67 us
    dynamic_update_slice x4, other arithmetic, shards_all(): lax.dynamic_update_slice_in_dim(cur, parts[sz], (z - sz) % n_o * n_d, axi...  3.35 us
  transfers between devices with their start and end apart: 14, of which 6 were waited for; matrix products, arithmetic and copies ran while one was open for 17% of the time, Pallas kernels for 0%

profile of v13, /device:TPU:0, one launch (start us, length us, event | category | flops | bytes accessed | tf_op | source)
XLA Modules:
  0.0 71.9 jit_solution(17284515493334154258)
XLA Ops:
  0.0 1.1 %dynamic-slice_convert_fusion.1 = bf16[64,1024]{1,0:T(8,128)(2,1)S(1)} fusion(f32[256,1024]{1,0:T(8,128)} %param.3, s32[]{:T(128)S(6)} %select_n.146), kind=kLoop, calls=%fused_computation.23 | loop fusion | bytes 262148 | tf_op jit(solution)/shard_map/convert_element_type | solution.py:69
  1.1 3.1 %collective-permute-start.2 = (bf16[64,1024]{1,0:T(8,128)(2,1)S(1)}, bf16[64,1024]{1,0:T(8,128)(2,1)S(1)}, u32[]{:S(2)}, u32[]{:S(2)}) collective-permute-start(bf16[64,1024]{1,0:T(8,128)(2,1)S(1)} %dynamic-slice_convert_fusion.1), channel_id=1, source_target_pairs={{0,8},{8,16},{16,24},{24,0},{1,9},{9,17},{17,25},{25,1},{2,10},{10... | collective-permute-start | bytes 393224 | tf_op jit(solution)/shard_map/ppermute | solution.py:85
  4.2 2.6 %collective-permute-start.6 = (bf16[64,1024]{1,0:T(8,128)(2,1)S(1)}, bf16[64,1024]{1,0:T(8,128)(2,1)S(1)}, u32[]{:S(2)}, u32[]{:S(2)}) collective-permute-start(bf16[64,1024]{1,0:T(8,128)(2,1)S(1)} %dynamic-slice_convert_fusion.1), channel_id=1, source_target_pairs={{0,16},{8,24},{16,0},{24,8},{1,17},{9,25},{17,1},{25,9},{2,18},{10... | collective-permute-start | bytes 393224 | tf_op jit(solution)/shard_map/ppermute | solution.py:85
  6.8 1.3 %collective-permute-start.10 = (bf16[64,1024]{1,0:T(8,128)(2,1)S(1)}, bf16[64,1024]{1,0:T(8,128)(2,1)S(1)}, u32[]{:S(2)}, u32[]{:S(2)}) collective-permute-start(bf16[64,1024]{1,0:T(8,128)(2,1)S(1)} %dynamic-slice_convert_fusion.1), channel_id=1, source_target_pairs={{0,24},{8,0},{16,8},{24,16},{1,25},{9,1},{17,9},{25,17},{2,26},{10... | collective-permute-start | bytes 393224 | tf_op jit(solution)/shard_map/ppermute | solution.py:85
  8.1 1.8 %dynamic-slice_convert_fusion = bf16[128,1024]{1,0:T(8,128)(2,1)} fusion(f32[256,1024]{1,0:T(8,128)} %param.3, s32[]{:T(128)S(6)} %select_n.143), kind=kLoop, calls=%fused_computation.18 | loop fusion | bytes 524292 | tf_op jit(solution)/shard_map/convert_element_type | solution.py:90
  9.9 1.5 %collective-permute-start = (bf16[128,1024]{1,0:T(8,128)(2,1)}, bf16[128,1024]{1,0:T(8,128)(2,1)}, u32[]{:S(2)}, u32[]{:S(2)}) collective-permute-start(bf16[128,1024]{1,0:T(8,128)(2,1)} %dynamic-slice_convert_fusion), channel_id=1, source_target_pairs={{0,4},{4,0},{1,5},{5,1},{2,6},{6,2},{3,7},{7,3},{8,12},{12,8},{9,1... | collective-permute-start | bytes 786440 | tf_op jit(solution)/shard_map/ppermute | solution.py:93
  11.4 1.3 %convert_bitcast_fusion = bf16[1,256,1024]{2,1,0:T(8,128)(2,1)S(1)} fusion(f32[256,1024]{1,0:T(8,128)} %param.3), kind=kLoop, calls=%fused_computation.19 | loop fusion | flops 262144 | bytes 1572864 | tf_op jit(solution)/shard_map/stack | solution.py:96
  12.8 0.7 fusion.17
  13.5 0.1 copy.27
  13.6 0.1 stack.128
  13.6 0.0 collective-permute-done.2
  13.6 0.6 collective-permute-start.3
  14.2 1.2 %collective-permute-done.6 = bf16[64,1024]{1,0:T(8,128)(2,1)S(1)} collective-permute-done((bf16[64,1024]{1,0:T(8,128)(2,1)S(1)}, bf16[64,1024]{1,0:T(8,128)(2,1)S(1)}, u32[]{:S(2)}, u32[]{:S(2)}) %collective-permute-start.6) | collective-permute-done | bytes 131104 | tf_op jit(solution)/shard_map/ppermute | solution.py:85
  15.4 1.5 %collective-permute-start.7 = (bf16[64,1024]{1,0:T(8,128)(2,1)S(1)}, bf16[64,1024]{1,0:T(8,128)(2,1)S(1)}, u32[]{:S(2)}, u32[]{:S(2)}) collective-permute-start(bf16[64,1024]{1,0:T(8,128)(2,1)S(1)} %collective-permute-done.6), channel_id=1, source_target_pairs={{0,4},{4,0},{1,5},{5,1},{2,6},{6,2},{3,7},{7,3},{8,12},{12,8},{9,1... | collective-permute-start | bytes 393224 | tf_op jit(solution)/shard_map/ppermute | solution.py:74
  16.9 0.0 collective-permute-done.10
  17.0 0.5 collective-permute-start.11
  17.5 4.7 %collective-permute-done.3 = bf16[64,1024]{1,0:T(8,128)(2,1)S(1)} collective-permute-done((bf16[64,1024]{1,0:T(8,128)(2,1)S(1)}, bf16[64,1024]{1,0:T(8,128)(2,1)S(1)}, u32[]{:S(2)}, u32[]{:S(2)}) %collective-permute-start.3) | collective-permute-done | bytes 131104 | tf_op jit(solution)/shard_map/ppermute | solution.py:74
  22.2 1.6 %collective-permute-start.4 = (bf16[2,64,1024]{2,1,0:T(8,128)(2,1)S(1)}, bf16[2,64,1024]{2,1,0:T(8,128)(2,1)S(1)}, u32[]{:S(2)}, u32[]{:S(2)}) collective-permute-start(bf16[2,64,1024]{2,1,0:T(8,128)(2,1)S(1)} %pad_maximum_fusion.3), channel_id=1, source_target_pairs={{0,2},{1,3},{2,0},{3,1},{4,6},{5,7},{6,4},{7,5},{8,10},{9,11},{10,... | collective-permute-start | bytes 786440 | tf_op jit(solution)/shard_map/ppermute | solution.py:79
  23.8 0.6 collective-permute-done.7
  24.4 0.7 %pad_maximum_fusion.4 = bf16[2,64,1024]{2,1,0:T(8,128)(2,1)} fusion(bf16[1,64,1024]{2,1,0:T(8,128)(2,1)S(1)} %bitcast.84, bf16[1,64,1024]{2,1,0:T(8,128)(2,1)S(1)} %bitcast.75), kind=kLoop, calls=%fused_computation.21 | loop fusion | flops 131072 | bytes 524288 | tf_op jit(solution)/shard_map/stack | solution.py:75
  25.1 1.5 %collective-permute-start.8 = (bf16[2,64,1024]{2,1,0:T(8,128)(2,1)}, bf16[2,64,1024]{2,1,0:T(8,128)(2,1)}, u32[]{:S(2)}, u32[]{:S(2)}) collective-permute-start(bf16[2,64,1024]{2,1,0:T(8,128)(2,1)} %pad_maximum_fusion.4), channel_id=1, source_target_pairs={{0,2},{1,3},{2,0},{3,1},{4,6},{5,7},{6,4},{7,5},{8,10},{9,11},{10,... | collective-permute-start | bytes 786440 | tf_op jit(solution)/shard_map/ppermute | solution.py:79
  26.6 0.0 collective-permute-done.11
  26.6 0.8 %pad_maximum_fusion.5 = bf16[2,64,1024]{2,1,0:T(8,128)(2,1)} fusion(bf16[1,64,1024]{2,1,0:T(8,128)(2,1)S(1)} %bitcast.81, bf16[1,64,1024]{2,1,0:T(8,128)(2,1)S(1)} %bitcast.72), kind=kLoop, calls=%fused_computation.22 | loop fusion | flops 131072 | bytes 524288 | tf_op jit(solution)/shard_map/stack | solution.py:75
  27.3 0.7 collective-permute-start.12
  28.0 0.0 collective-permute-done
  28.0 0.0 collective-permute-start.1
  28.0 3.5 %collective-permute-done.4 = bf16[2,64,1024]{2,1,0:T(8,128)(2,1)S(1)} collective-permute-done((bf16[2,64,1024]{2,1,0:T(8,128)(2,1)S(1)}, bf16[2,64,1024]{2,1,0:T(8,128)(2,1)S(1)}, u32[]{:S(2)}, u32[]{:S(2)}) %collective-permute-start.4) | collective-permute-done | bytes 262176 | tf_op jit(solution)/shard_map/ppermute | solution.py:79
  31.5 0.7 copy-done.4
  32.2 0.8 %pad_maximum_fusion = bf16[2,128,1024]{2,1,0:T(8,128)(2,1)} fusion(bf16[2,64,1024]{2,1,0:T(8,128)(2,1)S(1)} %collective-permute-done.4, bf16[1,64,1024]{2,1,0:T(8,128)(2,1)S(1)} %bitcast.88, bf16[1,64,1024]{2,1,0:T(8,128)(2,1)S(1)} %bitcast.79), kind=kLoop, calls=%fused_computation.15 | loop fusion | flops 1572864 | bytes 1048576 | tf_op jit(solution)/shard_map/concatenate | solution.py:80
  33.0 0.0 collective-permute-start.5
  33.0 0.2 multiply_reduce_fusion
  33.3 2.6 %collective-permute-done.8 = bf16[2,64,1024]{2,1,0:T(8,128)(2,1)} collective-permute-done((bf16[2,64,1024]{2,1,0:T(8,128)(2,1)}, bf16[2,64,1024]{2,1,0:T(8,128)(2,1)}, u32[]{:S(2)}, u32[]{:S(2)}) %collective-permute-start.8) | collective-permute-done | bytes 262176 | tf_op jit(solution)/shard_map/ppermute | solution.py:79
  35.9 1.0 %pad_maximum_fusion.1 = bf16[2,128,1024]{2,1,0:T(8,128)(2,1)S(1)} fusion(bf16[2,64,1024]{2,1,0:T(8,128)(2,1)} %collective-permute-done.8, bf16[1,64,1024]{2,1,0:T(8,128)(2,1)S(1)} %bitcast.85, bf16[1,64,1024]{2,1,0:T(8,128)(2,1)S(1)} %bitcast.76), kind=kLoop, calls=%fused_computation.16 | loop fusion | flops 1572864 | bytes 1048576 | tf_op jit(solution)/shard_map/concatenate | solution.py:80
  36.9 0.1 collective-permute-start.9
  37.0 1.7 %collective-permute-done.12 = bf16[2,64,1024]{2,1,0:T(8,128)(2,1)} collective-permute-done((bf16[2,64,1024]{2,1,0:T(8,128)(2,1)}, bf16[2,64,1024]{2,1,0:T(8,128)(2,1)}, u32[]{:S(2)}, u32[]{:S(2)}) %collective-permute-start.12) | collective-permute-done | bytes 262176 | tf_op jit(solution)/shard_map/ppermute | solution.py:79
  38.7 1.0 %pad_maximum_fusion.2 = bf16[2,128,1024]{2,1,0:T(8,128)(2,1)S(1)} fusion(bf16[2,64,1024]{2,1,0:T(8,128)(2,1)} %collective-permute-done.12, bf16[1,64,1024]{2,1,0:T(8,128)(2,1)S(1)} %bitcast.82, bf16[1,64,1024]{2,1,0:T(8,128)(2,1)S(1)} %bitcast.73), kind=kLoop, calls=%fused_computation.17 | loop fusion | flops 1572864 | bytes 1048576 | tf_op jit(solution)/shard_map/concatenate | solution.py:80
  39.7 0.1 collective-permute-start.13
  39.8 0.0 collective-permute-done.1
  39.8 1.1 %maximum_bitcast_fusion = bf16[1,256,1024]{2,1,0:T(8,128)(2,1)S(1)} fusion(bf16[128,1024]{1,0:T(8,128)(2,1)} %collective-permute-done.1, bf16[128,1024]{1,0:T(8,128)(2,1)} %collective-permute-done), kind=kLoop, calls=%fused_computation.14 | loop fusion | flops 1048576 | bytes 1048576 | tf_op jit(solution)/shard_map/stack | solution.py:96
  40.9 0.5 broadcast_in_dim.138
  41.4 0.1 maximum_dynamic-update-slice_fusion
  41.5 0.0 collective-permute-done.5
  41.5 1.1 %maximum_dynamic-update-slice_fusion.1 = bf16[8,256,1024]{2,1,0:T(8,128)(2,1)S(1)} fusion(bf16[8,256,1024]{2,1,0:T(8,128)(2,1)S(1)} %maximum_dynamic-update-slice_fusion, s32[]{:T(128)S(6)} %select_n.148, bf16[2,128,1024]{2,1,0:T(8,128)(2,1)} %collective-permute-done.5, bf16[2,64,1024]{2,1,0:T(8,128)(2,1)S(1)} %copy-done.5, ...), kind=kLoop, calls=%fused_computation.10 | loop fusion | flops 4194304 | bytes 2097156 | tf_op jit(solution)/shard_map/dynamic_update_slice | solution.py:100
  42.7 0.0 collective-permute-done.9
  42.7 1.1 %maximum_dynamic-update-slice_fusion.2 = bf16[8,256,1024]{2,1,0:T(8,128)(2,1)S(1)} fusion(bf16[8,256,1024]{2,1,0:T(8,128)(2,1)S(1)} %maximum_dynamic-update-slice_fusion.1, s32[]{:T(128)S(6)} %select_n.150, bf16[2,128,1024]{2,1,0:T(8,128)(2,1)S(1)} %collective-permute-done.9, bf16[2,64,1024]{2,1,0:T(8,128)(2,1)} %collective-permute-done.8, ...), kind=kLoop, calls=%fused_computation.11 | loop fusion | flops 4194304 | bytes 2097156 | tf_op jit(solution)/shard_map/dynamic_update_slice | solution.py:100
  43.7 0.0 collective-permute-done.13
  43.7 1.1 %maximum_dynamic-update-slice_fusion.3 = bf16[8,256,1024]{2,1,0:T(8,128)(2,1)S(1)} fusion(bf16[8,256,1024]{2,1,0:T(8,128)(2,1)S(1)} %maximum_dynamic-update-slice_fusion.2, s32[]{:T(128)S(6)} %select_n.152, bf16[2,128,1024]{2,1,0:T(8,128)(2,1)S(1)} %collective-permute-done.13, bf16[2,64,1024]{2,1,0:T(8,128)(2,1)} %collective-permute-done.12, ...), kind=kLoop, calls=%fused_computation.12 | loop fusion | flops 4194304 | bytes 2097156 | tf_op jit(solution)/shard_map/dynamic_update_slice | solution.py:100
  44.8 0.0 copy-start.1
  44.8 4.6 %fusion.21 = (f32[2048]{0:T(1024)S(1)}, f32[2048,512]{1,0:T(8,128)}) fusion(f32[512]{0:T(512)S(1)} %multiply_reduce_fusion, bf16[2048,1024]{1,0:T(8,128)(2,1)S(1)} %bitcast.68, f32[512,1024]{1,0:T(8,128)S(1)} %copy-done.3), kind=kOutput, calls=%fused_computation.74 | convolution fusion | flops 2152200192 | bytes 10496000 | tf_op jit(solution)/shard_map/dot_general | solution.py:10
  49.4 0.1 broadcast_in_dim.141
  49.5 3.3 %exponential_reduce_fusion = f32[2048]{0:T(1024)S(1)} fusion(f32[2048,512]{1,0:T(8,128)} %get-tuple-element.26, f32[2048]{0:T(1024)S(1)} %get-tuple-element.25), kind=kLoop, calls=%fused_computation.4 | loop fusion | flops 2095104 | bytes 4210688 | tf_op jit(solution)/shard_map/reduce_sum | solution.py:18
  52.8 0.1 broadcast_in_dim.146
  52.9 0.1 select_reduce_fusion.7
  53.0 0.2 select_reduce_fusion.3
  53.2 9.3 %all-gather = f32[16,8,4,64]{3,1,2,0:T(8,128)S(1)} all-gather(f32[2,8,4,64]{3,1,2,0:T(8,128)S(1)} %copy.30), channel_id=2, replica_groups=mesh['outer'=4,'dp'=2,'cent'=4] {'dp','cent'}, dimensions={0}, use_global_device_ids=true | all-gather | bytes 147456 | tf_op jit(solution)/shard_map/all_gather | solution.py:130
  62.6 0.1 select_reduce_fusion.1
  62.7 0.1 select_reduce_fusion.5
  62.9 0.1 div.62
  62.9 0.1 sub.65
  63.0 2.8 %bitcast_reduce_fusion = f32[4,512]{1,0:T(4,128)S(1)} fusion(f32[2048]{0:T(1024)S(1)} %div.62, f32[2048,512]{1,0:T(8,128)} %get-tuple-element.26, f32[2048]{0:T(1024)S(1)} %sub.65), kind=kLoop, calls=%fused_computation.2 | loop fusion | flops 5240832 | bytes 4218880 | tf_op jit(solution)/shard_map/reduce_sum | solution.py:141
  65.9 0.6 copy-done
  66.5 1.0 %fusion = bf16[2048,512]{1,0:T(8,128)(2,1)S(1)} fusion(f32[4,512]{1,0:T(4,128)S(1)} %broadcast_add_fusion, f32[2048]{0:T(1024)S(1)} %div.62, f32[2048,512]{1,0:T(8,128)S(1)} %copy-done, f32[2048]{0:T(1024)S(1)} %sub.65), kind=kLoop, calls=%fused_computation.1 | loop fusion | flops 6291456 | bytes 6316032 | tf_op jit(solution)/shard_map/convert_element_type | solution.py:142
  67.5 0.7 %copy-done.2 = bf16[8,256,1024]{2,1,0:T(8,128)(2,1)S(1)} copy-done((bf16[8,256,1024]{2,1,0:T(8,128)(2,1)S(1)}, bf16[8,256,1024]{2,1,0:T(8,128)(2,1)}, u32[]{:S(2)}) %copy-start.2) | copy-done | bytes 4194328
  68.2 3.7 %subtract_multiply_fusion.1 = f32[512,1024]{1,0:T(8,128)} fusion(f32[512,1024]{1,0:T(8,128)S(1)} %copy-done.3, bf16[2048,512]{1,0:T(8,128)(2,1)S(1)} %fusion, bf16[2048,1024]{1,0:T(8,128)(2,1)S(1)} %bitcast.69, f32[512]{0:T(512)S(1)} %fusion.8), kind=kOutput, calls=%fused_computation.7 | convolution fusion | flops 2149056512 | bytes 10487808 | tf_op jit(solution)/shard_map/dot_general | solution.py:143
  (25 shorter events, 0.2 us)
Async XLA Ops:
  0.0 33.0 %copy-start.3 = (f32[512,1024]{1,0:T(8,128)S(1)}, f32[512,1024]{1,0:T(8,128)}, u32[]{:S(2)}) copy-start(f32[512,1024]{1,0:T(8,128)} %param.4) | copy-start | bytes 6291460
  1.1 12.5 %collective-permute-start.2 = (bf16[64,1024]{1,0:T(8,128)(2,1)S(1)}, bf16[64,1024]{1,0:T(8,128)(2,1)S(1)}, u32[]{:S(2)}, u32[]{:S(2)}) collective-permute-start(bf16[64,1024]{1,0:T(8,128)(2,1)S(1)} %dynamic-slice_convert_fusion.1), channel_id=1, source_target_pairs={{0,8},{8,16},{16,24},{24,0},{1,9},{9,17},{17,25},{25,1},{2,10},{10... | collective-permute-start | bytes 393224 | tf_op jit(solution)/shard_map/ppermute | solution.py:85
  4.2 11.2 %collective-permute-start.6 = (bf16[64,1024]{1,0:T(8,128)(2,1)S(1)}, bf16[64,1024]{1,0:T(8,128)(2,1)S(1)}, u32[]{:S(2)}, u32[]{:S(2)}) collective-permute-start(bf16[64,1024]{1,0:T(8,128)(2,1)S(1)} %dynamic-slice_convert_fusion.1), channel_id=1, source_target_pairs={{0,16},{8,24},{16,0},{24,8},{1,17},{9,25},{17,1},{25,9},{2,18},{10... | collective-permute-start | bytes 393224 | tf_op jit(solution)/shard_map/ppermute | solution.py:85
  6.8 10.2 %collective-permute-start.10 = (bf16[64,1024]{1,0:T(8,128)(2,1)S(1)}, bf16[64,1024]{1,0:T(8,128)(2,1)S(1)}, u32[]{:S(2)}, u32[]{:S(2)}) collective-permute-start(bf16[64,1024]{1,0:T(8,128)(2,1)S(1)} %dynamic-slice_convert_fusion.1), channel_id=1, source_target_pairs={{0,24},{8,0},{16,8},{24,16},{1,25},{9,1},{17,9},{25,17},{2,26},{10... | collective-permute-start | bytes 393224 | tf_op jit(solution)/shard_map/ppermute | solution.py:85
  9.9 18.1 %collective-permute-start = (bf16[128,1024]{1,0:T(8,128)(2,1)}, bf16[128,1024]{1,0:T(8,128)(2,1)}, u32[]{:S(2)}, u32[]{:S(2)}) collective-permute-start(bf16[128,1024]{1,0:T(8,128)(2,1)} %dynamic-slice_convert_fusion), channel_id=1, source_target_pairs={{0,4},{4,0},{1,5},{5,1},{2,6},{6,2},{3,7},{7,3},{8,12},{12,8},{9,1... | collective-permute-start | bytes 786440 | tf_op jit(solution)/shard_map/ppermute | solution.py:93
  13.6 8.5 %collective-permute-start.3 = (bf16[64,1024]{1,0:T(8,128)(2,1)S(1)}, bf16[64,1024]{1,0:T(8,128)(2,1)S(1)}, u32[]{:S(2)}, u32[]{:S(2)}) collective-permute-start(bf16[64,1024]{1,0:T(8,128)(2,1)S(1)} %collective-permute-done.2), channel_id=1, source_target_pairs={{0,4},{4,0},{1,5},{5,1},{2,6},{6,2},{3,7},{7,3},{8,12},{12,8},{9,1... | collective-permute-start | bytes 393224 | tf_op jit(solution)/shard_map/ppermute | solution.py:74
  15.4 8.9 %collective-permute-start.7 = (bf16[64,1024]{1,0:T(8,128)(2,1)S(1)}, bf16[64,1024]{1,0:T(8,128)(2,1)S(1)}, u32[]{:S(2)}, u32[]{:S(2)}) collective-permute-start(bf16[64,1024]{1,0:T(8,128)(2,1)S(1)} %collective-permute-done.6), channel_id=1, source_target_pairs={{0,4},{4,0},{1,5},{5,1},{2,6},{6,2},{3,7},{7,3},{8,12},{12,8},{9,1... | collective-permute-start | bytes 393224 | tf_op jit(solution)/shard_map/ppermute | solution.py:74
  17.0 9.6 %collective-permute-start.11 = (bf16[64,1024]{1,0:T(8,128)(2,1)S(1)}, bf16[64,1024]{1,0:T(8,128)(2,1)S(1)}, u32[]{:S(2)}, u32[]{:S(2)}) collective-permute-start(bf16[64,1024]{1,0:T(8,128)(2,1)S(1)} %collective-permute-done.10), channel_id=1, source_target_pairs={{0,4},{4,0},{1,5},{5,1},{2,6},{6,2},{3,7},{7,3},{8,12},{12,8},{9,1... | collective-permute-start | bytes 393224 | tf_op jit(solution)/shard_map/ppermute | solution.py:74
  22.2 9.3 %collective-permute-start.4 = (bf16[2,64,1024]{2,1,0:T(8,128)(2,1)S(1)}, bf16[2,64,1024]{2,1,0:T(8,128)(2,1)S(1)}, u32[]{:S(2)}, u32[]{:S(2)}) collective-permute-start(bf16[2,64,1024]{2,1,0:T(8,128)(2,1)S(1)} %pad_maximum_fusion.3), channel_id=1, source_target_pairs={{0,2},{1,3},{2,0},{3,1},{4,6},{5,7},{6,4},{7,5},{8,10},{9,11},{10,... | collective-permute-start | bytes 786440 | tf_op jit(solution)/shard_map/ppermute | solution.py:79
  25.1 10.8 %collective-permute-start.8 = (bf16[2,64,1024]{2,1,0:T(8,128)(2,1)}, bf16[2,64,1024]{2,1,0:T(8,128)(2,1)}, u32[]{:S(2)}, u32[]{:S(2)}) collective-permute-start(bf16[2,64,1024]{2,1,0:T(8,128)(2,1)} %pad_maximum_fusion.4), channel_id=1, source_target_pairs={{0,2},{1,3},{2,0},{3,1},{4,6},{5,7},{6,4},{7,5},{8,10},{9,11},{10,... | collective-permute-start | bytes 786440 | tf_op jit(solution)/shard_map/ppermute | solution.py:79
  27.3 11.4 %collective-permute-start.12 = (bf16[2,64,1024]{2,1,0:T(8,128)(2,1)}, bf16[2,64,1024]{2,1,0:T(8,128)(2,1)}, u32[]{:S(2)}, u32[]{:S(2)}) collective-permute-start(bf16[2,64,1024]{2,1,0:T(8,128)(2,1)} %pad_maximum_fusion.5), channel_id=1, source_target_pairs={{0,2},{1,3},{2,0},{3,1},{4,6},{5,7},{6,4},{7,5},{8,10},{9,11},{10,... | collective-permute-start | bytes 786440 | tf_op jit(solution)/shard_map/ppermute | solution.py:79
  28.0 11.8 %collective-permute-start.1 = (bf16[128,1024]{1,0:T(8,128)(2,1)}, bf16[128,1024]{1,0:T(8,128)(2,1)}, u32[]{:S(2)}, u32[]{:S(2)}) collective-permute-start(bf16[128,1024]{1,0:T(8,128)(2,1)} %collective-permute-done), channel_id=1, source_target_pairs={{0,1},{1,0},{2,3},{3,2},{4,5},{5,4},{6,7},{7,6},{8,9},{9,8},{10,11... | collective-permute-start | bytes 786440 | tf_op jit(solution)/shard_map/ppermute | solution.py:94
  31.5 0.7 copy-start.4
  33.0 8.5 %collective-permute-start.5 = (bf16[2,128,1024]{2,1,0:T(8,128)(2,1)}, bf16[2,128,1024]{2,1,0:T(8,128)(2,1)}, u32[]{:S(2)}, u32[]{:S(2)}) collective-permute-start(bf16[2,128,1024]{2,1,0:T(8,128)(2,1)} %pad_maximum_fusion), channel_id=1, source_target_pairs={{0,1},{1,0},{2,3},{3,2},{4,5},{5,4},{6,7},{7,6},{8,9},{9,8},{10,11... | collective-permute-start | bytes 1572872 | tf_op jit(solution)/shard_map/ppermute | solution.py:79
  36.9 4.6 %copy-start.5 = (bf16[2,64,1024]{2,1,0:T(8,128)(2,1)S(1)}, bf16[2,64,1024]{2,1,0:T(8,128)(2,1)}, u32[]{:S(2)}) copy-start(bf16[2,64,1024]{2,1,0:T(8,128)(2,1)} %copy-done.4) | copy-start | bytes 786436
  36.9 5.8 %collective-permute-start.9 = (bf16[2,128,1024]{2,1,0:T(8,128)(2,1)S(1)}, bf16[2,128,1024]{2,1,0:T(8,128)(2,1)S(1)}, u32[]{:S(2)}, u32[]{:S(2)}) collective-permute-start(bf16[2,128,1024]{2,1,0:T(8,128)(2,1)S(1)} %pad_maximum_fusion.1), channel_id=1, source_target_pairs={{0,1},{1,0},{2,3},{3,2},{4,5},{5,4},{6,7},{7,6},{8,9},{9,8},{10,11... | collective-permute-start | bytes 1572872 | tf_op jit(solution)/shard_map/ppermute | solution.py:79
  39.7 4.0 %collective-permute-start.13 = (bf16[2,128,1024]{2,1,0:T(8,128)(2,1)S(1)}, bf16[2,128,1024]{2,1,0:T(8,128)(2,1)S(1)}, u32[]{:S(2)}, u32[]{:S(2)}) collective-permute-start(bf16[2,128,1024]{2,1,0:T(8,128)(2,1)S(1)} %pad_maximum_fusion.2), channel_id=1, source_target_pairs={{0,1},{1,0},{2,3},{3,2},{4,5},{5,4},{6,7},{7,6},{8,9},{9,8},{10,11... | collective-permute-start | bytes 1572872 | tf_op jit(solution)/shard_map/ppermute | solution.py:79
  44.8 4.6 %copy-start.1 = (bf16[8,256,1024]{2,1,0:T(8,128)(2,1)}, bf16[8,256,1024]{2,1,0:T(8,128)(2,1)S(1)}, u32[]{:S(2)}) copy-start(bf16[8,256,1024]{2,1,0:T(8,128)(2,1)S(1)} %maximum_dynamic-update-slice_fusion.3) | copy-start | bytes 12582916
  63.0 3.4 %copy-start = (f32[2048,512]{1,0:T(8,128)S(1)}, f32[2048,512]{1,0:T(8,128)}, u32[]{:S(2)}) copy-start(f32[2048,512]{1,0:T(8,128)} %get-tuple-element.26) | copy-start | bytes 12582916
  65.9 2.3 %copy-start.2 = (bf16[8,256,1024]{2,1,0:T(8,128)(2,1)S(1)}, bf16[8,256,1024]{2,1,0:T(8,128)(2,1)}, u32[]{:S(2)}) copy-start(bf16[8,256,1024]{2,1,0:T(8,128)(2,1)} %copy-done.1) | copy-start | bytes 12582916

commit v14 on v13

--- a/solution.py
+++ b/solution.py
@@ -3,6 +3,7 @@
 import jax
 import jax.numpy as jnp
 from jax import lax
+from jax.experimental import pallas as pl
 from jax.sharding import PartitionSpec as P
 
 
@@ -17,6 +18,43 @@
     local_max = jnp.max(logits, axis=1)
     local_sum = jnp.sum(jnp.exp(logits - local_max[:, None]), axis=1)
     return (local_max, local_sum)
+
+
+def _logit_kernel(r_ref, c_ref, sq_ref, l_ref, m_ref, s_ref):
+    prod = lax.dot_general(
+        r_ref[...], c_ref[...], (((1,), (1,)), ((), ())), preferred_element_type=jnp.float32
+    )
+    lg = 0.5 * (2.0 * prod - sq_ref[...])
+    l_ref[...] = lg
+    mx = jnp.max(lg, axis=1, keepdims=True)
+    m_ref[...] = mx
+    s_ref[...] = jnp.sum(jnp.exp(lg - mx), axis=1, keepdims=True)
+
+
+def logits_and_stats(rows_bf, cent_bf, squares):
+    n, d = rows_bf.shape
+    k = cent_bf.shape[0]
+    bm = 256 if n % 256 == 0 else n
+    lg, mx, sm = pl.pallas_call(
+        _logit_kernel,
+        grid=(n // bm,),
+        in_specs=[
+            pl.BlockSpec((bm, d), lambda i: (i, 0)),
+            pl.BlockSpec((k, d), lambda i: (0, 0)),
+            pl.BlockSpec((1, k), lambda i: (0, 0)),
+        ],
+        out_specs=[
+            pl.BlockSpec((bm, k), lambda i: (i, 0)),
+            pl.BlockSpec((bm, 1), lambda i: (i, 0)),
+            pl.BlockSpec((bm, 1), lambda i: (i, 0)),
+        ],
+        out_shape=[
+            jax.ShapeDtypeStruct((n, k), jnp.float32),
+            jax.ShapeDtypeStruct((n, 1), jnp.float32),
+            jax.ShapeDtypeStruct((n, 1), jnp.float32),
+        ],
+    )(rows_bf, cent_bf, squares[None, :])
+    return lg, mx[:, 0], sm[:, 0]
 
 
 def global_stats(local_max, local_sum):
@@ -100,8 +138,7 @@
         cur = lax.dynamic_update_slice_in_dim(cur, parts[sz], ((z - sz) % n_o) * n_d, axis=0)
     everything = cur.reshape(n_od * n_c * tq, d)
 
-    logits = scores_for(everything, cent_bf, squares)
-    local_max, local_sum = row_summary(logits)
+    logits, local_max, local_sum = logits_and_stats(everything, cent_bf, squares)
 
     src_vec = jnp.stack([a * n_d + (y - sy) % n_d for a, sy in shifts])
     hot_k = src_vec[None, :] == jnp.arange(n_od)[:, None]

time: 72.4 us -> 80.2 us (1.11)
  Pallas kernels: 0 us -> 9.23 us
  matrix products: 8.28 us -> 5.91 us
  waiting for transfers between devices: 14.3 us -> 15.2 us
    pallas_call x0 -> x1, Pallas kernels: none -> 9.23 us  [logits_and_stats(): pl.pallas_call(_logit_kernel, grid=(n // bm,), in_specs=[pl.BlockSpec((bm...]
    dot_general x1 -> x0, matrix products: 4.62 us -> none  [scores_for(): lax.dot_general(piece, cent_bf, (((1,), (1,)), ((), ())), preferred_eleme...]
    reduce_sum x1, other arithmetic: 0.21 us -> 4.06 us  [shards_all(): squares = jnp.sum(centroids * centroids, axis=1)]
    reduce_sum x1 -> x0, other arithmetic: 3.31 us -> none  [row_summary(): local_sum = jnp.sum(jnp.exp(logits - local_max[:, None]), axis=1)]
    ppermute x6, waiting for transfers between devices: 7.81 us -> 11 us  [spread(): other = lax.ppermute(cur, 'cent', [(i, i ^ bit) for i in range(n_c)])]
    pallas_call x0 -> x2, other arithmetic: none -> 3.13 us  [logits_and_stats(): pl.pallas_call(_logit_kernel, grid=(n // bm,), in_specs=[pl.BlockSpec((bm...]
    concatenate x3, other arithmetic: 2.8 us -> 0.1 us  [spread(): cur = jnp.concatenate([cur, other], axis=1)]
    dot_general x1, matrix products: 3.67 us -> 5.91 us  [shards_all(): lax.dot_general(scaled.reshape(n_o * pod, k), everything, (((0,), (0,)),...]
  transfers between devices with their start and end apart: 14 -> 14, of which waited for: 6 -> 5; matrix products, arithmetic and copies ran while one was open for 17% -> 16% of each run, Pallas kernels for 0% -> 0%
where the time goes in v14:
time: 80.2 us; the launch traced here: 79.7 us
  other arithmetic  17.8 us (22%)
  starting transfers between devices  15.2 us (19%)
  waiting for transfers between devices  15.2 us (19%)
  blocking collectives  9.65 us (12%)
  Pallas kernels  9.23 us (12%)
  local copies, waits for them, and re-layouts  6.34 us (8%)
  matrix products  5.91 us (7%)
    ppermute x6, waiting for transfers between devices, spread(): other = lax.ppermute(cur, 'cent', [(i, i ^ bit) for i in range(n_c)])  11 us
    all_gather x1, blocking collectives, shards_all(): every = lax.all_gather(both, ('dp', 'cent'), axis=0)  9.65 us
    pallas_call x1, Pallas kernels, logits_and_stats(): pl.pallas_call(_logit_kernel, grid=(n // bm,), in_specs=[pl.BlockSpec((bm...  9.23 us
    ppermute x3, starting transfers between devices, shards_all(): lax.ppermute(mine, 'outer', [(i, (i + sz) % n_o) for i in range(n_o)])  7.01 us
    dot_general x1, matrix products, shards_all(): lax.dot_general(scaled.reshape(n_o * pod, k), everything, (((0,), (0,)),...  5.91 us
    dynamic_update_slice x4, other arithmetic, shards_all(): lax.dynamic_update_slice_in_dim(cur, parts[sz], (z - sz) % n_o * n_d, axi...  4.25 us
    ppermute x3, waiting for transfers between devices, pair_of(): lax.ppermute(piece, 'dp', [(j, (j + sy) % n_d) for j in range(n_d)])  4.18 us
    reduce_sum x1, other arithmetic, shards_all(): squares = jnp.sum(centroids * centroids, axis=1)  4.06 us
  transfers between devices with their start and end apart: 14, of which 5 were waited for; matrix products, arithmetic and copies ran while one was open for 16% of the time, Pallas kernels for 0%

profile of v14, /device:TPU:0, one launch (start us, length us, event | category | flops | bytes accessed | tf_op | source)
XLA Modules:
  0.0 79.7 jit_solution(3288286598382215613)
XLA Ops:
  0.0 0.0 copy-start.2
  0.0 1.1 %dynamic-slice_convert_fusion.1 = bf16[64,1024]{1,0:T(8,128)(2,1)S(1)} fusion(f32[256,1024]{1,0:T(8,128)} %param.3, s32[]{:T(128)S(6)} %select_n.146), kind=kLoop, calls=%fused_computation.20 | loop fusion | bytes 262148 | tf_op jit(solution)/shard_map/convert_element_type | solution.py:107
  1.1 3.1 %collective-permute-start.2 = (bf16[64,1024]{1,0:T(8,128)(2,1)S(1)}, bf16[64,1024]{1,0:T(8,128)(2,1)S(1)}, u32[]{:S(2)}, u32[]{:S(2)}) collective-permute-start(bf16[64,1024]{1,0:T(8,128)(2,1)S(1)} %dynamic-slice_convert_fusion.1), channel_id=1, source_target_pairs={{0,8},{8,16},{16,24},{24,0},{1,9},{9,17},{17,25},{25,1},{2,10},{10... | collective-permute-start | bytes 393224 | tf_op jit(solution)/shard_map/ppermute | solution.py:123
  4.1 2.6 %collective-permute-start.6 = (bf16[64,1024]{1,0:T(8,128)(2,1)S(1)}, bf16[64,1024]{1,0:T(8,128)(2,1)S(1)}, u32[]{:S(2)}, u32[]{:S(2)}) collective-permute-start(bf16[64,1024]{1,0:T(8,128)(2,1)S(1)} %dynamic-slice_convert_fusion.1), channel_id=1, source_target_pairs={{0,16},{8,24},{16,0},{24,8},{1,17},{9,25},{17,1},{25,9},{2,18},{10... | collective-permute-start | bytes 393224 | tf_op jit(solution)/shard_map/ppermute | solution.py:123
  6.7 1.3 %collective-permute-start.10 = (bf16[64,1024]{1,0:T(8,128)(2,1)S(1)}, bf16[64,1024]{1,0:T(8,128)(2,1)S(1)}, u32[]{:S(2)}, u32[]{:S(2)}) collective-permute-start(bf16[64,1024]{1,0:T(8,128)(2,1)S(1)} %dynamic-slice_convert_fusion.1), channel_id=1, source_target_pairs={{0,24},{8,0},{16,8},{24,16},{1,25},{9,1},{17,9},{25,17},{2,26},{10... | collective-permute-start | bytes 393224 | tf_op jit(solution)/shard_map/ppermute | solution.py:123
  8.1 1.1 %dynamic-slice_convert_fusion = bf16[128,1024]{1,0:T(8,128)(2,1)S(1)} fusion(f32[256,1024]{1,0:T(8,128)} %param.3, s32[]{:T(128)S(6)} %select_n.143), kind=kLoop, calls=%fused_computation.15 | loop fusion | bytes 524292 | tf_op jit(solution)/shard_map/convert_element_type | solution.py:128
  9.2 0.0 copy-start.3
  9.2 1.6 %collective-permute-start = (bf16[128,1024]{1,0:T(8,128)(2,1)S(1)}, bf16[128,1024]{1,0:T(8,128)(2,1)}, u32[]{:S(2)}, u32[]{:S(2)}) collective-permute-start(bf16[128,1024]{1,0:T(8,128)(2,1)S(1)} %dynamic-slice_convert_fusion), channel_id=1, source_target_pairs={{0,4},{4,0},{1,5},{5,1},{2,6},{6,2},{3,7},{7,3},{8,12},{12,8},{9,1... | collective-permute-start | bytes 786440 | tf_op jit(solution)/shard_map/ppermute | solution.py:131
  10.7 4.1 %multiply_reduce_fusion = (f32[512]{0:T(512)}, bf16[512,1024]{1,0:T(8,128)(2,1)}) fusion(f32[512,1024]{1,0:T(8,128)} %param.4), kind=kLoop, calls=%fused_computation.6 | loop fusion | flops 1572352 | bytes 3147776 | tf_op jit(solution)/shard_map/reduce_sum | solution.py:96
  14.8 0.0 copy-done.2
  14.8 0.1 convert_bitcast_fusion
  14.9 0.0 collective-permute-done.2
  14.9 0.6 collective-permute-start.3
  15.5 0.0 copy-done.3
  15.5 0.1 copy.30
  15.6 0.0 collective-permute-done.6
  15.6 1.5 %collective-permute-start.7 = (bf16[64,1024]{1,0:T(8,128)(2,1)S(1)}, bf16[64,1024]{1,0:T(8,128)(2,1)S(1)}, u32[]{:S(2)}, u32[]{:S(2)}) collective-permute-start(bf16[64,1024]{1,0:T(8,128)(2,1)S(1)} %collective-permute-done.6), channel_id=1, source_target_pairs={{0,4},{4,0},{1,5},{5,1},{2,6},{6,2},{3,7},{7,3},{8,12},{12,8},{9,1... | collective-permute-start | bytes 393224 | tf_op jit(solution)/shard_map/ppermute | solution.py:112
  17.1 0.0 collective-permute-done.10
  17.1 0.5 collective-permute-start.11
  17.6 3.7 %collective-permute-done.3 = bf16[64,1024]{1,0:T(8,128)(2,1)S(1)} collective-permute-done((bf16[64,1024]{1,0:T(8,128)(2,1)S(1)}, bf16[64,1024]{1,0:T(8,128)(2,1)S(1)}, u32[]{:S(2)}, u32[]{:S(2)}) %collective-permute-start.3) | collective-permute-done | bytes 131104 | tf_op jit(solution)/shard_map/ppermute | solution.py:112
  21.3 1.6 %collective-permute-start.4 = (bf16[2,64,1024]{2,1,0:T(8,128)(2,1)S(1)}, bf16[2,64,1024]{2,1,0:T(8,128)(2,1)S(1)}, u32[]{:S(2)}, u32[]{:S(2)}) collective-permute-start(bf16[2,64,1024]{2,1,0:T(8,128)(2,1)S(1)} %pad_maximum_fusion.3), channel_id=1, source_target_pairs={{0,2},{1,3},{2,0},{3,1},{4,6},{5,7},{6,4},{7,5},{8,10},{9,11},{10,... | collective-permute-start | bytes 786440 | tf_op jit(solution)/shard_map/ppermute | solution.py:117
  22.9 0.1 stack.128
  23.0 0.5 collective-permute-done.7
  23.5 0.7 pad_maximum_fusion.4
  24.2 1.5 %collective-permute-start.8 = (bf16[2,64,1024]{2,1,0:T(8,128)(2,1)}, bf16[2,64,1024]{2,1,0:T(8,128)(2,1)S(1)}, u32[]{:S(2)}, u32[]{:S(2)}) collective-permute-start(bf16[2,64,1024]{2,1,0:T(8,128)(2,1)} %pad_maximum_fusion.4), channel_id=1, source_target_pairs={{0,2},{1,3},{2,0},{3,1},{4,6},{5,7},{6,4},{7,5},{8,10},{9,11},{10,... | collective-permute-start | bytes 786440 | tf_op jit(solution)/shard_map/ppermute | solution.py:117
  25.7 0.0 collective-permute-done.11
  25.8 0.7 collective-permute-start.12
  26.5 0.0 collective-permute-done
  26.5 0.0 collective-permute-start.1
  26.5 4.1 %collective-permute-done.4 = bf16[2,64,1024]{2,1,0:T(8,128)(2,1)S(1)} collective-permute-done((bf16[2,64,1024]{2,1,0:T(8,128)(2,1)S(1)}, bf16[2,64,1024]{2,1,0:T(8,128)(2,1)S(1)}, u32[]{:S(2)}, u32[]{:S(2)}) %collective-permute-start.4) | collective-permute-done | bytes 262176 | tf_op jit(solution)/shard_map/ppermute | solution.py:117
  30.6 0.1 collective-permute-start.5
  30.8 4.2 %collective-permute-done.8 = bf16[2,64,1024]{2,1,0:T(8,128)(2,1)S(1)} collective-permute-done((bf16[2,64,1024]{2,1,0:T(8,128)(2,1)}, bf16[2,64,1024]{2,1,0:T(8,128)(2,1)S(1)}, u32[]{:S(2)}, u32[]{:S(2)}) %collective-permute-start.8) | collective-permute-done | bytes 262176 | tf_op jit(solution)/shard_map/ppermute | solution.py:117
  35.0 0.1 collective-permute-start.9
  35.1 2.7 %collective-permute-done.12 = bf16[2,64,1024]{2,1,0:T(8,128)(2,1)S(1)} collective-permute-done((bf16[2,64,1024]{2,1,0:T(8,128)(2,1)S(1)}, bf16[2,64,1024]{2,1,0:T(8,128)(2,1)S(1)}, u32[]{:S(2)}, u32[]{:S(2)}) %collective-permute-start.12) | collective-permute-done | bytes 262176 | tf_op jit(solution)/shard_map/ppermute | solution.py:117
  37.8 0.1 collective-permute-start.13
  37.9 0.0 collective-permute-done.1
  37.9 1.1 %maximum_bitcast_fusion = bf16[1,256,1024]{2,1,0:T(8,128)(2,1)S(1)} fusion(bf16[128,1024]{1,0:T(8,128)(2,1)} %collective-permute-done.1, bf16[128,1024]{1,0:T(8,128)(2,1)} %collective-permute-done), kind=kLoop, calls=%fused_computation.11 | loop fusion | flops 1048576 | bytes 1048576 | tf_op jit(solution)/shard_map/stack | solution.py:134
  39.0 2.5 %broadcast_in_dim.139 = bf16[8,256,1024]{2,1,0:T(8,128)(2,1)} broadcast(bf16[]{:T(256)} %constant.102.clone.1), dimensions={} | broadcast | bytes 4194306 | tf_op jit(solution)/shard_map/broadcast_in_dim | solution.py:136
  41.5 1.0 %maximum_dynamic-update-slice_fusion = bf16[8,256,1024]{2,1,0:T(8,128)(2,1)} fusion(bf16[8,256,1024]{2,1,0:T(8,128)(2,1)} %broadcast_in_dim.139, s32[]{:T(128)S(6)} %select_n.145, bf16[1,256,1024]{2,1,0:T(8,128)(2,1)S(1)} %maximum_bitcast_fusion, bf16[1,256,1024]{2,1,0:T(8,128)(2,1)S(1)} %convert_bitcast_fusion), kind=kLoop, calls=%fused_computation.7 | loop fusion | flops 2097152 | bytes 2097156 | tf_op jit(solution)/shard_map/dynamic_update_slice | solution.py:138
  42.5 0.0 collective-permute-done.5
  42.5 1.0 %maximum_dynamic-update-slice_fusion.1 = bf16[8,256,1024]{2,1,0:T(8,128)(2,1)} fusion(bf16[8,256,1024]{2,1,0:T(8,128)(2,1)} %maximum_dynamic-update-slice_fusion, s32[]{:T(128)S(6)} %select_n.148, bf16[2,128,1024]{2,1,0:T(8,128)(2,1)S(1)} %collective-permute-done.5, bf16[2,64,1024]{2,1,0:T(8,128)(2,1)S(1)} %collective-permute-done.4, ...), kind=kLoop, calls=%fused_computation.8 | loop fusion | flops 4194304 | bytes 2097156 | tf_op jit(solution)/shard_map/dynamic_update_slice | solution.py:138
  43.6 0.0 collective-permute-done.9
  43.6 1.1 %maximum_dynamic-update-slice_fusion.2 = bf16[8,256,1024]{2,1,0:T(8,128)(2,1)} fusion(bf16[8,256,1024]{2,1,0:T(8,128)(2,1)} %maximum_dynamic-update-slice_fusion.1, s32[]{:T(128)S(6)} %select_n.150, bf16[2,128,1024]{2,1,0:T(8,128)(2,1)S(1)} %collective-permute-done.9, bf16[2,64,1024]{2,1,0:T(8,128)(2,1)S(1)} %collective-permute-done.8, ...), kind=kLoop, calls=%fused_computation.9 | loop fusion | flops 4194304 | bytes 2097156 | tf_op jit(solution)/shard_map/dynamic_update_slice | solution.py:138
  44.6 0.0 collective-permute-done.13
  44.6 1.1 %maximum_dynamic-update-slice_fusion.3 = bf16[8,256,1024]{2,1,0:T(8,128)(2,1)} fusion(bf16[8,256,1024]{2,1,0:T(8,128)(2,1)} %maximum_dynamic-update-slice_fusion.2, s32[]{:T(128)S(6)} %select_n.152, bf16[2,128,1024]{2,1,0:T(8,128)(2,1)S(1)} %collective-permute-done.13, bf16[2,64,1024]{2,1,0:T(8,128)(2,1)S(1)} %collective-permute-done.12, ...), kind=kLoop, calls=%fused_computation.10 | loop fusion | flops 4194304 | bytes 2097156 | tf_op jit(solution)/shard_map/dynamic_update_slice | solution.py:138
  45.7 9.2 %shard_map.37 = (f32[2048,512]{1,0:T(8,128)}, f32[2048,1]{1,0:T(8,128)}, f32[2048,1]{1,0:T(8,128)}) custom-call(bf16[2048,1024]{1,0:T(8,128)(2,1)} %bitcast.8.r_ref, bf16[512,1024]{1,0:T(8,128)(2,1)} %get-tuple-element.20.c_ref, f32[1,512]{1,0:T(1,128)} %bitcast.94), custom_call_target="tpu_custom_call" | custom-call | tf_op jit(solution)/shard_map/pallas_call | solution.py:38
  55.0 1.6 %reduce.1 = f32[2048]{0:T(1024)S(1)} reduce(f32[2048,1]{1,0:T(8,128)} %get-tuple-element.9, f32[]{:T(128)} %constant.124), dimensions={1}, to_apply=%get-tuple-element.9.reduce_sub_computation | reduce | bytes 16388 | tf_op jit(solution)/shard_map/pallas_call | solution.py:38
  56.5 0.1 broadcast_in_dim.143
  56.6 1.6 %reduce.2 = f32[2048]{0:T(1024)S(1)} reduce(f32[2048,1]{1,0:T(8,128)} %get-tuple-element.10, f32[]{:T(128)} %constant.124), dimensions={1}, to_apply=%get-tuple-element.10.reduce_sub_computation | reduce | bytes 16388 | tf_op jit(solution)/shard_map/pallas_call | solution.py:38
  58.2 0.1 broadcast_in_dim.148
  58.3 0.1 select_reduce_fusion.7
  58.4 0.2 select_reduce_fusion.3
  58.6 9.6 %all-gather = f32[16,8,4,64]{3,1,2,0:T(8,128)S(1)} all-gather(f32[2,8,4,64]{3,1,2,0:T(8,128)S(1)} %copy.33), channel_id=2, replica_groups=mesh['outer'=4,'dp'=2,'cent'=4] {'dp','cent'}, dimensions={0}, use_global_device_ids=true | all-gather | bytes 147456 | tf_op jit(solution)/shard_map/all_gather | solution.py:167
  68.3 0.1 select_reduce_fusion.1
  68.4 0.1 select_reduce_fusion.5
  68.5 0.1 div.62
  68.6 0.1 sub.45
  68.7 0.0 copy-start
  68.7 2.8 %bitcast_reduce_fusion = f32[4,512]{1,0:T(4,128)S(1)} fusion(f32[2048]{0:T(1024)S(1)} %div.62, f32[2048,512]{1,0:T(8,128)} %get-tuple-element.8, f32[2048]{0:T(1024)S(1)} %sub.45), kind=kLoop, calls=%fused_computation.2 | loop fusion | flops 5240832 | bytes 4218880 | tf_op jit(solution)/shard_map/reduce_sum | solution.py:178
  71.6 0.6 copy-done
  72.2 0.0 copy-start.1
  72.2 1.0 %fusion = bf16[2048,512]{1,0:T(8,128)(2,1)S(1)} fusion(f32[4,512]{1,0:T(4,128)S(1)} %broadcast_add_fusion, f32[2048]{0:T(1024)S(1)} %div.62, f32[2048,512]{1,0:T(8,128)S(1)} %copy-done, f32[2048]{0:T(1024)S(1)} %sub.45), kind=kLoop, calls=%fused_computation.1 | loop fusion | flops 6291456 | bytes 6316032 | tf_op jit(solution)/shard_map/convert_element_type | solution.py:179
  73.2 0.6 copy-done.1
  73.7 5.9 %subtract_multiply_fusion = f32[512,1024]{1,0:T(8,128)} fusion(f32[512,1024]{1,0:T(8,128)S(1)} %copy-done.1, bf16[2048,512]{1,0:T(8,128)(2,1)S(1)} %fusion, bf16[2048,1024]{1,0:T(8,128)(2,1)} %bitcast.8.r_ref, f32[512]{0:T(512)S(1)} %fusion.7), kind=kOutput, calls=%fused_computation.5 | convolution fusion | flops 2149056512 | bytes 10487808 | tf_op jit(solution)/shard_map/dot_general | solution.py:180
  (22 shorter events, 0.3 us)
Async XLA Ops:
  0.0 14.8 %copy-start.2 = (f32[256,1024]{1,0:T(8,128)S(1)}, f32[256,1024]{1,0:T(8,128)}, u32[]{:S(2)}) copy-start(f32[256,1024]{1,0:T(8,128)} %param.3) | copy-start | bytes 3145732
  1.1 13.8 %collective-permute-start.2 = (bf16[64,1024]{1,0:T(8,128)(2,1)S(1)}, bf16[64,1024]{1,0:T(8,128)(2,1)S(1)}, u32[]{:S(2)}, u32[]{:S(2)}) collective-permute-start(bf16[64,1024]{1,0:T(8,128)(2,1)S(1)} %dynamic-slice_convert_fusion.1), channel_id=1, source_target_pairs={{0,8},{8,16},{16,24},{24,0},{1,9},{9,17},{17,25},{25,1},{2,10},{10... | collective-permute-start | bytes 393224 | tf_op jit(solution)/shard_map/ppermute | solution.py:123
  4.1 11.5 %collective-permute-start.6 = (bf16[64,1024]{1,0:T(8,128)(2,1)S(1)}, bf16[64,1024]{1,0:T(8,128)(2,1)S(1)}, u32[]{:S(2)}, u32[]{:S(2)}) collective-permute-start(bf16[64,1024]{1,0:T(8,128)(2,1)S(1)} %dynamic-slice_convert_fusion.1), channel_id=1, source_target_pairs={{0,16},{8,24},{16,0},{24,8},{1,17},{9,25},{17,1},{25,9},{2,18},{10... | collective-permute-start | bytes 393224 | tf_op jit(solution)/shard_map/ppermute | solution.py:123
  6.7 10.4 %collective-permute-start.10 = (bf16[64,1024]{1,0:T(8,128)(2,1)S(1)}, bf16[64,1024]{1,0:T(8,128)(2,1)S(1)}, u32[]{:S(2)}, u32[]{:S(2)}) collective-permute-start(bf16[64,1024]{1,0:T(8,128)(2,1)S(1)} %dynamic-slice_convert_fusion.1), channel_id=1, source_target_pairs={{0,24},{8,0},{16,8},{24,16},{1,25},{9,1},{17,9},{25,17},{2,26},{10... | collective-permute-start | bytes 393224 | tf_op jit(solution)/shard_map/ppermute | solution.py:123
  9.2 6.3 %copy-start.3 = (s32[4]{0:T(128)S(1)}, s32[4]{0:T(128)}, u32[]{:S(2)}) copy-start(s32[4]{0:T(128)} %constant.123.clone) | copy-start | bytes 52
  9.2 17.3 %collective-permute-start = (bf16[128,1024]{1,0:T(8,128)(2,1)S(1)}, bf16[128,1024]{1,0:T(8,128)(2,1)}, u32[]{:S(2)}, u32[]{:S(2)}) collective-permute-start(bf16[128,1024]{1,0:T(8,128)(2,1)S(1)} %dynamic-slice_convert_fusion), channel_id=1, source_target_pairs={{0,4},{4,0},{1,5},{5,1},{2,6},{6,2},{3,7},{7,3},{8,12},{12,8},{9,1... | collective-permute-start | bytes 786440 | tf_op jit(solution)/shard_map/ppermute | solution.py:131
  14.9 6.4 %collective-permute-start.3 = (bf16[64,1024]{1,0:T(8,128)(2,1)S(1)}, bf16[64,1024]{1,0:T(8,128)(2,1)S(1)}, u32[]{:S(2)}, u32[]{:S(2)}) collective-permute-start(bf16[64,1024]{1,0:T(8,128)(2,1)S(1)} %collective-permute-done.2), channel_id=1, source_target_pairs={{0,4},{4,0},{1,5},{5,1},{2,6},{6,2},{3,7},{7,3},{8,12},{12,8},{9,1... | collective-permute-start | bytes 393224 | tf_op jit(solution)/shard_map/ppermute | solution.py:112
  15.6 7.9 %collective-permute-start.7 = (bf16[64,1024]{1,0:T(8,128)(2,1)S(1)}, bf16[64,1024]{1,0:T(8,128)(2,1)S(1)}, u32[]{:S(2)}, u32[]{:S(2)}) collective-permute-start(bf16[64,1024]{1,0:T(8,128)(2,1)S(1)} %collective-permute-done.6), channel_id=1, source_target_pairs={{0,4},{4,0},{1,5},{5,1},{2,6},{6,2},{3,7},{7,3},{8,12},{12,8},{9,1... | collective-permute-start | bytes 393224 | tf_op jit(solution)/shard_map/ppermute | solution.py:112
  17.1 8.6 %collective-permute-start.11 = (bf16[64,1024]{1,0:T(8,128)(2,1)S(1)}, bf16[64,1024]{1,0:T(8,128)(2,1)S(1)}, u32[]{:S(2)}, u32[]{:S(2)}) collective-permute-start(bf16[64,1024]{1,0:T(8,128)(2,1)S(1)} %collective-permute-done.10), channel_id=1, source_target_pairs={{0,4},{4,0},{1,5},{5,1},{2,6},{6,2},{3,7},{7,3},{8,12},{12,8},{9,1... | collective-permute-start | bytes 393224 | tf_op jit(solution)/shard_map/ppermute | solution.py:112
  21.3 9.3 %collective-permute-start.4 = (bf16[2,64,1024]{2,1,0:T(8,128)(2,1)S(1)}, bf16[2,64,1024]{2,1,0:T(8,128)(2,1)S(1)}, u32[]{:S(2)}, u32[]{:S(2)}) collective-permute-start(bf16[2,64,1024]{2,1,0:T(8,128)(2,1)S(1)} %pad_maximum_fusion.3), channel_id=1, source_target_pairs={{0,2},{1,3},{2,0},{3,1},{4,6},{5,7},{6,4},{7,5},{8,10},{9,11},{10,... | collective-permute-start | bytes 786440 | tf_op jit(solution)/shard_map/ppermute | solution.py:117
  24.2 10.7 %collective-permute-start.8 = (bf16[2,64,1024]{2,1,0:T(8,128)(2,1)}, bf16[2,64,1024]{2,1,0:T(8,128)(2,1)S(1)}, u32[]{:S(2)}, u32[]{:S(2)}) collective-permute-start(bf16[2,64,1024]{2,1,0:T(8,128)(2,1)} %pad_maximum_fusion.4), channel_id=1, source_target_pairs={{0,2},{1,3},{2,0},{3,1},{4,6},{5,7},{6,4},{7,5},{8,10},{9,11},{10,... | collective-permute-start | bytes 786440 | tf_op jit(solution)/shard_map/ppermute | solution.py:117
  25.8 12.0 %collective-permute-start.12 = (bf16[2,64,1024]{2,1,0:T(8,128)(2,1)S(1)}, bf16[2,64,1024]{2,1,0:T(8,128)(2,1)S(1)}, u32[]{:S(2)}, u32[]{:S(2)}) collective-permute-start(bf16[2,64,1024]{2,1,0:T(8,128)(2,1)S(1)} %pad_maximum_fusion.5), channel_id=1, source_target_pairs={{0,2},{1,3},{2,0},{3,1},{4,6},{5,7},{6,4},{7,5},{8,10},{9,11},{10,... | collective-permute-start | bytes 786440 | tf_op jit(solution)/shard_map/ppermute | solution.py:117
  26.5 11.4 %collective-permute-start.1 = (bf16[128,1024]{1,0:T(8,128)(2,1)}, bf16[128,1024]{1,0:T(8,128)(2,1)}, u32[]{:S(2)}, u32[]{:S(2)}) collective-permute-start(bf16[128,1024]{1,0:T(8,128)(2,1)} %collective-permute-done), channel_id=1, source_target_pairs={{0,1},{1,0},{2,3},{3,2},{4,5},{5,4},{6,7},{7,6},{8,9},{9,8},{10,11... | collective-permute-start | bytes 786440 | tf_op jit(solution)/shard_map/ppermute | solution.py:132
  30.6 11.9 %collective-permute-start.5 = (bf16[2,128,1024]{2,1,0:T(8,128)(2,1)S(1)}, bf16[2,128,1024]{2,1,0:T(8,128)(2,1)S(1)}, u32[]{:S(2)}, u32[]{:S(2)}) collective-permute-start(bf16[2,128,1024]{2,1,0:T(8,128)(2,1)S(1)} %pad_maximum_fusion), channel_id=1, source_target_pairs={{0,1},{1,0},{2,3},{3,2},{4,5},{5,4},{6,7},{7,6},{8,9},{9,8},{10,11... | collective-permute-start | bytes 1572872 | tf_op jit(solution)/shard_map/ppermute | solution.py:117
  35.0 8.6 %collective-permute-start.9 = (bf16[2,128,1024]{2,1,0:T(8,128)(2,1)S(1)}, bf16[2,128,1024]{2,1,0:T(8,128)(2,1)S(1)}, u32[]{:S(2)}, u32[]{:S(2)}) collective-permute-start(bf16[2,128,1024]{2,1,0:T(8,128)(2,1)S(1)} %pad_maximum_fusion.1), channel_id=1, source_target_pairs={{0,1},{1,0},{2,3},{3,2},{4,5},{5,4},{6,7},{7,6},{8,9},{9,8},{10,11... | collective-permute-start | bytes 1572872 | tf_op jit(solution)/shard_map/ppermute | solution.py:117
  37.8 6.8 %collective-permute-start.13 = (bf16[2,128,1024]{2,1,0:T(8,128)(2,1)S(1)}, bf16[2,128,1024]{2,1,0:T(8,128)(2,1)S(1)}, u32[]{:S(2)}, u32[]{:S(2)}) collective-permute-start(bf16[2,128,1024]{2,1,0:T(8,128)(2,1)S(1)} %pad_maximum_fusion.2), channel_id=1, source_target_pairs={{0,1},{1,0},{2,3},{3,2},{4,5},{5,4},{6,7},{7,6},{8,9},{9,8},{10,11... | collective-permute-start | bytes 1572872 | tf_op jit(solution)/shard_map/ppermute | solution.py:117
  68.7 3.4 %copy-start = (f32[2048,512]{1,0:T(8,128)S(1)}, f32[2048,512]{1,0:T(8,128)}, u32[]{:S(2)}) copy-start(f32[2048,512]{1,0:T(8,128)} %get-tuple-element.8) | copy-start | bytes 12582916
  72.2 1.6 %copy-start.1 = (f32[512,1024]{1,0:T(8,128)S(1)}, f32[512,1024]{1,0:T(8,128)}, u32[]{:S(2)}) copy-start(f32[512,1024]{1,0:T(8,128)} %param.4) | copy-start | bytes 6291460

commit v15 on v12

--- a/solution.py
+++ b/solution.py
@@ -82,7 +82,11 @@
 
     landed = [mine]
     for sz in range(1, n_o):
-        landed.append(lax.ppermute(mine, "outer", [(i, (i + sz) % n_o) for i in range(n_o)]))
+        if n_o & (n_o - 1) == 0:
+            pairs = [(i, i ^ sz) for i in range(n_o)]
+        else:
+            pairs = [(i, (i + sz) % n_o) for i in range(n_o)]
+        landed.append(lax.ppermute(mine, "outer", pairs))
     parts = [None] + [spread(pair_of(piece)) for piece in landed[1:]]
 
     h = q % 2
@@ -97,7 +101,8 @@
 
     cur = jnp.zeros((n_o * n_d,) + parts[0].shape[1:], parts[0].dtype)
     for sz in range(n_o):
-        cur = lax.dynamic_update_slice_in_dim(cur, parts[sz], ((z - sz) % n_o) * n_d, axis=0)
+        pod_of = (z ^ sz) if n_o & (n_o - 1) == 0 else (z - sz) % n_o
+        cur = lax.dynamic_update_slice_in_dim(cur, parts[sz], pod_of * n_d, axis=0)
     everything = cur.reshape(n_od * n_c * tq, d)
 
     logits = scores_for(everything, cent_bf, squares)

time: 71.9 us -> 70.6 us (0.982)
  starting transfers between devices: 15.3 us -> 13.9 us
    ppermute x3, waiting for transfers between devices: 2.28 us -> 5.31 us  [shards_all(): landed.append(lax.ppermute(mine, 'outer', pairs))]
    ppermute x3, waiting for transfers between devices: 3.9 us -> 1.27 us  [pair_of(): lax.ppermute(piece, 'dp', [(j, (j + sy) % n_d) for j in range(n_d)])]
    ppermute x3, starting transfers between devices: 7.01 us -> 5.68 us  [shards_all(): landed.append(lax.ppermute(mine, 'outer', pairs))]
where the time goes in v15:
time: 70.6 us; the launch traced here: 70.2 us
  other arithmetic  20 us (28%)
  waiting for transfers between devices  14.7 us (21%)
  starting transfers between devices  13.9 us (20%)
  blocking collectives  9.1 us (13%)
  matrix products  8.3 us (12%)
  local copies, waits for them, and re-layouts  3.83 us (5%)
    all_gather x1, blocking collectives, shards_all(): every = lax.all_gather(both, ('dp', 'cent'), axis=0)  9.1 us
    ppermute x6, waiting for transfers between devices, spread(): other = lax.ppermute(cur, 'cent', [(i, i ^ bit) for i in range(n_c)])  8.15 us
    ppermute x3, starting transfers between devices, shards_all(): landed.append(lax.ppermute(mine, 'outer', pairs))  5.68 us
    ppermute x3, waiting for transfers between devices, shards_all(): landed.append(lax.ppermute(mine, 'outer', pairs))  5.31 us
    dot_general x1, matrix products, scores_for(): lax.dot_general(piece, cent_bf, (((1,), (1,)), ((), ())), preferred_eleme...  4.62 us
    ppermute x6, starting transfers between devices, spread(): other = lax.ppermute(cur, 'cent', [(i, i ^ bit) for i in range(n_c)])  4.06 us
    dot_general x1, matrix products, shards_all(): lax.dot_general(scaled.reshape(n_o * pod, k), everything, (((0,), (0,)),...  3.68 us
    dynamic_update_slice x4, other arithmetic, shards_all(): cur = lax.dynamic_update_slice_in_dim(cur, parts[sz], pod_of * n_d, axis=0)  3.35 us
  transfers between devices with their start and end apart: 14, of which 6 were waited for; matrix products, arithmetic and copies ran while one was open for 16% of the time, Pallas kernels for 0%

profile of v15, /device:TPU:0, one launch (start us, length us, event | category | flops | bytes accessed | tf_op | source)
XLA Modules:
  0.0 70.2 jit_solution(15322130343523266568)
XLA Ops:
  0.0 1.4 %convert_element_type.22 = bf16[256,1024]{1,0:T(8,128)(2,1)S(1)} convert(f32[256,1024]{1,0:T(8,128)} %param.3) | non-fusion elementwise | flops 262144 | bytes 1572864 | tf_op jit(solution)/shard_map/convert_element_type | solution.py:56
  1.5 3.1 %collective-permute-start.2 = (bf16[64,1024]{1,0:T(8,128)(2,1)S(1)}, bf16[64,1024]{1,0:T(8,128)(2,1)S(1)}, u32[]{:S(2)}, u32[]{:S(2)}) collective-permute-start(bf16[64,1024]{1,0:T(8,128)(2,1)S(1)} %constant_dynamic-slice_fusion), channel_id=1, source_target_pairs={{0,8},{8,0},{16,24},{24,16},{1,9},{9,1},{17,25},{25,17},{2,10},{10... | collective-permute-start | bytes 393224 | tf_op jit(solution)/shard_map/ppermute | solution.py:89
  4.6 2.6 %collective-permute-start.6 = (bf16[64,1024]{1,0:T(8,128)(2,1)S(1)}, bf16[64,1024]{1,0:T(8,128)(2,1)S(1)}, u32[]{:S(2)}, u32[]{:S(2)}) collective-permute-start(bf16[64,1024]{1,0:T(8,128)(2,1)S(1)} %constant_dynamic-slice_fusion), channel_id=1, source_target_pairs={{0,16},{8,24},{16,0},{24,8},{1,17},{9,25},{17,1},{25,9},{2,18},{10... | collective-permute-start | bytes 393224 | tf_op jit(solution)/shard_map/ppermute | solution.py:89
  7.2 0.0 collective-permute-start.10
  7.2 0.7 %constant_dynamic-slice_fusion.1 = bf16[128,1024]{1,0:T(8,128)(2,1)} fusion(bf16[256,1024]{1,0:T(8,128)(2,1)S(1)} %convert_element_type.22, s32[]{:T(128)S(6)} %select_n.127), kind=kLoop, calls=%fused_computation.49 | loop fusion | bytes 524292 | tf_op jit(solution)/shard_map/dynamic_slice | solution.py:94
  7.9 1.7 %collective-permute-start = (bf16[128,1024]{1,0:T(8,128)(2,1)}, bf16[128,1024]{1,0:T(8,128)(2,1)}, u32[]{:S(2)}, u32[]{:S(2)}) collective-permute-start(bf16[128,1024]{1,0:T(8,128)(2,1)} %constant_dynamic-slice_fusion.1), channel_id=1, source_target_pairs={{0,4},{4,0},{1,5},{5,1},{2,6},{6,2},{3,7},{7,3},{8,12},{12,8},{9,1... | collective-permute-start | bytes 786440 | tf_op jit(solution)/shard_map/ppermute | solution.py:97
  9.6 1.3 %convert_bitcast_fusion = bf16[1,256,1024]{2,1,0:T(8,128)(2,1)S(1)} fusion(f32[256,1024]{1,0:T(8,128)} %param.3), kind=kLoop, calls=%fused_computation.74 | loop fusion | flops 262144 | bytes 1572864 | tf_op jit(solution)/shard_map/stack | solution.py:100
  11.0 0.7 fusion.17
  11.7 0.1 copy.27
  11.7 0.1 stack.128
  11.8 0.0 collective-permute-done.2
  11.8 0.4 collective-permute-start.3
  12.2 5.3 %collective-permute-done.6 = bf16[64,1024]{1,0:T(8,128)(2,1)S(1)} collective-permute-done((bf16[64,1024]{1,0:T(8,128)(2,1)S(1)}, bf16[64,1024]{1,0:T(8,128)(2,1)S(1)}, u32[]{:S(2)}, u32[]{:S(2)}) %collective-permute-start.6) | collective-permute-done | bytes 131104 | tf_op jit(solution)/shard_map/ppermute | solution.py:89
  17.5 1.5 %collective-permute-start.7 = (bf16[64,1024]{1,0:T(8,128)(2,1)S(1)}, bf16[64,1024]{1,0:T(8,128)(2,1)S(1)}, u32[]{:S(2)}, u32[]{:S(2)}) collective-permute-start(bf16[64,1024]{1,0:T(8,128)(2,1)S(1)} %collective-permute-done.6), channel_id=1, source_target_pairs={{0,4},{4,0},{1,5},{5,1},{2,6},{6,2},{3,7},{7,3},{8,12},{12,8},{9,1... | collective-permute-start | bytes 393224 | tf_op jit(solution)/shard_map/ppermute | solution.py:74
  19.0 0.0 collective-permute-done.10
  19.0 0.5 collective-permute-start.11
  19.5 0.6 collective-permute-done.3
  20.2 1.8 %collective-permute-start.4 = (bf16[2,64,1024]{2,1,0:T(8,128)(2,1)S(1)}, bf16[2,64,1024]{2,1,0:T(8,128)(2,1)S(1)}, u32[]{:S(2)}, u32[]{:S(2)}) collective-permute-start(bf16[2,64,1024]{2,1,0:T(8,128)(2,1)S(1)} %pad_maximum_fusion.3), channel_id=1, source_target_pairs={{0,2},{1,3},{2,0},{3,1},{4,6},{5,7},{6,4},{7,5},{8,10},{9,11},{10,... | collective-permute-start | bytes 786440 | tf_op jit(solution)/shard_map/ppermute | solution.py:79
  22.0 0.6 collective-permute-done.7
  22.6 0.7 %pad_maximum_fusion.4 = bf16[2,64,1024]{2,1,0:T(8,128)(2,1)} fusion(bf16[1,64,1024]{2,1,0:T(8,128)(2,1)S(1)} %bitcast.84, bf16[1,64,1024]{2,1,0:T(8,128)(2,1)S(1)} %bitcast.75), kind=kLoop, calls=%fused_computation.19 | loop fusion | flops 131072 | bytes 524288 | tf_op jit(solution)/shard_map/stack | solution.py:75
  23.3 1.5 %collective-permute-start.8 = (bf16[2,64,1024]{2,1,0:T(8,128)(2,1)}, bf16[2,64,1024]{2,1,0:T(8,128)(2,1)}, u32[]{:S(2)}, u32[]{:S(2)}) collective-permute-start(bf16[2,64,1024]{2,1,0:T(8,128)(2,1)} %pad_maximum_fusion.4), channel_id=1, source_target_pairs={{0,2},{1,3},{2,0},{3,1},{4,6},{5,7},{6,4},{7,5},{8,10},{9,11},{10,... | collective-permute-start | bytes 786440 | tf_op jit(solution)/shard_map/ppermute | solution.py:79
  24.8 0.0 collective-permute-done.11
  24.8 0.8 %pad_maximum_fusion.5 = bf16[2,64,1024]{2,1,0:T(8,128)(2,1)} fusion(bf16[1,64,1024]{2,1,0:T(8,128)(2,1)S(1)} %bitcast.81, bf16[1,64,1024]{2,1,0:T(8,128)(2,1)S(1)} %bitcast.72), kind=kLoop, calls=%fused_computation.20 | loop fusion | flops 131072 | bytes 524288 | tf_op jit(solution)/shard_map/stack | solution.py:75
  25.6 0.7 collective-permute-start.12
  26.2 0.0 collective-permute-done
  26.3 0.0 collective-permute-start.1
  26.3 3.1 %collective-permute-done.4 = bf16[2,64,1024]{2,1,0:T(8,128)(2,1)S(1)} collective-permute-done((bf16[2,64,1024]{2,1,0:T(8,128)(2,1)S(1)}, bf16[2,64,1024]{2,1,0:T(8,128)(2,1)S(1)}, u32[]{:S(2)}, u32[]{:S(2)}) %collective-permute-start.4) | collective-permute-done | bytes 262176 | tf_op jit(solution)/shard_map/ppermute | solution.py:79
  29.4 0.7 %copy-done.4 = bf16[2,64,1024]{2,1,0:T(8,128)(2,1)} copy-done((bf16[2,64,1024]{2,1,0:T(8,128)(2,1)}, bf16[2,64,1024]{2,1,0:T(8,128)(2,1)S(1)}, u32[]{:S(2)}) %copy-start.4) | copy-done | bytes 262168
  30.1 0.8 %pad_maximum_fusion = bf16[2,128,1024]{2,1,0:T(8,128)(2,1)} fusion(bf16[2,64,1024]{2,1,0:T(8,128)(2,1)S(1)} %collective-permute-done.4, bf16[1,64,1024]{2,1,0:T(8,128)(2,1)S(1)} %bitcast.88, bf16[1,64,1024]{2,1,0:T(8,128)(2,1)S(1)} %bitcast.79), kind=kLoop, calls=%fused_computation.15 | loop fusion | flops 1572864 | bytes 1048576 | tf_op jit(solution)/shard_map/concatenate | solution.py:80
  30.9 0.0 collective-permute-start.5
  30.9 0.0 copy-done.3
  30.9 0.2 multiply_reduce_fusion
  31.1 3.3 %collective-permute-done.8 = bf16[2,64,1024]{2,1,0:T(8,128)(2,1)} collective-permute-done((bf16[2,64,1024]{2,1,0:T(8,128)(2,1)}, bf16[2,64,1024]{2,1,0:T(8,128)(2,1)}, u32[]{:S(2)}, u32[]{:S(2)}) %collective-permute-start.8) | collective-permute-done | bytes 262176 | tf_op jit(solution)/shard_map/ppermute | solution.py:79
  34.4 1.0 %pad_maximum_fusion.1 = bf16[2,128,1024]{2,1,0:T(8,128)(2,1)S(1)} fusion(bf16[2,64,1024]{2,1,0:T(8,128)(2,1)} %collective-permute-done.8, bf16[1,64,1024]{2,1,0:T(8,128)(2,1)S(1)} %bitcast.85, bf16[1,64,1024]{2,1,0:T(8,128)(2,1)S(1)} %bitcast.76), kind=kLoop, calls=%fused_computation.16 | loop fusion | flops 1572864 | bytes 1048576 | tf_op jit(solution)/shard_map/concatenate | solution.py:80
  35.4 0.1 collective-permute-start.9
  35.5 1.7 %collective-permute-done.12 = bf16[2,64,1024]{2,1,0:T(8,128)(2,1)} collective-permute-done((bf16[2,64,1024]{2,1,0:T(8,128)(2,1)}, bf16[2,64,1024]{2,1,0:T(8,128)(2,1)}, u32[]{:S(2)}, u32[]{:S(2)}) %collective-permute-start.12) | collective-permute-done | bytes 262176 | tf_op jit(solution)/shard_map/ppermute | solution.py:79
  37.2 1.0 %pad_maximum_fusion.2 = bf16[2,128,1024]{2,1,0:T(8,128)(2,1)S(1)} fusion(bf16[2,64,1024]{2,1,0:T(8,128)(2,1)} %collective-permute-done.12, bf16[1,64,1024]{2,1,0:T(8,128)(2,1)S(1)} %bitcast.82, bf16[1,64,1024]{2,1,0:T(8,128)(2,1)S(1)} %bitcast.73), kind=kLoop, calls=%fused_computation.17 | loop fusion | flops 1572864 | bytes 1048576 | tf_op jit(solution)/shard_map/concatenate | solution.py:80
  38.2 0.1 collective-permute-start.13
  38.3 0.0 collective-permute-done.1
  38.3 1.1 %maximum_bitcast_fusion = bf16[1,256,1024]{2,1,0:T(8,128)(2,1)S(1)} fusion(bf16[128,1024]{1,0:T(8,128)(2,1)} %collective-permute-done.1, bf16[128,1024]{1,0:T(8,128)(2,1)} %collective-permute-done), kind=kLoop, calls=%fused_computation.14 | loop fusion | flops 1048576 | bytes 1048576 | tf_op jit(solution)/shard_map/stack | solution.py:100
  39.4 0.5 broadcast_in_dim.138
  39.9 0.1 maximum_dynamic-update-slice_fusion
  40.0 0.0 collective-permute-done.5
  40.0 1.1 %maximum_dynamic-update-slice_fusion.1 = bf16[8,256,1024]{2,1,0:T(8,128)(2,1)S(1)} fusion(bf16[8,256,1024]{2,1,0:T(8,128)(2,1)S(1)} %maximum_dynamic-update-slice_fusion, s32[]{:T(128)S(6)} %select_n.130, bf16[2,128,1024]{2,1,0:T(8,128)(2,1)} %collective-permute-done.5, bf16[2,64,1024]{2,1,0:T(8,128)(2,1)S(1)} %copy-done.5, ...), kind=kLoop, calls=%fused_computation.10 | loop fusion | flops 4194304 | bytes 2097156 | tf_op jit(solution)/shard_map/dynamic_update_slice | solution.py:105
  41.2 0.0 collective-permute-done.9
  41.2 1.1 %maximum_dynamic-update-slice_fusion.2 = bf16[8,256,1024]{2,1,0:T(8,128)(2,1)S(1)} fusion(bf16[8,256,1024]{2,1,0:T(8,128)(2,1)S(1)} %maximum_dynamic-update-slice_fusion.1, s32[]{:T(128)S(6)} %select_n.131, bf16[2,128,1024]{2,1,0:T(8,128)(2,1)S(1)} %collective-permute-done.9, bf16[2,64,1024]{2,1,0:T(8,128)(2,1)} %collective-permute-done.8, ...), kind=kLoop, calls=%fused_computation.11 | loop fusion | flops 4194304 | bytes 2097156 | tf_op jit(solution)/shard_map/dynamic_update_slice | solution.py:105
  42.3 0.0 collective-permute-done.13
  42.3 1.1 %maximum_dynamic-update-slice_fusion.3 = bf16[8,256,1024]{2,1,0:T(8,128)(2,1)S(1)} fusion(bf16[8,256,1024]{2,1,0:T(8,128)(2,1)S(1)} %maximum_dynamic-update-slice_fusion.2, s32[]{:T(128)S(6)} %select_n.132, bf16[2,128,1024]{2,1,0:T(8,128)(2,1)S(1)} %collective-permute-done.13, bf16[2,64,1024]{2,1,0:T(8,128)(2,1)} %collective-permute-done.12, ...), kind=kLoop, calls=%fused_computation.12 | loop fusion | flops 4194304 | bytes 2097156 | tf_op jit(solution)/shard_map/dynamic_update_slice | solution.py:105
  43.3 4.6 %fusion.21 = (f32[2048]{0:T(1024)S(1)}, f32[2048,512]{1,0:T(8,128)}) fusion(f32[512]{0:T(512)S(1)} %multiply_reduce_fusion, bf16[2048,1024]{1,0:T(8,128)(2,1)S(1)} %bitcast.68, f32[512,1024]{1,0:T(8,128)S(1)} %copy-done.3), kind=kOutput, calls=%fused_computation.73 | convolution fusion | flops 2152200192 | bytes 10496000 | tf_op jit(solution)/shard_map/dot_general | solution.py:10
  48.0 0.1 broadcast_in_dim.141
  48.0 3.3 %exponential_reduce_fusion = f32[2048]{0:T(1024)S(1)} fusion(f32[2048,512]{1,0:T(8,128)} %get-tuple-element.26, f32[2048]{0:T(1024)S(1)} %get-tuple-element.25), kind=kLoop, calls=%fused_computation.4 | loop fusion | flops 2095104 | bytes 4210688 | tf_op jit(solution)/shard_map/reduce_sum | solution.py:18
  51.4 0.1 broadcast_in_dim.146
  51.5 0.1 select_reduce_fusion.7
  51.6 0.2 select_reduce_fusion.3
  51.8 9.1 %all-gather = f32[16,8,4,64]{3,1,2,0:T(8,128)S(1)} all-gather(f32[2,8,4,64]{3,1,2,0:T(8,128)S(1)} %copy.30), channel_id=2, replica_groups=mesh['outer'=4,'dp'=2,'cent'=4] {'dp','cent'}, dimensions={0}, use_global_device_ids=true | all-gather | bytes 147456 | tf_op jit(solution)/shard_map/all_gather | solution.py:135
  61.0 0.1 select_reduce_fusion.1
  61.1 0.1 select_reduce_fusion.5
  61.2 0.1 div.62
  61.3 0.1 sub.53
  61.3 2.8 %bitcast_reduce_fusion = f32[4,512]{1,0:T(4,128)S(1)} fusion(f32[2048]{0:T(1024)S(1)} %div.62, f32[2048,512]{1,0:T(8,128)} %get-tuple-element.26, f32[2048]{0:T(1024)S(1)} %sub.53), kind=kLoop, calls=%fused_computation.2 | loop fusion | flops 5240832 | bytes 4218880 | tf_op jit(solution)/shard_map/reduce_sum | solution.py:146
  64.2 0.6 copy-done
  64.8 1.0 %fusion = bf16[2048,512]{1,0:T(8,128)(2,1)S(1)} fusion(f32[4,512]{1,0:T(4,128)S(1)} %broadcast_add_fusion, f32[2048]{0:T(1024)S(1)} %div.62, f32[2048,512]{1,0:T(8,128)S(1)} %copy-done, f32[2048]{0:T(1024)S(1)} %sub.53), kind=kLoop, calls=%fused_computation.1 | loop fusion | flops 6291456 | bytes 6316032 | tf_op jit(solution)/shard_map/convert_element_type | solution.py:147
  65.8 0.7 %copy-done.2 = bf16[8,256,1024]{2,1,0:T(8,128)(2,1)S(1)} copy-done((bf16[8,256,1024]{2,1,0:T(8,128)(2,1)S(1)}, bf16[8,256,1024]{2,1,0:T(8,128)(2,1)}, u32[]{:S(2)}) %copy-start.2) | copy-done | bytes 4194328
  66.5 3.7 %subtract_multiply_fusion.1 = f32[512,1024]{1,0:T(8,128)} fusion(f32[512,1024]{1,0:T(8,128)S(1)} %copy-done.3, bf16[2048,512]{1,0:T(8,128)(2,1)S(1)} %fusion, bf16[2048,1024]{1,0:T(8,128)(2,1)S(1)} %bitcast.69, f32[512]{0:T(512)S(1)} %fusion.8), kind=kOutput, calls=%fused_computation.7 | convolution fusion | flops 2149056512 | bytes 10487808 | tf_op jit(solution)/shard_map/dot_general | solution.py:148
  (26 shorter events, 0.2 us)
Async XLA Ops:
  0.0 30.9 %copy-start.3 = (f32[512,1024]{1,0:T(8,128)S(1)}, f32[512,1024]{1,0:T(8,128)}, u32[]{:S(2)}) copy-start(f32[512,1024]{1,0:T(8,128)} %param.4) | copy-start | bytes 6291460
  1.5 10.3 %collective-permute-start.2 = (bf16[64,1024]{1,0:T(8,128)(2,1)S(1)}, bf16[64,1024]{1,0:T(8,128)(2,1)S(1)}, u32[]{:S(2)}, u32[]{:S(2)}) collective-permute-start(bf16[64,1024]{1,0:T(8,128)(2,1)S(1)} %constant_dynamic-slice_fusion), channel_id=1, source_target_pairs={{0,8},{8,0},{16,24},{24,16},{1,9},{9,1},{17,25},{25,17},{2,10},{10... | collective-permute-start | bytes 393224 | tf_op jit(solution)/shard_map/ppermute | solution.py:89
  4.6 12.9 %collective-permute-start.6 = (bf16[64,1024]{1,0:T(8,128)(2,1)S(1)}, bf16[64,1024]{1,0:T(8,128)(2,1)S(1)}, u32[]{:S(2)}, u32[]{:S(2)}) collective-permute-start(bf16[64,1024]{1,0:T(8,128)(2,1)S(1)} %constant_dynamic-slice_fusion), channel_id=1, source_target_pairs={{0,16},{8,24},{16,0},{24,8},{1,17},{9,25},{17,1},{25,9},{2,18},{10... | collective-permute-start | bytes 393224 | tf_op jit(solution)/shard_map/ppermute | solution.py:89
  7.2 11.9 %collective-permute-start.10 = (bf16[64,1024]{1,0:T(8,128)(2,1)S(1)}, bf16[64,1024]{1,0:T(8,128)(2,1)S(1)}, u32[]{:S(2)}, u32[]{:S(2)}) collective-permute-start(bf16[64,1024]{1,0:T(8,128)(2,1)S(1)} %constant_dynamic-slice_fusion), channel_id=1, source_target_pairs={{0,24},{8,16},{16,8},{24,0},{1,25},{9,17},{17,9},{25,1},{2,26},{10... | collective-permute-start | bytes 393224 | tf_op jit(solution)/shard_map/ppermute | solution.py:89
  7.9 18.4 %collective-permute-start = (bf16[128,1024]{1,0:T(8,128)(2,1)}, bf16[128,1024]{1,0:T(8,128)(2,1)}, u32[]{:S(2)}, u32[]{:S(2)}) collective-permute-start(bf16[128,1024]{1,0:T(8,128)(2,1)} %constant_dynamic-slice_fusion.1), channel_id=1, source_target_pairs={{0,4},{4,0},{1,5},{5,1},{2,6},{6,2},{3,7},{7,3},{8,12},{12,8},{9,1... | collective-permute-start | bytes 786440 | tf_op jit(solution)/shard_map/ppermute | solution.py:97
  11.8 8.3 %collective-permute-start.3 = (bf16[64,1024]{1,0:T(8,128)(2,1)S(1)}, bf16[64,1024]{1,0:T(8,128)(2,1)S(1)}, u32[]{:S(2)}, u32[]{:S(2)}) collective-permute-start(bf16[64,1024]{1,0:T(8,128)(2,1)S(1)} %collective-permute-done.2), channel_id=1, source_target_pairs={{0,4},{4,0},{1,5},{5,1},{2,6},{6,2},{3,7},{7,3},{8,12},{12,8},{9,1... | collective-permute-start | bytes 393224 | tf_op jit(solution)/shard_map/ppermute | solution.py:74
  17.5 5.1 %collective-permute-start.7 = (bf16[64,1024]{1,0:T(8,128)(2,1)S(1)}, bf16[64,1024]{1,0:T(8,128)(2,1)S(1)}, u32[]{:S(2)}, u32[]{:S(2)}) collective-permute-start(bf16[64,1024]{1,0:T(8,128)(2,1)S(1)} %collective-permute-done.6), channel_id=1, source_target_pairs={{0,4},{4,0},{1,5},{5,1},{2,6},{6,2},{3,7},{7,3},{8,12},{12,8},{9,1... | collective-permute-start | bytes 393224 | tf_op jit(solution)/shard_map/ppermute | solution.py:74
  19.0 5.8 %collective-permute-start.11 = (bf16[64,1024]{1,0:T(8,128)(2,1)S(1)}, bf16[64,1024]{1,0:T(8,128)(2,1)S(1)}, u32[]{:S(2)}, u32[]{:S(2)}) collective-permute-start(bf16[64,1024]{1,0:T(8,128)(2,1)S(1)} %collective-permute-done.10), channel_id=1, source_target_pairs={{0,4},{4,0},{1,5},{5,1},{2,6},{6,2},{3,7},{7,3},{8,12},{12,8},{9,1... | collective-permute-start | bytes 393224 | tf_op jit(solution)/shard_map/ppermute | solution.py:74
  20.2 9.2 %collective-permute-start.4 = (bf16[2,64,1024]{2,1,0:T(8,128)(2,1)S(1)}, bf16[2,64,1024]{2,1,0:T(8,128)(2,1)S(1)}, u32[]{:S(2)}, u32[]{:S(2)}) collective-permute-start(bf16[2,64,1024]{2,1,0:T(8,128)(2,1)S(1)} %pad_maximum_fusion.3), channel_id=1, source_target_pairs={{0,2},{1,3},{2,0},{3,1},{4,6},{5,7},{6,4},{7,5},{8,10},{9,11},{10,... | collective-permute-start | bytes 786440 | tf_op jit(solution)/shard_map/ppermute | solution.py:79
  23.3 11.1 %collective-permute-start.8 = (bf16[2,64,1024]{2,1,0:T(8,128)(2,1)}, bf16[2,64,1024]{2,1,0:T(8,128)(2,1)}, u32[]{:S(2)}, u32[]{:S(2)}) collective-permute-start(bf16[2,64,1024]{2,1,0:T(8,128)(2,1)} %pad_maximum_fusion.4), channel_id=1, source_target_pairs={{0,2},{1,3},{2,0},{3,1},{4,6},{5,7},{6,4},{7,5},{8,10},{9,11},{10,... | collective-permute-start | bytes 786440 | tf_op jit(solution)/shard_map/ppermute | solution.py:79
  25.6 11.7 %collective-permute-start.12 = (bf16[2,64,1024]{2,1,0:T(8,128)(2,1)}, bf16[2,64,1024]{2,1,0:T(8,128)(2,1)}, u32[]{:S(2)}, u32[]{:S(2)}) collective-permute-start(bf16[2,64,1024]{2,1,0:T(8,128)(2,1)} %pad_maximum_fusion.5), channel_id=1, source_target_pairs={{0,2},{1,3},{2,0},{3,1},{4,6},{5,7},{6,4},{7,5},{8,10},{9,11},{10,... | collective-permute-start | bytes 786440 | tf_op jit(solution)/shard_map/ppermute | solution.py:79
  26.3 12.1 %collective-permute-start.1 = (bf16[128,1024]{1,0:T(8,128)(2,1)}, bf16[128,1024]{1,0:T(8,128)(2,1)}, u32[]{:S(2)}, u32[]{:S(2)}) collective-permute-start(bf16[128,1024]{1,0:T(8,128)(2,1)} %collective-permute-done), channel_id=1, source_target_pairs={{0,1},{1,0},{2,3},{3,2},{4,5},{5,4},{6,7},{7,6},{8,9},{9,8},{10,11... | collective-permute-start | bytes 786440 | tf_op jit(solution)/shard_map/ppermute | solution.py:98
  29.4 0.7 %copy-start.4 = (bf16[2,64,1024]{2,1,0:T(8,128)(2,1)}, bf16[2,64,1024]{2,1,0:T(8,128)(2,1)S(1)}, u32[]{:S(2)}) copy-start(bf16[2,64,1024]{2,1,0:T(8,128)(2,1)S(1)} %collective-permute-done.4) | copy-start | bytes 786436
  30.9 9.1 %collective-permute-start.5 = (bf16[2,128,1024]{2,1,0:T(8,128)(2,1)}, bf16[2,128,1024]{2,1,0:T(8,128)(2,1)}, u32[]{:S(2)}, u32[]{:S(2)}) collective-permute-start(bf16[2,128,1024]{2,1,0:T(8,128)(2,1)} %pad_maximum_fusion), channel_id=1, source_target_pairs={{0,1},{1,0},{2,3},{3,2},{4,5},{5,4},{6,7},{7,6},{8,9},{9,8},{10,11... | collective-permute-start | bytes 1572872 | tf_op jit(solution)/shard_map/ppermute | solution.py:79
  35.4 4.6 %copy-start.5 = (bf16[2,64,1024]{2,1,0:T(8,128)(2,1)S(1)}, bf16[2,64,1024]{2,1,0:T(8,128)(2,1)}, u32[]{:S(2)}) copy-start(bf16[2,64,1024]{2,1,0:T(8,128)(2,1)} %copy-done.4) | copy-start | bytes 786436
  35.4 5.8 %collective-permute-start.9 = (bf16[2,128,1024]{2,1,0:T(8,128)(2,1)S(1)}, bf16[2,128,1024]{2,1,0:T(8,128)(2,1)S(1)}, u32[]{:S(2)}, u32[]{:S(2)}) collective-permute-start(bf16[2,128,1024]{2,1,0:T(8,128)(2,1)S(1)} %pad_maximum_fusion.1), channel_id=1, source_target_pairs={{0,1},{1,0},{2,3},{3,2},{4,5},{5,4},{6,7},{7,6},{8,9},{9,8},{10,11... | collective-permute-start | bytes 1572872 | tf_op jit(solution)/shard_map/ppermute | solution.py:79
  38.2 4.0 %collective-permute-start.13 = (bf16[2,128,1024]{2,1,0:T(8,128)(2,1)S(1)}, bf16[2,128,1024]{2,1,0:T(8,128)(2,1)S(1)}, u32[]{:S(2)}, u32[]{:S(2)}) collective-permute-start(bf16[2,128,1024]{2,1,0:T(8,128)(2,1)S(1)} %pad_maximum_fusion.2), channel_id=1, source_target_pairs={{0,1},{1,0},{2,3},{3,2},{4,5},{5,4},{6,7},{7,6},{8,9},{9,8},{10,11... | collective-permute-start | bytes 1572872 | tf_op jit(solution)/shard_map/ppermute | solution.py:79
  43.3 4.6 %copy-start.1 = (bf16[8,256,1024]{2,1,0:T(8,128)(2,1)}, bf16[8,256,1024]{2,1,0:T(8,128)(2,1)S(1)}, u32[]{:S(2)}) copy-start(bf16[8,256,1024]{2,1,0:T(8,128)(2,1)S(1)} %maximum_dynamic-update-slice_fusion.3) | copy-start | bytes 12582916
  61.3 3.4 %copy-start = (f32[2048,512]{1,0:T(8,128)S(1)}, f32[2048,512]{1,0:T(8,128)}, u32[]{:S(2)}) copy-start(f32[2048,512]{1,0:T(8,128)} %get-tuple-element.26) | copy-start | bytes 12582916
  64.2 2.3 %copy-start.2 = (bf16[8,256,1024]{2,1,0:T(8,128)(2,1)S(1)}, bf16[8,256,1024]{2,1,0:T(8,128)(2,1)}, u32[]{:S(2)}) copy-start(bf16[8,256,1024]{2,1,0:T(8,128)(2,1)} %copy-done.1) | copy-start | bytes 12582916

commit v16 on v15

--- a/solution.py
+++ b/solution.py
@@ -87,7 +87,19 @@
         else:
             pairs = [(i, (i + sz) % n_o) for i in range(n_o)]
         landed.append(lax.ppermute(mine, "outer", pairs))
-    parts = [None] + [spread(pair_of(piece)) for piece in landed[1:]]
+    def spread_x_first(piece):
+        order = list(reversed(bits))
+        other = lax.ppermute(piece, "cent", [(i, i ^ order[0]) for i in range(n_c)])
+        cur = pair_of(jnp.concatenate([piece, other], axis=0))
+        for bit in order[1:]:
+            other = lax.ppermute(cur, "cent", [(i, i ^ bit) for i in range(n_c)])
+            cur = jnp.concatenate([cur, other], axis=1)
+        return cur
+
+    parts = [None] + [
+        spread_x_first(piece) if sz == 1 else spread(pair_of(piece))
+        for sz, piece in enumerate(landed[1:], start=1)
+    ]
 
     h = q % 2
     half = t // 2

time: 70.6 us -> 67.8 us (0.960)
  waiting for transfers between devices: 14.7 us -> 9.77 us
  local copies, waits for them, and re-layouts: 3.83 us -> 4.75 us
  starting transfers between devices: 13.9 us -> 14.8 us
    ppermute x6 -> x4, waiting for transfers between devices: 8.15 us -> 3.14 us  [spread(): other = lax.ppermute(cur, 'cent', [(i, i ^ bit) for i in range(n_c)])]
    ppermute x6 -> x4, starting transfers between devices: 4.06 us -> 2.32 us  [spread(): other = lax.ppermute(cur, 'cent', [(i, i ^ bit) for i in range(n_c)])]
    ppermute x0 -> x2, starting transfers between devices: none -> 1.49 us  [the longest x1 1.49 us: spread_x_first(): other = lax.ppermute(piece, 'cent', [(i, i ^ order[0]) for i in range(n_c)])]
    ppermute x3, starting transfers between devices: 2.38 us -> 3.61 us  [pair_of(): lax.ppermute(piece, 'dp', [(j, (j + sy) % n_d) for j in range(n_d)])]
    ppermute x3, waiting for transfers between devices: 1.27 us -> 2.41 us  [pair_of(): lax.ppermute(piece, 'dp', [(j, (j + sy) % n_d) for j in range(n_d)])]
    ppermute x3, waiting for transfers between devices: 5.31 us -> 4.2 us  [shards_all(): landed.append(lax.ppermute(mine, 'outer', pairs))]
    concatenate x0 -> x1, local copies, waits for them, and re-layouts: none -> 0.91 us  [spread_x_first(): cur = pair_of(jnp.concatenate([piece, other], axis=0))]
    concatenate x3 -> x2, other arithmetic: 2.8 us -> 1.97 us  [spread(): cur = jnp.concatenate([cur, other], axis=1)]
  transfers between devices with their start and end apart: 14 -> 14, of which waited for: 6 -> 5; matrix products, arithmetic and copies ran while one was open for 16% -> 18% of each run, Pallas kernels for 0% -> 0%
where the time goes in v16:
time: 67.8 us; the launch traced here: 67.3 us
  other arithmetic  20 us (29%)
  starting transfers between devices  14.8 us (22%)
  waiting for transfers between devices  9.77 us (14%)
  blocking collectives  9.29 us (14%)
  matrix products  8.3 us (12%)
  local copies, waits for them, and re-layouts  4.75 us (7%)
    all_gather x1, blocking collectives, shards_all(): every = lax.all_gather(both, ('dp', 'cent'), axis=0)  9.29 us
    ppermute x3, starting transfers between devices, shards_all(): landed.append(lax.ppermute(mine, 'outer', pairs))  5.68 us
    dot_general x1, matrix products, scores_for(): lax.dot_general(piece, cent_bf, (((1,), (1,)), ((), ())), preferred_eleme...  4.62 us
    ppermute x3, waiting for transfers between devices, shards_all(): landed.append(lax.ppermute(mine, 'outer', pairs))  4.2 us
    dot_general x1, matrix products, shards_all(): lax.dot_general(scaled.reshape(n_o * pod, k), everything, (((0,), (0,)),...  3.68 us
    ppermute x3, starting transfers between devices, pair_of(): lax.ppermute(piece, 'dp', [(j, (j + sy) % n_d) for j in range(n_d)])  3.61 us
    dynamic_update_slice x4, other arithmetic, shards_all(): cur = lax.dynamic_update_slice_in_dim(cur, parts[sz], pod_of * n_d, axis=0)  3.35 us
    reduce_sum x1, other arithmetic, row_summary(): local_sum = jnp.sum(jnp.exp(logits - local_max[:, None]), axis=1)  3.31 us
  transfers between devices with their start and end apart: 14, of which 5 were waited for; matrix products, arithmetic and copies ran while one was open for 18% of the time, Pallas kernels for 0%

profile of v16, /device:TPU:0, one launch (start us, length us, event | category | flops | bytes accessed | tf_op | source)
XLA Modules:
  0.0 67.3 jit_solution(7568332179244507702)
XLA Ops:
  0.0 1.4 %convert_element_type.22 = bf16[256,1024]{1,0:T(8,128)(2,1)S(1)} convert(f32[256,1024]{1,0:T(8,128)} %param.3) | non-fusion elementwise | flops 262144 | bytes 1572864 | tf_op jit(solution)/shard_map/convert_element_type | solution.py:56
  1.5 3.1 %collective-permute-start.2 = (bf16[64,1024]{1,0:T(8,128)(2,1)S(1)}, bf16[64,1024]{1,0:T(8,128)(2,1)S(1)}, u32[]{:S(2)}, u32[]{:S(2)}) collective-permute-start(bf16[64,1024]{1,0:T(8,128)(2,1)S(1)} %constant_dynamic-slice_fusion), channel_id=1, source_target_pairs={{0,8},{8,0},{16,24},{24,16},{1,9},{9,1},{17,25},{25,17},{2,10},{10... | collective-permute-start | bytes 393224 | tf_op jit(solution)/shard_map/ppermute | solution.py:89
  4.6 2.6 %collective-permute-start.6 = (bf16[64,1024]{1,0:T(8,128)(2,1)S(1)}, bf16[64,1024]{1,0:T(8,128)(2,1)S(1)}, u32[]{:S(2)}, u32[]{:S(2)}) collective-permute-start(bf16[64,1024]{1,0:T(8,128)(2,1)S(1)} %constant_dynamic-slice_fusion), channel_id=1, source_target_pairs={{0,16},{8,24},{16,0},{24,8},{1,17},{9,25},{17,1},{25,9},{2,18},{10... | collective-permute-start | bytes 393224 | tf_op jit(solution)/shard_map/ppermute | solution.py:89
  7.2 0.0 collective-permute-start.10
  7.2 0.7 %constant_dynamic-slice_fusion.1 = bf16[128,1024]{1,0:T(8,128)(2,1)} fusion(bf16[256,1024]{1,0:T(8,128)(2,1)S(1)} %convert_element_type.22, s32[]{:T(128)S(6)} %select_n.127), kind=kLoop, calls=%fused_computation.50 | loop fusion | bytes 524292 | tf_op jit(solution)/shard_map/dynamic_slice | solution.py:106
  7.9 1.7 %collective-permute-start = (bf16[128,1024]{1,0:T(8,128)(2,1)}, bf16[128,1024]{1,0:T(8,128)(2,1)}, u32[]{:S(2)}, u32[]{:S(2)}) collective-permute-start(bf16[128,1024]{1,0:T(8,128)(2,1)} %constant_dynamic-slice_fusion.1), channel_id=1, source_target_pairs={{0,4},{4,0},{1,5},{5,1},{2,6},{6,2},{3,7},{7,3},{8,12},{12,8},{9,1... | collective-permute-start | bytes 786440 | tf_op jit(solution)/shard_map/ppermute | solution.py:109
  9.6 1.3 %convert_bitcast_fusion = bf16[1,256,1024]{2,1,0:T(8,128)(2,1)S(1)} fusion(f32[256,1024]{1,0:T(8,128)} %param.3), kind=kLoop, calls=%fused_computation.75 | loop fusion | flops 262144 | bytes 1572864 | tf_op jit(solution)/shard_map/stack | solution.py:112
  10.9 0.7 fusion.17
  11.6 0.1 copy.27
  11.7 0.0 collective-permute-done.2
  11.7 1.5 %collective-permute-start.3 = (bf16[64,1024]{1,0:T(8,128)(2,1)S(1)}, bf16[64,1024]{1,0:T(8,128)(2,1)}, u32[]{:S(2)}, u32[]{:S(2)}) collective-permute-start(bf16[64,1024]{1,0:T(8,128)(2,1)S(1)} %collective-permute-done.2), channel_id=1, source_target_pairs={{0,2},{1,3},{2,0},{3,1},{4,6},{5,7},{6,4},{7,5},{8,10},{9,11},{10,... | collective-permute-start | bytes 393224 | tf_op jit(solution)/shard_map/ppermute | solution.py:92
  13.2 0.1 stack.128
  13.3 4.2 %collective-permute-done.6 = bf16[64,1024]{1,0:T(8,128)(2,1)S(1)} collective-permute-done((bf16[64,1024]{1,0:T(8,128)(2,1)S(1)}, bf16[64,1024]{1,0:T(8,128)(2,1)S(1)}, u32[]{:S(2)}, u32[]{:S(2)}) %collective-permute-start.6) | collective-permute-done | bytes 131104 | tf_op jit(solution)/shard_map/ppermute | solution.py:89
  17.5 1.5 %collective-permute-start.7 = (bf16[64,1024]{1,0:T(8,128)(2,1)S(1)}, bf16[64,1024]{1,0:T(8,128)(2,1)S(1)}, u32[]{:S(2)}, u32[]{:S(2)}) collective-permute-start(bf16[64,1024]{1,0:T(8,128)(2,1)S(1)} %collective-permute-done.6), channel_id=1, source_target_pairs={{0,4},{4,0},{1,5},{5,1},{2,6},{6,2},{3,7},{7,3},{8,12},{12,8},{9,1... | collective-permute-start | bytes 393224 | tf_op jit(solution)/shard_map/ppermute | solution.py:74
  19.0 0.0 collective-permute-done.10
  19.0 0.5 collective-permute-start.11
  19.5 0.0 collective-permute-done.3
  19.6 0.9 %constant_dynamic-update-slice_fusion = bf16[128,1024]{1,0:T(8,128)(2,1)S(1)} fusion(bf16[128,1024]{1,0:T(8,128)(2,1)S(1)} %constant_dynamic-update-slice_fusion.1, bf16[64,1024]{1,0:T(8,128)(2,1)} %collective-permute-done.3), kind=kLoop, calls=%fused_computation.36 | loop fusion | bytes 262144 | tf_op jit(solution)/shard_map/concatenate | solution.py:93
  20.5 1.6 %collective-permute-start.4 = (bf16[128,1024]{1,0:T(8,128)(2,1)S(1)}, bf16[128,1024]{1,0:T(8,128)(2,1)S(1)}, u32[]{:S(2)}, u32[]{:S(2)}) collective-permute-start(bf16[128,1024]{1,0:T(8,128)(2,1)S(1)} %constant_dynamic-update-slice_fusion), channel_id=1, source_target_pairs={{0,4},{4,0},{1,5},{5,1},{2,6},{6,2},{3,7},{7,3},{8,12},{12,8},{9,1... | collective-permute-start | bytes 786440 | tf_op jit(solution)/shard_map/ppermute | solution.py:74
  22.1 1.9 %collective-permute-done.7 = bf16[64,1024]{1,0:T(8,128)(2,1)S(1)} collective-permute-done((bf16[64,1024]{1,0:T(8,128)(2,1)S(1)}, bf16[64,1024]{1,0:T(8,128)(2,1)S(1)}, u32[]{:S(2)}, u32[]{:S(2)}) %collective-permute-start.7) | collective-permute-done | bytes 131104 | tf_op jit(solution)/shard_map/ppermute | solution.py:74
  23.9 0.7 %pad_maximum_fusion.3 = bf16[2,64,1024]{2,1,0:T(8,128)(2,1)} fusion(bf16[1,64,1024]{2,1,0:T(8,128)(2,1)S(1)} %bitcast.83, bf16[1,64,1024]{2,1,0:T(8,128)(2,1)S(1)} %bitcast.77), kind=kLoop, calls=%fused_computation.18 | loop fusion | flops 131072 | bytes 524288 | tf_op jit(solution)/shard_map/stack | solution.py:75
  24.7 1.5 %collective-permute-start.8 = (bf16[2,64,1024]{2,1,0:T(8,128)(2,1)}, bf16[2,64,1024]{2,1,0:T(8,128)(2,1)}, u32[]{:S(2)}, u32[]{:S(2)}) collective-permute-start(bf16[2,64,1024]{2,1,0:T(8,128)(2,1)} %pad_maximum_fusion.3), channel_id=1, source_target_pairs={{0,2},{1,3},{2,0},{3,1},{4,6},{5,7},{6,4},{7,5},{8,10},{9,11},{10,... | collective-permute-start | bytes 786440 | tf_op jit(solution)/shard_map/ppermute | solution.py:79
  26.1 0.0 collective-permute-done.11
  26.1 0.8 %pad_maximum_fusion.4 = bf16[2,64,1024]{2,1,0:T(8,128)(2,1)} fusion(bf16[1,64,1024]{2,1,0:T(8,128)(2,1)S(1)} %bitcast.80, bf16[1,64,1024]{2,1,0:T(8,128)(2,1)S(1)} %bitcast.74), kind=kLoop, calls=%fused_computation.19 | loop fusion | flops 131072 | bytes 524288 | tf_op jit(solution)/shard_map/stack | solution.py:75
  26.9 0.7 %collective-permute-start.12 = (bf16[2,64,1024]{2,1,0:T(8,128)(2,1)}, bf16[2,64,1024]{2,1,0:T(8,128)(2,1)}, u32[]{:S(2)}, u32[]{:S(2)}) collective-permute-start(bf16[2,64,1024]{2,1,0:T(8,128)(2,1)} %pad_maximum_fusion.4), channel_id=1, source_target_pairs={{0,2},{1,3},{2,0},{3,1},{4,6},{5,7},{6,4},{7,5},{8,10},{9,11},{10,... | collective-permute-start | bytes 786440 | tf_op jit(solution)/shard_map/ppermute | solution.py:79
  27.6 0.0 collective-permute-done
  27.6 0.0 collective-permute-start.1
  27.6 0.6 collective-permute-done.4
  28.2 0.7 %copy-done.4 = bf16[128,1024]{1,0:T(8,128)(2,1)} copy-done((bf16[128,1024]{1,0:T(8,128)(2,1)}, bf16[128,1024]{1,0:T(8,128)(2,1)S(1)}, u32[]{:S(2)}) %copy-start.4) | copy-done | bytes 262168
  28.9 0.8 %pad_maximum_fusion = bf16[2,128,1024]{2,1,0:T(8,128)(2,1)} fusion(bf16[1,128,1024]{2,1,0:T(8,128)(2,1)S(1)} %bitcast.86, bf16[1,128,1024]{2,1,0:T(8,128)(2,1)S(1)} %bitcast.70), kind=kLoop, calls=%fused_computation.15 | loop fusion | flops 262144 | bytes 1048576 | tf_op jit(solution)/shard_map/stack | solution.py:75
  29.7 0.0 collective-permute-start.5
  29.7 0.2 multiply_reduce_fusion
  29.9 1.4 %collective-permute-done.8 = bf16[2,64,1024]{2,1,0:T(8,128)(2,1)} collective-permute-done((bf16[2,64,1024]{2,1,0:T(8,128)(2,1)}, bf16[2,64,1024]{2,1,0:T(8,128)(2,1)}, u32[]{:S(2)}, u32[]{:S(2)}) %collective-permute-start.8) | collective-permute-done | bytes 262176 | tf_op jit(solution)/shard_map/ppermute | solution.py:79
  31.3 1.0 %pad_maximum_fusion.1 = bf16[2,128,1024]{2,1,0:T(8,128)(2,1)S(1)} fusion(bf16[2,64,1024]{2,1,0:T(8,128)(2,1)} %collective-permute-done.8, bf16[1,64,1024]{2,1,0:T(8,128)(2,1)S(1)} %bitcast.84, bf16[1,64,1024]{2,1,0:T(8,128)(2,1)S(1)} %bitcast.78), kind=kLoop, calls=%fused_computation.16 | loop fusion | flops 1572864 | bytes 1048576 | tf_op jit(solution)/shard_map/concatenate | solution.py:80
  32.3 0.1 collective-permute-start.9
  32.4 1.7 %collective-permute-done.12 = bf16[2,64,1024]{2,1,0:T(8,128)(2,1)} collective-permute-done((bf16[2,64,1024]{2,1,0:T(8,128)(2,1)}, bf16[2,64,1024]{2,1,0:T(8,128)(2,1)}, u32[]{:S(2)}, u32[]{:S(2)}) %collective-permute-start.12) | collective-permute-done | bytes 262176 | tf_op jit(solution)/shard_map/ppermute | solution.py:79
  34.1 1.0 %pad_maximum_fusion.2 = bf16[2,128,1024]{2,1,0:T(8,128)(2,1)S(1)} fusion(bf16[2,64,1024]{2,1,0:T(8,128)(2,1)} %collective-permute-done.12, bf16[1,64,1024]{2,1,0:T(8,128)(2,1)S(1)} %bitcast.81, bf16[1,64,1024]{2,1,0:T(8,128)(2,1)S(1)} %bitcast.75), kind=kLoop, calls=%fused_computation.17 | loop fusion | flops 1572864 | bytes 1048576 | tf_op jit(solution)/shard_map/concatenate | solution.py:80
  35.1 0.1 collective-permute-start.13
  35.2 0.0 collective-permute-done.1
  35.2 1.1 %maximum_bitcast_fusion = bf16[1,256,1024]{2,1,0:T(8,128)(2,1)S(1)} fusion(bf16[128,1024]{1,0:T(8,128)(2,1)} %collective-permute-done.1, bf16[128,1024]{1,0:T(8,128)(2,1)} %collective-permute-done), kind=kLoop, calls=%fused_computation.14 | loop fusion | flops 1048576 | bytes 1048576 | tf_op jit(solution)/shard_map/stack | solution.py:112
  36.3 0.5 broadcast_in_dim.138
  36.8 0.1 maximum_dynamic-update-slice_fusion
  36.9 0.0 collective-permute-done.5
  37.0 1.1 %maximum_dynamic-update-slice_fusion.1 = bf16[8,256,1024]{2,1,0:T(8,128)(2,1)S(1)} fusion(bf16[8,256,1024]{2,1,0:T(8,128)(2,1)S(1)} %maximum_dynamic-update-slice_fusion, s32[]{:T(128)S(6)} %select_n.130, bf16[2,128,1024]{2,1,0:T(8,128)(2,1)} %collective-permute-done.5, bf16[1,128,1024]{2,1,0:T(8,128)(2,1)S(1)} %bitcast.87, bf16[1,128,1024]{2,1,0:T(8,128)(2,1)S(1)} %bitcast.71), kind=kLoop, calls=%fused_computation.10 | loop fusion | flops 3145728 | bytes 2097156 | tf_op jit(solution)/shard_map/dynamic_update_slice | solution.py:117
  38.1 0.0 collective-permute-done.9
  38.1 1.1 %maximum_dynamic-update-slice_fusion.2 = bf16[8,256,1024]{2,1,0:T(8,128)(2,1)S(1)} fusion(bf16[8,256,1024]{2,1,0:T(8,128)(2,1)S(1)} %maximum_dynamic-update-slice_fusion.1, s32[]{:T(128)S(6)} %select_n.131, bf16[2,128,1024]{2,1,0:T(8,128)(2,1)S(1)} %collective-permute-done.9, bf16[2,64,1024]{2,1,0:T(8,128)(2,1)} %collective-permute-done.8, ...), kind=kLoop, calls=%fused_computation.11 | loop fusion | flops 4194304 | bytes 2097156 | tf_op jit(solution)/shard_map/dynamic_update_slice | solution.py:117
  39.2 0.0 collective-permute-done.13
  39.2 1.1 %maximum_dynamic-update-slice_fusion.3 = bf16[8,256,1024]{2,1,0:T(8,128)(2,1)S(1)} fusion(bf16[8,256,1024]{2,1,0:T(8,128)(2,1)S(1)} %maximum_dynamic-update-slice_fusion.2, s32[]{:T(128)S(6)} %select_n.132, bf16[2,128,1024]{2,1,0:T(8,128)(2,1)S(1)} %collective-permute-done.13, bf16[2,64,1024]{2,1,0:T(8,128)(2,1)} %collective-permute-done.12, ...), kind=kLoop, calls=%fused_computation.12 | loop fusion | flops 4194304 | bytes 2097156 | tf_op jit(solution)/shard_map/dynamic_update_slice | solution.py:117
  40.3 4.6 %fusion.21 = (f32[2048]{0:T(1024)S(1)}, f32[2048,512]{1,0:T(8,128)}) fusion(f32[512]{0:T(512)S(1)} %multiply_reduce_fusion, bf16[2048,1024]{1,0:T(8,128)(2,1)S(1)} %bitcast.68, f32[512,1024]{1,0:T(8,128)S(1)} %copy-done.3), kind=kOutput, calls=%fused_computation.74 | convolution fusion | flops 2152200192 | bytes 10496000 | tf_op jit(solution)/shard_map/dot_general | solution.py:10
  44.9 0.1 broadcast_in_dim.141
  45.0 3.3 %exponential_reduce_fusion = f32[2048]{0:T(1024)S(1)} fusion(f32[2048,512]{1,0:T(8,128)} %get-tuple-element.26, f32[2048]{0:T(1024)S(1)} %get-tuple-element.25), kind=kLoop, calls=%fused_computation.4 | loop fusion | flops 2095104 | bytes 4210688 | tf_op jit(solution)/shard_map/reduce_sum | solution.py:18
  48.3 0.1 broadcast_in_dim.146
  48.4 0.1 select_reduce_fusion.7
  48.5 0.2 select_reduce_fusion.3
  48.7 9.3 %all-gather = f32[16,8,4,64]{3,1,2,0:T(8,128)S(1)} all-gather(f32[2,8,4,64]{3,1,2,0:T(8,128)S(1)} %copy.30), channel_id=2, replica_groups=mesh['outer'=4,'dp'=2,'cent'=4] {'dp','cent'}, dimensions={0}, use_global_device_ids=true | all-gather | bytes 147456 | tf_op jit(solution)/shard_map/all_gather | solution.py:147
  58.1 0.1 select_reduce_fusion.1
  58.2 0.1 select_reduce_fusion.5
  58.3 0.1 div.62
  58.3 0.1 sub.53
  58.4 2.8 %bitcast_reduce_fusion = f32[4,512]{1,0:T(4,128)S(1)} fusion(f32[2048]{0:T(1024)S(1)} %div.62, f32[2048,512]{1,0:T(8,128)} %get-tuple-element.26, f32[2048]{0:T(1024)S(1)} %sub.53), kind=kLoop, calls=%fused_computation.2 | loop fusion | flops 5240832 | bytes 4218880 | tf_op jit(solution)/shard_map/reduce_sum | solution.py:158
  61.3 0.6 copy-done
  61.9 1.0 %fusion = bf16[2048,512]{1,0:T(8,128)(2,1)S(1)} fusion(f32[4,512]{1,0:T(4,128)S(1)} %broadcast_add_fusion, f32[2048]{0:T(1024)S(1)} %div.62, f32[2048,512]{1,0:T(8,128)S(1)} %copy-done, f32[2048]{0:T(1024)S(1)} %sub.53), kind=kLoop, calls=%fused_computation.1 | loop fusion | flops 6291456 | bytes 6316032 | tf_op jit(solution)/shard_map/convert_element_type | solution.py:159
  62.9 0.7 %copy-done.2 = bf16[8,256,1024]{2,1,0:T(8,128)(2,1)S(1)} copy-done((bf16[8,256,1024]{2,1,0:T(8,128)(2,1)S(1)}, bf16[8,256,1024]{2,1,0:T(8,128)(2,1)}, u32[]{:S(2)}) %copy-start.2) | copy-done | bytes 4194328
  63.6 3.7 %subtract_multiply_fusion.1 = f32[512,1024]{1,0:T(8,128)} fusion(f32[512,1024]{1,0:T(8,128)S(1)} %copy-done.3, bf16[2048,512]{1,0:T(8,128)(2,1)S(1)} %fusion, bf16[2048,1024]{1,0:T(8,128)(2,1)S(1)} %bitcast.69, f32[512]{0:T(512)S(1)} %fusion.8), kind=kOutput, calls=%fused_computation.7 | convolution fusion | flops 2149056512 | bytes 10487808 | tf_op jit(solution)/shard_map/dot_general | solution.py:160
  (27 shorter events, 0.2 us)
Async XLA Ops:
  0.0 29.7 %copy-start.3 = (f32[512,1024]{1,0:T(8,128)S(1)}, f32[512,1024]{1,0:T(8,128)}, u32[]{:S(2)}) copy-start(f32[512,1024]{1,0:T(8,128)} %param.4) | copy-start | bytes 6291460
  1.5 10.2 %collective-permute-start.2 = (bf16[64,1024]{1,0:T(8,128)(2,1)S(1)}, bf16[64,1024]{1,0:T(8,128)(2,1)S(1)}, u32[]{:S(2)}, u32[]{:S(2)}) collective-permute-start(bf16[64,1024]{1,0:T(8,128)(2,1)S(1)} %constant_dynamic-slice_fusion), channel_id=1, source_target_pairs={{0,8},{8,0},{16,24},{24,16},{1,9},{9,1},{17,25},{25,17},{2,10},{10... | collective-permute-start | bytes 393224 | tf_op jit(solution)/shard_map/ppermute | solution.py:89
  4.6 12.9 %collective-permute-start.6 = (bf16[64,1024]{1,0:T(8,128)(2,1)S(1)}, bf16[64,1024]{1,0:T(8,128)(2,1)S(1)}, u32[]{:S(2)}, u32[]{:S(2)}) collective-permute-start(bf16[64,1024]{1,0:T(8,128)(2,1)S(1)} %constant_dynamic-slice_fusion), channel_id=1, source_target_pairs={{0,16},{8,24},{16,0},{24,8},{1,17},{9,25},{17,1},{25,9},{2,18},{10... | collective-permute-start | bytes 393224 | tf_op jit(solution)/shard_map/ppermute | solution.py:89
  7.2 11.9 %collective-permute-start.10 = (bf16[64,1024]{1,0:T(8,128)(2,1)S(1)}, bf16[64,1024]{1,0:T(8,128)(2,1)S(1)}, u32[]{:S(2)}, u32[]{:S(2)}) collective-permute-start(bf16[64,1024]{1,0:T(8,128)(2,1)S(1)} %constant_dynamic-slice_fusion), channel_id=1, source_target_pairs={{0,24},{8,16},{16,8},{24,0},{1,25},{9,17},{17,9},{25,1},{2,26},{10... | collective-permute-start | bytes 393224 | tf_op jit(solution)/shard_map/ppermute | solution.py:89
  7.9 19.7 %collective-permute-start = (bf16[128,1024]{1,0:T(8,128)(2,1)}, bf16[128,1024]{1,0:T(8,128)(2,1)}, u32[]{:S(2)}, u32[]{:S(2)}) collective-permute-start(bf16[128,1024]{1,0:T(8,128)(2,1)} %constant_dynamic-slice_fusion.1), channel_id=1, source_target_pairs={{0,4},{4,0},{1,5},{5,1},{2,6},{6,2},{3,7},{7,3},{8,12},{12,8},{9,1... | collective-permute-start | bytes 786440 | tf_op jit(solution)/shard_map/ppermute | solution.py:109
  11.7 7.8 %collective-permute-start.3 = (bf16[64,1024]{1,0:T(8,128)(2,1)S(1)}, bf16[64,1024]{1,0:T(8,128)(2,1)}, u32[]{:S(2)}, u32[]{:S(2)}) collective-permute-start(bf16[64,1024]{1,0:T(8,128)(2,1)S(1)} %collective-permute-done.2), channel_id=1, source_target_pairs={{0,2},{1,3},{2,0},{3,1},{4,6},{5,7},{6,4},{7,5},{8,10},{9,11},{10,... | collective-permute-start | bytes 393224 | tf_op jit(solution)/shard_map/ppermute | solution.py:92
  17.5 6.4 %collective-permute-start.7 = (bf16[64,1024]{1,0:T(8,128)(2,1)S(1)}, bf16[64,1024]{1,0:T(8,128)(2,1)S(1)}, u32[]{:S(2)}, u32[]{:S(2)}) collective-permute-start(bf16[64,1024]{1,0:T(8,128)(2,1)S(1)} %collective-permute-done.6), channel_id=1, source_target_pairs={{0,4},{4,0},{1,5},{5,1},{2,6},{6,2},{3,7},{7,3},{8,12},{12,8},{9,1... | collective-permute-start | bytes 393224 | tf_op jit(solution)/shard_map/ppermute | solution.py:74
  19.0 7.1 %collective-permute-start.11 = (bf16[64,1024]{1,0:T(8,128)(2,1)S(1)}, bf16[64,1024]{1,0:T(8,128)(2,1)S(1)}, u32[]{:S(2)}, u32[]{:S(2)}) collective-permute-start(bf16[64,1024]{1,0:T(8,128)(2,1)S(1)} %collective-permute-done.10), channel_id=1, source_target_pairs={{0,4},{4,0},{1,5},{5,1},{2,6},{6,2},{3,7},{7,3},{8,12},{12,8},{9,1... | collective-permute-start | bytes 393224 | tf_op jit(solution)/shard_map/ppermute | solution.py:74
  20.5 7.7 %collective-permute-start.4 = (bf16[128,1024]{1,0:T(8,128)(2,1)S(1)}, bf16[128,1024]{1,0:T(8,128)(2,1)S(1)}, u32[]{:S(2)}, u32[]{:S(2)}) collective-permute-start(bf16[128,1024]{1,0:T(8,128)(2,1)S(1)} %constant_dynamic-update-slice_fusion), channel_id=1, source_target_pairs={{0,4},{4,0},{1,5},{5,1},{2,6},{6,2},{3,7},{7,3},{8,12},{12,8},{9,1... | collective-permute-start | bytes 786440 | tf_op jit(solution)/shard_map/ppermute | solution.py:74
  24.7 6.7 %collective-permute-start.8 = (bf16[2,64,1024]{2,1,0:T(8,128)(2,1)}, bf16[2,64,1024]{2,1,0:T(8,128)(2,1)}, u32[]{:S(2)}, u32[]{:S(2)}) collective-permute-start(bf16[2,64,1024]{2,1,0:T(8,128)(2,1)} %pad_maximum_fusion.3), channel_id=1, source_target_pairs={{0,2},{1,3},{2,0},{3,1},{4,6},{5,7},{6,4},{7,5},{8,10},{9,11},{10,... | collective-permute-start | bytes 786440 | tf_op jit(solution)/shard_map/ppermute | solution.py:79
  26.9 7.3 %collective-permute-start.12 = (bf16[2,64,1024]{2,1,0:T(8,128)(2,1)}, bf16[2,64,1024]{2,1,0:T(8,128)(2,1)}, u32[]{:S(2)}, u32[]{:S(2)}) collective-permute-start(bf16[2,64,1024]{2,1,0:T(8,128)(2,1)} %pad_maximum_fusion.4), channel_id=1, source_target_pairs={{0,2},{1,3},{2,0},{3,1},{4,6},{5,7},{6,4},{7,5},{8,10},{9,11},{10,... | collective-permute-start | bytes 786440 | tf_op jit(solution)/shard_map/ppermute | solution.py:79
  27.6 7.6 %collective-permute-start.1 = (bf16[128,1024]{1,0:T(8,128)(2,1)}, bf16[128,1024]{1,0:T(8,128)(2,1)}, u32[]{:S(2)}, u32[]{:S(2)}) collective-permute-start(bf16[128,1024]{1,0:T(8,128)(2,1)} %collective-permute-done), channel_id=1, source_target_pairs={{0,1},{1,0},{2,3},{3,2},{4,5},{5,4},{6,7},{7,6},{8,9},{9,8},{10,11... | collective-permute-start | bytes 786440 | tf_op jit(solution)/shard_map/ppermute | solution.py:110
  28.1 0.7 %copy-start.4 = (bf16[128,1024]{1,0:T(8,128)(2,1)}, bf16[128,1024]{1,0:T(8,128)(2,1)S(1)}, u32[]{:S(2)}) copy-start(bf16[128,1024]{1,0:T(8,128)(2,1)S(1)} %collective-permute-done.4) | copy-start | bytes 786436
  29.7 7.2 %collective-permute-start.5 = (bf16[2,128,1024]{2,1,0:T(8,128)(2,1)}, bf16[2,128,1024]{2,1,0:T(8,128)(2,1)}, u32[]{:S(2)}, u32[]{:S(2)}) collective-permute-start(bf16[2,128,1024]{2,1,0:T(8,128)(2,1)} %pad_maximum_fusion), channel_id=1, source_target_pairs={{0,1},{1,0},{2,3},{3,2},{4,5},{5,4},{6,7},{7,6},{8,9},{9,8},{10,11... | collective-permute-start | bytes 1572872 | tf_op jit(solution)/shard_map/ppermute | solution.py:95
  32.3 4.6 %copy-start.5 = (bf16[128,1024]{1,0:T(8,128)(2,1)S(1)}, bf16[128,1024]{1,0:T(8,128)(2,1)}, u32[]{:S(2)}) copy-start(bf16[128,1024]{1,0:T(8,128)(2,1)} %copy-done.4) | copy-start | bytes 786436
  32.3 5.8 %collective-permute-start.9 = (bf16[2,128,1024]{2,1,0:T(8,128)(2,1)S(1)}, bf16[2,128,1024]{2,1,0:T(8,128)(2,1)S(1)}, u32[]{:S(2)}, u32[]{:S(2)}) collective-permute-start(bf16[2,128,1024]{2,1,0:T(8,128)(2,1)S(1)} %pad_maximum_fusion.1), channel_id=1, source_target_pairs={{0,1},{1,0},{2,3},{3,2},{4,5},{5,4},{6,7},{7,6},{8,9},{9,8},{10,11... | collective-permute-start | bytes 1572872 | tf_op jit(solution)/shard_map/ppermute | solution.py:79
  35.1 4.0 %collective-permute-start.13 = (bf16[2,128,1024]{2,1,0:T(8,128)(2,1)S(1)}, bf16[2,128,1024]{2,1,0:T(8,128)(2,1)S(1)}, u32[]{:S(2)}, u32[]{:S(2)}) collective-permute-start(bf16[2,128,1024]{2,1,0:T(8,128)(2,1)S(1)} %pad_maximum_fusion.2), channel_id=1, source_target_pairs={{0,1},{1,0},{2,3},{3,2},{4,5},{5,4},{6,7},{7,6},{8,9},{9,8},{10,11... | collective-permute-start | bytes 1572872 | tf_op jit(solution)/shard_map/ppermute | solution.py:79
  40.2 4.6 %copy-start.1 = (bf16[8,256,1024]{2,1,0:T(8,128)(2,1)}, bf16[8,256,1024]{2,1,0:T(8,128)(2,1)S(1)}, u32[]{:S(2)}) copy-start(bf16[8,256,1024]{2,1,0:T(8,128)(2,1)S(1)} %maximum_dynamic-update-slice_fusion.3) | copy-start | bytes 12582916
  58.4 3.4 %copy-start = (f32[2048,512]{1,0:T(8,128)S(1)}, f32[2048,512]{1,0:T(8,128)}, u32[]{:S(2)}) copy-start(f32[2048,512]{1,0:T(8,128)} %get-tuple-element.26) | copy-start | bytes 12582916
  61.3 2.3 %copy-start.2 = (bf16[8,256,1024]{2,1,0:T(8,128)(2,1)S(1)}, bf16[8,256,1024]{2,1,0:T(8,128)(2,1)}, u32[]{:S(2)}) copy-start(bf16[8,256,1024]{2,1,0:T(8,128)(2,1)} %copy-done.1) | copy-start | bytes 12582916

commit v17 on v16

--- a/solution.py
+++ b/solution.py
@@ -97,7 +97,7 @@
         return cur
 
     parts = [None] + [
-        spread_x_first(piece) if sz == 1 else spread(pair_of(piece))
+        spread_x_first(piece) if sz <= 2 else spread(pair_of(piece))
         for sz, piece in enumerate(landed[1:], start=1)
     ]
 

time: 67.8 us -> 67.7 us (level)
  the two profiles are of different devices: /device:TPU:0 before, /device:TPU:17 now
where the time goes in v17:
time: 67.7 us; the launch traced here: 67.3 us
  starting transfers between devices  19.5 us (29%)
  other arithmetic  19.3 us (29%)
  blocking collectives  9.65 us (14%)
  matrix products  8.3 us (12%)
  waiting for transfers between devices  6.37 us (9%)
  local copies, waits for them, and re-layouts  3.86 us (6%)
    all_gather x1, blocking collectives, shards_all(): every = lax.all_gather(both, ('dp', 'cent'), axis=0)  9.65 us
    ppermute x3, waiting for transfers between devices, shards_all(): landed.append(lax.ppermute(mine, 'outer', pairs))  5.44 us
    ppermute x2, starting transfers between devices, spread_x_first(): other = lax.ppermute(cur, 'cent', [(i, i ^ bit) for i in range(n_c)])  5.24 us
    dot_general x1, matrix products, scores_for(): lax.dot_general(piece, cent_bf, (((1,), (1,)), ((), ())), preferred_eleme...  4.61 us
    ppermute x1, starting transfers between devices, shards_all(): mate = lax.ppermute(got, 'cent', [(i, i ^ 1) for i in range(n_c)])  4.52 us
    dot_general x1, matrix products, shards_all(): lax.dot_general(scaled.reshape(n_o * pod, k), everything, (((0,), (0,)),...  3.68 us
    dynamic_update_slice x4, other arithmetic, shards_all(): cur = lax.dynamic_update_slice_in_dim(cur, parts[sz], pod_of * n_d, axis=0)  3.34 us
    reduce_sum x1, other arithmetic, row_summary(): local_sum = jnp.sum(jnp.exp(logits - local_max[:, None]), axis=1)  3.31 us
  transfers between devices with their start and end apart: 14, of which 2 were waited for; matrix products, arithmetic and copies ran while one was open for 16% of the time, Pallas kernels for 0%

profile of v17, /device:TPU:17, one launch (start us, length us, event | category | flops | bytes accessed | tf_op | source)
XLA Modules:
  0.0 67.3 jit_solution(11071693435780388530)
XLA Ops:
  0.0 1.4 %convert_element_type.22 = bf16[256,1024]{1,0:T(8,128)(2,1)S(1)} convert(f32[256,1024]{1,0:T(8,128)} %param.3) | non-fusion elementwise | flops 262144 | bytes 1572864 | tf_op jit(solution)/shard_map/convert_element_type | solution.py:56
  1.5 1.4 %collective-permute-start.2 = (bf16[64,1024]{1,0:T(8,128)(2,1)S(1)}, bf16[64,1024]{1,0:T(8,128)(2,1)S(1)}, u32[]{:S(2)}, u32[]{:S(2)}) collective-permute-start(bf16[64,1024]{1,0:T(8,128)(2,1)S(1)} %constant_dynamic-slice_fusion), channel_id=1, source_target_pairs={{0,8},{8,0},{16,24},{24,16},{1,9},{9,1},{17,25},{25,17},{2,10},{10... | collective-permute-start | bytes 393224 | tf_op jit(solution)/shard_map/ppermute | solution.py:89
  2.8 0.1 collective-permute-start.6
  2.9 1.3 %collective-permute-start.10 = (bf16[64,1024]{1,0:T(8,128)(2,1)S(1)}, bf16[64,1024]{1,0:T(8,128)(2,1)S(1)}, u32[]{:S(2)}, u32[]{:S(2)}) collective-permute-start(bf16[64,1024]{1,0:T(8,128)(2,1)S(1)} %constant_dynamic-slice_fusion), channel_id=1, source_target_pairs={{0,24},{8,16},{16,8},{24,0},{1,25},{9,17},{17,9},{25,1},{2,26},{10... | collective-permute-start | bytes 393224 | tf_op jit(solution)/shard_map/ppermute | solution.py:89
  4.2 0.7 %constant_dynamic-slice_fusion.1 = bf16[128,1024]{1,0:T(8,128)(2,1)} fusion(bf16[256,1024]{1,0:T(8,128)(2,1)S(1)} %convert_element_type.22, s32[]{:T(128)S(6)} %select_n.127), kind=kLoop, calls=%fused_computation.51 | loop fusion | bytes 524292 | tf_op jit(solution)/shard_map/dynamic_slice | solution.py:106
  4.9 1.2 %collective-permute-start = (bf16[128,1024]{1,0:T(8,128)(2,1)}, bf16[128,1024]{1,0:T(8,128)(2,1)}, u32[]{:S(2)}, u32[]{:S(2)}) collective-permute-start(bf16[128,1024]{1,0:T(8,128)(2,1)} %constant_dynamic-slice_fusion.1), channel_id=1, source_target_pairs={{0,4},{4,0},{1,5},{5,1},{2,6},{6,2},{3,7},{7,3},{8,12},{12,8},{9,1... | collective-permute-start | bytes 786440 | tf_op jit(solution)/shard_map/ppermute | solution.py:109
  6.2 1.3 %convert_bitcast_fusion = bf16[1,256,1024]{2,1,0:T(8,128)(2,1)S(1)} fusion(f32[256,1024]{1,0:T(8,128)} %param.3), kind=kLoop, calls=%fused_computation.76 | loop fusion | flops 262144 | bytes 1572864 | tf_op jit(solution)/shard_map/stack | solution.py:112
  7.5 0.7 fusion.17
  8.2 0.1 copy.27
  8.3 0.1 stack.128
  8.4 0.0 collective-permute-done.2
  8.4 1.3 %collective-permute-start.3 = (bf16[64,1024]{1,0:T(8,128)(2,1)S(1)}, bf16[64,1024]{1,0:T(8,128)(2,1)S(1)}, u32[]{:S(2)}, u32[]{:S(2)}) collective-permute-start(bf16[64,1024]{1,0:T(8,128)(2,1)S(1)} %collective-permute-done.2), channel_id=1, source_target_pairs={{0,2},{1,3},{2,0},{3,1},{4,6},{5,7},{6,4},{7,5},{8,10},{9,11},{10,... | collective-permute-start | bytes 393224 | tf_op jit(solution)/shard_map/ppermute | solution.py:92
  9.7 0.0 collective-permute-done.6
  9.7 0.4 collective-permute-start.7
  10.0 5.4 %collective-permute-done.10 = bf16[64,1024]{1,0:T(8,128)(2,1)S(1)} collective-permute-done((bf16[64,1024]{1,0:T(8,128)(2,1)S(1)}, bf16[64,1024]{1,0:T(8,128)(2,1)S(1)}, u32[]{:S(2)}, u32[]{:S(2)}) %collective-permute-start.10) | collective-permute-done | bytes 131104 | tf_op jit(solution)/shard_map/ppermute | solution.py:89
  15.5 1.2 %collective-permute-start.11 = (bf16[64,1024]{1,0:T(8,128)(2,1)S(1)}, bf16[64,1024]{1,0:T(8,128)(2,1)S(1)}, u32[]{:S(2)}, u32[]{:S(2)}) collective-permute-start(bf16[64,1024]{1,0:T(8,128)(2,1)S(1)} %collective-permute-done.10), channel_id=1, source_target_pairs={{0,4},{4,0},{1,5},{5,1},{2,6},{6,2},{3,7},{7,3},{8,12},{12,8},{9,1... | collective-permute-start | bytes 393224 | tf_op jit(solution)/shard_map/ppermute | solution.py:74
  16.7 0.0 collective-permute-done.3
  16.8 0.3 collective-permute-start.4
  17.1 0.0 collective-permute-done.7
  17.1 1.3 %collective-permute-start.8 = (bf16[128,1024]{1,0:T(8,128)(2,1)S(1)}, bf16[128,1024]{1,0:T(8,128)(2,1)}, u32[]{:S(2)}, u32[]{:S(2)}) collective-permute-start(bf16[128,1024]{1,0:T(8,128)(2,1)S(1)} %constant_dynamic-update-slice_fusion.2), channel_id=1, source_target_pairs={{0,4},{4,0},{1,5},{5,1},{2,6},{6,2},{3,7},{7,3},{8,12},{12,8},{9,1... | collective-permute-start | bytes 786440 | tf_op jit(solution)/shard_map/ppermute | solution.py:74
  18.4 0.9 %collective-permute-done.11 = bf16[64,1024]{1,0:T(8,128)(2,1)S(1)} collective-permute-done((bf16[64,1024]{1,0:T(8,128)(2,1)S(1)}, bf16[64,1024]{1,0:T(8,128)(2,1)S(1)}, u32[]{:S(2)}, u32[]{:S(2)}) %collective-permute-start.11) | collective-permute-done | bytes 131104 | tf_op jit(solution)/shard_map/ppermute | solution.py:74
  19.3 0.7 %pad_maximum_fusion.3 = bf16[2,64,1024]{2,1,0:T(8,128)(2,1)} fusion(bf16[1,64,1024]{2,1,0:T(8,128)(2,1)S(1)} %bitcast.79, bf16[1,64,1024]{2,1,0:T(8,128)(2,1)S(1)} %bitcast.76), kind=kLoop, calls=%fused_computation.18 | loop fusion | flops 131072 | bytes 524288 | tf_op jit(solution)/shard_map/stack | solution.py:75
  20.0 1.2 %collective-permute-start.12 = (bf16[2,64,1024]{2,1,0:T(8,128)(2,1)}, bf16[2,64,1024]{2,1,0:T(8,128)(2,1)}, u32[]{:S(2)}, u32[]{:S(2)}) collective-permute-start(bf16[2,64,1024]{2,1,0:T(8,128)(2,1)} %pad_maximum_fusion.3), channel_id=1, source_target_pairs={{0,2},{1,3},{2,0},{3,1},{4,6},{5,7},{6,4},{7,5},{8,10},{9,11},{10,... | collective-permute-start | bytes 786440 | tf_op jit(solution)/shard_map/ppermute | solution.py:79
  21.2 0.0 collective-permute-done
  21.3 4.5 %collective-permute-start.1 = (bf16[128,1024]{1,0:T(8,128)(2,1)}, bf16[128,1024]{1,0:T(8,128)(2,1)}, u32[]{:S(2)}, u32[]{:S(2)}) collective-permute-start(bf16[128,1024]{1,0:T(8,128)(2,1)} %collective-permute-done), channel_id=1, source_target_pairs={{0,1},{1,0},{2,3},{3,2},{4,5},{5,4},{6,7},{7,6},{8,9},{9,8},{10,11... | collective-permute-start | bytes 786440 | tf_op jit(solution)/shard_map/ppermute | solution.py:110
  25.8 0.0 collective-permute-done.4
  25.8 0.7 %copy-done.4 = bf16[128,1024]{1,0:T(8,128)(2,1)} copy-done((bf16[128,1024]{1,0:T(8,128)(2,1)}, bf16[128,1024]{1,0:T(8,128)(2,1)S(1)}, u32[]{:S(2)}) %copy-start.4) | copy-done | bytes 262168
  26.5 0.8 %pad_maximum_fusion = bf16[2,128,1024]{2,1,0:T(8,128)(2,1)} fusion(bf16[1,128,1024]{2,1,0:T(8,128)(2,1)S(1)} %bitcast.82, bf16[1,128,1024]{2,1,0:T(8,128)(2,1)S(1)} %bitcast.70), kind=kLoop, calls=%fused_computation.15 | loop fusion | flops 262144 | bytes 1048576 | tf_op jit(solution)/shard_map/stack | solution.py:75
  27.3 3.4 %collective-permute-start.5 = (bf16[2,128,1024]{2,1,0:T(8,128)(2,1)}, bf16[2,128,1024]{2,1,0:T(8,128)(2,1)}, u32[]{:S(2)}, u32[]{:S(2)}) collective-permute-start(bf16[2,128,1024]{2,1,0:T(8,128)(2,1)} %pad_maximum_fusion), channel_id=1, source_target_pairs={{0,1},{1,0},{2,3},{3,2},{4,5},{5,4},{6,7},{7,6},{8,9},{9,8},{10,11... | collective-permute-start | bytes 1572872 | tf_op jit(solution)/shard_map/ppermute | solution.py:95
  30.7 0.0 copy-done.3
  30.7 0.2 multiply_reduce_fusion
  30.9 0.0 collective-permute-done.8
  30.9 1.0 %pad_maximum_fusion.1 = bf16[2,128,1024]{2,1,0:T(8,128)(2,1)S(1)} fusion(bf16[1,128,1024]{2,1,0:T(8,128)(2,1)} %bitcast.5, bf16[1,128,1024]{2,1,0:T(8,128)(2,1)S(1)} %bitcast.72), kind=kLoop, calls=%fused_computation.16 | loop fusion | flops 262144 | bytes 1048576 | tf_op jit(solution)/shard_map/stack | solution.py:75
  31.9 0.0 copy-start.5
  32.0 1.9 %collective-permute-start.9 = (bf16[2,128,1024]{2,1,0:T(8,128)(2,1)S(1)}, bf16[2,128,1024]{2,1,0:T(8,128)(2,1)S(1)}, u32[]{:S(2)}, u32[]{:S(2)}) collective-permute-start(bf16[2,128,1024]{2,1,0:T(8,128)(2,1)S(1)} %pad_maximum_fusion.1), channel_id=1, source_target_pairs={{0,1},{1,0},{2,3},{3,2},{4,5},{5,4},{6,7},{7,6},{8,9},{9,8},{10,11... | collective-permute-start | bytes 1572872 | tf_op jit(solution)/shard_map/ppermute | solution.py:95
  33.8 0.0 collective-permute-done.12
  33.8 1.0 %pad_maximum_fusion.2 = bf16[2,128,1024]{2,1,0:T(8,128)(2,1)S(1)} fusion(bf16[2,64,1024]{2,1,0:T(8,128)(2,1)} %collective-permute-done.12, bf16[1,64,1024]{2,1,0:T(8,128)(2,1)S(1)} %bitcast.80, bf16[1,64,1024]{2,1,0:T(8,128)(2,1)S(1)} %bitcast.77), kind=kLoop, calls=%fused_computation.17 | loop fusion | flops 1572864 | bytes 1048576 | tf_op jit(solution)/shard_map/concatenate | solution.py:80
  34.8 0.1 collective-permute-start.13
  34.9 0.0 collective-permute-done.1
  34.9 1.1 %maximum_bitcast_fusion = bf16[1,256,1024]{2,1,0:T(8,128)(2,1)S(1)} fusion(bf16[128,1024]{1,0:T(8,128)(2,1)} %collective-permute-done.1, bf16[128,1024]{1,0:T(8,128)(2,1)} %collective-permute-done), kind=kLoop, calls=%fused_computation.14 | loop fusion | flops 1048576 | bytes 1048576 | tf_op jit(solution)/shard_map/stack | solution.py:112
  36.0 0.5 broadcast_in_dim.138
  36.5 0.1 maximum_dynamic-update-slice_fusion
  36.6 0.0 collective-permute-done.5
  36.6 1.1 %maximum_dynamic-update-slice_fusion.1 = bf16[8,256,1024]{2,1,0:T(8,128)(2,1)S(1)} fusion(bf16[8,256,1024]{2,1,0:T(8,128)(2,1)S(1)} %maximum_dynamic-update-slice_fusion, s32[]{:T(128)S(6)} %select_n.130, bf16[2,128,1024]{2,1,0:T(8,128)(2,1)} %collective-permute-done.5, bf16[1,128,1024]{2,1,0:T(8,128)(2,1)S(1)} %bitcast.83, bf16[1,128,1024]{2,1,0:T(8,128)(2,1)S(1)} %bitcast.71), kind=kLoop, calls=%fused_computation.10 | loop fusion | flops 3145728 | bytes 2097156 | tf_op jit(solution)/shard_map/dynamic_update_slice | solution.py:117
  37.8 0.0 collective-permute-done.9
  37.8 1.0 %maximum_dynamic-update-slice_fusion.2 = bf16[8,256,1024]{2,1,0:T(8,128)(2,1)S(1)} fusion(bf16[8,256,1024]{2,1,0:T(8,128)(2,1)S(1)} %maximum_dynamic-update-slice_fusion.1, s32[]{:T(128)S(6)} %select_n.131, bf16[2,128,1024]{2,1,0:T(8,128)(2,1)S(1)} %collective-permute-done.9, bf16[1,128,1024]{2,1,0:T(8,128)(2,1)} %bitcast.5, ...), kind=kLoop, calls=%fused_computation.11 | loop fusion | flops 3145728 | bytes 2097156 | tf_op jit(solution)/shard_map/dynamic_update_slice | solution.py:117
  38.8 0.0 collective-permute-done.13
  38.9 1.1 %maximum_dynamic-update-slice_fusion.3 = bf16[8,256,1024]{2,1,0:T(8,128)(2,1)S(1)} fusion(bf16[8,256,1024]{2,1,0:T(8,128)(2,1)S(1)} %maximum_dynamic-update-slice_fusion.2, s32[]{:T(128)S(6)} %select_n.132, bf16[2,128,1024]{2,1,0:T(8,128)(2,1)S(1)} %collective-permute-done.13, bf16[2,64,1024]{2,1,0:T(8,128)(2,1)} %collective-permute-done.12, ...), kind=kLoop, calls=%fused_computation.12 | loop fusion | flops 4194304 | bytes 2097156 | tf_op jit(solution)/shard_map/dynamic_update_slice | solution.py:117
  39.9 4.6 %fusion.21 = (f32[2048]{0:T(1024)S(1)}, f32[2048,512]{1,0:T(8,128)}) fusion(f32[512]{0:T(512)S(1)} %multiply_reduce_fusion, bf16[2048,1024]{1,0:T(8,128)(2,1)S(1)} %bitcast.68, f32[512,1024]{1,0:T(8,128)S(1)} %copy-done.3), kind=kOutput, calls=%fused_computation.75 | convolution fusion | flops 2152200192 | bytes 10496000 | tf_op jit(solution)/shard_map/dot_general | solution.py:10
  44.5 0.1 broadcast_in_dim.141
  44.6 3.3 %exponential_reduce_fusion = f32[2048]{0:T(1024)S(1)} fusion(f32[2048,512]{1,0:T(8,128)} %get-tuple-element.26, f32[2048]{0:T(1024)S(1)} %get-tuple-element.25), kind=kLoop, calls=%fused_computation.4 | loop fusion | flops 2095104 | bytes 4210688 | tf_op jit(solution)/shard_map/reduce_sum | solution.py:18
  47.9 0.1 broadcast_in_dim.146
  48.0 0.1 select_reduce_fusion.7
  48.1 0.2 select_reduce_fusion.3
  48.3 9.6 %all-gather = f32[16,8,4,64]{3,1,2,0:T(8,128)S(1)} all-gather(f32[2,8,4,64]{3,1,2,0:T(8,128)S(1)} %copy.30), channel_id=2, replica_groups=mesh['outer'=4,'dp'=2,'cent'=4] {'dp','cent'}, dimensions={0}, use_global_device_ids=true | all-gather | bytes 147456 | tf_op jit(solution)/shard_map/all_gather | solution.py:147
  58.1 0.1 select_reduce_fusion.1
  58.2 0.1 select_reduce_fusion.5
  58.3 0.1 div.62
  58.4 0.1 sub.53
  58.4 2.8 %bitcast_reduce_fusion = f32[4,512]{1,0:T(4,128)S(1)} fusion(f32[2048]{0:T(1024)S(1)} %div.62, f32[2048,512]{1,0:T(8,128)} %get-tuple-element.26, f32[2048]{0:T(1024)S(1)} %sub.53), kind=kLoop, calls=%fused_computation.2 | loop fusion | flops 5240832 | bytes 4218880 | tf_op jit(solution)/shard_map/reduce_sum | solution.py:158
  61.3 0.6 copy-done
  61.9 1.0 %fusion = bf16[2048,512]{1,0:T(8,128)(2,1)S(1)} fusion(f32[4,512]{1,0:T(4,128)S(1)} %broadcast_add_fusion, f32[2048]{0:T(1024)S(1)} %div.62, f32[2048,512]{1,0:T(8,128)S(1)} %copy-done, f32[2048]{0:T(1024)S(1)} %sub.53), kind=kLoop, calls=%fused_computation.1 | loop fusion | flops 6291456 | bytes 6316032 | tf_op jit(solution)/shard_map/convert_element_type | solution.py:159
  62.9 0.7 %copy-done.2 = bf16[8,256,1024]{2,1,0:T(8,128)(2,1)S(1)} copy-done((bf16[8,256,1024]{2,1,0:T(8,128)(2,1)S(1)}, bf16[8,256,1024]{2,1,0:T(8,128)(2,1)}, u32[]{:S(2)}) %copy-start.2) | copy-done | bytes 4194328
  63.6 3.7 %subtract_multiply_fusion.1 = f32[512,1024]{1,0:T(8,128)} fusion(f32[512,1024]{1,0:T(8,128)S(1)} %copy-done.3, bf16[2048,512]{1,0:T(8,128)(2,1)S(1)} %fusion, bf16[2048,1024]{1,0:T(8,128)(2,1)S(1)} %bitcast.69, f32[512]{0:T(512)S(1)} %fusion.8), kind=kOutput, calls=%fused_computation.7 | convolution fusion | flops 2149056512 | bytes 10487808 | tf_op jit(solution)/shard_map/dot_general | solution.py:160
  (28 shorter events, 0.2 us)
Async XLA Ops:
  0.0 30.7 %copy-start.3 = (f32[512,1024]{1,0:T(8,128)S(1)}, f32[512,1024]{1,0:T(8,128)}, u32[]{:S(2)}) copy-start(f32[512,1024]{1,0:T(8,128)} %param.4) | copy-start | bytes 6291460
  1.5 6.9 %collective-permute-start.2 = (bf16[64,1024]{1,0:T(8,128)(2,1)S(1)}, bf16[64,1024]{1,0:T(8,128)(2,1)S(1)}, u32[]{:S(2)}, u32[]{:S(2)}) collective-permute-start(bf16[64,1024]{1,0:T(8,128)(2,1)S(1)} %constant_dynamic-slice_fusion), channel_id=1, source_target_pairs={{0,8},{8,0},{16,24},{24,16},{1,9},{9,1},{17,25},{25,17},{2,10},{10... | collective-permute-start | bytes 393224 | tf_op jit(solution)/shard_map/ppermute | solution.py:89
  2.8 6.8 %collective-permute-start.6 = (bf16[64,1024]{1,0:T(8,128)(2,1)S(1)}, bf16[64,1024]{1,0:T(8,128)(2,1)S(1)}, u32[]{:S(2)}, u32[]{:S(2)}) collective-permute-start(bf16[64,1024]{1,0:T(8,128)(2,1)S(1)} %constant_dynamic-slice_fusion), channel_id=1, source_target_pairs={{0,16},{8,24},{16,0},{24,8},{1,17},{9,25},{17,1},{25,9},{2,18},{10... | collective-permute-start | bytes 393224 | tf_op jit(solution)/shard_map/ppermute | solution.py:89
  2.9 12.6 %collective-permute-start.10 = (bf16[64,1024]{1,0:T(8,128)(2,1)S(1)}, bf16[64,1024]{1,0:T(8,128)(2,1)S(1)}, u32[]{:S(2)}, u32[]{:S(2)}) collective-permute-start(bf16[64,1024]{1,0:T(8,128)(2,1)S(1)} %constant_dynamic-slice_fusion), channel_id=1, source_target_pairs={{0,24},{8,16},{16,8},{24,0},{1,25},{9,17},{17,9},{25,1},{2,26},{10... | collective-permute-start | bytes 393224 | tf_op jit(solution)/shard_map/ppermute | solution.py:89
  4.9 16.3 %collective-permute-start = (bf16[128,1024]{1,0:T(8,128)(2,1)}, bf16[128,1024]{1,0:T(8,128)(2,1)}, u32[]{:S(2)}, u32[]{:S(2)}) collective-permute-start(bf16[128,1024]{1,0:T(8,128)(2,1)} %constant_dynamic-slice_fusion.1), channel_id=1, source_target_pairs={{0,4},{4,0},{1,5},{5,1},{2,6},{6,2},{3,7},{7,3},{8,12},{12,8},{9,1... | collective-permute-start | bytes 786440 | tf_op jit(solution)/shard_map/ppermute | solution.py:109
  8.4 8.4 %collective-permute-start.3 = (bf16[64,1024]{1,0:T(8,128)(2,1)S(1)}, bf16[64,1024]{1,0:T(8,128)(2,1)S(1)}, u32[]{:S(2)}, u32[]{:S(2)}) collective-permute-start(bf16[64,1024]{1,0:T(8,128)(2,1)S(1)} %collective-permute-done.2), channel_id=1, source_target_pairs={{0,2},{1,3},{2,0},{3,1},{4,6},{5,7},{6,4},{7,5},{8,10},{9,11},{10,... | collective-permute-start | bytes 393224 | tf_op jit(solution)/shard_map/ppermute | solution.py:92
  9.7 7.4 %collective-permute-start.7 = (bf16[64,1024]{1,0:T(8,128)(2,1)S(1)}, bf16[64,1024]{1,0:T(8,128)(2,1)S(1)}, u32[]{:S(2)}, u32[]{:S(2)}) collective-permute-start(bf16[64,1024]{1,0:T(8,128)(2,1)S(1)} %collective-permute-done.6), channel_id=1, source_target_pairs={{0,2},{1,3},{2,0},{3,1},{4,6},{5,7},{6,4},{7,5},{8,10},{9,11},{10,... | collective-permute-start | bytes 393224 | tf_op jit(solution)/shard_map/ppermute | solution.py:92
  15.5 3.8 %collective-permute-start.11 = (bf16[64,1024]{1,0:T(8,128)(2,1)S(1)}, bf16[64,1024]{1,0:T(8,128)(2,1)S(1)}, u32[]{:S(2)}, u32[]{:S(2)}) collective-permute-start(bf16[64,1024]{1,0:T(8,128)(2,1)S(1)} %collective-permute-done.10), channel_id=1, source_target_pairs={{0,4},{4,0},{1,5},{5,1},{2,6},{6,2},{3,7},{7,3},{8,12},{12,8},{9,1... | collective-permute-start | bytes 393224 | tf_op jit(solution)/shard_map/ppermute | solution.py:74
  16.8 9.0 %collective-permute-start.4 = (bf16[128,1024]{1,0:T(8,128)(2,1)S(1)}, bf16[128,1024]{1,0:T(8,128)(2,1)S(1)}, u32[]{:S(2)}, u32[]{:S(2)}) collective-permute-start(bf16[128,1024]{1,0:T(8,128)(2,1)S(1)} %constant_dynamic-update-slice_fusion), channel_id=1, source_target_pairs={{0,4},{4,0},{1,5},{5,1},{2,6},{6,2},{3,7},{7,3},{8,12},{12,8},{9,1... | collective-permute-start | bytes 786440 | tf_op jit(solution)/shard_map/ppermute | solution.py:74
  17.1 13.8 %collective-permute-start.8 = (bf16[128,1024]{1,0:T(8,128)(2,1)S(1)}, bf16[128,1024]{1,0:T(8,128)(2,1)}, u32[]{:S(2)}, u32[]{:S(2)}) collective-permute-start(bf16[128,1024]{1,0:T(8,128)(2,1)S(1)} %constant_dynamic-update-slice_fusion.2), channel_id=1, source_target_pairs={{0,4},{4,0},{1,5},{5,1},{2,6},{6,2},{3,7},{7,3},{8,12},{12,8},{9,1... | collective-permute-start | bytes 786440 | tf_op jit(solution)/shard_map/ppermute | solution.py:74
  20.0 13.8 %collective-permute-start.12 = (bf16[2,64,1024]{2,1,0:T(8,128)(2,1)}, bf16[2,64,1024]{2,1,0:T(8,128)(2,1)}, u32[]{:S(2)}, u32[]{:S(2)}) collective-permute-start(bf16[2,64,1024]{2,1,0:T(8,128)(2,1)} %pad_maximum_fusion.3), channel_id=1, source_target_pairs={{0,2},{1,3},{2,0},{3,1},{4,6},{5,7},{6,4},{7,5},{8,10},{9,11},{10,... | collective-permute-start | bytes 786440 | tf_op jit(solution)/shard_map/ppermute | solution.py:79
  21.3 13.6 %collective-permute-start.1 = (bf16[128,1024]{1,0:T(8,128)(2,1)}, bf16[128,1024]{1,0:T(8,128)(2,1)}, u32[]{:S(2)}, u32[]{:S(2)}) collective-permute-start(bf16[128,1024]{1,0:T(8,128)(2,1)} %collective-permute-done), channel_id=1, source_target_pairs={{0,1},{1,0},{2,3},{3,2},{4,5},{5,4},{6,7},{7,6},{8,9},{9,8},{10,11... | collective-permute-start | bytes 786440 | tf_op jit(solution)/shard_map/ppermute | solution.py:110
  25.8 0.7 %copy-start.4 = (bf16[128,1024]{1,0:T(8,128)(2,1)}, bf16[128,1024]{1,0:T(8,128)(2,1)S(1)}, u32[]{:S(2)}) copy-start(bf16[128,1024]{1,0:T(8,128)(2,1)S(1)} %collective-permute-done.4) | copy-start | bytes 786436
  27.3 9.3 %collective-permute-start.5 = (bf16[2,128,1024]{2,1,0:T(8,128)(2,1)}, bf16[2,128,1024]{2,1,0:T(8,128)(2,1)}, u32[]{:S(2)}, u32[]{:S(2)}) collective-permute-start(bf16[2,128,1024]{2,1,0:T(8,128)(2,1)} %pad_maximum_fusion), channel_id=1, source_target_pairs={{0,1},{1,0},{2,3},{3,2},{4,5},{5,4},{6,7},{7,6},{8,9},{9,8},{10,11... | collective-permute-start | bytes 1572872 | tf_op jit(solution)/shard_map/ppermute | solution.py:95
  31.9 4.7 %copy-start.5 = (bf16[128,1024]{1,0:T(8,128)(2,1)S(1)}, bf16[128,1024]{1,0:T(8,128)(2,1)}, u32[]{:S(2)}) copy-start(bf16[128,1024]{1,0:T(8,128)(2,1)} %copy-done.4) | copy-start | bytes 786436
  32.0 5.8 %collective-permute-start.9 = (bf16[2,128,1024]{2,1,0:T(8,128)(2,1)S(1)}, bf16[2,128,1024]{2,1,0:T(8,128)(2,1)S(1)}, u32[]{:S(2)}, u32[]{:S(2)}) collective-permute-start(bf16[2,128,1024]{2,1,0:T(8,128)(2,1)S(1)} %pad_maximum_fusion.1), channel_id=1, source_target_pairs={{0,1},{1,0},{2,3},{3,2},{4,5},{5,4},{6,7},{7,6},{8,9},{9,8},{10,11... | collective-permute-start | bytes 1572872 | tf_op jit(solution)/shard_map/ppermute | solution.py:95
  34.8 4.0 %collective-permute-start.13 = (bf16[2,128,1024]{2,1,0:T(8,128)(2,1)S(1)}, bf16[2,128,1024]{2,1,0:T(8,128)(2,1)S(1)}, u32[]{:S(2)}, u32[]{:S(2)}) collective-permute-start(bf16[2,128,1024]{2,1,0:T(8,128)(2,1)S(1)} %pad_maximum_fusion.2), channel_id=1, source_target_pairs={{0,1},{1,0},{2,3},{3,2},{4,5},{5,4},{6,7},{7,6},{8,9},{9,8},{10,11... | collective-permute-start | bytes 1572872 | tf_op jit(solution)/shard_map/ppermute | solution.py:79
  39.9 4.6 %copy-start.1 = (bf16[8,256,1024]{2,1,0:T(8,128)(2,1)}, bf16[8,256,1024]{2,1,0:T(8,128)(2,1)S(1)}, u32[]{:S(2)}) copy-start(bf16[8,256,1024]{2,1,0:T(8,128)(2,1)S(1)} %maximum_dynamic-update-slice_fusion.3) | copy-start | bytes 12582916
  58.4 3.4 %copy-start = (f32[2048,512]{1,0:T(8,128)S(1)}, f32[2048,512]{1,0:T(8,128)}, u32[]{:S(2)}) copy-start(f32[2048,512]{1,0:T(8,128)} %get-tuple-element.26) | copy-start | bytes 12582916
  61.3 2.3 %copy-start.2 = (bf16[8,256,1024]{2,1,0:T(8,128)(2,1)S(1)}, bf16[8,256,1024]{2,1,0:T(8,128)(2,1)}, u32[]{:S(2)}) copy-start(bf16[8,256,1024]{2,1,0:T(8,128)(2,1)} %copy-done.1) | copy-start | bytes 12582916

commit v18 on v15

--- a/solution.py
+++ b/solution.py
@@ -74,11 +74,22 @@
             across.append(lax.ppermute(piece, "dp", [(j, (j + sy) % n_d) for j in range(n_d)]))
         return jnp.stack(across)
 
-    def spread(cur):
-        for bit in reversed(bits):
-            other = lax.ppermute(cur, "cent", [(i, i ^ bit) for i in range(n_c)])
-            cur = jnp.concatenate([cur, other], axis=1)
-        return cur
+    def x_stage(pieces, bit):
+        keys = list(pieces)
+        got = lax.ppermute(tuple(pieces[kk] for kk in keys), "cent", [(i, i ^ bit) for i in range(n_c)])
+        out = dict(pieces)
+        for (sy, v), arr in zip(keys, got):
+            out[(sy, v ^ bit)] = arr
+        return out
+
+    def y_stage(pieces):
+        keys = list(pieces)
+        out = dict(pieces)
+        for sh in range(1, n_d):
+            got = lax.ppermute(tuple(pieces[kk] for kk in keys), "dp", [(j, (j + sh) % n_d) for j in range(n_d)])
+            for (sy, v), arr in zip(keys, got):
+                out[((sy + sh) % n_d, v)] = arr
+        return out
 
     landed = [mine]
     for sz in range(1, n_o):
@@ -87,23 +98,43 @@
         else:
             pairs = [(i, (i + sz) % n_o) for i in range(n_o)]
         landed.append(lax.ppermute(mine, "outer", pairs))
-    parts = [None] + [spread(pair_of(piece)) for piece in landed[1:]]
+
+    order = list(reversed(bits))
+    groups = [None]
+    for sz in range(1, n_o):
+        g = {(0, 0): landed[sz]}
+        if sz == 1:
+            g = x_stage(g, order[0])
+            g = y_stage(g)
+            for bit in order[1:]:
+                g = x_stage(g, bit)
+        else:
+            g = y_stage(g)
+            for bit in order:
+                g = x_stage(g, bit)
+        groups.append(g)
 
     h = q % 2
     half = t // 2
+    hq = n_c // 2
     my_half = lax.dynamic_slice_in_dim(rows_bf, h * half, half, 0)
-    own_blocks = [rows_bf]
+
+    def pod_of(sz):
+        return (z ^ sz) if n_o & (n_o - 1) == 0 else (z - sz) % n_o
+
+    buf = jnp.zeros((n_o * n_d, n_c, tq, d), rows_bf.dtype)
+    own = pod_of(0) * n_d
+    buf = lax.dynamic_update_slice(buf, rows_bf.reshape(1, n_c, tq, d), (own, 0, 0, 0))
     for sy in range(1, n_d):
         got = lax.ppermute(my_half, "dp", [(j, (j + sy) % n_d) for j in range(n_d)])
         mate = lax.ppermute(got, "cent", [(i, i ^ 1) for i in range(n_c)])
-        own_blocks.append(jnp.concatenate([got, mate], axis=0))
-    parts[0] = jnp.stack(own_blocks)
-
-    cur = jnp.zeros((n_o * n_d,) + parts[0].shape[1:], parts[0].dtype)
-    for sz in range(n_o):
-        pod_of = (z ^ sz) if n_o & (n_o - 1) == 0 else (z - sz) % n_o
-        cur = lax.dynamic_update_slice_in_dim(cur, parts[sz], pod_of * n_d, axis=0)
-    everything = cur.reshape(n_od * n_c * tq, d)
+        buf = lax.dynamic_update_slice(buf, got.reshape(1, hq, tq, d), (own + sy, 0, 0, 0))
+        buf = lax.dynamic_update_slice(buf, mate.reshape(1, hq, tq, d), (own + sy, hq, 0, 0))
+    for sz in range(1, n_o):
+        base = pod_of(sz) * n_d
+        for (sy, v), arr in groups[sz].items():
+            buf = lax.dynamic_update_slice(buf, arr[None, None], (base + sy, xs.index(v), 0, 0))
+    everything = buf.reshape(n_od * n_c * tq, d)
 
     logits = scores_for(everything, cent_bf, squares)
     local_max, local_sum = row_summary(logits)

time: 70.6 us -> 92.2 us (1.31)
  local copies, waits for them, and re-layouts: 3.83 us -> 22.3 us
  other arithmetic: 20 us -> 11.4 us
  starting transfers between devices: 13.9 us -> 20.3 us
  matrix products: 8.3 us -> 12.7 us
  waiting for transfers between devices: 14.7 us -> 15.8 us
    dynamic_update_slice x0 -> x27, local copies, waits for them, and re-layouts: none -> 18 us  [the longest x24 15.7 us: shards_all(): lax.dynamic_update_slice(buf, arr[None, None], (base + sy, xs.index(v), 0...]
    ppermute x9 -> x21, starting transfers between devices: 6.44 us -> 12.9 us  [the longest x17 7.79 us: x_stage(): lax.ppermute(tuple((pieces[kk] for kk in keys)), 'cent', [(i, i ^ bit) fo...]
    ppermute x3, waiting for transfers between devices: 5.31 us -> 0.01 us  [shards_all(): landed.append(lax.ppermute(mine, 'outer', pairs))]
    ppermute x1, waiting for transfers between devices: 0.01 us -> 4.87 us  [shards_all(): got = lax.ppermute(my_half, 'dp', [(j, (j + sy) % n_d) for j in range(n_d)])]
    another operation x5 -> x0, other arithmetic: 3.88 us -> none  [the longest x2 2.36 us: shards_all(): parts[0] = jnp.stack(own_blocks)]
    dynamic_update_slice x4 -> x0, other arithmetic: 3.35 us -> none  [shards_all(): cur = lax.dynamic_update_slice_in_dim(cur, parts[sz], pod_of * n_d, axis=0)]
    concatenate x3 -> x0, other arithmetic: 2.8 us -> none  [spread(): cur = jnp.concatenate([cur, other], axis=1)]
    dot_general x1, matrix products: 3.68 us -> 5.91 us  [shards_all(): lax.dot_general(scaled.reshape(n_o * pod, k), everything, (((0,), (0,)),...]
  transfers between devices with their start and end apart: 14 -> 26, of which waited for: 6 -> 8; matrix products, arithmetic and copies ran while one was open for 16% -> 24% of each run, Pallas kernels for 0% -> 0%
where the time goes in v18:
time: 92.2 us; the launch traced here: 91.9 us
  local copies, waits for them, and re-layouts  22.3 us (24%)
  starting transfers between devices  20.3 us (22%)
  waiting for transfers between devices  15.8 us (17%)
  matrix products  12.7 us (14%)
  other arithmetic  11.4 us (12%)
  blocking collectives  9.19 us (10%)
    dynamic_update_slice x24, local copies, waits for them, and re-layouts, shards_all(): lax.dynamic_update_slice(buf, arr[None, None], (base + sy, xs.index(v), 0...  15.7 us
    all_gather x1, blocking collectives, shards_all(): every = lax.all_gather(both, ('dp', 'cent'), axis=0)  9.19 us
    ppermute x17, waiting for transfers between devices, x_stage(): lax.ppermute(tuple((pieces[kk] for kk in keys)), 'cent', [(i, i ^ bit) fo...  8.08 us
    ppermute x17, starting transfers between devices, x_stage(): lax.ppermute(tuple((pieces[kk] for kk in keys)), 'cent', [(i, i ^ bit) fo...  7.79 us
    dot_general x1, matrix products, scores_for(): lax.dot_general(piece, cent_bf, (((1,), (1,)), ((), ())), preferred_eleme...  6.81 us
    dot_general x1, matrix products, shards_all(): lax.dot_general(scaled.reshape(n_o * pod, k), everything, (((0,), (0,)),...  5.91 us
    ppermute x3, starting transfers between devices, shards_all(): landed.append(lax.ppermute(mine, 'outer', pairs))  5.62 us
    ppermute x4, starting transfers between devices, y_stage(): lax.ppermute(tuple((pieces[kk] for kk in keys)), 'dp', [(j, (j + sh) % n_...  5.13 us
  transfers between devices with their start and end apart: 26, of which 8 were waited for; matrix products, arithmetic and copies ran while one was open for 24% of the time, Pallas kernels for 0%

profile of v18, /device:TPU:0, one launch (start us, length us, event | category | flops | bytes accessed | tf_op | source)
XLA Modules:
  0.0 91.9 jit_solution(13245339727484731999)
XLA Ops:
  0.0 1.3 %convert_element_type.22 = bf16[256,1024]{1,0:T(8,128)(2,1)S(1)} convert(f32[256,1024]{1,0:T(8,128)} %param.3) | non-fusion elementwise | flops 262144 | bytes 1572864 | tf_op jit(solution)/shard_map/convert_element_type | solution.py:56
  1.3 0.7 constant_dynamic-slice_fusion
  2.0 3.0 %collective-permute-start.2 = (bf16[64,1024]{1,0:T(8,128)(2,1)}, bf16[64,1024]{1,0:T(8,128)(2,1)S(1)}, u32[]{:S(2)}, u32[]{:S(2)}) collective-permute-start(bf16[64,1024]{1,0:T(8,128)(2,1)} %constant_dynamic-slice_fusion), channel_id=1, source_target_pairs={{0,8},{8,0},{16,24},{24,16},{1,9},{9,1},{17,25},{25,17},{2,10},{10... | collective-permute-start | bytes 393224 | tf_op jit(solution)/shard_map/ppermute | solution.py:100
  5.0 2.6 %collective-permute-start.10 = (bf16[64,1024]{1,0:T(8,128)(2,1)}, bf16[64,1024]{1,0:T(8,128)(2,1)S(1)}, u32[]{:S(2)}, u32[]{:S(2)}) collective-permute-start(bf16[64,1024]{1,0:T(8,128)(2,1)} %constant_dynamic-slice_fusion), channel_id=1, source_target_pairs={{0,16},{8,24},{16,0},{24,8},{1,17},{9,25},{17,1},{25,9},{2,18},{10... | collective-permute-start | bytes 393224 | tf_op jit(solution)/shard_map/ppermute | solution.py:100
  7.6 1.8 %collective-permute-start = (bf16[128,1024]{1,0:T(8,128)(2,1)S(1)}, bf16[128,1024]{1,0:T(8,128)(2,1)S(1)}, u32[]{:S(2)}, u32[]{:S(2)}) collective-permute-start(bf16[128,1024]{1,0:T(8,128)(2,1)S(1)} %constant_dynamic-slice_fusion.1), channel_id=1, source_target_pairs={{0,4},{4,0},{1,5},{5,1},{2,6},{6,2},{3,7},{7,3},{8,12},{12,8},{9,1... | collective-permute-start | bytes 786440 | tf_op jit(solution)/shard_map/ppermute | solution.py:129
  9.4 0.7 fusion.17
  10.3 4.9 %collective-permute-done = bf16[128,1024]{1,0:T(8,128)(2,1)S(1)} collective-permute-done((bf16[128,1024]{1,0:T(8,128)(2,1)S(1)}, bf16[128,1024]{1,0:T(8,128)(2,1)S(1)}, u32[]{:S(2)}, u32[]{:S(2)}) %collective-permute-start) | collective-permute-done | bytes 262176 | tf_op jit(solution)/shard_map/ppermute | solution.py:129
  15.2 1.8 %multiply_reduce_fusion = f32[512]{0:T(512)S(1)} fusion(f32[512,1024]{1,0:T(8,128)} %param.4), kind=kLoop, calls=%fused_computation.8 | loop fusion | flops 1048064 | bytes 2099200 | tf_op jit(solution)/shard_map/reduce_sum | solution.py:58
  17.0 2.5 %broadcast_in_dim.210 = bf16[8,4,64,1024]{3,2,1,0:T(8,128)(2,1)} broadcast(bf16[]{:T(256)} %constant.86.clone.1), dimensions={} | broadcast | bytes 4194306 | tf_op jit(solution)/shard_map/broadcast_in_dim | solution.py:125
  19.4 0.8 constant_dynamic-update-slice_fusion.2
  20.3 1.5 %collective-permute-start.3 = (bf16[64,1024]{1,0:T(8,128)(2,1)S(1)}, bf16[64,1024]{1,0:T(8,128)(2,1)S(1)}, u32[]{:S(2)}, u32[]{:S(2)}) collective-permute-start(bf16[64,1024]{1,0:T(8,128)(2,1)S(1)} %collective-permute-done.2), channel_id=1, source_target_pairs={{0,2},{1,3},{2,0},{3,1},{4,6},{5,7},{6,4},{7,5},{8,10},{9,11},{10,... | collective-permute-start | bytes 393224 | tf_op jit(solution)/shard_map/ppermute | solution.py:79
  21.8 1.5 %collective-permute-start.4 = (bf16[64,1024]{1,0:T(8,128)(2,1)S(1)}, bf16[64,1024]{1,0:T(8,128)(2,1)S(1)}, u32[]{:S(2)}, u32[]{:S(2)}) collective-permute-start(bf16[64,1024]{1,0:T(8,128)(2,1)S(1)} %collective-permute-done.2), channel_id=1, source_target_pairs={{0,4},{4,0},{1,5},{5,1},{2,6},{6,2},{3,7},{7,3},{8,12},{12,8},{9,1... | collective-permute-start | bytes 393224 | tf_op jit(solution)/shard_map/ppermute | solution.py:89
  23.3 0.7 constant_dynamic-update-slice_fusion.1
  24.0 0.6 collective-permute-start.11
  24.6 0.7 constant_dynamic-update-slice_fusion
  25.3 0.7 bitcast_dynamic-update-slice_fusion.23
  26.0 0.2 collective-permute-done.3
  26.2 1.5 %collective-permute-start.12 = (bf16[64,1024]{1,0:T(8,128)(2,1)S(1)}, bf16[64,1024]{1,0:T(8,128)(2,1)S(1)}, u32[]{:S(2)}, u32[]{:S(2)}) collective-permute-start(bf16[64,1024]{1,0:T(8,128)(2,1)S(1)} %collective-permute-done.10), channel_id=1, source_target_pairs={{0,2},{1,3},{2,0},{3,1},{4,6},{5,7},{6,4},{7,5},{8,10},{9,11},{10,... | collective-permute-start | bytes 393224 | tf_op jit(solution)/shard_map/ppermute | solution.py:79
  27.7 0.7 bitcast_dynamic-update-slice_fusion.22
  28.3 1.5 %collective-permute-start.5 = (bf16[64,1024]{1,0:T(8,128)(2,1)S(1)}, bf16[64,1024]{1,0:T(8,128)(2,1)S(1)}, u32[]{:S(2)}, u32[]{:S(2)}) collective-permute-start(bf16[64,1024]{1,0:T(8,128)(2,1)S(1)} %collective-permute-done.3), channel_id=1, source_target_pairs={{0,4},{4,0},{1,5},{5,1},{2,6},{6,2},{3,7},{7,3},{8,12},{12,8},{9,1... | collective-permute-start | bytes 393224 | tf_op jit(solution)/shard_map/ppermute | solution.py:89
  29.8 0.7 bitcast_dynamic-update-slice_fusion.21
  30.5 2.8 %collective-permute-done.5 = bf16[64,1024]{1,0:T(8,128)(2,1)S(1)} collective-permute-done((bf16[64,1024]{1,0:T(8,128)(2,1)S(1)}, bf16[64,1024]{1,0:T(8,128)(2,1)S(1)}, u32[]{:S(2)}, u32[]{:S(2)}) %collective-permute-start.5) | collective-permute-done | bytes 131104 | tf_op jit(solution)/shard_map/ppermute | solution.py:89
  33.3 1.5 %collective-permute-start.19 = (bf16[64,1024]{1,0:T(8,128)(2,1)S(1)}, bf16[64,1024]{1,0:T(8,128)(2,1)S(1)}, u32[]{:S(2)}, u32[]{:S(2)}) collective-permute-start(bf16[64,1024]{1,0:T(8,128)(2,1)S(1)} %collective-permute-done.18), channel_id=1, source_target_pairs={{0,4},{4,0},{1,5},{5,1},{2,6},{6,2},{3,7},{7,3},{8,12},{12,8},{9,1... | collective-permute-start | bytes 393224 | tf_op jit(solution)/shard_map/ppermute | solution.py:89
  34.8 0.7 bitcast_dynamic-update-slice_fusion.20
  35.5 0.7 bitcast_dynamic-update-slice_fusion.19
  36.1 0.7 collective-permute-done.7
  36.8 0.1 collective-permute-start.8
  37.0 0.7 bitcast_dynamic-update-slice_fusion.18
  37.6 0.5 collective-permute-done.8
  38.2 0.1 collective-permute-start.9
  38.3 0.6 bitcast_dynamic-update-slice_fusion.17
  39.0 0.6 collective-permute-done.9
  39.5 0.6 collective-permute-start.20
  40.2 0.7 bitcast_dynamic-update-slice_fusion.16
  40.8 0.7 bitcast_dynamic-update-slice_fusion.15
  41.5 0.6 bitcast_dynamic-update-slice_fusion.14
  42.1 1.4 %collective-permute-start.13 = (bf16[64,1024]{1,0:T(8,128)(2,1)S(1)}, bf16[64,1024]{1,0:T(8,128)(2,1)S(1)}, u32[]{:S(2)}, u32[]{:S(2)}) collective-permute-start(bf16[64,1024]{1,0:T(8,128)(2,1)S(1)} %collective-permute-done.11), channel_id=1, source_target_pairs={{0,2},{1,3},{2,0},{3,1},{4,6},{5,7},{6,4},{7,5},{8,10},{9,11},{10,... | collective-permute-start | bytes 393224 | tf_op jit(solution)/shard_map/ppermute | solution.py:79
  43.5 0.7 bitcast_dynamic-update-slice_fusion.13
  44.2 3.9 %collective-permute-done.13 = bf16[64,1024]{1,0:T(8,128)(2,1)S(1)} collective-permute-done((bf16[64,1024]{1,0:T(8,128)(2,1)S(1)}, bf16[64,1024]{1,0:T(8,128)(2,1)S(1)}, u32[]{:S(2)}, u32[]{:S(2)}) %collective-permute-start.13) | collective-permute-done | bytes 131104 | tf_op jit(solution)/shard_map/ppermute | solution.py:79
  48.1 0.7 bitcast_dynamic-update-slice_fusion.12
  48.7 0.5 collective-permute-start.16
  49.2 1.4 %collective-permute-start.21 = (bf16[64,1024]{1,0:T(8,128)(2,1)S(1)}, bf16[64,1024]{1,0:T(8,128)(2,1)S(1)}, u32[]{:S(2)}, u32[]{:S(2)}) collective-permute-start(bf16[64,1024]{1,0:T(8,128)(2,1)S(1)} %collective-permute-done.19), channel_id=1, source_target_pairs={{0,2},{1,3},{2,0},{3,1},{4,6},{5,7},{6,4},{7,5},{8,10},{9,11},{10,... | collective-permute-start | bytes 393224 | tf_op jit(solution)/shard_map/ppermute | solution.py:79
  50.6 0.7 bitcast_dynamic-update-slice_fusion.11
  51.3 0.5 collective-permute-start.24
  51.8 0.7 bitcast_dynamic-update-slice_fusion.10
  52.5 2.2 %collective-permute-done.21 = bf16[64,1024]{1,0:T(8,128)(2,1)S(1)} collective-permute-done((bf16[64,1024]{1,0:T(8,128)(2,1)S(1)}, bf16[64,1024]{1,0:T(8,128)(2,1)S(1)}, u32[]{:S(2)}, u32[]{:S(2)}) %collective-permute-start.21) | collective-permute-done | bytes 131104 | tf_op jit(solution)/shard_map/ppermute | solution.py:79
  54.7 0.7 bitcast_dynamic-update-slice_fusion.9
  55.4 0.7 bitcast_dynamic-update-slice_fusion.8
  56.0 0.7 bitcast_dynamic-update-slice_fusion.7
  56.7 0.6 bitcast_dynamic-update-slice_fusion.6
  57.3 0.7 bitcast_dynamic-update-slice_fusion.5
  58.0 0.7 bitcast_dynamic-update-slice_fusion.4
  58.7 0.7 bitcast_dynamic-update-slice_fusion.3
  59.3 0.6 bitcast_dynamic-update-slice_fusion.2
  60.0 0.7 bitcast_dynamic-update-slice_fusion.1
  60.6 0.7 bitcast_dynamic-update-slice_fusion
  61.3 6.8 %fusion.21 = (f32[2048]{0:T(1024)S(1)}, f32[2048,512]{1,0:T(8,128)}) fusion(f32[512]{0:T(512)S(1)} %multiply_reduce_fusion, bf16[2048,1024]{1,0:T(8,128)(2,1)} %bitcast.27, f32[512,1024]{1,0:T(8,128)S(1)} %copy-done.1), kind=kOutput, calls=%fused_computation.89 | convolution fusion | flops 2152200192 | bytes 10496000 | tf_op jit(solution)/shard_map/dot_general | solution.py:10
  68.2 3.3 %exponential_reduce_fusion = f32[2048]{0:T(1024)S(1)} fusion(f32[2048,512]{1,0:T(8,128)} %get-tuple-element.26, f32[2048]{0:T(1024)S(1)} %get-tuple-element.25), kind=kLoop, calls=%fused_computation.4 | loop fusion | flops 2095104 | bytes 4210688 | tf_op jit(solution)/shard_map/reduce_sum | solution.py:18
  71.7 0.2 select_reduce_fusion.3
  71.9 9.2 %all-gather = f32[16,8,4,64]{3,1,2,0:T(8,128)S(1)} all-gather(f32[2,8,4,64]{3,1,2,0:T(8,128)S(1)} %copy.30), channel_id=2, replica_groups=mesh['outer'=4,'dp'=2,'cent'=4] {'dp','cent'}, dimensions={0}, use_global_device_ids=true | all-gather | bytes 147456 | tf_op jit(solution)/shard_map/all_gather | solution.py:166
  81.6 2.8 %bitcast_reduce_fusion = f32[4,512]{1,0:T(4,128)S(1)} fusion(f32[2048]{0:T(1024)S(1)} %div.62, f32[2048,512]{1,0:T(8,128)} %get-tuple-element.26, f32[2048]{0:T(1024)S(1)} %sub.53), kind=kLoop, calls=%fused_computation.2 | loop fusion | flops 5240832 | bytes 4218880 | tf_op jit(solution)/shard_map/reduce_sum | solution.py:177
  84.4 0.6 copy-done
  85.0 1.0 %fusion = bf16[2048,512]{1,0:T(8,128)(2,1)S(1)} fusion(f32[4,512]{1,0:T(4,128)S(1)} %broadcast_add_fusion, f32[2048]{0:T(1024)S(1)} %div.62, f32[2048,512]{1,0:T(8,128)S(1)} %copy-done, f32[2048]{0:T(1024)S(1)} %sub.53), kind=kLoop, calls=%fused_computation.1 | loop fusion | flops 6291456 | bytes 6316032 | tf_op jit(solution)/shard_map/convert_element_type | solution.py:178
  86.0 5.9 %subtract_multiply_fusion.1 = f32[512,1024]{1,0:T(8,128)} fusion(f32[512,1024]{1,0:T(8,128)S(1)} %copy-done.1, bf16[2048,512]{1,0:T(8,128)(2,1)S(1)} %fusion, bf16[2048,1024]{1,0:T(8,128)(2,1)} %bitcast.27, f32[512]{0:T(512)S(1)} %fusion.8), kind=kOutput, calls=%fused_computation.7 | convolution fusion | flops 2149056512 | bytes 10487808 | tf_op jit(solution)/shard_map/dot_general | solution.py:179
  (57 shorter events, 1.1 us)
Async XLA Ops:
  2.0 18.3 %collective-permute-start.2 = (bf16[64,1024]{1,0:T(8,128)(2,1)}, bf16[64,1024]{1,0:T(8,128)(2,1)S(1)}, u32[]{:S(2)}, u32[]{:S(2)}) collective-permute-start(bf16[64,1024]{1,0:T(8,128)(2,1)} %constant_dynamic-slice_fusion), channel_id=1, source_target_pairs={{0,8},{8,0},{16,24},{24,16},{1,9},{9,1},{17,25},{25,17},{2,10},{10... | collective-permute-start | bytes 393224 | tf_op jit(solution)/shard_map/ppermute | solution.py:100
  5.0 19.0 %collective-permute-start.10 = (bf16[64,1024]{1,0:T(8,128)(2,1)}, bf16[64,1024]{1,0:T(8,128)(2,1)S(1)}, u32[]{:S(2)}, u32[]{:S(2)}) collective-permute-start(bf16[64,1024]{1,0:T(8,128)(2,1)} %constant_dynamic-slice_fusion), channel_id=1, source_target_pairs={{0,16},{8,24},{16,0},{24,8},{1,17},{9,25},{17,1},{25,9},{2,18},{10... | collective-permute-start | bytes 393224 | tf_op jit(solution)/shard_map/ppermute | solution.py:100
  7.6 22.9 %collective-permute-start.18 = (bf16[64,1024]{1,0:T(8,128)(2,1)}, bf16[64,1024]{1,0:T(8,128)(2,1)S(1)}, u32[]{:S(2)}, u32[]{:S(2)}) collective-permute-start(bf16[64,1024]{1,0:T(8,128)(2,1)} %constant_dynamic-slice_fusion), channel_id=1, source_target_pairs={{0,24},{8,16},{16,8},{24,0},{1,25},{9,17},{17,9},{25,1},{2,26},{10... | collective-permute-start | bytes 393224 | tf_op jit(solution)/shard_map/ppermute | solution.py:100
  7.6 7.6 %collective-permute-start = (bf16[128,1024]{1,0:T(8,128)(2,1)S(1)}, bf16[128,1024]{1,0:T(8,128)(2,1)S(1)}, u32[]{:S(2)}, u32[]{:S(2)}) collective-permute-start(bf16[128,1024]{1,0:T(8,128)(2,1)S(1)} %constant_dynamic-slice_fusion.1), channel_id=1, source_target_pairs={{0,4},{4,0},{1,5},{5,1},{2,6},{6,2},{3,7},{7,3},{8,12},{12,8},{9,1... | collective-permute-start | bytes 786440 | tf_op jit(solution)/shard_map/ppermute | solution.py:129
  15.2 8.8 %collective-permute-start.1 = (bf16[128,1024]{1,0:T(8,128)(2,1)S(1)}, bf16[128,1024]{1,0:T(8,128)(2,1)S(1)}, u32[]{:S(2)}, u32[]{:S(2)}) collective-permute-start(bf16[128,1024]{1,0:T(8,128)(2,1)S(1)} %collective-permute-done), channel_id=1, source_target_pairs={{0,1},{1,0},{2,3},{3,2},{4,5},{5,4},{6,7},{7,6},{8,9},{9,8},{10,11... | collective-permute-start | bytes 786440 | tf_op jit(solution)/shard_map/ppermute | solution.py:130
  19.4 41.9 %copy-start.1 = (f32[512,1024]{1,0:T(8,128)S(1)}, f32[512,1024]{1,0:T(8,128)}, u32[]{:S(2)}) copy-start(f32[512,1024]{1,0:T(8,128)} %param.4) | copy-start | bytes 6291460
  20.3 5.9 %collective-permute-start.3 = (bf16[64,1024]{1,0:T(8,128)(2,1)S(1)}, bf16[64,1024]{1,0:T(8,128)(2,1)S(1)}, u32[]{:S(2)}, u32[]{:S(2)}) collective-permute-start(bf16[64,1024]{1,0:T(8,128)(2,1)S(1)} %collective-permute-done.2), channel_id=1, source_target_pairs={{0,2},{1,3},{2,0},{3,1},{4,6},{5,7},{6,4},{7,5},{8,10},{9,11},{10,... | collective-permute-start | bytes 393224 | tf_op jit(solution)/shard_map/ppermute | solution.py:79
  21.8 6.6 %collective-permute-start.4 = (bf16[64,1024]{1,0:T(8,128)(2,1)S(1)}, bf16[64,1024]{1,0:T(8,128)(2,1)S(1)}, u32[]{:S(2)}, u32[]{:S(2)}) collective-permute-start(bf16[64,1024]{1,0:T(8,128)(2,1)S(1)} %collective-permute-done.2), channel_id=1, source_target_pairs={{0,4},{4,0},{1,5},{5,1},{2,6},{6,2},{3,7},{7,3},{8,12},{12,8},{9,1... | collective-permute-start | bytes 393224 | tf_op jit(solution)/shard_map/ppermute | solution.py:89
  24.0 11.5 %collective-permute-start.6 = (bf16[64,1024]{1,0:T(8,128)(2,1)S(1)}, bf16[64,1024]{1,0:T(8,128)(2,1)S(1)}, u32[]{:S(2)}, u32[]{:S(2)}) collective-permute-start(bf16[64,1024]{1,0:T(8,128)(2,1)S(1)} %collective-permute-done.2), channel_id=1, source_target_pairs={{0,1},{1,0},{2,3},{3,2},{4,5},{5,4},{6,7},{7,6},{8,9},{9,8},{10,11... | collective-permute-start | bytes 393224 | tf_op jit(solution)/shard_map/ppermute | solution.py:79
  24.0 17.5 %collective-permute-start.11 = (bf16[64,1024]{1,0:T(8,128)(2,1)S(1)}, bf16[64,1024]{1,0:T(8,128)(2,1)S(1)}, u32[]{:S(2)}, u32[]{:S(2)}) collective-permute-start(bf16[64,1024]{1,0:T(8,128)(2,1)S(1)} %collective-permute-done.10), channel_id=1, source_target_pairs={{0,4},{4,0},{1,5},{5,1},{2,6},{6,2},{3,7},{7,3},{8,12},{12,8},{9,1... | collective-permute-start | bytes 393224 | tf_op jit(solution)/shard_map/ppermute | solution.py:89
  26.2 16.0 %collective-permute-start.12 = (bf16[64,1024]{1,0:T(8,128)(2,1)S(1)}, bf16[64,1024]{1,0:T(8,128)(2,1)S(1)}, u32[]{:S(2)}, u32[]{:S(2)}) collective-permute-start(bf16[64,1024]{1,0:T(8,128)(2,1)S(1)} %collective-permute-done.10), channel_id=1, source_target_pairs={{0,2},{1,3},{2,0},{3,1},{4,6},{5,7},{6,4},{7,5},{8,10},{9,11},{10,... | collective-permute-start | bytes 393224 | tf_op jit(solution)/shard_map/ppermute | solution.py:79
  28.3 5.0 %collective-permute-start.5 = (bf16[64,1024]{1,0:T(8,128)(2,1)S(1)}, bf16[64,1024]{1,0:T(8,128)(2,1)S(1)}, u32[]{:S(2)}, u32[]{:S(2)}) collective-permute-start(bf16[64,1024]{1,0:T(8,128)(2,1)S(1)} %collective-permute-done.3), channel_id=1, source_target_pairs={{0,4},{4,0},{1,5},{5,1},{2,6},{6,2},{3,7},{7,3},{8,12},{12,8},{9,1... | collective-permute-start | bytes 393224 | tf_op jit(solution)/shard_map/ppermute | solution.py:89
  30.5 18.2 %collective-permute-start.14 = (bf16[64,1024]{1,0:T(8,128)(2,1)S(1)}, bf16[64,1024]{1,0:T(8,128)(2,1)S(1)}, u32[]{:S(2)}, u32[]{:S(2)}) collective-permute-start(bf16[64,1024]{1,0:T(8,128)(2,1)S(1)} %collective-permute-done.10), channel_id=1, source_target_pairs={{0,1},{1,0},{2,3},{3,2},{4,5},{5,4},{6,7},{7,6},{8,9},{9,8},{10,11... | collective-permute-start | bytes 393224 | tf_op jit(solution)/shard_map/ppermute | solution.py:79
  33.3 15.9 %collective-permute-start.19 = (bf16[64,1024]{1,0:T(8,128)(2,1)S(1)}, bf16[64,1024]{1,0:T(8,128)(2,1)S(1)}, u32[]{:S(2)}, u32[]{:S(2)}) collective-permute-start(bf16[64,1024]{1,0:T(8,128)(2,1)S(1)} %collective-permute-done.18), channel_id=1, source_target_pairs={{0,4},{4,0},{1,5},{5,1},{2,6},{6,2},{3,7},{7,3},{8,12},{12,8},{9,1... | collective-permute-start | bytes 393224 | tf_op jit(solution)/shard_map/ppermute | solution.py:89
  35.5 1.3 %collective-permute-start.7 = (bf16[64,1024]{1,0:T(8,128)(2,1)S(1)}, bf16[64,1024]{1,0:T(8,128)(2,1)S(1)}, u32[]{:S(2)}, u32[]{:S(2)}) collective-permute-start(bf16[64,1024]{1,0:T(8,128)(2,1)S(1)} %collective-permute-done.3), channel_id=1, source_target_pairs={{0,1},{1,0},{2,3},{3,2},{4,5},{5,4},{6,7},{7,6},{8,9},{9,8},{10,11... | collective-permute-start | bytes 393224 | tf_op jit(solution)/shard_map/ppermute | solution.py:79
  36.8 1.3 %collective-permute-start.8 = (bf16[64,1024]{1,0:T(8,128)(2,1)S(1)}, bf16[64,1024]{1,0:T(8,128)(2,1)S(1)}, u32[]{:S(2)}, u32[]{:S(2)}) collective-permute-start(bf16[64,1024]{1,0:T(8,128)(2,1)S(1)} %collective-permute-done.4), channel_id=1, source_target_pairs={{0,1},{1,0},{2,3},{3,2},{4,5},{5,4},{6,7},{7,6},{8,9},{9,8},{10,11... | collective-permute-start | bytes 393224 | tf_op jit(solution)/shard_map/ppermute | solution.py:79
  38.2 1.3 %collective-permute-start.9 = (bf16[64,1024]{1,0:T(8,128)(2,1)S(1)}, bf16[64,1024]{1,0:T(8,128)(2,1)S(1)}, u32[]{:S(2)}, u32[]{:S(2)}) collective-permute-start(bf16[64,1024]{1,0:T(8,128)(2,1)S(1)} %collective-permute-done.5), channel_id=1, source_target_pairs={{0,1},{1,0},{2,3},{3,2},{4,5},{5,4},{6,7},{7,6},{8,9},{9,8},{10,11... | collective-permute-start | bytes 393224 | tf_op jit(solution)/shard_map/ppermute | solution.py:79
  39.5 11.8 %collective-permute-start.20 = (bf16[64,1024]{1,0:T(8,128)(2,1)S(1)}, bf16[64,1024]{1,0:T(8,128)(2,1)S(1)}, u32[]{:S(2)}, u32[]{:S(2)}) collective-permute-start(bf16[64,1024]{1,0:T(8,128)(2,1)S(1)} %collective-permute-done.18), channel_id=1, source_target_pairs={{0,2},{1,3},{2,0},{3,1},{4,6},{5,7},{6,4},{7,5},{8,10},{9,11},{10,... | collective-permute-start | bytes 393224 | tf_op jit(solution)/shard_map/ppermute | solution.py:79
  41.5 17.2 %collective-permute-start.22 = (bf16[64,1024]{1,0:T(8,128)(2,1)S(1)}, bf16[64,1024]{1,0:T(8,128)(2,1)S(1)}, u32[]{:S(2)}, u32[]{:S(2)}) collective-permute-start(bf16[64,1024]{1,0:T(8,128)(2,1)S(1)} %collective-permute-done.18), channel_id=1, source_target_pairs={{0,1},{1,0},{2,3},{3,2},{4,5},{5,4},{6,7},{7,6},{8,9},{9,8},{10,11... | collective-permute-start | bytes 393224 | tf_op jit(solution)/shard_map/ppermute | solution.py:79
  42.1 5.9 %collective-permute-start.13 = (bf16[64,1024]{1,0:T(8,128)(2,1)S(1)}, bf16[64,1024]{1,0:T(8,128)(2,1)S(1)}, u32[]{:S(2)}, u32[]{:S(2)}) collective-permute-start(bf16[64,1024]{1,0:T(8,128)(2,1)S(1)} %collective-permute-done.11), channel_id=1, source_target_pairs={{0,2},{1,3},{2,0},{3,1},{4,6},{5,7},{6,4},{7,5},{8,10},{9,11},{10,... | collective-permute-start | bytes 393224 | tf_op jit(solution)/shard_map/ppermute | solution.py:79
  48.1 3.2 %collective-permute-start.15 = (bf16[64,1024]{1,0:T(8,128)(2,1)S(1)}, bf16[64,1024]{1,0:T(8,128)(2,1)S(1)}, u32[]{:S(2)}, u32[]{:S(2)}) collective-permute-start(bf16[64,1024]{1,0:T(8,128)(2,1)S(1)} %collective-permute-done.11), channel_id=1, source_target_pairs={{0,1},{1,0},{2,3},{3,2},{4,5},{5,4},{6,7},{7,6},{8,9},{9,8},{10,11... | collective-permute-start | bytes 393224 | tf_op jit(solution)/shard_map/ppermute | solution.py:79
  48.7 3.7 %collective-permute-start.16 = (bf16[64,1024]{1,0:T(8,128)(2,1)S(1)}, bf16[64,1024]{1,0:T(8,128)(2,1)S(1)}, u32[]{:S(2)}, u32[]{:S(2)}) collective-permute-start(bf16[64,1024]{1,0:T(8,128)(2,1)S(1)} %collective-permute-done.12), channel_id=1, source_target_pairs={{0,1},{1,0},{2,3},{3,2},{4,5},{5,4},{6,7},{7,6},{8,9},{9,8},{10,11... | collective-permute-start | bytes 393224 | tf_op jit(solution)/shard_map/ppermute | solution.py:79
  49.2 5.5 %collective-permute-start.21 = (bf16[64,1024]{1,0:T(8,128)(2,1)S(1)}, bf16[64,1024]{1,0:T(8,128)(2,1)S(1)}, u32[]{:S(2)}, u32[]{:S(2)}) collective-permute-start(bf16[64,1024]{1,0:T(8,128)(2,1)S(1)} %collective-permute-done.19), channel_id=1, source_target_pairs={{0,2},{1,3},{2,0},{3,1},{4,6},{5,7},{6,4},{7,5},{8,10},{9,11},{10,... | collective-permute-start | bytes 393224 | tf_op jit(solution)/shard_map/ppermute | solution.py:79
  51.3 8.0 %collective-permute-start.23 = (bf16[64,1024]{1,0:T(8,128)(2,1)S(1)}, bf16[64,1024]{1,0:T(8,128)(2,1)S(1)}, u32[]{:S(2)}, u32[]{:S(2)}) collective-permute-start(bf16[64,1024]{1,0:T(8,128)(2,1)S(1)} %collective-permute-done.19), channel_id=1, source_target_pairs={{0,1},{1,0},{2,3},{3,2},{4,5},{5,4},{6,7},{7,6},{8,9},{9,8},{10,11... | collective-permute-start | bytes 393224 | tf_op jit(solution)/shard_map/ppermute | solution.py:79
  51.3 8.7 %collective-permute-start.24 = (bf16[64,1024]{1,0:T(8,128)(2,1)S(1)}, bf16[64,1024]{1,0:T(8,128)(2,1)S(1)}, u32[]{:S(2)}, u32[]{:S(2)}) collective-permute-start(bf16[64,1024]{1,0:T(8,128)(2,1)S(1)} %collective-permute-done.20), channel_id=1, source_target_pairs={{0,1},{1,0},{2,3},{3,2},{4,5},{5,4},{6,7},{7,6},{8,9},{9,8},{10,11... | collective-permute-start | bytes 393224 | tf_op jit(solution)/shard_map/ppermute | solution.py:79
  52.5 2.9 %collective-permute-start.17 = (bf16[64,1024]{1,0:T(8,128)(2,1)S(1)}, bf16[64,1024]{1,0:T(8,128)(2,1)S(1)}, u32[]{:S(2)}, u32[]{:S(2)}) collective-permute-start(bf16[64,1024]{1,0:T(8,128)(2,1)S(1)} %collective-permute-done.13), channel_id=1, source_target_pairs={{0,1},{1,0},{2,3},{3,2},{4,5},{5,4},{6,7},{7,6},{8,9},{9,8},{10,11... | collective-permute-start | bytes 393224 | tf_op jit(solution)/shard_map/ppermute | solution.py:79
  54.7 5.9 %collective-permute-start.25 = (bf16[64,1024]{1,0:T(8,128)(2,1)S(1)}, bf16[64,1024]{1,0:T(8,128)(2,1)S(1)}, u32[]{:S(2)}, u32[]{:S(2)}) collective-permute-start(bf16[64,1024]{1,0:T(8,128)(2,1)S(1)} %collective-permute-done.21), channel_id=1, source_target_pairs={{0,1},{1,0},{2,3},{3,2},{4,5},{5,4},{6,7},{7,6},{8,9},{9,8},{10,11... | collective-permute-start | bytes 393224 | tf_op jit(solution)/shard_map/ppermute | solution.py:79
  81.5 3.4 %copy-start = (f32[2048,512]{1,0:T(8,128)S(1)}, f32[2048,512]{1,0:T(8,128)}, u32[]{:S(2)}) copy-start(f32[2048,512]{1,0:T(8,128)} %get-tuple-element.26) | copy-start | bytes 12582916

commit v19 on v17

--- a/solution.py
+++ b/solution.py
@@ -96,10 +96,13 @@
             cur = jnp.concatenate([cur, other], axis=1)
         return cur
 
-    parts = [None] + [
-        spread_x_first(piece) if sz <= 2 else spread(pair_of(piece))
-        for sz, piece in enumerate(landed[1:], start=1)
-    ]
+    parts = [None, spread_x_first(landed[1])] if n_o > 1 else [None]
+    if n_o > 2:
+        late = pair_of(jnp.stack(landed[2:]))
+        for bit in reversed(bits):
+            other = lax.ppermute(late, "cent", [(i, i ^ bit) for i in range(n_c)])
+            late = jnp.concatenate([late, other], axis=2)
+        parts += [late[:, g] for g in range(n_o - 2)]
 
     h = q % 2
     half = t // 2

time: 67.7 us -> 84.6 us (1.25)
  the two profiles are of different devices: /device:TPU:17 before, /device:TPU:0 now
where the time goes in v19:
time: 84.6 us; the launch traced here: 84.2 us
  waiting for transfers between devices  26.2 us (31%)
  other arithmetic  20.8 us (25%)
  starting transfers between devices  11.4 us (13%)
  blocking collectives  9.32 us (11%)
  matrix products  8.29 us (10%)
  local copies, waits for them, and re-layouts  7.81 us (9%)
    ppermute x3, waiting for transfers between devices, shards_all(): landed.append(lax.ppermute(mine, 'outer', pairs))  11.1 us
    all_gather x1, blocking collectives, shards_all(): every = lax.all_gather(both, ('dp', 'cent'), axis=0)  9.32 us
    ppermute x2, waiting for transfers between devices, pair_of(): lax.ppermute(piece, 'dp', [(j, (j + sy) % n_d) for j in range(n_d)])  7.91 us
    ppermute x1, waiting for transfers between devices, spread_x_first(): other = lax.ppermute(piece, 'cent', [(i, i ^ order[0]) for i in range(n_c)])  7.07 us
    ppermute x3, starting transfers between devices, shards_all(): landed.append(lax.ppermute(mine, 'outer', pairs))  5.12 us
    dot_general x1, matrix products, scores_for(): lax.dot_general(piece, cent_bf, (((1,), (1,)), ((), ())), preferred_eleme...  4.62 us
    concatenate x2, other arithmetic, shards_all(): late = jnp.concatenate([late, other], axis=2)  3.75 us
    dot_general x1, matrix products, shards_all(): lax.dot_general(scaled.reshape(n_o * pod, k), everything, (((0,), (0,)),...  3.67 us
  transfers between devices with their start and end apart: 11, of which 6 were waited for; matrix products, arithmetic and copies ran while one was open for 17% of the time, Pallas kernels for 0%

profile of v19, /device:TPU:0, one launch (start us, length us, event | category | flops | bytes accessed | tf_op | source)
XLA Modules:
  0.0 84.2 jit_solution(18321163126877150455)
XLA Ops:
  0.0 1.4 %convert_element_type.22 = bf16[256,1024]{1,0:T(8,128)(2,1)S(1)} convert(f32[256,1024]{1,0:T(8,128)} %param.3) | non-fusion elementwise | flops 262144 | bytes 1572864 | tf_op jit(solution)/shard_map/convert_element_type | solution.py:56
  1.5 0.0 copy-start.5
  1.5 0.8 copy-done.5
  2.3 0.0 copy-start.4
  2.3 5.1 %collective-permute-start.7 = (bf16[64,1024]{1,0:T(8,128)(2,1)S(1)}, bf16[64,1024]{1,0:T(8,128)(2,1)S(1)}, u32[]{:S(2)}, u32[]{:S(2)}) collective-permute-start(bf16[64,1024]{1,0:T(8,128)(2,1)S(1)} %constant_dynamic-slice_fusion), channel_id=1, source_target_pairs={{0,24},{8,16},{16,8},{24,0},{1,25},{9,17},{17,9},{25,1},{2,26},{10... | collective-permute-start | bytes 393224 | tf_op jit(solution)/shard_map/ppermute | solution.py:89
  7.4 0.0 collective-permute-start.6
  7.4 4.4 %collective-permute-done.7 = bf16[64,1024]{1,0:T(8,128)(2,1)S(1)} collective-permute-done((bf16[64,1024]{1,0:T(8,128)(2,1)S(1)}, bf16[64,1024]{1,0:T(8,128)(2,1)S(1)}, u32[]{:S(2)}, u32[]{:S(2)}) %collective-permute-start.7) | collective-permute-done | bytes 131104 | tf_op jit(solution)/shard_map/ppermute | solution.py:89
  11.8 6.6 %collective-permute-done.6 = bf16[64,1024]{1,0:T(8,128)(2,1)S(1)} collective-permute-done((bf16[64,1024]{1,0:T(8,128)(2,1)S(1)}, bf16[64,1024]{1,0:T(8,128)(2,1)S(1)}, u32[]{:S(2)}, u32[]{:S(2)}) %collective-permute-start.6) | collective-permute-done | bytes 131104 | tf_op jit(solution)/shard_map/ppermute | solution.py:89
  18.5 0.7 fusion.22
  19.2 1.5 %collective-permute-start.8 = (bf16[2,64,1024]{2,1,0:T(8,128)(2,1)}, bf16[2,64,1024]{2,1,0:T(8,128)(2,1)}, u32[]{:S(2)}, u32[]{:S(2)}) collective-permute-start(bf16[2,64,1024]{2,1,0:T(8,128)(2,1)} %get-tuple-element.14), channel_id=1, source_target_pairs={{0,4},{4,0},{1,5},{5,1},{2,6},{6,2},{3,7},{7,3},{8,12},{12,8},{9,1... | collective-permute-start | bytes 786440 | tf_op jit(solution)/shard_map/ppermute | solution.py:74
  20.7 0.0 collective-permute-start.2
  20.7 1.7 %constant_dynamic-slice_fusion.1 = bf16[128,1024]{1,0:T(8,128)(2,1)} fusion(bf16[256,1024]{1,0:T(8,128)(2,1)} %copy-done.5, s32[]{:T(128)S(6)} %select_n.127), kind=kLoop, calls=%fused_computation.52 | loop fusion | bytes 524292 | tf_op jit(solution)/shard_map/dynamic_slice | solution.py:109
  22.4 0.5 collective-permute-start
  22.9 5.8 %collective-permute-done.8 = bf16[2,64,1024]{2,1,0:T(8,128)(2,1)} collective-permute-done((bf16[2,64,1024]{2,1,0:T(8,128)(2,1)}, bf16[2,64,1024]{2,1,0:T(8,128)(2,1)}, u32[]{:S(2)}, u32[]{:S(2)}) %collective-permute-start.8) | collective-permute-done | bytes 262176 | tf_op jit(solution)/shard_map/ppermute | solution.py:74
  28.7 1.8 %pad_maximum_fusion.3 = bf16[2,2,64,1024]{3,2,1,0:T(8,128)(2,1)} fusion(bf16[1,2,64,1024]{3,2,1,0:T(8,128)(2,1)} %bitcast.7, bf16[1,2,64,1024]{3,2,1,0:T(8,128)(2,1)S(1)} %get-tuple-element.13), kind=kLoop, calls=%fused_computation.20 | loop fusion | flops 262144 | bytes 1048576 | tf_op jit(solution)/shard_map/stack | solution.py:75
  30.5 1.5 %collective-permute-start.9 = (bf16[2,2,64,1024]{3,2,1,0:T(8,128)(2,1)}, bf16[2,2,64,1024]{3,2,1,0:T(8,128)(2,1)}, u32[]{:S(2)}, u32[]{:S(2)}) collective-permute-start(bf16[2,2,64,1024]{3,2,1,0:T(8,128)(2,1)} %pad_maximum_fusion.3), channel_id=1, source_target_pairs={{0,2},{1,3},{2,0},{3,1},{4,6},{5,7},{6,4},{7,5},{8,10},{9,11},{10,... | collective-permute-start | bytes 1572872 | tf_op jit(solution)/shard_map/ppermute | solution.py:103
  32.0 1.2 %fusion.19 = (s32[1,4]{1,0:T(1,128)S(1)}, s32[1,4]{1,0:T(1,128)S(1)}, s32[1,4]{1,0:T(1,128)S(1)}, s32[1,4]{1,0:T(1,128)S(1)}, s32[1,4]{1,0:T(1,128)}, /*index=5*/s32[1,4]{1,0:T(1,128)}, s32[1,4]{1,0:T(1,128)}, s32[1,4]{1,0:T(1,128)}) fusion(s32[4]{0:T(128)} %constant.103.clone, pred[]{:T(512)S(6)} %eq.65, s32[]{:T(128)S(6)} %axis_index.32, ...), kind=kLoop, calls=%fused_computation.72 | loop fusion | flops 96 | bytes 156 | tf_op jit(solution)/shard_map/stack | solution.py:136
  33.3 0.6 stack.128
  33.9 0.0 collective-permute-done.2
  33.9 0.6 collective-permute-start.3
  34.5 0.6 iota_compare_fusion.1
  35.1 1.6 %constant_dynamic-update-slice_fusion.1 = bf16[128,1024]{1,0:T(8,128)(2,1)} fusion(bf16[64,1024]{1,0:T(8,128)(2,1)} %collective-permute-done.2), kind=kLoop, calls=%fused_computation.39 | loop fusion | bytes 262144
  36.7 7.1 %collective-permute-done.3 = bf16[64,1024]{1,0:T(8,128)(2,1)S(1)} collective-permute-done((bf16[64,1024]{1,0:T(8,128)(2,1)}, bf16[64,1024]{1,0:T(8,128)(2,1)S(1)}, u32[]{:S(2)}, u32[]{:S(2)}) %collective-permute-start.3) | collective-permute-done | bytes 131104 | tf_op jit(solution)/shard_map/ppermute | solution.py:92
  43.7 0.7 constant_dynamic-update-slice_fusion
  44.4 1.5 %collective-permute-start.4 = (bf16[128,1024]{1,0:T(8,128)(2,1)}, bf16[128,1024]{1,0:T(8,128)(2,1)}, u32[]{:S(2)}, u32[]{:S(2)}) collective-permute-start(bf16[128,1024]{1,0:T(8,128)(2,1)} %constant_dynamic-update-slice_fusion), channel_id=1, source_target_pairs={{0,4},{4,0},{1,5},{5,1},{2,6},{6,2},{3,7},{7,3},{8,12},{12,8},{9,1... | collective-permute-start | bytes 786440 | tf_op jit(solution)/shard_map/ppermute | solution.py:74
  45.9 0.0 collective-permute-done.9
  45.9 2.1 %pad_maximum_fusion.1 = bf16[2,2,128,1024]{3,2,1,0:T(8,128)(2,1)} fusion(bf16[2,2,64,1024]{3,2,1,0:T(8,128)(2,1)} %collective-permute-done.9, bf16[1,2,64,1024]{3,2,1,0:T(8,128)(2,1)} %bitcast.7, bf16[1,2,64,1024]{3,2,1,0:T(8,128)(2,1)S(1)} %get-tuple-element.13), kind=kLoop, calls=%fused_computation.16 | loop fusion | flops 3145728 | bytes 2097152 | tf_op jit(solution)/shard_map/concatenate | solution.py:104
  48.1 0.0 collective-permute-start.10
  48.1 0.2 multiply_reduce_fusion
  48.3 0.0 copy-done.6
  48.3 0.0 copy-done.7
  48.4 0.1 copy.27
  48.5 0.0 collective-permute-done
  48.5 0.6 collective-permute-start.1
  49.0 2.1 %collective-permute-done.4 = bf16[128,1024]{1,0:T(8,128)(2,1)} collective-permute-done((bf16[128,1024]{1,0:T(8,128)(2,1)}, bf16[128,1024]{1,0:T(8,128)(2,1)}, u32[]{:S(2)}, u32[]{:S(2)}) %collective-permute-start.4) | collective-permute-done | bytes 262176 | tf_op jit(solution)/shard_map/ppermute | solution.py:74
  51.1 1.1 %pad_maximum_fusion.2 = bf16[2,128,1024]{2,1,0:T(8,128)(2,1)S(1)} fusion(bf16[1,128,1024]{2,1,0:T(8,128)(2,1)} %bitcast.3, bf16[1,128,1024]{2,1,0:T(8,128)(2,1)} %bitcast.2), kind=kLoop, calls=%fused_computation.19 | loop fusion | flops 262144 | bytes 1048576 | tf_op jit(solution)/shard_map/stack | solution.py:75
  52.2 0.1 collective-permute-start.5
  52.3 0.1 convert_bitcast_fusion
  52.3 0.0 collective-permute-done.1
  52.3 1.0 %maximum_bitcast_fusion = bf16[1,256,1024]{2,1,0:T(8,128)(2,1)S(1)} fusion(bf16[128,1024]{1,0:T(8,128)(2,1)S(1)} %collective-permute-done.1, bf16[128,1024]{1,0:T(8,128)(2,1)} %collective-permute-done), kind=kLoop, calls=%fused_computation.18 | loop fusion | flops 1048576 | bytes 1048576 | tf_op jit(solution)/shard_map/stack | solution.py:115
  53.3 0.5 broadcast_in_dim.138
  53.9 0.1 maximum_dynamic-update-slice_fusion
  54.0 0.2 collective-permute-done.5
  54.1 1.1 %maximum_dynamic-update-slice_fusion.1 = bf16[8,256,1024]{2,1,0:T(8,128)(2,1)S(1)} fusion(bf16[8,256,1024]{2,1,0:T(8,128)(2,1)S(1)} %maximum_dynamic-update-slice_fusion, s32[]{:T(128)S(6)} %select_n.130, bf16[2,128,1024]{2,1,0:T(8,128)(2,1)S(1)} %collective-permute-done.5, bf16[1,128,1024]{2,1,0:T(8,128)(2,1)} %bitcast.3, bf16[1,128,1024]{2,1,0:T(8,128)(2,1)} %bitcast.2), kind=kLoop, calls=%fused_computation.15 | loop fusion | flops 3145728 | bytes 2097156 | tf_op jit(solution)/shard_map/dynamic_update_slice | solution.py:120
  55.3 0.0 collective-permute-done.10
  55.3 1.6 %pad_maximum_fusion = bf16[2,2,256,1024]{3,2,1,0:T(8,128)(2,1)S(1)} fusion(bf16[2,2,128,1024]{3,2,1,0:T(8,128)(2,1)} %collective-permute-done.10, bf16[2,2,64,1024]{3,2,1,0:T(8,128)(2,1)} %collective-permute-done.9, bf16[1,2,64,1024]{3,2,1,0:T(8,128)(2,1)} %bitcast.7, bf16[1,2,64,1024]{3,2,1,0:T(8,128)(2,1)S(1)} %get-tuple-element.13), kind=kLoop, calls=%fused_computation.7 | loop fusion | flops 8388608 | bytes 4194304 | tf_op jit(solution)/shard_map/concatenate | solution.py:104
  56.9 0.1 fusion.3
  57.0 0.1 fusion.2
  57.1 4.6 %fusion.24 = (f32[2048]{0:T(1024)S(1)}, f32[2048,512]{1,0:T(8,128)}) fusion(f32[512]{0:T(512)S(1)} %multiply_reduce_fusion, bf16[2048,1024]{1,0:T(8,128)(2,1)S(1)} %bitcast.77, f32[512,1024]{1,0:T(8,128)S(1)} %copy-done.3), kind=kOutput, calls=%fused_computation.77 | convolution fusion | flops 2152200192 | bytes 10496000 | tf_op jit(solution)/shard_map/dot_general | solution.py:10
  61.7 0.1 broadcast_in_dim.141
  61.8 3.3 %exponential_reduce_fusion = f32[2048]{0:T(1024)S(1)} fusion(f32[2048,512]{1,0:T(8,128)} %get-tuple-element.28, f32[2048]{0:T(1024)S(1)} %get-tuple-element.27), kind=kLoop, calls=%fused_computation.4 | loop fusion | flops 2095104 | bytes 4210688 | tf_op jit(solution)/shard_map/reduce_sum | solution.py:18
  65.1 0.1 broadcast_in_dim.146
  65.2 0.1 select_reduce_fusion.7
  65.3 0.2 select_reduce_fusion.3
  65.5 9.3 %all-gather = f32[16,8,4,64]{3,1,2,0:T(8,128)S(1)} all-gather(f32[2,8,4,64]{3,1,2,0:T(8,128)S(1)} %copy.30), channel_id=2, replica_groups=mesh['outer'=4,'dp'=2,'cent'=4] {'dp','cent'}, dimensions={0}, use_global_device_ids=true | all-gather | bytes 147456 | tf_op jit(solution)/shard_map/all_gather | solution.py:150
  74.9 0.1 select_reduce_fusion.1
  75.0 0.1 select_reduce_fusion.5
  75.1 0.1 div.62
  75.2 0.1 sub.53
  75.3 2.8 %bitcast_reduce_fusion = f32[4,512]{1,0:T(4,128)S(1)} fusion(f32[2048]{0:T(1024)S(1)} %div.62, f32[2048,512]{1,0:T(8,128)} %get-tuple-element.28, f32[2048]{0:T(1024)S(1)} %sub.53), kind=kLoop, calls=%fused_computation.2 | loop fusion | flops 5240832 | bytes 4218880 | tf_op jit(solution)/shard_map/reduce_sum | solution.py:161
  78.2 0.6 copy-done
  78.8 1.0 %fusion = bf16[2048,512]{1,0:T(8,128)(2,1)S(1)} fusion(f32[4,512]{1,0:T(4,128)S(1)} %broadcast_add_fusion, f32[2048]{0:T(1024)S(1)} %div.62, f32[2048,512]{1,0:T(8,128)S(1)} %copy-done, f32[2048]{0:T(1024)S(1)} %sub.53), kind=kLoop, calls=%fused_computation.1 | loop fusion | flops 6291456 | bytes 6316032 | tf_op jit(solution)/shard_map/convert_element_type | solution.py:162
  79.8 0.7 copy-done.2
  80.5 3.7 %subtract_multiply_fusion.1 = f32[512,1024]{1,0:T(8,128)} fusion(f32[512,1024]{1,0:T(8,128)S(1)} %copy-done.3, bf16[2048,512]{1,0:T(8,128)(2,1)S(1)} %fusion, bf16[2048,1024]{1,0:T(8,128)(2,1)S(1)} %bitcast.78, f32[512]{0:T(512)S(1)} %fusion.10), kind=kOutput, calls=%fused_computation.8 | convolution fusion | flops 2149056512 | bytes 10487808 | tf_op jit(solution)/shard_map/dot_general | solution.py:163
  (29 shorter events, 0.2 us)
Async XLA Ops:
  0.0 48.1 %copy-start.3 = (f32[512,1024]{1,0:T(8,128)S(1)}, f32[512,1024]{1,0:T(8,128)}, u32[]{:S(2)}) copy-start(f32[512,1024]{1,0:T(8,128)} %param.4) | copy-start | bytes 6291460
  1.5 0.8 copy-start.5
  2.3 50.0 %copy-start.4 = (f32[256,1024]{1,0:T(8,128)S(1)}, f32[256,1024]{1,0:T(8,128)}, u32[]{:S(2)}) copy-start(f32[256,1024]{1,0:T(8,128)} %param.3) | copy-start | bytes 3145732
  2.3 9.5 %collective-permute-start.7 = (bf16[64,1024]{1,0:T(8,128)(2,1)S(1)}, bf16[64,1024]{1,0:T(8,128)(2,1)S(1)}, u32[]{:S(2)}, u32[]{:S(2)}) collective-permute-start(bf16[64,1024]{1,0:T(8,128)(2,1)S(1)} %constant_dynamic-slice_fusion), channel_id=1, source_target_pairs={{0,24},{8,16},{16,8},{24,0},{1,25},{9,17},{17,9},{25,1},{2,26},{10... | collective-permute-start | bytes 393224 | tf_op jit(solution)/shard_map/ppermute | solution.py:89
  7.4 11.1 %collective-permute-start.6 = (bf16[64,1024]{1,0:T(8,128)(2,1)S(1)}, bf16[64,1024]{1,0:T(8,128)(2,1)S(1)}, u32[]{:S(2)}, u32[]{:S(2)}) collective-permute-start(bf16[64,1024]{1,0:T(8,128)(2,1)S(1)} %constant_dynamic-slice_fusion), channel_id=1, source_target_pairs={{0,16},{8,24},{16,0},{24,8},{1,17},{9,25},{17,1},{25,9},{2,18},{10... | collective-permute-start | bytes 393224 | tf_op jit(solution)/shard_map/ppermute | solution.py:89
  19.2 9.6 %collective-permute-start.8 = (bf16[2,64,1024]{2,1,0:T(8,128)(2,1)}, bf16[2,64,1024]{2,1,0:T(8,128)(2,1)}, u32[]{:S(2)}, u32[]{:S(2)}) collective-permute-start(bf16[2,64,1024]{2,1,0:T(8,128)(2,1)} %get-tuple-element.14), channel_id=1, source_target_pairs={{0,4},{4,0},{1,5},{5,1},{2,6},{6,2},{3,7},{7,3},{8,12},{12,8},{9,1... | collective-permute-start | bytes 786440 | tf_op jit(solution)/shard_map/ppermute | solution.py:74
  20.7 13.2 %collective-permute-start.2 = (bf16[64,1024]{1,0:T(8,128)(2,1)S(1)}, bf16[64,1024]{1,0:T(8,128)(2,1)}, u32[]{:S(2)}, u32[]{:S(2)}) collective-permute-start(bf16[64,1024]{1,0:T(8,128)(2,1)S(1)} %constant_dynamic-slice_fusion), channel_id=1, source_target_pairs={{0,8},{8,0},{16,24},{24,16},{1,9},{9,1},{17,25},{25,17},{2,10},{10... | collective-permute-start | bytes 393224 | tf_op jit(solution)/shard_map/ppermute | solution.py:89
  22.4 26.1 %collective-permute-start = (bf16[128,1024]{1,0:T(8,128)(2,1)}, bf16[128,1024]{1,0:T(8,128)(2,1)}, u32[]{:S(2)}, u32[]{:S(2)}) collective-permute-start(bf16[128,1024]{1,0:T(8,128)(2,1)} %constant_dynamic-slice_fusion.1), channel_id=1, source_target_pairs={{0,4},{4,0},{1,5},{5,1},{2,6},{6,2},{3,7},{7,3},{8,12},{12,8},{9,1... | collective-permute-start | bytes 786440 | tf_op jit(solution)/shard_map/ppermute | solution.py:112
  30.5 15.4 %collective-permute-start.9 = (bf16[2,2,64,1024]{3,2,1,0:T(8,128)(2,1)}, bf16[2,2,64,1024]{3,2,1,0:T(8,128)(2,1)}, u32[]{:S(2)}, u32[]{:S(2)}) collective-permute-start(bf16[2,2,64,1024]{3,2,1,0:T(8,128)(2,1)} %pad_maximum_fusion.3), channel_id=1, source_target_pairs={{0,2},{1,3},{2,0},{3,1},{4,6},{5,7},{6,4},{7,5},{8,10},{9,11},{10,... | collective-permute-start | bytes 1572872 | tf_op jit(solution)/shard_map/ppermute | solution.py:103
  33.9 14.4 %copy-start.6 = (s32[1,4]{1,0:T(1,128)S(1)}, s32[1,4]{1,0:T(1,128)}, u32[]{:S(2)}) copy-start(s32[1,4]{1,0:T(1,128)} %get-tuple-element.23) | copy-start | bytes 52
  33.9 14.4 %copy-start.7 = (s32[1,4]{1,0:T(1,128)S(1)}, s32[1,4]{1,0:T(1,128)}, u32[]{:S(2)}) copy-start(s32[1,4]{1,0:T(1,128)} %get-tuple-element.24) | copy-start | bytes 52
  33.9 14.4 %copy-start.8 = (s32[1,4]{1,0:T(1,128)S(1)}, s32[1,4]{1,0:T(1,128)}, u32[]{:S(2)}) copy-start(s32[1,4]{1,0:T(1,128)} %get-tuple-element.25) | copy-start | bytes 52
  33.9 14.4 %copy-start.9 = (s32[1,4]{1,0:T(1,128)S(1)}, s32[1,4]{1,0:T(1,128)}, u32[]{:S(2)}) copy-start(s32[1,4]{1,0:T(1,128)} %get-tuple-element.26) | copy-start | bytes 52
  33.9 9.8 %collective-permute-start.3 = (bf16[64,1024]{1,0:T(8,128)(2,1)}, bf16[64,1024]{1,0:T(8,128)(2,1)S(1)}, u32[]{:S(2)}, u32[]{:S(2)}) collective-permute-start(bf16[64,1024]{1,0:T(8,128)(2,1)} %collective-permute-done.2), channel_id=1, source_target_pairs={{0,2},{1,3},{2,0},{3,1},{4,6},{5,7},{6,4},{7,5},{8,10},{9,11},{10,... | collective-permute-start | bytes 393224 | tf_op jit(solution)/shard_map/ppermute | solution.py:92
  44.4 6.7 %collective-permute-start.4 = (bf16[128,1024]{1,0:T(8,128)(2,1)}, bf16[128,1024]{1,0:T(8,128)(2,1)}, u32[]{:S(2)}, u32[]{:S(2)}) collective-permute-start(bf16[128,1024]{1,0:T(8,128)(2,1)} %constant_dynamic-update-slice_fusion), channel_id=1, source_target_pairs={{0,4},{4,0},{1,5},{5,1},{2,6},{6,2},{3,7},{7,3},{8,12},{12,8},{9,1... | collective-permute-start | bytes 786440 | tf_op jit(solution)/shard_map/ppermute | solution.py:74
  48.1 7.2 %collective-permute-start.10 = (bf16[2,2,128,1024]{3,2,1,0:T(8,128)(2,1)}, bf16[2,2,128,1024]{3,2,1,0:T(8,128)(2,1)}, u32[]{:S(2)}, u32[]{:S(2)}) collective-permute-start(bf16[2,2,128,1024]{3,2,1,0:T(8,128)(2,1)} %pad_maximum_fusion.1), channel_id=1, source_target_pairs={{0,1},{1,0},{2,3},{3,2},{4,5},{5,4},{6,7},{7,6},{8,9},{9,8},{10,11... | collective-permute-start | bytes 3145736 | tf_op jit(solution)/shard_map/ppermute | solution.py:103
  48.5 3.9 %collective-permute-start.1 = (bf16[128,1024]{1,0:T(8,128)(2,1)}, bf16[128,1024]{1,0:T(8,128)(2,1)S(1)}, u32[]{:S(2)}, u32[]{:S(2)}) collective-permute-start(bf16[128,1024]{1,0:T(8,128)(2,1)} %collective-permute-done), channel_id=1, source_target_pairs={{0,1},{1,0},{2,3},{3,2},{4,5},{5,4},{6,7},{7,6},{8,9},{9,8},{10,11... | collective-permute-start | bytes 786440 | tf_op jit(solution)/shard_map/ppermute | solution.py:113
  52.2 2.0 %collective-permute-start.5 = (bf16[2,128,1024]{2,1,0:T(8,128)(2,1)S(1)}, bf16[2,128,1024]{2,1,0:T(8,128)(2,1)S(1)}, u32[]{:S(2)}, u32[]{:S(2)}) collective-permute-start(bf16[2,128,1024]{2,1,0:T(8,128)(2,1)S(1)} %pad_maximum_fusion.2), channel_id=1, source_target_pairs={{0,1},{1,0},{2,3},{3,2},{4,5},{5,4},{6,7},{7,6},{8,9},{9,8},{10,11... | collective-permute-start | bytes 1572872 | tf_op jit(solution)/shard_map/ppermute | solution.py:95
  57.1 4.6 %copy-start.1 = (bf16[8,256,1024]{2,1,0:T(8,128)(2,1)}, bf16[8,256,1024]{2,1,0:T(8,128)(2,1)S(1)}, u32[]{:S(2)}) copy-start(bf16[8,256,1024]{2,1,0:T(8,128)(2,1)S(1)} %fusion.2) | copy-start | bytes 12582916
  75.3 3.4 %copy-start = (f32[2048,512]{1,0:T(8,128)S(1)}, f32[2048,512]{1,0:T(8,128)}, u32[]{:S(2)}) copy-start(f32[2048,512]{1,0:T(8,128)} %get-tuple-element.28) | copy-start | bytes 12582916
  78.2 2.3 %copy-start.2 = (bf16[8,256,1024]{2,1,0:T(8,128)(2,1)S(1)}, bf16[8,256,1024]{2,1,0:T(8,128)(2,1)}, u32[]{:S(2)}) copy-start(bf16[8,256,1024]{2,1,0:T(8,128)(2,1)} %copy-done.1) | copy-start | bytes 12582916

commit v20 on v15

--- a/solution.py
+++ b/solution.py
@@ -74,11 +74,19 @@
             across.append(lax.ppermute(piece, "dp", [(j, (j + sy) % n_d) for j in range(n_d)]))
         return jnp.stack(across)
 
-    def spread(cur):
-        for bit in reversed(bits):
+    def spread(cur, first=None):
+        order = list(reversed(bits))
+        if first is not None:
+            other = lax.ppermute(cur, "cent", [(i, i ^ first) for i in range(n_c)])
+            cur = pair_of(jnp.concatenate([cur, other], axis=0))
+            order = order[1:]
+        else:
+            cur = pair_of(cur)
+        for bit in order[:-1]:
             other = lax.ppermute(cur, "cent", [(i, i ^ bit) for i in range(n_c)])
             cur = jnp.concatenate([cur, other], axis=1)
-        return cur
+        last = lax.ppermute(cur, "cent", [(i, i ^ order[-1]) for i in range(n_c)])
+        return cur, last
 
     landed = [mine]
     for sz in range(1, n_o):
@@ -87,22 +95,31 @@
         else:
             pairs = [(i, (i + sz) % n_o) for i in range(n_o)]
         landed.append(lax.ppermute(mine, "outer", pairs))
-    parts = [None] + [spread(pair_of(piece)) for piece in landed[1:]]
+
+    def pod_of(sz):
+        return (z ^ sz) if n_o & (n_o - 1) == 0 else (z - sz) % n_o
+
+    cur = jnp.zeros((n_o * n_d, n_c * tq, d), rows_bf.dtype)
+    hrows = (n_c // 2) * tq
 
     h = q % 2
     half = t // 2
     my_half = lax.dynamic_slice_in_dim(rows_bf, h * half, half, 0)
-    own_blocks = [rows_bf]
+    own = pod_of(0) * n_d
+    cur = lax.dynamic_update_slice(cur, rows_bf[None], (own, 0, 0))
     for sy in range(1, n_d):
         got = lax.ppermute(my_half, "dp", [(j, (j + sy) % n_d) for j in range(n_d)])
         mate = lax.ppermute(got, "cent", [(i, i ^ 1) for i in range(n_c)])
-        own_blocks.append(jnp.concatenate([got, mate], axis=0))
-    parts[0] = jnp.stack(own_blocks)
+        cur = lax.dynamic_update_slice(cur, got[None], (own + sy, 0, 0))
+        cur = lax.dynamic_update_slice(cur, mate[None], (own + sy, half, 0))
 
-    cur = jnp.zeros((n_o * n_d,) + parts[0].shape[1:], parts[0].dtype)
-    for sz in range(n_o):
-        pod_of = (z ^ sz) if n_o & (n_o - 1) == 0 else (z - sz) % n_o
-        cur = lax.dynamic_update_slice_in_dim(cur, parts[sz], pod_of * n_d, axis=0)
+    order = list(reversed(bits))
+    for sz in range(1, n_o):
+        kept, brought = spread(landed[sz], first=order[0] if sz == 1 and len(order) > 1 else None)
+        base = pod_of(sz) * n_d
+        cur = lax.dynamic_update_slice(cur, kept, (base, 0, 0))
+        cur = lax.dynamic_update_slice(cur, brought, (base, hrows, 0))
+
     everything = cur.reshape(n_od * n_c * tq, d)
 
     logits = scores_for(everything, cent_bf, squares)

time: 70.6 us -> 97.1 us (1.38)
  waiting for transfers between devices: 14.7 us -> 36.3 us
  other arithmetic: 20 us -> 13.3 us
  matrix products: 8.3 us -> 12.7 us
  local copies, waits for them, and re-layouts: 3.83 us -> 7.62 us
  starting transfers between devices: 13.9 us -> 17.4 us
    ppermute x3, waiting for transfers between devices: 1.27 us -> 14.4 us  [pair_of(): lax.ppermute(piece, 'dp', [(j, (j + sy) % n_d) for j in range(n_d)])]
    ppermute x3, waiting for transfers between devices: 5.31 us -> 10.4 us  [shards_all(): landed.append(lax.ppermute(mine, 'outer', pairs))]
    ppermute x0 -> x4, waiting for transfers between devices: none -> 4.83 us  [the longest x1 3.37 us: spread(): other = lax.ppermute(cur, 'cent', [(i, i ^ first) for i in range(n_c)])]
    dynamic_update_slice x0 -> x5, local copies, waits for them, and re-layouts: none -> 3.98 us  [the longest x3 2.53 us: shards_all(): cur = lax.dynamic_update_slice(cur, brought, (base, hrows, 0))]
    ppermute x3, starting transfers between devices: 5.68 us -> 8.13 us  [shards_all(): landed.append(lax.ppermute(mine, 'outer', pairs))]
    dynamic_update_slice x4 -> x1, other arithmetic: 3.35 us -> 0.93 us  [shards_all(): cur = lax.dynamic_update_slice(cur, rows_bf[None], (own, 0, 0))]
    another operation x2 -> x0, other arithmetic: 2.36 us -> none  [shards_all(): parts[0] = jnp.stack(own_blocks)]
    dot_general x1, matrix products: 4.62 us -> 6.8 us  [scores_for(): lax.dot_general(piece, cent_bf, (((1,), (1,)), ((), ())), preferred_eleme...]
  transfers between devices with their start and end apart: 14 -> 14, of which waited for: 6 -> 9; matrix products, arithmetic and copies ran while one was open for 16% -> 6% of each run, Pallas kernels for 0% -> 0%
where the time goes in v20:
time: 97.1 us; the launch traced here: 96.9 us
  waiting for transfers between devices  36.3 us (37%)
  starting transfers between devices  17.4 us (18%)
  other arithmetic  13.3 us (14%)
  matrix products  12.7 us (13%)
  blocking collectives  9.3 us (10%)
  local copies, waits for them, and re-layouts  7.62 us (8%)
    ppermute x3, waiting for transfers between devices, pair_of(): lax.ppermute(piece, 'dp', [(j, (j + sy) % n_d) for j in range(n_d)])  14.4 us
    ppermute x3, waiting for transfers between devices, shards_all(): landed.append(lax.ppermute(mine, 'outer', pairs))  10.4 us
    all_gather x1, blocking collectives, shards_all(): every = lax.all_gather(both, ('dp', 'cent'), axis=0)  9.3 us
    ppermute x3, starting transfers between devices, shards_all(): landed.append(lax.ppermute(mine, 'outer', pairs))  8.13 us
    dot_general x1, matrix products, scores_for(): lax.dot_general(piece, cent_bf, (((1,), (1,)), ((), ())), preferred_eleme...  6.8 us
    ppermute x2, waiting for transfers between devices, spread(): other = lax.ppermute(cur, 'cent', [(i, i ^ bit) for i in range(n_c)])  6.73 us
    dot_general x1, matrix products, shards_all(): lax.dot_general(scaled.reshape(n_o * pod, k), everything, (((0,), (0,)),...  5.86 us
    ppermute x1, waiting for transfers between devices, spread(): other = lax.ppermute(cur, 'cent', [(i, i ^ first) for i in range(n_c)])  3.37 us
  transfers between devices with their start and end apart: 14, of which 9 were waited for; matrix products, arithmetic and copies ran while one was open for 6% of the time, Pallas kernels for 0%

profile of v20, /device:TPU:0, one launch (start us, length us, event | category | flops | bytes accessed | tf_op | source)
XLA Modules:
  0.0 96.9 jit_solution(17771838757223356287)
XLA Ops:
  0.0 0.0 copy-start.2
  0.0 2.5 %broadcast_in_dim.147 = bf16[8,256,1024]{2,1,0:T(8,128)(2,1)} broadcast(bf16[]{:T(256)} %constant.83.clone.1), dimensions={} | broadcast | bytes 4194306 | tf_op jit(solution)/shard_map/broadcast_in_dim | solution.py:102
  2.5 0.0 copy-done.2
  2.5 0.9 bitcast_dynamic-update-slice_fusion
  3.4 0.0 copy-start.4
  3.4 3.0 %collective-permute-start = (bf16[128,1024]{1,0:T(8,128)(2,1)S(1)}, bf16[128,1024]{1,0:T(8,128)(2,1)S(1)}, u32[]{:S(2)}, u32[]{:S(2)}) collective-permute-start(bf16[128,1024]{1,0:T(8,128)(2,1)S(1)} %constant_dynamic-slice_fusion.1), channel_id=1, source_target_pairs={{0,4},{4,0},{1,5},{5,1},{2,6},{6,2},{3,7},{7,3},{8,12},{12,8},{9,1... | collective-permute-start | bytes 786440 | tf_op jit(solution)/shard_map/ppermute | solution.py:111
  6.5 0.0 copy-start.3
  6.5 1.7 %collective-permute-start.2 = (bf16[64,1024]{1,0:T(8,128)(2,1)S(1)}, bf16[64,1024]{1,0:T(8,128)(2,1)S(1)}, u32[]{:S(2)}, u32[]{:S(2)}) collective-permute-start(bf16[64,1024]{1,0:T(8,128)(2,1)S(1)} %constant_dynamic-slice_fusion), channel_id=1, source_target_pairs={{0,8},{8,0},{16,24},{24,16},{1,9},{9,1},{17,25},{25,17},{2,10},{10... | collective-permute-start | bytes 393224 | tf_op jit(solution)/shard_map/ppermute | solution.py:97
  8.1 3.4 %collective-permute-done.2 = bf16[64,1024]{1,0:T(8,128)(2,1)S(1)} collective-permute-done((bf16[64,1024]{1,0:T(8,128)(2,1)S(1)}, bf16[64,1024]{1,0:T(8,128)(2,1)S(1)}, u32[]{:S(2)}, u32[]{:S(2)}) %collective-permute-start.2) | collective-permute-done | bytes 131104 | tf_op jit(solution)/shard_map/ppermute | solution.py:97
  11.5 1.5 %collective-permute-start.3 = (bf16[64,1024]{1,0:T(8,128)(2,1)S(1)}, bf16[64,1024]{1,0:T(8,128)(2,1)S(1)}, u32[]{:S(2)}, u32[]{:S(2)}) collective-permute-start(bf16[64,1024]{1,0:T(8,128)(2,1)S(1)} %collective-permute-done.2), channel_id=1, source_target_pairs={{0,2},{1,3},{2,0},{3,1},{4,6},{5,7},{6,4},{7,5},{8,10},{9,11},{10,... | collective-permute-start | bytes 393224 | tf_op jit(solution)/shard_map/ppermute | solution.py:80
  13.0 0.0 collective-permute-done
  13.0 0.1 collective-permute-start.1
  13.1 3.4 %collective-permute-done.3 = bf16[64,1024]{1,0:T(8,128)(2,1)S(1)} collective-permute-done((bf16[64,1024]{1,0:T(8,128)(2,1)S(1)}, bf16[64,1024]{1,0:T(8,128)(2,1)S(1)}, u32[]{:S(2)}, u32[]{:S(2)}) %collective-permute-start.3) | collective-permute-done | bytes 131104 | tf_op jit(solution)/shard_map/ppermute | solution.py:80
  16.5 0.4 collective-permute-start.4
  16.9 0.7 bitcast_dynamic-update-slice_fusion.2
  17.6 0.0 collective-permute-done.1
  17.6 0.7 bitcast_dynamic-update-slice_fusion.1
  18.4 4.6 %collective-permute-done.4 = bf16[128,1024]{1,0:T(8,128)(2,1)S(1)} collective-permute-done((bf16[128,1024]{1,0:T(8,128)(2,1)S(1)}, bf16[128,1024]{1,0:T(8,128)(2,1)S(1)}, u32[]{:S(2)}, u32[]{:S(2)}) %collective-permute-start.4) | collective-permute-done | bytes 262176 | tf_op jit(solution)/shard_map/ppermute | solution.py:74
  22.9 0.9 pad_maximum_fusion
  23.9 0.0 collective-permute-start.5
  23.9 2.6 %collective-permute-start.6 = (bf16[64,1024]{1,0:T(8,128)(2,1)S(1)}, bf16[64,1024]{1,0:T(8,128)(2,1)S(1)}, u32[]{:S(2)}, u32[]{:S(2)}) collective-permute-start(bf16[64,1024]{1,0:T(8,128)(2,1)S(1)} %constant_dynamic-slice_fusion), channel_id=1, source_target_pairs={{0,16},{8,24},{16,0},{24,8},{1,17},{9,25},{17,1},{25,9},{2,18},{10... | collective-permute-start | bytes 393224 | tf_op jit(solution)/shard_map/ppermute | solution.py:97
  26.5 7.0 %collective-permute-done.6 = bf16[64,1024]{1,0:T(8,128)(2,1)S(1)} collective-permute-done((bf16[64,1024]{1,0:T(8,128)(2,1)S(1)}, bf16[64,1024]{1,0:T(8,128)(2,1)S(1)}, u32[]{:S(2)}, u32[]{:S(2)}) %collective-permute-start.6) | collective-permute-done | bytes 131104 | tf_op jit(solution)/shard_map/ppermute | solution.py:97
  33.5 0.5 collective-permute-start.7
  33.9 4.7 %collective-permute-done.7 = bf16[64,1024]{1,0:T(8,128)(2,1)S(1)} collective-permute-done((bf16[64,1024]{1,0:T(8,128)(2,1)S(1)}, bf16[64,1024]{1,0:T(8,128)(2,1)S(1)}, u32[]{:S(2)}, u32[]{:S(2)}) %collective-permute-start.7) | collective-permute-done | bytes 131104 | tf_op jit(solution)/shard_map/ppermute | solution.py:74
  38.6 0.7 pad_maximum_fusion.3
  39.3 0.0 copy-done.3
  39.3 1.5 %collective-permute-start.8 = (bf16[2,64,1024]{2,1,0:T(8,128)(2,1)}, bf16[2,64,1024]{2,1,0:T(8,128)(2,1)}, u32[]{:S(2)}, u32[]{:S(2)}) collective-permute-start(bf16[2,64,1024]{2,1,0:T(8,128)(2,1)} %pad_maximum_fusion.3), channel_id=1, source_target_pairs={{0,2},{1,3},{2,0},{3,1},{4,6},{5,7},{6,4},{7,5},{8,10},{9,11},{10,... | collective-permute-start | bytes 786440 | tf_op jit(solution)/shard_map/ppermute | solution.py:86
  40.8 3.9 %collective-permute-start.10 = (bf16[64,1024]{1,0:T(8,128)(2,1)}, bf16[64,1024]{1,0:T(8,128)(2,1)S(1)}, u32[]{:S(2)}, u32[]{:S(2)}) collective-permute-start(bf16[64,1024]{1,0:T(8,128)(2,1)} %copy-done.3), channel_id=1, source_target_pairs={{0,24},{8,16},{16,8},{24,0},{1,25},{9,17},{17,9},{25,1},{2,26},{10... | collective-permute-start | bytes 393224 | tf_op jit(solution)/shard_map/ppermute | solution.py:97
  44.7 0.0 collective-permute-done.5
  44.7 0.9 constant_dynamic-update-slice_fusion.6
  45.5 1.2 %collective-permute-done.8 = bf16[2,64,1024]{2,1,0:T(8,128)(2,1)} collective-permute-done((bf16[2,64,1024]{2,1,0:T(8,128)(2,1)}, bf16[2,64,1024]{2,1,0:T(8,128)(2,1)}, u32[]{:S(2)}, u32[]{:S(2)}) %collective-permute-start.8) | collective-permute-done | bytes 262176 | tf_op jit(solution)/shard_map/ppermute | solution.py:86
  46.7 1.9 %pad_maximum_fusion.1 = (bf16[2,128,1024]{2,1,0:T(8,128)(2,1)S(1)}, bf16[8,256,1024]{2,1,0:T(8,128)(2,1)}) fusion(bf16[2,64,1024]{2,1,0:T(8,128)(2,1)} %collective-permute-done.8, bf16[1,64,1024]{2,1,0:T(8,128)(2,1)S(1)} %bitcast.80, bf16[1,64,1024]{2,1,0:T(8,128)(2,1)S(1)} %bitcast.78, bf16[8,256,1024]{2,1,0:T(8,128)(2,1)} %constant_dynamic-update-slice_fusion.6, ...), kind=kLoop, calls=%fused_computation.11 | loop fusion | flops 1572864 | bytes 1572868 | tf_op jit(solution)/shard_map/concatenate | solution.py:87
  48.6 0.0 collective-permute-start.9
  48.6 0.0 collective-permute-done.10
  48.6 0.7 collective-permute-start.11
  49.3 5.2 %collective-permute-done.11 = bf16[64,1024]{1,0:T(8,128)(2,1)S(1)} collective-permute-done((bf16[64,1024]{1,0:T(8,128)(2,1)S(1)}, bf16[64,1024]{1,0:T(8,128)(2,1)S(1)}, u32[]{:S(2)}, u32[]{:S(2)}) %collective-permute-start.11) | collective-permute-done | bytes 131104 | tf_op jit(solution)/shard_map/ppermute | solution.py:74
  54.5 1.6 %collective-permute-start.12 = (bf16[2,64,1024]{2,1,0:T(8,128)(2,1)S(1)}, bf16[2,64,1024]{2,1,0:T(8,128)(2,1)S(1)}, u32[]{:S(2)}, u32[]{:S(2)}) collective-permute-start(bf16[2,64,1024]{2,1,0:T(8,128)(2,1)S(1)} %pad_maximum_fusion.4), channel_id=1, source_target_pairs={{0,2},{1,3},{2,0},{3,1},{4,6},{5,7},{6,4},{7,5},{8,10},{9,11},{10,... | collective-permute-start | bytes 786440 | tf_op jit(solution)/shard_map/ppermute | solution.py:86
  56.1 0.0 copy-done.4
  56.1 0.0 collective-permute-done.9
  56.1 0.8 constant_dynamic-update-slice_fusion.4
  57.0 5.6 %collective-permute-done.12 = bf16[2,64,1024]{2,1,0:T(8,128)(2,1)S(1)} collective-permute-done((bf16[2,64,1024]{2,1,0:T(8,128)(2,1)S(1)}, bf16[2,64,1024]{2,1,0:T(8,128)(2,1)S(1)}, u32[]{:S(2)}, u32[]{:S(2)}) %collective-permute-start.12) | collective-permute-done | bytes 262176 | tf_op jit(solution)/shard_map/ppermute | solution.py:86
  62.5 0.9 pad_maximum_fusion.2
  63.5 0.0 collective-permute-start.13
  63.5 0.0 copy-done.1
  63.5 0.2 multiply_reduce_fusion
  63.7 0.1 copy.27
  63.8 0.1 stack.116
  63.9 1.5 %collective-permute-done.13 = bf16[2,128,1024]{2,1,0:T(8,128)(2,1)S(1)} collective-permute-done((bf16[2,128,1024]{2,1,0:T(8,128)(2,1)S(1)}, bf16[2,128,1024]{2,1,0:T(8,128)(2,1)S(1)}, u32[]{:S(2)}, u32[]{:S(2)}) %collective-permute-start.13) | collective-permute-done | bytes 524320 | tf_op jit(solution)/shard_map/ppermute | solution.py:88
  65.4 0.8 constant_dynamic-update-slice_fusion.2
  66.2 6.8 %fusion.21 = (f32[2048]{0:T(1024)S(1)}, f32[2048,512]{1,0:T(8,128)}) fusion(f32[512]{0:T(512)S(1)} %multiply_reduce_fusion, bf16[2048,1024]{1,0:T(8,128)(2,1)} %bitcast.9, f32[512,1024]{1,0:T(8,128)S(1)} %copy-done.1), kind=kOutput, calls=%fused_computation.78 | convolution fusion | flops 2152200192 | bytes 10496000 | tf_op jit(solution)/shard_map/dot_general | solution.py:10
  73.0 0.1 broadcast_in_dim.153
  73.1 3.3 %exponential_reduce_fusion = f32[2048]{0:T(1024)S(1)} fusion(f32[2048,512]{1,0:T(8,128)} %get-tuple-element.34, f32[2048]{0:T(1024)S(1)} %get-tuple-element.33), kind=kLoop, calls=%fused_computation.4 | loop fusion | flops 2095104 | bytes 4210688 | tf_op jit(solution)/shard_map/reduce_sum | solution.py:18
  76.4 0.1 broadcast_in_dim.158
  76.5 0.1 select_reduce_fusion.7
  76.6 0.2 select_reduce_fusion.3
  76.8 9.3 %all-gather = f32[16,8,4,64]{3,1,2,0:T(8,128)S(1)} all-gather(f32[2,8,4,64]{3,1,2,0:T(8,128)S(1)} %copy.30), channel_id=2, replica_groups=mesh['outer'=4,'dp'=2,'cent'=4] {'dp','cent'}, dimensions={0}, use_global_device_ids=true | all-gather | bytes 147456 | tf_op jit(solution)/shard_map/all_gather | solution.py:152
  86.2 0.1 select_reduce_fusion.1
  86.3 0.1 select_reduce_fusion.5
  86.4 0.1 div.62
  86.5 0.1 sub.53
  86.6 2.8 %bitcast_reduce_fusion = f32[4,512]{1,0:T(4,128)S(1)} fusion(f32[2048]{0:T(1024)S(1)} %div.62, f32[2048,512]{1,0:T(8,128)} %get-tuple-element.34, f32[2048]{0:T(1024)S(1)} %sub.53), kind=kLoop, calls=%fused_computation.2 | loop fusion | flops 5240832 | bytes 4218880 | tf_op jit(solution)/shard_map/reduce_sum | solution.py:163
  89.5 0.6 copy-done
  90.0 1.0 %fusion = bf16[2048,512]{1,0:T(8,128)(2,1)S(1)} fusion(f32[4,512]{1,0:T(4,128)S(1)} %broadcast_add_fusion, f32[2048]{0:T(1024)S(1)} %div.62, f32[2048,512]{1,0:T(8,128)S(1)} %copy-done, f32[2048]{0:T(1024)S(1)} %sub.53), kind=kLoop, calls=%fused_computation.1 | loop fusion | flops 6291456 | bytes 6316032 | tf_op jit(solution)/shard_map/convert_element_type | solution.py:164
  91.0 5.9 %subtract_multiply_fusion.1 = f32[512,1024]{1,0:T(8,128)} fusion(f32[512,1024]{1,0:T(8,128)S(1)} %copy-done.1, bf16[2048,512]{1,0:T(8,128)(2,1)S(1)} %fusion, bf16[2048,1024]{1,0:T(8,128)(2,1)} %bitcast.9, f32[512]{0:T(512)S(1)} %fusion.8), kind=kOutput, calls=%fused_computation.7 | convolution fusion | flops 2149056512 | bytes 10487808 | tf_op jit(solution)/shard_map/dot_general | solution.py:165
  (24 shorter events, 0.2 us)
Async XLA Ops:
  0.0 2.5 %copy-start.2 = (f32[256,1024]{1,0:T(8,128)S(1)}, f32[256,1024]{1,0:T(8,128)}, u32[]{:S(2)}) copy-start(f32[256,1024]{1,0:T(8,128)} %param.3) | copy-start | bytes 3145732
  3.4 52.7 %copy-start.4 = (s32[4]{0:T(128)S(1)}, s32[4]{0:T(128)}, u32[]{:S(2)}) copy-start(s32[4]{0:T(128)} %constant.105.clone) | copy-start | bytes 52
  3.4 9.6 %collective-permute-start = (bf16[128,1024]{1,0:T(8,128)(2,1)S(1)}, bf16[128,1024]{1,0:T(8,128)(2,1)S(1)}, u32[]{:S(2)}, u32[]{:S(2)}) collective-permute-start(bf16[128,1024]{1,0:T(8,128)(2,1)S(1)} %constant_dynamic-slice_fusion.1), channel_id=1, source_target_pairs={{0,4},{4,0},{1,5},{5,1},{2,6},{6,2},{3,7},{7,3},{8,12},{12,8},{9,1... | collective-permute-start | bytes 786440 | tf_op jit(solution)/shard_map/ppermute | solution.py:111
  6.5 32.9 %copy-start.3 = (bf16[64,1024]{1,0:T(8,128)(2,1)}, bf16[64,1024]{1,0:T(8,128)(2,1)S(1)}, u32[]{:S(2)}) copy-start(bf16[64,1024]{1,0:T(8,128)(2,1)S(1)} %constant_dynamic-slice_fusion) | copy-start | bytes 393220
  6.5 5.0 %collective-permute-start.2 = (bf16[64,1024]{1,0:T(8,128)(2,1)S(1)}, bf16[64,1024]{1,0:T(8,128)(2,1)S(1)}, u32[]{:S(2)}, u32[]{:S(2)}) collective-permute-start(bf16[64,1024]{1,0:T(8,128)(2,1)S(1)} %constant_dynamic-slice_fusion), channel_id=1, source_target_pairs={{0,8},{8,0},{16,24},{24,16},{1,9},{9,1},{17,25},{25,17},{2,10},{10... | collective-permute-start | bytes 393224 | tf_op jit(solution)/shard_map/ppermute | solution.py:97
  11.5 5.0 %collective-permute-start.3 = (bf16[64,1024]{1,0:T(8,128)(2,1)S(1)}, bf16[64,1024]{1,0:T(8,128)(2,1)S(1)}, u32[]{:S(2)}, u32[]{:S(2)}) collective-permute-start(bf16[64,1024]{1,0:T(8,128)(2,1)S(1)} %collective-permute-done.2), channel_id=1, source_target_pairs={{0,2},{1,3},{2,0},{3,1},{4,6},{5,7},{6,4},{7,5},{8,10},{9,11},{10,... | collective-permute-start | bytes 393224 | tf_op jit(solution)/shard_map/ppermute | solution.py:80
  13.0 4.6 %collective-permute-start.1 = (bf16[128,1024]{1,0:T(8,128)(2,1)S(1)}, bf16[128,1024]{1,0:T(8,128)(2,1)S(1)}, u32[]{:S(2)}, u32[]{:S(2)}) collective-permute-start(bf16[128,1024]{1,0:T(8,128)(2,1)S(1)} %collective-permute-done), channel_id=1, source_target_pairs={{0,1},{1,0},{2,3},{3,2},{4,5},{5,4},{6,7},{7,6},{8,9},{9,8},{10,11... | collective-permute-start | bytes 786440 | tf_op jit(solution)/shard_map/ppermute | solution.py:112
  16.5 6.4 %collective-permute-start.4 = (bf16[128,1024]{1,0:T(8,128)(2,1)S(1)}, bf16[128,1024]{1,0:T(8,128)(2,1)S(1)}, u32[]{:S(2)}, u32[]{:S(2)}) collective-permute-start(bf16[128,1024]{1,0:T(8,128)(2,1)S(1)} %constant_dynamic-update-slice_fusion), channel_id=1, source_target_pairs={{0,4},{4,0},{1,5},{5,1},{2,6},{6,2},{3,7},{7,3},{8,12},{12,8},{9,1... | collective-permute-start | bytes 786440 | tf_op jit(solution)/shard_map/ppermute | solution.py:74
  17.6 45.8 %copy-start.1 = (f32[512,1024]{1,0:T(8,128)S(1)}, f32[512,1024]{1,0:T(8,128)}, u32[]{:S(2)}) copy-start(f32[512,1024]{1,0:T(8,128)} %param.4) | copy-start | bytes 6291460
  23.9 20.8 %collective-permute-start.5 = (bf16[2,128,1024]{2,1,0:T(8,128)(2,1)S(1)}, bf16[2,128,1024]{2,1,0:T(8,128)(2,1)S(1)}, u32[]{:S(2)}, u32[]{:S(2)}) collective-permute-start(bf16[2,128,1024]{2,1,0:T(8,128)(2,1)S(1)} %get-tuple-element.19), channel_id=1, source_target_pairs={{0,1},{1,0},{2,3},{3,2},{4,5},{5,4},{6,7},{7,6},{8,9},{9,8},{10,11... | collective-permute-start | bytes 1572872 | tf_op jit(solution)/shard_map/ppermute | solution.py:88
  23.9 9.6 %collective-permute-start.6 = (bf16[64,1024]{1,0:T(8,128)(2,1)S(1)}, bf16[64,1024]{1,0:T(8,128)(2,1)S(1)}, u32[]{:S(2)}, u32[]{:S(2)}) collective-permute-start(bf16[64,1024]{1,0:T(8,128)(2,1)S(1)} %constant_dynamic-slice_fusion), channel_id=1, source_target_pairs={{0,16},{8,24},{16,0},{24,8},{1,17},{9,25},{17,1},{25,9},{2,18},{10... | collective-permute-start | bytes 393224 | tf_op jit(solution)/shard_map/ppermute | solution.py:97
  33.5 5.1 %collective-permute-start.7 = (bf16[64,1024]{1,0:T(8,128)(2,1)S(1)}, bf16[64,1024]{1,0:T(8,128)(2,1)S(1)}, u32[]{:S(2)}, u32[]{:S(2)}) collective-permute-start(bf16[64,1024]{1,0:T(8,128)(2,1)S(1)} %collective-permute-done.6), channel_id=1, source_target_pairs={{0,4},{4,0},{1,5},{5,1},{2,6},{6,2},{3,7},{7,3},{8,12},{12,8},{9,1... | collective-permute-start | bytes 393224 | tf_op jit(solution)/shard_map/ppermute | solution.py:74
  39.3 7.4 %collective-permute-start.8 = (bf16[2,64,1024]{2,1,0:T(8,128)(2,1)}, bf16[2,64,1024]{2,1,0:T(8,128)(2,1)}, u32[]{:S(2)}, u32[]{:S(2)}) collective-permute-start(bf16[2,64,1024]{2,1,0:T(8,128)(2,1)} %pad_maximum_fusion.3), channel_id=1, source_target_pairs={{0,2},{1,3},{2,0},{3,1},{4,6},{5,7},{6,4},{7,5},{8,10},{9,11},{10,... | collective-permute-start | bytes 786440 | tf_op jit(solution)/shard_map/ppermute | solution.py:86
  40.8 7.8 %collective-permute-start.10 = (bf16[64,1024]{1,0:T(8,128)(2,1)}, bf16[64,1024]{1,0:T(8,128)(2,1)S(1)}, u32[]{:S(2)}, u32[]{:S(2)}) collective-permute-start(bf16[64,1024]{1,0:T(8,128)(2,1)} %copy-done.3), channel_id=1, source_target_pairs={{0,24},{8,16},{16,8},{24,0},{1,25},{9,17},{17,9},{25,1},{2,26},{10... | collective-permute-start | bytes 393224 | tf_op jit(solution)/shard_map/ppermute | solution.py:97
  48.6 7.5 %collective-permute-start.9 = (bf16[2,128,1024]{2,1,0:T(8,128)(2,1)S(1)}, bf16[2,128,1024]{2,1,0:T(8,128)(2,1)S(1)}, u32[]{:S(2)}, u32[]{:S(2)}) collective-permute-start(bf16[2,128,1024]{2,1,0:T(8,128)(2,1)S(1)} %get-tuple-element.17), channel_id=1, source_target_pairs={{0,1},{1,0},{2,3},{3,2},{4,5},{5,4},{6,7},{7,6},{8,9},{9,8},{10,11... | collective-permute-start | bytes 1572872 | tf_op jit(solution)/shard_map/ppermute | solution.py:88
  48.6 5.9 %collective-permute-start.11 = (bf16[64,1024]{1,0:T(8,128)(2,1)S(1)}, bf16[64,1024]{1,0:T(8,128)(2,1)S(1)}, u32[]{:S(2)}, u32[]{:S(2)}) collective-permute-start(bf16[64,1024]{1,0:T(8,128)(2,1)S(1)} %collective-permute-done.10), channel_id=1, source_target_pairs={{0,4},{4,0},{1,5},{5,1},{2,6},{6,2},{3,7},{7,3},{8,12},{12,8},{9,1... | collective-permute-start | bytes 393224 | tf_op jit(solution)/shard_map/ppermute | solution.py:74
  54.5 8.0 %collective-permute-start.12 = (bf16[2,64,1024]{2,1,0:T(8,128)(2,1)S(1)}, bf16[2,64,1024]{2,1,0:T(8,128)(2,1)S(1)}, u32[]{:S(2)}, u32[]{:S(2)}) collective-permute-start(bf16[2,64,1024]{2,1,0:T(8,128)(2,1)S(1)} %pad_maximum_fusion.4), channel_id=1, source_target_pairs={{0,2},{1,3},{2,0},{3,1},{4,6},{5,7},{6,4},{7,5},{8,10},{9,11},{10,... | collective-permute-start | bytes 786440 | tf_op jit(solution)/shard_map/ppermute | solution.py:86
  63.5 1.9 %collective-permute-start.13 = (bf16[2,128,1024]{2,1,0:T(8,128)(2,1)S(1)}, bf16[2,128,1024]{2,1,0:T(8,128)(2,1)S(1)}, u32[]{:S(2)}, u32[]{:S(2)}) collective-permute-start(bf16[2,128,1024]{2,1,0:T(8,128)(2,1)S(1)} %get-tuple-element.15), channel_id=1, source_target_pairs={{0,1},{1,0},{2,3},{3,2},{4,5},{5,4},{6,7},{7,6},{8,9},{9,8},{10,11... | collective-permute-start | bytes 1572872 | tf_op jit(solution)/shard_map/ppermute | solution.py:88
  86.6 3.4 %copy-start = (f32[2048,512]{1,0:T(8,128)S(1)}, f32[2048,512]{1,0:T(8,128)}, u32[]{:S(2)}) copy-start(f32[2048,512]{1,0:T(8,128)} %get-tuple-element.34) | copy-start | bytes 12582916

commit v21 on v17

--- a/solution.py
+++ b/solution.py
@@ -97,7 +97,7 @@
         return cur
 
     parts = [None] + [
-        spread_x_first(piece) if sz <= 2 else spread(pair_of(piece))
+        spread_x_first(piece) if sz in (1, 3) else spread(pair_of(piece))
         for sz, piece in enumerate(landed[1:], start=1)
     ]
 

time: 67.7 us -> 66.6 us (0.984)
  the two profiles are of different devices: /device:TPU:17 before, /device:TPU:0 now
where the time goes in v21:
time: 66.6 us; the launch traced here: 66.1 us
  other arithmetic  19.3 us (29%)
  starting transfers between devices  15.9 us (24%)
  blocking collectives  9.33 us (14%)
  waiting for transfers between devices  9.09 us (14%)
  matrix products  8.29 us (12%)
  local copies, waits for them, and re-layouts  3.87 us (6%)
    all_gather x1, blocking collectives, shards_all(): every = lax.all_gather(both, ('dp', 'cent'), axis=0)  9.33 us
    ppermute x3, starting transfers between devices, shards_all(): landed.append(lax.ppermute(mine, 'outer', pairs))  5.68 us
    dot_general x1, matrix products, scores_for(): lax.dot_general(piece, cent_bf, (((1,), (1,)), ((), ())), preferred_eleme...  4.61 us
    ppermute x3, waiting for transfers between devices, shards_all(): landed.append(lax.ppermute(mine, 'outer', pairs))  4.1 us
    ppermute x3, waiting for transfers between devices, pair_of(): lax.ppermute(piece, 'dp', [(j, (j + sy) % n_d) for j in range(n_d)])  4.03 us
    dot_general x1, matrix products, shards_all(): lax.dot_general(scaled.reshape(n_o * pod, k), everything, (((0,), (0,)),...  3.68 us
    ppermute x3, starting transfers between devices, pair_of(): lax.ppermute(piece, 'dp', [(j, (j + sy) % n_d) for j in range(n_d)])  3.67 us
    dynamic_update_slice x4, other arithmetic, shards_all(): cur = lax.dynamic_update_slice_in_dim(cur, parts[sz], pod_of * n_d, axis=0)  3.34 us
  transfers between devices with their start and end apart: 14, of which 4 were waited for; matrix products, arithmetic and copies ran while one was open for 16% of the time, Pallas kernels for 0%

profile of v21, /device:TPU:0, one launch (start us, length us, event | category | flops | bytes accessed | tf_op | source)
XLA Modules:
  0.0 66.1 jit_solution(18143908402475252080)
XLA Ops:
  0.0 1.4 %convert_element_type.22 = bf16[256,1024]{1,0:T(8,128)(2,1)S(1)} convert(f32[256,1024]{1,0:T(8,128)} %param.3) | non-fusion elementwise | flops 262144 | bytes 1572864 | tf_op jit(solution)/shard_map/convert_element_type | solution.py:56
  1.5 3.1 %collective-permute-start.2 = (bf16[64,1024]{1,0:T(8,128)(2,1)S(1)}, bf16[64,1024]{1,0:T(8,128)(2,1)S(1)}, u32[]{:S(2)}, u32[]{:S(2)}) collective-permute-start(bf16[64,1024]{1,0:T(8,128)(2,1)S(1)} %constant_dynamic-slice_fusion), channel_id=1, source_target_pairs={{0,8},{8,0},{16,24},{24,16},{1,9},{9,1},{17,25},{25,17},{2,10},{10... | collective-permute-start | bytes 393224 | tf_op jit(solution)/shard_map/ppermute | solution.py:89
  4.6 2.6 %collective-permute-start.6 = (bf16[64,1024]{1,0:T(8,128)(2,1)S(1)}, bf16[64,1024]{1,0:T(8,128)(2,1)S(1)}, u32[]{:S(2)}, u32[]{:S(2)}) collective-permute-start(bf16[64,1024]{1,0:T(8,128)(2,1)S(1)} %constant_dynamic-slice_fusion), channel_id=1, source_target_pairs={{0,16},{8,24},{16,0},{24,8},{1,17},{9,25},{17,1},{25,9},{2,18},{10... | collective-permute-start | bytes 393224 | tf_op jit(solution)/shard_map/ppermute | solution.py:89
  7.2 0.0 collective-permute-start.10
  7.2 0.7 %constant_dynamic-slice_fusion.1 = bf16[128,1024]{1,0:T(8,128)(2,1)} fusion(bf16[256,1024]{1,0:T(8,128)(2,1)S(1)} %convert_element_type.22, s32[]{:T(128)S(6)} %select_n.127), kind=kLoop, calls=%fused_computation.51 | loop fusion | bytes 524292 | tf_op jit(solution)/shard_map/dynamic_slice | solution.py:106
  7.9 1.7 %collective-permute-start = (bf16[128,1024]{1,0:T(8,128)(2,1)}, bf16[128,1024]{1,0:T(8,128)(2,1)}, u32[]{:S(2)}, u32[]{:S(2)}) collective-permute-start(bf16[128,1024]{1,0:T(8,128)(2,1)} %constant_dynamic-slice_fusion.1), channel_id=1, source_target_pairs={{0,4},{4,0},{1,5},{5,1},{2,6},{6,2},{3,7},{7,3},{8,12},{12,8},{9,1... | collective-permute-start | bytes 786440 | tf_op jit(solution)/shard_map/ppermute | solution.py:109
  9.6 1.3 %convert_bitcast_fusion = bf16[1,256,1024]{2,1,0:T(8,128)(2,1)S(1)} fusion(f32[256,1024]{1,0:T(8,128)} %param.3), kind=kLoop, calls=%fused_computation.76 | loop fusion | flops 262144 | bytes 1572864 | tf_op jit(solution)/shard_map/stack | solution.py:112
  11.0 0.7 %fusion.17 = (s32[1,4]{1,0:T(1,128)S(1)}, s32[1,4]{1,0:T(1,128)S(1)}, s32[1,4]{1,0:T(1,128)S(1)}, s32[1,4]{1,0:T(1,128)S(1)}, s32[1,4]{1,0:T(1,128)S(1)}, /*inde...) fusion(s32[4]{0:T(128)} %constant.103.clone, pred[]{:T(512)S(6)} %eq.65, s32[]{:T(128)S(6)} %axis_index.32, ...), kind=kLoop, calls=%fused_computation.71 | loop fusion | flops 96 | bytes 156 | tf_op jit(solution)/shard_map/stack | solution.py:133
  11.7 0.1 copy.27
  11.7 0.1 stack.128
  11.8 0.0 collective-permute-done.2
  11.8 1.6 %collective-permute-start.3 = (bf16[64,1024]{1,0:T(8,128)(2,1)S(1)}, bf16[64,1024]{1,0:T(8,128)(2,1)S(1)}, u32[]{:S(2)}, u32[]{:S(2)}) collective-permute-start(bf16[64,1024]{1,0:T(8,128)(2,1)S(1)} %collective-permute-done.2), channel_id=1, source_target_pairs={{0,2},{1,3},{2,0},{3,1},{4,6},{5,7},{6,4},{7,5},{8,10},{9,11},{10,... | collective-permute-start | bytes 393224 | tf_op jit(solution)/shard_map/ppermute | solution.py:92
  13.4 4.1 %collective-permute-done.6 = bf16[64,1024]{1,0:T(8,128)(2,1)S(1)} collective-permute-done((bf16[64,1024]{1,0:T(8,128)(2,1)S(1)}, bf16[64,1024]{1,0:T(8,128)(2,1)S(1)}, u32[]{:S(2)}, u32[]{:S(2)}) %collective-permute-start.6) | collective-permute-done | bytes 131104 | tf_op jit(solution)/shard_map/ppermute | solution.py:89
  17.5 1.5 %collective-permute-start.7 = (bf16[64,1024]{1,0:T(8,128)(2,1)S(1)}, bf16[64,1024]{1,0:T(8,128)(2,1)S(1)}, u32[]{:S(2)}, u32[]{:S(2)}) collective-permute-start(bf16[64,1024]{1,0:T(8,128)(2,1)S(1)} %collective-permute-done.6), channel_id=1, source_target_pairs={{0,4},{4,0},{1,5},{5,1},{2,6},{6,2},{3,7},{7,3},{8,12},{12,8},{9,1... | collective-permute-start | bytes 393224 | tf_op jit(solution)/shard_map/ppermute | solution.py:74
  19.0 0.0 collective-permute-done.10
  19.0 1.5 %collective-permute-start.11 = (bf16[64,1024]{1,0:T(8,128)(2,1)S(1)}, bf16[64,1024]{1,0:T(8,128)(2,1)S(1)}, u32[]{:S(2)}, u32[]{:S(2)}) collective-permute-start(bf16[64,1024]{1,0:T(8,128)(2,1)S(1)} %collective-permute-done.10), channel_id=1, source_target_pairs={{0,2},{1,3},{2,0},{3,1},{4,6},{5,7},{6,4},{7,5},{8,10},{9,11},{10,... | collective-permute-start | bytes 393224 | tf_op jit(solution)/shard_map/ppermute | solution.py:92
  20.5 0.0 collective-permute-done.3
  20.6 0.6 collective-permute-start.4
  21.1 2.8 %collective-permute-done.7 = bf16[64,1024]{1,0:T(8,128)(2,1)S(1)} collective-permute-done((bf16[64,1024]{1,0:T(8,128)(2,1)S(1)}, bf16[64,1024]{1,0:T(8,128)(2,1)S(1)}, u32[]{:S(2)}, u32[]{:S(2)}) %collective-permute-start.7) | collective-permute-done | bytes 131104 | tf_op jit(solution)/shard_map/ppermute | solution.py:74
  23.9 0.7 %pad_maximum_fusion.3 = bf16[2,64,1024]{2,1,0:T(8,128)(2,1)} fusion(bf16[1,64,1024]{2,1,0:T(8,128)(2,1)S(1)} %bitcast.79, bf16[1,64,1024]{2,1,0:T(8,128)(2,1)S(1)} %bitcast.76), kind=kLoop, calls=%fused_computation.18 | loop fusion | flops 131072 | bytes 524288 | tf_op jit(solution)/shard_map/stack | solution.py:75
  24.7 1.1 %collective-permute-start.8 = (bf16[2,64,1024]{2,1,0:T(8,128)(2,1)}, bf16[2,64,1024]{2,1,0:T(8,128)(2,1)}, u32[]{:S(2)}, u32[]{:S(2)}) collective-permute-start(bf16[2,64,1024]{2,1,0:T(8,128)(2,1)} %pad_maximum_fusion.3), channel_id=1, source_target_pairs={{0,2},{1,3},{2,0},{3,1},{4,6},{5,7},{6,4},{7,5},{8,10},{9,11},{10,... | collective-permute-start | bytes 786440 | tf_op jit(solution)/shard_map/ppermute | solution.py:79
  25.8 0.0 collective-permute-done.11
  25.8 1.6 %collective-permute-start.12 = (bf16[128,1024]{1,0:T(8,128)(2,1)S(1)}, bf16[128,1024]{1,0:T(8,128)(2,1)}, u32[]{:S(2)}, u32[]{:S(2)}) collective-permute-start(bf16[128,1024]{1,0:T(8,128)(2,1)S(1)} %constant_dynamic-update-slice_fusion.2), channel_id=1, source_target_pairs={{0,4},{4,0},{1,5},{5,1},{2,6},{6,2},{3,7},{7,3},{8,12},{12,8},{9,1... | collective-permute-start | bytes 786440 | tf_op jit(solution)/shard_map/ppermute | solution.py:74
  27.4 0.0 collective-permute-done
  27.4 0.0 collective-permute-start.1
  27.4 1.2 %collective-permute-done.4 = bf16[128,1024]{1,0:T(8,128)(2,1)S(1)} collective-permute-done((bf16[128,1024]{1,0:T(8,128)(2,1)S(1)}, bf16[128,1024]{1,0:T(8,128)(2,1)S(1)}, u32[]{:S(2)}, u32[]{:S(2)}) %collective-permute-start.4) | collective-permute-done | bytes 262176 | tf_op jit(solution)/shard_map/ppermute | solution.py:74
  28.6 0.7 %copy-done.4 = bf16[128,1024]{1,0:T(8,128)(2,1)} copy-done((bf16[128,1024]{1,0:T(8,128)(2,1)}, bf16[128,1024]{1,0:T(8,128)(2,1)S(1)}, u32[]{:S(2)}) %copy-start.4) | copy-done | bytes 262168
  29.3 0.8 %pad_maximum_fusion = bf16[2,128,1024]{2,1,0:T(8,128)(2,1)} fusion(bf16[1,128,1024]{2,1,0:T(8,128)(2,1)S(1)} %bitcast.82, bf16[1,128,1024]{2,1,0:T(8,128)(2,1)S(1)} %bitcast.72), kind=kLoop, calls=%fused_computation.15 | loop fusion | flops 262144 | bytes 1048576 | tf_op jit(solution)/shard_map/stack | solution.py:75
  30.2 0.0 collective-permute-start.5
  30.2 0.0 copy-done.3
  30.2 0.2 multiply_reduce_fusion
  30.4 1.0 %collective-permute-done.8 = bf16[2,64,1024]{2,1,0:T(8,128)(2,1)} collective-permute-done((bf16[2,64,1024]{2,1,0:T(8,128)(2,1)}, bf16[2,64,1024]{2,1,0:T(8,128)(2,1)}, u32[]{:S(2)}, u32[]{:S(2)}) %collective-permute-start.8) | collective-permute-done | bytes 262176 | tf_op jit(solution)/shard_map/ppermute | solution.py:79
  31.4 1.0 %pad_maximum_fusion.1 = bf16[2,128,1024]{2,1,0:T(8,128)(2,1)S(1)} fusion(bf16[2,64,1024]{2,1,0:T(8,128)(2,1)} %collective-permute-done.8, bf16[1,64,1024]{2,1,0:T(8,128)(2,1)S(1)} %bitcast.80, bf16[1,64,1024]{2,1,0:T(8,128)(2,1)S(1)} %bitcast.77), kind=kLoop, calls=%fused_computation.16 | loop fusion | flops 1572864 | bytes 1048576 | tf_op jit(solution)/shard_map/concatenate | solution.py:80
  32.3 0.1 collective-permute-start.9
  32.4 0.0 collective-permute-done.12
  32.4 0.0 copy-start.5
  32.4 1.0 %pad_maximum_fusion.2 = bf16[2,128,1024]{2,1,0:T(8,128)(2,1)S(1)} fusion(bf16[1,128,1024]{2,1,0:T(8,128)(2,1)} %bitcast.7, bf16[1,128,1024]{2,1,0:T(8,128)(2,1)S(1)} %bitcast.70), kind=kLoop, calls=%fused_computation.17 | loop fusion | flops 262144 | bytes 1048576 | tf_op jit(solution)/shard_map/stack | solution.py:75
  33.5 0.5 collective-permute-start.13
  34.0 0.0 collective-permute-done.1
  34.0 1.1 %maximum_bitcast_fusion = bf16[1,256,1024]{2,1,0:T(8,128)(2,1)S(1)} fusion(bf16[128,1024]{1,0:T(8,128)(2,1)} %collective-permute-done.1, bf16[128,1024]{1,0:T(8,128)(2,1)} %collective-permute-done), kind=kLoop, calls=%fused_computation.14 | loop fusion | flops 1048576 | bytes 1048576 | tf_op jit(solution)/shard_map/stack | solution.py:112
  35.1 0.5 broadcast_in_dim.138
  35.6 0.1 maximum_dynamic-update-slice_fusion
  35.8 0.0 collective-permute-done.5
  35.8 1.1 %maximum_dynamic-update-slice_fusion.1 = bf16[8,256,1024]{2,1,0:T(8,128)(2,1)S(1)} fusion(bf16[8,256,1024]{2,1,0:T(8,128)(2,1)S(1)} %maximum_dynamic-update-slice_fusion, s32[]{:T(128)S(6)} %select_n.130, bf16[2,128,1024]{2,1,0:T(8,128)(2,1)} %collective-permute-done.5, bf16[1,128,1024]{2,1,0:T(8,128)(2,1)S(1)} %bitcast.83, bf16[1,128,1024]{2,1,0:T(8,128)(2,1)S(1)} %bitcast.73), kind=kLoop, calls=%fused_computation.10 | loop fusion | flops 3145728 | bytes 2097156 | tf_op jit(solution)/shard_map/dynamic_update_slice | solution.py:117
  36.9 0.0 collective-permute-done.9
  36.9 1.1 %maximum_dynamic-update-slice_fusion.2 = bf16[8,256,1024]{2,1,0:T(8,128)(2,1)S(1)} fusion(bf16[8,256,1024]{2,1,0:T(8,128)(2,1)S(1)} %maximum_dynamic-update-slice_fusion.1, s32[]{:T(128)S(6)} %select_n.131, bf16[2,128,1024]{2,1,0:T(8,128)(2,1)S(1)} %collective-permute-done.9, bf16[2,64,1024]{2,1,0:T(8,128)(2,1)} %collective-permute-done.8, ...), kind=kLoop, calls=%fused_computation.11 | loop fusion | flops 4194304 | bytes 2097156 | tf_op jit(solution)/shard_map/dynamic_update_slice | solution.py:117
  38.0 0.0 collective-permute-done.13
  38.0 1.0 %maximum_dynamic-update-slice_fusion.3 = bf16[8,256,1024]{2,1,0:T(8,128)(2,1)S(1)} fusion(bf16[8,256,1024]{2,1,0:T(8,128)(2,1)S(1)} %maximum_dynamic-update-slice_fusion.2, s32[]{:T(128)S(6)} %select_n.132, bf16[2,128,1024]{2,1,0:T(8,128)(2,1)S(1)} %collective-permute-done.13, bf16[1,128,1024]{2,1,0:T(8,128)(2,1)} %bitcast.7, ...), kind=kLoop, calls=%fused_computation.12 | loop fusion | flops 3145728 | bytes 2097156 | tf_op jit(solution)/shard_map/dynamic_update_slice | solution.py:117
  39.1 4.6 %fusion.21 = (f32[2048]{0:T(1024)S(1)}, f32[2048,512]{1,0:T(8,128)}) fusion(f32[512]{0:T(512)S(1)} %multiply_reduce_fusion, bf16[2048,1024]{1,0:T(8,128)(2,1)S(1)} %bitcast.68, f32[512,1024]{1,0:T(8,128)S(1)} %copy-done.3), kind=kOutput, calls=%fused_computation.75 | convolution fusion | flops 2152200192 | bytes 10496000 | tf_op jit(solution)/shard_map/dot_general | solution.py:10
  43.7 0.1 broadcast_in_dim.141
  43.8 3.3 %exponential_reduce_fusion = f32[2048]{0:T(1024)S(1)} fusion(f32[2048,512]{1,0:T(8,128)} %get-tuple-element.26, f32[2048]{0:T(1024)S(1)} %get-tuple-element.25), kind=kLoop, calls=%fused_computation.4 | loop fusion | flops 2095104 | bytes 4210688 | tf_op jit(solution)/shard_map/reduce_sum | solution.py:18
  47.1 0.1 broadcast_in_dim.146
  47.2 0.1 select_reduce_fusion.7
  47.3 0.2 select_reduce_fusion.3
  47.5 9.3 %all-gather = f32[16,8,4,64]{3,1,2,0:T(8,128)S(1)} all-gather(f32[2,8,4,64]{3,1,2,0:T(8,128)S(1)} %copy.30), channel_id=2, replica_groups=mesh['outer'=4,'dp'=2,'cent'=4] {'dp','cent'}, dimensions={0}, use_global_device_ids=true | all-gather | bytes 147456 | tf_op jit(solution)/shard_map/all_gather | solution.py:147
  56.9 0.1 select_reduce_fusion.1
  57.0 0.1 select_reduce_fusion.5
  57.1 0.1 div.62
  57.2 0.1 sub.53
  57.3 2.8 %bitcast_reduce_fusion = f32[4,512]{1,0:T(4,128)S(1)} fusion(f32[2048]{0:T(1024)S(1)} %div.62, f32[2048,512]{1,0:T(8,128)} %get-tuple-element.26, f32[2048]{0:T(1024)S(1)} %sub.53), kind=kLoop, calls=%fused_computation.2 | loop fusion | flops 5240832 | bytes 4218880 | tf_op jit(solution)/shard_map/reduce_sum | solution.py:158
  60.2 0.6 copy-done
  60.7 1.0 %fusion = bf16[2048,512]{1,0:T(8,128)(2,1)S(1)} fusion(f32[4,512]{1,0:T(4,128)S(1)} %broadcast_add_fusion, f32[2048]{0:T(1024)S(1)} %div.62, f32[2048,512]{1,0:T(8,128)S(1)} %copy-done, f32[2048]{0:T(1024)S(1)} %sub.53), kind=kLoop, calls=%fused_computation.1 | loop fusion | flops 6291456 | bytes 6316032 | tf_op jit(solution)/shard_map/convert_element_type | solution.py:159
  61.7 0.7 %copy-done.2 = bf16[8,256,1024]{2,1,0:T(8,128)(2,1)S(1)} copy-done((bf16[8,256,1024]{2,1,0:T(8,128)(2,1)S(1)}, bf16[8,256,1024]{2,1,0:T(8,128)(2,1)}, u32[]{:S(2)}) %copy-start.2) | copy-done | bytes 4194328
  62.5 3.7 %subtract_multiply_fusion.1 = f32[512,1024]{1,0:T(8,128)} fusion(f32[512,1024]{1,0:T(8,128)S(1)} %copy-done.3, bf16[2048,512]{1,0:T(8,128)(2,1)S(1)} %fusion, bf16[2048,1024]{1,0:T(8,128)(2,1)S(1)} %bitcast.69, f32[512]{0:T(512)S(1)} %fusion.8), kind=kOutput, calls=%fused_computation.7 | convolution fusion | flops 2149056512 | bytes 10487808 | tf_op jit(solution)/shard_map/dot_general | solution.py:160
  (28 shorter events, 0.2 us)
Async XLA Ops:
  0.0 30.2 %copy-start.3 = (f32[512,1024]{1,0:T(8,128)S(1)}, f32[512,1024]{1,0:T(8,128)}, u32[]{:S(2)}) copy-start(f32[512,1024]{1,0:T(8,128)} %param.4) | copy-start | bytes 6291460
  1.5 10.4 %collective-permute-start.2 = (bf16[64,1024]{1,0:T(8,128)(2,1)S(1)}, bf16[64,1024]{1,0:T(8,128)(2,1)S(1)}, u32[]{:S(2)}, u32[]{:S(2)}) collective-permute-start(bf16[64,1024]{1,0:T(8,128)(2,1)S(1)} %constant_dynamic-slice_fusion), channel_id=1, source_target_pairs={{0,8},{8,0},{16,24},{24,16},{1,9},{9,1},{17,25},{25,17},{2,10},{10... | collective-permute-start | bytes 393224 | tf_op jit(solution)/shard_map/ppermute | solution.py:89
  4.6 12.9 %collective-permute-start.6 = (bf16[64,1024]{1,0:T(8,128)(2,1)S(1)}, bf16[64,1024]{1,0:T(8,128)(2,1)S(1)}, u32[]{:S(2)}, u32[]{:S(2)}) collective-permute-start(bf16[64,1024]{1,0:T(8,128)(2,1)S(1)} %constant_dynamic-slice_fusion), channel_id=1, source_target_pairs={{0,16},{8,24},{16,0},{24,8},{1,17},{9,25},{17,1},{25,9},{2,18},{10... | collective-permute-start | bytes 393224 | tf_op jit(solution)/shard_map/ppermute | solution.py:89
  7.2 11.9 %collective-permute-start.10 = (bf16[64,1024]{1,0:T(8,128)(2,1)S(1)}, bf16[64,1024]{1,0:T(8,128)(2,1)S(1)}, u32[]{:S(2)}, u32[]{:S(2)}) collective-permute-start(bf16[64,1024]{1,0:T(8,128)(2,1)S(1)} %constant_dynamic-slice_fusion), channel_id=1, source_target_pairs={{0,24},{8,16},{16,8},{24,0},{1,25},{9,17},{17,9},{25,1},{2,26},{10... | collective-permute-start | bytes 393224 | tf_op jit(solution)/shard_map/ppermute | solution.py:89
  7.9 19.5 %collective-permute-start = (bf16[128,1024]{1,0:T(8,128)(2,1)}, bf16[128,1024]{1,0:T(8,128)(2,1)}, u32[]{:S(2)}, u32[]{:S(2)}) collective-permute-start(bf16[128,1024]{1,0:T(8,128)(2,1)} %constant_dynamic-slice_fusion.1), channel_id=1, source_target_pairs={{0,4},{4,0},{1,5},{5,1},{2,6},{6,2},{3,7},{7,3},{8,12},{12,8},{9,1... | collective-permute-start | bytes 786440 | tf_op jit(solution)/shard_map/ppermute | solution.py:109
  11.8 8.7 %collective-permute-start.3 = (bf16[64,1024]{1,0:T(8,128)(2,1)S(1)}, bf16[64,1024]{1,0:T(8,128)(2,1)S(1)}, u32[]{:S(2)}, u32[]{:S(2)}) collective-permute-start(bf16[64,1024]{1,0:T(8,128)(2,1)S(1)} %collective-permute-done.2), channel_id=1, source_target_pairs={{0,2},{1,3},{2,0},{3,1},{4,6},{5,7},{6,4},{7,5},{8,10},{9,11},{10,... | collective-permute-start | bytes 393224 | tf_op jit(solution)/shard_map/ppermute | solution.py:92
  17.5 6.4 %collective-permute-start.7 = (bf16[64,1024]{1,0:T(8,128)(2,1)S(1)}, bf16[64,1024]{1,0:T(8,128)(2,1)S(1)}, u32[]{:S(2)}, u32[]{:S(2)}) collective-permute-start(bf16[64,1024]{1,0:T(8,128)(2,1)S(1)} %collective-permute-done.6), channel_id=1, source_target_pairs={{0,4},{4,0},{1,5},{5,1},{2,6},{6,2},{3,7},{7,3},{8,12},{12,8},{9,1... | collective-permute-start | bytes 393224 | tf_op jit(solution)/shard_map/ppermute | solution.py:74
  19.0 6.8 %collective-permute-start.11 = (bf16[64,1024]{1,0:T(8,128)(2,1)S(1)}, bf16[64,1024]{1,0:T(8,128)(2,1)S(1)}, u32[]{:S(2)}, u32[]{:S(2)}) collective-permute-start(bf16[64,1024]{1,0:T(8,128)(2,1)S(1)} %collective-permute-done.10), channel_id=1, source_target_pairs={{0,2},{1,3},{2,0},{3,1},{4,6},{5,7},{6,4},{7,5},{8,10},{9,11},{10,... | collective-permute-start | bytes 393224 | tf_op jit(solution)/shard_map/ppermute | solution.py:92
  20.6 8.1 %collective-permute-start.4 = (bf16[128,1024]{1,0:T(8,128)(2,1)S(1)}, bf16[128,1024]{1,0:T(8,128)(2,1)S(1)}, u32[]{:S(2)}, u32[]{:S(2)}) collective-permute-start(bf16[128,1024]{1,0:T(8,128)(2,1)S(1)} %constant_dynamic-update-slice_fusion), channel_id=1, source_target_pairs={{0,4},{4,0},{1,5},{5,1},{2,6},{6,2},{3,7},{7,3},{8,12},{12,8},{9,1... | collective-permute-start | bytes 786440 | tf_op jit(solution)/shard_map/ppermute | solution.py:74
  24.7 6.7 %collective-permute-start.8 = (bf16[2,64,1024]{2,1,0:T(8,128)(2,1)}, bf16[2,64,1024]{2,1,0:T(8,128)(2,1)}, u32[]{:S(2)}, u32[]{:S(2)}) collective-permute-start(bf16[2,64,1024]{2,1,0:T(8,128)(2,1)} %pad_maximum_fusion.3), channel_id=1, source_target_pairs={{0,2},{1,3},{2,0},{3,1},{4,6},{5,7},{6,4},{7,5},{8,10},{9,11},{10,... | collective-permute-start | bytes 786440 | tf_op jit(solution)/shard_map/ppermute | solution.py:79
  25.8 6.6 %collective-permute-start.12 = (bf16[128,1024]{1,0:T(8,128)(2,1)S(1)}, bf16[128,1024]{1,0:T(8,128)(2,1)}, u32[]{:S(2)}, u32[]{:S(2)}) collective-permute-start(bf16[128,1024]{1,0:T(8,128)(2,1)S(1)} %constant_dynamic-update-slice_fusion.2), channel_id=1, source_target_pairs={{0,4},{4,0},{1,5},{5,1},{2,6},{6,2},{3,7},{7,3},{8,12},{12,8},{9,1... | collective-permute-start | bytes 786440 | tf_op jit(solution)/shard_map/ppermute | solution.py:74
  27.4 6.7 %collective-permute-start.1 = (bf16[128,1024]{1,0:T(8,128)(2,1)}, bf16[128,1024]{1,0:T(8,128)(2,1)}, u32[]{:S(2)}, u32[]{:S(2)}) collective-permute-start(bf16[128,1024]{1,0:T(8,128)(2,1)} %collective-permute-done), channel_id=1, source_target_pairs={{0,1},{1,0},{2,3},{3,2},{4,5},{5,4},{6,7},{7,6},{8,9},{9,8},{10,11... | collective-permute-start | bytes 786440 | tf_op jit(solution)/shard_map/ppermute | solution.py:110
  28.6 0.7 %copy-start.4 = (bf16[128,1024]{1,0:T(8,128)(2,1)}, bf16[128,1024]{1,0:T(8,128)(2,1)S(1)}, u32[]{:S(2)}) copy-start(bf16[128,1024]{1,0:T(8,128)(2,1)S(1)} %collective-permute-done.4) | copy-start | bytes 786436
  30.2 5.6 %collective-permute-start.5 = (bf16[2,128,1024]{2,1,0:T(8,128)(2,1)}, bf16[2,128,1024]{2,1,0:T(8,128)(2,1)}, u32[]{:S(2)}, u32[]{:S(2)}) collective-permute-start(bf16[2,128,1024]{2,1,0:T(8,128)(2,1)} %pad_maximum_fusion), channel_id=1, source_target_pairs={{0,1},{1,0},{2,3},{3,2},{4,5},{5,4},{6,7},{7,6},{8,9},{9,8},{10,11... | collective-permute-start | bytes 1572872 | tf_op jit(solution)/shard_map/ppermute | solution.py:95
  32.3 4.6 %collective-permute-start.9 = (bf16[2,128,1024]{2,1,0:T(8,128)(2,1)S(1)}, bf16[2,128,1024]{2,1,0:T(8,128)(2,1)S(1)}, u32[]{:S(2)}, u32[]{:S(2)}) collective-permute-start(bf16[2,128,1024]{2,1,0:T(8,128)(2,1)S(1)} %pad_maximum_fusion.1), channel_id=1, source_target_pairs={{0,1},{1,0},{2,3},{3,2},{4,5},{5,4},{6,7},{7,6},{8,9},{9,8},{10,11... | collective-permute-start | bytes 1572872 | tf_op jit(solution)/shard_map/ppermute | solution.py:79
  32.4 3.3 %copy-start.5 = (bf16[128,1024]{1,0:T(8,128)(2,1)S(1)}, bf16[128,1024]{1,0:T(8,128)(2,1)}, u32[]{:S(2)}) copy-start(bf16[128,1024]{1,0:T(8,128)(2,1)} %copy-done.4) | copy-start | bytes 786436
  33.5 4.5 %collective-permute-start.13 = (bf16[2,128,1024]{2,1,0:T(8,128)(2,1)S(1)}, bf16[2,128,1024]{2,1,0:T(8,128)(2,1)S(1)}, u32[]{:S(2)}, u32[]{:S(2)}) collective-permute-start(bf16[2,128,1024]{2,1,0:T(8,128)(2,1)S(1)} %pad_maximum_fusion.2), channel_id=1, source_target_pairs={{0,1},{1,0},{2,3},{3,2},{4,5},{5,4},{6,7},{7,6},{8,9},{9,8},{10,11... | collective-permute-start | bytes 1572872 | tf_op jit(solution)/shard_map/ppermute | solution.py:95
  39.1 4.6 %copy-start.1 = (bf16[8,256,1024]{2,1,0:T(8,128)(2,1)}, bf16[8,256,1024]{2,1,0:T(8,128)(2,1)S(1)}, u32[]{:S(2)}) copy-start(bf16[8,256,1024]{2,1,0:T(8,128)(2,1)S(1)} %maximum_dynamic-update-slice_fusion.3) | copy-start | bytes 12582916
  57.3 3.4 %copy-start = (f32[2048,512]{1,0:T(8,128)S(1)}, f32[2048,512]{1,0:T(8,128)}, u32[]{:S(2)}) copy-start(f32[2048,512]{1,0:T(8,128)} %get-tuple-element.26) | copy-start | bytes 12582916
  60.1 2.3 %copy-start.2 = (bf16[8,256,1024]{2,1,0:T(8,128)(2,1)S(1)}, bf16[8,256,1024]{2,1,0:T(8,128)(2,1)}, u32[]{:S(2)}) copy-start(bf16[8,256,1024]{2,1,0:T(8,128)(2,1)} %copy-done.1) | copy-start | bytes 12582916

commit v22 on v21

--- a/solution.py
+++ b/solution.py
@@ -97,7 +97,7 @@
         return cur
 
     parts = [None] + [
-        spread_x_first(piece) if sz in (1, 3) else spread(pair_of(piece))
+        spread_x_first(piece)
         for sz, piece in enumerate(landed[1:], start=1)
     ]
 

time: 66.6 us -> 71.3 us (1.071); the launches traced: 66.1 us -> 69.9 us
  waiting for transfers between devices: 9.09 us -> 12.8 us
  local copies, waits for them, and re-layouts: 3.87 us -> 4.78 us
    ppermute x3, waiting for transfers between devices: 4.03 us -> 8.01 us  [pair_of(): lax.ppermute(piece, 'dp', [(j, (j + sy) % n_d) for j in range(n_d)])]
    ppermute x2 -> x0, starting transfers between devices: 1.18 us -> none  [spread(): other = lax.ppermute(cur, 'cent', [(i, i ^ bit) for i in range(n_c)])]
    concatenate x1 -> x0, other arithmetic: 0.98 us -> none  [spread(): cur = jnp.concatenate([cur, other], axis=1)]
    ppermute x2 -> x0, waiting for transfers between devices: 0.95 us -> none  [spread(): other = lax.ppermute(cur, 'cent', [(i, i ^ bit) for i in range(n_c)])]
    unnamed x14 -> x15, local copies, waits for them, and re-layouts: 2.03 us -> 2.93 us
    ppermute x3, starting transfers between devices: 3.67 us -> 4.55 us  [pair_of(): lax.ppermute(piece, 'dp', [(j, (j + sy) % n_d) for j in range(n_d)])]
    ppermute x2 -> x3, starting transfers between devices: 3.05 us -> 3.58 us  [spread_x_first(): other = lax.ppermute(piece, 'cent', [(i, i ^ order[0]) for i in range(n_c)])]
  transfers between devices with their start and end apart: 14 -> 14, of which waited for: 4 -> 5; matrix products, arithmetic and copies ran while one was open for 16% -> 15% of each run, Pallas kernels for 0% -> 0%
where the time goes in v22:
time: 71.3 us; the launch traced here: 69.9 us
  other arithmetic  18.6 us (26%)
  starting transfers between devices  15.7 us (22%)
  waiting for transfers between devices  12.8 us (18%)
  blocking collectives  9.32 us (13%)
  matrix products  8.3 us (12%)
  local copies, waits for them, and re-layouts  4.78 us (7%)
    all_gather x1, blocking collectives, shards_all(): every = lax.all_gather(both, ('dp', 'cent'), axis=0)  9.32 us
    ppermute x3, waiting for transfers between devices, pair_of(): lax.ppermute(piece, 'dp', [(j, (j + sy) % n_d) for j in range(n_d)])  8.01 us
    ppermute x3, starting transfers between devices, shards_all(): landed.append(lax.ppermute(mine, 'outer', pairs))  5.68 us
    dot_general x1, matrix products, scores_for(): lax.dot_general(piece, cent_bf, (((1,), (1,)), ((), ())), preferred_eleme...  4.62 us
    ppermute x3, starting transfers between devices, pair_of(): lax.ppermute(piece, 'dp', [(j, (j + sy) % n_d) for j in range(n_d)])  4.55 us
    ppermute x3, waiting for transfers between devices, shards_all(): landed.append(lax.ppermute(mine, 'outer', pairs))  4.19 us
    dot_general x1, matrix products, shards_all(): lax.dot_general(scaled.reshape(n_o * pod, k), everything, (((0,), (0,)),...  3.68 us
    ppermute x3, starting transfers between devices, spread_x_first(): other = lax.ppermute(piece, 'cent', [(i, i ^ order[0]) for i in range(n_c)])  3.58 us
  transfers between devices with their start and end apart: 14, of which 5 were waited for; matrix products, arithmetic and copies ran while one was open for 15% of the time, Pallas kernels for 0%

profile of v22, /device:TPU:0, one launch (start us, length us, event | category | flops | bytes accessed | tf_op | source)
XLA Modules:
  0.0 69.9 jit_solution(6325129749831722621)
XLA Ops:
  0.0 1.4 %convert_element_type.22 = bf16[256,1024]{1,0:T(8,128)(2,1)S(1)} convert(f32[256,1024]{1,0:T(8,128)} %param.3) | non-fusion elementwise | flops 262144 | bytes 1572864 | tf_op jit(solution)/shard_map/convert_element_type | solution.py:56
  1.5 3.1 %collective-permute-start.2 = (bf16[64,1024]{1,0:T(8,128)(2,1)S(1)}, bf16[64,1024]{1,0:T(8,128)(2,1)S(1)}, u32[]{:S(2)}, u32[]{:S(2)}) collective-permute-start(bf16[64,1024]{1,0:T(8,128)(2,1)S(1)} %constant_dynamic-slice_fusion), channel_id=1, source_target_pairs={{0,8},{8,0},{16,24},{24,16},{1,9},{9,1},{17,25},{25,17},{2,10},{10... | collective-permute-start | bytes 393224 | tf_op jit(solution)/shard_map/ppermute | solution.py:89
  4.6 2.6 %collective-permute-start.6 = (bf16[64,1024]{1,0:T(8,128)(2,1)S(1)}, bf16[64,1024]{1,0:T(8,128)(2,1)}, u32[]{:S(2)}, u32[]{:S(2)}) collective-permute-start(bf16[64,1024]{1,0:T(8,128)(2,1)S(1)} %constant_dynamic-slice_fusion), channel_id=1, source_target_pairs={{0,16},{8,24},{16,0},{24,8},{1,17},{9,25},{17,1},{25,9},{2,18},{10... | collective-permute-start | bytes 393224 | tf_op jit(solution)/shard_map/ppermute | solution.py:89
  7.2 0.0 collective-permute-start.10
  7.2 0.7 %constant_dynamic-slice_fusion.1 = bf16[128,1024]{1,0:T(8,128)(2,1)} fusion(bf16[256,1024]{1,0:T(8,128)(2,1)S(1)} %convert_element_type.22, s32[]{:T(128)S(6)} %select_n.127), kind=kLoop, calls=%fused_computation.52 | loop fusion | bytes 524292 | tf_op jit(solution)/shard_map/dynamic_slice | solution.py:106
  7.9 1.7 %collective-permute-start = (bf16[128,1024]{1,0:T(8,128)(2,1)}, bf16[128,1024]{1,0:T(8,128)(2,1)}, u32[]{:S(2)}, u32[]{:S(2)}) collective-permute-start(bf16[128,1024]{1,0:T(8,128)(2,1)} %constant_dynamic-slice_fusion.1), channel_id=1, source_target_pairs={{0,4},{4,0},{1,5},{5,1},{2,6},{6,2},{3,7},{7,3},{8,12},{12,8},{9,1... | collective-permute-start | bytes 786440 | tf_op jit(solution)/shard_map/ppermute | solution.py:109
  9.6 1.3 %convert_bitcast_fusion = bf16[1,256,1024]{2,1,0:T(8,128)(2,1)S(1)} fusion(f32[256,1024]{1,0:T(8,128)} %param.3), kind=kLoop, calls=%fused_computation.77 | loop fusion | flops 262144 | bytes 1572864 | tf_op jit(solution)/shard_map/stack | solution.py:112
  11.0 0.7 fusion.17
  11.7 0.1 copy.27
  11.8 0.1 stack.128
  11.8 0.0 collective-permute-done.2
  11.9 1.6 %collective-permute-start.3 = (bf16[64,1024]{1,0:T(8,128)(2,1)S(1)}, bf16[64,1024]{1,0:T(8,128)(2,1)S(1)}, u32[]{:S(2)}, u32[]{:S(2)}) collective-permute-start(bf16[64,1024]{1,0:T(8,128)(2,1)S(1)} %collective-permute-done.2), channel_id=1, source_target_pairs={{0,2},{1,3},{2,0},{3,1},{4,6},{5,7},{6,4},{7,5},{8,10},{9,11},{10,... | collective-permute-start | bytes 393224 | tf_op jit(solution)/shard_map/ppermute | solution.py:92
  13.4 4.2 %collective-permute-done.6 = bf16[64,1024]{1,0:T(8,128)(2,1)} collective-permute-done((bf16[64,1024]{1,0:T(8,128)(2,1)S(1)}, bf16[64,1024]{1,0:T(8,128)(2,1)}, u32[]{:S(2)}, u32[]{:S(2)}) %collective-permute-start.6) | collective-permute-done | bytes 131104 | tf_op jit(solution)/shard_map/ppermute | solution.py:89
  17.6 1.5 %collective-permute-start.7 = (bf16[64,1024]{1,0:T(8,128)(2,1)}, bf16[64,1024]{1,0:T(8,128)(2,1)S(1)}, u32[]{:S(2)}, u32[]{:S(2)}) collective-permute-start(bf16[64,1024]{1,0:T(8,128)(2,1)} %collective-permute-done.6), channel_id=1, source_target_pairs={{0,2},{1,3},{2,0},{3,1},{4,6},{5,7},{6,4},{7,5},{8,10},{9,11},{10,... | collective-permute-start | bytes 393224 | tf_op jit(solution)/shard_map/ppermute | solution.py:92
  19.1 0.0 collective-permute-done.10
  19.1 0.5 collective-permute-start.11
  19.6 0.9 %constant_dynamic-update-slice_fusion.3 = bf16[128,1024]{1,0:T(8,128)(2,1)S(1)} fusion(bf16[64,1024]{1,0:T(8,128)(2,1)} %collective-permute-done.6), kind=kLoop, calls=%fused_computation.36 | loop fusion | bytes 262144
  20.5 0.0 collective-permute-done.3
  20.6 1.6 %collective-permute-start.4 = (bf16[128,1024]{1,0:T(8,128)(2,1)S(1)}, bf16[128,1024]{1,0:T(8,128)(2,1)S(1)}, u32[]{:S(2)}, u32[]{:S(2)}) collective-permute-start(bf16[128,1024]{1,0:T(8,128)(2,1)S(1)} %constant_dynamic-update-slice_fusion), channel_id=1, source_target_pairs={{0,4},{4,0},{1,5},{5,1},{2,6},{6,2},{3,7},{7,3},{8,12},{12,8},{9,1... | collective-permute-start | bytes 786440 | tf_op jit(solution)/shard_map/ppermute | solution.py:74
  22.2 0.6 collective-permute-done.7
  22.8 1.6 %collective-permute-start.8 = (bf16[128,1024]{1,0:T(8,128)(2,1)S(1)}, bf16[128,1024]{1,0:T(8,128)(2,1)}, u32[]{:S(2)}, u32[]{:S(2)}) collective-permute-start(bf16[128,1024]{1,0:T(8,128)(2,1)S(1)} %constant_dynamic-update-slice_fusion.2), channel_id=1, source_target_pairs={{0,4},{4,0},{1,5},{5,1},{2,6},{6,2},{3,7},{7,3},{8,12},{12,8},{9,1... | collective-permute-start | bytes 786440 | tf_op jit(solution)/shard_map/ppermute | solution.py:74
  24.4 0.0 collective-permute-done.11
  24.4 1.4 %collective-permute-start.12 = (bf16[128,1024]{1,0:T(8,128)(2,1)S(1)}, bf16[128,1024]{1,0:T(8,128)(2,1)}, u32[]{:S(2)}, u32[]{:S(2)}) collective-permute-start(bf16[128,1024]{1,0:T(8,128)(2,1)S(1)} %constant_dynamic-update-slice_fusion.4), channel_id=1, source_target_pairs={{0,4},{4,0},{1,5},{5,1},{2,6},{6,2},{3,7},{7,3},{8,12},{12,8},{9,1... | collective-permute-start | bytes 786440 | tf_op jit(solution)/shard_map/ppermute | solution.py:74
  25.8 0.0 collective-permute-done
  25.8 0.0 collective-permute-start.1
  25.8 4.1 %collective-permute-done.4 = bf16[128,1024]{1,0:T(8,128)(2,1)S(1)} collective-permute-done((bf16[128,1024]{1,0:T(8,128)(2,1)S(1)}, bf16[128,1024]{1,0:T(8,128)(2,1)S(1)}, u32[]{:S(2)}, u32[]{:S(2)}) %collective-permute-start.4) | collective-permute-done | bytes 262176 | tf_op jit(solution)/shard_map/ppermute | solution.py:74
  29.9 0.7 %copy-done.4 = bf16[128,1024]{1,0:T(8,128)(2,1)} copy-done((bf16[128,1024]{1,0:T(8,128)(2,1)}, bf16[128,1024]{1,0:T(8,128)(2,1)S(1)}, u32[]{:S(2)}) %copy-start.4) | copy-done | bytes 262168
  30.6 0.8 %pad_maximum_fusion = bf16[2,128,1024]{2,1,0:T(8,128)(2,1)} fusion(bf16[1,128,1024]{2,1,0:T(8,128)(2,1)S(1)} %bitcast.78, bf16[1,128,1024]{2,1,0:T(8,128)(2,1)S(1)} %bitcast.70), kind=kLoop, calls=%fused_computation.15 | loop fusion | flops 262144 | bytes 1048576 | tf_op jit(solution)/shard_map/stack | solution.py:75
  31.4 0.0 collective-permute-start.5
  31.4 0.0 copy-done.3
  31.4 0.2 multiply_reduce_fusion
  31.7 2.2 %collective-permute-done.8 = bf16[128,1024]{1,0:T(8,128)(2,1)} collective-permute-done((bf16[128,1024]{1,0:T(8,128)(2,1)S(1)}, bf16[128,1024]{1,0:T(8,128)(2,1)}, u32[]{:S(2)}, u32[]{:S(2)}) %collective-permute-start.8) | collective-permute-done | bytes 262176 | tf_op jit(solution)/shard_map/ppermute | solution.py:74
  33.8 1.0 %pad_maximum_fusion.1 = bf16[2,128,1024]{2,1,0:T(8,128)(2,1)S(1)} fusion(bf16[1,128,1024]{2,1,0:T(8,128)(2,1)} %bitcast.5, bf16[1,128,1024]{2,1,0:T(8,128)(2,1)S(1)} %bitcast.72), kind=kLoop, calls=%fused_computation.16 | loop fusion | flops 262144 | bytes 1048576 | tf_op jit(solution)/shard_map/stack | solution.py:75
  34.9 0.1 collective-permute-start.9
  34.9 1.7 %collective-permute-done.12 = bf16[128,1024]{1,0:T(8,128)(2,1)} collective-permute-done((bf16[128,1024]{1,0:T(8,128)(2,1)S(1)}, bf16[128,1024]{1,0:T(8,128)(2,1)}, u32[]{:S(2)}, u32[]{:S(2)}) %collective-permute-start.12) | collective-permute-done | bytes 262176 | tf_op jit(solution)/shard_map/ppermute | solution.py:74
  36.7 1.0 %pad_maximum_fusion.2 = bf16[2,128,1024]{2,1,0:T(8,128)(2,1)S(1)} fusion(bf16[1,128,1024]{2,1,0:T(8,128)(2,1)} %bitcast.7, bf16[1,128,1024]{2,1,0:T(8,128)(2,1)S(1)} %bitcast.74), kind=kLoop, calls=%fused_computation.17 | loop fusion | flops 262144 | bytes 1048576 | tf_op jit(solution)/shard_map/stack | solution.py:75
  37.7 0.1 collective-permute-start.13
  37.8 0.0 collective-permute-done.1
  37.8 1.1 %maximum_bitcast_fusion = bf16[1,256,1024]{2,1,0:T(8,128)(2,1)S(1)} fusion(bf16[128,1024]{1,0:T(8,128)(2,1)} %collective-permute-done.1, bf16[128,1024]{1,0:T(8,128)(2,1)} %collective-permute-done), kind=kLoop, calls=%fused_computation.14 | loop fusion | flops 1048576 | bytes 1048576 | tf_op jit(solution)/shard_map/stack | solution.py:112
  38.9 0.5 broadcast_in_dim.138
  39.4 0.1 maximum_dynamic-update-slice_fusion
  39.5 0.0 collective-permute-done.5
  39.5 0.0 copy-done.5
  39.5 1.1 %maximum_dynamic-update-slice_fusion.1 = bf16[8,256,1024]{2,1,0:T(8,128)(2,1)S(1)} fusion(bf16[8,256,1024]{2,1,0:T(8,128)(2,1)S(1)} %maximum_dynamic-update-slice_fusion, s32[]{:T(128)S(6)} %select_n.130, bf16[2,128,1024]{2,1,0:T(8,128)(2,1)} %collective-permute-done.5, bf16[1,128,1024]{2,1,0:T(8,128)(2,1)S(1)} %bitcast.79, bf16[1,128,1024]{2,1,0:T(8,128)(2,1)S(1)} %bitcast.71), kind=kLoop, calls=%fused_computation.10 | loop fusion | flops 3145728 | bytes 2097156 | tf_op jit(solution)/shard_map/dynamic_update_slice | solution.py:117
  40.7 0.0 collective-permute-done.9
  40.7 1.0 %maximum_dynamic-update-slice_fusion.2 = bf16[8,256,1024]{2,1,0:T(8,128)(2,1)S(1)} fusion(bf16[8,256,1024]{2,1,0:T(8,128)(2,1)S(1)} %maximum_dynamic-update-slice_fusion.1, s32[]{:T(128)S(6)} %select_n.131, bf16[2,128,1024]{2,1,0:T(8,128)(2,1)S(1)} %collective-permute-done.9, bf16[1,128,1024]{2,1,0:T(8,128)(2,1)} %bitcast.5, ...), kind=kLoop, calls=%fused_computation.11 | loop fusion | flops 3145728 | bytes 2097156 | tf_op jit(solution)/shard_map/dynamic_update_slice | solution.py:117
  41.7 0.0 collective-permute-done.13
  41.7 1.0 %maximum_dynamic-update-slice_fusion.3 = bf16[8,256,1024]{2,1,0:T(8,128)(2,1)S(1)} fusion(bf16[8,256,1024]{2,1,0:T(8,128)(2,1)S(1)} %maximum_dynamic-update-slice_fusion.2, s32[]{:T(128)S(6)} %select_n.132, bf16[2,128,1024]{2,1,0:T(8,128)(2,1)S(1)} %collective-permute-done.13, bf16[1,128,1024]{2,1,0:T(8,128)(2,1)} %bitcast.7, ...), kind=kLoop, calls=%fused_computation.12 | loop fusion | flops 3145728 | bytes 2097156 | tf_op jit(solution)/shard_map/dynamic_update_slice | solution.py:117
  42.8 4.6 %fusion.21 = (f32[2048]{0:T(1024)S(1)}, f32[2048,512]{1,0:T(8,128)}) fusion(f32[512]{0:T(512)S(1)} %multiply_reduce_fusion, bf16[2048,1024]{1,0:T(8,128)(2,1)S(1)} %bitcast.68, f32[512,1024]{1,0:T(8,128)S(1)} %copy-done.3), kind=kOutput, calls=%fused_computation.76 | convolution fusion | flops 2152200192 | bytes 10496000 | tf_op jit(solution)/shard_map/dot_general | solution.py:10
  47.4 0.1 broadcast_in_dim.141
  47.5 3.3 %exponential_reduce_fusion = f32[2048]{0:T(1024)S(1)} fusion(f32[2048,512]{1,0:T(8,128)} %get-tuple-element.26, f32[2048]{0:T(1024)S(1)} %get-tuple-element.25), kind=kLoop, calls=%fused_computation.4 | loop fusion | flops 2095104 | bytes 4210688 | tf_op jit(solution)/shard_map/reduce_sum | solution.py:18
  50.8 0.1 broadcast_in_dim.146
  50.9 0.1 select_reduce_fusion.7
  51.0 0.2 select_reduce_fusion.3
  51.2 9.3 %all-gather = f32[16,8,4,64]{3,1,2,0:T(8,128)S(1)} all-gather(f32[2,8,4,64]{3,1,2,0:T(8,128)S(1)} %copy.30), channel_id=2, replica_groups=mesh['outer'=4,'dp'=2,'cent'=4] {'dp','cent'}, dimensions={0}, use_global_device_ids=true | all-gather | bytes 147456 | tf_op jit(solution)/shard_map/all_gather | solution.py:147
  60.6 0.1 select_reduce_fusion.1
  60.7 0.1 select_reduce_fusion.5
  60.8 0.1 div.62
  60.9 0.1 sub.53
  61.0 2.8 %bitcast_reduce_fusion = f32[4,512]{1,0:T(4,128)S(1)} fusion(f32[2048]{0:T(1024)S(1)} %div.62, f32[2048,512]{1,0:T(8,128)} %get-tuple-element.26, f32[2048]{0:T(1024)S(1)} %sub.53), kind=kLoop, calls=%fused_computation.2 | loop fusion | flops 5240832 | bytes 4218880 | tf_op jit(solution)/shard_map/reduce_sum | solution.py:158
  63.9 0.6 copy-done
  64.5 1.0 %fusion = bf16[2048,512]{1,0:T(8,128)(2,1)S(1)} fusion(f32[4,512]{1,0:T(4,128)S(1)} %broadcast_add_fusion, f32[2048]{0:T(1024)S(1)} %div.62, f32[2048,512]{1,0:T(8,128)S(1)} %copy-done, f32[2048]{0:T(1024)S(1)} %sub.53), kind=kLoop, calls=%fused_computation.1 | loop fusion | flops 6291456 | bytes 6316032 | tf_op jit(solution)/shard_map/convert_element_type | solution.py:159
  65.5 0.7 %copy-done.2 = bf16[8,256,1024]{2,1,0:T(8,128)(2,1)S(1)} copy-done((bf16[8,256,1024]{2,1,0:T(8,128)(2,1)S(1)}, bf16[8,256,1024]{2,1,0:T(8,128)(2,1)}, u32[]{:S(2)}) %copy-start.2) | copy-done | bytes 4194328
  66.2 3.7 %subtract_multiply_fusion.1 = f32[512,1024]{1,0:T(8,128)} fusion(f32[512,1024]{1,0:T(8,128)S(1)} %copy-done.3, bf16[2048,512]{1,0:T(8,128)(2,1)S(1)} %fusion, bf16[2048,1024]{1,0:T(8,128)(2,1)S(1)} %bitcast.69, f32[512]{0:T(512)S(1)} %fusion.8), kind=kOutput, calls=%fused_computation.7 | convolution fusion | flops 2149056512 | bytes 10487808 | tf_op jit(solution)/shard_map/dot_general | solution.py:160
  (29 shorter events, 0.2 us)
Async XLA Ops:
  0.0 31.4 %copy-start.3 = (f32[512,1024]{1,0:T(8,128)S(1)}, f32[512,1024]{1,0:T(8,128)}, u32[]{:S(2)}) copy-start(f32[512,1024]{1,0:T(8,128)} %param.4) | copy-start | bytes 6291460
  1.5 10.4 %collective-permute-start.2 = (bf16[64,1024]{1,0:T(8,128)(2,1)S(1)}, bf16[64,1024]{1,0:T(8,128)(2,1)S(1)}, u32[]{:S(2)}, u32[]{:S(2)}) collective-permute-start(bf16[64,1024]{1,0:T(8,128)(2,1)S(1)} %constant_dynamic-slice_fusion), channel_id=1, source_target_pairs={{0,8},{8,0},{16,24},{24,16},{1,9},{9,1},{17,25},{25,17},{2,10},{10... | collective-permute-start | bytes 393224 | tf_op jit(solution)/shard_map/ppermute | solution.py:89
  4.6 13.0 %collective-permute-start.6 = (bf16[64,1024]{1,0:T(8,128)(2,1)S(1)}, bf16[64,1024]{1,0:T(8,128)(2,1)}, u32[]{:S(2)}, u32[]{:S(2)}) collective-permute-start(bf16[64,1024]{1,0:T(8,128)(2,1)S(1)} %constant_dynamic-slice_fusion), channel_id=1, source_target_pairs={{0,16},{8,24},{16,0},{24,8},{1,17},{9,25},{17,1},{25,9},{2,18},{10... | collective-permute-start | bytes 393224 | tf_op jit(solution)/shard_map/ppermute | solution.py:89
  7.2 11.9 %collective-permute-start.10 = (bf16[64,1024]{1,0:T(8,128)(2,1)S(1)}, bf16[64,1024]{1,0:T(8,128)(2,1)S(1)}, u32[]{:S(2)}, u32[]{:S(2)}) collective-permute-start(bf16[64,1024]{1,0:T(8,128)(2,1)S(1)} %constant_dynamic-slice_fusion), channel_id=1, source_target_pairs={{0,24},{8,16},{16,8},{24,0},{1,25},{9,17},{17,9},{25,1},{2,26},{10... | collective-permute-start | bytes 393224 | tf_op jit(solution)/shard_map/ppermute | solution.py:89
  7.9 17.9 %collective-permute-start = (bf16[128,1024]{1,0:T(8,128)(2,1)}, bf16[128,1024]{1,0:T(8,128)(2,1)}, u32[]{:S(2)}, u32[]{:S(2)}) collective-permute-start(bf16[128,1024]{1,0:T(8,128)(2,1)} %constant_dynamic-slice_fusion.1), channel_id=1, source_target_pairs={{0,4},{4,0},{1,5},{5,1},{2,6},{6,2},{3,7},{7,3},{8,12},{12,8},{9,1... | collective-permute-start | bytes 786440 | tf_op jit(solution)/shard_map/ppermute | solution.py:109
  11.9 8.7 %collective-permute-start.3 = (bf16[64,1024]{1,0:T(8,128)(2,1)S(1)}, bf16[64,1024]{1,0:T(8,128)(2,1)S(1)}, u32[]{:S(2)}, u32[]{:S(2)}) collective-permute-start(bf16[64,1024]{1,0:T(8,128)(2,1)S(1)} %collective-permute-done.2), channel_id=1, source_target_pairs={{0,2},{1,3},{2,0},{3,1},{4,6},{5,7},{6,4},{7,5},{8,10},{9,11},{10,... | collective-permute-start | bytes 393224 | tf_op jit(solution)/shard_map/ppermute | solution.py:92
  17.6 5.2 %collective-permute-start.7 = (bf16[64,1024]{1,0:T(8,128)(2,1)}, bf16[64,1024]{1,0:T(8,128)(2,1)S(1)}, u32[]{:S(2)}, u32[]{:S(2)}) collective-permute-start(bf16[64,1024]{1,0:T(8,128)(2,1)} %collective-permute-done.6), channel_id=1, source_target_pairs={{0,2},{1,3},{2,0},{3,1},{4,6},{5,7},{6,4},{7,5},{8,10},{9,11},{10,... | collective-permute-start | bytes 393224 | tf_op jit(solution)/shard_map/ppermute | solution.py:92
  19.1 5.3 %collective-permute-start.11 = (bf16[64,1024]{1,0:T(8,128)(2,1)S(1)}, bf16[64,1024]{1,0:T(8,128)(2,1)S(1)}, u32[]{:S(2)}, u32[]{:S(2)}) collective-permute-start(bf16[64,1024]{1,0:T(8,128)(2,1)S(1)} %collective-permute-done.10), channel_id=1, source_target_pairs={{0,2},{1,3},{2,0},{3,1},{4,6},{5,7},{6,4},{7,5},{8,10},{9,11},{10,... | collective-permute-start | bytes 393224 | tf_op jit(solution)/shard_map/ppermute | solution.py:92
  20.6 9.3 %collective-permute-start.4 = (bf16[128,1024]{1,0:T(8,128)(2,1)S(1)}, bf16[128,1024]{1,0:T(8,128)(2,1)S(1)}, u32[]{:S(2)}, u32[]{:S(2)}) collective-permute-start(bf16[128,1024]{1,0:T(8,128)(2,1)S(1)} %constant_dynamic-update-slice_fusion), channel_id=1, source_target_pairs={{0,4},{4,0},{1,5},{5,1},{2,6},{6,2},{3,7},{7,3},{8,12},{12,8},{9,1... | collective-permute-start | bytes 786440 | tf_op jit(solution)/shard_map/ppermute | solution.py:74
  22.8 11.1 %collective-permute-start.8 = (bf16[128,1024]{1,0:T(8,128)(2,1)S(1)}, bf16[128,1024]{1,0:T(8,128)(2,1)}, u32[]{:S(2)}, u32[]{:S(2)}) collective-permute-start(bf16[128,1024]{1,0:T(8,128)(2,1)S(1)} %constant_dynamic-update-slice_fusion.2), channel_id=1, source_target_pairs={{0,4},{4,0},{1,5},{5,1},{2,6},{6,2},{3,7},{7,3},{8,12},{12,8},{9,1... | collective-permute-start | bytes 786440 | tf_op jit(solution)/shard_map/ppermute | solution.py:74
  24.4 12.3 %collective-permute-start.12 = (bf16[128,1024]{1,0:T(8,128)(2,1)S(1)}, bf16[128,1024]{1,0:T(8,128)(2,1)}, u32[]{:S(2)}, u32[]{:S(2)}) collective-permute-start(bf16[128,1024]{1,0:T(8,128)(2,1)S(1)} %constant_dynamic-update-slice_fusion.4), channel_id=1, source_target_pairs={{0,4},{4,0},{1,5},{5,1},{2,6},{6,2},{3,7},{7,3},{8,12},{12,8},{9,1... | collective-permute-start | bytes 786440 | tf_op jit(solution)/shard_map/ppermute | solution.py:74
  25.8 12.0 %collective-permute-start.1 = (bf16[128,1024]{1,0:T(8,128)(2,1)}, bf16[128,1024]{1,0:T(8,128)(2,1)}, u32[]{:S(2)}, u32[]{:S(2)}) collective-permute-start(bf16[128,1024]{1,0:T(8,128)(2,1)} %collective-permute-done), channel_id=1, source_target_pairs={{0,1},{1,0},{2,3},{3,2},{4,5},{5,4},{6,7},{7,6},{8,9},{9,8},{10,11... | collective-permute-start | bytes 786440 | tf_op jit(solution)/shard_map/ppermute | solution.py:110
  29.9 0.7 %copy-start.4 = (bf16[128,1024]{1,0:T(8,128)(2,1)}, bf16[128,1024]{1,0:T(8,128)(2,1)S(1)}, u32[]{:S(2)}) copy-start(bf16[128,1024]{1,0:T(8,128)(2,1)S(1)} %collective-permute-done.4) | copy-start | bytes 786436
  31.4 8.1 %collective-permute-start.5 = (bf16[2,128,1024]{2,1,0:T(8,128)(2,1)}, bf16[2,128,1024]{2,1,0:T(8,128)(2,1)}, u32[]{:S(2)}, u32[]{:S(2)}) collective-permute-start(bf16[2,128,1024]{2,1,0:T(8,128)(2,1)} %pad_maximum_fusion), channel_id=1, source_target_pairs={{0,1},{1,0},{2,3},{3,2},{4,5},{5,4},{6,7},{7,6},{8,9},{9,8},{10,11... | collective-permute-start | bytes 1572872 | tf_op jit(solution)/shard_map/ppermute | solution.py:95
  34.9 5.8 %collective-permute-start.9 = (bf16[2,128,1024]{2,1,0:T(8,128)(2,1)S(1)}, bf16[2,128,1024]{2,1,0:T(8,128)(2,1)S(1)}, u32[]{:S(2)}, u32[]{:S(2)}) collective-permute-start(bf16[2,128,1024]{2,1,0:T(8,128)(2,1)S(1)} %pad_maximum_fusion.1), channel_id=1, source_target_pairs={{0,1},{1,0},{2,3},{3,2},{4,5},{5,4},{6,7},{7,6},{8,9},{9,8},{10,11... | collective-permute-start | bytes 1572872 | tf_op jit(solution)/shard_map/ppermute | solution.py:95
  36.7 2.9 %copy-start.5 = (bf16[128,1024]{1,0:T(8,128)(2,1)S(1)}, bf16[128,1024]{1,0:T(8,128)(2,1)}, u32[]{:S(2)}) copy-start(bf16[128,1024]{1,0:T(8,128)(2,1)} %copy-done.4) | copy-start | bytes 786436
  37.7 4.0 %collective-permute-start.13 = (bf16[2,128,1024]{2,1,0:T(8,128)(2,1)S(1)}, bf16[2,128,1024]{2,1,0:T(8,128)(2,1)S(1)}, u32[]{:S(2)}, u32[]{:S(2)}) collective-permute-start(bf16[2,128,1024]{2,1,0:T(8,128)(2,1)S(1)} %pad_maximum_fusion.2), channel_id=1, source_target_pairs={{0,1},{1,0},{2,3},{3,2},{4,5},{5,4},{6,7},{7,6},{8,9},{9,8},{10,11... | collective-permute-start | bytes 1572872 | tf_op jit(solution)/shard_map/ppermute | solution.py:95
  42.8 4.6 %copy-start.1 = (bf16[8,256,1024]{2,1,0:T(8,128)(2,1)}, bf16[8,256,1024]{2,1,0:T(8,128)(2,1)S(1)}, u32[]{:S(2)}) copy-start(bf16[8,256,1024]{2,1,0:T(8,128)(2,1)S(1)} %maximum_dynamic-update-slice_fusion.3) | copy-start | bytes 12582916
  61.0 3.4 %copy-start = (f32[2048,512]{1,0:T(8,128)S(1)}, f32[2048,512]{1,0:T(8,128)}, u32[]{:S(2)}) copy-start(f32[2048,512]{1,0:T(8,128)} %get-tuple-element.26) | copy-start | bytes 12582916
  63.9 2.3 %copy-start.2 = (bf16[8,256,1024]{2,1,0:T(8,128)(2,1)S(1)}, bf16[8,256,1024]{2,1,0:T(8,128)(2,1)}, u32[]{:S(2)}) copy-start(bf16[8,256,1024]{2,1,0:T(8,128)(2,1)} %copy-done.1) | copy-start | bytes 12582916

commit v23 on v21

--- a/solution.py
+++ b/solution.py
@@ -66,7 +66,7 @@
     for bit in reversed(bits):
         xs = xs + [x ^ bit for x in xs]
 
-    mine = lax.dynamic_slice_in_dim(rows_bf, q * tq, tq, 0)
+    mine = lax.dynamic_slice_in_dim(rows, q * tq, tq, 0).astype(jnp.bfloat16)
     shifts = list(itertools.product(range(n_o), range(n_d)))
     def pair_of(piece):
         across = [piece]
@@ -103,7 +103,7 @@
 
     h = q % 2
     half = t // 2
-    my_half = lax.dynamic_slice_in_dim(rows_bf, h * half, half, 0)
+    my_half = lax.dynamic_slice_in_dim(rows, h * half, half, 0).astype(jnp.bfloat16)
     own_blocks = [rows_bf]
     for sy in range(1, n_d):
         got = lax.ppermute(my_half, "dp", [(j, (j + sy) % n_d) for j in range(n_d)])

time: 66.6 us -> 66.2 us (level)
  local copies, waits for them, and re-layouts: 3.87 us -> 6.02 us
  other arithmetic: 19.3 us -> 17.9 us
  waiting for transfers between devices: 9.09 us -> 7.95 us
    convert_element_type x0 -> x2, local copies, waits for them, and re-layouts: none -> 2.89 us  [the longest x1 1.78 us: shards_all(): lax.dynamic_slice_in_dim(rows, h * half, half, 0).astype(jnp.bfloat16)]
    convert_element_type x1 -> x0, other arithmetic: 1.44 us -> none  [shards_all(): rows_bf = rows.astype(jnp.bfloat16)]
    ppermute x3, waiting for transfers between devices: 4.1 us -> 3.04 us  [shards_all(): landed.append(lax.ppermute(mine, 'outer', pairs))]
    dynamic_slice x2 -> x0, local copies, waits for them, and re-layouts: 0.74 us -> none  [the longest x1 0.72 us: shards_all(): my_half = lax.dynamic_slice_in_dim(rows_bf, h * half, half, 0)]
    ppermute x2, starting transfers between devices: 1.18 us -> 1.87 us  [spread(): other = lax.ppermute(cur, 'cent', [(i, i ^ bit) for i in range(n_c)])]
  transfers between devices with their start and end apart: 14 -> 14, of which waited for: 4 -> 5; matrix products, arithmetic and copies ran while one was open for 16% -> 18% of each run, Pallas kernels for 0% -> 0%
where the time goes in v23:
time: 66.2 us; the launch traced here: 65.7 us
  other arithmetic  17.9 us (27%)
  starting transfers between devices  15.7 us (24%)
  blocking collectives  9.47 us (14%)
  matrix products  8.28 us (13%)
  waiting for transfers between devices  7.95 us (12%)
  local copies, waits for them, and re-layouts  6.02 us (9%)
    all_gather x1, blocking collectives, shards_all(): every = lax.all_gather(both, ('dp', 'cent'), axis=0)  9.47 us
    ppermute x3, starting transfers between devices, shards_all(): landed.append(lax.ppermute(mine, 'outer', pairs))  5.68 us
    dot_general x1, matrix products, scores_for(): lax.dot_general(piece, cent_bf, (((1,), (1,)), ((), ())), preferred_eleme...  4.61 us
    ppermute x3, waiting for transfers between devices, pair_of(): lax.ppermute(piece, 'dp', [(j, (j + sy) % n_d) for j in range(n_d)])  4.29 us
    dot_general x1, matrix products, shards_all(): lax.dot_general(scaled.reshape(n_o * pod, k), everything, (((0,), (0,)),...  3.67 us
    dynamic_update_slice x4, other arithmetic, shards_all(): cur = lax.dynamic_update_slice_in_dim(cur, parts[sz], pod_of * n_d, axis=0)  3.34 us
    ppermute x3, starting transfers between devices, pair_of(): lax.ppermute(piece, 'dp', [(j, (j + sy) % n_d) for j in range(n_d)])  3.33 us
    reduce_sum x1, other arithmetic, row_summary(): local_sum = jnp.sum(jnp.exp(logits - local_max[:, None]), axis=1)  3.31 us
  transfers between devices with their start and end apart: 14, of which 5 were waited for; matrix products, arithmetic and copies ran while one was open for 18% of the time, Pallas kernels for 0%

profile of v23, /device:TPU:0, one launch (start us, length us, event | category | flops | bytes accessed | tf_op | source)
XLA Modules:
  0.0 65.7 jit_solution(18126579333297002310)
XLA Ops:
  0.0 1.1 %dynamic-slice_convert_fusion.1 = bf16[64,1024]{1,0:T(8,128)(2,1)S(1)} fusion(f32[256,1024]{1,0:T(8,128)} %param.3, s32[]{:T(128)S(6)} %select_n.129), kind=kLoop, calls=%fused_computation.21 | loop fusion | bytes 262148 | tf_op jit(solution)/shard_map/convert_element_type | solution.py:69
  1.1 3.1 %collective-permute-start.2 = (bf16[64,1024]{1,0:T(8,128)(2,1)S(1)}, bf16[64,1024]{1,0:T(8,128)(2,1)S(1)}, u32[]{:S(2)}, u32[]{:S(2)}) collective-permute-start(bf16[64,1024]{1,0:T(8,128)(2,1)S(1)} %dynamic-slice_convert_fusion.1), channel_id=1, source_target_pairs={{0,8},{8,0},{16,24},{24,16},{1,9},{9,1},{17,25},{25,17},{2,10},{10... | collective-permute-start | bytes 393224 | tf_op jit(solution)/shard_map/ppermute | solution.py:89
  4.2 2.6 %collective-permute-start.6 = (bf16[64,1024]{1,0:T(8,128)(2,1)S(1)}, bf16[64,1024]{1,0:T(8,128)(2,1)S(1)}, u32[]{:S(2)}, u32[]{:S(2)}) collective-permute-start(bf16[64,1024]{1,0:T(8,128)(2,1)S(1)} %dynamic-slice_convert_fusion.1), channel_id=1, source_target_pairs={{0,16},{8,24},{16,0},{24,8},{1,17},{9,25},{17,1},{25,9},{2,18},{10... | collective-permute-start | bytes 393224 | tf_op jit(solution)/shard_map/ppermute | solution.py:89
  6.8 0.0 collective-permute-start.10
  6.8 1.8 %dynamic-slice_convert_fusion = bf16[128,1024]{1,0:T(8,128)(2,1)} fusion(f32[256,1024]{1,0:T(8,128)} %param.3, s32[]{:T(128)S(6)} %select_n.127), kind=kLoop, calls=%fused_computation.18 | loop fusion | bytes 524292 | tf_op jit(solution)/shard_map/convert_element_type | solution.py:106
  8.6 1.7 %collective-permute-start = (bf16[128,1024]{1,0:T(8,128)(2,1)}, bf16[128,1024]{1,0:T(8,128)(2,1)}, u32[]{:S(2)}, u32[]{:S(2)}) collective-permute-start(bf16[128,1024]{1,0:T(8,128)(2,1)} %dynamic-slice_convert_fusion), channel_id=1, source_target_pairs={{0,4},{4,0},{1,5},{5,1},{2,6},{6,2},{3,7},{7,3},{8,12},{12,8},{9,1... | collective-permute-start | bytes 786440 | tf_op jit(solution)/shard_map/ppermute | solution.py:109
  10.3 1.3 %convert_bitcast_fusion = bf16[1,256,1024]{2,1,0:T(8,128)(2,1)S(1)} fusion(f32[256,1024]{1,0:T(8,128)} %param.3), kind=kLoop, calls=%fused_computation.19 | loop fusion | flops 262144 | bytes 1572864 | tf_op jit(solution)/shard_map/stack | solution.py:112
  11.7 0.7 %fusion.17 = (s32[1,4]{1,0:T(1,128)S(1)}, s32[1,4]{1,0:T(1,128)S(1)}, s32[1,4]{1,0:T(1,128)S(1)}, s32[1,4]{1,0:T(1,128)S(1)}, s32[1,4]{1,0:T(1,128)S(1)}, /*inde...) fusion(s32[4]{0:T(128)} %constant.103.clone, pred[]{:T(512)S(6)} %eq.65, s32[]{:T(128)S(6)} %axis_index.32, ...), kind=kLoop, calls=%fused_computation.72 | loop fusion | flops 96 | bytes 156 | tf_op jit(solution)/shard_map/stack | solution.py:133
  12.4 0.1 copy.27
  12.4 0.1 stack.128
  12.5 0.0 collective-permute-done.2
  12.5 1.6 %collective-permute-start.3 = (bf16[64,1024]{1,0:T(8,128)(2,1)S(1)}, bf16[64,1024]{1,0:T(8,128)(2,1)S(1)}, u32[]{:S(2)}, u32[]{:S(2)}) collective-permute-start(bf16[64,1024]{1,0:T(8,128)(2,1)S(1)} %collective-permute-done.2), channel_id=1, source_target_pairs={{0,2},{1,3},{2,0},{3,1},{4,6},{5,7},{6,4},{7,5},{8,10},{9,11},{10,... | collective-permute-start | bytes 393224 | tf_op jit(solution)/shard_map/ppermute | solution.py:92
  14.1 3.0 %collective-permute-done.6 = bf16[64,1024]{1,0:T(8,128)(2,1)S(1)} collective-permute-done((bf16[64,1024]{1,0:T(8,128)(2,1)S(1)}, bf16[64,1024]{1,0:T(8,128)(2,1)S(1)}, u32[]{:S(2)}, u32[]{:S(2)}) %collective-permute-start.6) | collective-permute-done | bytes 131104 | tf_op jit(solution)/shard_map/ppermute | solution.py:89
  17.1 1.5 %collective-permute-start.7 = (bf16[64,1024]{1,0:T(8,128)(2,1)S(1)}, bf16[64,1024]{1,0:T(8,128)(2,1)S(1)}, u32[]{:S(2)}, u32[]{:S(2)}) collective-permute-start(bf16[64,1024]{1,0:T(8,128)(2,1)S(1)} %collective-permute-done.6), channel_id=1, source_target_pairs={{0,4},{4,0},{1,5},{5,1},{2,6},{6,2},{3,7},{7,3},{8,12},{12,8},{9,1... | collective-permute-start | bytes 393224 | tf_op jit(solution)/shard_map/ppermute | solution.py:74
  18.7 0.0 collective-permute-done.10
  18.7 1.5 %collective-permute-start.11 = (bf16[64,1024]{1,0:T(8,128)(2,1)S(1)}, bf16[64,1024]{1,0:T(8,128)(2,1)S(1)}, u32[]{:S(2)}, u32[]{:S(2)}) collective-permute-start(bf16[64,1024]{1,0:T(8,128)(2,1)S(1)} %collective-permute-done.10), channel_id=1, source_target_pairs={{0,2},{1,3},{2,0},{3,1},{4,6},{5,7},{6,4},{7,5},{8,10},{9,11},{10,... | collective-permute-start | bytes 393224 | tf_op jit(solution)/shard_map/ppermute | solution.py:92
  20.2 0.0 collective-permute-done.3
  20.2 0.6 collective-permute-start.4
  20.8 2.4 %collective-permute-done.7 = bf16[64,1024]{1,0:T(8,128)(2,1)S(1)} collective-permute-done((bf16[64,1024]{1,0:T(8,128)(2,1)S(1)}, bf16[64,1024]{1,0:T(8,128)(2,1)S(1)}, u32[]{:S(2)}, u32[]{:S(2)}) %collective-permute-start.7) | collective-permute-done | bytes 131104 | tf_op jit(solution)/shard_map/ppermute | solution.py:74
  23.2 0.7 %pad_maximum_fusion.3 = bf16[2,64,1024]{2,1,0:T(8,128)(2,1)} fusion(bf16[1,64,1024]{2,1,0:T(8,128)(2,1)S(1)} %bitcast.79, bf16[1,64,1024]{2,1,0:T(8,128)(2,1)S(1)} %bitcast.76), kind=kLoop, calls=%fused_computation.20 | loop fusion | flops 131072 | bytes 524288 | tf_op jit(solution)/shard_map/stack | solution.py:75
  24.0 1.8 %collective-permute-start.8 = (bf16[2,64,1024]{2,1,0:T(8,128)(2,1)}, bf16[2,64,1024]{2,1,0:T(8,128)(2,1)}, u32[]{:S(2)}, u32[]{:S(2)}) collective-permute-start(bf16[2,64,1024]{2,1,0:T(8,128)(2,1)} %pad_maximum_fusion.3), channel_id=1, source_target_pairs={{0,2},{1,3},{2,0},{3,1},{4,6},{5,7},{6,4},{7,5},{8,10},{9,11},{10,... | collective-permute-start | bytes 786440 | tf_op jit(solution)/shard_map/ppermute | solution.py:79
  25.8 0.0 collective-permute-done.11
  25.8 1.2 %collective-permute-start.12 = (bf16[128,1024]{1,0:T(8,128)(2,1)S(1)}, bf16[128,1024]{1,0:T(8,128)(2,1)}, u32[]{:S(2)}, u32[]{:S(2)}) collective-permute-start(bf16[128,1024]{1,0:T(8,128)(2,1)S(1)} %constant_dynamic-update-slice_fusion.2), channel_id=1, source_target_pairs={{0,4},{4,0},{1,5},{5,1},{2,6},{6,2},{3,7},{7,3},{8,12},{12,8},{9,1... | collective-permute-start | bytes 786440 | tf_op jit(solution)/shard_map/ppermute | solution.py:74
  27.0 0.0 collective-permute-done
  27.0 0.0 collective-permute-start.1
  27.0 1.2 %collective-permute-done.4 = bf16[128,1024]{1,0:T(8,128)(2,1)S(1)} collective-permute-done((bf16[128,1024]{1,0:T(8,128)(2,1)S(1)}, bf16[128,1024]{1,0:T(8,128)(2,1)S(1)}, u32[]{:S(2)}, u32[]{:S(2)}) %collective-permute-start.4) | collective-permute-done | bytes 262176 | tf_op jit(solution)/shard_map/ppermute | solution.py:74
  28.3 0.7 %copy-done.4 = bf16[128,1024]{1,0:T(8,128)(2,1)} copy-done((bf16[128,1024]{1,0:T(8,128)(2,1)}, bf16[128,1024]{1,0:T(8,128)(2,1)S(1)}, u32[]{:S(2)}) %copy-start.4) | copy-done | bytes 262168
  29.0 0.8 %pad_maximum_fusion = bf16[2,128,1024]{2,1,0:T(8,128)(2,1)} fusion(bf16[1,128,1024]{2,1,0:T(8,128)(2,1)S(1)} %bitcast.82, bf16[1,128,1024]{2,1,0:T(8,128)(2,1)S(1)} %bitcast.72), kind=kLoop, calls=%fused_computation.15 | loop fusion | flops 262144 | bytes 1048576 | tf_op jit(solution)/shard_map/stack | solution.py:75
  29.8 0.0 collective-permute-start.5
  29.8 0.0 copy-done.3
  29.8 0.2 multiply_reduce_fusion
  30.0 0.6 collective-permute-done.8
  30.7 1.0 %pad_maximum_fusion.1 = bf16[2,128,1024]{2,1,0:T(8,128)(2,1)S(1)} fusion(bf16[2,64,1024]{2,1,0:T(8,128)(2,1)} %collective-permute-done.8, bf16[1,64,1024]{2,1,0:T(8,128)(2,1)S(1)} %bitcast.80, bf16[1,64,1024]{2,1,0:T(8,128)(2,1)S(1)} %bitcast.77), kind=kLoop, calls=%fused_computation.16 | loop fusion | flops 1572864 | bytes 1048576 | tf_op jit(solution)/shard_map/concatenate | solution.py:80
  31.6 0.1 collective-permute-start.9
  31.7 0.6 collective-permute-done.12
  32.3 1.0 %pad_maximum_fusion.2 = bf16[2,128,1024]{2,1,0:T(8,128)(2,1)S(1)} fusion(bf16[1,128,1024]{2,1,0:T(8,128)(2,1)} %bitcast.7, bf16[1,128,1024]{2,1,0:T(8,128)(2,1)S(1)} %bitcast.70), kind=kLoop, calls=%fused_computation.17 | loop fusion | flops 262144 | bytes 1048576 | tf_op jit(solution)/shard_map/stack | solution.py:75
  33.4 0.1 collective-permute-start.13
  33.5 0.0 collective-permute-done.1
  33.5 1.1 %maximum_bitcast_fusion = bf16[1,256,1024]{2,1,0:T(8,128)(2,1)S(1)} fusion(bf16[128,1024]{1,0:T(8,128)(2,1)} %collective-permute-done.1, bf16[128,1024]{1,0:T(8,128)(2,1)} %collective-permute-done), kind=kLoop, calls=%fused_computation.14 | loop fusion | flops 1048576 | bytes 1048576 | tf_op jit(solution)/shard_map/stack | solution.py:112
  34.5 0.5 broadcast_in_dim.138
  35.1 0.1 maximum_dynamic-update-slice_fusion
  35.2 0.0 collective-permute-done.5
  35.2 1.1 %maximum_dynamic-update-slice_fusion.1 = bf16[8,256,1024]{2,1,0:T(8,128)(2,1)S(1)} fusion(bf16[8,256,1024]{2,1,0:T(8,128)(2,1)S(1)} %maximum_dynamic-update-slice_fusion, s32[]{:T(128)S(6)} %select_n.130, bf16[2,128,1024]{2,1,0:T(8,128)(2,1)} %collective-permute-done.5, bf16[1,128,1024]{2,1,0:T(8,128)(2,1)S(1)} %bitcast.83, bf16[1,128,1024]{2,1,0:T(8,128)(2,1)S(1)} %bitcast.73), kind=kLoop, calls=%fused_computation.10 | loop fusion | flops 3145728 | bytes 2097156 | tf_op jit(solution)/shard_map/dynamic_update_slice | solution.py:117
  36.3 0.0 collective-permute-done.9
  36.4 1.1 %maximum_dynamic-update-slice_fusion.2 = bf16[8,256,1024]{2,1,0:T(8,128)(2,1)S(1)} fusion(bf16[8,256,1024]{2,1,0:T(8,128)(2,1)S(1)} %maximum_dynamic-update-slice_fusion.1, s32[]{:T(128)S(6)} %select_n.131, bf16[2,128,1024]{2,1,0:T(8,128)(2,1)S(1)} %collective-permute-done.9, bf16[2,64,1024]{2,1,0:T(8,128)(2,1)} %collective-permute-done.8, ...), kind=kLoop, calls=%fused_computation.11 | loop fusion | flops 4194304 | bytes 2097156 | tf_op jit(solution)/shard_map/dynamic_update_slice | solution.py:117
  37.4 0.0 collective-permute-done.13
  37.4 1.0 %maximum_dynamic-update-slice_fusion.3 = bf16[8,256,1024]{2,1,0:T(8,128)(2,1)S(1)} fusion(bf16[8,256,1024]{2,1,0:T(8,128)(2,1)S(1)} %maximum_dynamic-update-slice_fusion.2, s32[]{:T(128)S(6)} %select_n.132, bf16[2,128,1024]{2,1,0:T(8,128)(2,1)S(1)} %collective-permute-done.13, bf16[1,128,1024]{2,1,0:T(8,128)(2,1)} %bitcast.7, ...), kind=kLoop, calls=%fused_computation.12 | loop fusion | flops 3145728 | bytes 2097156 | tf_op jit(solution)/shard_map/dynamic_update_slice | solution.py:117
  38.5 0.0 copy-start.1
  38.5 4.6 %fusion.21 = (f32[2048]{0:T(1024)S(1)}, f32[2048,512]{1,0:T(8,128)}) fusion(f32[512]{0:T(512)S(1)} %multiply_reduce_fusion, bf16[2048,1024]{1,0:T(8,128)(2,1)S(1)} %bitcast.68, f32[512,1024]{1,0:T(8,128)S(1)} %copy-done.3), kind=kOutput, calls=%fused_computation.76 | convolution fusion | flops 2152200192 | bytes 10496000 | tf_op jit(solution)/shard_map/dot_general | solution.py:10
  43.1 0.1 broadcast_in_dim.141
  43.2 3.3 %exponential_reduce_fusion = f32[2048]{0:T(1024)S(1)} fusion(f32[2048,512]{1,0:T(8,128)} %get-tuple-element.26, f32[2048]{0:T(1024)S(1)} %get-tuple-element.25), kind=kLoop, calls=%fused_computation.4 | loop fusion | flops 2095104 | bytes 4210688 | tf_op jit(solution)/shard_map/reduce_sum | solution.py:18
  46.5 0.1 broadcast_in_dim.146
  46.6 0.1 select_reduce_fusion.7
  46.7 0.2 select_reduce_fusion.3
  46.9 9.5 %all-gather = f32[16,8,4,64]{3,1,2,0:T(8,128)S(1)} all-gather(f32[2,8,4,64]{3,1,2,0:T(8,128)S(1)} %copy.30), channel_id=2, replica_groups=mesh['outer'=4,'dp'=2,'cent'=4] {'dp','cent'}, dimensions={0}, use_global_device_ids=true | all-gather | bytes 147456 | tf_op jit(solution)/shard_map/all_gather | solution.py:147
  56.5 0.1 select_reduce_fusion.1
  56.6 0.1 select_reduce_fusion.5
  56.7 0.1 div.62
  56.8 0.1 sub.53
  56.8 2.8 %bitcast_reduce_fusion = f32[4,512]{1,0:T(4,128)S(1)} fusion(f32[2048]{0:T(1024)S(1)} %div.62, f32[2048,512]{1,0:T(8,128)} %get-tuple-element.26, f32[2048]{0:T(1024)S(1)} %sub.53), kind=kLoop, calls=%fused_computation.2 | loop fusion | flops 5240832 | bytes 4218880 | tf_op jit(solution)/shard_map/reduce_sum | solution.py:158
  59.7 0.6 copy-done
  60.3 1.0 %fusion = bf16[2048,512]{1,0:T(8,128)(2,1)S(1)} fusion(f32[4,512]{1,0:T(4,128)S(1)} %broadcast_add_fusion, f32[2048]{0:T(1024)S(1)} %div.62, f32[2048,512]{1,0:T(8,128)S(1)} %copy-done, f32[2048]{0:T(1024)S(1)} %sub.53), kind=kLoop, calls=%fused_computation.1 | loop fusion | flops 6291456 | bytes 6316032 | tf_op jit(solution)/shard_map/convert_element_type | solution.py:159
  61.3 0.7 %copy-done.2 = bf16[8,256,1024]{2,1,0:T(8,128)(2,1)S(1)} copy-done((bf16[8,256,1024]{2,1,0:T(8,128)(2,1)S(1)}, bf16[8,256,1024]{2,1,0:T(8,128)(2,1)}, u32[]{:S(2)}) %copy-start.2) | copy-done | bytes 4194328
  62.0 3.7 %subtract_multiply_fusion.1 = f32[512,1024]{1,0:T(8,128)} fusion(f32[512,1024]{1,0:T(8,128)S(1)} %copy-done.3, bf16[2048,512]{1,0:T(8,128)(2,1)S(1)} %fusion, bf16[2048,1024]{1,0:T(8,128)(2,1)S(1)} %bitcast.69, f32[512]{0:T(512)S(1)} %fusion.8), kind=kOutput, calls=%fused_computation.7 | convolution fusion | flops 2149056512 | bytes 10487808 | tf_op jit(solution)/shard_map/dot_general | solution.py:160
  (27 shorter events, 0.2 us)
Async XLA Ops:
  0.0 29.8 %copy-start.3 = (f32[512,1024]{1,0:T(8,128)S(1)}, f32[512,1024]{1,0:T(8,128)}, u32[]{:S(2)}) copy-start(f32[512,1024]{1,0:T(8,128)} %param.4) | copy-start | bytes 6291460
  1.1 11.4 %collective-permute-start.2 = (bf16[64,1024]{1,0:T(8,128)(2,1)S(1)}, bf16[64,1024]{1,0:T(8,128)(2,1)S(1)}, u32[]{:S(2)}, u32[]{:S(2)}) collective-permute-start(bf16[64,1024]{1,0:T(8,128)(2,1)S(1)} %dynamic-slice_convert_fusion.1), channel_id=1, source_target_pairs={{0,8},{8,0},{16,24},{24,16},{1,9},{9,1},{17,25},{25,17},{2,10},{10... | collective-permute-start | bytes 393224 | tf_op jit(solution)/shard_map/ppermute | solution.py:89
  4.2 12.9 %collective-permute-start.6 = (bf16[64,1024]{1,0:T(8,128)(2,1)S(1)}, bf16[64,1024]{1,0:T(8,128)(2,1)S(1)}, u32[]{:S(2)}, u32[]{:S(2)}) collective-permute-start(bf16[64,1024]{1,0:T(8,128)(2,1)S(1)} %dynamic-slice_convert_fusion.1), channel_id=1, source_target_pairs={{0,16},{8,24},{16,0},{24,8},{1,17},{9,25},{17,1},{25,9},{2,18},{10... | collective-permute-start | bytes 393224 | tf_op jit(solution)/shard_map/ppermute | solution.py:89
  6.8 11.9 %collective-permute-start.10 = (bf16[64,1024]{1,0:T(8,128)(2,1)S(1)}, bf16[64,1024]{1,0:T(8,128)(2,1)S(1)}, u32[]{:S(2)}, u32[]{:S(2)}) collective-permute-start(bf16[64,1024]{1,0:T(8,128)(2,1)S(1)} %dynamic-slice_convert_fusion.1), channel_id=1, source_target_pairs={{0,24},{8,16},{16,8},{24,0},{1,25},{9,17},{17,9},{25,1},{2,26},{10... | collective-permute-start | bytes 393224 | tf_op jit(solution)/shard_map/ppermute | solution.py:89
  8.6 18.4 %collective-permute-start = (bf16[128,1024]{1,0:T(8,128)(2,1)}, bf16[128,1024]{1,0:T(8,128)(2,1)}, u32[]{:S(2)}, u32[]{:S(2)}) collective-permute-start(bf16[128,1024]{1,0:T(8,128)(2,1)} %dynamic-slice_convert_fusion), channel_id=1, source_target_pairs={{0,4},{4,0},{1,5},{5,1},{2,6},{6,2},{3,7},{7,3},{8,12},{12,8},{9,1... | collective-permute-start | bytes 786440 | tf_op jit(solution)/shard_map/ppermute | solution.py:109
  12.5 7.6 %collective-permute-start.3 = (bf16[64,1024]{1,0:T(8,128)(2,1)S(1)}, bf16[64,1024]{1,0:T(8,128)(2,1)S(1)}, u32[]{:S(2)}, u32[]{:S(2)}) collective-permute-start(bf16[64,1024]{1,0:T(8,128)(2,1)S(1)} %collective-permute-done.2), channel_id=1, source_target_pairs={{0,2},{1,3},{2,0},{3,1},{4,6},{5,7},{6,4},{7,5},{8,10},{9,11},{10,... | collective-permute-start | bytes 393224 | tf_op jit(solution)/shard_map/ppermute | solution.py:92
  17.1 6.1 %collective-permute-start.7 = (bf16[64,1024]{1,0:T(8,128)(2,1)S(1)}, bf16[64,1024]{1,0:T(8,128)(2,1)S(1)}, u32[]{:S(2)}, u32[]{:S(2)}) collective-permute-start(bf16[64,1024]{1,0:T(8,128)(2,1)S(1)} %collective-permute-done.6), channel_id=1, source_target_pairs={{0,4},{4,0},{1,5},{5,1},{2,6},{6,2},{3,7},{7,3},{8,12},{12,8},{9,1... | collective-permute-start | bytes 393224 | tf_op jit(solution)/shard_map/ppermute | solution.py:74
  18.7 7.1 %collective-permute-start.11 = (bf16[64,1024]{1,0:T(8,128)(2,1)S(1)}, bf16[64,1024]{1,0:T(8,128)(2,1)S(1)}, u32[]{:S(2)}, u32[]{:S(2)}) collective-permute-start(bf16[64,1024]{1,0:T(8,128)(2,1)S(1)} %collective-permute-done.10), channel_id=1, source_target_pairs={{0,2},{1,3},{2,0},{3,1},{4,6},{5,7},{6,4},{7,5},{8,10},{9,11},{10,... | collective-permute-start | bytes 393224 | tf_op jit(solution)/shard_map/ppermute | solution.py:92
  20.2 8.1 %collective-permute-start.4 = (bf16[128,1024]{1,0:T(8,128)(2,1)S(1)}, bf16[128,1024]{1,0:T(8,128)(2,1)S(1)}, u32[]{:S(2)}, u32[]{:S(2)}) collective-permute-start(bf16[128,1024]{1,0:T(8,128)(2,1)S(1)} %constant_dynamic-update-slice_fusion), channel_id=1, source_target_pairs={{0,4},{4,0},{1,5},{5,1},{2,6},{6,2},{3,7},{7,3},{8,12},{12,8},{9,1... | collective-permute-start | bytes 786440 | tf_op jit(solution)/shard_map/ppermute | solution.py:74
  24.0 6.7 %collective-permute-start.8 = (bf16[2,64,1024]{2,1,0:T(8,128)(2,1)}, bf16[2,64,1024]{2,1,0:T(8,128)(2,1)}, u32[]{:S(2)}, u32[]{:S(2)}) collective-permute-start(bf16[2,64,1024]{2,1,0:T(8,128)(2,1)} %pad_maximum_fusion.3), channel_id=1, source_target_pairs={{0,2},{1,3},{2,0},{3,1},{4,6},{5,7},{6,4},{7,5},{8,10},{9,11},{10,... | collective-permute-start | bytes 786440 | tf_op jit(solution)/shard_map/ppermute | solution.py:79
  25.8 6.5 %collective-permute-start.12 = (bf16[128,1024]{1,0:T(8,128)(2,1)S(1)}, bf16[128,1024]{1,0:T(8,128)(2,1)}, u32[]{:S(2)}, u32[]{:S(2)}) collective-permute-start(bf16[128,1024]{1,0:T(8,128)(2,1)S(1)} %constant_dynamic-update-slice_fusion.2), channel_id=1, source_target_pairs={{0,4},{4,0},{1,5},{5,1},{2,6},{6,2},{3,7},{7,3},{8,12},{12,8},{9,1... | collective-permute-start | bytes 786440 | tf_op jit(solution)/shard_map/ppermute | solution.py:74
  27.0 6.4 %collective-permute-start.1 = (bf16[128,1024]{1,0:T(8,128)(2,1)}, bf16[128,1024]{1,0:T(8,128)(2,1)}, u32[]{:S(2)}, u32[]{:S(2)}) collective-permute-start(bf16[128,1024]{1,0:T(8,128)(2,1)} %collective-permute-done), channel_id=1, source_target_pairs={{0,1},{1,0},{2,3},{3,2},{4,5},{5,4},{6,7},{7,6},{8,9},{9,8},{10,11... | collective-permute-start | bytes 786440 | tf_op jit(solution)/shard_map/ppermute | solution.py:110
  28.3 0.7 %copy-start.4 = (bf16[128,1024]{1,0:T(8,128)(2,1)}, bf16[128,1024]{1,0:T(8,128)(2,1)S(1)}, u32[]{:S(2)}) copy-start(bf16[128,1024]{1,0:T(8,128)(2,1)S(1)} %collective-permute-done.4) | copy-start | bytes 786436
  29.8 5.4 %collective-permute-start.5 = (bf16[2,128,1024]{2,1,0:T(8,128)(2,1)}, bf16[2,128,1024]{2,1,0:T(8,128)(2,1)}, u32[]{:S(2)}, u32[]{:S(2)}) collective-permute-start(bf16[2,128,1024]{2,1,0:T(8,128)(2,1)} %pad_maximum_fusion), channel_id=1, source_target_pairs={{0,1},{1,0},{2,3},{3,2},{4,5},{5,4},{6,7},{7,6},{8,9},{9,8},{10,11... | collective-permute-start | bytes 1572872 | tf_op jit(solution)/shard_map/ppermute | solution.py:95
  31.6 4.7 %collective-permute-start.9 = (bf16[2,128,1024]{2,1,0:T(8,128)(2,1)S(1)}, bf16[2,128,1024]{2,1,0:T(8,128)(2,1)S(1)}, u32[]{:S(2)}, u32[]{:S(2)}) collective-permute-start(bf16[2,128,1024]{2,1,0:T(8,128)(2,1)S(1)} %pad_maximum_fusion.1), channel_id=1, source_target_pairs={{0,1},{1,0},{2,3},{3,2},{4,5},{5,4},{6,7},{7,6},{8,9},{9,8},{10,11... | collective-permute-start | bytes 1572872 | tf_op jit(solution)/shard_map/ppermute | solution.py:79
  32.3 2.9 %copy-start.5 = (bf16[128,1024]{1,0:T(8,128)(2,1)S(1)}, bf16[128,1024]{1,0:T(8,128)(2,1)}, u32[]{:S(2)}) copy-start(bf16[128,1024]{1,0:T(8,128)(2,1)} %copy-done.4) | copy-start | bytes 786436
  33.4 4.0 %collective-permute-start.13 = (bf16[2,128,1024]{2,1,0:T(8,128)(2,1)S(1)}, bf16[2,128,1024]{2,1,0:T(8,128)(2,1)S(1)}, u32[]{:S(2)}, u32[]{:S(2)}) collective-permute-start(bf16[2,128,1024]{2,1,0:T(8,128)(2,1)S(1)} %pad_maximum_fusion.2), channel_id=1, source_target_pairs={{0,1},{1,0},{2,3},{3,2},{4,5},{5,4},{6,7},{7,6},{8,9},{9,8},{10,11... | collective-permute-start | bytes 1572872 | tf_op jit(solution)/shard_map/ppermute | solution.py:95
  38.5 4.6 %copy-start.1 = (bf16[8,256,1024]{2,1,0:T(8,128)(2,1)}, bf16[8,256,1024]{2,1,0:T(8,128)(2,1)S(1)}, u32[]{:S(2)}) copy-start(bf16[8,256,1024]{2,1,0:T(8,128)(2,1)S(1)} %maximum_dynamic-update-slice_fusion.3) | copy-start | bytes 12582916
  56.8 3.4 %copy-start = (f32[2048,512]{1,0:T(8,128)S(1)}, f32[2048,512]{1,0:T(8,128)}, u32[]{:S(2)}) copy-start(f32[2048,512]{1,0:T(8,128)} %get-tuple-element.26) | copy-start | bytes 12582916
  59.7 2.3 %copy-start.2 = (bf16[8,256,1024]{2,1,0:T(8,128)(2,1)S(1)}, bf16[8,256,1024]{2,1,0:T(8,128)(2,1)}, u32[]{:S(2)}) copy-start(bf16[8,256,1024]{2,1,0:T(8,128)(2,1)} %copy-done.1) | copy-start | bytes 12582916

commit v24 on v23

--- a/solution.py
+++ b/solution.py
@@ -101,15 +101,7 @@
         for sz, piece in enumerate(landed[1:], start=1)
     ]
 
-    h = q % 2
-    half = t // 2
-    my_half = lax.dynamic_slice_in_dim(rows, h * half, half, 0).astype(jnp.bfloat16)
-    own_blocks = [rows_bf]
-    for sy in range(1, n_d):
-        got = lax.ppermute(my_half, "dp", [(j, (j + sy) % n_d) for j in range(n_d)])
-        mate = lax.ppermute(got, "cent", [(i, i ^ 1) for i in range(n_c)])
-        own_blocks.append(jnp.concatenate([got, mate], axis=0))
-    parts[0] = jnp.stack(own_blocks)
+    parts[0] = spread(pair_of(mine))
 
     cur = jnp.zeros((n_o * n_d,) + parts[0].shape[1:], parts[0].dtype)
     for sz in range(n_o):
@@ -124,13 +116,7 @@
     hot_k = src_vec[None, :] == jnp.arange(n_od)[:, None]
     jj = jnp.arange(n_c)
     xor_map = q ^ jnp.asarray(xs, jnp.int32)
-    hq = n_c // 2
-    half_map = ((jj // hq) ^ h) * hq + jj % hq
-    maps = []
-    for a, sy in shifts:
-        own_map = jj if sy == 0 else half_map
-        maps.append(jnp.where(a == z, own_map, xor_map))
-    c_map = jnp.stack(maps)
+    c_map = jnp.broadcast_to(xor_map[None, :], (n_od, n_c))
     hot_kc = c_map[:, None, :] == jj[None, :, None]
 
     def to_absolute(v):

time: 66.2 us -> 62.6 us (0.946)
  other arithmetic: 17.9 us -> 9.24 us
  waiting for transfers between devices: 7.95 us -> 13.4 us
    another operation x3 -> x0, other arithmetic: 3.03 us -> none  [the longest x2 2.36 us: shards_all(): parts[0] = jnp.stack(own_blocks)]
    dynamic_update_slice x4, other arithmetic: 3.34 us -> 0.39 us  [shards_all(): cur = lax.dynamic_update_slice_in_dim(cur, parts[sz], pod_of * n_d, axis=0)]
    another operation x3 -> x4, other arithmetic: 2.62 us -> 0.15 us  [pair_of(): return jnp.stack(across)]
    unnamed x14 -> x12, local copies, waits for them, and re-layouts: 2.03 us -> 4.38 us
    ppermute x3 -> x4, starting transfers between devices: 3.33 us -> 5.63 us  [pair_of(): lax.ppermute(piece, 'dp', [(j, (j + sy) % n_d) for j in range(n_d)])]
    ppermute x3, waiting for transfers between devices: 3.04 us -> 5.26 us  [shards_all(): landed.append(lax.ppermute(mine, 'outer', pairs))]
    ppermute x3 -> x4, waiting for transfers between devices: 4.29 us -> 6.1 us  [pair_of(): lax.ppermute(piece, 'dp', [(j, (j + sy) % n_d) for j in range(n_d)])]
    convert_element_type x1 -> x0, local copies, waits for them, and re-layouts: 1.78 us -> none  [shards_all(): lax.dynamic_slice_in_dim(rows, h * half, half, 0).astype(jnp.bfloat16)]
  transfers between devices with their start and end apart: 14 -> 15, of which waited for: 5 -> 6; matrix products, arithmetic and copies ran while one was open for 18% -> 6% of each run, Pallas kernels for 0% -> 0%
where the time goes in v24:
time: 62.6 us; the launch traced here: 62.4 us
  starting transfers between devices  16.2 us (26%)
  waiting for transfers between devices  13.4 us (21%)
  other arithmetic  9.24 us (15%)
  blocking collectives  8.84 us (14%)
  matrix products  8.3 us (13%)
  local copies, waits for them, and re-layouts  6.06 us (10%)
    all_gather x1, blocking collectives, shards_all(): every = lax.all_gather(both, ('dp', 'cent'), axis=0)  8.84 us
    ppermute x4, waiting for transfers between devices, pair_of(): lax.ppermute(piece, 'dp', [(j, (j + sy) % n_d) for j in range(n_d)])  6.1 us
    ppermute x4, starting transfers between devices, pair_of(): lax.ppermute(piece, 'dp', [(j, (j + sy) % n_d) for j in range(n_d)])  5.63 us
    ppermute x3, waiting for transfers between devices, shards_all(): landed.append(lax.ppermute(mine, 'outer', pairs))  5.26 us
    dot_general x1, matrix products, scores_for(): lax.dot_general(piece, cent_bf, (((1,), (1,)), ((), ())), preferred_eleme...  4.61 us
    ppermute x3, starting transfers between devices, shards_all(): landed.append(lax.ppermute(mine, 'outer', pairs))  4.39 us
    unnamed x12, local copies, waits for them, and re-layouts  4.38 us
    dot_general x1, matrix products, shards_all(): lax.dot_general(scaled.reshape(n_o * pod, k), everything, (((0,), (0,)),...  3.68 us
  transfers between devices with their start and end apart: 15, of which 6 were waited for; matrix products, arithmetic and copies ran while one was open for 6% of the time, Pallas kernels for 0%

profile of v24, /device:TPU:0, one launch (start us, length us, event | category | flops | bytes accessed | tf_op | source)
XLA Modules:
  0.0 62.4 jit_solution(14755789348625956666)
XLA Ops:
  0.0 0.0 copy-start
  0.0 1.2 %copy-done = f32[256,1024]{1,0:T(8,128)S(1)} copy-done((f32[256,1024]{1,0:T(8,128)S(1)}, f32[256,1024]{1,0:T(8,128)}, u32[]{:S(2)}) %copy-start) | copy-done | bytes 1048600
  1.2 0.7 %dynamic-slice_convert_fusion = bf16[64,1024]{1,0:T(8,128)(2,1)} fusion(f32[256,1024]{1,0:T(8,128)S(1)} %copy-done, s32[]{:T(128)S(6)} %select_n.66), kind=kLoop, calls=%fused_computation.20 | loop fusion | bytes 262148 | tf_op jit(solution)/shard_map/convert_element_type | solution.py:69
  1.9 3.0 %collective-permute-start = (bf16[64,1024]{1,0:T(8,128)(2,1)}, bf16[64,1024]{1,0:T(8,128)(2,1)S(1)}, u32[]{:S(2)}, u32[]{:S(2)}) collective-permute-start(bf16[64,1024]{1,0:T(8,128)(2,1)} %dynamic-slice_convert_fusion), channel_id=1, source_target_pairs={{0,4},{4,0},{1,5},{5,1},{2,6},{6,2},{3,7},{7,3},{8,12},{12,8},{9,1... | collective-permute-start | bytes 393224 | tf_op jit(solution)/shard_map/ppermute | solution.py:74
  4.9 1.6 %collective-permute-start.3 = (bf16[64,1024]{1,0:T(8,128)(2,1)}, bf16[64,1024]{1,0:T(8,128)(2,1)}, u32[]{:S(2)}, u32[]{:S(2)}) collective-permute-start(bf16[64,1024]{1,0:T(8,128)(2,1)} %dynamic-slice_convert_fusion), channel_id=1, source_target_pairs={{0,8},{8,0},{16,24},{24,16},{1,9},{9,1},{17,25},{25,17},{2,10},{10... | collective-permute-start | bytes 393224 | tf_op jit(solution)/shard_map/ppermute | solution.py:89
  6.4 2.6 %collective-permute-start.7 = (bf16[64,1024]{1,0:T(8,128)(2,1)}, bf16[64,1024]{1,0:T(8,128)(2,1)S(1)}, u32[]{:S(2)}, u32[]{:S(2)}) collective-permute-start(bf16[64,1024]{1,0:T(8,128)(2,1)} %dynamic-slice_convert_fusion), channel_id=1, source_target_pairs={{0,16},{8,24},{16,0},{24,8},{1,17},{9,25},{17,1},{25,9},{2,18},{10... | collective-permute-start | bytes 393224 | tf_op jit(solution)/shard_map/ppermute | solution.py:89
  9.0 0.2 collective-permute-start.11
  9.3 0.7 %broadcast_xor_fusion = s32[4]{0:T(128)S(1)} fusion(s32[4]{0:T(128)} %constant.75.clone, s32[]{:T(128)S(6)} %axis_index.32), kind=kLoop, calls=%fused_computation.50 | loop fusion | flops 4 | bytes 36 | tf_op jit(solution)/shard_map/xor | solution.py:118
  9.9 0.1 iota_compare_fusion
  10.0 0.1 stack.92
  10.1 0.0 collective-permute-done
  10.2 1.6 %collective-permute-start.1 = (bf16[2,64,1024]{2,1,0:T(8,128)(2,1)S(1)}, bf16[2,64,1024]{2,1,0:T(8,128)(2,1)S(1)}, u32[]{:S(2)}, u32[]{:S(2)}) collective-permute-start(bf16[2,64,1024]{2,1,0:T(8,128)(2,1)S(1)} %pad_maximum_fusion.4), channel_id=1, source_target_pairs={{0,2},{1,3},{2,0},{3,1},{4,6},{5,7},{6,4},{7,5},{8,10},{9,11},{10,... | collective-permute-start | bytes 786440 | tf_op jit(solution)/shard_map/ppermute | solution.py:79
  11.7 0.0 collective-permute-done.3
  11.7 1.4 %collective-permute-start.4 = (bf16[64,1024]{1,0:T(8,128)(2,1)}, bf16[64,1024]{1,0:T(8,128)(2,1)S(1)}, u32[]{:S(2)}, u32[]{:S(2)}) collective-permute-start(bf16[64,1024]{1,0:T(8,128)(2,1)} %collective-permute-done.3), channel_id=1, source_target_pairs={{0,2},{1,3},{2,0},{3,1},{4,6},{5,7},{6,4},{7,5},{8,10},{9,11},{10,... | collective-permute-start | bytes 393224 | tf_op jit(solution)/shard_map/ppermute | solution.py:92
  13.1 0.9 %constant_dynamic-update-slice_fusion.1 = bf16[128,1024]{1,0:T(8,128)(2,1)S(1)} fusion(bf16[64,1024]{1,0:T(8,128)(2,1)} %collective-permute-done.3), kind=kLoop, calls=%fused_computation.37 | loop fusion | bytes 262144
  14.1 5.3 %collective-permute-done.7 = bf16[64,1024]{1,0:T(8,128)(2,1)S(1)} collective-permute-done((bf16[64,1024]{1,0:T(8,128)(2,1)}, bf16[64,1024]{1,0:T(8,128)(2,1)S(1)}, u32[]{:S(2)}, u32[]{:S(2)}) %collective-permute-start.7) | collective-permute-done | bytes 131104 | tf_op jit(solution)/shard_map/ppermute | solution.py:89
  19.3 0.5 collective-permute-start.8
  19.8 0.0 collective-permute-done.11
  19.8 0.9 %constant_dynamic-update-slice_fusion.3 = bf16[128,1024]{1,0:T(8,128)(2,1)S(1)} fusion(bf16[64,1024]{1,0:T(8,128)(2,1)} %collective-permute-done.11), kind=kLoop, calls=%fused_computation.39 | loop fusion | bytes 262144
  20.7 1.6 %collective-permute-start.12 = (bf16[64,1024]{1,0:T(8,128)(2,1)}, bf16[64,1024]{1,0:T(8,128)(2,1)S(1)}, u32[]{:S(2)}, u32[]{:S(2)}) collective-permute-start(bf16[64,1024]{1,0:T(8,128)(2,1)} %collective-permute-done.11), channel_id=1, source_target_pairs={{0,2},{1,3},{2,0},{3,1},{4,6},{5,7},{6,4},{7,5},{8,10},{9,11},{10,... | collective-permute-start | bytes 393224 | tf_op jit(solution)/shard_map/ppermute | solution.py:92
  22.3 0.0 collective-permute-done.4
  22.3 1.6 %collective-permute-start.5 = (bf16[128,1024]{1,0:T(8,128)(2,1)S(1)}, bf16[128,1024]{1,0:T(8,128)(2,1)S(1)}, u32[]{:S(2)}, u32[]{:S(2)}) collective-permute-start(bf16[128,1024]{1,0:T(8,128)(2,1)S(1)} %constant_dynamic-update-slice_fusion), channel_id=1, source_target_pairs={{0,4},{4,0},{1,5},{5,1},{2,6},{6,2},{3,7},{7,3},{8,12},{12,8},{9,1... | collective-permute-start | bytes 786440 | tf_op jit(solution)/shard_map/ppermute | solution.py:74
  23.9 1.8 %collective-permute-done.8 = bf16[64,1024]{1,0:T(8,128)(2,1)S(1)} collective-permute-done((bf16[64,1024]{1,0:T(8,128)(2,1)S(1)}, bf16[64,1024]{1,0:T(8,128)(2,1)S(1)}, u32[]{:S(2)}, u32[]{:S(2)}) %collective-permute-start.8) | collective-permute-done | bytes 131104 | tf_op jit(solution)/shard_map/ppermute | solution.py:74
  25.8 1.4 %collective-permute-start.9 = (bf16[2,64,1024]{2,1,0:T(8,128)(2,1)S(1)}, bf16[2,64,1024]{2,1,0:T(8,128)(2,1)S(1)}, u32[]{:S(2)}, u32[]{:S(2)}) collective-permute-start(bf16[2,64,1024]{2,1,0:T(8,128)(2,1)S(1)} %pad_maximum_fusion.5), channel_id=1, source_target_pairs={{0,2},{1,3},{2,0},{3,1},{4,6},{5,7},{6,4},{7,5},{8,10},{9,11},{10,... | collective-permute-start | bytes 786440 | tf_op jit(solution)/shard_map/ppermute | solution.py:79
  27.2 0.0 collective-permute-done.12
  27.2 0.6 collective-permute-start.13
  27.8 0.0 collective-permute-done.1
  27.8 0.1 collective-permute-start.2
  27.9 2.9 %collective-permute-done.5 = bf16[128,1024]{1,0:T(8,128)(2,1)S(1)} collective-permute-done((bf16[128,1024]{1,0:T(8,128)(2,1)S(1)}, bf16[128,1024]{1,0:T(8,128)(2,1)S(1)}, u32[]{:S(2)}, u32[]{:S(2)}) %collective-permute-start.5) | collective-permute-done | bytes 262176 | tf_op jit(solution)/shard_map/ppermute | solution.py:74
  30.8 0.1 pad_maximum_fusion.1
  30.9 0.1 collective-permute-start.6
  31.0 1.2 %collective-permute-done.9 = bf16[2,64,1024]{2,1,0:T(8,128)(2,1)S(1)} collective-permute-done((bf16[2,64,1024]{2,1,0:T(8,128)(2,1)S(1)}, bf16[2,64,1024]{2,1,0:T(8,128)(2,1)S(1)}, u32[]{:S(2)}, u32[]{:S(2)}) %collective-permute-start.9) | collective-permute-done | bytes 262176 | tf_op jit(solution)/shard_map/ppermute | solution.py:79
  32.3 0.1 collective-permute-start.10
  32.3 1.3 %collective-permute-done.13 = bf16[128,1024]{1,0:T(8,128)(2,1)S(1)} collective-permute-done((bf16[128,1024]{1,0:T(8,128)(2,1)S(1)}, bf16[128,1024]{1,0:T(8,128)(2,1)S(1)}, u32[]{:S(2)}, u32[]{:S(2)}) %collective-permute-start.13) | collective-permute-done | bytes 262176 | tf_op jit(solution)/shard_map/ppermute | solution.py:74
  33.7 0.1 pad_maximum_fusion.3
  33.7 0.1 collective-permute-start.14
  33.8 0.0 copy-done.4
  33.8 0.2 multiply_reduce_fusion
  34.0 0.0 collective-permute-done.2
  34.0 0.5 broadcast_in_dim.138
  34.6 0.1 maximum_dynamic-update-slice_fusion
  34.7 0.0 collective-permute-done.6
  34.7 0.1 maximum_dynamic-update-slice_fusion.1
  34.8 0.0 collective-permute-done.10
  34.8 0.1 maximum_dynamic-update-slice_fusion.2
  34.9 0.8 %collective-permute-done.14 = bf16[2,128,1024]{2,1,0:T(8,128)(2,1)S(1)} collective-permute-done((bf16[2,128,1024]{2,1,0:T(8,128)(2,1)S(1)}, bf16[2,128,1024]{2,1,0:T(8,128)(2,1)S(1)}, u32[]{:S(2)}, u32[]{:S(2)}) %collective-permute-start.14) | collective-permute-done | bytes 524320 | tf_op jit(solution)/shard_map/ppermute | solution.py:95
  35.7 0.1 maximum_dynamic-update-slice_fusion.3
  35.8 0.0 copy-start.2
  35.8 4.6 %fusion.10 = (f32[2048]{0:T(1024)S(1)}, f32[2048,512]{1,0:T(8,128)}) fusion(f32[512]{0:T(512)S(1)} %multiply_reduce_fusion, bf16[2048,1024]{1,0:T(8,128)(2,1)S(1)} %bitcast.51, f32[512,1024]{1,0:T(8,128)S(1)} %copy-done.4), kind=kOutput, calls=%fused_computation.52 | convolution fusion | flops 2152200192 | bytes 10496000 | tf_op jit(solution)/shard_map/dot_general | solution.py:10
  40.4 0.1 broadcast_in_dim.141
  40.5 3.3 %exponential_reduce_fusion = f32[2048]{0:T(1024)S(1)} fusion(f32[2048,512]{1,0:T(8,128)} %get-tuple-element.18, f32[2048]{0:T(1024)S(1)} %get-tuple-element.17), kind=kLoop, calls=%fused_computation.4 | loop fusion | flops 2095104 | bytes 4210688 | tf_op jit(solution)/shard_map/reduce_sum | solution.py:18
  43.8 0.1 broadcast_in_dim.146
  43.9 0.1 select_reduce_fusion.7
  44.0 0.2 select_reduce_fusion.3
  44.2 8.8 %all-gather = f32[16,8,4,64]{3,1,2,0:T(8,128)S(1)} all-gather(f32[2,8,4,64]{3,1,2,0:T(8,128)S(1)} %copy.27), channel_id=2, replica_groups=mesh['outer'=4,'dp'=2,'cent'=4] {'dp','cent'}, dimensions={0}, use_global_device_ids=true | all-gather | bytes 147456 | tf_op jit(solution)/shard_map/all_gather | solution.py:133
  53.1 0.1 select_reduce_fusion.1
  53.2 0.1 select_reduce_fusion.5
  53.4 0.1 div.55
  53.4 0.1 sub.48
  53.5 2.8 %bitcast_reduce_fusion = f32[4,512]{1,0:T(4,128)S(1)} fusion(f32[2048]{0:T(1024)S(1)} %div.55, f32[2048,512]{1,0:T(8,128)} %get-tuple-element.18, f32[2048]{0:T(1024)S(1)} %sub.48), kind=kLoop, calls=%fused_computation.2 | loop fusion | flops 5240832 | bytes 4218880 | tf_op jit(solution)/shard_map/reduce_sum | solution.py:144
  56.4 0.6 copy-done.1
  57.0 1.0 %fusion = bf16[2048,512]{1,0:T(8,128)(2,1)S(1)} fusion(f32[4,512]{1,0:T(4,128)S(1)} %broadcast_add_fusion, f32[2048]{0:T(1024)S(1)} %div.55, f32[2048,512]{1,0:T(8,128)S(1)} %copy-done.1, f32[2048]{0:T(1024)S(1)} %sub.48), kind=kLoop, calls=%fused_computation.1 | loop fusion | flops 6291456 | bytes 6316032 | tf_op jit(solution)/shard_map/convert_element_type | solution.py:145
  58.0 0.7 %copy-done.3 = bf16[8,256,1024]{2,1,0:T(8,128)(2,1)S(1)} copy-done((bf16[8,256,1024]{2,1,0:T(8,128)(2,1)S(1)}, bf16[8,256,1024]{2,1,0:T(8,128)(2,1)}, u32[]{:S(2)}) %copy-start.3) | copy-done | bytes 4194328
  58.7 3.7 %subtract_multiply_fusion.1 = f32[512,1024]{1,0:T(8,128)} fusion(f32[512,1024]{1,0:T(8,128)S(1)} %copy-done.4, bf16[2048,512]{1,0:T(8,128)(2,1)S(1)} %fusion, bf16[2048,1024]{1,0:T(8,128)(2,1)S(1)} %bitcast.52, f32[512]{0:T(512)S(1)} %fusion.8), kind=kOutput, calls=%fused_computation.7 | convolution fusion | flops 2149056512 | bytes 10487808 | tf_op jit(solution)/shard_map/dot_general | solution.py:146
  (25 shorter events, 0.3 us)
Async XLA Ops:
  0.0 1.2 %copy-start = (f32[256,1024]{1,0:T(8,128)S(1)}, f32[256,1024]{1,0:T(8,128)}, u32[]{:S(2)}) copy-start(f32[256,1024]{1,0:T(8,128)} %param.3) | copy-start | bytes 3145732
  0.0 33.8 %copy-start.4 = (f32[512,1024]{1,0:T(8,128)S(1)}, f32[512,1024]{1,0:T(8,128)}, u32[]{:S(2)}) copy-start(f32[512,1024]{1,0:T(8,128)} %param.4) | copy-start | bytes 6291460
  1.9 8.2 %collective-permute-start = (bf16[64,1024]{1,0:T(8,128)(2,1)}, bf16[64,1024]{1,0:T(8,128)(2,1)S(1)}, u32[]{:S(2)}, u32[]{:S(2)}) collective-permute-start(bf16[64,1024]{1,0:T(8,128)(2,1)} %dynamic-slice_convert_fusion), channel_id=1, source_target_pairs={{0,4},{4,0},{1,5},{5,1},{2,6},{6,2},{3,7},{7,3},{8,12},{12,8},{9,1... | collective-permute-start | bytes 393224 | tf_op jit(solution)/shard_map/ppermute | solution.py:74
  4.9 6.9 %collective-permute-start.3 = (bf16[64,1024]{1,0:T(8,128)(2,1)}, bf16[64,1024]{1,0:T(8,128)(2,1)}, u32[]{:S(2)}, u32[]{:S(2)}) collective-permute-start(bf16[64,1024]{1,0:T(8,128)(2,1)} %dynamic-slice_convert_fusion), channel_id=1, source_target_pairs={{0,8},{8,0},{16,24},{24,16},{1,9},{9,1},{17,25},{25,17},{2,10},{10... | collective-permute-start | bytes 393224 | tf_op jit(solution)/shard_map/ppermute | solution.py:89
  6.4 12.9 %collective-permute-start.7 = (bf16[64,1024]{1,0:T(8,128)(2,1)}, bf16[64,1024]{1,0:T(8,128)(2,1)S(1)}, u32[]{:S(2)}, u32[]{:S(2)}) collective-permute-start(bf16[64,1024]{1,0:T(8,128)(2,1)} %dynamic-slice_convert_fusion), channel_id=1, source_target_pairs={{0,16},{8,24},{16,0},{24,8},{1,17},{9,25},{17,1},{25,9},{2,18},{10... | collective-permute-start | bytes 393224 | tf_op jit(solution)/shard_map/ppermute | solution.py:89
  9.0 10.8 %collective-permute-start.11 = (bf16[64,1024]{1,0:T(8,128)(2,1)}, bf16[64,1024]{1,0:T(8,128)(2,1)}, u32[]{:S(2)}, u32[]{:S(2)}) collective-permute-start(bf16[64,1024]{1,0:T(8,128)(2,1)} %dynamic-slice_convert_fusion), channel_id=1, source_target_pairs={{0,24},{8,16},{16,8},{24,0},{1,25},{9,17},{17,9},{25,1},{2,26},{10... | collective-permute-start | bytes 393224 | tf_op jit(solution)/shard_map/ppermute | solution.py:89
  10.2 17.6 %collective-permute-start.1 = (bf16[2,64,1024]{2,1,0:T(8,128)(2,1)S(1)}, bf16[2,64,1024]{2,1,0:T(8,128)(2,1)S(1)}, u32[]{:S(2)}, u32[]{:S(2)}) collective-permute-start(bf16[2,64,1024]{2,1,0:T(8,128)(2,1)S(1)} %pad_maximum_fusion.4), channel_id=1, source_target_pairs={{0,2},{1,3},{2,0},{3,1},{4,6},{5,7},{6,4},{7,5},{8,10},{9,11},{10,... | collective-permute-start | bytes 786440 | tf_op jit(solution)/shard_map/ppermute | solution.py:79
  11.7 10.6 %collective-permute-start.4 = (bf16[64,1024]{1,0:T(8,128)(2,1)}, bf16[64,1024]{1,0:T(8,128)(2,1)S(1)}, u32[]{:S(2)}, u32[]{:S(2)}) collective-permute-start(bf16[64,1024]{1,0:T(8,128)(2,1)} %collective-permute-done.3), channel_id=1, source_target_pairs={{0,2},{1,3},{2,0},{3,1},{4,6},{5,7},{6,4},{7,5},{8,10},{9,11},{10,... | collective-permute-start | bytes 393224 | tf_op jit(solution)/shard_map/ppermute | solution.py:92
  19.3 6.4 %collective-permute-start.8 = (bf16[64,1024]{1,0:T(8,128)(2,1)S(1)}, bf16[64,1024]{1,0:T(8,128)(2,1)S(1)}, u32[]{:S(2)}, u32[]{:S(2)}) collective-permute-start(bf16[64,1024]{1,0:T(8,128)(2,1)S(1)} %collective-permute-done.7), channel_id=1, source_target_pairs={{0,4},{4,0},{1,5},{5,1},{2,6},{6,2},{3,7},{7,3},{8,12},{12,8},{9,1... | collective-permute-start | bytes 393224 | tf_op jit(solution)/shard_map/ppermute | solution.py:74
  20.7 6.5 %collective-permute-start.12 = (bf16[64,1024]{1,0:T(8,128)(2,1)}, bf16[64,1024]{1,0:T(8,128)(2,1)S(1)}, u32[]{:S(2)}, u32[]{:S(2)}) collective-permute-start(bf16[64,1024]{1,0:T(8,128)(2,1)} %collective-permute-done.11), channel_id=1, source_target_pairs={{0,2},{1,3},{2,0},{3,1},{4,6},{5,7},{6,4},{7,5},{8,10},{9,11},{10,... | collective-permute-start | bytes 393224 | tf_op jit(solution)/shard_map/ppermute | solution.py:92
  22.3 8.5 %collective-permute-start.5 = (bf16[128,1024]{1,0:T(8,128)(2,1)S(1)}, bf16[128,1024]{1,0:T(8,128)(2,1)S(1)}, u32[]{:S(2)}, u32[]{:S(2)}) collective-permute-start(bf16[128,1024]{1,0:T(8,128)(2,1)S(1)} %constant_dynamic-update-slice_fusion), channel_id=1, source_target_pairs={{0,4},{4,0},{1,5},{5,1},{2,6},{6,2},{3,7},{7,3},{8,12},{12,8},{9,1... | collective-permute-start | bytes 786440 | tf_op jit(solution)/shard_map/ppermute | solution.py:74
  25.8 6.4 %collective-permute-start.9 = (bf16[2,64,1024]{2,1,0:T(8,128)(2,1)S(1)}, bf16[2,64,1024]{2,1,0:T(8,128)(2,1)S(1)}, u32[]{:S(2)}, u32[]{:S(2)}) collective-permute-start(bf16[2,64,1024]{2,1,0:T(8,128)(2,1)S(1)} %pad_maximum_fusion.5), channel_id=1, source_target_pairs={{0,2},{1,3},{2,0},{3,1},{4,6},{5,7},{6,4},{7,5},{8,10},{9,11},{10,... | collective-permute-start | bytes 786440 | tf_op jit(solution)/shard_map/ppermute | solution.py:79
  27.2 6.4 %collective-permute-start.13 = (bf16[128,1024]{1,0:T(8,128)(2,1)S(1)}, bf16[128,1024]{1,0:T(8,128)(2,1)S(1)}, u32[]{:S(2)}, u32[]{:S(2)}) collective-permute-start(bf16[128,1024]{1,0:T(8,128)(2,1)S(1)} %constant_dynamic-update-slice_fusion.2), channel_id=1, source_target_pairs={{0,4},{4,0},{1,5},{5,1},{2,6},{6,2},{3,7},{7,3},{8,12},{12,8},{9,1... | collective-permute-start | bytes 786440 | tf_op jit(solution)/shard_map/ppermute | solution.py:74
  27.8 6.2 %collective-permute-start.2 = (bf16[2,128,1024]{2,1,0:T(8,128)(2,1)S(1)}, bf16[2,128,1024]{2,1,0:T(8,128)(2,1)S(1)}, u32[]{:S(2)}, u32[]{:S(2)}) collective-permute-start(bf16[2,128,1024]{2,1,0:T(8,128)(2,1)S(1)} %pad_maximum_fusion), channel_id=1, source_target_pairs={{0,1},{1,0},{2,3},{3,2},{4,5},{5,4},{6,7},{7,6},{8,9},{9,8},{10,11... | collective-permute-start | bytes 1572872 | tf_op jit(solution)/shard_map/ppermute | solution.py:79
  30.9 3.8 %collective-permute-start.6 = (bf16[2,128,1024]{2,1,0:T(8,128)(2,1)S(1)}, bf16[2,128,1024]{2,1,0:T(8,128)(2,1)S(1)}, u32[]{:S(2)}, u32[]{:S(2)}) collective-permute-start(bf16[2,128,1024]{2,1,0:T(8,128)(2,1)S(1)} %pad_maximum_fusion.1), channel_id=1, source_target_pairs={{0,1},{1,0},{2,3},{3,2},{4,5},{5,4},{6,7},{7,6},{8,9},{9,8},{10,11... | collective-permute-start | bytes 1572872 | tf_op jit(solution)/shard_map/ppermute | solution.py:95
  32.3 2.5 %collective-permute-start.10 = (bf16[2,128,1024]{2,1,0:T(8,128)(2,1)S(1)}, bf16[2,128,1024]{2,1,0:T(8,128)(2,1)S(1)}, u32[]{:S(2)}, u32[]{:S(2)}) collective-permute-start(bf16[2,128,1024]{2,1,0:T(8,128)(2,1)S(1)} %pad_maximum_fusion.2), channel_id=1, source_target_pairs={{0,1},{1,0},{2,3},{3,2},{4,5},{5,4},{6,7},{7,6},{8,9},{9,8},{10,11... | collective-permute-start | bytes 1572872 | tf_op jit(solution)/shard_map/ppermute | solution.py:79
  33.7 2.0 %collective-permute-start.14 = (bf16[2,128,1024]{2,1,0:T(8,128)(2,1)S(1)}, bf16[2,128,1024]{2,1,0:T(8,128)(2,1)S(1)}, u32[]{:S(2)}, u32[]{:S(2)}) collective-permute-start(bf16[2,128,1024]{2,1,0:T(8,128)(2,1)S(1)} %pad_maximum_fusion.3), channel_id=1, source_target_pairs={{0,1},{1,0},{2,3},{3,2},{4,5},{5,4},{6,7},{7,6},{8,9},{9,8},{10,11... | collective-permute-start | bytes 1572872 | tf_op jit(solution)/shard_map/ppermute | solution.py:95
  35.8 4.6 %copy-start.2 = (bf16[8,256,1024]{2,1,0:T(8,128)(2,1)}, bf16[8,256,1024]{2,1,0:T(8,128)(2,1)S(1)}, u32[]{:S(2)}) copy-start(bf16[8,256,1024]{2,1,0:T(8,128)(2,1)S(1)} %maximum_dynamic-update-slice_fusion.3) | copy-start | bytes 12582916
  53.5 3.4 %copy-start.1 = (f32[2048,512]{1,0:T(8,128)S(1)}, f32[2048,512]{1,0:T(8,128)}, u32[]{:S(2)}) copy-start(f32[2048,512]{1,0:T(8,128)} %get-tuple-element.18) | copy-start | bytes 12582916
  56.4 2.3 %copy-start.3 = (bf16[8,256,1024]{2,1,0:T(8,128)(2,1)S(1)}, bf16[8,256,1024]{2,1,0:T(8,128)(2,1)}, u32[]{:S(2)}) copy-start(bf16[8,256,1024]{2,1,0:T(8,128)(2,1)} %copy-done.2) | copy-start | bytes 12582916

commit v25 on v24

--- a/solution.py
+++ b/solution.py
@@ -129,11 +129,25 @@
         v = jnp.sum(jnp.where(hot_kc[:, :, :, None], v[:, :, None, :], 0.0), axis=1)
         return v.reshape(n_od * n_c * tq)
 
-    both = jnp.stack([to_absolute(local_max), to_absolute(local_sum)])
-    every = lax.all_gather(both, ("dp", "cent"), axis=0)
-    maxes, sums = every[:, 0], every[:, 1]
-    peak_abs = jnp.max(maxes, axis=0)
-    mass_abs = jnp.sum(sums * jnp.exp(maxes - peak_abs[None]), axis=0)
+    peak_abs = to_absolute(local_max)
+    mass_abs = to_absolute(local_sum)
+    if n_d & (n_d - 1) == 0:
+        rounds = [("cent", bit, n_c) for bit in bits]
+        bd = 1
+        while bd < n_d:
+            rounds.append(("dp", bd, n_d))
+            bd *= 2
+        for axis, bit, n in rounds:
+            other = lax.ppermute(jnp.stack([peak_abs, mass_abs]), axis, [(i, i ^ bit) for i in range(n)])
+            top = jnp.maximum(peak_abs, other[0])
+            mass_abs = mass_abs * jnp.exp(peak_abs - top) + other[1] * jnp.exp(other[0] - top)
+            peak_abs = top
+    else:
+        both = jnp.stack([peak_abs, mass_abs])
+        every = lax.all_gather(both, ("dp", "cent"), axis=0)
+        maxes, sums = every[:, 0], every[:, 1]
+        peak_abs = jnp.max(maxes, axis=0)
+        mass_abs = jnp.sum(sums * jnp.exp(maxes - peak_abs[None]), axis=0)
     row_peak = to_local(peak_abs)
     row_mass = to_local(mass_abs)
 

time: 62.6 us -> 63 us (level)
  blocking collectives: 8.84 us -> 0 us
  waiting for transfers between devices: 13.4 us -> 20.8 us
  starting transfers between devices: 16.2 us -> 18.1 us
    all_gather x1 -> x0, blocking collectives: 8.84 us -> none  [shards_all(): every = lax.all_gather(both, ('dp', 'cent'), axis=0)]
    ppermute x0 -> x3, waiting for transfers between devices: none -> 7.36 us  [shards_all(): lax.ppermute(jnp.stack([peak_abs, mass_abs]), axis, [(i, i ^ bit) for i i...]
    ppermute x0 -> x3, starting transfers between devices: none -> 1.87 us  [shards_all(): lax.ppermute(jnp.stack([peak_abs, mass_abs]), axis, [(i, i ^ bit) for i i...]
  transfers between devices with their start and end apart: 15 -> 18, of which waited for: 6 -> 9; matrix products, arithmetic and copies ran while one was open for 6% -> 6% of each run, Pallas kernels for 0% -> 0%
where the time goes in v25:
time: 63 us; the launch traced here: 62.8 us
  waiting for transfers between devices  20.8 us (33%)
  starting transfers between devices  18.1 us (29%)
  other arithmetic  9.29 us (15%)
  matrix products  8.3 us (13%)
  local copies, waits for them, and re-layouts  6.04 us (10%)
    ppermute x3, waiting for transfers between devices, shards_all(): lax.ppermute(jnp.stack([peak_abs, mass_abs]), axis, [(i, i ^ bit) for i i...  7.36 us
    ppermute x4, waiting for transfers between devices, pair_of(): lax.ppermute(piece, 'dp', [(j, (j + sy) % n_d) for j in range(n_d)])  6.1 us
    ppermute x4, starting transfers between devices, pair_of(): lax.ppermute(piece, 'dp', [(j, (j + sy) % n_d) for j in range(n_d)])  5.63 us
    ppermute x3, waiting for transfers between devices, shards_all(): landed.append(lax.ppermute(mine, 'outer', pairs))  5.26 us
    dot_general x1, matrix products, scores_for(): lax.dot_general(piece, cent_bf, (((1,), (1,)), ((), ())), preferred_eleme...  4.61 us
    ppermute x3, starting transfers between devices, shards_all(): landed.append(lax.ppermute(mine, 'outer', pairs))  4.39 us
    unnamed x12, local copies, waits for them, and re-layouts  4.38 us
    dot_general x1, matrix products, shards_all(): lax.dot_general(scaled.reshape(n_o * pod, k), everything, (((0,), (0,)),...  3.68 us
  transfers between devices with their start and end apart: 18, of which 9 were waited for; matrix products, arithmetic and copies ran while one was open for 6% of the time, Pallas kernels for 0%

profile of v25, /device:TPU:0, one launch (start us, length us, event | category | flops | bytes accessed | tf_op | source)
XLA Modules:
  0.0 62.8 jit_solution(6545388478083850941)
XLA Ops:
  0.0 1.2 %copy-done = f32[256,1024]{1,0:T(8,128)S(1)} copy-done((f32[256,1024]{1,0:T(8,128)S(1)}, f32[256,1024]{1,0:T(8,128)}, u32[]{:S(2)}) %copy-start) | copy-done | bytes 1048600
  1.2 0.7 %dynamic-slice_convert_fusion = bf16[64,1024]{1,0:T(8,128)(2,1)} fusion(f32[256,1024]{1,0:T(8,128)S(1)} %copy-done, s32[]{:T(128)S(6)} %select_n.66), kind=kLoop, calls=%fused_computation.20 | loop fusion | bytes 262148 | tf_op jit(solution)/shard_map/convert_element_type | solution.py:69
  1.9 3.0 %collective-permute-start = (bf16[64,1024]{1,0:T(8,128)(2,1)}, bf16[64,1024]{1,0:T(8,128)(2,1)S(1)}, u32[]{:S(2)}, u32[]{:S(2)}) collective-permute-start(bf16[64,1024]{1,0:T(8,128)(2,1)} %dynamic-slice_convert_fusion), channel_id=1, source_target_pairs={{0,4},{4,0},{1,5},{5,1},{2,6},{6,2},{3,7},{7,3},{8,12},{12,8},{9,1... | collective-permute-start | bytes 393224 | tf_op jit(solution)/shard_map/ppermute | solution.py:74
  4.9 1.6 %collective-permute-start.3 = (bf16[64,1024]{1,0:T(8,128)(2,1)}, bf16[64,1024]{1,0:T(8,128)(2,1)}, u32[]{:S(2)}, u32[]{:S(2)}) collective-permute-start(bf16[64,1024]{1,0:T(8,128)(2,1)} %dynamic-slice_convert_fusion), channel_id=1, source_target_pairs={{0,8},{8,0},{16,24},{24,16},{1,9},{9,1},{17,25},{25,17},{2,10},{10... | collective-permute-start | bytes 393224 | tf_op jit(solution)/shard_map/ppermute | solution.py:89
  6.4 2.6 %collective-permute-start.7 = (bf16[64,1024]{1,0:T(8,128)(2,1)}, bf16[64,1024]{1,0:T(8,128)(2,1)S(1)}, u32[]{:S(2)}, u32[]{:S(2)}) collective-permute-start(bf16[64,1024]{1,0:T(8,128)(2,1)} %dynamic-slice_convert_fusion), channel_id=1, source_target_pairs={{0,16},{8,24},{16,0},{24,8},{1,17},{9,25},{17,1},{25,9},{2,18},{10... | collective-permute-start | bytes 393224 | tf_op jit(solution)/shard_map/ppermute | solution.py:89
  9.0 0.2 collective-permute-start.11
  9.3 0.7 %broadcast_xor_fusion = s32[4]{0:T(128)S(1)} fusion(s32[4]{0:T(128)} %constant.75.clone, s32[]{:T(128)S(6)} %axis_index.32), kind=kLoop, calls=%fused_computation.69 | loop fusion | flops 4 | bytes 36 | tf_op jit(solution)/shard_map/xor | solution.py:118
  9.9 0.1 iota_compare_fusion
  10.0 0.1 stack.102
  10.1 0.0 collective-permute-done
  10.2 1.6 %collective-permute-start.1 = (bf16[2,64,1024]{2,1,0:T(8,128)(2,1)S(1)}, bf16[2,64,1024]{2,1,0:T(8,128)(2,1)S(1)}, u32[]{:S(2)}, u32[]{:S(2)}) collective-permute-start(bf16[2,64,1024]{2,1,0:T(8,128)(2,1)S(1)} %pad_maximum_fusion.4), channel_id=1, source_target_pairs={{0,2},{1,3},{2,0},{3,1},{4,6},{5,7},{6,4},{7,5},{8,10},{9,11},{10,... | collective-permute-start | bytes 786440 | tf_op jit(solution)/shard_map/ppermute | solution.py:79
  11.7 0.0 collective-permute-done.3
  11.7 1.4 %collective-permute-start.4 = (bf16[64,1024]{1,0:T(8,128)(2,1)}, bf16[64,1024]{1,0:T(8,128)(2,1)S(1)}, u32[]{:S(2)}, u32[]{:S(2)}) collective-permute-start(bf16[64,1024]{1,0:T(8,128)(2,1)} %collective-permute-done.3), channel_id=1, source_target_pairs={{0,2},{1,3},{2,0},{3,1},{4,6},{5,7},{6,4},{7,5},{8,10},{9,11},{10,... | collective-permute-start | bytes 393224 | tf_op jit(solution)/shard_map/ppermute | solution.py:92
  13.1 0.9 %constant_dynamic-update-slice_fusion.1 = bf16[128,1024]{1,0:T(8,128)(2,1)S(1)} fusion(bf16[64,1024]{1,0:T(8,128)(2,1)} %collective-permute-done.3), kind=kLoop, calls=%fused_computation.56 | loop fusion | bytes 262144
  14.1 5.3 %collective-permute-done.7 = bf16[64,1024]{1,0:T(8,128)(2,1)S(1)} collective-permute-done((bf16[64,1024]{1,0:T(8,128)(2,1)}, bf16[64,1024]{1,0:T(8,128)(2,1)S(1)}, u32[]{:S(2)}, u32[]{:S(2)}) %collective-permute-start.7) | collective-permute-done | bytes 131104 | tf_op jit(solution)/shard_map/ppermute | solution.py:89
  19.3 0.5 collective-permute-start.8
  19.8 0.0 collective-permute-done.11
  19.8 0.9 %constant_dynamic-update-slice_fusion.3 = bf16[128,1024]{1,0:T(8,128)(2,1)S(1)} fusion(bf16[64,1024]{1,0:T(8,128)(2,1)} %collective-permute-done.11), kind=kLoop, calls=%fused_computation.58 | loop fusion | bytes 262144
  20.7 1.6 %collective-permute-start.12 = (bf16[64,1024]{1,0:T(8,128)(2,1)}, bf16[64,1024]{1,0:T(8,128)(2,1)S(1)}, u32[]{:S(2)}, u32[]{:S(2)}) collective-permute-start(bf16[64,1024]{1,0:T(8,128)(2,1)} %collective-permute-done.11), channel_id=1, source_target_pairs={{0,2},{1,3},{2,0},{3,1},{4,6},{5,7},{6,4},{7,5},{8,10},{9,11},{10,... | collective-permute-start | bytes 393224 | tf_op jit(solution)/shard_map/ppermute | solution.py:92
  22.3 0.0 collective-permute-done.4
  22.3 1.6 %collective-permute-start.5 = (bf16[128,1024]{1,0:T(8,128)(2,1)S(1)}, bf16[128,1024]{1,0:T(8,128)(2,1)S(1)}, u32[]{:S(2)}, u32[]{:S(2)}) collective-permute-start(bf16[128,1024]{1,0:T(8,128)(2,1)S(1)} %constant_dynamic-update-slice_fusion), channel_id=1, source_target_pairs={{0,4},{4,0},{1,5},{5,1},{2,6},{6,2},{3,7},{7,3},{8,12},{12,8},{9,1... | collective-permute-start | bytes 786440 | tf_op jit(solution)/shard_map/ppermute | solution.py:74
  23.9 1.8 %collective-permute-done.8 = bf16[64,1024]{1,0:T(8,128)(2,1)S(1)} collective-permute-done((bf16[64,1024]{1,0:T(8,128)(2,1)S(1)}, bf16[64,1024]{1,0:T(8,128)(2,1)S(1)}, u32[]{:S(2)}, u32[]{:S(2)}) %collective-permute-start.8) | collective-permute-done | bytes 131104 | tf_op jit(solution)/shard_map/ppermute | solution.py:74
  25.8 1.4 %collective-permute-start.9 = (bf16[2,64,1024]{2,1,0:T(8,128)(2,1)S(1)}, bf16[2,64,1024]{2,1,0:T(8,128)(2,1)S(1)}, u32[]{:S(2)}, u32[]{:S(2)}) collective-permute-start(bf16[2,64,1024]{2,1,0:T(8,128)(2,1)S(1)} %pad_maximum_fusion.5), channel_id=1, source_target_pairs={{0,2},{1,3},{2,0},{3,1},{4,6},{5,7},{6,4},{7,5},{8,10},{9,11},{10,... | collective-permute-start | bytes 786440 | tf_op jit(solution)/shard_map/ppermute | solution.py:79
  27.2 0.6 collective-permute-start.13
  27.8 0.0 collective-permute-done.1
  27.8 0.1 collective-permute-start.2
  27.9 2.9 %collective-permute-done.5 = bf16[128,1024]{1,0:T(8,128)(2,1)S(1)} collective-permute-done((bf16[128,1024]{1,0:T(8,128)(2,1)S(1)}, bf16[128,1024]{1,0:T(8,128)(2,1)S(1)}, u32[]{:S(2)}, u32[]{:S(2)}) %collective-permute-start.5) | collective-permute-done | bytes 262176 | tf_op jit(solution)/shard_map/ppermute | solution.py:74
  30.8 0.1 pad_maximum_fusion.1
  30.9 0.1 collective-permute-start.6
  31.0 1.2 %collective-permute-done.9 = bf16[2,64,1024]{2,1,0:T(8,128)(2,1)S(1)} collective-permute-done((bf16[2,64,1024]{2,1,0:T(8,128)(2,1)S(1)}, bf16[2,64,1024]{2,1,0:T(8,128)(2,1)S(1)}, u32[]{:S(2)}, u32[]{:S(2)}) %collective-permute-start.9) | collective-permute-done | bytes 262176 | tf_op jit(solution)/shard_map/ppermute | solution.py:79
  32.3 0.1 collective-permute-start.10
  32.3 1.3 %collective-permute-done.13 = bf16[128,1024]{1,0:T(8,128)(2,1)S(1)} collective-permute-done((bf16[128,1024]{1,0:T(8,128)(2,1)S(1)}, bf16[128,1024]{1,0:T(8,128)(2,1)S(1)}, u32[]{:S(2)}, u32[]{:S(2)}) %collective-permute-start.13) | collective-permute-done | bytes 262176 | tf_op jit(solution)/shard_map/ppermute | solution.py:74
  33.7 0.1 pad_maximum_fusion.3
  33.7 0.1 collective-permute-start.14
  33.8 0.2 multiply_reduce_fusion
  34.0 0.0 collective-permute-done.2
  34.0 0.5 broadcast_in_dim.137
  34.6 0.1 maximum_dynamic-update-slice_fusion
  34.7 0.0 collective-permute-done.6
  34.7 0.1 maximum_dynamic-update-slice_fusion.1
  34.8 0.1 maximum_dynamic-update-slice_fusion.2
  34.9 0.8 %collective-permute-done.14 = bf16[2,128,1024]{2,1,0:T(8,128)(2,1)S(1)} collective-permute-done((bf16[2,128,1024]{2,1,0:T(8,128)(2,1)S(1)}, bf16[2,128,1024]{2,1,0:T(8,128)(2,1)S(1)}, u32[]{:S(2)}, u32[]{:S(2)}) %collective-permute-start.14) | collective-permute-done | bytes 524320 | tf_op jit(solution)/shard_map/ppermute | solution.py:95
  35.7 0.1 maximum_dynamic-update-slice_fusion.3
  35.8 4.6 %fusion.19 = (f32[2048]{0:T(1024)S(1)}, f32[2048,512]{1,0:T(8,128)}) fusion(f32[512]{0:T(512)S(1)} %multiply_reduce_fusion, bf16[2048,1024]{1,0:T(8,128)(2,1)S(1)} %bitcast.96, f32[512,1024]{1,0:T(8,128)S(1)} %copy-done.4), kind=kOutput, calls=%fused_computation.71 | convolution fusion | flops 2152200192 | bytes 10496000 | tf_op jit(solution)/shard_map/dot_general | solution.py:10
  40.4 0.1 broadcast_in_dim.140
  40.5 3.3 %exponential_reduce_fusion = f32[2048]{0:T(1024)S(1)} fusion(f32[2048,512]{1,0:T(8,128)} %get-tuple-element.24, f32[2048]{0:T(1024)S(1)} %get-tuple-element.23), kind=kLoop, calls=%fused_computation.4 | loop fusion | flops 2095104 | bytes 4210688 | tf_op jit(solution)/shard_map/reduce_sum | solution.py:18
  43.8 0.1 broadcast_in_dim.145
  43.9 0.1 select_reduce_fusion.7
  44.0 0.2 select_reduce_fusion.3
  44.2 0.2 collective-permute-start.15
  44.4 1.1 %collective-permute-done.15 = f32[2,8,4,64]{3,2,1,0:T(4,128)S(1)} collective-permute-done((f32[2,8,4,64]{3,2,1,0:T(4,128)S(1)}, f32[2,8,4,64]{3,2,1,0:T(4,128)S(1)}, u32[]{:S(2)}, u32[]{:S(2)}) %collective-permute-start.15) | collective-permute-done | bytes 16416 | tf_op jit(solution)/shard_map/ppermute | solution.py:141
  45.5 1.1 %collective-permute-start.16 = (f32[2,8,4,64]{3,2,1,0:T(4,128)S(1)}, f32[2,8,4,64]{3,2,1,0:T(4,128)S(1)}, u32[]{:S(2)}, u32[]{:S(2)}) collective-permute-start(f32[2,8,4,64]{3,2,1,0:T(4,128)S(1)} %pad_maximum_fusion.7), channel_id=1, source_target_pairs={{0,2},{1,3},{2,0},{3,1},{4,6},{5,7},{6,4},{7,5},{8,10},{9,11},{10,... | collective-permute-start | bytes 49160 | tf_op jit(solution)/shard_map/ppermute | solution.py:141
  46.6 2.9 %collective-permute-done.16 = f32[2,8,4,64]{3,2,1,0:T(4,128)S(1)} collective-permute-done((f32[2,8,4,64]{3,2,1,0:T(4,128)S(1)}, f32[2,8,4,64]{3,2,1,0:T(4,128)S(1)}, u32[]{:S(2)}, u32[]{:S(2)}) %collective-permute-start.16) | collective-permute-done | bytes 16416 | tf_op jit(solution)/shard_map/ppermute | solution.py:141
  49.5 0.6 collective-permute-start.17
  50.1 3.4 %collective-permute-done.17 = f32[2,8,4,64]{3,2,1,0:T(4,128)S(1)} collective-permute-done((f32[2,8,4,64]{3,2,1,0:T(4,128)S(1)}, f32[2,8,4,64]{3,2,1,0:T(4,128)S(1)}, u32[]{:S(2)}, u32[]{:S(2)}) %collective-permute-start.17) | collective-permute-done | bytes 16416 | tf_op jit(solution)/shard_map/ppermute | solution.py:141
  53.6 0.1 select_reduce_fusion.1
  53.7 0.1 select_reduce_fusion.5
  53.8 0.1 div.55
  53.9 0.1 sub.100
  53.9 2.8 %bitcast_reduce_fusion = f32[4,512]{1,0:T(4,128)S(1)} fusion(f32[2048]{0:T(1024)S(1)} %div.55, f32[2048,512]{1,0:T(8,128)} %get-tuple-element.24, f32[2048]{0:T(1024)S(1)} %sub.100), kind=kLoop, calls=%fused_computation.2 | loop fusion | flops 5240832 | bytes 4218880 | tf_op jit(solution)/shard_map/reduce_sum | solution.py:158
  56.8 0.6 copy-done.1
  57.4 1.0 %fusion = bf16[2048,512]{1,0:T(8,128)(2,1)S(1)} fusion(f32[4,512]{1,0:T(4,128)S(1)} %broadcast_add_fusion, f32[2048]{0:T(1024)S(1)} %div.55, f32[2048,512]{1,0:T(8,128)S(1)} %copy-done.1, f32[2048]{0:T(1024)S(1)} %sub.100), kind=kLoop, calls=%fused_computation.1 | loop fusion | flops 6291456 | bytes 6316032 | tf_op jit(solution)/shard_map/convert_element_type | solution.py:159
  58.4 0.7 %copy-done.3 = bf16[8,256,1024]{2,1,0:T(8,128)(2,1)S(1)} copy-done((bf16[8,256,1024]{2,1,0:T(8,128)(2,1)S(1)}, bf16[8,256,1024]{2,1,0:T(8,128)(2,1)}, u32[]{:S(2)}) %copy-start.3) | copy-done | bytes 4194328
  59.1 3.7 %subtract_multiply_fusion.1 = f32[512,1024]{1,0:T(8,128)} fusion(f32[512,1024]{1,0:T(8,128)S(1)} %copy-done.4, bf16[2048,512]{1,0:T(8,128)(2,1)S(1)} %fusion, bf16[2048,1024]{1,0:T(8,128)(2,1)S(1)} %bitcast.97, f32[512]{0:T(512)S(1)} %fusion.16), kind=kOutput, calls=%fused_computation.7 | convolution fusion | flops 2149056512 | bytes 10487808 | tf_op jit(solution)/shard_map/dot_general | solution.py:160
  (30 shorter events, 0.4 us)
Async XLA Ops:
  0.0 1.2 %copy-start = (f32[256,1024]{1,0:T(8,128)S(1)}, f32[256,1024]{1,0:T(8,128)}, u32[]{:S(2)}) copy-start(f32[256,1024]{1,0:T(8,128)} %param.3) | copy-start | bytes 3145732
  0.0 33.8 %copy-start.4 = (f32[512,1024]{1,0:T(8,128)S(1)}, f32[512,1024]{1,0:T(8,128)}, u32[]{:S(2)}) copy-start(f32[512,1024]{1,0:T(8,128)} %param.4) | copy-start | bytes 6291460
  1.9 8.2 %collective-permute-start = (bf16[64,1024]{1,0:T(8,128)(2,1)}, bf16[64,1024]{1,0:T(8,128)(2,1)S(1)}, u32[]{:S(2)}, u32[]{:S(2)}) collective-permute-start(bf16[64,1024]{1,0:T(8,128)(2,1)} %dynamic-slice_convert_fusion), channel_id=1, source_target_pairs={{0,4},{4,0},{1,5},{5,1},{2,6},{6,2},{3,7},{7,3},{8,12},{12,8},{9,1... | collective-permute-start | bytes 393224 | tf_op jit(solution)/shard_map/ppermute | solution.py:74
  4.9 6.9 %collective-permute-start.3 = (bf16[64,1024]{1,0:T(8,128)(2,1)}, bf16[64,1024]{1,0:T(8,128)(2,1)}, u32[]{:S(2)}, u32[]{:S(2)}) collective-permute-start(bf16[64,1024]{1,0:T(8,128)(2,1)} %dynamic-slice_convert_fusion), channel_id=1, source_target_pairs={{0,8},{8,0},{16,24},{24,16},{1,9},{9,1},{17,25},{25,17},{2,10},{10... | collective-permute-start | bytes 393224 | tf_op jit(solution)/shard_map/ppermute | solution.py:89
  6.4 12.9 %collective-permute-start.7 = (bf16[64,1024]{1,0:T(8,128)(2,1)}, bf16[64,1024]{1,0:T(8,128)(2,1)S(1)}, u32[]{:S(2)}, u32[]{:S(2)}) collective-permute-start(bf16[64,1024]{1,0:T(8,128)(2,1)} %dynamic-slice_convert_fusion), channel_id=1, source_target_pairs={{0,16},{8,24},{16,0},{24,8},{1,17},{9,25},{17,1},{25,9},{2,18},{10... | collective-permute-start | bytes 393224 | tf_op jit(solution)/shard_map/ppermute | solution.py:89
  9.0 10.8 %collective-permute-start.11 = (bf16[64,1024]{1,0:T(8,128)(2,1)}, bf16[64,1024]{1,0:T(8,128)(2,1)}, u32[]{:S(2)}, u32[]{:S(2)}) collective-permute-start(bf16[64,1024]{1,0:T(8,128)(2,1)} %dynamic-slice_convert_fusion), channel_id=1, source_target_pairs={{0,24},{8,16},{16,8},{24,0},{1,25},{9,17},{17,9},{25,1},{2,26},{10... | collective-permute-start | bytes 393224 | tf_op jit(solution)/shard_map/ppermute | solution.py:89
  10.2 17.6 %collective-permute-start.1 = (bf16[2,64,1024]{2,1,0:T(8,128)(2,1)S(1)}, bf16[2,64,1024]{2,1,0:T(8,128)(2,1)S(1)}, u32[]{:S(2)}, u32[]{:S(2)}) collective-permute-start(bf16[2,64,1024]{2,1,0:T(8,128)(2,1)S(1)} %pad_maximum_fusion.4), channel_id=1, source_target_pairs={{0,2},{1,3},{2,0},{3,1},{4,6},{5,7},{6,4},{7,5},{8,10},{9,11},{10,... | collective-permute-start | bytes 786440 | tf_op jit(solution)/shard_map/ppermute | solution.py:79
  11.7 10.6 %collective-permute-start.4 = (bf16[64,1024]{1,0:T(8,128)(2,1)}, bf16[64,1024]{1,0:T(8,128)(2,1)S(1)}, u32[]{:S(2)}, u32[]{:S(2)}) collective-permute-start(bf16[64,1024]{1,0:T(8,128)(2,1)} %collective-permute-done.3), channel_id=1, source_target_pairs={{0,2},{1,3},{2,0},{3,1},{4,6},{5,7},{6,4},{7,5},{8,10},{9,11},{10,... | collective-permute-start | bytes 393224 | tf_op jit(solution)/shard_map/ppermute | solution.py:92
  19.3 6.4 %collective-permute-start.8 = (bf16[64,1024]{1,0:T(8,128)(2,1)S(1)}, bf16[64,1024]{1,0:T(8,128)(2,1)S(1)}, u32[]{:S(2)}, u32[]{:S(2)}) collective-permute-start(bf16[64,1024]{1,0:T(8,128)(2,1)S(1)} %collective-permute-done.7), channel_id=1, source_target_pairs={{0,4},{4,0},{1,5},{5,1},{2,6},{6,2},{3,7},{7,3},{8,12},{12,8},{9,1... | collective-permute-start | bytes 393224 | tf_op jit(solution)/shard_map/ppermute | solution.py:74
  20.7 6.5 %collective-permute-start.12 = (bf16[64,1024]{1,0:T(8,128)(2,1)}, bf16[64,1024]{1,0:T(8,128)(2,1)S(1)}, u32[]{:S(2)}, u32[]{:S(2)}) collective-permute-start(bf16[64,1024]{1,0:T(8,128)(2,1)} %collective-permute-done.11), channel_id=1, source_target_pairs={{0,2},{1,3},{2,0},{3,1},{4,6},{5,7},{6,4},{7,5},{8,10},{9,11},{10,... | collective-permute-start | bytes 393224 | tf_op jit(solution)/shard_map/ppermute | solution.py:92
  22.3 8.5 %collective-permute-start.5 = (bf16[128,1024]{1,0:T(8,128)(2,1)S(1)}, bf16[128,1024]{1,0:T(8,128)(2,1)S(1)}, u32[]{:S(2)}, u32[]{:S(2)}) collective-permute-start(bf16[128,1024]{1,0:T(8,128)(2,1)S(1)} %constant_dynamic-update-slice_fusion), channel_id=1, source_target_pairs={{0,4},{4,0},{1,5},{5,1},{2,6},{6,2},{3,7},{7,3},{8,12},{12,8},{9,1... | collective-permute-start | bytes 786440 | tf_op jit(solution)/shard_map/ppermute | solution.py:74
  25.8 6.4 %collective-permute-start.9 = (bf16[2,64,1024]{2,1,0:T(8,128)(2,1)S(1)}, bf16[2,64,1024]{2,1,0:T(8,128)(2,1)S(1)}, u32[]{:S(2)}, u32[]{:S(2)}) collective-permute-start(bf16[2,64,1024]{2,1,0:T(8,128)(2,1)S(1)} %pad_maximum_fusion.5), channel_id=1, source_target_pairs={{0,2},{1,3},{2,0},{3,1},{4,6},{5,7},{6,4},{7,5},{8,10},{9,11},{10,... | collective-permute-start | bytes 786440 | tf_op jit(solution)/shard_map/ppermute | solution.py:79
  27.2 6.4 %collective-permute-start.13 = (bf16[128,1024]{1,0:T(8,128)(2,1)S(1)}, bf16[128,1024]{1,0:T(8,128)(2,1)S(1)}, u32[]{:S(2)}, u32[]{:S(2)}) collective-permute-start(bf16[128,1024]{1,0:T(8,128)(2,1)S(1)} %constant_dynamic-update-slice_fusion.2), channel_id=1, source_target_pairs={{0,4},{4,0},{1,5},{5,1},{2,6},{6,2},{3,7},{7,3},{8,12},{12,8},{9,1... | collective-permute-start | bytes 786440 | tf_op jit(solution)/shard_map/ppermute | solution.py:74
  27.8 6.2 %collective-permute-start.2 = (bf16[2,128,1024]{2,1,0:T(8,128)(2,1)S(1)}, bf16[2,128,1024]{2,1,0:T(8,128)(2,1)S(1)}, u32[]{:S(2)}, u32[]{:S(2)}) collective-permute-start(bf16[2,128,1024]{2,1,0:T(8,128)(2,1)S(1)} %pad_maximum_fusion), channel_id=1, source_target_pairs={{0,1},{1,0},{2,3},{3,2},{4,5},{5,4},{6,7},{7,6},{8,9},{9,8},{10,11... | collective-permute-start | bytes 1572872 | tf_op jit(solution)/shard_map/ppermute | solution.py:79
  30.9 3.8 %collective-permute-start.6 = (bf16[2,128,1024]{2,1,0:T(8,128)(2,1)S(1)}, bf16[2,128,1024]{2,1,0:T(8,128)(2,1)S(1)}, u32[]{:S(2)}, u32[]{:S(2)}) collective-permute-start(bf16[2,128,1024]{2,1,0:T(8,128)(2,1)S(1)} %pad_maximum_fusion.1), channel_id=1, source_target_pairs={{0,1},{1,0},{2,3},{3,2},{4,5},{5,4},{6,7},{7,6},{8,9},{9,8},{10,11... | collective-permute-start | bytes 1572872 | tf_op jit(solution)/shard_map/ppermute | solution.py:95
  32.3 2.5 %collective-permute-start.10 = (bf16[2,128,1024]{2,1,0:T(8,128)(2,1)S(1)}, bf16[2,128,1024]{2,1,0:T(8,128)(2,1)S(1)}, u32[]{:S(2)}, u32[]{:S(2)}) collective-permute-start(bf16[2,128,1024]{2,1,0:T(8,128)(2,1)S(1)} %pad_maximum_fusion.2), channel_id=1, source_target_pairs={{0,1},{1,0},{2,3},{3,2},{4,5},{5,4},{6,7},{7,6},{8,9},{9,8},{10,11... | collective-permute-start | bytes 1572872 | tf_op jit(solution)/shard_map/ppermute | solution.py:79
  33.7 2.0 %collective-permute-start.14 = (bf16[2,128,1024]{2,1,0:T(8,128)(2,1)S(1)}, bf16[2,128,1024]{2,1,0:T(8,128)(2,1)S(1)}, u32[]{:S(2)}, u32[]{:S(2)}) collective-permute-start(bf16[2,128,1024]{2,1,0:T(8,128)(2,1)S(1)} %pad_maximum_fusion.3), channel_id=1, source_target_pairs={{0,1},{1,0},{2,3},{3,2},{4,5},{5,4},{6,7},{7,6},{8,9},{9,8},{10,11... | collective-permute-start | bytes 1572872 | tf_op jit(solution)/shard_map/ppermute | solution.py:95
  35.8 4.6 %copy-start.2 = (bf16[8,256,1024]{2,1,0:T(8,128)(2,1)}, bf16[8,256,1024]{2,1,0:T(8,128)(2,1)S(1)}, u32[]{:S(2)}) copy-start(bf16[8,256,1024]{2,1,0:T(8,128)(2,1)S(1)} %maximum_dynamic-update-slice_fusion.3) | copy-start | bytes 12582916
  44.2 1.3 %collective-permute-start.15 = (f32[2,8,4,64]{3,2,1,0:T(4,128)S(1)}, f32[2,8,4,64]{3,2,1,0:T(4,128)S(1)}, u32[]{:S(2)}, u32[]{:S(2)}) collective-permute-start(f32[2,8,4,64]{3,2,1,0:T(4,128)S(1)} %pad_maximum_fusion.6), channel_id=1, source_target_pairs={{0,1},{1,0},{2,3},{3,2},{4,5},{5,4},{6,7},{7,6},{8,9},{9,8},{10,11... | collective-permute-start | bytes 49160 | tf_op jit(solution)/shard_map/ppermute | solution.py:141
  45.5 4.0 %collective-permute-start.16 = (f32[2,8,4,64]{3,2,1,0:T(4,128)S(1)}, f32[2,8,4,64]{3,2,1,0:T(4,128)S(1)}, u32[]{:S(2)}, u32[]{:S(2)}) collective-permute-start(f32[2,8,4,64]{3,2,1,0:T(4,128)S(1)} %pad_maximum_fusion.7), channel_id=1, source_target_pairs={{0,2},{1,3},{2,0},{3,1},{4,6},{5,7},{6,4},{7,5},{8,10},{9,11},{10,... | collective-permute-start | bytes 49160 | tf_op jit(solution)/shard_map/ppermute | solution.py:141
  49.5 4.0 %collective-permute-start.17 = (f32[2,8,4,64]{3,2,1,0:T(4,128)S(1)}, f32[2,8,4,64]{3,2,1,0:T(4,128)S(1)}, u32[]{:S(2)}, u32[]{:S(2)}) collective-permute-start(f32[2,8,4,64]{3,2,1,0:T(4,128)S(1)} %pad_maximum_fusion.8), channel_id=1, source_target_pairs={{0,4},{4,0},{1,5},{5,1},{2,6},{6,2},{3,7},{7,3},{8,12},{12,8},{9,1... | collective-permute-start | bytes 49160 | tf_op jit(solution)/shard_map/ppermute | solution.py:141
  53.9 3.4 %copy-start.1 = (f32[2048,512]{1,0:T(8,128)S(1)}, f32[2048,512]{1,0:T(8,128)}, u32[]{:S(2)}) copy-start(f32[2048,512]{1,0:T(8,128)} %get-tuple-element.24) | copy-start | bytes 12582916
  56.8 2.3 %copy-start.3 = (bf16[8,256,1024]{2,1,0:T(8,128)(2,1)S(1)}, bf16[8,256,1024]{2,1,0:T(8,128)(2,1)}, u32[]{:S(2)}) copy-start(bf16[8,256,1024]{2,1,0:T(8,128)(2,1)} %copy-done.2) | copy-start | bytes 12582916

commit v26 on v24

--- a/solution.py
+++ b/solution.py
@@ -97,11 +97,17 @@
         return cur
 
     parts = [None] + [
-        spread_x_first(piece) if sz in (1, 3) else spread(pair_of(piece))
+        spread_x_first(piece) if sz == 1 else spread(pair_of(piece))
         for sz, piece in enumerate(landed[1:], start=1)
     ]
 
-    parts[0] = spread(pair_of(mine))
+    order = list(reversed(bits))
+    own = lax.dynamic_slice_in_dim(rows, (q ^ order[0]) * tq, tq, 0).astype(jnp.bfloat16)
+    own = pair_of(jnp.concatenate([mine, own], axis=0))
+    for bit in order[1:]:
+        other = lax.ppermute(own, "cent", [(i, i ^ bit) for i in range(n_c)])
+        own = jnp.concatenate([own, other], axis=1)
+    parts[0] = own
 
     cur = jnp.zeros((n_o * n_d,) + parts[0].shape[1:], parts[0].dtype)
     for sz in range(n_o):

time: 62.6 us -> 61.5 us (0.982)
  local copies, waits for them, and re-layouts: 6.06 us -> 3.49 us
  waiting for transfers between devices: 13.4 us -> 14.7 us
    ppermute x4, waiting for transfers between devices: 1.26 us -> 5.6 us  [spread(): other = lax.ppermute(cur, 'cent', [(i, i ^ bit) for i in range(n_c)])]
    ppermute x4, waiting for transfers between devices: 6.1 us -> 2.97 us  [pair_of(): lax.ppermute(piece, 'dp', [(j, (j + sy) % n_d) for j in range(n_d)])]
    unnamed x12 -> x9, local copies, waits for them, and re-layouts: 4.38 us -> 1.31 us
    ppermute x2 -> x1, starting transfers between devices: 2.93 us -> 1.5 us  [spread_x_first(): other = lax.ppermute(piece, 'cent', [(i, i ^ order[0]) for i in range(n_c)])]
    ppermute x3, starting transfers between devices: 4.39 us -> 5.68 us  [shards_all(): landed.append(lax.ppermute(mine, 'outer', pairs))]
    ppermute x3, waiting for transfers between devices: 5.26 us -> 6.15 us  [shards_all(): landed.append(lax.ppermute(mine, 'outer', pairs))]
    ppermute x2 -> x1, waiting for transfers between devices: 0.8 us -> 0.01 us  [spread_x_first(): other = lax.ppermute(cur, 'cent', [(i, i ^ bit) for i in range(n_c)])]
  transfers between devices with their start and end apart: 15 -> 14, of which waited for: 6 -> 6; matrix products, arithmetic and copies ran while one was open for 6% -> 4% of each run, Pallas kernels for 0% -> 0%
where the time goes in v26:
time: 61.5 us; the launch traced here: 61.3 us
  starting transfers between devices  15.9 us (26%)
  waiting for transfers between devices  14.7 us (24%)
  blocking collectives  9.32 us (15%)
  other arithmetic  9.28 us (15%)
  matrix products  8.28 us (13%)
  local copies, waits for them, and re-layouts  3.49 us (6%)
    all_gather x1, blocking collectives, shards_all(): every = lax.all_gather(both, ('dp', 'cent'), axis=0)  9.32 us
    ppermute x3, waiting for transfers between devices, shards_all(): landed.append(lax.ppermute(mine, 'outer', pairs))  6.15 us
    ppermute x3, starting transfers between devices, shards_all(): landed.append(lax.ppermute(mine, 'outer', pairs))  5.68 us
    ppermute x4, waiting for transfers between devices, spread(): other = lax.ppermute(cur, 'cent', [(i, i ^ bit) for i in range(n_c)])  5.6 us
    ppermute x4, starting transfers between devices, pair_of(): lax.ppermute(piece, 'dp', [(j, (j + sy) % n_d) for j in range(n_d)])  5.48 us
    dot_general x1, matrix products, scores_for(): lax.dot_general(piece, cent_bf, (((1,), (1,)), ((), ())), preferred_eleme...  4.61 us
    dot_general x1, matrix products, shards_all(): lax.dot_general(scaled.reshape(n_o * pod, k), everything, (((0,), (0,)),...  3.67 us
    reduce_sum x1, other arithmetic, row_summary(): local_sum = jnp.sum(jnp.exp(logits - local_max[:, None]), axis=1)  3.31 us
  transfers between devices with their start and end apart: 14, of which 6 were waited for; matrix products, arithmetic and copies ran while one was open for 4% of the time, Pallas kernels for 0%

profile of v26, /device:TPU:0, one launch (start us, length us, event | category | flops | bytes accessed | tf_op | source)
XLA Modules:
  0.0 61.3 jit_solution(1662532342259386470)
XLA Ops:
  0.0 0.0 copy-start.3
  0.0 1.2 %dynamic-slice_convert_fusion.1 = (bf16[64,1024]{1,0:T(8,128)(2,1)S(1)}, bf16[64,1024]{1,0:T(8,128)(2,1)S(1)}) fusion(f32[256,1024]{1,0:T(8,128)} %param.3, s32[]{:T(128)S(6)} %select_n.69, s32[]{:T(128)S(6)} %select_n.70), kind=kLoop, calls=%fused_computation.22 | loop fusion | bytes 524296 | tf_op jit(solution)/shard_map/convert_element_type | solution.py:69
  1.2 3.1 %collective-permute-start.2 = (bf16[64,1024]{1,0:T(8,128)(2,1)S(1)}, bf16[64,1024]{1,0:T(8,128)(2,1)S(1)}, u32[]{:S(2)}, u32[]{:S(2)}) collective-permute-start(bf16[64,1024]{1,0:T(8,128)(2,1)S(1)} %get-tuple-element.13), channel_id=1, source_target_pairs={{0,8},{8,0},{16,24},{24,16},{1,9},{9,1},{17,25},{25,17},{2,10},{10... | collective-permute-start | bytes 393224 | tf_op jit(solution)/shard_map/ppermute | solution.py:89
  4.3 2.6 %collective-permute-start.6 = (bf16[64,1024]{1,0:T(8,128)(2,1)S(1)}, bf16[64,1024]{1,0:T(8,128)(2,1)S(1)}, u32[]{:S(2)}, u32[]{:S(2)}) collective-permute-start(bf16[64,1024]{1,0:T(8,128)(2,1)S(1)} %get-tuple-element.13), channel_id=1, source_target_pairs={{0,16},{8,24},{16,0},{24,8},{1,17},{9,25},{17,1},{25,9},{2,18},{10... | collective-permute-start | bytes 393224 | tf_op jit(solution)/shard_map/ppermute | solution.py:89
  6.9 0.0 collective-permute-start.10
  6.9 0.1 fusion.9
  7.0 1.8 %collective-permute-start = (bf16[128,1024]{1,0:T(8,128)(2,1)S(1)}, bf16[128,1024]{1,0:T(8,128)(2,1)S(1)}, u32[]{:S(2)}, u32[]{:S(2)}) collective-permute-start(bf16[128,1024]{1,0:T(8,128)(2,1)S(1)} %get-tuple-element.16), channel_id=1, source_target_pairs={{0,4},{4,0},{1,5},{5,1},{2,6},{6,2},{3,7},{7,3},{8,12},{12,8},{9,1... | collective-permute-start | bytes 786440 | tf_op jit(solution)/shard_map/ppermute | solution.py:74
  8.8 0.7 %broadcast_xor_fusion = s32[4]{0:T(128)S(1)} fusion(s32[4]{0:T(128)} %constant.75.clone, s32[]{:T(128)S(6)} %axis_index.32), kind=kLoop, calls=%fused_computation.50 | loop fusion | flops 4 | bytes 36 | tf_op jit(solution)/shard_map/xor | solution.py:124
  9.4 0.1 stack.92
  9.5 0.1 iota_compare_fusion
  9.6 0.0 collective-permute-done.2
  9.6 1.5 %collective-permute-start.3 = (bf16[64,1024]{1,0:T(8,128)(2,1)S(1)}, bf16[64,1024]{1,0:T(8,128)(2,1)S(1)}, u32[]{:S(2)}, u32[]{:S(2)}) collective-permute-start(bf16[64,1024]{1,0:T(8,128)(2,1)S(1)} %collective-permute-done.2), channel_id=1, source_target_pairs={{0,2},{1,3},{2,0},{3,1},{4,6},{5,7},{6,4},{7,5},{8,10},{9,11},{10,... | collective-permute-start | bytes 393224 | tf_op jit(solution)/shard_map/ppermute | solution.py:92
  11.1 6.1 %collective-permute-done.6 = bf16[64,1024]{1,0:T(8,128)(2,1)S(1)} collective-permute-done((bf16[64,1024]{1,0:T(8,128)(2,1)S(1)}, bf16[64,1024]{1,0:T(8,128)(2,1)S(1)}, u32[]{:S(2)}, u32[]{:S(2)}) %collective-permute-start.6) | collective-permute-done | bytes 131104 | tf_op jit(solution)/shard_map/ppermute | solution.py:89
  17.2 1.5 %collective-permute-start.7 = (bf16[64,1024]{1,0:T(8,128)(2,1)S(1)}, bf16[64,1024]{1,0:T(8,128)(2,1)S(1)}, u32[]{:S(2)}, u32[]{:S(2)}) collective-permute-start(bf16[64,1024]{1,0:T(8,128)(2,1)S(1)} %collective-permute-done.6), channel_id=1, source_target_pairs={{0,4},{4,0},{1,5},{5,1},{2,6},{6,2},{3,7},{7,3},{8,12},{12,8},{9,1... | collective-permute-start | bytes 393224 | tf_op jit(solution)/shard_map/ppermute | solution.py:74
  18.8 0.0 collective-permute-done.10
  18.8 0.6 collective-permute-start.11
  19.4 0.0 collective-permute-done.3
  19.4 1.6 %collective-permute-start.4 = (bf16[128,1024]{1,0:T(8,128)(2,1)S(1)}, bf16[128,1024]{1,0:T(8,128)(2,1)S(1)}, u32[]{:S(2)}, u32[]{:S(2)}) collective-permute-start(bf16[128,1024]{1,0:T(8,128)(2,1)S(1)} %constant_dynamic-update-slice_fusion), channel_id=1, source_target_pairs={{0,4},{4,0},{1,5},{5,1},{2,6},{6,2},{3,7},{7,3},{8,12},{12,8},{9,1... | collective-permute-start | bytes 786440 | tf_op jit(solution)/shard_map/ppermute | solution.py:74
  21.0 1.9 %collective-permute-done.7 = bf16[64,1024]{1,0:T(8,128)(2,1)S(1)} collective-permute-done((bf16[64,1024]{1,0:T(8,128)(2,1)S(1)}, bf16[64,1024]{1,0:T(8,128)(2,1)S(1)}, u32[]{:S(2)}, u32[]{:S(2)}) %collective-permute-start.7) | collective-permute-done | bytes 131104 | tf_op jit(solution)/shard_map/ppermute | solution.py:74
  22.9 1.6 %collective-permute-start.8 = (bf16[2,64,1024]{2,1,0:T(8,128)(2,1)S(1)}, bf16[2,64,1024]{2,1,0:T(8,128)(2,1)S(1)}, u32[]{:S(2)}, u32[]{:S(2)}) collective-permute-start(bf16[2,64,1024]{2,1,0:T(8,128)(2,1)S(1)} %pad_maximum_fusion.5), channel_id=1, source_target_pairs={{0,2},{1,3},{2,0},{3,1},{4,6},{5,7},{6,4},{7,5},{8,10},{9,11},{10,... | collective-permute-start | bytes 786440 | tf_op jit(solution)/shard_map/ppermute | solution.py:79
  24.4 0.0 collective-permute-done.11
  24.5 1.4 %collective-permute-start.12 = (bf16[2,64,1024]{2,1,0:T(8,128)(2,1)S(1)}, bf16[2,64,1024]{2,1,0:T(8,128)(2,1)S(1)}, u32[]{:S(2)}, u32[]{:S(2)}) collective-permute-start(bf16[2,64,1024]{2,1,0:T(8,128)(2,1)S(1)} %pad_maximum_fusion.6), channel_id=1, source_target_pairs={{0,2},{1,3},{2,0},{3,1},{4,6},{5,7},{6,4},{7,5},{8,10},{9,11},{10,... | collective-permute-start | bytes 786440 | tf_op jit(solution)/shard_map/ppermute | solution.py:79
  25.8 0.0 collective-permute-done
  25.8 0.1 pad_maximum_fusion
  25.9 0.1 collective-permute-start.1
  26.0 1.1 %collective-permute-done.4 = bf16[128,1024]{1,0:T(8,128)(2,1)S(1)} collective-permute-done((bf16[128,1024]{1,0:T(8,128)(2,1)S(1)}, bf16[128,1024]{1,0:T(8,128)(2,1)S(1)}, u32[]{:S(2)}, u32[]{:S(2)}) %collective-permute-start.4) | collective-permute-done | bytes 262176 | tf_op jit(solution)/shard_map/ppermute | solution.py:74
  27.0 0.1 pad_maximum_fusion.1
  27.1 0.1 collective-permute-start.5
  27.2 2.1 %collective-permute-done.8 = bf16[2,64,1024]{2,1,0:T(8,128)(2,1)S(1)} collective-permute-done((bf16[2,64,1024]{2,1,0:T(8,128)(2,1)S(1)}, bf16[2,64,1024]{2,1,0:T(8,128)(2,1)S(1)}, u32[]{:S(2)}, u32[]{:S(2)}) %collective-permute-start.8) | collective-permute-done | bytes 262176 | tf_op jit(solution)/shard_map/ppermute | solution.py:79
  29.3 0.1 collective-permute-start.9
  29.4 2.7 %collective-permute-done.12 = bf16[2,64,1024]{2,1,0:T(8,128)(2,1)S(1)} collective-permute-done((bf16[2,64,1024]{2,1,0:T(8,128)(2,1)S(1)}, bf16[2,64,1024]{2,1,0:T(8,128)(2,1)S(1)}, u32[]{:S(2)}, u32[]{:S(2)}) %collective-permute-start.12) | collective-permute-done | bytes 262176 | tf_op jit(solution)/shard_map/ppermute | solution.py:79
  32.2 0.1 collective-permute-start.13
  32.2 0.0 copy-done.3
  32.2 0.2 multiply_reduce_fusion
  32.5 0.0 collective-permute-done.1
  32.5 0.5 broadcast_in_dim.138
  33.0 0.1 maximum_dynamic-update-slice_fusion
  33.1 0.0 collective-permute-done.5
  33.1 0.1 maximum_dynamic-update-slice_fusion.1
  33.2 0.0 collective-permute-done.9
  33.2 0.1 maximum_dynamic-update-slice_fusion.2
  33.3 0.8 %collective-permute-done.13 = bf16[2,128,1024]{2,1,0:T(8,128)(2,1)S(1)} collective-permute-done((bf16[2,128,1024]{2,1,0:T(8,128)(2,1)S(1)}, bf16[2,128,1024]{2,1,0:T(8,128)(2,1)S(1)}, u32[]{:S(2)}, u32[]{:S(2)}) %collective-permute-start.13) | collective-permute-done | bytes 524320 | tf_op jit(solution)/shard_map/ppermute | solution.py:79
  34.1 0.1 maximum_dynamic-update-slice_fusion.3
  34.2 0.0 copy-start.1
  34.2 4.6 %fusion.11 = (f32[2048]{0:T(1024)S(1)}, f32[2048,512]{1,0:T(8,128)}) fusion(f32[512]{0:T(512)S(1)} %multiply_reduce_fusion, bf16[2048,1024]{1,0:T(8,128)(2,1)S(1)} %bitcast.51, f32[512,1024]{1,0:T(8,128)S(1)} %copy-done.3), kind=kOutput, calls=%fused_computation.53 | convolution fusion | flops 2152200192 | bytes 10496000 | tf_op jit(solution)/shard_map/dot_general | solution.py:10
  38.8 0.0 copy-done.1
  38.9 0.1 broadcast_in_dim.141
  38.9 3.3 %exponential_reduce_fusion = f32[2048]{0:T(1024)S(1)} fusion(f32[2048,512]{1,0:T(8,128)} %get-tuple-element.22, f32[2048]{0:T(1024)S(1)} %get-tuple-element.21), kind=kLoop, calls=%fused_computation.4 | loop fusion | flops 2095104 | bytes 4210688 | tf_op jit(solution)/shard_map/reduce_sum | solution.py:18
  42.3 0.1 broadcast_in_dim.146
  42.3 0.1 select_reduce_fusion.7
  42.4 0.2 select_reduce_fusion.3
  42.6 9.3 %all-gather = f32[16,8,4,64]{3,1,2,0:T(8,128)S(1)} all-gather(f32[2,8,4,64]{3,1,2,0:T(8,128)S(1)} %copy.27), channel_id=2, replica_groups=mesh['outer'=4,'dp'=2,'cent'=4] {'dp','cent'}, dimensions={0}, use_global_device_ids=true | all-gather | bytes 147456 | tf_op jit(solution)/shard_map/all_gather | solution.py:139
  52.1 0.1 select_reduce_fusion.1
  52.2 0.1 select_reduce_fusion.5
  52.3 0.1 div.55
  52.3 0.1 sub.48
  52.4 0.0 copy-start
  52.4 2.8 %bitcast_reduce_fusion = f32[4,512]{1,0:T(4,128)S(1)} fusion(f32[2048]{0:T(1024)S(1)} %div.55, f32[2048,512]{1,0:T(8,128)} %get-tuple-element.22, f32[2048]{0:T(1024)S(1)} %sub.48), kind=kLoop, calls=%fused_computation.2 | loop fusion | flops 5240832 | bytes 4218880 | tf_op jit(solution)/shard_map/reduce_sum | solution.py:150
  55.3 0.0 copy-start.2
  55.3 0.6 copy-done
  55.9 1.0 %fusion = bf16[2048,512]{1,0:T(8,128)(2,1)S(1)} fusion(f32[4,512]{1,0:T(4,128)S(1)} %broadcast_add_fusion, f32[2048]{0:T(1024)S(1)} %div.55, f32[2048,512]{1,0:T(8,128)S(1)} %copy-done, f32[2048]{0:T(1024)S(1)} %sub.48), kind=kLoop, calls=%fused_computation.1 | loop fusion | flops 6291456 | bytes 6316032 | tf_op jit(solution)/shard_map/convert_element_type | solution.py:151
  56.9 0.7 %copy-done.2 = bf16[8,256,1024]{2,1,0:T(8,128)(2,1)S(1)} copy-done((bf16[8,256,1024]{2,1,0:T(8,128)(2,1)S(1)}, bf16[8,256,1024]{2,1,0:T(8,128)(2,1)}, u32[]{:S(2)}) %copy-start.2) | copy-done | bytes 4194328
  57.6 3.7 %subtract_multiply_fusion.1 = f32[512,1024]{1,0:T(8,128)} fusion(f32[512,1024]{1,0:T(8,128)S(1)} %copy-done.3, bf16[2048,512]{1,0:T(8,128)(2,1)S(1)} %fusion, bf16[2048,1024]{1,0:T(8,128)(2,1)S(1)} %bitcast.52, f32[512]{0:T(512)S(1)} %fusion.8), kind=kOutput, calls=%fused_computation.7 | convolution fusion | flops 2149056512 | bytes 10487808 | tf_op jit(solution)/shard_map/dot_general | solution.py:152
  (20 shorter events, 0.3 us)
Async XLA Ops:
  0.0 32.2 %copy-start.3 = (f32[512,1024]{1,0:T(8,128)S(1)}, f32[512,1024]{1,0:T(8,128)}, u32[]{:S(2)}) copy-start(f32[512,1024]{1,0:T(8,128)} %param.4) | copy-start | bytes 6291460
  1.2 8.4 %collective-permute-start.2 = (bf16[64,1024]{1,0:T(8,128)(2,1)S(1)}, bf16[64,1024]{1,0:T(8,128)(2,1)S(1)}, u32[]{:S(2)}, u32[]{:S(2)}) collective-permute-start(bf16[64,1024]{1,0:T(8,128)(2,1)S(1)} %get-tuple-element.13), channel_id=1, source_target_pairs={{0,8},{8,0},{16,24},{24,16},{1,9},{9,1},{17,25},{25,17},{2,10},{10... | collective-permute-start | bytes 393224 | tf_op jit(solution)/shard_map/ppermute | solution.py:89
  4.3 12.9 %collective-permute-start.6 = (bf16[64,1024]{1,0:T(8,128)(2,1)S(1)}, bf16[64,1024]{1,0:T(8,128)(2,1)S(1)}, u32[]{:S(2)}, u32[]{:S(2)}) collective-permute-start(bf16[64,1024]{1,0:T(8,128)(2,1)S(1)} %get-tuple-element.13), channel_id=1, source_target_pairs={{0,16},{8,24},{16,0},{24,8},{1,17},{9,25},{17,1},{25,9},{2,18},{10... | collective-permute-start | bytes 393224 | tf_op jit(solution)/shard_map/ppermute | solution.py:89
  6.9 11.9 %collective-permute-start.10 = (bf16[64,1024]{1,0:T(8,128)(2,1)S(1)}, bf16[64,1024]{1,0:T(8,128)(2,1)S(1)}, u32[]{:S(2)}, u32[]{:S(2)}) collective-permute-start(bf16[64,1024]{1,0:T(8,128)(2,1)S(1)} %get-tuple-element.13), channel_id=1, source_target_pairs={{0,24},{8,16},{16,8},{24,0},{1,25},{9,17},{17,9},{25,1},{2,26},{10... | collective-permute-start | bytes 393224 | tf_op jit(solution)/shard_map/ppermute | solution.py:89
  7.0 18.9 %collective-permute-start = (bf16[128,1024]{1,0:T(8,128)(2,1)S(1)}, bf16[128,1024]{1,0:T(8,128)(2,1)S(1)}, u32[]{:S(2)}, u32[]{:S(2)}) collective-permute-start(bf16[128,1024]{1,0:T(8,128)(2,1)S(1)} %get-tuple-element.16), channel_id=1, source_target_pairs={{0,4},{4,0},{1,5},{5,1},{2,6},{6,2},{3,7},{7,3},{8,12},{12,8},{9,1... | collective-permute-start | bytes 786440 | tf_op jit(solution)/shard_map/ppermute | solution.py:74
  9.6 9.8 %collective-permute-start.3 = (bf16[64,1024]{1,0:T(8,128)(2,1)S(1)}, bf16[64,1024]{1,0:T(8,128)(2,1)S(1)}, u32[]{:S(2)}, u32[]{:S(2)}) collective-permute-start(bf16[64,1024]{1,0:T(8,128)(2,1)S(1)} %collective-permute-done.2), channel_id=1, source_target_pairs={{0,2},{1,3},{2,0},{3,1},{4,6},{5,7},{6,4},{7,5},{8,10},{9,11},{10,... | collective-permute-start | bytes 393224 | tf_op jit(solution)/shard_map/ppermute | solution.py:92
  17.2 5.6 %collective-permute-start.7 = (bf16[64,1024]{1,0:T(8,128)(2,1)S(1)}, bf16[64,1024]{1,0:T(8,128)(2,1)S(1)}, u32[]{:S(2)}, u32[]{:S(2)}) collective-permute-start(bf16[64,1024]{1,0:T(8,128)(2,1)S(1)} %collective-permute-done.6), channel_id=1, source_target_pairs={{0,4},{4,0},{1,5},{5,1},{2,6},{6,2},{3,7},{7,3},{8,12},{12,8},{9,1... | collective-permute-start | bytes 393224 | tf_op jit(solution)/shard_map/ppermute | solution.py:74
  18.8 5.6 %collective-permute-start.11 = (bf16[64,1024]{1,0:T(8,128)(2,1)S(1)}, bf16[64,1024]{1,0:T(8,128)(2,1)S(1)}, u32[]{:S(2)}, u32[]{:S(2)}) collective-permute-start(bf16[64,1024]{1,0:T(8,128)(2,1)S(1)} %collective-permute-done.10), channel_id=1, source_target_pairs={{0,4},{4,0},{1,5},{5,1},{2,6},{6,2},{3,7},{7,3},{8,12},{12,8},{9,1... | collective-permute-start | bytes 393224 | tf_op jit(solution)/shard_map/ppermute | solution.py:74
  19.4 7.7 %collective-permute-start.4 = (bf16[128,1024]{1,0:T(8,128)(2,1)S(1)}, bf16[128,1024]{1,0:T(8,128)(2,1)S(1)}, u32[]{:S(2)}, u32[]{:S(2)}) collective-permute-start(bf16[128,1024]{1,0:T(8,128)(2,1)S(1)} %constant_dynamic-update-slice_fusion), channel_id=1, source_target_pairs={{0,4},{4,0},{1,5},{5,1},{2,6},{6,2},{3,7},{7,3},{8,12},{12,8},{9,1... | collective-permute-start | bytes 786440 | tf_op jit(solution)/shard_map/ppermute | solution.py:74
  22.9 6.4 %collective-permute-start.8 = (bf16[2,64,1024]{2,1,0:T(8,128)(2,1)S(1)}, bf16[2,64,1024]{2,1,0:T(8,128)(2,1)S(1)}, u32[]{:S(2)}, u32[]{:S(2)}) collective-permute-start(bf16[2,64,1024]{2,1,0:T(8,128)(2,1)S(1)} %pad_maximum_fusion.5), channel_id=1, source_target_pairs={{0,2},{1,3},{2,0},{3,1},{4,6},{5,7},{6,4},{7,5},{8,10},{9,11},{10,... | collective-permute-start | bytes 786440 | tf_op jit(solution)/shard_map/ppermute | solution.py:79
  24.5 7.7 %collective-permute-start.12 = (bf16[2,64,1024]{2,1,0:T(8,128)(2,1)S(1)}, bf16[2,64,1024]{2,1,0:T(8,128)(2,1)S(1)}, u32[]{:S(2)}, u32[]{:S(2)}) collective-permute-start(bf16[2,64,1024]{2,1,0:T(8,128)(2,1)S(1)} %pad_maximum_fusion.6), channel_id=1, source_target_pairs={{0,2},{1,3},{2,0},{3,1},{4,6},{5,7},{6,4},{7,5},{8,10},{9,11},{10,... | collective-permute-start | bytes 786440 | tf_op jit(solution)/shard_map/ppermute | solution.py:79
  25.9 6.6 %collective-permute-start.1 = (bf16[2,128,1024]{2,1,0:T(8,128)(2,1)S(1)}, bf16[2,128,1024]{2,1,0:T(8,128)(2,1)S(1)}, u32[]{:S(2)}, u32[]{:S(2)}) collective-permute-start(bf16[2,128,1024]{2,1,0:T(8,128)(2,1)S(1)} %pad_maximum_fusion), channel_id=1, source_target_pairs={{0,1},{1,0},{2,3},{3,2},{4,5},{5,4},{6,7},{7,6},{8,9},{9,8},{10,11... | collective-permute-start | bytes 1572872 | tf_op jit(solution)/shard_map/ppermute | solution.py:108
  27.1 6.0 %collective-permute-start.5 = (bf16[2,128,1024]{2,1,0:T(8,128)(2,1)S(1)}, bf16[2,128,1024]{2,1,0:T(8,128)(2,1)S(1)}, u32[]{:S(2)}, u32[]{:S(2)}) collective-permute-start(bf16[2,128,1024]{2,1,0:T(8,128)(2,1)S(1)} %pad_maximum_fusion.1), channel_id=1, source_target_pairs={{0,1},{1,0},{2,3},{3,2},{4,5},{5,4},{6,7},{7,6},{8,9},{9,8},{10,11... | collective-permute-start | bytes 1572872 | tf_op jit(solution)/shard_map/ppermute | solution.py:95
  29.3 3.9 %collective-permute-start.9 = (bf16[2,128,1024]{2,1,0:T(8,128)(2,1)S(1)}, bf16[2,128,1024]{2,1,0:T(8,128)(2,1)S(1)}, u32[]{:S(2)}, u32[]{:S(2)}) collective-permute-start(bf16[2,128,1024]{2,1,0:T(8,128)(2,1)S(1)} %pad_maximum_fusion.2), channel_id=1, source_target_pairs={{0,1},{1,0},{2,3},{3,2},{4,5},{5,4},{6,7},{7,6},{8,9},{9,8},{10,11... | collective-permute-start | bytes 1572872 | tf_op jit(solution)/shard_map/ppermute | solution.py:79
  32.2 2.0 %collective-permute-start.13 = (bf16[2,128,1024]{2,1,0:T(8,128)(2,1)S(1)}, bf16[2,128,1024]{2,1,0:T(8,128)(2,1)S(1)}, u32[]{:S(2)}, u32[]{:S(2)}) collective-permute-start(bf16[2,128,1024]{2,1,0:T(8,128)(2,1)S(1)} %pad_maximum_fusion.3), channel_id=1, source_target_pairs={{0,1},{1,0},{2,3},{3,2},{4,5},{5,4},{6,7},{7,6},{8,9},{9,8},{10,11... | collective-permute-start | bytes 1572872 | tf_op jit(solution)/shard_map/ppermute | solution.py:79
  34.2 4.6 %copy-start.1 = (bf16[8,256,1024]{2,1,0:T(8,128)(2,1)}, bf16[8,256,1024]{2,1,0:T(8,128)(2,1)S(1)}, u32[]{:S(2)}) copy-start(bf16[8,256,1024]{2,1,0:T(8,128)(2,1)S(1)} %maximum_dynamic-update-slice_fusion.3) | copy-start | bytes 12582916
  52.4 3.4 %copy-start = (f32[2048,512]{1,0:T(8,128)S(1)}, f32[2048,512]{1,0:T(8,128)}, u32[]{:S(2)}) copy-start(f32[2048,512]{1,0:T(8,128)} %get-tuple-element.22) | copy-start | bytes 12582916
  55.3 2.3 %copy-start.2 = (bf16[8,256,1024]{2,1,0:T(8,128)(2,1)S(1)}, bf16[8,256,1024]{2,1,0:T(8,128)(2,1)}, u32[]{:S(2)}) copy-start(bf16[8,256,1024]{2,1,0:T(8,128)(2,1)} %copy-done.1) | copy-start | bytes 12582916

commit v27 on v26

--- a/solution.py
+++ b/solution.py
@@ -97,7 +97,7 @@
         return cur
 
     parts = [None] + [
-        spread_x_first(piece) if sz == 1 else spread(pair_of(piece))
+        spread_x_first(piece) if sz in (1, 3) else spread(pair_of(piece))
         for sz, piece in enumerate(landed[1:], start=1)
     ]
 

time: 61.5 us -> 60.8 us (0.989)
    ppermute x4 -> x2, waiting for transfers between devices: 5.6 us -> 1.59 us  [spread(): other = lax.ppermute(cur, 'cent', [(i, i ^ bit) for i in range(n_c)])]
    ppermute x4, waiting for transfers between devices: 2.97 us -> 5.63 us  [pair_of(): lax.ppermute(piece, 'dp', [(j, (j + sy) % n_d) for j in range(n_d)])]
    ppermute x4 -> x2, starting transfers between devices: 3.07 us -> 1.25 us  [spread(): other = lax.ppermute(cur, 'cent', [(i, i ^ bit) for i in range(n_c)])]
    ppermute x1 -> x2, starting transfers between devices: 1.5 us -> 3.11 us  [spread_x_first(): other = lax.ppermute(piece, 'cent', [(i, i ^ order[0]) for i in range(n_c)])]
    ppermute x1 -> x2, waiting for transfers between devices: 0.01 us -> 0.8 us  [spread_x_first(): other = lax.ppermute(cur, 'cent', [(i, i ^ bit) for i in range(n_c)])]
    unnamed x9 -> x10, local copies, waits for them, and re-layouts: 1.31 us -> 1.32 us
where the time goes in v27:
time: 60.8 us; the launch traced here: 60.5 us
  starting transfers between devices  15.7 us (26%)
  waiting for transfers between devices  14.1 us (23%)
  blocking collectives  9.32 us (15%)
  other arithmetic  9.28 us (15%)
  matrix products  8.28 us (14%)
  local copies, waits for them, and re-layouts  3.51 us (6%)
    all_gather x1, blocking collectives, shards_all(): every = lax.all_gather(both, ('dp', 'cent'), axis=0)  9.32 us
    ppermute x3, waiting for transfers between devices, shards_all(): landed.append(lax.ppermute(mine, 'outer', pairs))  6.05 us
    ppermute x3, starting transfers between devices, shards_all(): landed.append(lax.ppermute(mine, 'outer', pairs))  5.68 us
    ppermute x4, waiting for transfers between devices, pair_of(): lax.ppermute(piece, 'dp', [(j, (j + sy) % n_d) for j in range(n_d)])  5.63 us
    ppermute x4, starting transfers between devices, pair_of(): lax.ppermute(piece, 'dp', [(j, (j + sy) % n_d) for j in range(n_d)])  5.48 us
    dot_general x1, matrix products, scores_for(): lax.dot_general(piece, cent_bf, (((1,), (1,)), ((), ())), preferred_eleme...  4.61 us
    dot_general x1, matrix products, shards_all(): lax.dot_general(scaled.reshape(n_o * pod, k), everything, (((0,), (0,)),...  3.67 us
    reduce_sum x1, other arithmetic, row_summary(): local_sum = jnp.sum(jnp.exp(logits - local_max[:, None]), axis=1)  3.31 us
  transfers between devices with their start and end apart: 14, of which 6 were waited for; matrix products, arithmetic and copies ran while one was open for 4% of the time, Pallas kernels for 0%

profile of v27, /device:TPU:0, one launch (start us, length us, event | category | flops | bytes accessed | tf_op | source)
XLA Modules:
  0.0 60.5 jit_solution(45136019983257250)
XLA Ops:
  0.0 0.0 copy-start.3
  0.0 1.2 %dynamic-slice_convert_fusion.1 = (bf16[64,1024]{1,0:T(8,128)(2,1)S(1)}, bf16[64,1024]{1,0:T(8,128)(2,1)S(1)}) fusion(f32[256,1024]{1,0:T(8,128)} %param.3, s32[]{:T(128)S(6)} %select_n.69, s32[]{:T(128)S(6)} %select_n.70), kind=kLoop, calls=%fused_computation.21 | loop fusion | bytes 524296 | tf_op jit(solution)/shard_map/convert_element_type | solution.py:69
  1.2 3.1 %collective-permute-start.2 = (bf16[64,1024]{1,0:T(8,128)(2,1)S(1)}, bf16[64,1024]{1,0:T(8,128)(2,1)S(1)}, u32[]{:S(2)}, u32[]{:S(2)}) collective-permute-start(bf16[64,1024]{1,0:T(8,128)(2,1)S(1)} %get-tuple-element.13), channel_id=1, source_target_pairs={{0,8},{8,0},{16,24},{24,16},{1,9},{9,1},{17,25},{25,17},{2,10},{10... | collective-permute-start | bytes 393224 | tf_op jit(solution)/shard_map/ppermute | solution.py:89
  4.3 2.6 %collective-permute-start.6 = (bf16[64,1024]{1,0:T(8,128)(2,1)S(1)}, bf16[64,1024]{1,0:T(8,128)(2,1)S(1)}, u32[]{:S(2)}, u32[]{:S(2)}) collective-permute-start(bf16[64,1024]{1,0:T(8,128)(2,1)S(1)} %get-tuple-element.13), channel_id=1, source_target_pairs={{0,16},{8,24},{16,0},{24,8},{1,17},{9,25},{17,1},{25,9},{2,18},{10... | collective-permute-start | bytes 393224 | tf_op jit(solution)/shard_map/ppermute | solution.py:89
  6.9 0.0 collective-permute-start.10
  6.9 0.1 fusion.9
  7.0 1.8 %collective-permute-start = (bf16[128,1024]{1,0:T(8,128)(2,1)S(1)}, bf16[128,1024]{1,0:T(8,128)(2,1)S(1)}, u32[]{:S(2)}, u32[]{:S(2)}) collective-permute-start(bf16[128,1024]{1,0:T(8,128)(2,1)S(1)} %get-tuple-element.16), channel_id=1, source_target_pairs={{0,4},{4,0},{1,5},{5,1},{2,6},{6,2},{3,7},{7,3},{8,12},{12,8},{9,1... | collective-permute-start | bytes 786440 | tf_op jit(solution)/shard_map/ppermute | solution.py:74
  8.8 0.7 %broadcast_xor_fusion = s32[4]{0:T(128)S(1)} fusion(s32[4]{0:T(128)} %constant.75.clone, s32[]{:T(128)S(6)} %axis_index.32), kind=kLoop, calls=%fused_computation.51 | loop fusion | flops 4 | bytes 36 | tf_op jit(solution)/shard_map/xor | solution.py:124
  9.4 0.1 iota_compare_fusion
  9.5 0.1 stack.92
  9.6 0.0 collective-permute-done.2
  9.6 1.6 %collective-permute-start.3 = (bf16[64,1024]{1,0:T(8,128)(2,1)S(1)}, bf16[64,1024]{1,0:T(8,128)(2,1)S(1)}, u32[]{:S(2)}, u32[]{:S(2)}) collective-permute-start(bf16[64,1024]{1,0:T(8,128)(2,1)S(1)} %collective-permute-done.2), channel_id=1, source_target_pairs={{0,2},{1,3},{2,0},{3,1},{4,6},{5,7},{6,4},{7,5},{8,10},{9,11},{10,... | collective-permute-start | bytes 393224 | tf_op jit(solution)/shard_map/ppermute | solution.py:92
  11.2 6.0 %collective-permute-done.6 = bf16[64,1024]{1,0:T(8,128)(2,1)S(1)} collective-permute-done((bf16[64,1024]{1,0:T(8,128)(2,1)S(1)}, bf16[64,1024]{1,0:T(8,128)(2,1)S(1)}, u32[]{:S(2)}, u32[]{:S(2)}) %collective-permute-start.6) | collective-permute-done | bytes 131104 | tf_op jit(solution)/shard_map/ppermute | solution.py:89
  17.2 1.5 %collective-permute-start.7 = (bf16[64,1024]{1,0:T(8,128)(2,1)S(1)}, bf16[64,1024]{1,0:T(8,128)(2,1)S(1)}, u32[]{:S(2)}, u32[]{:S(2)}) collective-permute-start(bf16[64,1024]{1,0:T(8,128)(2,1)S(1)} %collective-permute-done.6), channel_id=1, source_target_pairs={{0,4},{4,0},{1,5},{5,1},{2,6},{6,2},{3,7},{7,3},{8,12},{12,8},{9,1... | collective-permute-start | bytes 393224 | tf_op jit(solution)/shard_map/ppermute | solution.py:74
  18.8 0.0 collective-permute-done.10
  18.8 1.6 %collective-permute-start.11 = (bf16[64,1024]{1,0:T(8,128)(2,1)S(1)}, bf16[64,1024]{1,0:T(8,128)(2,1)S(1)}, u32[]{:S(2)}, u32[]{:S(2)}) collective-permute-start(bf16[64,1024]{1,0:T(8,128)(2,1)S(1)} %collective-permute-done.10), channel_id=1, source_target_pairs={{0,2},{1,3},{2,0},{3,1},{4,6},{5,7},{6,4},{7,5},{8,10},{9,11},{10,... | collective-permute-start | bytes 393224 | tf_op jit(solution)/shard_map/ppermute | solution.py:92
  20.3 0.0 collective-permute-done.3
  20.3 0.6 collective-permute-start.4
  20.9 2.8 %collective-permute-done.7 = bf16[64,1024]{1,0:T(8,128)(2,1)S(1)} collective-permute-done((bf16[64,1024]{1,0:T(8,128)(2,1)S(1)}, bf16[64,1024]{1,0:T(8,128)(2,1)S(1)}, u32[]{:S(2)}, u32[]{:S(2)}) %collective-permute-start.7) | collective-permute-done | bytes 131104 | tf_op jit(solution)/shard_map/ppermute | solution.py:74
  23.7 1.2 %collective-permute-start.8 = (bf16[2,64,1024]{2,1,0:T(8,128)(2,1)S(1)}, bf16[2,64,1024]{2,1,0:T(8,128)(2,1)S(1)}, u32[]{:S(2)}, u32[]{:S(2)}) collective-permute-start(bf16[2,64,1024]{2,1,0:T(8,128)(2,1)S(1)} %pad_maximum_fusion.5), channel_id=1, source_target_pairs={{0,2},{1,3},{2,0},{3,1},{4,6},{5,7},{6,4},{7,5},{8,10},{9,11},{10,... | collective-permute-start | bytes 786440 | tf_op jit(solution)/shard_map/ppermute | solution.py:79
  24.9 0.0 collective-permute-done.11
  24.9 1.6 %collective-permute-start.12 = (bf16[128,1024]{1,0:T(8,128)(2,1)S(1)}, bf16[128,1024]{1,0:T(8,128)(2,1)S(1)}, u32[]{:S(2)}, u32[]{:S(2)}) collective-permute-start(bf16[128,1024]{1,0:T(8,128)(2,1)S(1)} %constant_dynamic-update-slice_fusion.2), channel_id=1, source_target_pairs={{0,4},{4,0},{1,5},{5,1},{2,6},{6,2},{3,7},{7,3},{8,12},{12,8},{9,1... | collective-permute-start | bytes 786440 | tf_op jit(solution)/shard_map/ppermute | solution.py:74
  26.5 0.0 collective-permute-done
  26.5 0.1 pad_maximum_fusion
  26.5 0.1 collective-permute-start.1
  26.6 1.8 %collective-permute-done.4 = bf16[128,1024]{1,0:T(8,128)(2,1)S(1)} collective-permute-done((bf16[128,1024]{1,0:T(8,128)(2,1)S(1)}, bf16[128,1024]{1,0:T(8,128)(2,1)S(1)}, u32[]{:S(2)}, u32[]{:S(2)}) %collective-permute-start.4) | collective-permute-done | bytes 262176 | tf_op jit(solution)/shard_map/ppermute | solution.py:74
  28.4 0.1 pad_maximum_fusion.1
  28.5 0.1 collective-permute-start.5
  28.6 1.6 %collective-permute-done.8 = bf16[2,64,1024]{2,1,0:T(8,128)(2,1)S(1)} collective-permute-done((bf16[2,64,1024]{2,1,0:T(8,128)(2,1)S(1)}, bf16[2,64,1024]{2,1,0:T(8,128)(2,1)S(1)}, u32[]{:S(2)}, u32[]{:S(2)}) %collective-permute-start.8) | collective-permute-done | bytes 262176 | tf_op jit(solution)/shard_map/ppermute | solution.py:79
  30.2 0.1 collective-permute-start.9
  30.3 1.1 %collective-permute-done.12 = bf16[128,1024]{1,0:T(8,128)(2,1)S(1)} collective-permute-done((bf16[128,1024]{1,0:T(8,128)(2,1)S(1)}, bf16[128,1024]{1,0:T(8,128)(2,1)S(1)}, u32[]{:S(2)}, u32[]{:S(2)}) %collective-permute-start.12) | collective-permute-done | bytes 262176 | tf_op jit(solution)/shard_map/ppermute | solution.py:74
  31.3 0.1 pad_maximum_fusion.3
  31.4 0.1 collective-permute-start.13
  31.5 0.0 copy-done.3
  31.5 0.2 multiply_reduce_fusion
  31.7 0.0 collective-permute-done.1
  31.7 0.5 broadcast_in_dim.138
  32.2 0.1 maximum_dynamic-update-slice_fusion
  32.3 0.0 collective-permute-done.5
  32.4 0.1 maximum_dynamic-update-slice_fusion.1
  32.5 0.0 collective-permute-done.9
  32.5 0.1 maximum_dynamic-update-slice_fusion.2
  32.6 0.8 %collective-permute-done.13 = bf16[2,128,1024]{2,1,0:T(8,128)(2,1)S(1)} collective-permute-done((bf16[2,128,1024]{2,1,0:T(8,128)(2,1)S(1)}, bf16[2,128,1024]{2,1,0:T(8,128)(2,1)S(1)}, u32[]{:S(2)}, u32[]{:S(2)}) %collective-permute-start.13) | collective-permute-done | bytes 524320 | tf_op jit(solution)/shard_map/ppermute | solution.py:95
  33.4 0.1 maximum_dynamic-update-slice_fusion.3
  33.5 0.0 copy-start.1
  33.5 4.6 %fusion.11 = (f32[2048]{0:T(1024)S(1)}, f32[2048,512]{1,0:T(8,128)}) fusion(f32[512]{0:T(512)S(1)} %multiply_reduce_fusion, bf16[2048,1024]{1,0:T(8,128)(2,1)S(1)} %bitcast.51, f32[512,1024]{1,0:T(8,128)S(1)} %copy-done.3), kind=kOutput, calls=%fused_computation.54 | convolution fusion | flops 2152200192 | bytes 10496000 | tf_op jit(solution)/shard_map/dot_general | solution.py:10
  38.1 0.0 copy-done.1
  38.1 0.1 broadcast_in_dim.141
  38.2 3.3 %exponential_reduce_fusion = f32[2048]{0:T(1024)S(1)} fusion(f32[2048,512]{1,0:T(8,128)} %get-tuple-element.22, f32[2048]{0:T(1024)S(1)} %get-tuple-element.21), kind=kLoop, calls=%fused_computation.4 | loop fusion | flops 2095104 | bytes 4210688 | tf_op jit(solution)/shard_map/reduce_sum | solution.py:18
  41.5 0.1 broadcast_in_dim.146
  41.6 0.1 select_reduce_fusion.7
  41.7 0.2 select_reduce_fusion.3
  41.9 9.3 %all-gather = f32[16,8,4,64]{3,1,2,0:T(8,128)S(1)} all-gather(f32[2,8,4,64]{3,1,2,0:T(8,128)S(1)} %copy.27), channel_id=2, replica_groups=mesh['outer'=4,'dp'=2,'cent'=4] {'dp','cent'}, dimensions={0}, use_global_device_ids=true | all-gather | bytes 147456 | tf_op jit(solution)/shard_map/all_gather | solution.py:139
  51.3 0.1 select_reduce_fusion.1
  51.4 0.1 select_reduce_fusion.5
  51.5 0.1 div.55
  51.6 0.1 sub.48
  51.7 0.0 copy-start
  51.7 2.8 %bitcast_reduce_fusion = f32[4,512]{1,0:T(4,128)S(1)} fusion(f32[2048]{0:T(1024)S(1)} %div.55, f32[2048,512]{1,0:T(8,128)} %get-tuple-element.22, f32[2048]{0:T(1024)S(1)} %sub.48), kind=kLoop, calls=%fused_computation.2 | loop fusion | flops 5240832 | bytes 4218880 | tf_op jit(solution)/shard_map/reduce_sum | solution.py:150
  54.5 0.0 copy-start.2
  54.6 0.6 copy-done
  55.1 1.0 %fusion = bf16[2048,512]{1,0:T(8,128)(2,1)S(1)} fusion(f32[4,512]{1,0:T(4,128)S(1)} %broadcast_add_fusion, f32[2048]{0:T(1024)S(1)} %div.55, f32[2048,512]{1,0:T(8,128)S(1)} %copy-done, f32[2048]{0:T(1024)S(1)} %sub.48), kind=kLoop, calls=%fused_computation.1 | loop fusion | flops 6291456 | bytes 6316032 | tf_op jit(solution)/shard_map/convert_element_type | solution.py:151
  56.1 0.7 %copy-done.2 = bf16[8,256,1024]{2,1,0:T(8,128)(2,1)S(1)} copy-done((bf16[8,256,1024]{2,1,0:T(8,128)(2,1)S(1)}, bf16[8,256,1024]{2,1,0:T(8,128)(2,1)}, u32[]{:S(2)}) %copy-start.2) | copy-done | bytes 4194328
  56.9 3.7 %subtract_multiply_fusion.1 = f32[512,1024]{1,0:T(8,128)} fusion(f32[512,1024]{1,0:T(8,128)S(1)} %copy-done.3, bf16[2048,512]{1,0:T(8,128)(2,1)S(1)} %fusion, bf16[2048,1024]{1,0:T(8,128)(2,1)S(1)} %bitcast.52, f32[512]{0:T(512)S(1)} %fusion.8), kind=kOutput, calls=%fused_computation.7 | convolution fusion | flops 2149056512 | bytes 10487808 | tf_op jit(solution)/shard_map/dot_general | solution.py:152
  (20 shorter events, 0.2 us)
Async XLA Ops:
  0.0 31.5 %copy-start.3 = (f32[512,1024]{1,0:T(8,128)S(1)}, f32[512,1024]{1,0:T(8,128)}, u32[]{:S(2)}) copy-start(f32[512,1024]{1,0:T(8,128)} %param.4) | copy-start | bytes 6291460
  1.2 8.4 %collective-permute-start.2 = (bf16[64,1024]{1,0:T(8,128)(2,1)S(1)}, bf16[64,1024]{1,0:T(8,128)(2,1)S(1)}, u32[]{:S(2)}, u32[]{:S(2)}) collective-permute-start(bf16[64,1024]{1,0:T(8,128)(2,1)S(1)} %get-tuple-element.13), channel_id=1, source_target_pairs={{0,8},{8,0},{16,24},{24,16},{1,9},{9,1},{17,25},{25,17},{2,10},{10... | collective-permute-start | bytes 393224 | tf_op jit(solution)/shard_map/ppermute | solution.py:89
  4.3 12.9 %collective-permute-start.6 = (bf16[64,1024]{1,0:T(8,128)(2,1)S(1)}, bf16[64,1024]{1,0:T(8,128)(2,1)S(1)}, u32[]{:S(2)}, u32[]{:S(2)}) collective-permute-start(bf16[64,1024]{1,0:T(8,128)(2,1)S(1)} %get-tuple-element.13), channel_id=1, source_target_pairs={{0,16},{8,24},{16,0},{24,8},{1,17},{9,25},{17,1},{25,9},{2,18},{10... | collective-permute-start | bytes 393224 | tf_op jit(solution)/shard_map/ppermute | solution.py:89
  6.9 11.9 %collective-permute-start.10 = (bf16[64,1024]{1,0:T(8,128)(2,1)S(1)}, bf16[64,1024]{1,0:T(8,128)(2,1)S(1)}, u32[]{:S(2)}, u32[]{:S(2)}) collective-permute-start(bf16[64,1024]{1,0:T(8,128)(2,1)S(1)} %get-tuple-element.13), channel_id=1, source_target_pairs={{0,24},{8,16},{16,8},{24,0},{1,25},{9,17},{17,9},{25,1},{2,26},{10... | collective-permute-start | bytes 393224 | tf_op jit(solution)/shard_map/ppermute | solution.py:89
  7.0 19.5 %collective-permute-start = (bf16[128,1024]{1,0:T(8,128)(2,1)S(1)}, bf16[128,1024]{1,0:T(8,128)(2,1)S(1)}, u32[]{:S(2)}, u32[]{:S(2)}) collective-permute-start(bf16[128,1024]{1,0:T(8,128)(2,1)S(1)} %get-tuple-element.16), channel_id=1, source_target_pairs={{0,4},{4,0},{1,5},{5,1},{2,6},{6,2},{3,7},{7,3},{8,12},{12,8},{9,1... | collective-permute-start | bytes 786440 | tf_op jit(solution)/shard_map/ppermute | solution.py:74
  9.6 10.7 %collective-permute-start.3 = (bf16[64,1024]{1,0:T(8,128)(2,1)S(1)}, bf16[64,1024]{1,0:T(8,128)(2,1)S(1)}, u32[]{:S(2)}, u32[]{:S(2)}) collective-permute-start(bf16[64,1024]{1,0:T(8,128)(2,1)S(1)} %collective-permute-done.2), channel_id=1, source_target_pairs={{0,2},{1,3},{2,0},{3,1},{4,6},{5,7},{6,4},{7,5},{8,10},{9,11},{10,... | collective-permute-start | bytes 393224 | tf_op jit(solution)/shard_map/ppermute | solution.py:92
  17.2 6.4 %collective-permute-start.7 = (bf16[64,1024]{1,0:T(8,128)(2,1)S(1)}, bf16[64,1024]{1,0:T(8,128)(2,1)S(1)}, u32[]{:S(2)}, u32[]{:S(2)}) collective-permute-start(bf16[64,1024]{1,0:T(8,128)(2,1)S(1)} %collective-permute-done.6), channel_id=1, source_target_pairs={{0,4},{4,0},{1,5},{5,1},{2,6},{6,2},{3,7},{7,3},{8,12},{12,8},{9,1... | collective-permute-start | bytes 393224 | tf_op jit(solution)/shard_map/ppermute | solution.py:74
  18.8 6.1 %collective-permute-start.11 = (bf16[64,1024]{1,0:T(8,128)(2,1)S(1)}, bf16[64,1024]{1,0:T(8,128)(2,1)S(1)}, u32[]{:S(2)}, u32[]{:S(2)}) collective-permute-start(bf16[64,1024]{1,0:T(8,128)(2,1)S(1)} %collective-permute-done.10), channel_id=1, source_target_pairs={{0,2},{1,3},{2,0},{3,1},{4,6},{5,7},{6,4},{7,5},{8,10},{9,11},{10,... | collective-permute-start | bytes 393224 | tf_op jit(solution)/shard_map/ppermute | solution.py:92
  20.3 8.1 %collective-permute-start.4 = (bf16[128,1024]{1,0:T(8,128)(2,1)S(1)}, bf16[128,1024]{1,0:T(8,128)(2,1)S(1)}, u32[]{:S(2)}, u32[]{:S(2)}) collective-permute-start(bf16[128,1024]{1,0:T(8,128)(2,1)S(1)} %constant_dynamic-update-slice_fusion), channel_id=1, source_target_pairs={{0,4},{4,0},{1,5},{5,1},{2,6},{6,2},{3,7},{7,3},{8,12},{12,8},{9,1... | collective-permute-start | bytes 786440 | tf_op jit(solution)/shard_map/ppermute | solution.py:74
  23.7 6.4 %collective-permute-start.8 = (bf16[2,64,1024]{2,1,0:T(8,128)(2,1)S(1)}, bf16[2,64,1024]{2,1,0:T(8,128)(2,1)S(1)}, u32[]{:S(2)}, u32[]{:S(2)}) collective-permute-start(bf16[2,64,1024]{2,1,0:T(8,128)(2,1)S(1)} %pad_maximum_fusion.5), channel_id=1, source_target_pairs={{0,2},{1,3},{2,0},{3,1},{4,6},{5,7},{6,4},{7,5},{8,10},{9,11},{10,... | collective-permute-start | bytes 786440 | tf_op jit(solution)/shard_map/ppermute | solution.py:79
  24.9 6.4 %collective-permute-start.12 = (bf16[128,1024]{1,0:T(8,128)(2,1)S(1)}, bf16[128,1024]{1,0:T(8,128)(2,1)S(1)}, u32[]{:S(2)}, u32[]{:S(2)}) collective-permute-start(bf16[128,1024]{1,0:T(8,128)(2,1)S(1)} %constant_dynamic-update-slice_fusion.2), channel_id=1, source_target_pairs={{0,4},{4,0},{1,5},{5,1},{2,6},{6,2},{3,7},{7,3},{8,12},{12,8},{9,1... | collective-permute-start | bytes 786440 | tf_op jit(solution)/shard_map/ppermute | solution.py:74
  26.5 5.2 %collective-permute-start.1 = (bf16[2,128,1024]{2,1,0:T(8,128)(2,1)S(1)}, bf16[2,128,1024]{2,1,0:T(8,128)(2,1)S(1)}, u32[]{:S(2)}, u32[]{:S(2)}) collective-permute-start(bf16[2,128,1024]{2,1,0:T(8,128)(2,1)S(1)} %pad_maximum_fusion), channel_id=1, source_target_pairs={{0,1},{1,0},{2,3},{3,2},{4,5},{5,4},{6,7},{7,6},{8,9},{9,8},{10,11... | collective-permute-start | bytes 1572872 | tf_op jit(solution)/shard_map/ppermute | solution.py:108
  28.5 3.9 %collective-permute-start.5 = (bf16[2,128,1024]{2,1,0:T(8,128)(2,1)S(1)}, bf16[2,128,1024]{2,1,0:T(8,128)(2,1)S(1)}, u32[]{:S(2)}, u32[]{:S(2)}) collective-permute-start(bf16[2,128,1024]{2,1,0:T(8,128)(2,1)S(1)} %pad_maximum_fusion.1), channel_id=1, source_target_pairs={{0,1},{1,0},{2,3},{3,2},{4,5},{5,4},{6,7},{7,6},{8,9},{9,8},{10,11... | collective-permute-start | bytes 1572872 | tf_op jit(solution)/shard_map/ppermute | solution.py:95
  30.2 2.3 %collective-permute-start.9 = (bf16[2,128,1024]{2,1,0:T(8,128)(2,1)S(1)}, bf16[2,128,1024]{2,1,0:T(8,128)(2,1)S(1)}, u32[]{:S(2)}, u32[]{:S(2)}) collective-permute-start(bf16[2,128,1024]{2,1,0:T(8,128)(2,1)S(1)} %pad_maximum_fusion.2), channel_id=1, source_target_pairs={{0,1},{1,0},{2,3},{3,2},{4,5},{5,4},{6,7},{7,6},{8,9},{9,8},{10,11... | collective-permute-start | bytes 1572872 | tf_op jit(solution)/shard_map/ppermute | solution.py:79
  31.4 2.0 %collective-permute-start.13 = (bf16[2,128,1024]{2,1,0:T(8,128)(2,1)S(1)}, bf16[2,128,1024]{2,1,0:T(8,128)(2,1)S(1)}, u32[]{:S(2)}, u32[]{:S(2)}) collective-permute-start(bf16[2,128,1024]{2,1,0:T(8,128)(2,1)S(1)} %pad_maximum_fusion.3), channel_id=1, source_target_pairs={{0,1},{1,0},{2,3},{3,2},{4,5},{5,4},{6,7},{7,6},{8,9},{9,8},{10,11... | collective-permute-start | bytes 1572872 | tf_op jit(solution)/shard_map/ppermute | solution.py:95
  33.5 4.6 %copy-start.1 = (bf16[8,256,1024]{2,1,0:T(8,128)(2,1)}, bf16[8,256,1024]{2,1,0:T(8,128)(2,1)S(1)}, u32[]{:S(2)}) copy-start(bf16[8,256,1024]{2,1,0:T(8,128)(2,1)S(1)} %maximum_dynamic-update-slice_fusion.3) | copy-start | bytes 12582916
  51.7 3.4 %copy-start = (f32[2048,512]{1,0:T(8,128)S(1)}, f32[2048,512]{1,0:T(8,128)}, u32[]{:S(2)}) copy-start(f32[2048,512]{1,0:T(8,128)} %get-tuple-element.22) | copy-start | bytes 12582916
  54.5 2.3 %copy-start.2 = (bf16[8,256,1024]{2,1,0:T(8,128)(2,1)S(1)}, bf16[8,256,1024]{2,1,0:T(8,128)(2,1)}, u32[]{:S(2)}) copy-start(bf16[8,256,1024]{2,1,0:T(8,128)(2,1)} %copy-done.1) | copy-start | bytes 12582916

commit v28 on v27

--- a/solution.py
+++ b/solution.py
@@ -97,7 +97,7 @@
         return cur
 
     parts = [None] + [
-        spread_x_first(piece) if sz in (1, 3) else spread(pair_of(piece))
+        spread_x_first(piece) if sz in (2, 3) else spread(pair_of(piece))
         for sz, piece in enumerate(landed[1:], start=1)
     ]
 

time: 60.8 us -> 61.6 us (1.013)
    ppermute x2, waiting for transfers between devices: 0.01 us -> 1.9 us  [spread_x_first(): other = lax.ppermute(piece, 'cent', [(i, i ^ order[0]) for i in range(n_c)])]
    ppermute x2, starting transfers between devices: 3.11 us -> 2.16 us  [spread_x_first(): other = lax.ppermute(piece, 'cent', [(i, i ^ order[0]) for i in range(n_c)])]
    ppermute x4, waiting for transfers between devices: 5.63 us -> 4.8 us  [pair_of(): lax.ppermute(piece, 'dp', [(j, (j + sy) % n_d) for j in range(n_d)])]
    ppermute x4, starting transfers between devices: 5.48 us -> 6.23 us  [pair_of(): lax.ppermute(piece, 'dp', [(j, (j + sy) % n_d) for j in range(n_d)])]
where the time goes in v28:
time: 61.6 us; the launch traced here: 61.4 us
  starting transfers between devices  15.9 us (26%)
  waiting for transfers between devices  14.7 us (24%)
  blocking collectives  9.32 us (15%)
  other arithmetic  9.28 us (15%)
  matrix products  8.29 us (13%)
  local copies, waits for them, and re-layouts  3.51 us (6%)
    all_gather x1, blocking collectives, shards_all(): every = lax.all_gather(both, ('dp', 'cent'), axis=0)  9.32 us
    ppermute x4, starting transfers between devices, pair_of(): lax.ppermute(piece, 'dp', [(j, (j + sy) % n_d) for j in range(n_d)])  6.23 us
    ppermute x3, waiting for transfers between devices, shards_all(): landed.append(lax.ppermute(mine, 'outer', pairs))  6.16 us
    ppermute x3, starting transfers between devices, shards_all(): landed.append(lax.ppermute(mine, 'outer', pairs))  5.68 us
    ppermute x4, waiting for transfers between devices, pair_of(): lax.ppermute(piece, 'dp', [(j, (j + sy) % n_d) for j in range(n_d)])  4.8 us
    dot_general x1, matrix products, scores_for(): lax.dot_general(piece, cent_bf, (((1,), (1,)), ((), ())), preferred_eleme...  4.62 us
    dot_general x1, matrix products, shards_all(): lax.dot_general(scaled.reshape(n_o * pod, k), everything, (((0,), (0,)),...  3.67 us
    reduce_sum x1, other arithmetic, row_summary(): local_sum = jnp.sum(jnp.exp(logits - local_max[:, None]), axis=1)  3.31 us
  transfers between devices with their start and end apart: 14, of which 6 were waited for; matrix products, arithmetic and copies ran while one was open for 4% of the time, Pallas kernels for 0%

profile of v28, /device:TPU:0, one launch (start us, length us, event | category | flops | bytes accessed | tf_op | source)
XLA Modules:
  0.0 61.4 jit_solution(9126992947665010765)
XLA Ops:
  0.0 0.0 copy-start.3
  0.0 1.2 %dynamic-slice_convert_fusion.1 = (bf16[64,1024]{1,0:T(8,128)(2,1)S(1)}, bf16[64,1024]{1,0:T(8,128)(2,1)S(1)}) fusion(f32[256,1024]{1,0:T(8,128)} %param.3, s32[]{:T(128)S(6)} %select_n.69, s32[]{:T(128)S(6)} %select_n.70), kind=kLoop, calls=%fused_computation.21 | loop fusion | bytes 524296 | tf_op jit(solution)/shard_map/convert_element_type | solution.py:69
  1.2 3.1 %collective-permute-start.2 = (bf16[64,1024]{1,0:T(8,128)(2,1)S(1)}, bf16[64,1024]{1,0:T(8,128)(2,1)S(1)}, u32[]{:S(2)}, u32[]{:S(2)}) collective-permute-start(bf16[64,1024]{1,0:T(8,128)(2,1)S(1)} %get-tuple-element.13), channel_id=1, source_target_pairs={{0,8},{8,0},{16,24},{24,16},{1,9},{9,1},{17,25},{25,17},{2,10},{10... | collective-permute-start | bytes 393224 | tf_op jit(solution)/shard_map/ppermute | solution.py:89
  4.3 2.6 %collective-permute-start.6 = (bf16[64,1024]{1,0:T(8,128)(2,1)S(1)}, bf16[64,1024]{1,0:T(8,128)(2,1)S(1)}, u32[]{:S(2)}, u32[]{:S(2)}) collective-permute-start(bf16[64,1024]{1,0:T(8,128)(2,1)S(1)} %get-tuple-element.13), channel_id=1, source_target_pairs={{0,16},{8,24},{16,0},{24,8},{1,17},{9,25},{17,1},{25,9},{2,18},{10... | collective-permute-start | bytes 393224 | tf_op jit(solution)/shard_map/ppermute | solution.py:89
  6.9 0.0 collective-permute-start.10
  6.9 0.1 fusion.9
  7.0 1.8 %collective-permute-start = (bf16[128,1024]{1,0:T(8,128)(2,1)S(1)}, bf16[128,1024]{1,0:T(8,128)(2,1)S(1)}, u32[]{:S(2)}, u32[]{:S(2)}) collective-permute-start(bf16[128,1024]{1,0:T(8,128)(2,1)S(1)} %get-tuple-element.16), channel_id=1, source_target_pairs={{0,4},{4,0},{1,5},{5,1},{2,6},{6,2},{3,7},{7,3},{8,12},{12,8},{9,1... | collective-permute-start | bytes 786440 | tf_op jit(solution)/shard_map/ppermute | solution.py:74
  8.8 0.7 %broadcast_xor_fusion = s32[4]{0:T(128)S(1)} fusion(s32[4]{0:T(128)} %constant.75.clone, s32[]{:T(128)S(6)} %axis_index.32), kind=kLoop, calls=%fused_computation.51 | loop fusion | flops 4 | bytes 36 | tf_op jit(solution)/shard_map/xor | solution.py:124
  9.4 0.1 iota_compare_fusion
  9.5 0.1 stack.92
  9.6 0.0 collective-permute-done.2
  9.6 1.5 %collective-permute-start.3 = (bf16[64,1024]{1,0:T(8,128)(2,1)S(1)}, bf16[64,1024]{1,0:T(8,128)(2,1)S(1)}, u32[]{:S(2)}, u32[]{:S(2)}) collective-permute-start(bf16[64,1024]{1,0:T(8,128)(2,1)S(1)} %collective-permute-done.2), channel_id=1, source_target_pairs={{0,4},{4,0},{1,5},{5,1},{2,6},{6,2},{3,7},{7,3},{8,12},{12,8},{9,1... | collective-permute-start | bytes 393224 | tf_op jit(solution)/shard_map/ppermute | solution.py:74
  11.1 6.2 %collective-permute-done.6 = bf16[64,1024]{1,0:T(8,128)(2,1)S(1)} collective-permute-done((bf16[64,1024]{1,0:T(8,128)(2,1)S(1)}, bf16[64,1024]{1,0:T(8,128)(2,1)S(1)}, u32[]{:S(2)}, u32[]{:S(2)}) %collective-permute-start.6) | collective-permute-done | bytes 131104 | tf_op jit(solution)/shard_map/ppermute | solution.py:89
  17.2 1.6 %collective-permute-start.7 = (bf16[64,1024]{1,0:T(8,128)(2,1)S(1)}, bf16[64,1024]{1,0:T(8,128)(2,1)S(1)}, u32[]{:S(2)}, u32[]{:S(2)}) collective-permute-start(bf16[64,1024]{1,0:T(8,128)(2,1)S(1)} %collective-permute-done.6), channel_id=1, source_target_pairs={{0,2},{1,3},{2,0},{3,1},{4,6},{5,7},{6,4},{7,5},{8,10},{9,11},{10,... | collective-permute-start | bytes 393224 | tf_op jit(solution)/shard_map/ppermute | solution.py:92
  18.8 0.0 collective-permute-done.10
  18.8 0.6 collective-permute-start.11
  19.4 0.0 collective-permute-done.3
  19.5 1.6 %collective-permute-start.4 = (bf16[2,64,1024]{2,1,0:T(8,128)(2,1)S(1)}, bf16[2,64,1024]{2,1,0:T(8,128)(2,1)S(1)}, u32[]{:S(2)}, u32[]{:S(2)}) collective-permute-start(bf16[2,64,1024]{2,1,0:T(8,128)(2,1)S(1)} %pad_maximum_fusion.5), channel_id=1, source_target_pairs={{0,2},{1,3},{2,0},{3,1},{4,6},{5,7},{6,4},{7,5},{8,10},{9,11},{10,... | collective-permute-start | bytes 786440 | tf_op jit(solution)/shard_map/ppermute | solution.py:79
  21.0 1.9 %collective-permute-done.7 = bf16[64,1024]{1,0:T(8,128)(2,1)S(1)} collective-permute-done((bf16[64,1024]{1,0:T(8,128)(2,1)S(1)}, bf16[64,1024]{1,0:T(8,128)(2,1)S(1)}, u32[]{:S(2)}, u32[]{:S(2)}) %collective-permute-start.7) | collective-permute-done | bytes 131104 | tf_op jit(solution)/shard_map/ppermute | solution.py:92
  22.9 1.6 %collective-permute-start.8 = (bf16[128,1024]{1,0:T(8,128)(2,1)S(1)}, bf16[128,1024]{1,0:T(8,128)(2,1)S(1)}, u32[]{:S(2)}, u32[]{:S(2)}) collective-permute-start(bf16[128,1024]{1,0:T(8,128)(2,1)S(1)} %constant_dynamic-update-slice_fusion), channel_id=1, source_target_pairs={{0,4},{4,0},{1,5},{5,1},{2,6},{6,2},{3,7},{7,3},{8,12},{12,8},{9,1... | collective-permute-start | bytes 786440 | tf_op jit(solution)/shard_map/ppermute | solution.py:74
  24.5 0.0 collective-permute-done.11
  24.5 1.4 %collective-permute-start.12 = (bf16[128,1024]{1,0:T(8,128)(2,1)S(1)}, bf16[128,1024]{1,0:T(8,128)(2,1)S(1)}, u32[]{:S(2)}, u32[]{:S(2)}) collective-permute-start(bf16[128,1024]{1,0:T(8,128)(2,1)S(1)} %constant_dynamic-update-slice_fusion.2), channel_id=1, source_target_pairs={{0,4},{4,0},{1,5},{5,1},{2,6},{6,2},{3,7},{7,3},{8,12},{12,8},{9,1... | collective-permute-start | bytes 786440 | tf_op jit(solution)/shard_map/ppermute | solution.py:74
  25.9 0.0 collective-permute-done
  25.9 0.1 pad_maximum_fusion
  26.0 0.1 collective-permute-start.1
  26.1 1.1 %collective-permute-done.4 = bf16[2,64,1024]{2,1,0:T(8,128)(2,1)S(1)} collective-permute-done((bf16[2,64,1024]{2,1,0:T(8,128)(2,1)S(1)}, bf16[2,64,1024]{2,1,0:T(8,128)(2,1)S(1)}, u32[]{:S(2)}, u32[]{:S(2)}) %collective-permute-start.4) | collective-permute-done | bytes 262176 | tf_op jit(solution)/shard_map/ppermute | solution.py:79
  27.2 0.1 collective-permute-start.5
  27.2 2.1 %collective-permute-done.8 = bf16[128,1024]{1,0:T(8,128)(2,1)S(1)} collective-permute-done((bf16[128,1024]{1,0:T(8,128)(2,1)S(1)}, bf16[128,1024]{1,0:T(8,128)(2,1)S(1)}, u32[]{:S(2)}, u32[]{:S(2)}) %collective-permute-start.8) | collective-permute-done | bytes 262176 | tf_op jit(solution)/shard_map/ppermute | solution.py:74
  29.4 0.1 pad_maximum_fusion.2
  29.4 0.1 collective-permute-start.9
  29.5 2.7 %collective-permute-done.12 = bf16[128,1024]{1,0:T(8,128)(2,1)S(1)} collective-permute-done((bf16[128,1024]{1,0:T(8,128)(2,1)S(1)}, bf16[128,1024]{1,0:T(8,128)(2,1)S(1)}, u32[]{:S(2)}, u32[]{:S(2)}) %collective-permute-start.12) | collective-permute-done | bytes 262176 | tf_op jit(solution)/shard_map/ppermute | solution.py:74
  32.2 0.1 pad_maximum_fusion.3
  32.2 0.1 collective-permute-start.13
  32.3 0.0 copy-done.3
  32.3 0.2 multiply_reduce_fusion
  32.5 0.0 collective-permute-done.1
  32.5 0.5 broadcast_in_dim.138
  33.1 0.1 maximum_dynamic-update-slice_fusion
  33.2 0.0 collective-permute-done.5
  33.2 0.1 maximum_dynamic-update-slice_fusion.1
  33.3 0.0 collective-permute-done.9
  33.3 0.1 maximum_dynamic-update-slice_fusion.2
  33.4 0.8 %collective-permute-done.13 = bf16[2,128,1024]{2,1,0:T(8,128)(2,1)S(1)} collective-permute-done((bf16[2,128,1024]{2,1,0:T(8,128)(2,1)S(1)}, bf16[2,128,1024]{2,1,0:T(8,128)(2,1)S(1)}, u32[]{:S(2)}, u32[]{:S(2)}) %collective-permute-start.13) | collective-permute-done | bytes 524320 | tf_op jit(solution)/shard_map/ppermute | solution.py:95
  34.2 0.1 maximum_dynamic-update-slice_fusion.3
  34.3 0.0 copy-start.1
  34.3 4.6 %fusion.11 = (f32[2048]{0:T(1024)S(1)}, f32[2048,512]{1,0:T(8,128)}) fusion(f32[512]{0:T(512)S(1)} %multiply_reduce_fusion, bf16[2048,1024]{1,0:T(8,128)(2,1)S(1)} %bitcast.51, f32[512,1024]{1,0:T(8,128)S(1)} %copy-done.3), kind=kOutput, calls=%fused_computation.54 | convolution fusion | flops 2152200192 | bytes 10496000 | tf_op jit(solution)/shard_map/dot_general | solution.py:10
  38.9 0.0 copy-done.1
  38.9 0.1 broadcast_in_dim.141
  39.0 3.3 %exponential_reduce_fusion = f32[2048]{0:T(1024)S(1)} fusion(f32[2048,512]{1,0:T(8,128)} %get-tuple-element.22, f32[2048]{0:T(1024)S(1)} %get-tuple-element.21), kind=kLoop, calls=%fused_computation.4 | loop fusion | flops 2095104 | bytes 4210688 | tf_op jit(solution)/shard_map/reduce_sum | solution.py:18
  42.3 0.1 broadcast_in_dim.146
  42.4 0.1 select_reduce_fusion.7
  42.5 0.2 select_reduce_fusion.3
  42.7 9.3 %all-gather = f32[16,8,4,64]{3,1,2,0:T(8,128)S(1)} all-gather(f32[2,8,4,64]{3,1,2,0:T(8,128)S(1)} %copy.27), channel_id=2, replica_groups=mesh['outer'=4,'dp'=2,'cent'=4] {'dp','cent'}, dimensions={0}, use_global_device_ids=true | all-gather | bytes 147456 | tf_op jit(solution)/shard_map/all_gather | solution.py:139
  52.1 0.1 select_reduce_fusion.1
  52.2 0.1 select_reduce_fusion.5
  52.3 0.1 div.55
  52.4 0.1 sub.48
  52.5 0.0 copy-start
  52.5 2.8 %bitcast_reduce_fusion = f32[4,512]{1,0:T(4,128)S(1)} fusion(f32[2048]{0:T(1024)S(1)} %div.55, f32[2048,512]{1,0:T(8,128)} %get-tuple-element.22, f32[2048]{0:T(1024)S(1)} %sub.48), kind=kLoop, calls=%fused_computation.2 | loop fusion | flops 5240832 | bytes 4218880 | tf_op jit(solution)/shard_map/reduce_sum | solution.py:150
  55.4 0.0 copy-start.2
  55.4 0.6 copy-done
  56.0 1.0 %fusion = bf16[2048,512]{1,0:T(8,128)(2,1)S(1)} fusion(f32[4,512]{1,0:T(4,128)S(1)} %broadcast_add_fusion, f32[2048]{0:T(1024)S(1)} %div.55, f32[2048,512]{1,0:T(8,128)S(1)} %copy-done, f32[2048]{0:T(1024)S(1)} %sub.48), kind=kLoop, calls=%fused_computation.1 | loop fusion | flops 6291456 | bytes 6316032 | tf_op jit(solution)/shard_map/convert_element_type | solution.py:151
  57.0 0.7 %copy-done.2 = bf16[8,256,1024]{2,1,0:T(8,128)(2,1)S(1)} copy-done((bf16[8,256,1024]{2,1,0:T(8,128)(2,1)S(1)}, bf16[8,256,1024]{2,1,0:T(8,128)(2,1)}, u32[]{:S(2)}) %copy-start.2) | copy-done | bytes 4194328
  57.7 3.7 %subtract_multiply_fusion.1 = f32[512,1024]{1,0:T(8,128)} fusion(f32[512,1024]{1,0:T(8,128)S(1)} %copy-done.3, bf16[2048,512]{1,0:T(8,128)(2,1)S(1)} %fusion, bf16[2048,1024]{1,0:T(8,128)(2,1)S(1)} %bitcast.52, f32[512]{0:T(512)S(1)} %fusion.8), kind=kOutput, calls=%fused_computation.7 | convolution fusion | flops 2149056512 | bytes 10487808 | tf_op jit(solution)/shard_map/dot_general | solution.py:152
  (20 shorter events, 0.2 us)
Async XLA Ops:
  0.0 32.3 %copy-start.3 = (f32[512,1024]{1,0:T(8,128)S(1)}, f32[512,1024]{1,0:T(8,128)}, u32[]{:S(2)}) copy-start(f32[512,1024]{1,0:T(8,128)} %param.4) | copy-start | bytes 6291460
  1.2 8.4 %collective-permute-start.2 = (bf16[64,1024]{1,0:T(8,128)(2,1)S(1)}, bf16[64,1024]{1,0:T(8,128)(2,1)S(1)}, u32[]{:S(2)}, u32[]{:S(2)}) collective-permute-start(bf16[64,1024]{1,0:T(8,128)(2,1)S(1)} %get-tuple-element.13), channel_id=1, source_target_pairs={{0,8},{8,0},{16,24},{24,16},{1,9},{9,1},{17,25},{25,17},{2,10},{10... | collective-permute-start | bytes 393224 | tf_op jit(solution)/shard_map/ppermute | solution.py:89
  4.3 12.9 %collective-permute-start.6 = (bf16[64,1024]{1,0:T(8,128)(2,1)S(1)}, bf16[64,1024]{1,0:T(8,128)(2,1)S(1)}, u32[]{:S(2)}, u32[]{:S(2)}) collective-permute-start(bf16[64,1024]{1,0:T(8,128)(2,1)S(1)} %get-tuple-element.13), channel_id=1, source_target_pairs={{0,16},{8,24},{16,0},{24,8},{1,17},{9,25},{17,1},{25,9},{2,18},{10... | collective-permute-start | bytes 393224 | tf_op jit(solution)/shard_map/ppermute | solution.py:89
  6.9 11.9 %collective-permute-start.10 = (bf16[64,1024]{1,0:T(8,128)(2,1)S(1)}, bf16[64,1024]{1,0:T(8,128)(2,1)S(1)}, u32[]{:S(2)}, u32[]{:S(2)}) collective-permute-start(bf16[64,1024]{1,0:T(8,128)(2,1)S(1)} %get-tuple-element.13), channel_id=1, source_target_pairs={{0,24},{8,16},{16,8},{24,0},{1,25},{9,17},{17,9},{25,1},{2,26},{10... | collective-permute-start | bytes 393224 | tf_op jit(solution)/shard_map/ppermute | solution.py:89
  7.0 19.0 %collective-permute-start = (bf16[128,1024]{1,0:T(8,128)(2,1)S(1)}, bf16[128,1024]{1,0:T(8,128)(2,1)S(1)}, u32[]{:S(2)}, u32[]{:S(2)}) collective-permute-start(bf16[128,1024]{1,0:T(8,128)(2,1)S(1)} %get-tuple-element.16), channel_id=1, source_target_pairs={{0,4},{4,0},{1,5},{5,1},{2,6},{6,2},{3,7},{7,3},{8,12},{12,8},{9,1... | collective-permute-start | bytes 786440 | tf_op jit(solution)/shard_map/ppermute | solution.py:74
  9.6 9.8 %collective-permute-start.3 = (bf16[64,1024]{1,0:T(8,128)(2,1)S(1)}, bf16[64,1024]{1,0:T(8,128)(2,1)S(1)}, u32[]{:S(2)}, u32[]{:S(2)}) collective-permute-start(bf16[64,1024]{1,0:T(8,128)(2,1)S(1)} %collective-permute-done.2), channel_id=1, source_target_pairs={{0,4},{4,0},{1,5},{5,1},{2,6},{6,2},{3,7},{7,3},{8,12},{12,8},{9,1... | collective-permute-start | bytes 393224 | tf_op jit(solution)/shard_map/ppermute | solution.py:74
  17.2 5.7 %collective-permute-start.7 = (bf16[64,1024]{1,0:T(8,128)(2,1)S(1)}, bf16[64,1024]{1,0:T(8,128)(2,1)S(1)}, u32[]{:S(2)}, u32[]{:S(2)}) collective-permute-start(bf16[64,1024]{1,0:T(8,128)(2,1)S(1)} %collective-permute-done.6), channel_id=1, source_target_pairs={{0,2},{1,3},{2,0},{3,1},{4,6},{5,7},{6,4},{7,5},{8,10},{9,11},{10,... | collective-permute-start | bytes 393224 | tf_op jit(solution)/shard_map/ppermute | solution.py:92
  18.8 5.7 %collective-permute-start.11 = (bf16[64,1024]{1,0:T(8,128)(2,1)S(1)}, bf16[64,1024]{1,0:T(8,128)(2,1)S(1)}, u32[]{:S(2)}, u32[]{:S(2)}) collective-permute-start(bf16[64,1024]{1,0:T(8,128)(2,1)S(1)} %collective-permute-done.10), channel_id=1, source_target_pairs={{0,2},{1,3},{2,0},{3,1},{4,6},{5,7},{6,4},{7,5},{8,10},{9,11},{10,... | collective-permute-start | bytes 393224 | tf_op jit(solution)/shard_map/ppermute | solution.py:92
  19.5 7.7 %collective-permute-start.4 = (bf16[2,64,1024]{2,1,0:T(8,128)(2,1)S(1)}, bf16[2,64,1024]{2,1,0:T(8,128)(2,1)S(1)}, u32[]{:S(2)}, u32[]{:S(2)}) collective-permute-start(bf16[2,64,1024]{2,1,0:T(8,128)(2,1)S(1)} %pad_maximum_fusion.5), channel_id=1, source_target_pairs={{0,2},{1,3},{2,0},{3,1},{4,6},{5,7},{6,4},{7,5},{8,10},{9,11},{10,... | collective-permute-start | bytes 786440 | tf_op jit(solution)/shard_map/ppermute | solution.py:79
  22.9 6.4 %collective-permute-start.8 = (bf16[128,1024]{1,0:T(8,128)(2,1)S(1)}, bf16[128,1024]{1,0:T(8,128)(2,1)S(1)}, u32[]{:S(2)}, u32[]{:S(2)}) collective-permute-start(bf16[128,1024]{1,0:T(8,128)(2,1)S(1)} %constant_dynamic-update-slice_fusion), channel_id=1, source_target_pairs={{0,4},{4,0},{1,5},{5,1},{2,6},{6,2},{3,7},{7,3},{8,12},{12,8},{9,1... | collective-permute-start | bytes 786440 | tf_op jit(solution)/shard_map/ppermute | solution.py:74
  24.5 7.6 %collective-permute-start.12 = (bf16[128,1024]{1,0:T(8,128)(2,1)S(1)}, bf16[128,1024]{1,0:T(8,128)(2,1)S(1)}, u32[]{:S(2)}, u32[]{:S(2)}) collective-permute-start(bf16[128,1024]{1,0:T(8,128)(2,1)S(1)} %constant_dynamic-update-slice_fusion.2), channel_id=1, source_target_pairs={{0,4},{4,0},{1,5},{5,1},{2,6},{6,2},{3,7},{7,3},{8,12},{12,8},{9,1... | collective-permute-start | bytes 786440 | tf_op jit(solution)/shard_map/ppermute | solution.py:74
  26.0 6.6 %collective-permute-start.1 = (bf16[2,128,1024]{2,1,0:T(8,128)(2,1)S(1)}, bf16[2,128,1024]{2,1,0:T(8,128)(2,1)S(1)}, u32[]{:S(2)}, u32[]{:S(2)}) collective-permute-start(bf16[2,128,1024]{2,1,0:T(8,128)(2,1)S(1)} %pad_maximum_fusion), channel_id=1, source_target_pairs={{0,1},{1,0},{2,3},{3,2},{4,5},{5,4},{6,7},{7,6},{8,9},{9,8},{10,11... | collective-permute-start | bytes 1572872 | tf_op jit(solution)/shard_map/ppermute | solution.py:108
  27.2 6.0 %collective-permute-start.5 = (bf16[2,128,1024]{2,1,0:T(8,128)(2,1)S(1)}, bf16[2,128,1024]{2,1,0:T(8,128)(2,1)S(1)}, u32[]{:S(2)}, u32[]{:S(2)}) collective-permute-start(bf16[2,128,1024]{2,1,0:T(8,128)(2,1)S(1)} %pad_maximum_fusion.1), channel_id=1, source_target_pairs={{0,1},{1,0},{2,3},{3,2},{4,5},{5,4},{6,7},{7,6},{8,9},{9,8},{10,11... | collective-permute-start | bytes 1572872 | tf_op jit(solution)/shard_map/ppermute | solution.py:79
  29.4 3.9 %collective-permute-start.9 = (bf16[2,128,1024]{2,1,0:T(8,128)(2,1)S(1)}, bf16[2,128,1024]{2,1,0:T(8,128)(2,1)S(1)}, u32[]{:S(2)}, u32[]{:S(2)}) collective-permute-start(bf16[2,128,1024]{2,1,0:T(8,128)(2,1)S(1)} %pad_maximum_fusion.2), channel_id=1, source_target_pairs={{0,1},{1,0},{2,3},{3,2},{4,5},{5,4},{6,7},{7,6},{8,9},{9,8},{10,11... | collective-permute-start | bytes 1572872 | tf_op jit(solution)/shard_map/ppermute | solution.py:95
  32.2 2.0 %collective-permute-start.13 = (bf16[2,128,1024]{2,1,0:T(8,128)(2,1)S(1)}, bf16[2,128,1024]{2,1,0:T(8,128)(2,1)S(1)}, u32[]{:S(2)}, u32[]{:S(2)}) collective-permute-start(bf16[2,128,1024]{2,1,0:T(8,128)(2,1)S(1)} %pad_maximum_fusion.3), channel_id=1, source_target_pairs={{0,1},{1,0},{2,3},{3,2},{4,5},{5,4},{6,7},{7,6},{8,9},{9,8},{10,11... | collective-permute-start | bytes 1572872 | tf_op jit(solution)/shard_map/ppermute | solution.py:95
  34.3 4.6 %copy-start.1 = (bf16[8,256,1024]{2,1,0:T(8,128)(2,1)}, bf16[8,256,1024]{2,1,0:T(8,128)(2,1)S(1)}, u32[]{:S(2)}) copy-start(bf16[8,256,1024]{2,1,0:T(8,128)(2,1)S(1)} %maximum_dynamic-update-slice_fusion.3) | copy-start | bytes 12582916
  52.5 3.4 %copy-start = (f32[2048,512]{1,0:T(8,128)S(1)}, f32[2048,512]{1,0:T(8,128)}, u32[]{:S(2)}) copy-start(f32[2048,512]{1,0:T(8,128)} %get-tuple-element.22) | copy-start | bytes 12582916
  55.4 2.3 %copy-start.2 = (bf16[8,256,1024]{2,1,0:T(8,128)(2,1)S(1)}, bf16[8,256,1024]{2,1,0:T(8,128)(2,1)}, u32[]{:S(2)}) copy-start(bf16[8,256,1024]{2,1,0:T(8,128)(2,1)} %copy-done.1) | copy-start | bytes 12582916

commit v29 on v25

--- a/solution.py
+++ b/solution.py
@@ -101,7 +101,13 @@
         for sz, piece in enumerate(landed[1:], start=1)
     ]
 
-    parts[0] = spread(pair_of(mine))
+    order = list(reversed(bits))
+    own = lax.dynamic_slice_in_dim(rows, (q ^ order[0]) * tq, tq, 0).astype(jnp.bfloat16)
+    own = pair_of(jnp.concatenate([mine, own], axis=0))
+    for bit in order[1:]:
+        other = lax.ppermute(own, "cent", [(i, i ^ bit) for i in range(n_c)])
+        own = jnp.concatenate([own, other], axis=1)
+    parts[0] = own
 
     cur = jnp.zeros((n_o * n_d,) + parts[0].shape[1:], parts[0].dtype)
     for sz in range(n_o):

time: 63 us -> 60.7 us (0.963)
  local copies, waits for them, and re-layouts: 6.04 us -> 3.49 us
    unnamed x12 -> x10, local copies, waits for them, and re-layouts: 4.38 us -> 1.32 us
    ppermute x4 -> x2, starting transfers between devices: 3.13 us -> 1.25 us  [spread(): other = lax.ppermute(cur, 'cent', [(i, i ^ bit) for i in range(n_c)])]
    ppermute x3, starting transfers between devices: 4.39 us -> 5.68 us  [shards_all(): landed.append(lax.ppermute(mine, 'outer', pairs))]
    ppermute x3, starting transfers between devices: 1.87 us -> 2.75 us  [shards_all(): lax.ppermute(jnp.stack([peak_abs, mass_abs]), axis, [(i, i ^ bit) for i i...]
    ppermute x3, waiting for transfers between devices: 7.36 us -> 6.48 us  [shards_all(): lax.ppermute(jnp.stack([peak_abs, mass_abs]), axis, [(i, i ^ bit) for i i...]
    ppermute x3, waiting for transfers between devices: 5.26 us -> 6.05 us  [shards_all(): landed.append(lax.ppermute(mine, 'outer', pairs))]
    ppermute x4 -> x2, waiting for transfers between devices: 1.26 us -> 1.59 us  [spread(): other = lax.ppermute(cur, 'cent', [(i, i ^ bit) for i in range(n_c)])]
  transfers between devices with their start and end apart: 18 -> 17, of which waited for: 9 -> 9; matrix products, arithmetic and copies ran while one was open for 6% -> 4% of each run, Pallas kernels for 0% -> 0%
where the time goes in v29:
time: 60.7 us; the launch traced here: 60.5 us
  waiting for transfers between devices  20.6 us (34%)
  starting transfers between devices  18.5 us (30%)
  other arithmetic  9.33 us (15%)
  matrix products  8.28 us (14%)
  local copies, waits for them, and re-layouts  3.49 us (6%)
    ppermute x3, waiting for transfers between devices, shards_all(): lax.ppermute(jnp.stack([peak_abs, mass_abs]), axis, [(i, i ^ bit) for i i...  6.48 us
    ppermute x3, waiting for transfers between devices, shards_all(): landed.append(lax.ppermute(mine, 'outer', pairs))  6.05 us
    ppermute x3, starting transfers between devices, shards_all(): landed.append(lax.ppermute(mine, 'outer', pairs))  5.68 us
    ppermute x4, waiting for transfers between devices, pair_of(): lax.ppermute(piece, 'dp', [(j, (j + sy) % n_d) for j in range(n_d)])  5.63 us
    ppermute x4, starting transfers between devices, pair_of(): lax.ppermute(piece, 'dp', [(j, (j + sy) % n_d) for j in range(n_d)])  5.48 us
    dot_general x1, matrix products, scores_for(): lax.dot_general(piece, cent_bf, (((1,), (1,)), ((), ())), preferred_eleme...  4.61 us
    dot_general x1, matrix products, shards_all(): lax.dot_general(scaled.reshape(n_o * pod, k), everything, (((0,), (0,)),...  3.67 us
    reduce_sum x1, other arithmetic, row_summary(): local_sum = jnp.sum(jnp.exp(logits - local_max[:, None]), axis=1)  3.31 us
  transfers between devices with their start and end apart: 17, of which 9 were waited for; matrix products, arithmetic and copies ran while one was open for 4% of the time, Pallas kernels for 0%

profile of v29, /device:TPU:0, one launch (start us, length us, event | category | flops | bytes accessed | tf_op | source)
XLA Modules:
  0.0 60.5 jit_solution(11567968427629724507)
XLA Ops:
  0.0 1.2 %dynamic-slice_convert_fusion.1 = (bf16[64,1024]{1,0:T(8,128)(2,1)S(1)}, bf16[64,1024]{1,0:T(8,128)(2,1)S(1)}) fusion(f32[256,1024]{1,0:T(8,128)} %param.3, s32[]{:T(128)S(6)} %select_n.69, s32[]{:T(128)S(6)} %select_n.70), kind=kLoop, calls=%fused_computation.21 | loop fusion | bytes 524296 | tf_op jit(solution)/shard_map/convert_element_type | solution.py:69
  1.2 3.1 %collective-permute-start.2 = (bf16[64,1024]{1,0:T(8,128)(2,1)S(1)}, bf16[64,1024]{1,0:T(8,128)(2,1)S(1)}, u32[]{:S(2)}, u32[]{:S(2)}) collective-permute-start(bf16[64,1024]{1,0:T(8,128)(2,1)S(1)} %get-tuple-element.17), channel_id=1, source_target_pairs={{0,8},{8,0},{16,24},{24,16},{1,9},{9,1},{17,25},{25,17},{2,10},{10... | collective-permute-start | bytes 393224 | tf_op jit(solution)/shard_map/ppermute | solution.py:89
  4.3 2.6 %collective-permute-start.6 = (bf16[64,1024]{1,0:T(8,128)(2,1)S(1)}, bf16[64,1024]{1,0:T(8,128)(2,1)S(1)}, u32[]{:S(2)}, u32[]{:S(2)}) collective-permute-start(bf16[64,1024]{1,0:T(8,128)(2,1)S(1)} %get-tuple-element.17), channel_id=1, source_target_pairs={{0,16},{8,24},{16,0},{24,8},{1,17},{9,25},{17,1},{25,9},{2,18},{10... | collective-permute-start | bytes 393224 | tf_op jit(solution)/shard_map/ppermute | solution.py:89
  6.9 0.0 collective-permute-start.10
  6.9 0.1 fusion.17
  7.0 1.8 %collective-permute-start = (bf16[128,1024]{1,0:T(8,128)(2,1)S(1)}, bf16[128,1024]{1,0:T(8,128)(2,1)S(1)}, u32[]{:S(2)}, u32[]{:S(2)}) collective-permute-start(bf16[128,1024]{1,0:T(8,128)(2,1)S(1)} %get-tuple-element.20), channel_id=1, source_target_pairs={{0,4},{4,0},{1,5},{5,1},{2,6},{6,2},{3,7},{7,3},{8,12},{12,8},{9,1... | collective-permute-start | bytes 786440 | tf_op jit(solution)/shard_map/ppermute | solution.py:74
  8.8 0.7 %broadcast_xor_fusion = s32[4]{0:T(128)S(1)} fusion(s32[4]{0:T(128)} %constant.75.clone, s32[]{:T(128)S(6)} %axis_index.32), kind=kLoop, calls=%fused_computation.70 | loop fusion | flops 4 | bytes 36 | tf_op jit(solution)/shard_map/xor | solution.py:124
  9.4 0.1 iota_compare_fusion
  9.5 0.1 stack.102
  9.6 0.0 collective-permute-done.2
  9.6 1.6 %collective-permute-start.3 = (bf16[64,1024]{1,0:T(8,128)(2,1)S(1)}, bf16[64,1024]{1,0:T(8,128)(2,1)S(1)}, u32[]{:S(2)}, u32[]{:S(2)}) collective-permute-start(bf16[64,1024]{1,0:T(8,128)(2,1)S(1)} %collective-permute-done.2), channel_id=1, source_target_pairs={{0,2},{1,3},{2,0},{3,1},{4,6},{5,7},{6,4},{7,5},{8,10},{9,11},{10,... | collective-permute-start | bytes 393224 | tf_op jit(solution)/shard_map/ppermute | solution.py:92
  11.2 6.0 %collective-permute-done.6 = bf16[64,1024]{1,0:T(8,128)(2,1)S(1)} collective-permute-done((bf16[64,1024]{1,0:T(8,128)(2,1)S(1)}, bf16[64,1024]{1,0:T(8,128)(2,1)S(1)}, u32[]{:S(2)}, u32[]{:S(2)}) %collective-permute-start.6) | collective-permute-done | bytes 131104 | tf_op jit(solution)/shard_map/ppermute | solution.py:89
  17.2 1.5 %collective-permute-start.7 = (bf16[64,1024]{1,0:T(8,128)(2,1)S(1)}, bf16[64,1024]{1,0:T(8,128)(2,1)S(1)}, u32[]{:S(2)}, u32[]{:S(2)}) collective-permute-start(bf16[64,1024]{1,0:T(8,128)(2,1)S(1)} %collective-permute-done.6), channel_id=1, source_target_pairs={{0,4},{4,0},{1,5},{5,1},{2,6},{6,2},{3,7},{7,3},{8,12},{12,8},{9,1... | collective-permute-start | bytes 393224 | tf_op jit(solution)/shard_map/ppermute | solution.py:74
  18.8 0.0 collective-permute-done.10
  18.8 1.6 %collective-permute-start.11 = (bf16[64,1024]{1,0:T(8,128)(2,1)S(1)}, bf16[64,1024]{1,0:T(8,128)(2,1)S(1)}, u32[]{:S(2)}, u32[]{:S(2)}) collective-permute-start(bf16[64,1024]{1,0:T(8,128)(2,1)S(1)} %collective-permute-done.10), channel_id=1, source_target_pairs={{0,2},{1,3},{2,0},{3,1},{4,6},{5,7},{6,4},{7,5},{8,10},{9,11},{10,... | collective-permute-start | bytes 393224 | tf_op jit(solution)/shard_map/ppermute | solution.py:92
  20.3 0.0 collective-permute-done.3
  20.3 0.6 collective-permute-start.4
  20.9 2.8 %collective-permute-done.7 = bf16[64,1024]{1,0:T(8,128)(2,1)S(1)} collective-permute-done((bf16[64,1024]{1,0:T(8,128)(2,1)S(1)}, bf16[64,1024]{1,0:T(8,128)(2,1)S(1)}, u32[]{:S(2)}, u32[]{:S(2)}) %collective-permute-start.7) | collective-permute-done | bytes 131104 | tf_op jit(solution)/shard_map/ppermute | solution.py:74
  23.7 1.2 %collective-permute-start.8 = (bf16[2,64,1024]{2,1,0:T(8,128)(2,1)S(1)}, bf16[2,64,1024]{2,1,0:T(8,128)(2,1)S(1)}, u32[]{:S(2)}, u32[]{:S(2)}) collective-permute-start(bf16[2,64,1024]{2,1,0:T(8,128)(2,1)S(1)} %pad_maximum_fusion.5), channel_id=1, source_target_pairs={{0,2},{1,3},{2,0},{3,1},{4,6},{5,7},{6,4},{7,5},{8,10},{9,11},{10,... | collective-permute-start | bytes 786440 | tf_op jit(solution)/shard_map/ppermute | solution.py:79
  24.9 0.0 collective-permute-done.11
  24.9 1.6 %collective-permute-start.12 = (bf16[128,1024]{1,0:T(8,128)(2,1)S(1)}, bf16[128,1024]{1,0:T(8,128)(2,1)S(1)}, u32[]{:S(2)}, u32[]{:S(2)}) collective-permute-start(bf16[128,1024]{1,0:T(8,128)(2,1)S(1)} %constant_dynamic-update-slice_fusion.2), channel_id=1, source_target_pairs={{0,4},{4,0},{1,5},{5,1},{2,6},{6,2},{3,7},{7,3},{8,12},{12,8},{9,1... | collective-permute-start | bytes 786440 | tf_op jit(solution)/shard_map/ppermute | solution.py:74
  26.5 0.0 collective-permute-done
  26.5 0.1 pad_maximum_fusion
  26.5 0.1 collective-permute-start.1
  26.6 1.8 %collective-permute-done.4 = bf16[128,1024]{1,0:T(8,128)(2,1)S(1)} collective-permute-done((bf16[128,1024]{1,0:T(8,128)(2,1)S(1)}, bf16[128,1024]{1,0:T(8,128)(2,1)S(1)}, u32[]{:S(2)}, u32[]{:S(2)}) %collective-permute-start.4) | collective-permute-done | bytes 262176 | tf_op jit(solution)/shard_map/ppermute | solution.py:74
  28.4 0.1 pad_maximum_fusion.1
  28.5 0.1 collective-permute-start.5
  28.6 1.6 %collective-permute-done.8 = bf16[2,64,1024]{2,1,0:T(8,128)(2,1)S(1)} collective-permute-done((bf16[2,64,1024]{2,1,0:T(8,128)(2,1)S(1)}, bf16[2,64,1024]{2,1,0:T(8,128)(2,1)S(1)}, u32[]{:S(2)}, u32[]{:S(2)}) %collective-permute-start.8) | collective-permute-done | bytes 262176 | tf_op jit(solution)/shard_map/ppermute | solution.py:79
  30.2 0.1 collective-permute-start.9
  30.3 1.1 %collective-permute-done.12 = bf16[128,1024]{1,0:T(8,128)(2,1)S(1)} collective-permute-done((bf16[128,1024]{1,0:T(8,128)(2,1)S(1)}, bf16[128,1024]{1,0:T(8,128)(2,1)S(1)}, u32[]{:S(2)}, u32[]{:S(2)}) %collective-permute-start.12) | collective-permute-done | bytes 262176 | tf_op jit(solution)/shard_map/ppermute | solution.py:74
  31.3 0.1 pad_maximum_fusion.3
  31.4 0.1 collective-permute-start.13
  31.5 0.0 copy-done.3
  31.5 0.2 multiply_reduce_fusion
  31.7 0.0 collective-permute-done.1
  31.7 0.5 broadcast_in_dim.137
  32.2 0.1 maximum_dynamic-update-slice_fusion
  32.3 0.0 collective-permute-done.5
  32.4 0.1 maximum_dynamic-update-slice_fusion.1
  32.5 0.0 collective-permute-done.9
  32.5 0.1 maximum_dynamic-update-slice_fusion.2
  32.6 0.8 %collective-permute-done.13 = bf16[2,128,1024]{2,1,0:T(8,128)(2,1)S(1)} collective-permute-done((bf16[2,128,1024]{2,1,0:T(8,128)(2,1)S(1)}, bf16[2,128,1024]{2,1,0:T(8,128)(2,1)S(1)}, u32[]{:S(2)}, u32[]{:S(2)}) %collective-permute-start.13) | collective-permute-done | bytes 524320 | tf_op jit(solution)/shard_map/ppermute | solution.py:95
  33.4 0.1 maximum_dynamic-update-slice_fusion.3
  33.5 4.6 %fusion.20 = (f32[2048]{0:T(1024)S(1)}, f32[2048,512]{1,0:T(8,128)}) fusion(f32[512]{0:T(512)S(1)} %multiply_reduce_fusion, bf16[2048,1024]{1,0:T(8,128)(2,1)S(1)} %bitcast.96, f32[512,1024]{1,0:T(8,128)S(1)} %copy-done.3), kind=kOutput, calls=%fused_computation.73 | convolution fusion | flops 2152200192 | bytes 10496000 | tf_op jit(solution)/shard_map/dot_general | solution.py:10
  38.1 0.1 broadcast_in_dim.140
  38.2 3.3 %exponential_reduce_fusion = f32[2048]{0:T(1024)S(1)} fusion(f32[2048,512]{1,0:T(8,128)} %get-tuple-element.28, f32[2048]{0:T(1024)S(1)} %get-tuple-element.27), kind=kLoop, calls=%fused_computation.4 | loop fusion | flops 2095104 | bytes 4210688 | tf_op jit(solution)/shard_map/reduce_sum | solution.py:18
  41.5 0.1 broadcast_in_dim.145
  41.6 0.1 select_reduce_fusion.7
  41.7 0.2 select_reduce_fusion.3
  41.9 0.2 collective-permute-start.14
  42.1 1.1 %collective-permute-done.14 = f32[2,8,4,64]{3,2,1,0:T(4,128)S(1)} collective-permute-done((f32[2,8,4,64]{3,2,1,0:T(4,128)S(1)}, f32[2,8,4,64]{3,2,1,0:T(4,128)S(1)}, u32[]{:S(2)}, u32[]{:S(2)}) %collective-permute-start.14) | collective-permute-done | bytes 16416 | tf_op jit(solution)/shard_map/ppermute | solution.py:147
  43.2 1.0 %collective-permute-start.15 = (f32[2,8,4,64]{3,2,1,0:T(4,128)S(1)}, f32[2,8,4,64]{3,2,1,0:T(4,128)S(1)}, u32[]{:S(2)}, u32[]{:S(2)}) collective-permute-start(f32[2,8,4,64]{3,2,1,0:T(4,128)S(1)} %pad_maximum_fusion.7), channel_id=1, source_target_pairs={{0,2},{1,3},{2,0},{3,1},{4,6},{5,7},{6,4},{7,5},{8,10},{9,11},{10,... | collective-permute-start | bytes 49160 | tf_op jit(solution)/shard_map/ppermute | solution.py:147
  44.2 3.0 %collective-permute-done.15 = f32[2,8,4,64]{3,2,1,0:T(4,128)S(1)} collective-permute-done((f32[2,8,4,64]{3,2,1,0:T(4,128)S(1)}, f32[2,8,4,64]{3,2,1,0:T(4,128)S(1)}, u32[]{:S(2)}, u32[]{:S(2)}) %collective-permute-start.15) | collective-permute-done | bytes 16416 | tf_op jit(solution)/shard_map/ppermute | solution.py:147
  47.2 1.6 %collective-permute-start.16 = (f32[2,8,4,64]{3,2,1,0:T(4,128)S(1)}, f32[2,8,4,64]{3,2,1,0:T(4,128)S(1)}, u32[]{:S(2)}, u32[]{:S(2)}) collective-permute-start(f32[2,8,4,64]{3,2,1,0:T(4,128)S(1)} %pad_maximum_fusion.8), channel_id=1, source_target_pairs={{0,4},{4,0},{1,5},{5,1},{2,6},{6,2},{3,7},{7,3},{8,12},{12,8},{9,1... | collective-permute-start | bytes 49160 | tf_op jit(solution)/shard_map/ppermute | solution.py:147
  48.8 2.4 %collective-permute-done.16 = f32[2,8,4,64]{3,2,1,0:T(4,128)S(1)} collective-permute-done((f32[2,8,4,64]{3,2,1,0:T(4,128)S(1)}, f32[2,8,4,64]{3,2,1,0:T(4,128)S(1)}, u32[]{:S(2)}, u32[]{:S(2)}) %collective-permute-start.16) | collective-permute-done | bytes 16416 | tf_op jit(solution)/shard_map/ppermute | solution.py:147
  51.2 0.1 select_reduce_fusion.1
  51.3 0.1 select_reduce_fusion.5
  51.5 0.1 div.55
  51.5 0.1 sub.100
  51.6 2.8 %bitcast_reduce_fusion = f32[4,512]{1,0:T(4,128)S(1)} fusion(f32[2048]{0:T(1024)S(1)} %div.55, f32[2048,512]{1,0:T(8,128)} %get-tuple-element.28, f32[2048]{0:T(1024)S(1)} %sub.100), kind=kLoop, calls=%fused_computation.2 | loop fusion | flops 5240832 | bytes 4218880 | tf_op jit(solution)/shard_map/reduce_sum | solution.py:164
  54.5 0.6 copy-done
  55.1 1.0 %fusion = bf16[2048,512]{1,0:T(8,128)(2,1)S(1)} fusion(f32[4,512]{1,0:T(4,128)S(1)} %broadcast_add_fusion, f32[2048]{0:T(1024)S(1)} %div.55, f32[2048,512]{1,0:T(8,128)S(1)} %copy-done, f32[2048]{0:T(1024)S(1)} %sub.100), kind=kLoop, calls=%fused_computation.1 | loop fusion | flops 6291456 | bytes 6316032 | tf_op jit(solution)/shard_map/convert_element_type | solution.py:165
  56.1 0.7 %copy-done.2 = bf16[8,256,1024]{2,1,0:T(8,128)(2,1)S(1)} copy-done((bf16[8,256,1024]{2,1,0:T(8,128)(2,1)S(1)}, bf16[8,256,1024]{2,1,0:T(8,128)(2,1)}, u32[]{:S(2)}) %copy-start.2) | copy-done | bytes 4194328
  56.8 3.7 %subtract_multiply_fusion.1 = f32[512,1024]{1,0:T(8,128)} fusion(f32[512,1024]{1,0:T(8,128)S(1)} %copy-done.3, bf16[2048,512]{1,0:T(8,128)(2,1)S(1)} %fusion, bf16[2048,1024]{1,0:T(8,128)(2,1)S(1)} %bitcast.97, f32[512]{0:T(512)S(1)} %fusion.16), kind=kOutput, calls=%fused_computation.7 | convolution fusion | flops 2149056512 | bytes 10487808 | tf_op jit(solution)/shard_map/dot_general | solution.py:166
  (25 shorter events, 0.3 us)
Async XLA Ops:
  0.0 31.5 %copy-start.3 = (f32[512,1024]{1,0:T(8,128)S(1)}, f32[512,1024]{1,0:T(8,128)}, u32[]{:S(2)}) copy-start(f32[512,1024]{1,0:T(8,128)} %param.4) | copy-start | bytes 6291460
  1.2 8.4 %collective-permute-start.2 = (bf16[64,1024]{1,0:T(8,128)(2,1)S(1)}, bf16[64,1024]{1,0:T(8,128)(2,1)S(1)}, u32[]{:S(2)}, u32[]{:S(2)}) collective-permute-start(bf16[64,1024]{1,0:T(8,128)(2,1)S(1)} %get-tuple-element.17), channel_id=1, source_target_pairs={{0,8},{8,0},{16,24},{24,16},{1,9},{9,1},{17,25},{25,17},{2,10},{10... | collective-permute-start | bytes 393224 | tf_op jit(solution)/shard_map/ppermute | solution.py:89
  4.3 12.9 %collective-permute-start.6 = (bf16[64,1024]{1,0:T(8,128)(2,1)S(1)}, bf16[64,1024]{1,0:T(8,128)(2,1)S(1)}, u32[]{:S(2)}, u32[]{:S(2)}) collective-permute-start(bf16[64,1024]{1,0:T(8,128)(2,1)S(1)} %get-tuple-element.17), channel_id=1, source_target_pairs={{0,16},{8,24},{16,0},{24,8},{1,17},{9,25},{17,1},{25,9},{2,18},{10... | collective-permute-start | bytes 393224 | tf_op jit(solution)/shard_map/ppermute | solution.py:89
  6.9 11.9 %collective-permute-start.10 = (bf16[64,1024]{1,0:T(8,128)(2,1)S(1)}, bf16[64,1024]{1,0:T(8,128)(2,1)S(1)}, u32[]{:S(2)}, u32[]{:S(2)}) collective-permute-start(bf16[64,1024]{1,0:T(8,128)(2,1)S(1)} %get-tuple-element.17), channel_id=1, source_target_pairs={{0,24},{8,16},{16,8},{24,0},{1,25},{9,17},{17,9},{25,1},{2,26},{10... | collective-permute-start | bytes 393224 | tf_op jit(solution)/shard_map/ppermute | solution.py:89
  7.0 19.5 %collective-permute-start = (bf16[128,1024]{1,0:T(8,128)(2,1)S(1)}, bf16[128,1024]{1,0:T(8,128)(2,1)S(1)}, u32[]{:S(2)}, u32[]{:S(2)}) collective-permute-start(bf16[128,1024]{1,0:T(8,128)(2,1)S(1)} %get-tuple-element.20), channel_id=1, source_target_pairs={{0,4},{4,0},{1,5},{5,1},{2,6},{6,2},{3,7},{7,3},{8,12},{12,8},{9,1... | collective-permute-start | bytes 786440 | tf_op jit(solution)/shard_map/ppermute | solution.py:74
  9.6 10.7 %collective-permute-start.3 = (bf16[64,1024]{1,0:T(8,128)(2,1)S(1)}, bf16[64,1024]{1,0:T(8,128)(2,1)S(1)}, u32[]{:S(2)}, u32[]{:S(2)}) collective-permute-start(bf16[64,1024]{1,0:T(8,128)(2,1)S(1)} %collective-permute-done.2), channel_id=1, source_target_pairs={{0,2},{1,3},{2,0},{3,1},{4,6},{5,7},{6,4},{7,5},{8,10},{9,11},{10,... | collective-permute-start | bytes 393224 | tf_op jit(solution)/shard_map/ppermute | solution.py:92
  17.2 6.4 %collective-permute-start.7 = (bf16[64,1024]{1,0:T(8,128)(2,1)S(1)}, bf16[64,1024]{1,0:T(8,128)(2,1)S(1)}, u32[]{:S(2)}, u32[]{:S(2)}) collective-permute-start(bf16[64,1024]{1,0:T(8,128)(2,1)S(1)} %collective-permute-done.6), channel_id=1, source_target_pairs={{0,4},{4,0},{1,5},{5,1},{2,6},{6,2},{3,7},{7,3},{8,12},{12,8},{9,1... | collective-permute-start | bytes 393224 | tf_op jit(solution)/shard_map/ppermute | solution.py:74
  18.8 6.1 %collective-permute-start.11 = (bf16[64,1024]{1,0:T(8,128)(2,1)S(1)}, bf16[64,1024]{1,0:T(8,128)(2,1)S(1)}, u32[]{:S(2)}, u32[]{:S(2)}) collective-permute-start(bf16[64,1024]{1,0:T(8,128)(2,1)S(1)} %collective-permute-done.10), channel_id=1, source_target_pairs={{0,2},{1,3},{2,0},{3,1},{4,6},{5,7},{6,4},{7,5},{8,10},{9,11},{10,... | collective-permute-start | bytes 393224 | tf_op jit(solution)/shard_map/ppermute | solution.py:92
  20.3 8.1 %collective-permute-start.4 = (bf16[128,1024]{1,0:T(8,128)(2,1)S(1)}, bf16[128,1024]{1,0:T(8,128)(2,1)S(1)}, u32[]{:S(2)}, u32[]{:S(2)}) collective-permute-start(bf16[128,1024]{1,0:T(8,128)(2,1)S(1)} %constant_dynamic-update-slice_fusion), channel_id=1, source_target_pairs={{0,4},{4,0},{1,5},{5,1},{2,6},{6,2},{3,7},{7,3},{8,12},{12,8},{9,1... | collective-permute-start | bytes 786440 | tf_op jit(solution)/shard_map/ppermute | solution.py:74
  23.7 6.4 %collective-permute-start.8 = (bf16[2,64,1024]{2,1,0:T(8,128)(2,1)S(1)}, bf16[2,64,1024]{2,1,0:T(8,128)(2,1)S(1)}, u32[]{:S(2)}, u32[]{:S(2)}) collective-permute-start(bf16[2,64,1024]{2,1,0:T(8,128)(2,1)S(1)} %pad_maximum_fusion.5), channel_id=1, source_target_pairs={{0,2},{1,3},{2,0},{3,1},{4,6},{5,7},{6,4},{7,5},{8,10},{9,11},{10,... | collective-permute-start | bytes 786440 | tf_op jit(solution)/shard_map/ppermute | solution.py:79
  24.9 6.4 %collective-permute-start.12 = (bf16[128,1024]{1,0:T(8,128)(2,1)S(1)}, bf16[128,1024]{1,0:T(8,128)(2,1)S(1)}, u32[]{:S(2)}, u32[]{:S(2)}) collective-permute-start(bf16[128,1024]{1,0:T(8,128)(2,1)S(1)} %constant_dynamic-update-slice_fusion.2), channel_id=1, source_target_pairs={{0,4},{4,0},{1,5},{5,1},{2,6},{6,2},{3,7},{7,3},{8,12},{12,8},{9,1... | collective-permute-start | bytes 786440 | tf_op jit(solution)/shard_map/ppermute | solution.py:74
  26.5 5.2 %collective-permute-start.1 = (bf16[2,128,1024]{2,1,0:T(8,128)(2,1)S(1)}, bf16[2,128,1024]{2,1,0:T(8,128)(2,1)S(1)}, u32[]{:S(2)}, u32[]{:S(2)}) collective-permute-start(bf16[2,128,1024]{2,1,0:T(8,128)(2,1)S(1)} %pad_maximum_fusion), channel_id=1, source_target_pairs={{0,1},{1,0},{2,3},{3,2},{4,5},{5,4},{6,7},{7,6},{8,9},{9,8},{10,11... | collective-permute-start | bytes 1572872 | tf_op jit(solution)/shard_map/ppermute | solution.py:108
  28.5 3.9 %collective-permute-start.5 = (bf16[2,128,1024]{2,1,0:T(8,128)(2,1)S(1)}, bf16[2,128,1024]{2,1,0:T(8,128)(2,1)S(1)}, u32[]{:S(2)}, u32[]{:S(2)}) collective-permute-start(bf16[2,128,1024]{2,1,0:T(8,128)(2,1)S(1)} %pad_maximum_fusion.1), channel_id=1, source_target_pairs={{0,1},{1,0},{2,3},{3,2},{4,5},{5,4},{6,7},{7,6},{8,9},{9,8},{10,11... | collective-permute-start | bytes 1572872 | tf_op jit(solution)/shard_map/ppermute | solution.py:95
  30.2 2.3 %collective-permute-start.9 = (bf16[2,128,1024]{2,1,0:T(8,128)(2,1)S(1)}, bf16[2,128,1024]{2,1,0:T(8,128)(2,1)S(1)}, u32[]{:S(2)}, u32[]{:S(2)}) collective-permute-start(bf16[2,128,1024]{2,1,0:T(8,128)(2,1)S(1)} %pad_maximum_fusion.2), channel_id=1, source_target_pairs={{0,1},{1,0},{2,3},{3,2},{4,5},{5,4},{6,7},{7,6},{8,9},{9,8},{10,11... | collective-permute-start | bytes 1572872 | tf_op jit(solution)/shard_map/ppermute | solution.py:79
  31.4 2.0 %collective-permute-start.13 = (bf16[2,128,1024]{2,1,0:T(8,128)(2,1)S(1)}, bf16[2,128,1024]{2,1,0:T(8,128)(2,1)S(1)}, u32[]{:S(2)}, u32[]{:S(2)}) collective-permute-start(bf16[2,128,1024]{2,1,0:T(8,128)(2,1)S(1)} %pad_maximum_fusion.3), channel_id=1, source_target_pairs={{0,1},{1,0},{2,3},{3,2},{4,5},{5,4},{6,7},{7,6},{8,9},{9,8},{10,11... | collective-permute-start | bytes 1572872 | tf_op jit(solution)/shard_map/ppermute | solution.py:95
  33.5 4.6 %copy-start.1 = (bf16[8,256,1024]{2,1,0:T(8,128)(2,1)}, bf16[8,256,1024]{2,1,0:T(8,128)(2,1)S(1)}, u32[]{:S(2)}) copy-start(bf16[8,256,1024]{2,1,0:T(8,128)(2,1)S(1)} %maximum_dynamic-update-slice_fusion.3) | copy-start | bytes 12582916
  41.9 1.3 %collective-permute-start.14 = (f32[2,8,4,64]{3,2,1,0:T(4,128)S(1)}, f32[2,8,4,64]{3,2,1,0:T(4,128)S(1)}, u32[]{:S(2)}, u32[]{:S(2)}) collective-permute-start(f32[2,8,4,64]{3,2,1,0:T(4,128)S(1)} %pad_maximum_fusion.6), channel_id=1, source_target_pairs={{0,1},{1,0},{2,3},{3,2},{4,5},{5,4},{6,7},{7,6},{8,9},{9,8},{10,11... | collective-permute-start | bytes 49160 | tf_op jit(solution)/shard_map/ppermute | solution.py:147
  43.2 4.0 %collective-permute-start.15 = (f32[2,8,4,64]{3,2,1,0:T(4,128)S(1)}, f32[2,8,4,64]{3,2,1,0:T(4,128)S(1)}, u32[]{:S(2)}, u32[]{:S(2)}) collective-permute-start(f32[2,8,4,64]{3,2,1,0:T(4,128)S(1)} %pad_maximum_fusion.7), channel_id=1, source_target_pairs={{0,2},{1,3},{2,0},{3,1},{4,6},{5,7},{6,4},{7,5},{8,10},{9,11},{10,... | collective-permute-start | bytes 49160 | tf_op jit(solution)/shard_map/ppermute | solution.py:147
  47.2 4.0 %collective-permute-start.16 = (f32[2,8,4,64]{3,2,1,0:T(4,128)S(1)}, f32[2,8,4,64]{3,2,1,0:T(4,128)S(1)}, u32[]{:S(2)}, u32[]{:S(2)}) collective-permute-start(f32[2,8,4,64]{3,2,1,0:T(4,128)S(1)} %pad_maximum_fusion.8), channel_id=1, source_target_pairs={{0,4},{4,0},{1,5},{5,1},{2,6},{6,2},{3,7},{7,3},{8,12},{12,8},{9,1... | collective-permute-start | bytes 49160 | tf_op jit(solution)/shard_map/ppermute | solution.py:147
  51.6 3.4 %copy-start = (f32[2048,512]{1,0:T(8,128)S(1)}, f32[2048,512]{1,0:T(8,128)}, u32[]{:S(2)}) copy-start(f32[2048,512]{1,0:T(8,128)} %get-tuple-element.28) | copy-start | bytes 12582916
  54.5 2.3 %copy-start.2 = (bf16[8,256,1024]{2,1,0:T(8,128)(2,1)S(1)}, bf16[8,256,1024]{2,1,0:T(8,128)(2,1)}, u32[]{:S(2)}) copy-start(bf16[8,256,1024]{2,1,0:T(8,128)(2,1)} %copy-done.1) | copy-start | bytes 12582916

commit v30 on v29

--- a/solution.py
+++ b/solution.py
@@ -97,7 +97,7 @@
         return cur
 
     parts = [None] + [
-        spread_x_first(piece) if sz in (1, 3) else spread(pair_of(piece))
+        spread_x_first(piece) if sz == 3 else spread(pair_of(piece))
         for sz, piece in enumerate(landed[1:], start=1)
     ]
 

time: 60.7 us -> 61.9 us (1.020)
  starting transfers between devices: 18.5 us -> 19.7 us
    ppermute x4, waiting for transfers between devices: 5.63 us -> 1.51 us  [pair_of(): lax.ppermute(piece, 'dp', [(j, (j + sy) % n_d) for j in range(n_d)])]
    ppermute x2 -> x4, waiting for transfers between devices: 1.59 us -> 5.24 us  [spread(): other = lax.ppermute(cur, 'cent', [(i, i ^ bit) for i in range(n_c)])]
    ppermute x2 -> x4, starting transfers between devices: 1.25 us -> 3.04 us  [spread(): other = lax.ppermute(cur, 'cent', [(i, i ^ bit) for i in range(n_c)])]
    ppermute x2 -> x1, starting transfers between devices: 3.11 us -> 1.56 us  [spread_x_first(): other = lax.ppermute(piece, 'cent', [(i, i ^ order[0]) for i in range(n_c)])]
    ppermute x2 -> x1, waiting for transfers between devices: 0.01 us -> 0.74 us  [spread_x_first(): other = lax.ppermute(piece, 'cent', [(i, i ^ order[0]) for i in range(n_c)])]
    unnamed x10 -> x9, local copies, waits for them, and re-layouts: 1.32 us -> 1.31 us
  transfers between devices with their start and end apart: 17 -> 17, of which waited for: 9 -> 11; matrix products, arithmetic and copies ran while one was open for 4% -> 3% of each run, Pallas kernels for 0% -> 0%
where the time goes in v30:
time: 61.9 us; the launch traced here: 61.2 us
  waiting for transfers between devices  20.2 us (33%)
  starting transfers between devices  19.7 us (32%)
  other arithmetic  9.33 us (15%)
  matrix products  8.28 us (13%)
  local copies, waits for them, and re-layouts  3.47 us (6%)
    ppermute x3, waiting for transfers between devices, shards_all(): landed.append(lax.ppermute(mine, 'outer', pairs))  6.15 us
    ppermute x3, waiting for transfers between devices, shards_all(): lax.ppermute(jnp.stack([peak_abs, mass_abs]), axis, [(i, i ^ bit) for i i...  5.89 us
    ppermute x4, starting transfers between devices, pair_of(): lax.ppermute(piece, 'dp', [(j, (j + sy) % n_d) for j in range(n_d)])  5.68 us
    ppermute x3, starting transfers between devices, shards_all(): landed.append(lax.ppermute(mine, 'outer', pairs))  5.68 us
    ppermute x4, waiting for transfers between devices, spread(): other = lax.ppermute(cur, 'cent', [(i, i ^ bit) for i in range(n_c)])  5.24 us
    dot_general x1, matrix products, scores_for(): lax.dot_general(piece, cent_bf, (((1,), (1,)), ((), ())), preferred_eleme...  4.61 us
    dot_general x1, matrix products, shards_all(): lax.dot_general(scaled.reshape(n_o * pod, k), everything, (((0,), (0,)),...  3.67 us
    ppermute x3, starting transfers between devices, shards_all(): lax.ppermute(jnp.stack([peak_abs, mass_abs]), axis, [(i, i ^ bit) for i i...  3.34 us
  transfers between devices with their start and end apart: 17, of which 11 were waited for; matrix products, arithmetic and copies ran while one was open for 3% of the time, Pallas kernels for 0%

profile of v30, /device:TPU:0, one launch (start us, length us, event | category | flops | bytes accessed | tf_op | source)
XLA Modules:
  0.0 61.2 jit_solution(8935392678733322246)
XLA Ops:
  0.0 1.2 %dynamic-slice_convert_fusion.1 = (bf16[64,1024]{1,0:T(8,128)(2,1)S(1)}, bf16[64,1024]{1,0:T(8,128)(2,1)S(1)}) fusion(f32[256,1024]{1,0:T(8,128)} %param.3, s32[]{:T(128)S(6)} %select_n.69, s32[]{:T(128)S(6)} %select_n.70), kind=kLoop, calls=%fused_computation.22 | loop fusion | bytes 524296 | tf_op jit(solution)/shard_map/convert_element_type | solution.py:69
  1.2 3.1 %collective-permute-start.2 = (bf16[64,1024]{1,0:T(8,128)(2,1)S(1)}, bf16[64,1024]{1,0:T(8,128)(2,1)S(1)}, u32[]{:S(2)}, u32[]{:S(2)}) collective-permute-start(bf16[64,1024]{1,0:T(8,128)(2,1)S(1)} %get-tuple-element.17), channel_id=1, source_target_pairs={{0,8},{8,0},{16,24},{24,16},{1,9},{9,1},{17,25},{25,17},{2,10},{10... | collective-permute-start | bytes 393224 | tf_op jit(solution)/shard_map/ppermute | solution.py:89
  4.3 2.6 %collective-permute-start.6 = (bf16[64,1024]{1,0:T(8,128)(2,1)S(1)}, bf16[64,1024]{1,0:T(8,128)(2,1)S(1)}, u32[]{:S(2)}, u32[]{:S(2)}) collective-permute-start(bf16[64,1024]{1,0:T(8,128)(2,1)S(1)} %get-tuple-element.17), channel_id=1, source_target_pairs={{0,16},{8,24},{16,0},{24,8},{1,17},{9,25},{17,1},{25,9},{2,18},{10... | collective-permute-start | bytes 393224 | tf_op jit(solution)/shard_map/ppermute | solution.py:89
  6.9 0.0 collective-permute-start.10
  6.9 0.1 fusion.17
  7.0 1.8 %collective-permute-start = (bf16[128,1024]{1,0:T(8,128)(2,1)S(1)}, bf16[128,1024]{1,0:T(8,128)(2,1)S(1)}, u32[]{:S(2)}, u32[]{:S(2)}) collective-permute-start(bf16[128,1024]{1,0:T(8,128)(2,1)S(1)} %get-tuple-element.20), channel_id=1, source_target_pairs={{0,4},{4,0},{1,5},{5,1},{2,6},{6,2},{3,7},{7,3},{8,12},{12,8},{9,1... | collective-permute-start | bytes 786440 | tf_op jit(solution)/shard_map/ppermute | solution.py:74
  8.8 0.7 %broadcast_xor_fusion = s32[4]{0:T(128)S(1)} fusion(s32[4]{0:T(128)} %constant.75.clone, s32[]{:T(128)S(6)} %axis_index.32), kind=kLoop, calls=%fused_computation.69 | loop fusion | flops 4 | bytes 36 | tf_op jit(solution)/shard_map/xor | solution.py:124
  9.4 0.1 stack.102
  9.5 0.1 iota_compare_fusion
  9.6 0.0 collective-permute-done.2
  9.6 1.5 %collective-permute-start.3 = (bf16[64,1024]{1,0:T(8,128)(2,1)S(1)}, bf16[64,1024]{1,0:T(8,128)(2,1)S(1)}, u32[]{:S(2)}, u32[]{:S(2)}) collective-permute-start(bf16[64,1024]{1,0:T(8,128)(2,1)S(1)} %collective-permute-done.2), channel_id=1, source_target_pairs={{0,4},{4,0},{1,5},{5,1},{2,6},{6,2},{3,7},{7,3},{8,12},{12,8},{9,1... | collective-permute-start | bytes 393224 | tf_op jit(solution)/shard_map/ppermute | solution.py:74
  11.1 6.1 %collective-permute-done.6 = bf16[64,1024]{1,0:T(8,128)(2,1)S(1)} collective-permute-done((bf16[64,1024]{1,0:T(8,128)(2,1)S(1)}, bf16[64,1024]{1,0:T(8,128)(2,1)S(1)}, u32[]{:S(2)}, u32[]{:S(2)}) %collective-permute-start.6) | collective-permute-done | bytes 131104 | tf_op jit(solution)/shard_map/ppermute | solution.py:89
  17.2 1.5 %collective-permute-start.7 = (bf16[64,1024]{1,0:T(8,128)(2,1)S(1)}, bf16[64,1024]{1,0:T(8,128)(2,1)S(1)}, u32[]{:S(2)}, u32[]{:S(2)}) collective-permute-start(bf16[64,1024]{1,0:T(8,128)(2,1)S(1)} %collective-permute-done.6), channel_id=1, source_target_pairs={{0,4},{4,0},{1,5},{5,1},{2,6},{6,2},{3,7},{7,3},{8,12},{12,8},{9,1... | collective-permute-start | bytes 393224 | tf_op jit(solution)/shard_map/ppermute | solution.py:74
  18.8 0.0 collective-permute-done.10
  18.8 1.6 %collective-permute-start.11 = (bf16[64,1024]{1,0:T(8,128)(2,1)S(1)}, bf16[64,1024]{1,0:T(8,128)(2,1)S(1)}, u32[]{:S(2)}, u32[]{:S(2)}) collective-permute-start(bf16[64,1024]{1,0:T(8,128)(2,1)S(1)} %collective-permute-done.10), channel_id=1, source_target_pairs={{0,2},{1,3},{2,0},{3,1},{4,6},{5,7},{6,4},{7,5},{8,10},{9,11},{10,... | collective-permute-start | bytes 393224 | tf_op jit(solution)/shard_map/ppermute | solution.py:92
  20.3 0.0 collective-permute-done.3
  20.4 0.6 collective-permute-start.4
  21.0 1.2 %collective-permute-done.7 = bf16[64,1024]{1,0:T(8,128)(2,1)S(1)} collective-permute-done((bf16[64,1024]{1,0:T(8,128)(2,1)S(1)}, bf16[64,1024]{1,0:T(8,128)(2,1)S(1)}, u32[]{:S(2)}, u32[]{:S(2)}) %collective-permute-start.7) | collective-permute-done | bytes 131104 | tf_op jit(solution)/shard_map/ppermute | solution.py:74
  22.2 2.3 %collective-permute-start.8 = (bf16[2,64,1024]{2,1,0:T(8,128)(2,1)S(1)}, bf16[2,64,1024]{2,1,0:T(8,128)(2,1)S(1)}, u32[]{:S(2)}, u32[]{:S(2)}) collective-permute-start(bf16[2,64,1024]{2,1,0:T(8,128)(2,1)S(1)} %pad_maximum_fusion.6), channel_id=1, source_target_pairs={{0,2},{1,3},{2,0},{3,1},{4,6},{5,7},{6,4},{7,5},{8,10},{9,11},{10,... | collective-permute-start | bytes 786440 | tf_op jit(solution)/shard_map/ppermute | solution.py:79
  24.5 0.7 %collective-permute-done.11 = bf16[64,1024]{1,0:T(8,128)(2,1)S(1)} collective-permute-done((bf16[64,1024]{1,0:T(8,128)(2,1)S(1)}, bf16[64,1024]{1,0:T(8,128)(2,1)S(1)}, u32[]{:S(2)}, u32[]{:S(2)}) %collective-permute-start.11) | collective-permute-done | bytes 131104 | tf_op jit(solution)/shard_map/ppermute | solution.py:92
  25.3 0.9 %collective-permute-start.12 = (bf16[128,1024]{1,0:T(8,128)(2,1)S(1)}, bf16[128,1024]{1,0:T(8,128)(2,1)S(1)}, u32[]{:S(2)}, u32[]{:S(2)}) collective-permute-start(bf16[128,1024]{1,0:T(8,128)(2,1)S(1)} %constant_dynamic-update-slice_fusion), channel_id=1, source_target_pairs={{0,4},{4,0},{1,5},{5,1},{2,6},{6,2},{3,7},{7,3},{8,12},{12,8},{9,1... | collective-permute-start | bytes 786440 | tf_op jit(solution)/shard_map/ppermute | solution.py:74
  26.1 0.0 collective-permute-done
  26.2 0.1 pad_maximum_fusion
  26.2 0.1 collective-permute-start.1
  26.3 2.2 %collective-permute-done.4 = bf16[2,64,1024]{2,1,0:T(8,128)(2,1)S(1)} collective-permute-done((bf16[2,64,1024]{2,1,0:T(8,128)(2,1)S(1)}, bf16[2,64,1024]{2,1,0:T(8,128)(2,1)S(1)}, u32[]{:S(2)}, u32[]{:S(2)}) %collective-permute-start.4) | collective-permute-done | bytes 262176 | tf_op jit(solution)/shard_map/ppermute | solution.py:79
  28.6 0.1 collective-permute-start.5
  28.7 2.7 %collective-permute-done.8 = bf16[2,64,1024]{2,1,0:T(8,128)(2,1)S(1)} collective-permute-done((bf16[2,64,1024]{2,1,0:T(8,128)(2,1)S(1)}, bf16[2,64,1024]{2,1,0:T(8,128)(2,1)S(1)}, u32[]{:S(2)}, u32[]{:S(2)}) %collective-permute-start.8) | collective-permute-done | bytes 262176 | tf_op jit(solution)/shard_map/ppermute | solution.py:79
  31.4 0.1 collective-permute-start.9
  31.5 0.3 collective-permute-done.12
  31.7 0.1 pad_maximum_fusion.3
  31.8 0.3 collective-permute-start.13
  32.1 0.0 copy-done.3
  32.1 0.2 multiply_reduce_fusion
  32.3 0.0 collective-permute-done.1
  32.3 0.5 broadcast_in_dim.137
  32.8 0.1 maximum_dynamic-update-slice_fusion
  32.9 0.0 collective-permute-done.5
  33.0 0.1 maximum_dynamic-update-slice_fusion.1
  33.1 0.3 collective-permute-done.9
  33.4 0.1 maximum_dynamic-update-slice_fusion.2
  33.5 0.6 %collective-permute-done.13 = bf16[2,128,1024]{2,1,0:T(8,128)(2,1)S(1)} collective-permute-done((bf16[2,128,1024]{2,1,0:T(8,128)(2,1)S(1)}, bf16[2,128,1024]{2,1,0:T(8,128)(2,1)S(1)}, u32[]{:S(2)}, u32[]{:S(2)}) %collective-permute-start.13) | collective-permute-done | bytes 524320 | tf_op jit(solution)/shard_map/ppermute | solution.py:95
  34.1 0.1 maximum_dynamic-update-slice_fusion.3
  34.2 0.0 copy-start.1
  34.2 4.6 %fusion.20 = (f32[2048]{0:T(1024)S(1)}, f32[2048,512]{1,0:T(8,128)}) fusion(f32[512]{0:T(512)S(1)} %multiply_reduce_fusion, bf16[2048,1024]{1,0:T(8,128)(2,1)S(1)} %bitcast.96, f32[512,1024]{1,0:T(8,128)S(1)} %copy-done.3), kind=kOutput, calls=%fused_computation.72 | convolution fusion | flops 2152200192 | bytes 10496000 | tf_op jit(solution)/shard_map/dot_general | solution.py:10
  38.8 0.1 broadcast_in_dim.140
  38.9 3.3 %exponential_reduce_fusion = f32[2048]{0:T(1024)S(1)} fusion(f32[2048,512]{1,0:T(8,128)} %get-tuple-element.28, f32[2048]{0:T(1024)S(1)} %get-tuple-element.27), kind=kLoop, calls=%fused_computation.4 | loop fusion | flops 2095104 | bytes 4210688 | tf_op jit(solution)/shard_map/reduce_sum | solution.py:18
  42.2 0.1 broadcast_in_dim.145
  42.3 0.1 select_reduce_fusion.7
  42.4 0.2 select_reduce_fusion.3
  42.6 0.2 collective-permute-start.14
  42.8 1.1 %collective-permute-done.14 = f32[2,8,4,64]{3,2,1,0:T(4,128)S(1)} collective-permute-done((f32[2,8,4,64]{3,2,1,0:T(4,128)S(1)}, f32[2,8,4,64]{3,2,1,0:T(4,128)S(1)}, u32[]{:S(2)}, u32[]{:S(2)}) %collective-permute-start.14) | collective-permute-done | bytes 16416 | tf_op jit(solution)/shard_map/ppermute | solution.py:147
  43.9 1.6 %collective-permute-start.15 = (f32[2,8,4,64]{3,2,1,0:T(4,128)S(1)}, f32[2,8,4,64]{3,2,1,0:T(4,128)S(1)}, u32[]{:S(2)}, u32[]{:S(2)}) collective-permute-start(f32[2,8,4,64]{3,2,1,0:T(4,128)S(1)} %pad_maximum_fusion.8), channel_id=1, source_target_pairs={{0,2},{1,3},{2,0},{3,1},{4,6},{5,7},{6,4},{7,5},{8,10},{9,11},{10,... | collective-permute-start | bytes 49160 | tf_op jit(solution)/shard_map/ppermute | solution.py:147
  45.5 2.4 %collective-permute-done.15 = f32[2,8,4,64]{3,2,1,0:T(4,128)S(1)} collective-permute-done((f32[2,8,4,64]{3,2,1,0:T(4,128)S(1)}, f32[2,8,4,64]{3,2,1,0:T(4,128)S(1)}, u32[]{:S(2)}, u32[]{:S(2)}) %collective-permute-start.15) | collective-permute-done | bytes 16416 | tf_op jit(solution)/shard_map/ppermute | solution.py:147
  48.0 1.6 %collective-permute-start.16 = (f32[2,8,4,64]{3,2,1,0:T(4,128)S(1)}, f32[2,8,4,64]{3,2,1,0:T(4,128)S(1)}, u32[]{:S(2)}, u32[]{:S(2)}) collective-permute-start(f32[2,8,4,64]{3,2,1,0:T(4,128)S(1)} %pad_maximum_fusion.9), channel_id=1, source_target_pairs={{0,4},{4,0},{1,5},{5,1},{2,6},{6,2},{3,7},{7,3},{8,12},{12,8},{9,1... | collective-permute-start | bytes 49160 | tf_op jit(solution)/shard_map/ppermute | solution.py:147
  49.5 2.4 %collective-permute-done.16 = f32[2,8,4,64]{3,2,1,0:T(4,128)S(1)} collective-permute-done((f32[2,8,4,64]{3,2,1,0:T(4,128)S(1)}, f32[2,8,4,64]{3,2,1,0:T(4,128)S(1)}, u32[]{:S(2)}, u32[]{:S(2)}) %collective-permute-start.16) | collective-permute-done | bytes 16416 | tf_op jit(solution)/shard_map/ppermute | solution.py:147
  52.0 0.1 select_reduce_fusion.1
  52.1 0.1 select_reduce_fusion.5
  52.2 0.1 div.55
  52.3 0.1 sub.100
  52.4 2.8 %bitcast_reduce_fusion = f32[4,512]{1,0:T(4,128)S(1)} fusion(f32[2048]{0:T(1024)S(1)} %div.55, f32[2048,512]{1,0:T(8,128)} %get-tuple-element.28, f32[2048]{0:T(1024)S(1)} %sub.100), kind=kLoop, calls=%fused_computation.2 | loop fusion | flops 5240832 | bytes 4218880 | tf_op jit(solution)/shard_map/reduce_sum | solution.py:164
  55.3 0.6 copy-done
  55.8 1.0 %fusion = bf16[2048,512]{1,0:T(8,128)(2,1)S(1)} fusion(f32[4,512]{1,0:T(4,128)S(1)} %broadcast_add_fusion, f32[2048]{0:T(1024)S(1)} %div.55, f32[2048,512]{1,0:T(8,128)S(1)} %copy-done, f32[2048]{0:T(1024)S(1)} %sub.100), kind=kLoop, calls=%fused_computation.1 | loop fusion | flops 6291456 | bytes 6316032 | tf_op jit(solution)/shard_map/convert_element_type | solution.py:165
  56.8 0.7 %copy-done.2 = bf16[8,256,1024]{2,1,0:T(8,128)(2,1)S(1)} copy-done((bf16[8,256,1024]{2,1,0:T(8,128)(2,1)S(1)}, bf16[8,256,1024]{2,1,0:T(8,128)(2,1)}, u32[]{:S(2)}) %copy-start.2) | copy-done | bytes 4194328
  57.6 3.7 %subtract_multiply_fusion.1 = f32[512,1024]{1,0:T(8,128)} fusion(f32[512,1024]{1,0:T(8,128)S(1)} %copy-done.3, bf16[2048,512]{1,0:T(8,128)(2,1)S(1)} %fusion, bf16[2048,1024]{1,0:T(8,128)(2,1)S(1)} %bitcast.97, f32[512]{0:T(512)S(1)} %fusion.16), kind=kOutput, calls=%fused_computation.7 | convolution fusion | flops 2149056512 | bytes 10487808 | tf_op jit(solution)/shard_map/dot_general | solution.py:166
  (24 shorter events, 0.3 us)
Async XLA Ops:
  0.0 32.1 %copy-start.3 = (f32[512,1024]{1,0:T(8,128)S(1)}, f32[512,1024]{1,0:T(8,128)}, u32[]{:S(2)}) copy-start(f32[512,1024]{1,0:T(8,128)} %param.4) | copy-start | bytes 6291460
  1.2 8.4 %collective-permute-start.2 = (bf16[64,1024]{1,0:T(8,128)(2,1)S(1)}, bf16[64,1024]{1,0:T(8,128)(2,1)S(1)}, u32[]{:S(2)}, u32[]{:S(2)}) collective-permute-start(bf16[64,1024]{1,0:T(8,128)(2,1)S(1)} %get-tuple-element.17), channel_id=1, source_target_pairs={{0,8},{8,0},{16,24},{24,16},{1,9},{9,1},{17,25},{25,17},{2,10},{10... | collective-permute-start | bytes 393224 | tf_op jit(solution)/shard_map/ppermute | solution.py:89
  4.3 12.9 %collective-permute-start.6 = (bf16[64,1024]{1,0:T(8,128)(2,1)S(1)}, bf16[64,1024]{1,0:T(8,128)(2,1)S(1)}, u32[]{:S(2)}, u32[]{:S(2)}) collective-permute-start(bf16[64,1024]{1,0:T(8,128)(2,1)S(1)} %get-tuple-element.17), channel_id=1, source_target_pairs={{0,16},{8,24},{16,0},{24,8},{1,17},{9,25},{17,1},{25,9},{2,18},{10... | collective-permute-start | bytes 393224 | tf_op jit(solution)/shard_map/ppermute | solution.py:89
  6.9 11.9 %collective-permute-start.10 = (bf16[64,1024]{1,0:T(8,128)(2,1)S(1)}, bf16[64,1024]{1,0:T(8,128)(2,1)S(1)}, u32[]{:S(2)}, u32[]{:S(2)}) collective-permute-start(bf16[64,1024]{1,0:T(8,128)(2,1)S(1)} %get-tuple-element.17), channel_id=1, source_target_pairs={{0,24},{8,16},{16,8},{24,0},{1,25},{9,17},{17,9},{25,1},{2,26},{10... | collective-permute-start | bytes 393224 | tf_op jit(solution)/shard_map/ppermute | solution.py:89
  7.0 19.2 %collective-permute-start = (bf16[128,1024]{1,0:T(8,128)(2,1)S(1)}, bf16[128,1024]{1,0:T(8,128)(2,1)S(1)}, u32[]{:S(2)}, u32[]{:S(2)}) collective-permute-start(bf16[128,1024]{1,0:T(8,128)(2,1)S(1)} %get-tuple-element.20), channel_id=1, source_target_pairs={{0,4},{4,0},{1,5},{5,1},{2,6},{6,2},{3,7},{7,3},{8,12},{12,8},{9,1... | collective-permute-start | bytes 786440 | tf_op jit(solution)/shard_map/ppermute | solution.py:74
  9.6 10.7 %collective-permute-start.3 = (bf16[64,1024]{1,0:T(8,128)(2,1)S(1)}, bf16[64,1024]{1,0:T(8,128)(2,1)S(1)}, u32[]{:S(2)}, u32[]{:S(2)}) collective-permute-start(bf16[64,1024]{1,0:T(8,128)(2,1)S(1)} %collective-permute-done.2), channel_id=1, source_target_pairs={{0,4},{4,0},{1,5},{5,1},{2,6},{6,2},{3,7},{7,3},{8,12},{12,8},{9,1... | collective-permute-start | bytes 393224 | tf_op jit(solution)/shard_map/ppermute | solution.py:74
  17.2 5.0 %collective-permute-start.7 = (bf16[64,1024]{1,0:T(8,128)(2,1)S(1)}, bf16[64,1024]{1,0:T(8,128)(2,1)S(1)}, u32[]{:S(2)}, u32[]{:S(2)}) collective-permute-start(bf16[64,1024]{1,0:T(8,128)(2,1)S(1)} %collective-permute-done.6), channel_id=1, source_target_pairs={{0,4},{4,0},{1,5},{5,1},{2,6},{6,2},{3,7},{7,3},{8,12},{12,8},{9,1... | collective-permute-start | bytes 393224 | tf_op jit(solution)/shard_map/ppermute | solution.py:74
  18.8 6.5 %collective-permute-start.11 = (bf16[64,1024]{1,0:T(8,128)(2,1)S(1)}, bf16[64,1024]{1,0:T(8,128)(2,1)S(1)}, u32[]{:S(2)}, u32[]{:S(2)}) collective-permute-start(bf16[64,1024]{1,0:T(8,128)(2,1)S(1)} %collective-permute-done.10), channel_id=1, source_target_pairs={{0,2},{1,3},{2,0},{3,1},{4,6},{5,7},{6,4},{7,5},{8,10},{9,11},{10,... | collective-permute-start | bytes 393224 | tf_op jit(solution)/shard_map/ppermute | solution.py:92
  20.4 8.2 %collective-permute-start.4 = (bf16[2,64,1024]{2,1,0:T(8,128)(2,1)S(1)}, bf16[2,64,1024]{2,1,0:T(8,128)(2,1)S(1)}, u32[]{:S(2)}, u32[]{:S(2)}) collective-permute-start(bf16[2,64,1024]{2,1,0:T(8,128)(2,1)S(1)} %pad_maximum_fusion.5), channel_id=1, source_target_pairs={{0,2},{1,3},{2,0},{3,1},{4,6},{5,7},{6,4},{7,5},{8,10},{9,11},{10,... | collective-permute-start | bytes 786440 | tf_op jit(solution)/shard_map/ppermute | solution.py:79
  22.2 9.1 %collective-permute-start.8 = (bf16[2,64,1024]{2,1,0:T(8,128)(2,1)S(1)}, bf16[2,64,1024]{2,1,0:T(8,128)(2,1)S(1)}, u32[]{:S(2)}, u32[]{:S(2)}) collective-permute-start(bf16[2,64,1024]{2,1,0:T(8,128)(2,1)S(1)} %pad_maximum_fusion.6), channel_id=1, source_target_pairs={{0,2},{1,3},{2,0},{3,1},{4,6},{5,7},{6,4},{7,5},{8,10},{9,11},{10,... | collective-permute-start | bytes 786440 | tf_op jit(solution)/shard_map/ppermute | solution.py:79
  25.3 6.4 %collective-permute-start.12 = (bf16[128,1024]{1,0:T(8,128)(2,1)S(1)}, bf16[128,1024]{1,0:T(8,128)(2,1)S(1)}, u32[]{:S(2)}, u32[]{:S(2)}) collective-permute-start(bf16[128,1024]{1,0:T(8,128)(2,1)S(1)} %constant_dynamic-update-slice_fusion), channel_id=1, source_target_pairs={{0,4},{4,0},{1,5},{5,1},{2,6},{6,2},{3,7},{7,3},{8,12},{12,8},{9,1... | collective-permute-start | bytes 786440 | tf_op jit(solution)/shard_map/ppermute | solution.py:74
  26.2 6.1 %collective-permute-start.1 = (bf16[2,128,1024]{2,1,0:T(8,128)(2,1)S(1)}, bf16[2,128,1024]{2,1,0:T(8,128)(2,1)S(1)}, u32[]{:S(2)}, u32[]{:S(2)}) collective-permute-start(bf16[2,128,1024]{2,1,0:T(8,128)(2,1)S(1)} %pad_maximum_fusion), channel_id=1, source_target_pairs={{0,1},{1,0},{2,3},{3,2},{4,5},{5,4},{6,7},{7,6},{8,9},{9,8},{10,11... | collective-permute-start | bytes 1572872 | tf_op jit(solution)/shard_map/ppermute | solution.py:108
  28.6 4.4 %collective-permute-start.5 = (bf16[2,128,1024]{2,1,0:T(8,128)(2,1)S(1)}, bf16[2,128,1024]{2,1,0:T(8,128)(2,1)S(1)}, u32[]{:S(2)}, u32[]{:S(2)}) collective-permute-start(bf16[2,128,1024]{2,1,0:T(8,128)(2,1)S(1)} %pad_maximum_fusion.1), channel_id=1, source_target_pairs={{0,1},{1,0},{2,3},{3,2},{4,5},{5,4},{6,7},{7,6},{8,9},{9,8},{10,11... | collective-permute-start | bytes 1572872 | tf_op jit(solution)/shard_map/ppermute | solution.py:79
  31.4 2.0 %collective-permute-start.9 = (bf16[2,128,1024]{2,1,0:T(8,128)(2,1)S(1)}, bf16[2,128,1024]{2,1,0:T(8,128)(2,1)S(1)}, u32[]{:S(2)}, u32[]{:S(2)}) collective-permute-start(bf16[2,128,1024]{2,1,0:T(8,128)(2,1)S(1)} %pad_maximum_fusion.2), channel_id=1, source_target_pairs={{0,1},{1,0},{2,3},{3,2},{4,5},{5,4},{6,7},{7,6},{8,9},{9,8},{10,11... | collective-permute-start | bytes 1572872 | tf_op jit(solution)/shard_map/ppermute | solution.py:79
  31.8 2.3 %collective-permute-start.13 = (bf16[2,128,1024]{2,1,0:T(8,128)(2,1)S(1)}, bf16[2,128,1024]{2,1,0:T(8,128)(2,1)S(1)}, u32[]{:S(2)}, u32[]{:S(2)}) collective-permute-start(bf16[2,128,1024]{2,1,0:T(8,128)(2,1)S(1)} %pad_maximum_fusion.3), channel_id=1, source_target_pairs={{0,1},{1,0},{2,3},{3,2},{4,5},{5,4},{6,7},{7,6},{8,9},{9,8},{10,11... | collective-permute-start | bytes 1572872 | tf_op jit(solution)/shard_map/ppermute | solution.py:95
  34.2 4.6 %copy-start.1 = (bf16[8,256,1024]{2,1,0:T(8,128)(2,1)}, bf16[8,256,1024]{2,1,0:T(8,128)(2,1)S(1)}, u32[]{:S(2)}) copy-start(bf16[8,256,1024]{2,1,0:T(8,128)(2,1)S(1)} %maximum_dynamic-update-slice_fusion.3) | copy-start | bytes 12582916
  42.6 1.3 %collective-permute-start.14 = (f32[2,8,4,64]{3,2,1,0:T(4,128)S(1)}, f32[2,8,4,64]{3,2,1,0:T(4,128)S(1)}, u32[]{:S(2)}, u32[]{:S(2)}) collective-permute-start(f32[2,8,4,64]{3,2,1,0:T(4,128)S(1)} %pad_maximum_fusion.7), channel_id=1, source_target_pairs={{0,1},{1,0},{2,3},{3,2},{4,5},{5,4},{6,7},{7,6},{8,9},{9,8},{10,11... | collective-permute-start | bytes 49160 | tf_op jit(solution)/shard_map/ppermute | solution.py:147
  43.9 4.0 %collective-permute-start.15 = (f32[2,8,4,64]{3,2,1,0:T(4,128)S(1)}, f32[2,8,4,64]{3,2,1,0:T(4,128)S(1)}, u32[]{:S(2)}, u32[]{:S(2)}) collective-permute-start(f32[2,8,4,64]{3,2,1,0:T(4,128)S(1)} %pad_maximum_fusion.8), channel_id=1, source_target_pairs={{0,2},{1,3},{2,0},{3,1},{4,6},{5,7},{6,4},{7,5},{8,10},{9,11},{10,... | collective-permute-start | bytes 49160 | tf_op jit(solution)/shard_map/ppermute | solution.py:147
  48.0 4.0 %collective-permute-start.16 = (f32[2,8,4,64]{3,2,1,0:T(4,128)S(1)}, f32[2,8,4,64]{3,2,1,0:T(4,128)S(1)}, u32[]{:S(2)}, u32[]{:S(2)}) collective-permute-start(f32[2,8,4,64]{3,2,1,0:T(4,128)S(1)} %pad_maximum_fusion.9), channel_id=1, source_target_pairs={{0,4},{4,0},{1,5},{5,1},{2,6},{6,2},{3,7},{7,3},{8,12},{12,8},{9,1... | collective-permute-start | bytes 49160 | tf_op jit(solution)/shard_map/ppermute | solution.py:147
  52.4 3.4 %copy-start = (f32[2048,512]{1,0:T(8,128)S(1)}, f32[2048,512]{1,0:T(8,128)}, u32[]{:S(2)}) copy-start(f32[2048,512]{1,0:T(8,128)} %get-tuple-element.28) | copy-start | bytes 12582916
  55.2 2.3 %copy-start.2 = (bf16[8,256,1024]{2,1,0:T(8,128)(2,1)S(1)}, bf16[8,256,1024]{2,1,0:T(8,128)(2,1)}, u32[]{:S(2)}) copy-start(bf16[8,256,1024]{2,1,0:T(8,128)(2,1)} %copy-done.1) | copy-start | bytes 12582916

commit v31 on v29

--- a/solution.py
+++ b/solution.py
@@ -138,11 +138,12 @@
     peak_abs = to_absolute(local_max)
     mass_abs = to_absolute(local_sum)
     if n_d & (n_d - 1) == 0:
-        rounds = [("cent", bit, n_c) for bit in bits]
+        rounds = []
         bd = 1
         while bd < n_d:
             rounds.append(("dp", bd, n_d))
             bd *= 2
+        rounds += [("cent", bit, n_c) for bit in reversed(bits)]
         for axis, bit, n in rounds:
             other = lax.ppermute(jnp.stack([peak_abs, mass_abs]), axis, [(i, i ^ bit) for i in range(n)])
             top = jnp.maximum(peak_abs, other[0])

time: 60.7 us -> 60.7 us (level)
  no operation moved by 1% of the time
where the time goes in v31:
time: 60.7 us; the launch traced here: 60.5 us
  waiting for transfers between devices  20.7 us (34%)
  starting transfers between devices  18.4 us (30%)
  other arithmetic  9.33 us (15%)
  matrix products  8.28 us (14%)
  local copies, waits for them, and re-layouts  3.49 us (6%)
    ppermute x3, waiting for transfers between devices, shards_all(): lax.ppermute(jnp.stack([peak_abs, mass_abs]), axis, [(i, i ^ bit) for i i...  6.6 us
    ppermute x3, waiting for transfers between devices, shards_all(): landed.append(lax.ppermute(mine, 'outer', pairs))  6.05 us
    ppermute x3, starting transfers between devices, shards_all(): landed.append(lax.ppermute(mine, 'outer', pairs))  5.68 us
    ppermute x4, waiting for transfers between devices, pair_of(): lax.ppermute(piece, 'dp', [(j, (j + sy) % n_d) for j in range(n_d)])  5.63 us
    ppermute x4, starting transfers between devices, pair_of(): lax.ppermute(piece, 'dp', [(j, (j + sy) % n_d) for j in range(n_d)])  5.48 us
    dot_general x1, matrix products, scores_for(): lax.dot_general(piece, cent_bf, (((1,), (1,)), ((), ())), preferred_eleme...  4.61 us
    dot_general x1, matrix products, shards_all(): lax.dot_general(scaled.reshape(n_o * pod, k), everything, (((0,), (0,)),...  3.67 us
    reduce_sum x1, other arithmetic, row_summary(): local_sum = jnp.sum(jnp.exp(logits - local_max[:, None]), axis=1)  3.31 us
  transfers between devices with their start and end apart: 17, of which 9 were waited for; matrix products, arithmetic and copies ran while one was open for 4% of the time, Pallas kernels for 0%

profile of v31, /device:TPU:0, one launch (start us, length us, event | category | flops | bytes accessed | tf_op | source)
XLA Modules:
  0.0 60.5 jit_solution(16085079559638058549)
XLA Ops:
  0.0 1.2 %dynamic-slice_convert_fusion.1 = (bf16[64,1024]{1,0:T(8,128)(2,1)S(1)}, bf16[64,1024]{1,0:T(8,128)(2,1)S(1)}) fusion(f32[256,1024]{1,0:T(8,128)} %param.3, s32[]{:T(128)S(6)} %select_n.69, s32[]{:T(128)S(6)} %select_n.70), kind=kLoop, calls=%fused_computation.21 | loop fusion | bytes 524296 | tf_op jit(solution)/shard_map/convert_element_type | solution.py:69
  1.2 3.1 %collective-permute-start.2 = (bf16[64,1024]{1,0:T(8,128)(2,1)S(1)}, bf16[64,1024]{1,0:T(8,128)(2,1)S(1)}, u32[]{:S(2)}, u32[]{:S(2)}) collective-permute-start(bf16[64,1024]{1,0:T(8,128)(2,1)S(1)} %get-tuple-element.17), channel_id=1, source_target_pairs={{0,8},{8,0},{16,24},{24,16},{1,9},{9,1},{17,25},{25,17},{2,10},{10... | collective-permute-start | bytes 393224 | tf_op jit(solution)/shard_map/ppermute | solution.py:89
  4.3 2.6 %collective-permute-start.6 = (bf16[64,1024]{1,0:T(8,128)(2,1)S(1)}, bf16[64,1024]{1,0:T(8,128)(2,1)S(1)}, u32[]{:S(2)}, u32[]{:S(2)}) collective-permute-start(bf16[64,1024]{1,0:T(8,128)(2,1)S(1)} %get-tuple-element.17), channel_id=1, source_target_pairs={{0,16},{8,24},{16,0},{24,8},{1,17},{9,25},{17,1},{25,9},{2,18},{10... | collective-permute-start | bytes 393224 | tf_op jit(solution)/shard_map/ppermute | solution.py:89
  6.9 0.0 collective-permute-start.10
  6.9 0.1 fusion.17
  7.0 1.8 %collective-permute-start = (bf16[128,1024]{1,0:T(8,128)(2,1)S(1)}, bf16[128,1024]{1,0:T(8,128)(2,1)S(1)}, u32[]{:S(2)}, u32[]{:S(2)}) collective-permute-start(bf16[128,1024]{1,0:T(8,128)(2,1)S(1)} %get-tuple-element.20), channel_id=1, source_target_pairs={{0,4},{4,0},{1,5},{5,1},{2,6},{6,2},{3,7},{7,3},{8,12},{12,8},{9,1... | collective-permute-start | bytes 786440 | tf_op jit(solution)/shard_map/ppermute | solution.py:74
  8.8 0.7 %broadcast_xor_fusion = s32[4]{0:T(128)S(1)} fusion(s32[4]{0:T(128)} %constant.75.clone, s32[]{:T(128)S(6)} %axis_index.32), kind=kLoop, calls=%fused_computation.70 | loop fusion | flops 4 | bytes 36 | tf_op jit(solution)/shard_map/xor | solution.py:124
  9.4 0.1 iota_compare_fusion
  9.5 0.1 stack.102
  9.6 0.0 collective-permute-done.2
  9.6 1.6 %collective-permute-start.3 = (bf16[64,1024]{1,0:T(8,128)(2,1)S(1)}, bf16[64,1024]{1,0:T(8,128)(2,1)S(1)}, u32[]{:S(2)}, u32[]{:S(2)}) collective-permute-start(bf16[64,1024]{1,0:T(8,128)(2,1)S(1)} %collective-permute-done.2), channel_id=1, source_target_pairs={{0,2},{1,3},{2,0},{3,1},{4,6},{5,7},{6,4},{7,5},{8,10},{9,11},{10,... | collective-permute-start | bytes 393224 | tf_op jit(solution)/shard_map/ppermute | solution.py:92
  11.2 6.0 %collective-permute-done.6 = bf16[64,1024]{1,0:T(8,128)(2,1)S(1)} collective-permute-done((bf16[64,1024]{1,0:T(8,128)(2,1)S(1)}, bf16[64,1024]{1,0:T(8,128)(2,1)S(1)}, u32[]{:S(2)}, u32[]{:S(2)}) %collective-permute-start.6) | collective-permute-done | bytes 131104 | tf_op jit(solution)/shard_map/ppermute | solution.py:89
  17.2 1.5 %collective-permute-start.7 = (bf16[64,1024]{1,0:T(8,128)(2,1)S(1)}, bf16[64,1024]{1,0:T(8,128)(2,1)S(1)}, u32[]{:S(2)}, u32[]{:S(2)}) collective-permute-start(bf16[64,1024]{1,0:T(8,128)(2,1)S(1)} %collective-permute-done.6), channel_id=1, source_target_pairs={{0,4},{4,0},{1,5},{5,1},{2,6},{6,2},{3,7},{7,3},{8,12},{12,8},{9,1... | collective-permute-start | bytes 393224 | tf_op jit(solution)/shard_map/ppermute | solution.py:74
  18.8 0.0 collective-permute-done.10
  18.8 1.6 %collective-permute-start.11 = (bf16[64,1024]{1,0:T(8,128)(2,1)S(1)}, bf16[64,1024]{1,0:T(8,128)(2,1)S(1)}, u32[]{:S(2)}, u32[]{:S(2)}) collective-permute-start(bf16[64,1024]{1,0:T(8,128)(2,1)S(1)} %collective-permute-done.10), channel_id=1, source_target_pairs={{0,2},{1,3},{2,0},{3,1},{4,6},{5,7},{6,4},{7,5},{8,10},{9,11},{10,... | collective-permute-start | bytes 393224 | tf_op jit(solution)/shard_map/ppermute | solution.py:92
  20.3 0.0 collective-permute-done.3
  20.3 0.6 collective-permute-start.4
  20.9 2.8 %collective-permute-done.7 = bf16[64,1024]{1,0:T(8,128)(2,1)S(1)} collective-permute-done((bf16[64,1024]{1,0:T(8,128)(2,1)S(1)}, bf16[64,1024]{1,0:T(8,128)(2,1)S(1)}, u32[]{:S(2)}, u32[]{:S(2)}) %collective-permute-start.7) | collective-permute-done | bytes 131104 | tf_op jit(solution)/shard_map/ppermute | solution.py:74
  23.7 1.2 %collective-permute-start.8 = (bf16[2,64,1024]{2,1,0:T(8,128)(2,1)S(1)}, bf16[2,64,1024]{2,1,0:T(8,128)(2,1)S(1)}, u32[]{:S(2)}, u32[]{:S(2)}) collective-permute-start(bf16[2,64,1024]{2,1,0:T(8,128)(2,1)S(1)} %pad_maximum_fusion.5), channel_id=1, source_target_pairs={{0,2},{1,3},{2,0},{3,1},{4,6},{5,7},{6,4},{7,5},{8,10},{9,11},{10,... | collective-permute-start | bytes 786440 | tf_op jit(solution)/shard_map/ppermute | solution.py:79
  24.9 0.0 collective-permute-done.11
  24.9 1.6 %collective-permute-start.12 = (bf16[128,1024]{1,0:T(8,128)(2,1)S(1)}, bf16[128,1024]{1,0:T(8,128)(2,1)S(1)}, u32[]{:S(2)}, u32[]{:S(2)}) collective-permute-start(bf16[128,1024]{1,0:T(8,128)(2,1)S(1)} %constant_dynamic-update-slice_fusion.2), channel_id=1, source_target_pairs={{0,4},{4,0},{1,5},{5,1},{2,6},{6,2},{3,7},{7,3},{8,12},{12,8},{9,1... | collective-permute-start | bytes 786440 | tf_op jit(solution)/shard_map/ppermute | solution.py:74
  26.5 0.0 collective-permute-done
  26.5 0.1 pad_maximum_fusion
  26.5 0.1 collective-permute-start.1
  26.6 1.8 %collective-permute-done.4 = bf16[128,1024]{1,0:T(8,128)(2,1)S(1)} collective-permute-done((bf16[128,1024]{1,0:T(8,128)(2,1)S(1)}, bf16[128,1024]{1,0:T(8,128)(2,1)S(1)}, u32[]{:S(2)}, u32[]{:S(2)}) %collective-permute-start.4) | collective-permute-done | bytes 262176 | tf_op jit(solution)/shard_map/ppermute | solution.py:74
  28.4 0.1 pad_maximum_fusion.1
  28.5 0.1 collective-permute-start.5
  28.6 1.6 %collective-permute-done.8 = bf16[2,64,1024]{2,1,0:T(8,128)(2,1)S(1)} collective-permute-done((bf16[2,64,1024]{2,1,0:T(8,128)(2,1)S(1)}, bf16[2,64,1024]{2,1,0:T(8,128)(2,1)S(1)}, u32[]{:S(2)}, u32[]{:S(2)}) %collective-permute-start.8) | collective-permute-done | bytes 262176 | tf_op jit(solution)/shard_map/ppermute | solution.py:79
  30.2 0.1 collective-permute-start.9
  30.3 1.1 %collective-permute-done.12 = bf16[128,1024]{1,0:T(8,128)(2,1)S(1)} collective-permute-done((bf16[128,1024]{1,0:T(8,128)(2,1)S(1)}, bf16[128,1024]{1,0:T(8,128)(2,1)S(1)}, u32[]{:S(2)}, u32[]{:S(2)}) %collective-permute-start.12) | collective-permute-done | bytes 262176 | tf_op jit(solution)/shard_map/ppermute | solution.py:74
  31.3 0.1 pad_maximum_fusion.3
  31.4 0.1 collective-permute-start.13
  31.5 0.0 copy-done.3
  31.5 0.2 multiply_reduce_fusion
  31.7 0.0 collective-permute-done.1
  31.7 0.5 broadcast_in_dim.137
  32.2 0.1 maximum_dynamic-update-slice_fusion
  32.3 0.0 collective-permute-done.5
  32.4 0.1 maximum_dynamic-update-slice_fusion.1
  32.5 0.0 collective-permute-done.9
  32.5 0.1 maximum_dynamic-update-slice_fusion.2
  32.6 0.8 %collective-permute-done.13 = bf16[2,128,1024]{2,1,0:T(8,128)(2,1)S(1)} collective-permute-done((bf16[2,128,1024]{2,1,0:T(8,128)(2,1)S(1)}, bf16[2,128,1024]{2,1,0:T(8,128)(2,1)S(1)}, u32[]{:S(2)}, u32[]{:S(2)}) %collective-permute-start.13) | collective-permute-done | bytes 524320 | tf_op jit(solution)/shard_map/ppermute | solution.py:95
  33.4 0.1 maximum_dynamic-update-slice_fusion.3
  33.5 4.6 %fusion.20 = (f32[2048]{0:T(1024)S(1)}, f32[2048,512]{1,0:T(8,128)}) fusion(f32[512]{0:T(512)S(1)} %multiply_reduce_fusion, bf16[2048,1024]{1,0:T(8,128)(2,1)S(1)} %bitcast.96, f32[512,1024]{1,0:T(8,128)S(1)} %copy-done.3), kind=kOutput, calls=%fused_computation.73 | convolution fusion | flops 2152200192 | bytes 10496000 | tf_op jit(solution)/shard_map/dot_general | solution.py:10
  38.1 0.1 broadcast_in_dim.140
  38.2 3.3 %exponential_reduce_fusion = f32[2048]{0:T(1024)S(1)} fusion(f32[2048,512]{1,0:T(8,128)} %get-tuple-element.28, f32[2048]{0:T(1024)S(1)} %get-tuple-element.27), kind=kLoop, calls=%fused_computation.4 | loop fusion | flops 2095104 | bytes 4210688 | tf_op jit(solution)/shard_map/reduce_sum | solution.py:18
  41.5 0.1 broadcast_in_dim.145
  41.6 0.1 select_reduce_fusion.7
  41.7 0.2 select_reduce_fusion.3
  41.9 1.6 %collective-permute-start.14 = (f32[2,8,4,64]{3,2,1,0:T(4,128)S(1)}, f32[2,8,4,64]{3,2,1,0:T(4,128)S(1)}, u32[]{:S(2)}, u32[]{:S(2)}) collective-permute-start(f32[2,8,4,64]{3,2,1,0:T(4,128)S(1)} %pad_maximum_fusion.6), channel_id=1, source_target_pairs={{0,4},{4,0},{1,5},{5,1},{2,6},{6,2},{3,7},{7,3},{8,12},{12,8},{9,1... | collective-permute-start | bytes 49160 | tf_op jit(solution)/shard_map/ppermute | solution.py:148
  43.5 2.4 %collective-permute-done.14 = f32[2,8,4,64]{3,2,1,0:T(4,128)S(1)} collective-permute-done((f32[2,8,4,64]{3,2,1,0:T(4,128)S(1)}, f32[2,8,4,64]{3,2,1,0:T(4,128)S(1)}, u32[]{:S(2)}, u32[]{:S(2)}) %collective-permute-start.14) | collective-permute-done | bytes 16416 | tf_op jit(solution)/shard_map/ppermute | solution.py:148
  45.9 1.0 %collective-permute-start.15 = (f32[2,8,4,64]{3,2,1,0:T(4,128)S(1)}, f32[2,8,4,64]{3,2,1,0:T(4,128)S(1)}, u32[]{:S(2)}, u32[]{:S(2)}) collective-permute-start(f32[2,8,4,64]{3,2,1,0:T(4,128)S(1)} %pad_maximum_fusion.7), channel_id=1, source_target_pairs={{0,2},{1,3},{2,0},{3,1},{4,6},{5,7},{6,4},{7,5},{8,10},{9,11},{10,... | collective-permute-start | bytes 49160 | tf_op jit(solution)/shard_map/ppermute | solution.py:148
  46.9 3.0 %collective-permute-done.15 = f32[2,8,4,64]{3,2,1,0:T(4,128)S(1)} collective-permute-done((f32[2,8,4,64]{3,2,1,0:T(4,128)S(1)}, f32[2,8,4,64]{3,2,1,0:T(4,128)S(1)}, u32[]{:S(2)}, u32[]{:S(2)}) %collective-permute-start.15) | collective-permute-done | bytes 16416 | tf_op jit(solution)/shard_map/ppermute | solution.py:148
  49.9 0.1 collective-permute-start.16
  50.0 1.2 %collective-permute-done.16 = f32[2,8,4,64]{3,2,1,0:T(4,128)S(1)} collective-permute-done((f32[2,8,4,64]{3,2,1,0:T(4,128)S(1)}, f32[2,8,4,64]{3,2,1,0:T(4,128)S(1)}, u32[]{:S(2)}, u32[]{:S(2)}) %collective-permute-start.16) | collective-permute-done | bytes 16416 | tf_op jit(solution)/shard_map/ppermute | solution.py:148
  51.2 0.1 select_reduce_fusion.1
  51.3 0.1 select_reduce_fusion.5
  51.5 0.1 div.55
  51.5 0.1 sub.100
  51.6 2.8 %bitcast_reduce_fusion = f32[4,512]{1,0:T(4,128)S(1)} fusion(f32[2048]{0:T(1024)S(1)} %div.55, f32[2048,512]{1,0:T(8,128)} %get-tuple-element.28, f32[2048]{0:T(1024)S(1)} %sub.100), kind=kLoop, calls=%fused_computation.2 | loop fusion | flops 5240832 | bytes 4218880 | tf_op jit(solution)/shard_map/reduce_sum | solution.py:165
  54.5 0.6 copy-done
  55.1 1.0 %fusion = bf16[2048,512]{1,0:T(8,128)(2,1)S(1)} fusion(f32[4,512]{1,0:T(4,128)S(1)} %broadcast_add_fusion, f32[2048]{0:T(1024)S(1)} %div.55, f32[2048,512]{1,0:T(8,128)S(1)} %copy-done, f32[2048]{0:T(1024)S(1)} %sub.100), kind=kLoop, calls=%fused_computation.1 | loop fusion | flops 6291456 | bytes 6316032 | tf_op jit(solution)/shard_map/convert_element_type | solution.py:166
  56.1 0.7 %copy-done.2 = bf16[8,256,1024]{2,1,0:T(8,128)(2,1)S(1)} copy-done((bf16[8,256,1024]{2,1,0:T(8,128)(2,1)S(1)}, bf16[8,256,1024]{2,1,0:T(8,128)(2,1)}, u32[]{:S(2)}) %copy-start.2) | copy-done | bytes 4194328
  56.8 3.7 %subtract_multiply_fusion.1 = f32[512,1024]{1,0:T(8,128)} fusion(f32[512,1024]{1,0:T(8,128)S(1)} %copy-done.3, bf16[2048,512]{1,0:T(8,128)(2,1)S(1)} %fusion, bf16[2048,1024]{1,0:T(8,128)(2,1)S(1)} %bitcast.97, f32[512]{0:T(512)S(1)} %fusion.16), kind=kOutput, calls=%fused_computation.7 | convolution fusion | flops 2149056512 | bytes 10487808 | tf_op jit(solution)/shard_map/dot_general | solution.py:167
  (25 shorter events, 0.3 us)
Async XLA Ops:
  0.0 31.5 %copy-start.3 = (f32[512,1024]{1,0:T(8,128)S(1)}, f32[512,1024]{1,0:T(8,128)}, u32[]{:S(2)}) copy-start(f32[512,1024]{1,0:T(8,128)} %param.4) | copy-start | bytes 6291460
  1.2 8.4 %collective-permute-start.2 = (bf16[64,1024]{1,0:T(8,128)(2,1)S(1)}, bf16[64,1024]{1,0:T(8,128)(2,1)S(1)}, u32[]{:S(2)}, u32[]{:S(2)}) collective-permute-start(bf16[64,1024]{1,0:T(8,128)(2,1)S(1)} %get-tuple-element.17), channel_id=1, source_target_pairs={{0,8},{8,0},{16,24},{24,16},{1,9},{9,1},{17,25},{25,17},{2,10},{10... | collective-permute-start | bytes 393224 | tf_op jit(solution)/shard_map/ppermute | solution.py:89
  4.3 12.9 %collective-permute-start.6 = (bf16[64,1024]{1,0:T(8,128)(2,1)S(1)}, bf16[64,1024]{1,0:T(8,128)(2,1)S(1)}, u32[]{:S(2)}, u32[]{:S(2)}) collective-permute-start(bf16[64,1024]{1,0:T(8,128)(2,1)S(1)} %get-tuple-element.17), channel_id=1, source_target_pairs={{0,16},{8,24},{16,0},{24,8},{1,17},{9,25},{17,1},{25,9},{2,18},{10... | collective-permute-start | bytes 393224 | tf_op jit(solution)/shard_map/ppermute | solution.py:89
  6.9 11.9 %collective-permute-start.10 = (bf16[64,1024]{1,0:T(8,128)(2,1)S(1)}, bf16[64,1024]{1,0:T(8,128)(2,1)S(1)}, u32[]{:S(2)}, u32[]{:S(2)}) collective-permute-start(bf16[64,1024]{1,0:T(8,128)(2,1)S(1)} %get-tuple-element.17), channel_id=1, source_target_pairs={{0,24},{8,16},{16,8},{24,0},{1,25},{9,17},{17,9},{25,1},{2,26},{10... | collective-permute-start | bytes 393224 | tf_op jit(solution)/shard_map/ppermute | solution.py:89
  7.0 19.5 %collective-permute-start = (bf16[128,1024]{1,0:T(8,128)(2,1)S(1)}, bf16[128,1024]{1,0:T(8,128)(2,1)S(1)}, u32[]{:S(2)}, u32[]{:S(2)}) collective-permute-start(bf16[128,1024]{1,0:T(8,128)(2,1)S(1)} %get-tuple-element.20), channel_id=1, source_target_pairs={{0,4},{4,0},{1,5},{5,1},{2,6},{6,2},{3,7},{7,3},{8,12},{12,8},{9,1... | collective-permute-start | bytes 786440 | tf_op jit(solution)/shard_map/ppermute | solution.py:74
  9.6 10.7 %collective-permute-start.3 = (bf16[64,1024]{1,0:T(8,128)(2,1)S(1)}, bf16[64,1024]{1,0:T(8,128)(2,1)S(1)}, u32[]{:S(2)}, u32[]{:S(2)}) collective-permute-start(bf16[64,1024]{1,0:T(8,128)(2,1)S(1)} %collective-permute-done.2), channel_id=1, source_target_pairs={{0,2},{1,3},{2,0},{3,1},{4,6},{5,7},{6,4},{7,5},{8,10},{9,11},{10,... | collective-permute-start | bytes 393224 | tf_op jit(solution)/shard_map/ppermute | solution.py:92
  17.2 6.4 %collective-permute-start.7 = (bf16[64,1024]{1,0:T(8,128)(2,1)S(1)}, bf16[64,1024]{1,0:T(8,128)(2,1)S(1)}, u32[]{:S(2)}, u32[]{:S(2)}) collective-permute-start(bf16[64,1024]{1,0:T(8,128)(2,1)S(1)} %collective-permute-done.6), channel_id=1, source_target_pairs={{0,4},{4,0},{1,5},{5,1},{2,6},{6,2},{3,7},{7,3},{8,12},{12,8},{9,1... | collective-permute-start | bytes 393224 | tf_op jit(solution)/shard_map/ppermute | solution.py:74
  18.8 6.1 %collective-permute-start.11 = (bf16[64,1024]{1,0:T(8,128)(2,1)S(1)}, bf16[64,1024]{1,0:T(8,128)(2,1)S(1)}, u32[]{:S(2)}, u32[]{:S(2)}) collective-permute-start(bf16[64,1024]{1,0:T(8,128)(2,1)S(1)} %collective-permute-done.10), channel_id=1, source_target_pairs={{0,2},{1,3},{2,0},{3,1},{4,6},{5,7},{6,4},{7,5},{8,10},{9,11},{10,... | collective-permute-start | bytes 393224 | tf_op jit(solution)/shard_map/ppermute | solution.py:92
  20.3 8.1 %collective-permute-start.4 = (bf16[128,1024]{1,0:T(8,128)(2,1)S(1)}, bf16[128,1024]{1,0:T(8,128)(2,1)S(1)}, u32[]{:S(2)}, u32[]{:S(2)}) collective-permute-start(bf16[128,1024]{1,0:T(8,128)(2,1)S(1)} %constant_dynamic-update-slice_fusion), channel_id=1, source_target_pairs={{0,4},{4,0},{1,5},{5,1},{2,6},{6,2},{3,7},{7,3},{8,12},{12,8},{9,1... | collective-permute-start | bytes 786440 | tf_op jit(solution)/shard_map/ppermute | solution.py:74
  23.7 6.4 %collective-permute-start.8 = (bf16[2,64,1024]{2,1,0:T(8,128)(2,1)S(1)}, bf16[2,64,1024]{2,1,0:T(8,128)(2,1)S(1)}, u32[]{:S(2)}, u32[]{:S(2)}) collective-permute-start(bf16[2,64,1024]{2,1,0:T(8,128)(2,1)S(1)} %pad_maximum_fusion.5), channel_id=1, source_target_pairs={{0,2},{1,3},{2,0},{3,1},{4,6},{5,7},{6,4},{7,5},{8,10},{9,11},{10,... | collective-permute-start | bytes 786440 | tf_op jit(solution)/shard_map/ppermute | solution.py:79
  24.9 6.4 %collective-permute-start.12 = (bf16[128,1024]{1,0:T(8,128)(2,1)S(1)}, bf16[128,1024]{1,0:T(8,128)(2,1)S(1)}, u32[]{:S(2)}, u32[]{:S(2)}) collective-permute-start(bf16[128,1024]{1,0:T(8,128)(2,1)S(1)} %constant_dynamic-update-slice_fusion.2), channel_id=1, source_target_pairs={{0,4},{4,0},{1,5},{5,1},{2,6},{6,2},{3,7},{7,3},{8,12},{12,8},{9,1... | collective-permute-start | bytes 786440 | tf_op jit(solution)/shard_map/ppermute | solution.py:74
  26.5 5.2 %collective-permute-start.1 = (bf16[2,128,1024]{2,1,0:T(8,128)(2,1)S(1)}, bf16[2,128,1024]{2,1,0:T(8,128)(2,1)S(1)}, u32[]{:S(2)}, u32[]{:S(2)}) collective-permute-start(bf16[2,128,1024]{2,1,0:T(8,128)(2,1)S(1)} %pad_maximum_fusion), channel_id=1, source_target_pairs={{0,1},{1,0},{2,3},{3,2},{4,5},{5,4},{6,7},{7,6},{8,9},{9,8},{10,11... | collective-permute-start | bytes 1572872 | tf_op jit(solution)/shard_map/ppermute | solution.py:108
  28.5 3.9 %collective-permute-start.5 = (bf16[2,128,1024]{2,1,0:T(8,128)(2,1)S(1)}, bf16[2,128,1024]{2,1,0:T(8,128)(2,1)S(1)}, u32[]{:S(2)}, u32[]{:S(2)}) collective-permute-start(bf16[2,128,1024]{2,1,0:T(8,128)(2,1)S(1)} %pad_maximum_fusion.1), channel_id=1, source_target_pairs={{0,1},{1,0},{2,3},{3,2},{4,5},{5,4},{6,7},{7,6},{8,9},{9,8},{10,11... | collective-permute-start | bytes 1572872 | tf_op jit(solution)/shard_map/ppermute | solution.py:95
  30.2 2.3 %collective-permute-start.9 = (bf16[2,128,1024]{2,1,0:T(8,128)(2,1)S(1)}, bf16[2,128,1024]{2,1,0:T(8,128)(2,1)S(1)}, u32[]{:S(2)}, u32[]{:S(2)}) collective-permute-start(bf16[2,128,1024]{2,1,0:T(8,128)(2,1)S(1)} %pad_maximum_fusion.2), channel_id=1, source_target_pairs={{0,1},{1,0},{2,3},{3,2},{4,5},{5,4},{6,7},{7,6},{8,9},{9,8},{10,11... | collective-permute-start | bytes 1572872 | tf_op jit(solution)/shard_map/ppermute | solution.py:79
  31.4 2.0 %collective-permute-start.13 = (bf16[2,128,1024]{2,1,0:T(8,128)(2,1)S(1)}, bf16[2,128,1024]{2,1,0:T(8,128)(2,1)S(1)}, u32[]{:S(2)}, u32[]{:S(2)}) collective-permute-start(bf16[2,128,1024]{2,1,0:T(8,128)(2,1)S(1)} %pad_maximum_fusion.3), channel_id=1, source_target_pairs={{0,1},{1,0},{2,3},{3,2},{4,5},{5,4},{6,7},{7,6},{8,9},{9,8},{10,11... | collective-permute-start | bytes 1572872 | tf_op jit(solution)/shard_map/ppermute | solution.py:95
  33.5 4.6 %copy-start.1 = (bf16[8,256,1024]{2,1,0:T(8,128)(2,1)}, bf16[8,256,1024]{2,1,0:T(8,128)(2,1)S(1)}, u32[]{:S(2)}) copy-start(bf16[8,256,1024]{2,1,0:T(8,128)(2,1)S(1)} %maximum_dynamic-update-slice_fusion.3) | copy-start | bytes 12582916
  41.9 4.0 %collective-permute-start.14 = (f32[2,8,4,64]{3,2,1,0:T(4,128)S(1)}, f32[2,8,4,64]{3,2,1,0:T(4,128)S(1)}, u32[]{:S(2)}, u32[]{:S(2)}) collective-permute-start(f32[2,8,4,64]{3,2,1,0:T(4,128)S(1)} %pad_maximum_fusion.6), channel_id=1, source_target_pairs={{0,4},{4,0},{1,5},{5,1},{2,6},{6,2},{3,7},{7,3},{8,12},{12,8},{9,1... | collective-permute-start | bytes 49160 | tf_op jit(solution)/shard_map/ppermute | solution.py:148
  45.9 4.0 %collective-permute-start.15 = (f32[2,8,4,64]{3,2,1,0:T(4,128)S(1)}, f32[2,8,4,64]{3,2,1,0:T(4,128)S(1)}, u32[]{:S(2)}, u32[]{:S(2)}) collective-permute-start(f32[2,8,4,64]{3,2,1,0:T(4,128)S(1)} %pad_maximum_fusion.7), channel_id=1, source_target_pairs={{0,2},{1,3},{2,0},{3,1},{4,6},{5,7},{6,4},{7,5},{8,10},{9,11},{10,... | collective-permute-start | bytes 49160 | tf_op jit(solution)/shard_map/ppermute | solution.py:148
  49.9 1.3 %collective-permute-start.16 = (f32[2,8,4,64]{3,2,1,0:T(4,128)S(1)}, f32[2,8,4,64]{3,2,1,0:T(4,128)S(1)}, u32[]{:S(2)}, u32[]{:S(2)}) collective-permute-start(f32[2,8,4,64]{3,2,1,0:T(4,128)S(1)} %pad_maximum_fusion.8), channel_id=1, source_target_pairs={{0,1},{1,0},{2,3},{3,2},{4,5},{5,4},{6,7},{7,6},{8,9},{9,8},{10,11... | collective-permute-start | bytes 49160 | tf_op jit(solution)/shard_map/ppermute | solution.py:148
  51.6 3.4 %copy-start = (f32[2048,512]{1,0:T(8,128)S(1)}, f32[2048,512]{1,0:T(8,128)}, u32[]{:S(2)}) copy-start(f32[2048,512]{1,0:T(8,128)} %get-tuple-element.28) | copy-start | bytes 12582916
  54.5 2.3 %copy-start.2 = (bf16[8,256,1024]{2,1,0:T(8,128)(2,1)S(1)}, bf16[8,256,1024]{2,1,0:T(8,128)(2,1)}, u32[]{:S(2)}) copy-start(bf16[8,256,1024]{2,1,0:T(8,128)(2,1)} %copy-done.1) | copy-start | bytes 12582916
